TPU v7x, 32 devices: a whole 2x2x4 slice. The times are simulated.
32 devices in a mesh: aug: 4 (over x, core), dp: 8 (over z, y).
Axes of the slice: x: 2, y: 2, z: 4, core: 2. Of those that a mesh axis runs over, the one named last changes fastest.
Arguments:
- hidden: bfloat16 [4, 8, 128, 5120], P('aug', 'dp'), may hold values from -30 to 30, as said below
- output_grad: bfloat16 [4, 8, 128, 1280], P('aug', 'dp'), may hold values from -30 to 30, as said below
- down_weight: bfloat16 [5120, 1280], P('aug'), may hold values from -0.15625 to 0.15625
- first_moment: float32 [5120, 1280], P(('aug', 'dp')), may hold values from -6 to 6
- second_moment: float32 [5120, 1280], P(('aug', 'dp')), may hold values from 0.01 to 1
- noise: float32 [5120, 1280], P(('aug', 'dp')), may hold values from -6 to 6
Outputs:
- image_norms: float32 [8], P('dp')
- clipped_mean: float32 [5120, 1280], P(('aug', 'dp'))
- new_first: float32 [5120, 1280], P(('aug', 'dp'))
- new_second: float32 [5120, 1280], P(('aug', 'dp'))
- update: float32 [5120, 1280], P(('aug', 'dp'))
- hidden_grad: bfloat16 [4, 8, 128, 5120], P(None, 'dp', None, 'aug')
Inputs may be any that keep to these rules, and one draw needn't show every extreme that they name: `hidden`: finite activations of every view. `output_grad`: finite output gradients of every view.
All inputs are finite; a program needn't handle non-finite values.
Results may differ from a plain program's by a relative error of at most 0.0004.
Values may be sent and summed in bfloat16 or wider, within the bound.
No kernel may reach another device: no remote copies, remote signals or barrier semaphores. Data moves between devices by JAX's collectives and lax.ppermute only.
A program may use at most 64 MiB of HBM per device.

v0:
```python
import math

import jax
import jax.numpy as jnp
from jax import lax
from jax.sharding import PartitionSpec as P

clip_ratio = 1.9
noise_ratio = 0.002
beta_one = 0.9
beta_two = 0.999
adam_step = 10
adam_eps = 1e-08


def project_back(rows, down_weight):
    return lax.dot_general(
        rows, down_weight, (((1,), (1,)), ((), ())), preferred_element_type=jnp.float32
    )


def per_device(hidden, output_grad, down_weight, first_moment, second_moment, noise):
    views = lax.axis_size("aug")
    groups = lax.axis_size("dp")
    images_here = hidden.shape[1]
    patches = hidden.shape[2]
    width = hidden.shape[3]
    model_width = output_grad.shape[3]
    images_all = images_here * groups
    clip = clip_ratio * math.sqrt(patches * width * model_width / views)
    local_rows = images_here * patches
    swapped = lax.all_to_all(
        hidden.reshape(local_rows, width), "aug", split_axis=1, concat_axis=0, tiled=True
    )
    slice_width = swapped.shape[1]
    grad_rows = output_grad.reshape(local_rows, model_width)
    every = lax.all_gather(grad_rows, "aug", axis=0, tiled=True)
    h_four = swapped.reshape(views, images_here, patches, slice_width)
    g_four = every.reshape(views, images_here, patches, model_width)
    summed = jnp.einsum("vipf,vipd->ifd", h_four, g_four, preferred_element_type=jnp.float32)
    back_rows = project_back(every, down_weight)
    hidden_grad = back_rows.astype(jnp.bfloat16).reshape(views, images_here, patches, slice_width)
    grads = summed / views
    partial_value = jnp.sum(grads * grads, axis=(1, 2))
    squares = lax.psum(partial_value, "aug")
    image_norms = jnp.sqrt(squares)
    factor = clip / jnp.maximum(image_norms, clip)
    clipped_local = jnp.sum(factor[:, None, None] * grads, axis=0)
    owned = lax.psum_scatter(clipped_local, "dp", scatter_dimension=0, tiled=True)
    clipped_mean = owned / images_all
    noisy = clipped_mean + noise_ratio * clip * noise / images_all
    new_first = beta_one * first_moment + (1.0 - beta_one) * noisy
    new_second = beta_two * second_moment + (1.0 - beta_two) * noisy * noisy
    update = (
        new_first
        / (1.0 - beta_one**adam_step)
        / (jnp.sqrt(new_second / (1.0 - beta_two**adam_step)) + adam_eps)
    )
    return (image_norms, clipped_mean, new_first, new_second, update, hidden_grad)


def solution(mesh):
    in_specs = (
        P("aug", "dp", None, None),
        P("aug", "dp", None, None),
        P("aug", None),
        P(("aug", "dp"), None),
        P(("aug", "dp"), None),
        P(("aug", "dp"), None),
    )
    out_specs = (
        P("dp"),
        P(("aug", "dp"), None),
        P(("aug", "dp"), None),
        P(("aug", "dp"), None),
        P(("aug", "dp"), None),
        P(None, "dp", None, "aug"),
    )
    return jax.shard_map(
        per_device, mesh=mesh, in_specs=in_specs, out_specs=out_specs, check_vma=False
    )
```

profile of v0, /device:TPU:0, one launch (start us, length us, event | category | flops | bytes accessed | tf_op | source)
XLA Modules:
  0.0 195.1 jit_solution(4917992396035061875)
XLA Ops:
  7.2 0.0 copy-start
  7.2 0.0 all-gather.3.cloned.1.call-start
  7.2 0.7 all-gather.3.cloned.1.call-update
  7.9 0.0 reduce-scatter.2.cloned.1.call-start
  8.0 2.6 %copy.12 = bf16[1,1,128,5120]{2,3,1,0:T(8,128)(2,1)} copy(bf16[1,1,128,5120]{3,2,1,0:T(8,128)(2,1)} %param.6) | data formatting | bytes 2621440 | tf_op args[0]
  10.6 29.3 %all_to_all.16 = bf16[128,4,1280]{0,2,1:T(8,128)(2,1)} all-to-all(bf16[128,4,1280]{0,2,1:T(8,128)(2,1)} %bitcast.19), channel_id=1, replica_groups=mesh['aug'=4,'dp'=8] {'aug'}, dimensions={1} | all-to-all | bytes 2621440 | tf_op jit(solution)/shard_map/all_to_all | solution.py:32
  39.8 0.0 all-gather.3.cloned.1.call-done
  39.8 6.9 %multiply_reduce_fusion = (f32[]{:T(128)}, f32[1280,1280]{1,0:T(8,128)}) fusion(bf16[4,128,1280]{2,1,0:T(8,128)(2,1)} %bitcast.20, bf16[128,4,1280]{0,2,1:T(8,128)(2,1)} %all_to_all.16), kind=kOutput, calls=%fused_computation.1 | convolution fusion | flops 1682636800 | bytes 9175044 | tf_op jit(solution)/shard_map/vipf,vipd->ifd/dot_general | solution.py:40
  46.7 6.4 %psum.7 = f32[1]{0:T(128)} all-reduce(f32[1]{0:T(128)} %bitcast.4), channel_id=1, replica_groups=mesh['aug'=4,'dp'=8] {'aug'}, use_global_device_ids=true, to_apply=%region_1.0 | all-reduce | flops 1 | bytes 8 | tf_op jit(solution)/shard_map/psum | solution.py:45
  53.8 6.0 %broadcast_multiply_fusion = f32[1280,1280]{1,0:T(8,128)} fusion(f32[1280,1280]{1,0:T(8,128)} %get-tuple-element.17, f32[]{:T(128)} %bitcast.5), kind=kLoop, calls=%fused_computation.2 | loop fusion | flops 1638400 | bytes 13107204 | tf_op jit(solution)/shard_map/mul | solution.py:48
  59.9 0.0 reduce-scatter.2.cloned.1.call-update
  59.9 0.0 copy-done
  59.9 4.3 %convolution_convert_fusion = bf16[512,1280]{1,0:T(8,128)(2,1)} fusion(bf16[1280,1280]{1,0:T(8,128)(2,1)S(1)} %copy-done, bf16[1,1,512,1280]{3,2,1,0:T(8,128)(2,1)} %all-gather.3.cloned.1.call-done), kind=kOutput, calls=%fused_computation.3 | convolution fusion | flops 1678376960 | bytes 5898240 | tf_op jit(solution)/shard_map/dot_general | solution.py:17
  64.1 119.2 %reduce-scatter.2.cloned.1.call-done = f32[160,1280]{1,0:T(8,128)} async-done(((f32[1280,1280]{1,0:T(8,128)}), f32[160,1280]{1,0:T(8,128)}) %reduce-scatter.2.cloned.1.call-update) | async-done | bytes 819216 | tf_op jit(solution)/shard_map/reduce_scatter | solution.py:49
  183.3 3.8 %add_divide_fusion = (f32[160,1280]{1,0:T(8,128)}, f32[160,1280]{1,0:T(8,128)}, f32[160,1280]{1,0:T(8,128)}, f32[160,1280]{1,0:T(8,128)}) fusion(f32[160,1280]{1,0:T(8,128)} %param.11, f32[160,1280]{1,0:T(8,128)} %param.10, f32[160,1280]{1,0:T(8,128)} %param.9, f32[160,1280]{1,0:T(8,128)} %reduce-scatter.2.cloned.1.call-done), kind=kLoop, calls=%fused_computation.8 | loop fusion | flops 2867200 | bytes 6553600 | tf_op jit(solution)/shard_map/div | solution.py:55
Async XLA Ops:
  7.2 52.7 %copy-start = (bf16[1280,1280]{1,0:T(8,128)(2,1)S(1)}, bf16[1280,1280]{1,0:T(8,128)(2,1)}, u32[]{:S(2)}) copy-start(bf16[1280,1280]{1,0:T(8,128)(2,1)} %param.8) | copy-start | bytes 9830404
  7.2 32.7 %all-gather.3.cloned.1.call-start = ((), (), s32[]{:S(2)}) async-start(), calls=%async_computation.3 | async-start | bytes 1638400 | tf_op jit(solution)/shard_map/all_gather | solution.py:37
  7.9 175.4 %reduce-scatter.2.cloned.1.call-start = ((), (), s32[]{:S(2)}) async-start(), calls=%async_computation.2 | async-start | bytes 7372800 | tf_op jit(solution)/shard_map/reduce_scatter | solution.py:49
Sparse Core Ops, SparseCore 0:
  9.6 28.0 all-gather.2
  60.0 123.2 reduce-scatter.1
where the time goes:
time: 195 us
  waiting for transfers between devices  120 us (62%)
  blocking collectives  35.6 us (18%)
  between operations  15.9 us (8%)
  matrix products  11.1 us (6%)
  other arithmetic  9.86 us (5%)
  local copies, waits for them, and re-layouts  2.62 us (1%)
    reduce_scatter x1, waiting for transfers between devices, per_device(): lax.psum_scatter(clipped_local, 'dp', scatter_dimension=0, tiled=True)  119 us
    all_to_all x1, blocking collectives, per_device(): lax.all_to_all(hidden.reshape(local_rows, width), 'aug', split_axis=1, co...  29.3 us
    dot_general x1, matrix products, per_device(): jnp.einsum('vipf,vipd->ifd', h_four, g_four, preferred_element_type=jnp.f...  6.88 us
    psum x1, blocking collectives, per_device(): squares = lax.psum(partial_value, 'aug')  6.36 us
    mul x1, other arithmetic, per_device(): clipped_local = jnp.sum(factor[:, None, None] * grads, axis=0)  6.03 us
    dot_general x1, matrix products, project_back(): lax.dot_general(rows, down_weight, (((1,), (1,)), ((), ())), preferred_el...  4.26 us
  transfers between devices with their start and end apart: 2, of which 1 were waited for; matrix products, arithmetic and copies ran while one was open for 4% of the time, Pallas kernels for 0%

commit v1 on v0

--- a/solution.py
+++ b/solution.py
@@ -19,7 +19,67 @@
     )
 
 
-def per_device(hidden, output_grad, down_weight, first_moment, second_moment, noise):
+def grid_cycle(points):
+    zs = sorted({z for z, _ in points})
+    ys = sorted({y for _, y in points})
+    if len(zs) * len(ys) != len(points):
+        return None
+    swap = len(zs) % 2 == 1
+    if swap:
+        zs, ys = ys, zs
+    rows, cols = len(zs), len(ys)
+    if rows % 2 == 1 or cols < 2:
+        return None
+    walk = [(0, c) for c in range(cols)]
+    for r in range(1, rows):
+        order = range(cols - 1, 0, -1) if r % 2 == 1 else range(1, cols)
+        walk += [(r, c) for c in order]
+    walk += [(r, 0) for r in range(rows - 1, 0, -1)]
+    cycle = [(zs[r], ys[c]) for r, c in walk]
+    if swap:
+        cycle = [(y, z) for z, y in cycle]
+    return cycle
+
+
+def ring_order(mesh):
+    column = list(mesh.devices[0, :])
+    n = len(column)
+    try:
+        places = [(int(d.coords[2]), int(d.coords[1])) for d in column]
+    except Exception:
+        return list(range(n))
+    cycle = grid_cycle(places)
+    if cycle is None or len(set(places)) != n:
+        return list(range(n))
+    return [places.index(p) for p in cycle]
+
+
+def ring_reduce_scatter(parts, ring, step_fn):
+    n = len(ring)
+    pos_of = [0] * n
+    for k, d in enumerate(ring):
+        pos_of[d] = k
+    ring_arr = jnp.array(ring, jnp.int32)
+    me = lax.axis_index("dp")
+    pos = jnp.array(pos_of, jnp.int32)[me]
+    right = [(ring[k], ring[(k + 1) % n]) for k in range(n)]
+    left = [(ring[k], ring[(k - 1) % n]) for k in range(n)]
+    acc_r = None
+    acc_l = None
+    for s in range(n - 1):
+        blk_r = ring_arr[(pos - 1 - s) % n]
+        blk_l = ring_arr[(pos + 1 + s) % n]
+        own_r = parts(blk_r)[0]
+        own_l = parts(blk_l)[1]
+        send_r = own_r if acc_r is None else acc_r + own_r
+        send_l = own_l if acc_l is None else acc_l + own_l
+        acc_r = lax.ppermute(send_r, "dp", right)
+        acc_l = lax.ppermute(send_l, "dp", left)
+    mine = parts(me)
+    return jnp.concatenate([acc_r + mine[0], acc_l + mine[1]], axis=0)
+
+
+def per_device(ring, hidden, output_grad, down_weight, first_moment, second_moment, noise):
     views = lax.axis_size("aug")
     groups = lax.axis_size("dp")
     images_here = hidden.shape[1]
@@ -45,8 +105,16 @@
     squares = lax.psum(partial_value, "aug")
     image_norms = jnp.sqrt(squares)
     factor = clip / jnp.maximum(image_norms, clip)
-    clipped_local = jnp.sum(factor[:, None, None] * grads, axis=0)
-    owned = lax.psum_scatter(clipped_local, "dp", scatter_dimension=0, tiled=True)
+    owned_rows = slice_width // groups
+    half = owned_rows // 2
+
+    def parts(block):
+        start = block * owned_rows
+        rows = lax.dynamic_slice_in_dim(grads, start, owned_rows, axis=1)
+        clipped = jnp.sum(factor[:, None, None] * rows, axis=0)
+        return clipped[:half], clipped[half:]
+
+    owned = ring_reduce_scatter(parts, ring, None)
     clipped_mean = owned / images_all
     noisy = clipped_mean + noise_ratio * clip * noise / images_all
     new_first = beta_one * first_moment + (1.0 - beta_one) * noisy
@@ -76,6 +144,11 @@
         P(("aug", "dp"), None),
         P(None, "dp", None, "aug"),
     )
+    ring = ring_order(mesh)
+
+    def body(*args):
+        return per_device(ring, *args)
+
     return jax.shard_map(
-        per_device, mesh=mesh, in_specs=in_specs, out_specs=out_specs, check_vma=False
+        body, mesh=mesh, in_specs=in_specs, out_specs=out_specs, check_vma=False
     )

time: 195 us -> 146 us (0.75)
  waiting for transfers between devices: 120 us -> 59.5 us
  blocking collectives: 35.6 us -> 6.36 us
  starting transfers between devices: 0.08 us -> 19.4 us
  between operations: 15.9 us -> 34.3 us
  local copies, waits for them, and re-layouts: 2.62 us -> 6.22 us
    reduce_scatter x1 -> x0, waiting for transfers between devices: 119 us -> none  [per_device(): lax.psum_scatter(clipped_local, 'dp', scatter_dimension=0, tiled=True)]
    ppermute x0 -> x14, waiting for transfers between devices: none -> 53.4 us  [the longest x7 48.9 us: ring_reduce_scatter(): acc_r = lax.ppermute(send_r, 'dp', right)]
    all_to_all x1 -> x0, blocking collectives: 29.3 us -> none  [per_device(): lax.all_to_all(hidden.reshape(local_rows, width), 'aug', split_axis=1, co...]
    ppermute x0 -> x14, starting transfers between devices: none -> 14.9 us  [the longest x7 11.6 us: ring_reduce_scatter(): acc_r = lax.ppermute(send_r, 'dp', right)]
    all_to_all x0 -> x1, waiting for transfers between devices: none -> 5.41 us  [per_device(): lax.all_to_all(hidden.reshape(local_rows, width), 'aug', split_axis=1, co...]
    all_to_all x0 -> x1, starting transfers between devices: none -> 4.46 us  [per_device(): lax.all_to_all(hidden.reshape(local_rows, width), 'aug', split_axis=1, co...]
    slice x0 -> x2, local copies, waits for them, and re-layouts: none -> 2.18 us  [parts(): return (clipped[:half], clipped[half:])]
  transfers between devices with their start and end apart: 2 -> 16, of which waited for: 1 -> 15; matrix products, arithmetic and copies ran while one was open for 4% -> 6% of each run, Pallas kernels for 0% -> 0%
where the time goes in v1:
time: 146 us
  waiting for transfers between devices  59.5 us (41%)
  between operations  34.3 us (23%)
  starting transfers between devices  19.4 us (13%)
  other arithmetic  10.3 us (7%)
  matrix products  9.88 us (7%)
  blocking collectives  6.36 us (4%)
  local copies, waits for them, and re-layouts  6.22 us (4%)
    ppermute x7, waiting for transfers between devices, ring_reduce_scatter(): acc_r = lax.ppermute(send_r, 'dp', right)  48.9 us
    ppermute x7, starting transfers between devices, ring_reduce_scatter(): acc_r = lax.ppermute(send_r, 'dp', right)  11.6 us
    mul x1, other arithmetic, parts(): clipped = jnp.sum(factor[:, None, None] * rows, axis=0)  7.67 us
    dot_general x1, matrix products, per_device(): jnp.einsum('vipf,vipd->ifd', h_four, g_four, preferred_element_type=jnp.f...  6.93 us
    psum x1, blocking collectives, per_device(): squares = lax.psum(partial_value, 'aug')  6.36 us
    all_to_all x1, waiting for transfers between devices, per_device(): lax.all_to_all(hidden.reshape(local_rows, width), 'aug', split_axis=1, co...  5.41 us
    ppermute x7, waiting for transfers between devices, ring_reduce_scatter(): acc_l = lax.ppermute(send_l, 'dp', left)  4.49 us
    all_to_all x1, starting transfers between devices, per_device(): lax.all_to_all(hidden.reshape(local_rows, width), 'aug', split_axis=1, co...  4.46 us
  transfers between devices with their start and end apart: 16, of which 15 were waited for; matrix products, arithmetic and copies ran while one was open for 6% of the time, Pallas kernels for 0%

profile of v1, /device:TPU:0, one launch (start us, length us, event | category | flops | bytes accessed | tf_op | source)
XLA Modules:
  0.0 145.9 jit_solution(13919195115871357747)
XLA Ops:
  7.2 0.0 copy-start
  7.2 0.0 all-gather.3.cloned.1.call-start
  7.2 0.7 all-gather.3.cloned.1.call-update
  7.9 2.7 %copy.14 = bf16[1,1,128,5120]{2,3,1,0:T(8,128)(2,1)} copy(bf16[1,1,128,5120]{3,2,1,0:T(8,128)(2,1)} %param.8) | data formatting | bytes 2621440 | tf_op args[0]
  10.6 4.5 %all-to-all-start = ((bf16[128,4,1280]{0,2,1:T(8,128)(2,1)}), bf16[128,4,1280]{0,2,1:T(8,128)(2,1)}, u32[]{:S(2)}, u32[]{:S(2)}) async-start(bf16[128,4,1280]{0,2,1:T(8,128)(2,1)} %bitcast.139), calls=%async_computation | async-start | bytes 2621440 | tf_op jit(solution)/shard_map/all_to_all | solution.py:92
  15.0 0.0 copy-done.13
  15.1 0.6 dynamic_slice.60
  25.0 0.0 copy-done.11
  25.0 0.7 fusion.19
  34.6 5.4 %all-to-all-done = bf16[128,4,1280]{0,2,1:T(8,128)(2,1)} async-done(((bf16[128,4,1280]{0,2,1:T(8,128)(2,1)}), bf16[128,4,1280]{0,2,1:T(8,128)(2,1)}, u32[]{:S(2)}, u32[]{:S(2)}) %all-to-all-start) | async-done | bytes 1310752 | tf_op jit(solution)/shard_map/all_to_all | solution.py:92
  40.0 6.9 %multiply_reduce_fusion = (f32[]{:T(128)}, f32[1280,1280]{1,0:T(8,128)}) fusion(bf16[4,128,1280]{2,1,0:T(8,128)(2,1)} %bitcast.140, bf16[128,4,1280]{0,2,1:T(8,128)(2,1)} %all-to-all-done), kind=kOutput, calls=%fused_computation.2 | convolution fusion | flops 1682636800 | bytes 9175044 | tf_op jit(solution)/shard_map/vipf,vipd->ifd/dot_general | solution.py:100
  46.9 6.4 %psum.7 = f32[1]{0:T(128)} all-reduce(f32[1]{0:T(128)} %bitcast.4), channel_id=1, replica_groups=mesh['aug'=4,'dp'=8] {'aug'}, use_global_device_ids=true, to_apply=%region_1.0 | all-reduce | flops 1 | bytes 8 | tf_op jit(solution)/shard_map/psum | solution.py:105
  54.0 7.7 %multiply_bitcast_fusion.8 = (f32[1,160,1280]{2,1,0:T(8,128)S(1)}, f32[1,160,1280]{2,1,0:T(8,128)S(1)}, f32[1,160,1280]{2,1,0:T(8,128)S(1)}, f32[1,160,1280]{2,1...) fusion(f32[1280,1280]{1,0:T(8,128)} %get-tuple-element.48, ...), kind=kLoop, calls=%fused_computation.20 | loop fusion | flops 3072000 | bytes 24576064 | tf_op jit(solution)/shard_map/mul | solution.py:114
  61.7 0.0 copy-start.6
  61.7 1.1 slice_bitcast_fusion.15
  62.9 2.4 %collective-permute-start = (f32[80,1280]{1,0:T(8,128)S(1)}, f32[80,1280]{1,0:T(8,128)S(1)}, u32[]{:S(2)}, u32[]{:S(2)}) collective-permute-start(f32[80,1280]{1,0:T(8,128)S(1)} %slice_bitcast_fusion.15), channel_id=1, source_target_pairs={{0,1},{1,3},{3,5},{5,7},{7,6},{6,4},{4,2},{2,0},{8,9},{9,11},{11,1... | collective-permute-start | bytes 1228808 | tf_op jit(solution)/shard_map/ppermute | solution.py:76
  65.3 1.0 slice_bitcast_fusion.7
  66.3 0.0 copy-start.5
  66.3 0.1 collective-permute-start.7
  66.4 8.3 %collective-permute-done = f32[80,1280]{1,0:T(8,128)S(1)} collective-permute-done((f32[80,1280]{1,0:T(8,128)S(1)}, f32[80,1280]{1,0:T(8,128)S(1)}, u32[]{:S(2)}, u32[]{:S(2)}) %collective-permute-start) | collective-permute-done | bytes 409632 | tf_op jit(solution)/shard_map/ppermute | solution.py:76
  74.7 0.0 copy-done.7
  74.8 0.0 copy-start.4
  74.8 1.8 %collective-permute-start.1 = (f32[80,1280]{1,0:T(8,128)S(1)}, f32[80,1280]{1,0:T(8,128)S(1)}, u32[]{:S(2)}, u32[]{:S(2)}) collective-permute-start(f32[80,1280]{1,0:T(8,128)S(1)} %fusion.17), channel_id=1, source_target_pairs={{0,1},{1,3},{3,5},{5,7},{7,6},{6,4},{4,2},{2,0},{8,9},{9,11},{11,1... | collective-permute-start | bytes 1228808 | tf_op jit(solution)/shard_map/ppermute | solution.py:76
  76.5 0.7 collective-permute-done.7
  77.2 0.0 copy-done.6
  77.3 0.0 copy-start.3
  77.3 0.4 collective-permute-start.8
  77.7 7.7 %collective-permute-done.1 = f32[80,1280]{1,0:T(8,128)S(1)} collective-permute-done((f32[80,1280]{1,0:T(8,128)S(1)}, f32[80,1280]{1,0:T(8,128)S(1)}, u32[]{:S(2)}, u32[]{:S(2)}) %collective-permute-start.1) | collective-permute-done | bytes 409632 | tf_op jit(solution)/shard_map/ppermute | solution.py:76
  85.4 0.0 copy-done.5
  85.4 0.0 copy-start.2
  85.5 1.4 collective-permute-start.2
  86.9 0.4 collective-permute-done.8
  87.3 0.0 copy-done.4
  87.3 0.0 copy-start.1
  87.3 0.7 collective-permute-start.9
  88.0 7.1 %collective-permute-done.2 = f32[80,1280]{1,0:T(8,128)S(1)} collective-permute-done((f32[80,1280]{1,0:T(8,128)S(1)}, f32[80,1280]{1,0:T(8,128)S(1)}, u32[]{:S(2)}, u32[]{:S(2)}) %collective-permute-start.2) | collective-permute-done | bytes 409632 | tf_op jit(solution)/shard_map/ppermute | solution.py:76
  95.2 0.0 copy-done.3
  95.2 1.3 collective-permute-start.3
  96.5 0.4 collective-permute-done.9
  96.9 0.0 copy-done.2
  97.0 0.7 collective-permute-start.10
  97.7 7.1 %collective-permute-done.3 = f32[80,1280]{1,0:T(8,128)S(1)} collective-permute-done((f32[80,1280]{1,0:T(8,128)S(1)}, f32[80,1280]{1,0:T(8,128)S(1)}, u32[]{:S(2)}, u32[]{:S(2)}) %collective-permute-start.3) | collective-permute-done | bytes 409632 | tf_op jit(solution)/shard_map/ppermute | solution.py:76
  104.8 0.0 copy-done.1
  104.8 1.3 collective-permute-start.4
  106.2 0.4 collective-permute-done.10
  106.6 0.1 fusion.7
  106.6 0.7 collective-permute-start.11
  107.3 7.4 %collective-permute-done.4 = f32[80,1280]{1,0:T(8,128)S(1)} collective-permute-done((f32[80,1280]{1,0:T(8,128)S(1)}, f32[80,1280]{1,0:T(8,128)S(1)}, u32[]{:S(2)}, u32[]{:S(2)}) %collective-permute-start.4) | collective-permute-done | bytes 409632 | tf_op jit(solution)/shard_map/ppermute | solution.py:76
  114.7 0.1 fusion.13
  114.8 1.6 %collective-permute-start.5 = (f32[80,1280]{1,0:T(8,128)S(1)}, f32[80,1280]{1,0:T(8,128)S(1)}, u32[]{:S(2)}, u32[]{:S(2)}) collective-permute-start(f32[80,1280]{1,0:T(8,128)S(1)} %fusion.13), channel_id=1, source_target_pairs={{0,1},{1,3},{3,5},{5,7},{7,6},{6,4},{4,2},{2,0},{8,9},{9,11},{11,1... | collective-permute-start | bytes 1228808 | tf_op jit(solution)/shard_map/ppermute | solution.py:76
  116.4 0.4 collective-permute-done.11
  116.8 0.1 fusion.6
  116.8 0.4 collective-permute-start.12
  117.2 8.6 %collective-permute-done.5 = f32[80,1280]{1,0:T(8,128)S(1)} collective-permute-done((f32[80,1280]{1,0:T(8,128)S(1)}, f32[80,1280]{1,0:T(8,128)S(1)}, u32[]{:S(2)}, u32[]{:S(2)}) %collective-permute-start.5) | collective-permute-done | bytes 409632 | tf_op jit(solution)/shard_map/ppermute | solution.py:76
  125.8 0.1 fusion.12
  125.8 1.8 %collective-permute-start.6 = (f32[80,1280]{1,0:T(8,128)S(1)}, f32[80,1280]{1,0:T(8,128)S(1)}, u32[]{:S(2)}, u32[]{:S(2)}) collective-permute-start(f32[80,1280]{1,0:T(8,128)S(1)} %fusion.12), channel_id=1, source_target_pairs={{0,1},{1,3},{3,5},{5,7},{7,6},{6,4},{4,2},{2,0},{8,9},{9,11},{11,1... | collective-permute-start | bytes 1228808 | tf_op jit(solution)/shard_map/ppermute | solution.py:76
  127.6 0.2 collective-permute-done.12
  127.8 0.1 fusion.5
  127.8 0.3 collective-permute-start.13
  128.2 2.9 %convolution_convert_fusion = bf16[512,1280]{1,0:T(8,128)(2,1)} fusion(bf16[1280,1280]{1,0:T(8,128)(2,1)S(1)} %copy-done, bf16[1,1,512,1280]{3,2,1,0:T(8,128)(2,1)S(1)} %copy-done.12), kind=kOutput, calls=%fused_computation.3 | convolution fusion | flops 1678376960 | bytes 5898240 | tf_op jit(solution)/shard_map/dot_general | solution.py:17
  131.1 2.7 %collective-permute-done.6 = f32[80,1280]{1,0:T(8,128)S(1)} collective-permute-done((f32[80,1280]{1,0:T(8,128)S(1)}, f32[80,1280]{1,0:T(8,128)S(1)}, u32[]{:S(2)}, u32[]{:S(2)}) %collective-permute-start.6) | collective-permute-done | bytes 409632 | tf_op jit(solution)/shard_map/ppermute | solution.py:76
  133.8 2.0 %collective-permute-done.13 = f32[80,1280]{1,0:T(8,128)S(1)} collective-permute-done((f32[80,1280]{1,0:T(8,128)S(1)}, f32[80,1280]{1,0:T(8,128)S(1)}, u32[]{:S(2)}, u32[]{:S(2)}) %collective-permute-start.13) | collective-permute-done | bytes 409632 | tf_op jit(solution)/shard_map/ppermute | solution.py:77
  135.8 0.1 fusion.11
  136.0 1.9 %add_divide_fusion = (f32[160,1280]{1,0:T(8,128)}, f32[160,1280]{1,0:T(8,128)}, f32[160,1280]{1,0:T(8,128)}, f32[160,1280]{1,0:T(8,128)}) fusion(f32[160,1280]{1,0:T(8,128)S(1)} %copy-done.8, f32[160,1280]{1,0:T(8,128)S(1)} %copy-done.9, f32[160,1280]{1,0:T(8,128)S(1)} %copy-done.10, f32[80,1280]{1,0:T(8,128)S(1)} %get-tuple-element.32, ...), kind=kLoop, calls=%fused_computation.9 | loop fusion | flops 3072000 | bytes 6553600 | tf_op jit(solution)/shard_map/div | solution.py:123
  (20 shorter events, 0.3 us)
Async XLA Ops:
  7.2 121.0 %copy-start = (bf16[1280,1280]{1,0:T(8,128)(2,1)S(1)}, bf16[1280,1280]{1,0:T(8,128)(2,1)}, u32[]{:S(2)}) copy-start(bf16[1280,1280]{1,0:T(8,128)(2,1)} %param.10) | copy-start | bytes 9830404
  7.2 32.8 %all-gather.3.cloned.1.call-start = ((), (), s32[]{:S(2)}) async-start(), calls=%async_computation.1 | async-start | bytes 1638400 | tf_op jit(solution)/shard_map/all_gather | solution.py:97
  10.6 4.5 %copy-start.13 = (s32[8]{0:T(128)S(1)}, s32[8]{0:T(128)}, u32[]{:S(2)}) copy-start(s32[8]{0:T(128)} %constant.177.clone) | copy-start | bytes 100
  10.6 14.4 %copy-start.11 = (s32[8]{0:T(128)S(1)}, s32[8]{0:T(128)}, u32[]{:S(2)}) copy-start(s32[8]{0:T(128)} %constant.176.clone) | copy-start | bytes 100
  10.6 29.4 %all-to-all-start = ((bf16[128,4,1280]{0,2,1:T(8,128)(2,1)}), bf16[128,4,1280]{0,2,1:T(8,128)(2,1)}, u32[]{:S(2)}, u32[]{:S(2)}) async-start(bf16[128,4,1280]{0,2,1:T(8,128)(2,1)} %bitcast.139), calls=%async_computation | async-start | bytes 2621440 | tf_op jit(solution)/shard_map/all_to_all | solution.py:92
  61.7 13.0 %copy-start.7 = (f32[1,160,1280]{2,1,0:T(8,128)S(1)}, f32[1,160,1280]{2,1,0:T(8,128)}, u32[]{:S(2)}) copy-start(f32[1,160,1280]{2,1,0:T(8,128)} %get-tuple-element.29) | copy-start | bytes 2457604
  61.7 15.5 %copy-start.6 = (f32[1,160,1280]{2,1,0:T(8,128)S(1)}, f32[1,160,1280]{2,1,0:T(8,128)}, u32[]{:S(2)}) copy-start(f32[1,160,1280]{2,1,0:T(8,128)} %get-tuple-element.22) | copy-start | bytes 2457604
  62.9 11.8 %collective-permute-start = (f32[80,1280]{1,0:T(8,128)S(1)}, f32[80,1280]{1,0:T(8,128)S(1)}, u32[]{:S(2)}, u32[]{:S(2)}) collective-permute-start(f32[80,1280]{1,0:T(8,128)S(1)} %slice_bitcast_fusion.15), channel_id=1, source_target_pairs={{0,1},{1,3},{3,5},{5,7},{7,6},{6,4},{4,2},{2,0},{8,9},{9,11},{11,1... | collective-permute-start | bytes 1228808 | tf_op jit(solution)/shard_map/ppermute | solution.py:76
  66.3 19.1 %copy-start.5 = (f32[1,160,1280]{2,1,0:T(8,128)S(1)}, f32[1,160,1280]{2,1,0:T(8,128)}, u32[]{:S(2)}) copy-start(f32[1,160,1280]{2,1,0:T(8,128)} %get-tuple-element.28) | copy-start | bytes 2457604
  66.3 10.9 %collective-permute-start.7 = (f32[80,1280]{1,0:T(8,128)S(1)}, f32[80,1280]{1,0:T(8,128)S(1)}, u32[]{:S(2)}, u32[]{:S(2)}) collective-permute-start(f32[80,1280]{1,0:T(8,128)S(1)} %slice_bitcast_fusion.7), channel_id=1, source_target_pairs={{0,2},{1,0},{3,1},{5,3},{7,5},{6,7},{4,6},{2,4},{8,10},{9,8},{11,9... | collective-permute-start | bytes 1228808 | tf_op jit(solution)/shard_map/ppermute | solution.py:77
  74.8 12.5 %copy-start.4 = (f32[1,160,1280]{2,1,0:T(8,128)S(1)}, f32[1,160,1280]{2,1,0:T(8,128)}, u32[]{:S(2)}) copy-start(f32[1,160,1280]{2,1,0:T(8,128)} %get-tuple-element.21) | copy-start | bytes 2457604
  74.8 10.6 %collective-permute-start.1 = (f32[80,1280]{1,0:T(8,128)S(1)}, f32[80,1280]{1,0:T(8,128)S(1)}, u32[]{:S(2)}, u32[]{:S(2)}) collective-permute-start(f32[80,1280]{1,0:T(8,128)S(1)} %fusion.17), channel_id=1, source_target_pairs={{0,1},{1,3},{3,5},{5,7},{7,6},{6,4},{4,2},{2,0},{8,9},{9,11},{11,1... | collective-permute-start | bytes 1228808 | tf_op jit(solution)/shard_map/ppermute | solution.py:76
  77.3 17.9 %copy-start.3 = (f32[1,160,1280]{2,1,0:T(8,128)S(1)}, f32[1,160,1280]{2,1,0:T(8,128)}, u32[]{:S(2)}) copy-start(f32[1,160,1280]{2,1,0:T(8,128)} %get-tuple-element.27) | copy-start | bytes 2457604
  77.3 10.0 %collective-permute-start.8 = (f32[80,1280]{1,0:T(8,128)S(1)}, f32[80,1280]{1,0:T(8,128)S(1)}, u32[]{:S(2)}, u32[]{:S(2)}) collective-permute-start(f32[80,1280]{1,0:T(8,128)S(1)} %fusion.10), channel_id=1, source_target_pairs={{0,2},{1,0},{3,1},{5,3},{7,5},{6,7},{4,6},{2,4},{8,10},{9,8},{11,9... | collective-permute-start | bytes 1228808 | tf_op jit(solution)/shard_map/ppermute | solution.py:77
  85.4 11.5 %copy-start.2 = (f32[1,160,1280]{2,1,0:T(8,128)S(1)}, f32[1,160,1280]{2,1,0:T(8,128)}, u32[]{:S(2)}) copy-start(f32[1,160,1280]{2,1,0:T(8,128)} %get-tuple-element.20) | copy-start | bytes 2457604
  85.5 9.7 %collective-permute-start.2 = (f32[80,1280]{1,0:T(8,128)S(1)}, f32[80,1280]{1,0:T(8,128)S(1)}, u32[]{:S(2)}, u32[]{:S(2)}) collective-permute-start(f32[80,1280]{1,0:T(8,128)S(1)} %fusion.16), channel_id=1, source_target_pairs={{0,1},{1,3},{3,5},{5,7},{7,6},{6,4},{4,2},{2,0},{8,9},{9,11},{11,1... | collective-permute-start | bytes 1228808 | tf_op jit(solution)/shard_map/ppermute | solution.py:76
  87.3 17.5 %copy-start.1 = (f32[1,160,1280]{2,1,0:T(8,128)S(1)}, f32[1,160,1280]{2,1,0:T(8,128)}, u32[]{:S(2)}) copy-start(f32[1,160,1280]{2,1,0:T(8,128)} %get-tuple-element.26) | copy-start | bytes 2457604
  87.3 9.6 %collective-permute-start.9 = (f32[80,1280]{1,0:T(8,128)S(1)}, f32[80,1280]{1,0:T(8,128)S(1)}, u32[]{:S(2)}, u32[]{:S(2)}) collective-permute-start(f32[80,1280]{1,0:T(8,128)S(1)} %fusion.9), channel_id=1, source_target_pairs={{0,2},{1,0},{3,1},{5,3},{7,5},{6,7},{4,6},{2,4},{8,10},{9,8},{11,9... | collective-permute-start | bytes 1228808 | tf_op jit(solution)/shard_map/ppermute | solution.py:77
  95.2 9.6 %collective-permute-start.3 = (f32[80,1280]{1,0:T(8,128)S(1)}, f32[80,1280]{1,0:T(8,128)S(1)}, u32[]{:S(2)}, u32[]{:S(2)}) collective-permute-start(f32[80,1280]{1,0:T(8,128)S(1)} %fusion.15), channel_id=1, source_target_pairs={{0,1},{1,3},{3,5},{5,7},{7,6},{6,4},{4,2},{2,0},{8,9},{9,11},{11,1... | collective-permute-start | bytes 1228808 | tf_op jit(solution)/shard_map/ppermute | solution.py:76
  97.0 9.6 %collective-permute-start.10 = (f32[80,1280]{1,0:T(8,128)S(1)}, f32[80,1280]{1,0:T(8,128)S(1)}, u32[]{:S(2)}, u32[]{:S(2)}) collective-permute-start(f32[80,1280]{1,0:T(8,128)S(1)} %fusion.8), channel_id=1, source_target_pairs={{0,2},{1,0},{3,1},{5,3},{7,5},{6,7},{4,6},{2,4},{8,10},{9,8},{11,9... | collective-permute-start | bytes 1228808 | tf_op jit(solution)/shard_map/ppermute | solution.py:77
  104.8 9.9 %collective-permute-start.4 = (f32[80,1280]{1,0:T(8,128)S(1)}, f32[80,1280]{1,0:T(8,128)S(1)}, u32[]{:S(2)}, u32[]{:S(2)}) collective-permute-start(f32[80,1280]{1,0:T(8,128)S(1)} %fusion.14), channel_id=1, source_target_pairs={{0,1},{1,3},{3,5},{5,7},{7,6},{6,4},{4,2},{2,0},{8,9},{9,11},{11,1... | collective-permute-start | bytes 1228808 | tf_op jit(solution)/shard_map/ppermute | solution.py:76
  106.6 10.1 %collective-permute-start.11 = (f32[80,1280]{1,0:T(8,128)S(1)}, f32[80,1280]{1,0:T(8,128)S(1)}, u32[]{:S(2)}, u32[]{:S(2)}) collective-permute-start(f32[80,1280]{1,0:T(8,128)S(1)} %fusion.7), channel_id=1, source_target_pairs={{0,2},{1,0},{3,1},{5,3},{7,5},{6,7},{4,6},{2,4},{8,10},{9,8},{11,9... | collective-permute-start | bytes 1228808 | tf_op jit(solution)/shard_map/ppermute | solution.py:77
  114.8 11.0 %collective-permute-start.5 = (f32[80,1280]{1,0:T(8,128)S(1)}, f32[80,1280]{1,0:T(8,128)S(1)}, u32[]{:S(2)}, u32[]{:S(2)}) collective-permute-start(f32[80,1280]{1,0:T(8,128)S(1)} %fusion.13), channel_id=1, source_target_pairs={{0,1},{1,3},{3,5},{5,7},{7,6},{6,4},{4,2},{2,0},{8,9},{9,11},{11,1... | collective-permute-start | bytes 1228808 | tf_op jit(solution)/shard_map/ppermute | solution.py:76
  116.8 11.4 %copy-start.12 = (bf16[1,1,512,1280]{3,2,1,0:T(8,128)(2,1)S(1)}, bf16[1,1,512,1280]{3,2,1,0:T(8,128)(2,1)}, u32[]{:S(2)}) copy-start(bf16[1,1,512,1280]{3,2,1,0:T(8,128)(2,1)} %all-gather.3.cloned.1.call-done) | copy-start | bytes 3932164
  116.8 11.0 %collective-permute-start.12 = (f32[80,1280]{1,0:T(8,128)S(1)}, f32[80,1280]{1,0:T(8,128)S(1)}, u32[]{:S(2)}, u32[]{:S(2)}) collective-permute-start(f32[80,1280]{1,0:T(8,128)S(1)} %fusion.6), channel_id=1, source_target_pairs={{0,2},{1,0},{3,1},{5,3},{7,5},{6,7},{4,6},{2,4},{8,10},{9,8},{11,9... | collective-permute-start | bytes 1228808 | tf_op jit(solution)/shard_map/ppermute | solution.py:77
  125.8 8.0 %collective-permute-start.6 = (f32[80,1280]{1,0:T(8,128)S(1)}, f32[80,1280]{1,0:T(8,128)S(1)}, u32[]{:S(2)}, u32[]{:S(2)}) collective-permute-start(f32[80,1280]{1,0:T(8,128)S(1)} %fusion.12), channel_id=1, source_target_pairs={{0,1},{1,3},{3,5},{5,7},{7,6},{6,4},{4,2},{2,0},{8,9},{9,11},{11,1... | collective-permute-start | bytes 1228808 | tf_op jit(solution)/shard_map/ppermute | solution.py:76
  127.8 8.0 %collective-permute-start.13 = (f32[80,1280]{1,0:T(8,128)S(1)}, f32[80,1280]{1,0:T(8,128)S(1)}, u32[]{:S(2)}, u32[]{:S(2)}) collective-permute-start(f32[80,1280]{1,0:T(8,128)S(1)} %fusion.5), channel_id=1, source_target_pairs={{0,2},{1,0},{3,1},{5,3},{7,5},{6,7},{4,6},{2,4},{8,10},{9,8},{11,9... | collective-permute-start | bytes 1228808 | tf_op jit(solution)/shard_map/ppermute | solution.py:77
  131.1 4.8 %copy-start.8 = (f32[160,1280]{1,0:T(8,128)S(1)}, f32[160,1280]{1,0:T(8,128)}, u32[]{:S(2)}) copy-start(f32[160,1280]{1,0:T(8,128)} %param.13) | copy-start | bytes 2457604
  131.1 4.8 %copy-start.9 = (f32[160,1280]{1,0:T(8,128)S(1)}, f32[160,1280]{1,0:T(8,128)}, u32[]{:S(2)}) copy-start(f32[160,1280]{1,0:T(8,128)} %param.12) | copy-start | bytes 2457604
  131.1 4.8 %copy-start.10 = (f32[160,1280]{1,0:T(8,128)S(1)}, f32[160,1280]{1,0:T(8,128)}, u32[]{:S(2)}) copy-start(f32[160,1280]{1,0:T(8,128)} %param.11) | copy-start | bytes 2457604
Sparse Core Ops, SparseCore 0:
  9.6 28.0 all-gather.2

commit v2 on v1

--- a/solution.py
+++ b/solution.py
@@ -69,14 +69,59 @@
     for s in range(n - 1):
         blk_r = ring_arr[(pos - 1 - s) % n]
         blk_l = ring_arr[(pos + 1 + s) % n]
-        own_r = parts(blk_r)[0]
-        own_l = parts(blk_l)[1]
-        send_r = own_r if acc_r is None else acc_r + own_r
-        send_l = own_l if acc_l is None else acc_l + own_l
+        if acc_r is None:
+            send_r = parts(blk_r, 0, None)
+            send_l = parts(blk_l, 1, None)
+        else:
+            send_r = acc_r + parts(blk_r, 0, acc_r)
+            send_l = acc_l + parts(blk_l, 1, acc_l)
         acc_r = lax.ppermute(send_r, "dp", right)
         acc_l = lax.ppermute(send_l, "dp", left)
-    mine = parts(me)
-    return jnp.concatenate([acc_r + mine[0], acc_l + mine[1]], axis=0)
+    return jnp.concatenate(
+        [acc_r + parts(me, 0, acc_r), acc_l + parts(me, 1, acc_l)], axis=0
+    )
+
+
+def exchange_four(h_rows, grad_rows):
+    a = lax.axis_index("aug")
+    rows = h_rows.shape[0]
+    sw = h_rows.shape[1] // 4
+
+    def cols(b):
+        return lax.dynamic_slice_in_dim(h_rows, b * sw, sw, axis=1)
+
+    over_x = [(i, i ^ 2) for i in range(4)]
+    over_core = [(i, i ^ 1) for i in range(4)]
+    far = lax.ppermute(
+        jnp.concatenate([cols(a ^ 2), cols(a ^ 3), grad_rows], axis=1), "aug", over_x
+    )
+    near = lax.ppermute(cols(a ^ 1), "aug", over_core)
+    far_mine = far[:, :sw]
+    relay = lax.ppermute(
+        jnp.concatenate([far[:, sw:2 * sw], far[:, 2 * sw:], grad_rows], axis=1),
+        "aug",
+        over_core,
+    )
+    d = grad_rows.shape[1]
+    h_from = {0: cols(a), 1: near, 2: far_mine, 3: relay[:, :sw]}
+    g_from = {0: grad_rows, 1: relay[:, sw + d:], 2: far[:, 2 * sw:], 3: relay[:, sw:sw + d]}
+    h_all = jnp.zeros((4 * rows, sw), h_rows.dtype)
+    g_all = jnp.zeros((4 * rows, grad_rows.shape[1]), grad_rows.dtype)
+    for m in range(4):
+        at = (a ^ m) * rows
+        h_all = lax.dynamic_update_slice_in_dim(h_all, h_from[m], at, axis=0)
+        g_all = lax.dynamic_update_slice_in_dim(g_all, g_from[m], at, axis=0)
+    return h_all, g_all
+
+
+def butterfly_sum(value, n):
+    if n & (n - 1):
+        return lax.psum(value, "aug")
+    bit = 1
+    while bit < n:
+        value = value + lax.ppermute(value, "aug", [(i, i ^ bit) for i in range(n)])
+        bit *= 2
+    return value
 
 
 def per_device(ring, hidden, output_grad, down_weight, first_moment, second_moment, noise):
@@ -89,12 +134,14 @@
     images_all = images_here * groups
     clip = clip_ratio * math.sqrt(patches * width * model_width / views)
     local_rows = images_here * patches
-    swapped = lax.all_to_all(
-        hidden.reshape(local_rows, width), "aug", split_axis=1, concat_axis=0, tiled=True
-    )
+    h_rows = hidden.reshape(local_rows, width)
+    grad_rows = output_grad.reshape(local_rows, model_width)
+    if views == 4:
+        swapped, every = exchange_four(h_rows, grad_rows)
+    else:
+        swapped = lax.all_to_all(h_rows, "aug", split_axis=1, concat_axis=0, tiled=True)
+        every = lax.all_gather(grad_rows, "aug", axis=0, tiled=True)
     slice_width = swapped.shape[1]
-    grad_rows = output_grad.reshape(local_rows, model_width)
-    every = lax.all_gather(grad_rows, "aug", axis=0, tiled=True)
     h_four = swapped.reshape(views, images_here, patches, slice_width)
     g_four = every.reshape(views, images_here, patches, model_width)
     summed = jnp.einsum("vipf,vipd->ifd", h_four, g_four, preferred_element_type=jnp.float32)
@@ -102,17 +149,19 @@
     hidden_grad = back_rows.astype(jnp.bfloat16).reshape(views, images_here, patches, slice_width)
     grads = summed / views
     partial_value = jnp.sum(grads * grads, axis=(1, 2))
-    squares = lax.psum(partial_value, "aug")
+    squares = butterfly_sum(partial_value, views)
     image_norms = jnp.sqrt(squares)
     factor = clip / jnp.maximum(image_norms, clip)
     owned_rows = slice_width // groups
     half = owned_rows // 2
 
-    def parts(block):
-        start = block * owned_rows
-        rows = lax.dynamic_slice_in_dim(grads, start, owned_rows, axis=1)
-        clipped = jnp.sum(factor[:, None, None] * rows, axis=0)
-        return clipped[:half], clipped[half:]
+    def parts(block, which, after):
+        source = grads
+        if after is not None:
+            _, source = lax.optimization_barrier((after, grads))
+        start = block * owned_rows + which * half
+        rows = lax.dynamic_slice_in_dim(source, start, half, axis=1)
+        return jnp.sum(factor[:, None, None] * rows, axis=0)
 
     owned = ring_reduce_scatter(parts, ring, None)
     clipped_mean = owned / images_all

time: 146 us -> 150 us (1.027)
  waiting for transfers between devices: 59.5 us -> 72.2 us
  between operations: 34.3 us -> 22 us
  local copies, waits for them, and re-layouts: 6.22 us -> 12.9 us
  blocking collectives: 6.36 us -> 0 us
  starting transfers between devices: 19.4 us -> 22.3 us
    ppermute x0 -> x5, waiting for transfers between devices: none -> 23.8 us  [the longest x1 21.8 us: exchange_four(): lax.ppermute(jnp.concatenate([cols(a ^ 2), cols(a ^ 3), grad_rows], axis=...]
    ppermute x7, starting transfers between devices: 3.27 us -> 13.7 us  [ring_reduce_scatter(): acc_l = lax.ppermute(send_l, 'dp', left)]
    ppermute x7, starting transfers between devices: 11.6 us -> 2.04 us  [ring_reduce_scatter(): acc_r = lax.ppermute(send_r, 'dp', right)]
    dynamic_update_slice x0 -> x6, local copies, waits for them, and re-layouts: none -> 7.2 us  [the longest x4 5.11 us: exchange_four(): g_all = lax.dynamic_update_slice_in_dim(g_all, g_from[m], at, axis=0)]
    mul x1, other arithmetic: 7.67 us -> 0.95 us  [parts(): return jnp.sum(factor[:, None, None] * rows, axis=0)]
    ppermute x0 -> x5, starting transfers between devices: none -> 6.62 us  [the longest x2 3.1 us: butterfly_sum(): value = value + lax.ppermute(value, 'aug', [(i, i ^ bit) for i in range(n)])]
    psum x1 -> x0, blocking collectives: 6.36 us -> none  [per_device(): squares = lax.psum(partial_value, 'aug')]
    add x13 -> x14, other arithmetic: 0.68 us -> 6.97 us  [the longest x6 3.57 us: ring_reduce_scatter(): send_l = acc_l + parts(blk_l, 1, acc_l)]
  transfers between devices with their start and end apart: 16 -> 19, of which waited for: 15 -> 15; matrix products, arithmetic and copies ran while one was open for 6% -> 11% of each run, Pallas kernels for 0% -> 0%
where the time goes in v2:
time: 150 us; the launch traced here: 149 us
  waiting for transfers between devices  72.2 us (48%)
  starting transfers between devices  22.3 us (15%)
  between operations  22 us (15%)
  local copies, waits for them, and re-layouts  12.9 us (9%)
  other arithmetic  10.9 us (7%)
  matrix products  8.81 us (6%)
    ppermute x7, waiting for transfers between devices, ring_reduce_scatter(): acc_r = lax.ppermute(send_r, 'dp', right)  45.5 us
    ppermute x1, waiting for transfers between devices, exchange_four(): lax.ppermute(jnp.concatenate([cols(a ^ 2), cols(a ^ 3), grad_rows], axis=...  21.8 us
    ppermute x7, starting transfers between devices, ring_reduce_scatter(): acc_l = lax.ppermute(send_l, 'dp', left)  13.7 us
    dynamic_update_slice x4, local copies, waits for them, and re-layouts, exchange_four(): g_all = lax.dynamic_update_slice_in_dim(g_all, g_from[m], at, axis=0)  5.11 us
    dot_general x1, matrix products, per_device(): jnp.einsum('vipf,vipd->ifd', h_four, g_four, preferred_element_type=jnp.f...  4.54 us
    dot_general x1, matrix products, project_back(): lax.dot_general(rows, down_weight, (((1,), (1,)), ((), ())), preferred_el...  4.27 us
    add x6, other arithmetic, ring_reduce_scatter(): send_l = acc_l + parts(blk_l, 1, acc_l)  3.57 us
    add x6, other arithmetic, ring_reduce_scatter(): send_r = acc_r + parts(blk_r, 0, acc_r)  3.3 us
  transfers between devices with their start and end apart: 19, of which 15 were waited for; matrix products, arithmetic and copies ran while one was open for 11% of the time, Pallas kernels for 0%

profile of v2, /device:TPU:0, one launch (start us, length us, event | category | flops | bytes accessed | tf_op | source)
XLA Modules:
  0.0 149.1 jit_solution(11089795722166944659)
XLA Ops:
  0.6 0.0 copy-start
  0.7 0.0 copy-start.3
  0.7 2.1 %dynamic-slice_bitcast_fusion.1 = (bf16[128,1280]{1,0:T(8,128)(2,1)S(1)}, bf16[128,1280]{1,0:T(8,128)(2,1)}, bf16[128,1280]{1,0:T(8,128)(2,1)S(1)}) fusion(bf16[1,1,128,5120]{3,2,1,0:T(8,128)(2,1)} %param.8, s32[]{:T(128)S(6)} %select_n.184, s32[]{:T(128)S(6)} %select_n.182, s32[]{:T(128)S(6)} %select_n.185), kind=kLoop, calls=%fused_computation.35 | loop fusion | bytes 1966092 | tf_op jit(solution)/shard_map/dynamic_slice | solution.py:91
  2.8 0.1 pad_maximum_fusion.1
  2.9 3.0 %collective-permute-start.1 = (bf16[128,3840]{1,0:T(8,128)(2,1)S(1)}, bf16[128,3840]{1,0:T(8,128)(2,1)S(1)}, u32[]{:S(2)}, u32[]{:S(2)}) collective-permute-start(bf16[128,3840]{1,0:T(8,128)(2,1)S(1)} %pad_maximum_fusion.1), channel_id=1, source_target_pairs={{0,16},{8,24},{16,0},{24,8},{1,17},{9,25},{17,1},{25,9},{2,18},{10... | collective-permute-start | bytes 2949128 | tf_op jit(solution)/shard_map/ppermute | solution.py:95
  5.9 21.8 %collective-permute-done.1 = bf16[128,3840]{1,0:T(8,128)(2,1)S(1)} collective-permute-done((bf16[128,3840]{1,0:T(8,128)(2,1)S(1)}, bf16[128,3840]{1,0:T(8,128)(2,1)S(1)}, u32[]{:S(2)}, u32[]{:S(2)}) %collective-permute-start.1) | collective-permute-done | bytes 983072 | tf_op jit(solution)/shard_map/ppermute | solution.py:95
  27.6 0.9 copy-done.5
  28.6 1.0 pad_maximum_fusion
  29.6 0.0 collective-permute-start.2
  29.6 0.5 collective-permute-start
  30.1 1.2 broadcast.30.clone
  31.3 0.8 constant_dynamic-update-slice_fusion
  32.1 0.6 dynamic_slice.117
  42.0 0.7 fusion.3
  44.1 0.1 broadcast.30.clone.1
  44.2 1.1 bitcast_dynamic-update-slice_fusion
  45.3 0.0 collective-permute-done
  45.3 1.0 constant_dynamic-update-slice_fusion.1
  46.3 0.0 collective-permute-done.2
  46.3 1.7 %slice_dynamic-update-slice_fusion.2 = bf16[512,1280]{1,0:T(8,128)(2,1)} fusion(bf16[512,1280]{1,0:T(8,128)(2,1)} %constant_dynamic-update-slice_fusion, s32[]{:T(128)S(6)} %select_n.183, bf16[128,3840]{1,0:T(8,128)(2,1)} %collective-permute-done.2), kind=kLoop, calls=%fused_computation.30 | loop fusion | bytes 655364 | tf_op jit(solution)/shard_map/dynamic_update_slice | solution.py:113
  48.0 0.8 slice_dynamic-update-slice_fusion.1
  48.8 1.9 %slice_dynamic-update-slice_fusion = (bf16[512,1280]{1,0:T(8,128)(2,1)}, bf16[512,1280]{1,0:T(8,128)(2,1)S(1)}) fusion(bf16[512,1280]{1,0:T(8,128)(2,1)} %get-tuple-element.57, s32[]{:T(128)S(6)} %select_n.187, bf16[128,3840]{1,0:T(8,128)(2,1)} %collective-permute-done.2, bf16[512,1280]{1,0:T(8,128)(2,1)S(1)} %get-tuple-element.58), kind=kLoop, calls=%fused_computation.28 | loop fusion | bytes 1310724 | tf_op jit(solution)/shard_map/dynamic_update_slice | solution.py:113
  50.6 4.5 %multiply_reduce_fusion = (f32[]{:T(128)}, f32[1280,1280]{1,0:T(8,128)S(1)}) fusion(bf16[4,128,1280]{2,1,0:T(8,128)(2,1)S(1)} %bitcast.105, bf16[4,128,1280]{2,1,0:T(8,128)(2,1)} %bitcast.6), kind=kOutput, calls=%fused_computation.2 | convolution fusion | flops 1682636800 | bytes 9175044 | tf_op jit(solution)/shard_map/vipf,vipd->ifd/dot_general | solution.py:147
  55.2 0.0 collective-permute-start.3
  55.2 1.4 collective-permute-done.3
  57.8 3.1 %collective-permute-start.4 = (f32[1]{0:T(128)}, f32[1]{0:T(128)}, u32[]{:S(2)}, u32[]{:S(2)}) collective-permute-start(f32[1]{0:T(128)} %add.403), channel_id=1, source_target_pairs={{0,16},{8,24},{16,0},{24,8},{1,17},{9,25},{17,1},{25,9},{2,18},{10... | collective-permute-start | bytes 20 | tf_op jit(solution)/shard_map/ppermute | solution.py:122
  60.9 0.6 collective-permute-done.4
  62.2 1.0 dynamic-slice_multiply_fusion.1
  63.1 1.8 %collective-permute-start.12 = (f32[80,1280]{1,0:T(8,128)}, f32[80,1280]{1,0:T(8,128)}, u32[]{:S(2)}, u32[]{:S(2)}) collective-permute-start(f32[80,1280]{1,0:T(8,128)} %get-tuple-element.51), channel_id=1, source_target_pairs={{0,2},{1,0},{3,1},{5,3},{7,5},{6,7},{4,6},{2,4},{8,10},{9,8},{11,9... | collective-permute-start | bytes 1228808 | tf_op jit(solution)/shard_map/ppermute | solution.py:79
  72.4 0.3 collective-permute-start.5
  72.7 1.1 collective-permute-done.12
  73.7 1.3 bitcast_add_fusion.6
  75.1 1.8 %collective-permute-start.13 = (f32[80,1280]{1,0:T(8,128)S(1)}, f32[80,1280]{1,0:T(8,128)S(1)}, u32[]{:S(2)}, u32[]{:S(2)}) collective-permute-start(f32[80,1280]{1,0:T(8,128)S(1)} %bitcast_add_fusion.6), channel_id=1, source_target_pairs={{0,2},{1,0},{3,1},{5,3},{7,5},{6,7},{4,6},{2,4},{8,10},{9,8},{11,9... | collective-permute-start | bytes 1228808 | tf_op jit(solution)/shard_map/ppermute | solution.py:79
  76.9 5.7 %collective-permute-done.5 = f32[80,1280]{1,0:T(8,128)S(1)} collective-permute-done((f32[80,1280]{1,0:T(8,128)}, f32[80,1280]{1,0:T(8,128)S(1)}, u32[]{:S(2)}, u32[]{:S(2)}) %collective-permute-start.5) | collective-permute-done | bytes 409632 | tf_op jit(solution)/shard_map/ppermute | solution.py:78
  82.7 1.1 bitcast_add_fusion.13
  83.7 0.3 collective-permute-start.6
  84.0 0.4 collective-permute-done.13
  84.5 1.1 bitcast_add_fusion.5
  85.5 1.8 %collective-permute-start.14 = (f32[80,1280]{1,0:T(8,128)S(1)}, f32[80,1280]{1,0:T(8,128)S(1)}, u32[]{:S(2)}, u32[]{:S(2)}) collective-permute-start(f32[80,1280]{1,0:T(8,128)S(1)} %bitcast_add_fusion.5), channel_id=1, source_target_pairs={{0,2},{1,0},{3,1},{5,3},{7,5},{6,7},{4,6},{2,4},{8,10},{9,8},{11,9... | collective-permute-start | bytes 1228808 | tf_op jit(solution)/shard_map/ppermute | solution.py:79
  87.3 5.5 %collective-permute-done.6 = f32[80,1280]{1,0:T(8,128)S(1)} collective-permute-done((f32[80,1280]{1,0:T(8,128)S(1)}, f32[80,1280]{1,0:T(8,128)S(1)}, u32[]{:S(2)}, u32[]{:S(2)}) %collective-permute-start.6) | collective-permute-done | bytes 409632 | tf_op jit(solution)/shard_map/ppermute | solution.py:78
  92.8 1.1 bitcast_add_fusion.12
  93.9 0.4 collective-permute-start.7
  94.3 1.1 bitcast_add_fusion.4
  95.4 1.7 %collective-permute-start.15 = (f32[80,1280]{1,0:T(8,128)S(1)}, f32[80,1280]{1,0:T(8,128)S(1)}, u32[]{:S(2)}, u32[]{:S(2)}) collective-permute-start(f32[80,1280]{1,0:T(8,128)S(1)} %bitcast_add_fusion.4), channel_id=1, source_target_pairs={{0,2},{1,0},{3,1},{5,3},{7,5},{6,7},{4,6},{2,4},{8,10},{9,8},{11,9... | collective-permute-start | bytes 1228808 | tf_op jit(solution)/shard_map/ppermute | solution.py:79
  97.1 5.4 %collective-permute-done.7 = f32[80,1280]{1,0:T(8,128)S(1)} collective-permute-done((f32[80,1280]{1,0:T(8,128)S(1)}, f32[80,1280]{1,0:T(8,128)S(1)}, u32[]{:S(2)}, u32[]{:S(2)}) %collective-permute-start.7) | collective-permute-done | bytes 409632 | tf_op jit(solution)/shard_map/ppermute | solution.py:78
  102.4 1.1 bitcast_add_fusion.11
  103.5 0.4 collective-permute-start.8
  103.9 0.8 collective-permute-done.15
  104.8 1.9 %collective-permute-start.16 = (f32[80,1280]{1,0:T(8,128)S(1)}, f32[80,1280]{1,0:T(8,128)S(1)}, u32[]{:S(2)}, u32[]{:S(2)}) collective-permute-start(f32[80,1280]{1,0:T(8,128)S(1)} %bitcast_add_fusion.3), channel_id=1, source_target_pairs={{0,2},{1,0},{3,1},{5,3},{7,5},{6,7},{4,6},{2,4},{8,10},{9,8},{11,9... | collective-permute-start | bytes 1228808 | tf_op jit(solution)/shard_map/ppermute | solution.py:79
  106.6 7.4 %collective-permute-done.8 = f32[80,1280]{1,0:T(8,128)S(1)} collective-permute-done((f32[80,1280]{1,0:T(8,128)S(1)}, f32[80,1280]{1,0:T(8,128)S(1)}, u32[]{:S(2)}, u32[]{:S(2)}) %collective-permute-start.8) | collective-permute-done | bytes 409632 | tf_op jit(solution)/shard_map/ppermute | solution.py:78
  114.0 0.3 collective-permute-start.9
  114.4 0.5 collective-permute-done.16
  114.9 2.0 %collective-permute-start.17 = (f32[80,1280]{1,0:T(8,128)S(1)}, f32[80,1280]{1,0:T(8,128)S(1)}, u32[]{:S(2)}, u32[]{:S(2)}) collective-permute-start(f32[80,1280]{1,0:T(8,128)S(1)} %bitcast_add_fusion.2), channel_id=1, source_target_pairs={{0,2},{1,0},{3,1},{5,3},{7,5},{6,7},{4,6},{2,4},{8,10},{9,8},{11,9... | collective-permute-start | bytes 1228808 | tf_op jit(solution)/shard_map/ppermute | solution.py:79
  117.0 8.7 %collective-permute-done.9 = f32[80,1280]{1,0:T(8,128)S(1)} collective-permute-done((f32[80,1280]{1,0:T(8,128)S(1)}, f32[80,1280]{1,0:T(8,128)S(1)}, u32[]{:S(2)}, u32[]{:S(2)}) %collective-permute-start.9) | collective-permute-done | bytes 409632 | tf_op jit(solution)/shard_map/ppermute | solution.py:78
  125.8 0.1 collective-permute-start.10
  125.8 0.1 collective-permute-done.17
  126.0 2.5 %collective-permute-start.18 = (f32[80,1280]{1,0:T(8,128)S(1)}, f32[80,1280]{1,0:T(8,128)S(1)}, u32[]{:S(2)}, u32[]{:S(2)}) collective-permute-start(f32[80,1280]{1,0:T(8,128)S(1)} %bitcast_add_fusion.1), channel_id=1, source_target_pairs={{0,2},{1,0},{3,1},{5,3},{7,5},{6,7},{4,6},{2,4},{8,10},{9,8},{11,9... | collective-permute-start | bytes 1228808 | tf_op jit(solution)/shard_map/ppermute | solution.py:79
  128.5 9.3 %collective-permute-done.10 = f32[80,1280]{1,0:T(8,128)S(1)} collective-permute-done((f32[80,1280]{1,0:T(8,128)S(1)}, f32[80,1280]{1,0:T(8,128)S(1)}, u32[]{:S(2)}, u32[]{:S(2)}) %collective-permute-start.10) | collective-permute-done | bytes 409632 | tf_op jit(solution)/shard_map/ppermute | solution.py:78
  137.9 0.2 collective-permute-start.11
  138.1 4.3 %convolution_convert_fusion = bf16[512,1280]{1,0:T(8,128)(2,1)} fusion(bf16[512,1280]{1,0:T(8,128)(2,1)} %get-tuple-element.55, bf16[1280,1280]{1,0:T(8,128)(2,1)S(1)} %copy-done), kind=kOutput, calls=%fused_computation.3 | convolution fusion | flops 1678376960 | bytes 5898240 | tf_op jit(solution)/shard_map/dot_general | solution.py:17
  142.4 0.0 collective-permute-done.18
  142.4 3.5 %collective-permute-done.11 = f32[80,1280]{1,0:T(8,128)S(1)} collective-permute-done((f32[80,1280]{1,0:T(8,128)S(1)}, f32[80,1280]{1,0:T(8,128)S(1)}, u32[]{:S(2)}, u32[]{:S(2)}) %collective-permute-start.11) | collective-permute-done | bytes 409632 | tf_op jit(solution)/shard_map/ppermute | solution.py:78
  146.0 0.1 bitcast_add_fusion.7
  146.0 1.9 %add_divide_fusion = (f32[160,1280]{1,0:T(8,128)}, f32[160,1280]{1,0:T(8,128)}, f32[160,1280]{1,0:T(8,128)}, f32[160,1280]{1,0:T(8,128)}) fusion(f32[160,1280]{1,0:T(8,128)S(1)} %copy-done.7, f32[160,1280]{1,0:T(8,128)S(1)} %copy-done.8, f32[160,1280]{1,0:T(8,128)S(1)} %copy-done.9, f32[80,1280]{1,0:T(8,128)S(1)} %bitcast_add_fusion, ...), kind=kLoop, calls=%fused_computation.9 | loop fusion | flops 3072000 | bytes 6553600 | tf_op jit(solution)/shard_map/div | solution.py:172
  (30 shorter events, 0.4 us)
Async XLA Ops:
  0.6 137.5 %copy-start = (bf16[1280,1280]{1,0:T(8,128)(2,1)S(1)}, bf16[1280,1280]{1,0:T(8,128)(2,1)}, u32[]{:S(2)}) copy-start(bf16[1280,1280]{1,0:T(8,128)(2,1)} %param.10) | copy-start | bytes 9830404
  0.7 2.1 %copy-start.3 = (bf16[1,1,128,1280]{3,2,1,0:T(8,128)(2,1)S(1)}, bf16[1,1,128,1280]{3,2,1,0:T(8,128)(2,1)}, u32[]{:S(2)}) copy-start(bf16[1,1,128,1280]{3,2,1,0:T(8,128)(2,1)} %param.9) | copy-start | bytes 983044
  2.9 24.8 %collective-permute-start.1 = (bf16[128,3840]{1,0:T(8,128)(2,1)S(1)}, bf16[128,3840]{1,0:T(8,128)(2,1)S(1)}, u32[]{:S(2)}, u32[]{:S(2)}) collective-permute-start(bf16[128,3840]{1,0:T(8,128)(2,1)S(1)} %pad_maximum_fusion.1), channel_id=1, source_target_pairs={{0,16},{8,24},{16,0},{24,8},{1,17},{9,25},{17,1},{25,9},{2,18},{10... | collective-permute-start | bytes 2949128 | tf_op jit(solution)/shard_map/ppermute | solution.py:95
  27.6 0.9 copy-start.5
  29.6 2.4 %copy-start.11 = (s32[8]{0:T(128)S(1)}, s32[8]{0:T(128)}, u32[]{:S(2)}) copy-start(s32[8]{0:T(128)} %constant.223.clone) | copy-start | bytes 100
  29.6 12.4 %copy-start.10 = (s32[8]{0:T(128)S(1)}, s32[8]{0:T(128)}, u32[]{:S(2)}) copy-start(s32[8]{0:T(128)} %constant.222.clone) | copy-start | bytes 100
  29.6 16.6 %collective-permute-start.2 = (bf16[128,3840]{1,0:T(8,128)(2,1)}, bf16[128,3840]{1,0:T(8,128)(2,1)}, u32[]{:S(2)}, u32[]{:S(2)}) collective-permute-start(bf16[128,3840]{1,0:T(8,128)(2,1)} %pad_maximum_fusion), channel_id=1, source_target_pairs={{0,8},{8,0},{16,24},{24,16},{1,9},{9,1},{17,25},{25,17},{2,10},{10... | collective-permute-start | bytes 2949128 | tf_op jit(solution)/shard_map/ppermute | solution.py:100
  29.6 15.6 %collective-permute-start = (bf16[128,1280]{1,0:T(8,128)(2,1)}, bf16[128,1280]{1,0:T(8,128)(2,1)}, u32[]{:S(2)}, u32[]{:S(2)}) collective-permute-start(bf16[128,1280]{1,0:T(8,128)(2,1)} %get-tuple-element.53), channel_id=1, source_target_pairs={{0,8},{8,0},{16,24},{24,16},{1,9},{9,1},{17,25},{25,17},{2,10},{10... | collective-permute-start | bytes 983048 | tf_op jit(solution)/shard_map/ppermute | solution.py:98
  30.1 1.2 copy-start.4
  44.2 3.8 %copy-start.6 = (bf16[128,3840]{1,0:T(8,128)(2,1)S(1)}, bf16[128,3840]{1,0:T(8,128)(2,1)}, u32[]{:S(2)}) copy-start(bf16[128,3840]{1,0:T(8,128)(2,1)} %copy-done.5) | copy-start | bytes 2949124
  55.2 7.0 %copy-start.1 = (f32[1280,1280]{1,0:T(8,128)}, f32[1280,1280]{1,0:T(8,128)S(1)}, u32[]{:S(2)}) copy-start(f32[1280,1280]{1,0:T(8,128)S(1)} %get-tuple-element.74) | copy-start | bytes 19660804
  55.2 1.4 collective-permute-start.3
  57.8 3.7 %collective-permute-start.4 = (f32[1]{0:T(128)}, f32[1]{0:T(128)}, u32[]{:S(2)}, u32[]{:S(2)}) collective-permute-start(f32[1]{0:T(128)} %add.403), channel_id=1, source_target_pairs={{0,16},{8,24},{16,0},{24,8},{1,17},{9,25},{17,1},{25,9},{2,18},{10... | collective-permute-start | bytes 20 | tf_op jit(solution)/shard_map/ppermute | solution.py:122
  63.1 10.6 %collective-permute-start.12 = (f32[80,1280]{1,0:T(8,128)}, f32[80,1280]{1,0:T(8,128)}, u32[]{:S(2)}, u32[]{:S(2)}) collective-permute-start(f32[80,1280]{1,0:T(8,128)} %get-tuple-element.51), channel_id=1, source_target_pairs={{0,2},{1,0},{3,1},{5,3},{7,5},{6,7},{4,6},{2,4},{8,10},{9,8},{11,9... | collective-permute-start | bytes 1228808 | tf_op jit(solution)/shard_map/ppermute | solution.py:79
  72.4 10.2 %collective-permute-start.5 = (f32[80,1280]{1,0:T(8,128)}, f32[80,1280]{1,0:T(8,128)S(1)}, u32[]{:S(2)}, u32[]{:S(2)}) collective-permute-start(f32[80,1280]{1,0:T(8,128)} %get-tuple-element.50), channel_id=1, source_target_pairs={{0,1},{1,3},{3,5},{5,7},{7,6},{6,4},{4,2},{2,0},{8,9},{9,11},{11,1... | collective-permute-start | bytes 1228808 | tf_op jit(solution)/shard_map/ppermute | solution.py:78
  73.7 31.0 %copy-start.2 = (f32[1280,1280]{1,0:T(8,128)S(1)}, f32[1280,1280]{1,0:T(8,128)}, u32[]{:S(2)}) copy-start(f32[1280,1280]{1,0:T(8,128)} %copy-done.1) | copy-start | bytes 19660804
  75.1 9.4 %collective-permute-start.13 = (f32[80,1280]{1,0:T(8,128)S(1)}, f32[80,1280]{1,0:T(8,128)S(1)}, u32[]{:S(2)}, u32[]{:S(2)}) collective-permute-start(f32[80,1280]{1,0:T(8,128)S(1)} %bitcast_add_fusion.6), channel_id=1, source_target_pairs={{0,2},{1,0},{3,1},{5,3},{7,5},{6,7},{4,6},{2,4},{8,10},{9,8},{11,9... | collective-permute-start | bytes 1228808 | tf_op jit(solution)/shard_map/ppermute | solution.py:79
  83.7 9.1 %collective-permute-start.6 = (f32[80,1280]{1,0:T(8,128)S(1)}, f32[80,1280]{1,0:T(8,128)S(1)}, u32[]{:S(2)}, u32[]{:S(2)}) collective-permute-start(f32[80,1280]{1,0:T(8,128)S(1)} %bitcast_add_fusion.13), channel_id=1, source_target_pairs={{0,1},{1,3},{3,5},{5,7},{7,6},{6,4},{4,2},{2,0},{8,9},{9,11},{11,1... | collective-permute-start | bytes 1228808 | tf_op jit(solution)/shard_map/ppermute | solution.py:78
  85.5 8.8 %collective-permute-start.14 = (f32[80,1280]{1,0:T(8,128)S(1)}, f32[80,1280]{1,0:T(8,128)S(1)}, u32[]{:S(2)}, u32[]{:S(2)}) collective-permute-start(f32[80,1280]{1,0:T(8,128)S(1)} %bitcast_add_fusion.5), channel_id=1, source_target_pairs={{0,2},{1,0},{3,1},{5,3},{7,5},{6,7},{4,6},{2,4},{8,10},{9,8},{11,9... | collective-permute-start | bytes 1228808 | tf_op jit(solution)/shard_map/ppermute | solution.py:79
  93.9 8.6 %collective-permute-start.7 = (f32[80,1280]{1,0:T(8,128)S(1)}, f32[80,1280]{1,0:T(8,128)S(1)}, u32[]{:S(2)}, u32[]{:S(2)}) collective-permute-start(f32[80,1280]{1,0:T(8,128)S(1)} %bitcast_add_fusion.12), channel_id=1, source_target_pairs={{0,1},{1,3},{3,5},{5,7},{7,6},{6,4},{4,2},{2,0},{8,9},{9,11},{11,1... | collective-permute-start | bytes 1228808 | tf_op jit(solution)/shard_map/ppermute | solution.py:78
  95.4 9.4 %collective-permute-start.15 = (f32[80,1280]{1,0:T(8,128)S(1)}, f32[80,1280]{1,0:T(8,128)S(1)}, u32[]{:S(2)}, u32[]{:S(2)}) collective-permute-start(f32[80,1280]{1,0:T(8,128)S(1)} %bitcast_add_fusion.4), channel_id=1, source_target_pairs={{0,2},{1,0},{3,1},{5,3},{7,5},{6,7},{4,6},{2,4},{8,10},{9,8},{11,9... | collective-permute-start | bytes 1228808 | tf_op jit(solution)/shard_map/ppermute | solution.py:79
  103.5 10.5 %collective-permute-start.8 = (f32[80,1280]{1,0:T(8,128)S(1)}, f32[80,1280]{1,0:T(8,128)S(1)}, u32[]{:S(2)}, u32[]{:S(2)}) collective-permute-start(f32[80,1280]{1,0:T(8,128)S(1)} %bitcast_add_fusion.11), channel_id=1, source_target_pairs={{0,1},{1,3},{3,5},{5,7},{7,6},{6,4},{4,2},{2,0},{8,9},{9,11},{11,1... | collective-permute-start | bytes 1228808 | tf_op jit(solution)/shard_map/ppermute | solution.py:78
  104.8 10.1 %collective-permute-start.16 = (f32[80,1280]{1,0:T(8,128)S(1)}, f32[80,1280]{1,0:T(8,128)S(1)}, u32[]{:S(2)}, u32[]{:S(2)}) collective-permute-start(f32[80,1280]{1,0:T(8,128)S(1)} %bitcast_add_fusion.3), channel_id=1, source_target_pairs={{0,2},{1,0},{3,1},{5,3},{7,5},{6,7},{4,6},{2,4},{8,10},{9,8},{11,9... | collective-permute-start | bytes 1228808 | tf_op jit(solution)/shard_map/ppermute | solution.py:79
  114.0 11.7 %collective-permute-start.9 = (f32[80,1280]{1,0:T(8,128)S(1)}, f32[80,1280]{1,0:T(8,128)S(1)}, u32[]{:S(2)}, u32[]{:S(2)}) collective-permute-start(f32[80,1280]{1,0:T(8,128)S(1)} %bitcast_add_fusion.10), channel_id=1, source_target_pairs={{0,1},{1,3},{3,5},{5,7},{7,6},{6,4},{4,2},{2,0},{8,9},{9,11},{11,1... | collective-permute-start | bytes 1228808 | tf_op jit(solution)/shard_map/ppermute | solution.py:78
  114.9 11.0 %collective-permute-start.17 = (f32[80,1280]{1,0:T(8,128)S(1)}, f32[80,1280]{1,0:T(8,128)S(1)}, u32[]{:S(2)}, u32[]{:S(2)}) collective-permute-start(f32[80,1280]{1,0:T(8,128)S(1)} %bitcast_add_fusion.2), channel_id=1, source_target_pairs={{0,2},{1,0},{3,1},{5,3},{7,5},{6,7},{4,6},{2,4},{8,10},{9,8},{11,9... | collective-permute-start | bytes 1228808 | tf_op jit(solution)/shard_map/ppermute | solution.py:79
  125.8 12.1 %collective-permute-start.10 = (f32[80,1280]{1,0:T(8,128)S(1)}, f32[80,1280]{1,0:T(8,128)S(1)}, u32[]{:S(2)}, u32[]{:S(2)}) collective-permute-start(f32[80,1280]{1,0:T(8,128)S(1)} %bitcast_add_fusion.9), channel_id=1, source_target_pairs={{0,1},{1,3},{3,5},{5,7},{7,6},{6,4},{4,2},{2,0},{8,9},{9,11},{11,1... | collective-permute-start | bytes 1228808 | tf_op jit(solution)/shard_map/ppermute | solution.py:78
  126.0 16.4 %collective-permute-start.18 = (f32[80,1280]{1,0:T(8,128)S(1)}, f32[80,1280]{1,0:T(8,128)S(1)}, u32[]{:S(2)}, u32[]{:S(2)}) collective-permute-start(f32[80,1280]{1,0:T(8,128)S(1)} %bitcast_add_fusion.1), channel_id=1, source_target_pairs={{0,2},{1,0},{3,1},{5,3},{7,5},{6,7},{4,6},{2,4},{8,10},{9,8},{11,9... | collective-permute-start | bytes 1228808 | tf_op jit(solution)/shard_map/ppermute | solution.py:79
  137.9 8.0 %collective-permute-start.11 = (f32[80,1280]{1,0:T(8,128)S(1)}, f32[80,1280]{1,0:T(8,128)S(1)}, u32[]{:S(2)}, u32[]{:S(2)}) collective-permute-start(f32[80,1280]{1,0:T(8,128)S(1)} %bitcast_add_fusion.8), channel_id=1, source_target_pairs={{0,1},{1,3},{3,5},{5,7},{7,6},{6,4},{4,2},{2,0},{8,9},{9,11},{11,1... | collective-permute-start | bytes 1228808 | tf_op jit(solution)/shard_map/ppermute | solution.py:78
  142.4 3.6 %copy-start.7 = (f32[160,1280]{1,0:T(8,128)S(1)}, f32[160,1280]{1,0:T(8,128)}, u32[]{:S(2)}) copy-start(f32[160,1280]{1,0:T(8,128)} %param.13) | copy-start | bytes 2457604
  142.4 3.6 %copy-start.8 = (f32[160,1280]{1,0:T(8,128)S(1)}, f32[160,1280]{1,0:T(8,128)}, u32[]{:S(2)}) copy-start(f32[160,1280]{1,0:T(8,128)} %param.12) | copy-start | bytes 2457604
  142.4 3.6 %copy-start.9 = (f32[160,1280]{1,0:T(8,128)S(1)}, f32[160,1280]{1,0:T(8,128)}, u32[]{:S(2)}) copy-start(f32[160,1280]{1,0:T(8,128)} %param.11) | copy-start | bytes 2457604

commit v3 on v2

--- a/solution.py
+++ b/solution.py
@@ -64,28 +64,28 @@
     pos = jnp.array(pos_of, jnp.int32)[me]
     right = [(ring[k], ring[(k + 1) % n]) for k in range(n)]
     left = [(ring[k], ring[(k - 1) % n]) for k in range(n)]
+    def block(s, step):
+        return ring_arr[(pos - 1 - s) % n] if step < 0 else ring_arr[(pos + 1 + s) % n]
+
+    own_r = parts(block(0, -1), 0, None)
+    own_l = parts(block(0, 1), 1, None)
     acc_r = None
     acc_l = None
     for s in range(n - 1):
-        blk_r = ring_arr[(pos - 1 - s) % n]
-        blk_l = ring_arr[(pos + 1 + s) % n]
-        if acc_r is None:
-            send_r = parts(blk_r, 0, None)
-            send_l = parts(blk_l, 1, None)
-        else:
-            send_r = acc_r + parts(blk_r, 0, acc_r)
-            send_l = acc_l + parts(blk_l, 1, acc_l)
+        send_r = own_r if acc_r is None else acc_r + own_r
+        send_l = own_l if acc_l is None else acc_l + own_l
         acc_r = lax.ppermute(send_r, "dp", right)
         acc_l = lax.ppermute(send_l, "dp", left)
-    return jnp.concatenate(
-        [acc_r + parts(me, 0, acc_r), acc_l + parts(me, 1, acc_l)], axis=0
-    )
+        own_r = parts(block(s + 1, -1), 0, send_r)
+        own_l = parts(block(s + 1, 1), 1, send_l)
+    return jnp.concatenate([acc_r + own_r, acc_l + own_l], axis=0)
 
 
 def exchange_four(h_rows, grad_rows):
     a = lax.axis_index("aug")
     rows = h_rows.shape[0]
     sw = h_rows.shape[1] // 4
+    d = grad_rows.shape[1]
 
     def cols(b):
         return lax.dynamic_slice_in_dim(h_rows, b * sw, sw, axis=1)
@@ -95,23 +95,14 @@
     far = lax.ppermute(
         jnp.concatenate([cols(a ^ 2), cols(a ^ 3), grad_rows], axis=1), "aug", over_x
     )
-    near = lax.ppermute(cols(a ^ 1), "aug", over_core)
-    far_mine = far[:, :sw]
-    relay = lax.ppermute(
-        jnp.concatenate([far[:, sw:2 * sw], far[:, 2 * sw:], grad_rows], axis=1),
-        "aug",
-        over_core,
-    )
-    d = grad_rows.shape[1]
-    h_from = {0: cols(a), 1: near, 2: far_mine, 3: relay[:, :sw]}
-    g_from = {0: grad_rows, 1: relay[:, sw + d:], 2: far[:, 2 * sw:], 3: relay[:, sw:sw + d]}
-    h_all = jnp.zeros((4 * rows, sw), h_rows.dtype)
-    g_all = jnp.zeros((4 * rows, grad_rows.shape[1]), grad_rows.dtype)
-    for m in range(4):
-        at = (a ^ m) * rows
-        h_all = lax.dynamic_update_slice_in_dim(h_all, h_from[m], at, axis=0)
-        g_all = lax.dynamic_update_slice_in_dim(g_all, g_from[m], at, axis=0)
-    return h_all, g_all
+    near = lax.ppermute(jnp.concatenate([cols(a ^ 1), grad_rows], axis=1), "aug", over_core)
+    relay = lax.ppermute(far[:, sw:], "aug", over_core)
+    return [
+        (a * rows, cols(a), grad_rows),
+        ((a ^ 1) * rows, near[:, :sw], near[:, sw:]),
+        ((a ^ 2) * rows, far[:, :sw], far[:, 2 * sw:]),
+        ((a ^ 3) * rows, relay[:, :sw], relay[:, sw:]),
+    ]
 
 
 def butterfly_sum(value, n):
@@ -136,17 +127,27 @@
     local_rows = images_here * patches
     h_rows = hidden.reshape(local_rows, width)
     grad_rows = output_grad.reshape(local_rows, model_width)
-    if views == 4:
-        swapped, every = exchange_four(h_rows, grad_rows)
+    if views == 4 and images_here == 1:
+        pieces = exchange_four(h_rows, grad_rows)
+        slice_width = pieces[0][1].shape[1]
+        summed = None
+        hidden_grad = jnp.zeros((views * local_rows, slice_width), jnp.bfloat16)
+        for at, h_piece, g_piece in pieces:
+            term = jnp.dot(h_piece.T, g_piece, preferred_element_type=jnp.float32)
+            summed = term if summed is None else summed + term
+            back = project_back(g_piece, down_weight).astype(jnp.bfloat16)
+            hidden_grad = lax.dynamic_update_slice_in_dim(hidden_grad, back, at, axis=0)
+        summed = summed[None]
+        hidden_grad = hidden_grad.reshape(views, images_here, patches, slice_width)
     else:
         swapped = lax.all_to_all(h_rows, "aug", split_axis=1, concat_axis=0, tiled=True)
         every = lax.all_gather(grad_rows, "aug", axis=0, tiled=True)
-    slice_width = swapped.shape[1]
-    h_four = swapped.reshape(views, images_here, patches, slice_width)
-    g_four = every.reshape(views, images_here, patches, model_width)
-    summed = jnp.einsum("vipf,vipd->ifd", h_four, g_four, preferred_element_type=jnp.float32)
-    back_rows = project_back(every, down_weight)
-    hidden_grad = back_rows.astype(jnp.bfloat16).reshape(views, images_here, patches, slice_width)
+        slice_width = swapped.shape[1]
+        h_four = swapped.reshape(views, images_here, patches, slice_width)
+        g_four = every.reshape(views, images_here, patches, model_width)
+        summed = jnp.einsum("vipf,vipd->ifd", h_four, g_four, preferred_element_type=jnp.float32)
+        back_rows = project_back(every, down_weight)
+        hidden_grad = back_rows.astype(jnp.bfloat16).reshape(views, images_here, patches, slice_width)
     grads = summed / views
     partial_value = jnp.sum(grads * grads, axis=(1, 2))
     squares = butterfly_sum(partial_value, views)
@@ -161,7 +162,7 @@
             _, source = lax.optimization_barrier((after, grads))
         start = block * owned_rows + which * half
         rows = lax.dynamic_slice_in_dim(source, start, half, axis=1)
-        return jnp.sum(factor[:, None, None] * rows, axis=0)
+        return lax.optimization_barrier(jnp.sum(factor[:, None, None] * rows, axis=0))
 
     owned = ring_reduce_scatter(parts, ring, None)
     clipped_mean = owned / images_all

time: 150 us -> 131 us (0.87)
  waiting for transfers between devices: 72.2 us -> 57.8 us
  local copies, waits for them, and re-layouts: 12.9 us -> 4.04 us
  matrix products: 8.81 us -> 16.8 us
  other arithmetic: 10.9 us -> 6.06 us
  between operations: 22 us -> 25.1 us
  starting transfers between devices: 22.3 us -> 20.1 us
    ppermute x1, waiting for transfers between devices: 21.8 us -> 0.01 us  [exchange_four(): lax.ppermute(jnp.concatenate([cols(a ^ 2), cols(a ^ 3), grad_rows], axis=...]
    ppermute x7, starting transfers between devices: 13.7 us -> 4.18 us  [ring_reduce_scatter(): acc_l = lax.ppermute(send_l, 'dp', left)]
    ppermute x7, starting transfers between devices: 2.04 us -> 11 us  [ring_reduce_scatter(): acc_r = lax.ppermute(send_r, 'dp', right)]
    ppermute x7, waiting for transfers between devices: 45.5 us -> 54 us  [ring_reduce_scatter(): acc_r = lax.ppermute(send_r, 'dp', right)]
    dynamic_update_slice x6 -> x0, local copies, waits for them, and re-layouts: 7.2 us -> none  [the longest x4 5.11 us: exchange_four(): g_all = lax.dynamic_update_slice_in_dim(g_all, g_from[m], at, axis=0)]
    add x14, other arithmetic: 6.97 us -> 0.7 us  [the longest x6 0.31 us: ring_reduce_scatter(): send_r = own_r if acc_r is None else acc_r + own_r]
    dot_general x1 -> x4, matrix products: 4.54 us -> 9.13 us  [per_device(): term = jnp.dot(h_piece.T, g_piece, preferred_element_type=jnp.float32)]
    dot_general x1 -> x4, matrix products: 4.27 us -> 7.72 us  [project_back(): lax.dot_general(rows, down_weight, (((1,), (1,)), ((), ())), preferred_el...]
  transfers between devices with their start and end apart: 19 -> 19, of which waited for: 15 -> 9; matrix products, arithmetic and copies ran while one was open for 11% -> 13% of each run, Pallas kernels for 0% -> 0%
where the time goes in v3:
time: 131 us; the launch traced here: 130 us
  waiting for transfers between devices  57.8 us (44%)
  between operations  25.1 us (19%)
  starting transfers between devices  20.1 us (15%)
  matrix products  16.8 us (13%)
  other arithmetic  6.06 us (5%)
  local copies, waits for them, and re-layouts  4.04 us (3%)
    ppermute x7, waiting for transfers between devices, ring_reduce_scatter(): acc_r = lax.ppermute(send_r, 'dp', right)  54 us
    ppermute x7, starting transfers between devices, ring_reduce_scatter(): acc_r = lax.ppermute(send_r, 'dp', right)  11 us
    dot_general x4, matrix products, per_device(): term = jnp.dot(h_piece.T, g_piece, preferred_element_type=jnp.float32)  9.13 us
    dot_general x4, matrix products, project_back(): lax.dot_general(rows, down_weight, (((1,), (1,)), ((), ())), preferred_el...  7.72 us
    ppermute x7, starting transfers between devices, ring_reduce_scatter(): acc_l = lax.ppermute(send_l, 'dp', left)  4.18 us
    ppermute x1, starting transfers between devices, exchange_four(): lax.ppermute(jnp.concatenate([cols(a ^ 2), cols(a ^ 3), grad_rows], axis=...  2.94 us
  transfers between devices with their start and end apart: 19, of which 9 were waited for; matrix products, arithmetic and copies ran while one was open for 13% of the time, Pallas kernels for 0%

profile of v3, /device:TPU:0, one launch (start us, length us, event | category | flops | bytes accessed | tf_op | source)
XLA Modules:
  0.0 129.9 jit_solution(11096374476599327822)
XLA Ops:
  0.6 0.0 copy-start
  0.6 0.0 copy-start.8
  0.7 0.0 copy-start.7
  0.7 0.0 copy-start.1
  0.7 1.4 %dynamic-slice_bitcast_fusion.2 = (bf16[128,1280]{1,0:T(8,128)(2,1)S(1)}, bf16[128,1280]{1,0:T(8,128)(2,1)S(1)}, bf16[128,1280]{1,0:T(8,128)(2,1)S(1)}) fusion(bf16[1,1,128,5120]{3,2,1,0:T(8,128)(2,1)} %param.8, s32[]{:T(128)S(6)} %select_n.191, s32[]{:T(128)S(6)} %select_n.193, s32[]{:T(128)S(6)} %select_n.192), kind=kLoop, calls=%fused_computation.45 | loop fusion | bytes 1966092 | tf_op jit(solution)/shard_map/dynamic_slice | solution.py:91
  2.1 2.0 %pad_maximum_fusion = bf16[128,3840]{1,0:T(8,128)(2,1)} fusion(bf16[128,1280]{1,0:T(8,128)(2,1)} %bitcast.104, bf16[128,1280]{1,0:T(8,128)(2,1)S(1)} %get-tuple-element.41, bf16[128,1280]{1,0:T(8,128)(2,1)S(1)} %get-tuple-element.42), kind=kLoop, calls=%fused_computation.14 | loop fusion | flops 2949120 | bytes 1966080 | tf_op jit(solution)/shard_map/concatenate | solution.py:96
  4.1 2.9 %collective-permute-start.1 = (bf16[128,3840]{1,0:T(8,128)(2,1)}, bf16[128,3840]{1,0:T(8,128)(2,1)}, u32[]{:S(2)}, u32[]{:S(2)}) collective-permute-start(bf16[128,3840]{1,0:T(8,128)(2,1)} %pad_maximum_fusion), channel_id=1, source_target_pairs={{0,16},{8,24},{16,0},{24,8},{1,17},{9,25},{17,1},{25,9},{2,18},{10... | collective-permute-start | bytes 2949128 | tf_op jit(solution)/shard_map/ppermute | solution.py:95
  7.0 0.9 pad_maximum_fusion.1
  7.9 0.6 dynamic_slice.123
  19.2 0.8 fusion.24
  30.3 0.0 copy-start.2
  30.3 0.1 broadcast_in_dim.2
  30.4 2.2 %fusion.5 = bf16[512,1280]{1,0:T(8,128)(2,1)S(1)} fusion(bf16[512,1280]{1,0:T(8,128)(2,1)S(1)} %broadcast_in_dim.2, s32[]{:T(128)S(6)} %select_n.243, bf16[1280,1280]{1,0:T(8,128)(2,1)S(1)} %copy-done, bf16[1,1,128,1280]{3,2,1,0:T(8,128)(2,1)} %param.9), kind=kOutput, calls=%fused_computation.12 | convolution fusion | flops 419594240 | bytes 3932164 | tf_op jit(solution)/shard_map/dot_general | solution.py:17
  32.6 2.0 %fusion.11 = f32[1280,1280]{1,0:T(8,128)S(1)} fusion(bf16[1,1,128,5120]{3,2,1,0:T(8,128)(2,1)} %param.8, s32[]{:T(128)S(6)} %select_n.190, bf16[1,1,128,1280]{3,2,1,0:T(8,128)(2,1)S(1)} %copy-done.2), kind=kOutput, calls=%fused_computation.41 | convolution fusion | flops 419430400 | bytes 7208964 | tf_op jit(solution)/shard_map/dot_general | solution.py:136
  34.6 0.0 collective-permute-done.1
  34.6 1.1 slice.32
  35.7 0.6 collective-permute-start.2
  36.3 0.0 collective-permute-done
  36.3 2.1 %convolution_add_fusion.1 = f32[1280,1280]{1,0:T(8,128)S(1)} fusion(f32[1280,1280]{1,0:T(8,128)S(1)} %fusion.11, bf16[128,2560]{1,0:T(8,128)(2,1)} %collective-permute-done), kind=kOutput, calls=%fused_computation.1 | convolution fusion | flops 421068800 | bytes 13762560 | tf_op jit(solution)/shard_map/dot_general | solution.py:136
  38.4 2.2 %fusion.4 = bf16[512,1280]{1,0:T(8,128)(2,1)S(1)} fusion(bf16[512,1280]{1,0:T(8,128)(2,1)S(1)} %fusion.5, s32[]{:T(128)S(6)} %select_n.244, bf16[1280,1280]{1,0:T(8,128)(2,1)S(1)} %copy-done, bf16[128,2560]{1,0:T(8,128)(2,1)} %collective-permute-done), kind=kOutput, calls=%fused_computation.10 | convolution fusion | flops 419594240 | bytes 3932164 | tf_op jit(solution)/shard_map/dot_general | solution.py:17
  40.6 2.2 %fusion.3 = bf16[512,1280]{1,0:T(8,128)(2,1)S(1)} fusion(bf16[512,1280]{1,0:T(8,128)(2,1)S(1)} %fusion.4, s32[]{:T(128)S(6)} %select_n.245, bf16[1280,1280]{1,0:T(8,128)(2,1)S(1)} %copy-done, bf16[128,3840]{1,0:T(8,128)(2,1)} %collective-permute-done.1), kind=kOutput, calls=%fused_computation.8 | convolution fusion | flops 419594240 | bytes 3932164 | tf_op jit(solution)/shard_map/dot_general | solution.py:17
  42.8 0.0 collective-permute-done.2
  42.8 1.0 fusion.7
  43.9 3.9 %multiply_reduce_fusion = (f32[]{:T(128)}, f32[1280,1280]{1,0:T(8,128)S(1)}) fusion(f32[1280,1280]{1,0:T(8,128)S(1)} %fusion.7, f32[1280,1280]{1,0:T(8,128)S(1)} %convolution_add_fusion.1, bf16[128,3840]{1,0:T(8,128)(2,1)} %collective-permute-done.1), kind=kOutput, calls=%fused_computation.4 | convolution fusion | flops 427622400 | bytes 20316164 | tf_op jit(solution)/shard_map/dot_general | solution.py:136
  47.8 0.0 collective-permute-start.3
  47.8 1.2 fusion.2
  49.0 0.0 copy-start.3
  49.0 0.0 collective-permute-done.3
  50.3 1.4 %collective-permute-start.4 = (f32[1]{0:T(128)}, f32[1]{0:T(128)}, u32[]{:S(2)}, u32[]{:S(2)}) collective-permute-start(f32[1]{0:T(128)} %add.438), channel_id=1, source_target_pairs={{0,16},{8,24},{16,0},{24,8},{1,17},{9,25},{17,1},{25,9},{2,18},{10... | collective-permute-start | bytes 20 | tf_op jit(solution)/shard_map/ppermute | solution.py:113
  51.7 2.2 %collective-permute-done.4 = f32[1]{0:T(128)} collective-permute-done((f32[1]{0:T(128)}, f32[1]{0:T(128)}, u32[]{:S(2)}, u32[]{:S(2)}) %collective-permute-start.4) | collective-permute-done | bytes 36 | tf_op jit(solution)/shard_map/ppermute | solution.py:113
  54.6 0.1 dynamic-slice_multiply_fusion.1
  54.7 1.6 %collective-permute-start.5 = (f32[80,1280]{1,0:T(8,128)S(1)}, f32[80,1280]{1,0:T(8,128)S(1)}, u32[]{:S(2)}, u32[]{:S(2)}) collective-permute-start(f32[80,1280]{1,0:T(8,128)S(1)} %get-tuple-element.38), channel_id=1, source_target_pairs={{0,1},{1,3},{3,5},{5,7},{7,6},{6,4},{4,2},{2,0},{8,9},{9,11},{11,1... | collective-permute-start | bytes 1228808 | tf_op jit(solution)/shard_map/ppermute | solution.py:77
  56.2 0.5 collective-permute-start.12
  56.8 8.8 %collective-permute-done.5 = f32[80,1280]{1,0:T(8,128)S(1)} collective-permute-done((f32[80,1280]{1,0:T(8,128)S(1)}, f32[80,1280]{1,0:T(8,128)S(1)}, u32[]{:S(2)}, u32[]{:S(2)}) %collective-permute-start.5) | collective-permute-done | bytes 409632 | tf_op jit(solution)/shard_map/ppermute | solution.py:77
  65.6 0.1 add.447
  65.6 1.6 %collective-permute-start.6 = (f32[80,1280]{1,0:T(8,128)S(1)}, f32[80,1280]{1,0:T(8,128)S(1)}, u32[]{:S(2)}, u32[]{:S(2)}) collective-permute-start(f32[80,1280]{1,0:T(8,128)S(1)} %add.447), channel_id=1, source_target_pairs={{0,1},{1,3},{3,5},{5,7},{7,6},{6,4},{4,2},{2,0},{8,9},{9,11},{11,1... | collective-permute-start | bytes 1228808 | tf_op jit(solution)/shard_map/ppermute | solution.py:77
  67.2 0.1 add.488
  67.3 0.6 collective-permute-start.13
  67.9 7.7 %collective-permute-done.6 = f32[80,1280]{1,0:T(8,128)S(1)} collective-permute-done((f32[80,1280]{1,0:T(8,128)S(1)}, f32[80,1280]{1,0:T(8,128)S(1)}, u32[]{:S(2)}, u32[]{:S(2)}) %collective-permute-start.6) | collective-permute-done | bytes 409632 | tf_op jit(solution)/shard_map/ppermute | solution.py:77
  75.6 0.1 add.451
  75.7 1.6 %collective-permute-start.7 = (f32[80,1280]{1,0:T(8,128)S(1)}, f32[80,1280]{1,0:T(8,128)S(1)}, u32[]{:S(2)}, u32[]{:S(2)}) collective-permute-start(f32[80,1280]{1,0:T(8,128)S(1)} %add.451), channel_id=1, source_target_pairs={{0,1},{1,3},{3,5},{5,7},{7,6},{6,4},{4,2},{2,0},{8,9},{9,11},{11,1... | collective-permute-start | bytes 1228808 | tf_op jit(solution)/shard_map/ppermute | solution.py:77
  77.3 0.1 add.497
  77.3 0.6 collective-permute-start.14
  78.0 7.3 %collective-permute-done.7 = f32[80,1280]{1,0:T(8,128)S(1)} collective-permute-done((f32[80,1280]{1,0:T(8,128)S(1)}, f32[80,1280]{1,0:T(8,128)S(1)}, u32[]{:S(2)}, u32[]{:S(2)}) %collective-permute-start.7) | collective-permute-done | bytes 409632 | tf_op jit(solution)/shard_map/ppermute | solution.py:77
  85.3 0.1 add.455
  85.3 1.6 %collective-permute-start.8 = (f32[80,1280]{1,0:T(8,128)S(1)}, f32[80,1280]{1,0:T(8,128)S(1)}, u32[]{:S(2)}, u32[]{:S(2)}) collective-permute-start(f32[80,1280]{1,0:T(8,128)S(1)} %add.455), channel_id=1, source_target_pairs={{0,1},{1,3},{3,5},{5,7},{7,6},{6,4},{4,2},{2,0},{8,9},{9,11},{11,1... | collective-permute-start | bytes 1228808 | tf_op jit(solution)/shard_map/ppermute | solution.py:77
  86.9 0.1 add.506
  87.0 0.6 collective-permute-start.15
  87.6 7.3 %collective-permute-done.8 = f32[80,1280]{1,0:T(8,128)S(1)} collective-permute-done((f32[80,1280]{1,0:T(8,128)S(1)}, f32[80,1280]{1,0:T(8,128)S(1)}, u32[]{:S(2)}, u32[]{:S(2)}) %collective-permute-start.8) | collective-permute-done | bytes 409632 | tf_op jit(solution)/shard_map/ppermute | solution.py:77
  95.0 1.6 %collective-permute-start.9 = (f32[80,1280]{1,0:T(8,128)S(1)}, f32[80,1280]{1,0:T(8,128)S(1)}, u32[]{:S(2)}, u32[]{:S(2)}) collective-permute-start(f32[80,1280]{1,0:T(8,128)S(1)} %add.459), channel_id=1, source_target_pairs={{0,1},{1,3},{3,5},{5,7},{7,6},{6,4},{4,2},{2,0},{8,9},{9,11},{11,1... | collective-permute-start | bytes 1228808 | tf_op jit(solution)/shard_map/ppermute | solution.py:77
  96.6 0.6 collective-permute-start.16
  97.2 8.2 %collective-permute-done.9 = f32[80,1280]{1,0:T(8,128)S(1)} collective-permute-done((f32[80,1280]{1,0:T(8,128)S(1)}, f32[80,1280]{1,0:T(8,128)S(1)}, u32[]{:S(2)}, u32[]{:S(2)}) %collective-permute-start.9) | collective-permute-done | bytes 409632 | tf_op jit(solution)/shard_map/ppermute | solution.py:77
  105.5 1.6 %collective-permute-start.10 = (f32[80,1280]{1,0:T(8,128)S(1)}, f32[80,1280]{1,0:T(8,128)S(1)}, u32[]{:S(2)}, u32[]{:S(2)}) collective-permute-start(f32[80,1280]{1,0:T(8,128)S(1)} %add.463), channel_id=1, source_target_pairs={{0,1},{1,3},{3,5},{5,7},{7,6},{6,4},{4,2},{2,0},{8,9},{9,11},{11,1... | collective-permute-start | bytes 1228808 | tf_op jit(solution)/shard_map/ppermute | solution.py:77
  107.1 0.7 collective-permute-start.17
  107.8 0.0 copy-start.4
  107.8 0.0 copy-start.5
  107.9 0.0 copy-start.6
  107.9 9.2 %collective-permute-done.10 = f32[80,1280]{1,0:T(8,128)S(1)} collective-permute-done((f32[80,1280]{1,0:T(8,128)S(1)}, f32[80,1280]{1,0:T(8,128)S(1)}, u32[]{:S(2)}, u32[]{:S(2)}) %collective-permute-start.10) | collective-permute-done | bytes 409632 | tf_op jit(solution)/shard_map/ppermute | solution.py:77
  117.1 1.6 %collective-permute-start.11 = (f32[80,1280]{1,0:T(8,128)S(1)}, f32[80,1280]{1,0:T(8,128)S(1)}, u32[]{:S(2)}, u32[]{:S(2)}) collective-permute-start(f32[80,1280]{1,0:T(8,128)S(1)} %add.467), channel_id=1, source_target_pairs={{0,1},{1,3},{3,5},{5,7},{7,6},{6,4},{4,2},{2,0},{8,9},{9,11},{11,1... | collective-permute-start | bytes 1228808 | tf_op jit(solution)/shard_map/ppermute | solution.py:77
  118.7 0.0 collective-permute-done.17
  118.8 0.8 collective-permute-start.18
  119.7 5.5 %collective-permute-done.11 = f32[80,1280]{1,0:T(8,128)S(1)} collective-permute-done((f32[80,1280]{1,0:T(8,128)S(1)}, f32[80,1280]{1,0:T(8,128)S(1)}, u32[]{:S(2)}, u32[]{:S(2)}) %collective-permute-start.11) | collective-permute-done | bytes 409632 | tf_op jit(solution)/shard_map/ppermute | solution.py:77
  125.2 1.6 %collective-permute-done.18 = f32[80,1280]{1,0:T(8,128)S(1)} collective-permute-done((f32[80,1280]{1,0:T(8,128)S(1)}, f32[80,1280]{1,0:T(8,128)S(1)}, u32[]{:S(2)}, u32[]{:S(2)}) %collective-permute-start.18) | collective-permute-done | bytes 409632 | tf_op jit(solution)/shard_map/ppermute | solution.py:78
  126.8 1.9 %add_divide_fusion = (f32[160,1280]{1,0:T(8,128)}, f32[160,1280]{1,0:T(8,128)}, f32[160,1280]{1,0:T(8,128)}, f32[160,1280]{1,0:T(8,128)}) fusion(f32[160,1280]{1,0:T(8,128)S(1)} %copy-done.4, f32[160,1280]{1,0:T(8,128)S(1)} %copy-done.5, f32[160,1280]{1,0:T(8,128)S(1)} %copy-done.6, f32[80,1280]{1,0:T(8,128)S(1)} %add.542, f32[80,1280]{1,0:T(8,128)S(1)} %add.471), kind=kLoop, calls=%fused_computation.17 | loop fusion | flops 3072000 | bytes 6553600 | tf_op jit(solution)/shard_map/div | solution.py:173
  (37 shorter events, 0.9 us)
Async XLA Ops:
  0.6 29.7 %copy-start = (bf16[1280,1280]{1,0:T(8,128)(2,1)S(1)}, bf16[1280,1280]{1,0:T(8,128)(2,1)}, u32[]{:S(2)}) copy-start(bf16[1280,1280]{1,0:T(8,128)(2,1)} %param.10) | copy-start | bytes 9830404
  0.6 7.3 %copy-start.8 = (s32[8]{0:T(128)S(1)}, s32[8]{0:T(128)}, u32[]{:S(2)}) copy-start(s32[8]{0:T(128)} %constant.240.clone) | copy-start | bytes 100
  0.7 18.5 %copy-start.7 = (s32[8]{0:T(128)S(1)}, s32[8]{0:T(128)}, u32[]{:S(2)}) copy-start(s32[8]{0:T(128)} %constant.239.clone) | copy-start | bytes 100
  0.7 6.4 %copy-start.1 = (bf16[1,1,128,1280]{3,2,1,0:T(8,128)(2,1)S(1)}, bf16[1,1,128,1280]{3,2,1,0:T(8,128)(2,1)}, u32[]{:S(2)}) copy-start(bf16[1,1,128,1280]{3,2,1,0:T(8,128)(2,1)} %param.9) | copy-start | bytes 983044
  4.1 30.5 %collective-permute-start.1 = (bf16[128,3840]{1,0:T(8,128)(2,1)}, bf16[128,3840]{1,0:T(8,128)(2,1)}, u32[]{:S(2)}, u32[]{:S(2)}) collective-permute-start(bf16[128,3840]{1,0:T(8,128)(2,1)} %pad_maximum_fusion), channel_id=1, source_target_pairs={{0,16},{8,24},{16,0},{24,8},{1,17},{9,25},{17,1},{25,9},{2,18},{10... | collective-permute-start | bytes 2949128 | tf_op jit(solution)/shard_map/ppermute | solution.py:95
  7.9 28.4 %collective-permute-start = (bf16[128,2560]{1,0:T(8,128)(2,1)}, bf16[128,2560]{1,0:T(8,128)(2,1)}, u32[]{:S(2)}, u32[]{:S(2)}) collective-permute-start(bf16[128,2560]{1,0:T(8,128)(2,1)} %pad_maximum_fusion.1), channel_id=1, source_target_pairs={{0,8},{8,0},{16,24},{24,16},{1,9},{9,1},{17,25},{25,17},{2,10},{10... | collective-permute-start | bytes 1966088 | tf_op jit(solution)/shard_map/ppermute | solution.py:98
  30.3 2.3 %copy-start.2 = (bf16[1,1,128,1280]{3,2,1,0:T(8,128)(2,1)S(1)}, bf16[1,1,128,1280]{3,2,1,0:T(8,128)(2,1)}, u32[]{:S(2)}) copy-start(bf16[1,1,128,1280]{3,2,1,0:T(8,128)(2,1)} %param.9) | copy-start | bytes 983044
  35.7 7.1 %collective-permute-start.2 = (bf16[128,2560]{1,0:T(8,128)(2,1)S(1)}, bf16[128,2560]{1,0:T(8,128)(2,1)S(1)}, u32[]{:S(2)}, u32[]{:S(2)}) collective-permute-start(bf16[128,2560]{1,0:T(8,128)(2,1)S(1)} %slice.32), channel_id=1, source_target_pairs={{0,8},{8,0},{16,24},{24,16},{1,9},{9,1},{17,25},{25,17},{2,10},{10... | collective-permute-start | bytes 1966088 | tf_op jit(solution)/shard_map/ppermute | solution.py:99
  47.8 1.2 collective-permute-start.3
  49.0 18.8 %copy-start.3 = (bf16[512,1280]{1,0:T(8,128)(2,1)}, bf16[512,1280]{1,0:T(8,128)(2,1)S(1)}, u32[]{:S(2)}) copy-start(bf16[512,1280]{1,0:T(8,128)(2,1)S(1)} %fusion.2) | copy-start | bytes 3932164
  50.3 3.6 %collective-permute-start.4 = (f32[1]{0:T(128)}, f32[1]{0:T(128)}, u32[]{:S(2)}, u32[]{:S(2)}) collective-permute-start(f32[1]{0:T(128)} %add.438), channel_id=1, source_target_pairs={{0,16},{8,24},{16,0},{24,8},{1,17},{9,25},{17,1},{25,9},{2,18},{10... | collective-permute-start | bytes 20 | tf_op jit(solution)/shard_map/ppermute | solution.py:113
  54.7 10.9 %collective-permute-start.5 = (f32[80,1280]{1,0:T(8,128)S(1)}, f32[80,1280]{1,0:T(8,128)S(1)}, u32[]{:S(2)}, u32[]{:S(2)}) collective-permute-start(f32[80,1280]{1,0:T(8,128)S(1)} %get-tuple-element.38), channel_id=1, source_target_pairs={{0,1},{1,3},{3,5},{5,7},{7,6},{6,4},{4,2},{2,0},{8,9},{9,11},{11,1... | collective-permute-start | bytes 1228808 | tf_op jit(solution)/shard_map/ppermute | solution.py:77
  56.2 11.0 %collective-permute-start.12 = (f32[80,1280]{1,0:T(8,128)S(1)}, f32[80,1280]{1,0:T(8,128)S(1)}, u32[]{:S(2)}, u32[]{:S(2)}) collective-permute-start(f32[80,1280]{1,0:T(8,128)S(1)} %get-tuple-element.39), channel_id=1, source_target_pairs={{0,2},{1,0},{3,1},{5,3},{7,5},{6,7},{4,6},{2,4},{8,10},{9,8},{11,9... | collective-permute-start | bytes 1228808 | tf_op jit(solution)/shard_map/ppermute | solution.py:78
  65.6 10.0 %collective-permute-start.6 = (f32[80,1280]{1,0:T(8,128)S(1)}, f32[80,1280]{1,0:T(8,128)S(1)}, u32[]{:S(2)}, u32[]{:S(2)}) collective-permute-start(f32[80,1280]{1,0:T(8,128)S(1)} %add.447), channel_id=1, source_target_pairs={{0,1},{1,3},{3,5},{5,7},{7,6},{6,4},{4,2},{2,0},{8,9},{9,11},{11,1... | collective-permute-start | bytes 1228808 | tf_op jit(solution)/shard_map/ppermute | solution.py:77
  67.3 10.0 %collective-permute-start.13 = (f32[80,1280]{1,0:T(8,128)S(1)}, f32[80,1280]{1,0:T(8,128)S(1)}, u32[]{:S(2)}, u32[]{:S(2)}) collective-permute-start(f32[80,1280]{1,0:T(8,128)S(1)} %add.488), channel_id=1, source_target_pairs={{0,2},{1,0},{3,1},{5,3},{7,5},{6,7},{4,6},{2,4},{8,10},{9,8},{11,9... | collective-permute-start | bytes 1228808 | tf_op jit(solution)/shard_map/ppermute | solution.py:78
  75.7 9.6 %collective-permute-start.7 = (f32[80,1280]{1,0:T(8,128)S(1)}, f32[80,1280]{1,0:T(8,128)S(1)}, u32[]{:S(2)}, u32[]{:S(2)}) collective-permute-start(f32[80,1280]{1,0:T(8,128)S(1)} %add.451), channel_id=1, source_target_pairs={{0,1},{1,3},{3,5},{5,7},{7,6},{6,4},{4,2},{2,0},{8,9},{9,11},{11,1... | collective-permute-start | bytes 1228808 | tf_op jit(solution)/shard_map/ppermute | solution.py:77
  77.3 9.6 %collective-permute-start.14 = (f32[80,1280]{1,0:T(8,128)S(1)}, f32[80,1280]{1,0:T(8,128)S(1)}, u32[]{:S(2)}, u32[]{:S(2)}) collective-permute-start(f32[80,1280]{1,0:T(8,128)S(1)} %add.497), channel_id=1, source_target_pairs={{0,2},{1,0},{3,1},{5,3},{7,5},{6,7},{4,6},{2,4},{8,10},{9,8},{11,9... | collective-permute-start | bytes 1228808 | tf_op jit(solution)/shard_map/ppermute | solution.py:78
  85.3 9.6 %collective-permute-start.8 = (f32[80,1280]{1,0:T(8,128)S(1)}, f32[80,1280]{1,0:T(8,128)S(1)}, u32[]{:S(2)}, u32[]{:S(2)}) collective-permute-start(f32[80,1280]{1,0:T(8,128)S(1)} %add.455), channel_id=1, source_target_pairs={{0,1},{1,3},{3,5},{5,7},{7,6},{6,4},{4,2},{2,0},{8,9},{9,11},{11,1... | collective-permute-start | bytes 1228808 | tf_op jit(solution)/shard_map/ppermute | solution.py:77
  87.0 9.6 %collective-permute-start.15 = (f32[80,1280]{1,0:T(8,128)S(1)}, f32[80,1280]{1,0:T(8,128)S(1)}, u32[]{:S(2)}, u32[]{:S(2)}) collective-permute-start(f32[80,1280]{1,0:T(8,128)S(1)} %add.506), channel_id=1, source_target_pairs={{0,2},{1,0},{3,1},{5,3},{7,5},{6,7},{4,6},{2,4},{8,10},{9,8},{11,9... | collective-permute-start | bytes 1228808 | tf_op jit(solution)/shard_map/ppermute | solution.py:78
  95.0 10.5 %collective-permute-start.9 = (f32[80,1280]{1,0:T(8,128)S(1)}, f32[80,1280]{1,0:T(8,128)S(1)}, u32[]{:S(2)}, u32[]{:S(2)}) collective-permute-start(f32[80,1280]{1,0:T(8,128)S(1)} %add.459), channel_id=1, source_target_pairs={{0,1},{1,3},{3,5},{5,7},{7,6},{6,4},{4,2},{2,0},{8,9},{9,11},{11,1... | collective-permute-start | bytes 1228808 | tf_op jit(solution)/shard_map/ppermute | solution.py:77
  96.6 10.5 %collective-permute-start.16 = (f32[80,1280]{1,0:T(8,128)S(1)}, f32[80,1280]{1,0:T(8,128)S(1)}, u32[]{:S(2)}, u32[]{:S(2)}) collective-permute-start(f32[80,1280]{1,0:T(8,128)S(1)} %add.515), channel_id=1, source_target_pairs={{0,2},{1,0},{3,1},{5,3},{7,5},{6,7},{4,6},{2,4},{8,10},{9,8},{11,9... | collective-permute-start | bytes 1228808 | tf_op jit(solution)/shard_map/ppermute | solution.py:78
  105.5 11.6 %collective-permute-start.10 = (f32[80,1280]{1,0:T(8,128)S(1)}, f32[80,1280]{1,0:T(8,128)S(1)}, u32[]{:S(2)}, u32[]{:S(2)}) collective-permute-start(f32[80,1280]{1,0:T(8,128)S(1)} %add.463), channel_id=1, source_target_pairs={{0,1},{1,3},{3,5},{5,7},{7,6},{6,4},{4,2},{2,0},{8,9},{9,11},{11,1... | collective-permute-start | bytes 1228808 | tf_op jit(solution)/shard_map/ppermute | solution.py:77
  107.1 11.6 %collective-permute-start.17 = (f32[80,1280]{1,0:T(8,128)S(1)}, f32[80,1280]{1,0:T(8,128)S(1)}, u32[]{:S(2)}, u32[]{:S(2)}) collective-permute-start(f32[80,1280]{1,0:T(8,128)S(1)} %add.524), channel_id=1, source_target_pairs={{0,2},{1,0},{3,1},{5,3},{7,5},{6,7},{4,6},{2,4},{8,10},{9,8},{11,9... | collective-permute-start | bytes 1228808 | tf_op jit(solution)/shard_map/ppermute | solution.py:78
  107.8 19.0 %copy-start.4 = (f32[160,1280]{1,0:T(8,128)S(1)}, f32[160,1280]{1,0:T(8,128)}, u32[]{:S(2)}) copy-start(f32[160,1280]{1,0:T(8,128)} %param.13) | copy-start | bytes 2457604
  107.8 19.0 %copy-start.5 = (f32[160,1280]{1,0:T(8,128)S(1)}, f32[160,1280]{1,0:T(8,128)}, u32[]{:S(2)}) copy-start(f32[160,1280]{1,0:T(8,128)} %param.12) | copy-start | bytes 2457604
  107.9 19.0 %copy-start.6 = (f32[160,1280]{1,0:T(8,128)S(1)}, f32[160,1280]{1,0:T(8,128)}, u32[]{:S(2)}) copy-start(f32[160,1280]{1,0:T(8,128)} %param.11) | copy-start | bytes 2457604
  117.1 8.0 %collective-permute-start.11 = (f32[80,1280]{1,0:T(8,128)S(1)}, f32[80,1280]{1,0:T(8,128)S(1)}, u32[]{:S(2)}, u32[]{:S(2)}) collective-permute-start(f32[80,1280]{1,0:T(8,128)S(1)} %add.467), channel_id=1, source_target_pairs={{0,1},{1,3},{3,5},{5,7},{7,6},{6,4},{4,2},{2,0},{8,9},{9,11},{11,1... | collective-permute-start | bytes 1228808 | tf_op jit(solution)/shard_map/ppermute | solution.py:77
  118.8 8.0 %collective-permute-start.18 = (f32[80,1280]{1,0:T(8,128)S(1)}, f32[80,1280]{1,0:T(8,128)S(1)}, u32[]{:S(2)}, u32[]{:S(2)}) collective-permute-start(f32[80,1280]{1,0:T(8,128)S(1)} %add.533), channel_id=1, source_target_pairs={{0,2},{1,0},{3,1},{5,3},{7,5},{6,7},{4,6},{2,4},{8,10},{9,8},{11,9... | collective-permute-start | bytes 1228808 | tf_op jit(solution)/shard_map/ppermute | solution.py:78

commit v4 on v3

--- a/solution.py
+++ b/solution.py
@@ -54,18 +54,24 @@
     return [places.index(p) for p in cycle]
 
 
+def lookup(table, index):
+    out = jnp.int32(table[0])
+    for k in range(1, len(table)):
+        out = jnp.where(index == k, jnp.int32(table[k]), out)
+    return out
+
+
 def ring_reduce_scatter(parts, ring, step_fn):
     n = len(ring)
     pos_of = [0] * n
     for k, d in enumerate(ring):
         pos_of[d] = k
-    ring_arr = jnp.array(ring, jnp.int32)
     me = lax.axis_index("dp")
-    pos = jnp.array(pos_of, jnp.int32)[me]
+    pos = lookup(pos_of, me)
     right = [(ring[k], ring[(k + 1) % n]) for k in range(n)]
     left = [(ring[k], ring[(k - 1) % n]) for k in range(n)]
     def block(s, step):
-        return ring_arr[(pos - 1 - s) % n] if step < 0 else ring_arr[(pos + 1 + s) % n]
+        return lookup(ring, (pos - 1 - s) % n if step < 0 else (pos + 1 + s) % n)
 
     own_r = parts(block(0, -1), 0, None)
     own_l = parts(block(0, 1), 1, None)
@@ -92,20 +98,34 @@
 
     over_x = [(i, i ^ 2) for i in range(4)]
     over_core = [(i, i ^ 1) for i in range(4)]
-    far = lax.ppermute(
-        jnp.concatenate([cols(a ^ 2), cols(a ^ 3), grad_rows], axis=1), "aug", over_x
+    far_first = lax.ppermute(
+        jnp.concatenate([cols(a ^ 3), grad_rows], axis=1), "aug", over_x
     )
     near = lax.ppermute(jnp.concatenate([cols(a ^ 1), grad_rows], axis=1), "aug", over_core)
-    relay = lax.ppermute(far[:, sw:], "aug", over_core)
+    _, second = lax.optimization_barrier((far_first, cols(a ^ 2)))
+    far_second = lax.ppermute(second, "aug", over_x)
+    relay = lax.ppermute(far_first, "aug", over_core)
     return [
         (a * rows, cols(a), grad_rows),
         ((a ^ 1) * rows, near[:, :sw], near[:, sw:]),
-        ((a ^ 2) * rows, far[:, :sw], far[:, 2 * sw:]),
+        ((a ^ 2) * rows, far_second, far_first[:, sw:]),
         ((a ^ 3) * rows, relay[:, :sw], relay[:, sw:]),
     ]
 
 
 def butterfly_sum(value, n):
+    if n == 4:
+        a = lax.axis_index("aug")
+        got = {0: value}
+        for m in (1, 2, 3):
+            got[m] = lax.ppermute(value, "aug", [(i, i ^ m) for i in range(4)])
+        total = None
+        for k in range(4):
+            term = got[3]
+            for m in (2, 1, 0):
+                term = jnp.where((a ^ m) == k, got[m], term)
+            total = term if total is None else total + term
+        return total
     if n & (n - 1):
         return lax.psum(value, "aug")
     bit = 1

time: 131 us -> 129 us (0.985)
  between operations: 25.1 us -> 12.2 us
  waiting for transfers between devices: 57.8 us -> 70.5 us
  local copies, waits for them, and re-layouts: 4.04 us -> 2.25 us
    ppermute x7, waiting for transfers between devices: 1.6 us -> 54.5 us  [ring_reduce_scatter(): acc_l = lax.ppermute(send_l, 'dp', left)]
    ppermute x7, waiting for transfers between devices: 54 us -> 1.64 us  [ring_reduce_scatter(): acc_r = lax.ppermute(send_r, 'dp', right)]
    ppermute x4 -> x6, waiting for transfers between devices: 2.2 us -> 14.3 us  [the longest x1 11.3 us: exchange_four(): lax.ppermute(jnp.concatenate([cols(a ^ 3), grad_rows], axis=1), 'aug', ov...]
    ppermute x7, starting transfers between devices: 11 us -> 3.48 us  [ring_reduce_scatter(): acc_r = lax.ppermute(send_r, 'dp', right)]
    ppermute x7, starting transfers between devices: 4.18 us -> 11.4 us  [ring_reduce_scatter(): acc_l = lax.ppermute(send_l, 'dp', left)]
    dynamic_slice x2 -> x0, local copies, waits for them, and re-layouts: 1.35 us -> none  [the longest x1 0.77 us: block(): ring_arr[(pos - 1 - s) % n]]
    ppermute x4 -> x6, starting transfers between devices: 4.89 us -> 6.1 us  [the longest x1 2.49 us: exchange_four(): lax.ppermute(jnp.concatenate([cols(a ^ 3), grad_rows], axis=1), 'aug', ov...]
    concatenate x2 -> x1, other arithmetic: 2.86 us -> 2.11 us  [exchange_four(): jnp.concatenate([cols(a ^ 3), grad_rows], axis=1)]
  transfers between devices with their start and end apart: 19 -> 21, of which waited for: 9 -> 12; matrix products, arithmetic and copies ran while one was open for 13% -> 12% of each run, Pallas kernels for 0% -> 0%
where the time goes in v4:
time: 129 us; the launch traced here: 128 us
  waiting for transfers between devices  70.5 us (55%)
  starting transfers between devices  21.4 us (17%)
  matrix products  16.4 us (13%)
  between operations  12.2 us (9%)
  other arithmetic  5.25 us (4%)
  local copies, waits for them, and re-layouts  2.25 us (2%)
    ppermute x7, waiting for transfers between devices, ring_reduce_scatter(): acc_l = lax.ppermute(send_l, 'dp', left)  54.5 us
    ppermute x7, starting transfers between devices, ring_reduce_scatter(): acc_l = lax.ppermute(send_l, 'dp', left)  11.4 us
    ppermute x1, waiting for transfers between devices, exchange_four(): lax.ppermute(jnp.concatenate([cols(a ^ 3), grad_rows], axis=1), 'aug', ov...  11.3 us
    dot_general x4, matrix products, per_device(): term = jnp.dot(h_piece.T, g_piece, preferred_element_type=jnp.float32)  8.7 us
    dot_general x4, matrix products, project_back(): lax.dot_general(rows, down_weight, (((1,), (1,)), ((), ())), preferred_el...  7.72 us
    ppermute x7, starting transfers between devices, ring_reduce_scatter(): acc_r = lax.ppermute(send_r, 'dp', right)  3.48 us
  transfers between devices with their start and end apart: 21, of which 12 were waited for; matrix products, arithmetic and copies ran while one was open for 12% of the time, Pallas kernels for 0%

profile of v4, /device:TPU:0, one launch (start us, length us, event | category | flops | bytes accessed | tf_op | source)
XLA Modules:
  0.0 128.0 jit_solution(6439761123261131082)
XLA Ops:
  0.6 0.0 copy-start
  0.7 2.1 %dynamic-slice_bitcast_fusion = (bf16[128,1280]{1,0:T(8,128)(2,1)}, bf16[128,1280]{1,0:T(8,128)(2,1)S(1)}, bf16[128,1280]{1,0:T(8,128)(2,1)S(1)}) fusion(bf16[1,1,128,5120]{3,2,1,0:T(8,128)(2,1)} %param.6, s32[]{:T(128)S(6)} %select_n.574, s32[]{:T(128)S(6)} %select_n.572, s32[]{:T(128)S(6)} %select_n.573), kind=kLoop, calls=%fused_computation.41 | loop fusion | bytes 1966092 | tf_op jit(solution)/shard_map/dynamic_slice | solution.py:97
  2.8 2.1 %pad_maximum_fusion = (bf16[128,2560]{1,0:T(8,128)(2,1)}, bf16[128,2560]{1,0:T(8,128)(2,1)}) fusion(bf16[128,1280]{1,0:T(8,128)(2,1)} %bitcast.77, bf16[128,1280]{1,0:T(8,128)(2,1)S(1)} %get-tuple-element.44, bf16[128,1280]{1,0:T(8,128)(2,1)S(1)} %get-tuple-element.43), kind=kLoop, calls=%fused_computation.19 | loop fusion | flops 2293760 | bytes 2293760 | tf_op jit(solution)/shard_map/concatenate | solution.py:102
  4.9 0.5 collective-permute-start
  5.4 2.5 %collective-permute-start.1 = (bf16[128,2560]{1,0:T(8,128)(2,1)}, bf16[128,2560]{1,0:T(8,128)(2,1)}, u32[]{:S(2)}, u32[]{:S(2)}) collective-permute-start(bf16[128,2560]{1,0:T(8,128)(2,1)} %get-tuple-element.45), channel_id=1, source_target_pairs={{0,16},{8,24},{16,0},{24,8},{1,17},{9,25},{17,1},{25,9},{2,18},{10... | collective-permute-start | bytes 1966088 | tf_op jit(solution)/shard_map/ppermute | solution.py:101
  7.8 0.1 broadcast_in_dim.2
  7.9 2.2 %fusion.4 = bf16[512,1280]{1,0:T(8,128)(2,1)S(1)} fusion(bf16[512,1280]{1,0:T(8,128)(2,1)S(1)} %broadcast_in_dim.2, s32[]{:T(128)S(6)} %select_n.749, bf16[1280,1280]{1,0:T(8,128)(2,1)S(1)} %copy-done, bf16[1,1,128,1280]{3,2,1,0:T(8,128)(2,1)} %param.7), kind=kOutput, calls=%fused_computation.12 | convolution fusion | flops 419594240 | bytes 3932164 | tf_op jit(solution)/shard_map/dot_general | solution.py:17
  10.1 0.0 copy-start.6
  10.1 2.1 %fusion.8 = f32[1280,1280]{1,0:T(8,128)S(1)} fusion(bf16[1,1,128,5120]{3,2,1,0:T(8,128)(2,1)} %param.6, s32[]{:T(128)S(6)} %select_n.571, bf16[1,1,128,1280]{3,2,1,0:T(8,128)(2,1)S(1)} %copy-done.1), kind=kOutput, calls=%fused_computation.39 | convolution fusion | flops 419430400 | bytes 7208964 | tf_op jit(solution)/shard_map/dot_general | solution.py:156
  12.2 11.3 %collective-permute-done.1 = bf16[128,2560]{1,0:T(8,128)(2,1)} collective-permute-done((bf16[128,2560]{1,0:T(8,128)(2,1)}, bf16[128,2560]{1,0:T(8,128)(2,1)}, u32[]{:S(2)}, u32[]{:S(2)}) %collective-permute-start.1) | collective-permute-done | bytes 655392 | tf_op jit(solution)/shard_map/ppermute | solution.py:101
  23.6 1.7 %collective-permute-start.2 = (bf16[128,1280]{1,0:T(8,128)(2,1)S(1)}, bf16[128,1280]{1,0:T(8,128)(2,1)S(1)}, u32[]{:S(2)}, u32[]{:S(2)}) collective-permute-start(bf16[128,1280]{1,0:T(8,128)(2,1)S(1)} %copy-done.6), channel_id=1, source_target_pairs={{0,16},{8,24},{16,0},{24,8},{1,17},{9,25},{17,1},{25,9},{2,18},{10... | collective-permute-start | bytes 983048 | tf_op jit(solution)/shard_map/ppermute | solution.py:106
  25.3 0.0 collective-permute-start.3
  25.3 0.0 collective-permute-done
  25.3 2.1 %convolution_add_fusion.2 = f32[1280,1280]{1,0:T(8,128)S(1)} fusion(f32[1280,1280]{1,0:T(8,128)S(1)} %fusion.8, bf16[128,2560]{1,0:T(8,128)(2,1)} %collective-permute-done), kind=kOutput, calls=%fused_computation.2 | convolution fusion | flops 421068800 | bytes 13762560 | tf_op jit(solution)/shard_map/dot_general | solution.py:156
  27.4 2.2 %fusion.3 = bf16[512,1280]{1,0:T(8,128)(2,1)S(1)} fusion(bf16[512,1280]{1,0:T(8,128)(2,1)S(1)} %fusion.4, s32[]{:T(128)S(6)} %select_n.750, bf16[1280,1280]{1,0:T(8,128)(2,1)S(1)} %copy-done, bf16[128,2560]{1,0:T(8,128)(2,1)} %collective-permute-done), kind=kOutput, calls=%fused_computation.10 | convolution fusion | flops 419594240 | bytes 3932164 | tf_op jit(solution)/shard_map/dot_general | solution.py:17
  29.6 2.2 %fusion.2 = bf16[512,1280]{1,0:T(8,128)(2,1)S(1)} fusion(bf16[512,1280]{1,0:T(8,128)(2,1)S(1)} %fusion.3, s32[]{:T(128)S(6)} %select_n.751, bf16[1280,1280]{1,0:T(8,128)(2,1)S(1)} %copy-done, bf16[128,2560]{1,0:T(8,128)(2,1)} %collective-permute-done.1), kind=kOutput, calls=%fused_computation.8 | convolution fusion | flops 419594240 | bytes 3932164 | tf_op jit(solution)/shard_map/dot_general | solution.py:17
  31.8 1.3 %collective-permute-done.2 = bf16[128,1280]{1,0:T(8,128)(2,1)S(1)} collective-permute-done((bf16[128,1280]{1,0:T(8,128)(2,1)S(1)}, bf16[128,1280]{1,0:T(8,128)(2,1)S(1)}, u32[]{:S(2)}, u32[]{:S(2)}) %collective-permute-start.2) | collective-permute-done | bytes 327712 | tf_op jit(solution)/shard_map/ppermute | solution.py:106
  33.1 2.0 %convolution_add_fusion.1 = f32[1280,1280]{1,0:T(8,128)S(1)} fusion(f32[1280,1280]{1,0:T(8,128)S(1)} %convolution_add_fusion.2, bf16[128,1280]{1,0:T(8,128)(2,1)S(1)} %collective-permute-done.2, bf16[128,2560]{1,0:T(8,128)(2,1)} %collective-permute-done.1), kind=kOutput, calls=%fused_computation.1 | convolution fusion | flops 421068800 | bytes 13762560 | tf_op jit(solution)/shard_map/dot_general | solution.py:156
  35.1 0.0 collective-permute-done.3
  35.1 2.5 %multiply_reduce_fusion = (f32[]{:T(128)}, f32[1280,1280]{1,0:T(8,128)S(1)}) fusion(f32[1280,1280]{1,0:T(8,128)S(1)} %convolution_add_fusion.1, bf16[128,2560]{1,0:T(8,128)(2,1)S(1)} %collective-permute-done.3), kind=kOutput, calls=%fused_computation.4 | convolution fusion | flops 425984000 | bytes 13762564 | tf_op jit(solution)/shard_map/dot_general | solution.py:156
  37.6 0.0 collective-permute-start.4
  37.6 1.5 %collective-permute-start.5 = (f32[1]{0:T(128)}, f32[1]{0:T(128)}, u32[]{:S(2)}, u32[]{:S(2)}) collective-permute-start(f32[1]{0:T(128)} %bitcast.6), channel_id=1, source_target_pairs={{0,16},{8,24},{16,0},{24,8},{1,17},{9,25},{17,1},{25,9},{2,18},{10... | collective-permute-start | bytes 20 | tf_op jit(solution)/shard_map/ppermute | solution.py:121
  39.2 0.3 collective-permute-start.6
  39.5 1.2 fusion.1
  40.7 0.0 copy-start.2
  40.7 0.6 collective-permute-done.5
  41.3 1.1 collective-permute-done.6
  43.7 0.0 collective-permute-done.4
  52.5 0.1 dynamic-slice_multiply_fusion.1
  52.6 1.6 %collective-permute-start.14 = (f32[80,1280]{1,0:T(8,128)S(1)}, f32[80,1280]{1,0:T(8,128)S(1)}, u32[]{:S(2)}, u32[]{:S(2)}) collective-permute-start(f32[80,1280]{1,0:T(8,128)S(1)} %get-tuple-element.41), channel_id=1, source_target_pairs={{0,2},{1,0},{3,1},{5,3},{7,5},{6,7},{4,6},{2,4},{8,10},{9,8},{11,9... | collective-permute-start | bytes 1228808 | tf_op jit(solution)/shard_map/ppermute | solution.py:84
  54.2 0.5 collective-permute-start.7
  54.8 9.3 %collective-permute-done.14 = f32[80,1280]{1,0:T(8,128)S(1)} collective-permute-done((f32[80,1280]{1,0:T(8,128)S(1)}, f32[80,1280]{1,0:T(8,128)S(1)}, u32[]{:S(2)}, u32[]{:S(2)}) %collective-permute-start.14) | collective-permute-done | bytes 409632 | tf_op jit(solution)/shard_map/ppermute | solution.py:84
  64.1 0.1 add.344
  64.2 1.6 %collective-permute-start.15 = (f32[80,1280]{1,0:T(8,128)S(1)}, f32[80,1280]{1,0:T(8,128)S(1)}, u32[]{:S(2)}, u32[]{:S(2)}) collective-permute-start(f32[80,1280]{1,0:T(8,128)S(1)} %add.344), channel_id=1, source_target_pairs={{0,2},{1,0},{3,1},{5,3},{7,5},{6,7},{4,6},{2,4},{8,10},{9,8},{11,9... | collective-permute-start | bytes 1228808 | tf_op jit(solution)/shard_map/ppermute | solution.py:84
  65.8 0.0 collective-permute-done.7
  65.8 0.1 add.317
  65.9 0.5 collective-permute-start.8
  66.5 8.4 %collective-permute-done.15 = f32[80,1280]{1,0:T(8,128)S(1)} collective-permute-done((f32[80,1280]{1,0:T(8,128)S(1)}, f32[80,1280]{1,0:T(8,128)S(1)}, u32[]{:S(2)}, u32[]{:S(2)}) %collective-permute-start.15) | collective-permute-done | bytes 409632 | tf_op jit(solution)/shard_map/ppermute | solution.py:84
  74.8 0.1 add.349
  74.9 1.6 %collective-permute-start.16 = (f32[80,1280]{1,0:T(8,128)S(1)}, f32[80,1280]{1,0:T(8,128)S(1)}, u32[]{:S(2)}, u32[]{:S(2)}) collective-permute-start(f32[80,1280]{1,0:T(8,128)S(1)} %add.349), channel_id=1, source_target_pairs={{0,2},{1,0},{3,1},{5,3},{7,5},{6,7},{4,6},{2,4},{8,10},{9,8},{11,9... | collective-permute-start | bytes 1228808 | tf_op jit(solution)/shard_map/ppermute | solution.py:84
  76.5 0.0 collective-permute-done.8
  76.6 0.5 collective-permute-start.9
  77.1 7.5 %collective-permute-done.16 = f32[80,1280]{1,0:T(8,128)S(1)} collective-permute-done((f32[80,1280]{1,0:T(8,128)S(1)}, f32[80,1280]{1,0:T(8,128)S(1)}, u32[]{:S(2)}, u32[]{:S(2)}) %collective-permute-start.16) | collective-permute-done | bytes 409632 | tf_op jit(solution)/shard_map/ppermute | solution.py:84
  84.7 1.6 %collective-permute-start.17 = (f32[80,1280]{1,0:T(8,128)S(1)}, f32[80,1280]{1,0:T(8,128)S(1)}, u32[]{:S(2)}, u32[]{:S(2)}) collective-permute-start(f32[80,1280]{1,0:T(8,128)S(1)} %add.354), channel_id=1, source_target_pairs={{0,2},{1,0},{3,1},{5,3},{7,5},{6,7},{4,6},{2,4},{8,10},{9,8},{11,9... | collective-permute-start | bytes 1228808 | tf_op jit(solution)/shard_map/ppermute | solution.py:84
  86.3 0.0 collective-permute-done.9
  86.3 0.5 collective-permute-start.10
  86.9 7.3 %collective-permute-done.17 = f32[80,1280]{1,0:T(8,128)S(1)} collective-permute-done((f32[80,1280]{1,0:T(8,128)S(1)}, f32[80,1280]{1,0:T(8,128)S(1)}, u32[]{:S(2)}, u32[]{:S(2)}) %collective-permute-start.17) | collective-permute-done | bytes 409632 | tf_op jit(solution)/shard_map/ppermute | solution.py:84
  94.3 1.6 %collective-permute-start.18 = (f32[80,1280]{1,0:T(8,128)S(1)}, f32[80,1280]{1,0:T(8,128)S(1)}, u32[]{:S(2)}, u32[]{:S(2)}) collective-permute-start(f32[80,1280]{1,0:T(8,128)S(1)} %add.359), channel_id=1, source_target_pairs={{0,2},{1,0},{3,1},{5,3},{7,5},{6,7},{4,6},{2,4},{8,10},{9,8},{11,9... | collective-permute-start | bytes 1228808 | tf_op jit(solution)/shard_map/ppermute | solution.py:84
  95.9 0.0 collective-permute-done.10
  96.0 0.5 collective-permute-start.11
  96.6 7.6 %collective-permute-done.18 = f32[80,1280]{1,0:T(8,128)S(1)} collective-permute-done((f32[80,1280]{1,0:T(8,128)S(1)}, f32[80,1280]{1,0:T(8,128)S(1)}, u32[]{:S(2)}, u32[]{:S(2)}) %collective-permute-start.18) | collective-permute-done | bytes 409632 | tf_op jit(solution)/shard_map/ppermute | solution.py:84
  104.2 1.6 %collective-permute-start.19 = (f32[80,1280]{1,0:T(8,128)S(1)}, f32[80,1280]{1,0:T(8,128)S(1)}, u32[]{:S(2)}, u32[]{:S(2)}) collective-permute-start(f32[80,1280]{1,0:T(8,128)S(1)} %add.364), channel_id=1, source_target_pairs={{0,2},{1,0},{3,1},{5,3},{7,5},{6,7},{4,6},{2,4},{8,10},{9,8},{11,9... | collective-permute-start | bytes 1228808 | tf_op jit(solution)/shard_map/ppermute | solution.py:84
  105.8 0.0 collective-permute-done.11
  105.9 0.5 collective-permute-start.12
  106.5 0.0 copy-start.3
  106.5 0.0 copy-start.4
  106.5 0.0 copy-start.5
  106.5 8.7 %collective-permute-done.19 = f32[80,1280]{1,0:T(8,128)S(1)} collective-permute-done((f32[80,1280]{1,0:T(8,128)S(1)}, f32[80,1280]{1,0:T(8,128)S(1)}, u32[]{:S(2)}, u32[]{:S(2)}) %collective-permute-start.19) | collective-permute-done | bytes 409632 | tf_op jit(solution)/shard_map/ppermute | solution.py:84
  115.2 1.6 %collective-permute-start.20 = (f32[80,1280]{1,0:T(8,128)S(1)}, f32[80,1280]{1,0:T(8,128)S(1)}, u32[]{:S(2)}, u32[]{:S(2)}) collective-permute-start(f32[80,1280]{1,0:T(8,128)S(1)} %add.369), channel_id=1, source_target_pairs={{0,2},{1,0},{3,1},{5,3},{7,5},{6,7},{4,6},{2,4},{8,10},{9,8},{11,9... | collective-permute-start | bytes 1228808 | tf_op jit(solution)/shard_map/ppermute | solution.py:84
  116.8 0.0 collective-permute-done.12
  116.9 0.5 collective-permute-start.13
  117.5 5.7 %collective-permute-done.20 = f32[80,1280]{1,0:T(8,128)S(1)} collective-permute-done((f32[80,1280]{1,0:T(8,128)S(1)}, f32[80,1280]{1,0:T(8,128)S(1)}, u32[]{:S(2)}, u32[]{:S(2)}) %collective-permute-start.20) | collective-permute-done | bytes 409632 | tf_op jit(solution)/shard_map/ppermute | solution.py:84
  123.3 1.6 %collective-permute-done.13 = f32[80,1280]{1,0:T(8,128)S(1)} collective-permute-done((f32[80,1280]{1,0:T(8,128)S(1)}, f32[80,1280]{1,0:T(8,128)S(1)}, u32[]{:S(2)}, u32[]{:S(2)}) %collective-permute-start.13) | collective-permute-done | bytes 409632 | tf_op jit(solution)/shard_map/ppermute | solution.py:83
  125.0 1.9 %add_divide_fusion = (f32[160,1280]{1,0:T(8,128)}, f32[160,1280]{1,0:T(8,128)}, f32[160,1280]{1,0:T(8,128)}, f32[160,1280]{1,0:T(8,128)}) fusion(f32[160,1280]{1,0:T(8,128)S(1)} %copy-done.3, f32[160,1280]{1,0:T(8,128)S(1)} %copy-done.4, f32[160,1280]{1,0:T(8,128)S(1)} %copy-done.5, f32[80,1280]{1,0:T(8,128)S(1)} %add.374, f32[80,1280]{1,0:T(8,128)S(1)} %add.335), kind=kLoop, calls=%fused_computation.16 | loop fusion | flops 3072000 | bytes 6553600 | tf_op jit(solution)/shard_map/div | solution.py:193
  (33 shorter events, 1.0 us)
Async XLA Ops:
  0.6 7.3 %copy-start = (bf16[1280,1280]{1,0:T(8,128)(2,1)S(1)}, bf16[1280,1280]{1,0:T(8,128)(2,1)}, u32[]{:S(2)}) copy-start(bf16[1280,1280]{1,0:T(8,128)(2,1)} %param.8) | copy-start | bytes 9830404
  4.9 20.4 %collective-permute-start = (bf16[128,2560]{1,0:T(8,128)(2,1)}, bf16[128,2560]{1,0:T(8,128)(2,1)}, u32[]{:S(2)}, u32[]{:S(2)}) collective-permute-start(bf16[128,2560]{1,0:T(8,128)(2,1)} %get-tuple-element.46), channel_id=1, source_target_pairs={{0,8},{8,0},{16,24},{24,16},{1,9},{9,1},{17,25},{25,17},{2,10},{10... | collective-permute-start | bytes 1966088 | tf_op jit(solution)/shard_map/ppermute | solution.py:104
  5.4 18.2 %collective-permute-start.1 = (bf16[128,2560]{1,0:T(8,128)(2,1)}, bf16[128,2560]{1,0:T(8,128)(2,1)}, u32[]{:S(2)}, u32[]{:S(2)}) collective-permute-start(bf16[128,2560]{1,0:T(8,128)(2,1)} %get-tuple-element.45), channel_id=1, source_target_pairs={{0,16},{8,24},{16,0},{24,8},{1,17},{9,25},{17,1},{25,9},{2,18},{10... | collective-permute-start | bytes 1966088 | tf_op jit(solution)/shard_map/ppermute | solution.py:101
  7.8 2.3 %copy-start.1 = (bf16[1,1,128,1280]{3,2,1,0:T(8,128)(2,1)S(1)}, bf16[1,1,128,1280]{3,2,1,0:T(8,128)(2,1)}, u32[]{:S(2)}) copy-start(bf16[1,1,128,1280]{3,2,1,0:T(8,128)(2,1)} %param.7) | copy-start | bytes 983044
  10.1 13.4 %copy-start.6 = (bf16[128,1280]{1,0:T(8,128)(2,1)S(1)}, bf16[128,1280]{1,0:T(8,128)(2,1)}, u32[]{:S(2)}) copy-start(bf16[128,1280]{1,0:T(8,128)(2,1)} %get-tuple-element.21) | copy-start | bytes 983044
  23.6 9.5 %collective-permute-start.2 = (bf16[128,1280]{1,0:T(8,128)(2,1)S(1)}, bf16[128,1280]{1,0:T(8,128)(2,1)S(1)}, u32[]{:S(2)}, u32[]{:S(2)}) collective-permute-start(bf16[128,1280]{1,0:T(8,128)(2,1)S(1)} %copy-done.6), channel_id=1, source_target_pairs={{0,16},{8,24},{16,0},{24,8},{1,17},{9,25},{17,1},{25,9},{2,18},{10... | collective-permute-start | bytes 983048 | tf_op jit(solution)/shard_map/ppermute | solution.py:106
  25.3 9.8 %collective-permute-start.3 = (bf16[128,2560]{1,0:T(8,128)(2,1)}, bf16[128,2560]{1,0:T(8,128)(2,1)S(1)}, u32[]{:S(2)}, u32[]{:S(2)}) collective-permute-start(bf16[128,2560]{1,0:T(8,128)(2,1)} %collective-permute-done.1), channel_id=1, source_target_pairs={{0,8},{8,0},{16,24},{24,16},{1,9},{9,1},{17,25},{25,17},{2,10},{10... | collective-permute-start | bytes 1966088 | tf_op jit(solution)/shard_map/ppermute | solution.py:107
  37.6 6.0 %collective-permute-start.4 = (f32[1]{0:T(128)}, f32[1]{0:T(128)}, u32[]{:S(2)}, u32[]{:S(2)}) collective-permute-start(f32[1]{0:T(128)} %bitcast.6), channel_id=1, source_target_pairs={{0,8},{8,0},{16,24},{24,16},{1,9},{9,1},{17,25},{25,17},{2,10},{10... | collective-permute-start | bytes 20 | tf_op jit(solution)/shard_map/ppermute | solution.py:121
  37.6 3.6 %collective-permute-start.5 = (f32[1]{0:T(128)}, f32[1]{0:T(128)}, u32[]{:S(2)}, u32[]{:S(2)}) collective-permute-start(f32[1]{0:T(128)} %bitcast.6), channel_id=1, source_target_pairs={{0,16},{8,24},{16,0},{24,8},{1,17},{9,25},{17,1},{25,9},{2,18},{10... | collective-permute-start | bytes 20 | tf_op jit(solution)/shard_map/ppermute | solution.py:121
  39.2 3.2 %collective-permute-start.6 = (f32[1]{0:T(128)}, f32[1]{0:T(128)}, u32[]{:S(2)}, u32[]{:S(2)}) collective-permute-start(f32[1]{0:T(128)} %bitcast.6), channel_id=1, source_target_pairs={{0,24},{8,16},{16,8},{24,0},{1,25},{9,17},{17,9},{25,1},{2,26},{10... | collective-permute-start | bytes 20 | tf_op jit(solution)/shard_map/ppermute | solution.py:121
  40.7 25.7 %copy-start.2 = (bf16[512,1280]{1,0:T(8,128)(2,1)}, bf16[512,1280]{1,0:T(8,128)(2,1)S(1)}, u32[]{:S(2)}) copy-start(bf16[512,1280]{1,0:T(8,128)(2,1)S(1)} %fusion.1) | copy-start | bytes 3932164
  52.6 11.5 %collective-permute-start.14 = (f32[80,1280]{1,0:T(8,128)S(1)}, f32[80,1280]{1,0:T(8,128)S(1)}, u32[]{:S(2)}, u32[]{:S(2)}) collective-permute-start(f32[80,1280]{1,0:T(8,128)S(1)} %get-tuple-element.41), channel_id=1, source_target_pairs={{0,2},{1,0},{3,1},{5,3},{7,5},{6,7},{4,6},{2,4},{8,10},{9,8},{11,9... | collective-permute-start | bytes 1228808 | tf_op jit(solution)/shard_map/ppermute | solution.py:84
  54.2 11.6 %collective-permute-start.7 = (f32[80,1280]{1,0:T(8,128)S(1)}, f32[80,1280]{1,0:T(8,128)S(1)}, u32[]{:S(2)}, u32[]{:S(2)}) collective-permute-start(f32[80,1280]{1,0:T(8,128)S(1)} %get-tuple-element.40), channel_id=1, source_target_pairs={{0,1},{1,3},{3,5},{5,7},{7,6},{6,4},{4,2},{2,0},{8,9},{9,11},{11,1... | collective-permute-start | bytes 1228808 | tf_op jit(solution)/shard_map/ppermute | solution.py:83
  64.2 10.7 %collective-permute-start.15 = (f32[80,1280]{1,0:T(8,128)S(1)}, f32[80,1280]{1,0:T(8,128)S(1)}, u32[]{:S(2)}, u32[]{:S(2)}) collective-permute-start(f32[80,1280]{1,0:T(8,128)S(1)} %add.344), channel_id=1, source_target_pairs={{0,2},{1,0},{3,1},{5,3},{7,5},{6,7},{4,6},{2,4},{8,10},{9,8},{11,9... | collective-permute-start | bytes 1228808 | tf_op jit(solution)/shard_map/ppermute | solution.py:84
  65.9 10.7 %collective-permute-start.8 = (f32[80,1280]{1,0:T(8,128)S(1)}, f32[80,1280]{1,0:T(8,128)S(1)}, u32[]{:S(2)}, u32[]{:S(2)}) collective-permute-start(f32[80,1280]{1,0:T(8,128)S(1)} %add.317), channel_id=1, source_target_pairs={{0,1},{1,3},{3,5},{5,7},{7,6},{6,4},{4,2},{2,0},{8,9},{9,11},{11,1... | collective-permute-start | bytes 1228808 | tf_op jit(solution)/shard_map/ppermute | solution.py:83
  74.9 9.7 %collective-permute-start.16 = (f32[80,1280]{1,0:T(8,128)S(1)}, f32[80,1280]{1,0:T(8,128)S(1)}, u32[]{:S(2)}, u32[]{:S(2)}) collective-permute-start(f32[80,1280]{1,0:T(8,128)S(1)} %add.349), channel_id=1, source_target_pairs={{0,2},{1,0},{3,1},{5,3},{7,5},{6,7},{4,6},{2,4},{8,10},{9,8},{11,9... | collective-permute-start | bytes 1228808 | tf_op jit(solution)/shard_map/ppermute | solution.py:84
  76.6 9.7 %collective-permute-start.9 = (f32[80,1280]{1,0:T(8,128)S(1)}, f32[80,1280]{1,0:T(8,128)S(1)}, u32[]{:S(2)}, u32[]{:S(2)}) collective-permute-start(f32[80,1280]{1,0:T(8,128)S(1)} %add.320), channel_id=1, source_target_pairs={{0,1},{1,3},{3,5},{5,7},{7,6},{6,4},{4,2},{2,0},{8,9},{9,11},{11,1... | collective-permute-start | bytes 1228808 | tf_op jit(solution)/shard_map/ppermute | solution.py:83
  84.7 9.6 %collective-permute-start.17 = (f32[80,1280]{1,0:T(8,128)S(1)}, f32[80,1280]{1,0:T(8,128)S(1)}, u32[]{:S(2)}, u32[]{:S(2)}) collective-permute-start(f32[80,1280]{1,0:T(8,128)S(1)} %add.354), channel_id=1, source_target_pairs={{0,2},{1,0},{3,1},{5,3},{7,5},{6,7},{4,6},{2,4},{8,10},{9,8},{11,9... | collective-permute-start | bytes 1228808 | tf_op jit(solution)/shard_map/ppermute | solution.py:84
  86.3 9.6 %collective-permute-start.10 = (f32[80,1280]{1,0:T(8,128)S(1)}, f32[80,1280]{1,0:T(8,128)S(1)}, u32[]{:S(2)}, u32[]{:S(2)}) collective-permute-start(f32[80,1280]{1,0:T(8,128)S(1)} %add.323), channel_id=1, source_target_pairs={{0,1},{1,3},{3,5},{5,7},{7,6},{6,4},{4,2},{2,0},{8,9},{9,11},{11,1... | collective-permute-start | bytes 1228808 | tf_op jit(solution)/shard_map/ppermute | solution.py:83
  94.3 9.9 %collective-permute-start.18 = (f32[80,1280]{1,0:T(8,128)S(1)}, f32[80,1280]{1,0:T(8,128)S(1)}, u32[]{:S(2)}, u32[]{:S(2)}) collective-permute-start(f32[80,1280]{1,0:T(8,128)S(1)} %add.359), channel_id=1, source_target_pairs={{0,2},{1,0},{3,1},{5,3},{7,5},{6,7},{4,6},{2,4},{8,10},{9,8},{11,9... | collective-permute-start | bytes 1228808 | tf_op jit(solution)/shard_map/ppermute | solution.py:84
  96.0 9.9 %collective-permute-start.11 = (f32[80,1280]{1,0:T(8,128)S(1)}, f32[80,1280]{1,0:T(8,128)S(1)}, u32[]{:S(2)}, u32[]{:S(2)}) collective-permute-start(f32[80,1280]{1,0:T(8,128)S(1)} %add.326), channel_id=1, source_target_pairs={{0,1},{1,3},{3,5},{5,7},{7,6},{6,4},{4,2},{2,0},{8,9},{9,11},{11,1... | collective-permute-start | bytes 1228808 | tf_op jit(solution)/shard_map/ppermute | solution.py:83
  104.2 11.0 %collective-permute-start.19 = (f32[80,1280]{1,0:T(8,128)S(1)}, f32[80,1280]{1,0:T(8,128)S(1)}, u32[]{:S(2)}, u32[]{:S(2)}) collective-permute-start(f32[80,1280]{1,0:T(8,128)S(1)} %add.364), channel_id=1, source_target_pairs={{0,2},{1,0},{3,1},{5,3},{7,5},{6,7},{4,6},{2,4},{8,10},{9,8},{11,9... | collective-permute-start | bytes 1228808 | tf_op jit(solution)/shard_map/ppermute | solution.py:84
  105.9 11.0 %collective-permute-start.12 = (f32[80,1280]{1,0:T(8,128)S(1)}, f32[80,1280]{1,0:T(8,128)S(1)}, u32[]{:S(2)}, u32[]{:S(2)}) collective-permute-start(f32[80,1280]{1,0:T(8,128)S(1)} %add.329), channel_id=1, source_target_pairs={{0,1},{1,3},{3,5},{5,7},{7,6},{6,4},{4,2},{2,0},{8,9},{9,11},{11,1... | collective-permute-start | bytes 1228808 | tf_op jit(solution)/shard_map/ppermute | solution.py:83
  106.5 18.5 %copy-start.3 = (f32[160,1280]{1,0:T(8,128)S(1)}, f32[160,1280]{1,0:T(8,128)}, u32[]{:S(2)}) copy-start(f32[160,1280]{1,0:T(8,128)} %param.11) | copy-start | bytes 2457604
  106.5 18.5 %copy-start.4 = (f32[160,1280]{1,0:T(8,128)S(1)}, f32[160,1280]{1,0:T(8,128)}, u32[]{:S(2)}) copy-start(f32[160,1280]{1,0:T(8,128)} %param.10) | copy-start | bytes 2457604
  106.5 18.5 %copy-start.5 = (f32[160,1280]{1,0:T(8,128)S(1)}, f32[160,1280]{1,0:T(8,128)}, u32[]{:S(2)}) copy-start(f32[160,1280]{1,0:T(8,128)} %param.9) | copy-start | bytes 2457604
  115.2 8.0 %collective-permute-start.20 = (f32[80,1280]{1,0:T(8,128)S(1)}, f32[80,1280]{1,0:T(8,128)S(1)}, u32[]{:S(2)}, u32[]{:S(2)}) collective-permute-start(f32[80,1280]{1,0:T(8,128)S(1)} %add.369), channel_id=1, source_target_pairs={{0,2},{1,0},{3,1},{5,3},{7,5},{6,7},{4,6},{2,4},{8,10},{9,8},{11,9... | collective-permute-start | bytes 1228808 | tf_op jit(solution)/shard_map/ppermute | solution.py:84
  116.9 8.0 %collective-permute-start.13 = (f32[80,1280]{1,0:T(8,128)S(1)}, f32[80,1280]{1,0:T(8,128)S(1)}, u32[]{:S(2)}, u32[]{:S(2)}) collective-permute-start(f32[80,1280]{1,0:T(8,128)S(1)} %add.332), channel_id=1, source_target_pairs={{0,1},{1,3},{3,5},{5,7},{7,6},{6,4},{4,2},{2,0},{8,9},{9,11},{11,1... | collective-permute-start | bytes 1228808 | tf_op jit(solution)/shard_map/ppermute | solution.py:83

commit v5 on v4

--- a/solution.py
+++ b/solution.py
@@ -115,17 +115,10 @@
 
 def butterfly_sum(value, n):
     if n == 4:
-        a = lax.axis_index("aug")
-        got = {0: value}
+        got = {}
         for m in (1, 2, 3):
             got[m] = lax.ppermute(value, "aug", [(i, i ^ m) for i in range(4)])
-        total = None
-        for k in range(4):
-            term = got[3]
-            for m in (2, 1, 0):
-                term = jnp.where((a ^ m) == k, got[m], term)
-            total = term if total is None else total + term
-        return total
+        return (value + got[1]) + (got[2] + got[3])
     if n & (n - 1):
         return lax.psum(value, "aug")
     bit = 1

time: 129 us -> 120 us (0.930)
  between operations: 12.2 us -> 4.72 us
  waiting for transfers between devices: 70.5 us -> 69.2 us
    ppermute x3, waiting for transfers between devices: 1.68 us -> 0.38 us  [butterfly_sum(): got[m] = lax.ppermute(value, 'aug', [(i, i ^ m) for i in range(4)])]
  transfers between devices with their start and end apart: 21 -> 21, of which waited for: 12 -> 11; matrix products, arithmetic and copies ran while one was open for 12% -> 13% of each run, Pallas kernels for 0% -> 0%
where the time goes in v5:
time: 120 us; the launch traced here: 119 us
  waiting for transfers between devices  69.2 us (58%)
  starting transfers between devices  21.4 us (18%)
  matrix products  16.4 us (14%)
  other arithmetic  5.25 us (4%)
  between operations  4.72 us (4%)
  local copies, waits for them, and re-layouts  2.25 us (2%)
    ppermute x7, waiting for transfers between devices, ring_reduce_scatter(): acc_l = lax.ppermute(send_l, 'dp', left)  54.5 us
    ppermute x7, starting transfers between devices, ring_reduce_scatter(): acc_l = lax.ppermute(send_l, 'dp', left)  11.4 us
    ppermute x1, waiting for transfers between devices, exchange_four(): lax.ppermute(jnp.concatenate([cols(a ^ 3), grad_rows], axis=1), 'aug', ov...  11.3 us
    dot_general x4, matrix products, per_device(): term = jnp.dot(h_piece.T, g_piece, preferred_element_type=jnp.float32)  8.7 us
    dot_general x4, matrix products, project_back(): lax.dot_general(rows, down_weight, (((1,), (1,)), ((), ())), preferred_el...  7.72 us
    ppermute x7, starting transfers between devices, ring_reduce_scatter(): acc_r = lax.ppermute(send_r, 'dp', right)  3.46 us
    ppermute x1, starting transfers between devices, exchange_four(): lax.ppermute(jnp.concatenate([cols(a ^ 3), grad_rows], axis=1), 'aug', ov...  2.49 us
  transfers between devices with their start and end apart: 21, of which 11 were waited for; matrix products, arithmetic and copies ran while one was open for 13% of the time, Pallas kernels for 0%

profile of v5, /device:TPU:0, one launch (start us, length us, event | category | flops | bytes accessed | tf_op | source)
XLA Modules:
  0.0 119.2 jit_solution(5721233653630535598)
XLA Ops:
  0.6 0.0 copy-start
  0.7 2.1 %dynamic-slice_bitcast_fusion = (bf16[128,1280]{1,0:T(8,128)(2,1)}, bf16[128,1280]{1,0:T(8,128)(2,1)S(1)}, bf16[128,1280]{1,0:T(8,128)(2,1)S(1)}) fusion(bf16[1,1,128,5120]{3,2,1,0:T(8,128)(2,1)} %param.6, s32[]{:T(128)S(6)} %select_n.499, s32[]{:T(128)S(6)} %select_n.497, s32[]{:T(128)S(6)} %select_n.498), kind=kLoop, calls=%fused_computation.41 | loop fusion | bytes 1966092 | tf_op jit(solution)/shard_map/dynamic_slice | solution.py:97
  2.8 2.1 %pad_maximum_fusion = (bf16[128,2560]{1,0:T(8,128)(2,1)}, bf16[128,2560]{1,0:T(8,128)(2,1)}) fusion(bf16[128,1280]{1,0:T(8,128)(2,1)} %bitcast.65, bf16[128,1280]{1,0:T(8,128)(2,1)S(1)} %get-tuple-element.44, bf16[128,1280]{1,0:T(8,128)(2,1)S(1)} %get-tuple-element.43), kind=kLoop, calls=%fused_computation.19 | loop fusion | flops 2293760 | bytes 2293760 | tf_op jit(solution)/shard_map/concatenate | solution.py:102
  4.9 0.5 collective-permute-start
  5.4 2.5 %collective-permute-start.1 = (bf16[128,2560]{1,0:T(8,128)(2,1)}, bf16[128,2560]{1,0:T(8,128)(2,1)}, u32[]{:S(2)}, u32[]{:S(2)}) collective-permute-start(bf16[128,2560]{1,0:T(8,128)(2,1)} %get-tuple-element.45), channel_id=1, source_target_pairs={{0,16},{8,24},{16,0},{24,8},{1,17},{9,25},{17,1},{25,9},{2,18},{10... | collective-permute-start | bytes 1966088 | tf_op jit(solution)/shard_map/ppermute | solution.py:101
  7.8 0.1 broadcast_in_dim.2
  7.9 2.2 %fusion.4 = bf16[512,1280]{1,0:T(8,128)(2,1)S(1)} fusion(bf16[512,1280]{1,0:T(8,128)(2,1)S(1)} %broadcast_in_dim.2, s32[]{:T(128)S(6)} %select_n.651, bf16[1280,1280]{1,0:T(8,128)(2,1)S(1)} %copy-done, bf16[1,1,128,1280]{3,2,1,0:T(8,128)(2,1)} %param.7), kind=kOutput, calls=%fused_computation.12 | convolution fusion | flops 419594240 | bytes 3932164 | tf_op jit(solution)/shard_map/dot_general | solution.py:17
  10.1 0.0 copy-start.6
  10.1 2.1 %fusion.8 = f32[1280,1280]{1,0:T(8,128)S(1)} fusion(bf16[1,1,128,5120]{3,2,1,0:T(8,128)(2,1)} %param.6, s32[]{:T(128)S(6)} %select_n.496, bf16[1,1,128,1280]{3,2,1,0:T(8,128)(2,1)S(1)} %copy-done.1), kind=kOutput, calls=%fused_computation.39 | convolution fusion | flops 419430400 | bytes 7208964 | tf_op jit(solution)/shard_map/dot_general | solution.py:149
  12.2 11.3 %collective-permute-done.1 = bf16[128,2560]{1,0:T(8,128)(2,1)} collective-permute-done((bf16[128,2560]{1,0:T(8,128)(2,1)}, bf16[128,2560]{1,0:T(8,128)(2,1)}, u32[]{:S(2)}, u32[]{:S(2)}) %collective-permute-start.1) | collective-permute-done | bytes 655392 | tf_op jit(solution)/shard_map/ppermute | solution.py:101
  23.6 1.7 %collective-permute-start.2 = (bf16[128,1280]{1,0:T(8,128)(2,1)S(1)}, bf16[128,1280]{1,0:T(8,128)(2,1)S(1)}, u32[]{:S(2)}, u32[]{:S(2)}) collective-permute-start(bf16[128,1280]{1,0:T(8,128)(2,1)S(1)} %copy-done.6), channel_id=1, source_target_pairs={{0,16},{8,24},{16,0},{24,8},{1,17},{9,25},{17,1},{25,9},{2,18},{10... | collective-permute-start | bytes 983048 | tf_op jit(solution)/shard_map/ppermute | solution.py:106
  25.3 0.0 collective-permute-start.3
  25.3 0.0 collective-permute-done
  25.3 2.1 %convolution_add_fusion.2 = f32[1280,1280]{1,0:T(8,128)S(1)} fusion(f32[1280,1280]{1,0:T(8,128)S(1)} %fusion.8, bf16[128,2560]{1,0:T(8,128)(2,1)} %collective-permute-done), kind=kOutput, calls=%fused_computation.2 | convolution fusion | flops 421068800 | bytes 13762560 | tf_op jit(solution)/shard_map/dot_general | solution.py:149
  27.4 2.2 %fusion.3 = bf16[512,1280]{1,0:T(8,128)(2,1)S(1)} fusion(bf16[512,1280]{1,0:T(8,128)(2,1)S(1)} %fusion.4, s32[]{:T(128)S(6)} %select_n.652, bf16[1280,1280]{1,0:T(8,128)(2,1)S(1)} %copy-done, bf16[128,2560]{1,0:T(8,128)(2,1)} %collective-permute-done), kind=kOutput, calls=%fused_computation.10 | convolution fusion | flops 419594240 | bytes 3932164 | tf_op jit(solution)/shard_map/dot_general | solution.py:17
  29.6 2.2 %fusion.2 = bf16[512,1280]{1,0:T(8,128)(2,1)S(1)} fusion(bf16[512,1280]{1,0:T(8,128)(2,1)S(1)} %fusion.3, s32[]{:T(128)S(6)} %select_n.653, bf16[1280,1280]{1,0:T(8,128)(2,1)S(1)} %copy-done, bf16[128,2560]{1,0:T(8,128)(2,1)} %collective-permute-done.1), kind=kOutput, calls=%fused_computation.8 | convolution fusion | flops 419594240 | bytes 3932164 | tf_op jit(solution)/shard_map/dot_general | solution.py:17
  31.8 1.3 %collective-permute-done.2 = bf16[128,1280]{1,0:T(8,128)(2,1)S(1)} collective-permute-done((bf16[128,1280]{1,0:T(8,128)(2,1)S(1)}, bf16[128,1280]{1,0:T(8,128)(2,1)S(1)}, u32[]{:S(2)}, u32[]{:S(2)}) %collective-permute-start.2) | collective-permute-done | bytes 327712 | tf_op jit(solution)/shard_map/ppermute | solution.py:106
  33.1 2.0 %convolution_add_fusion.1 = f32[1280,1280]{1,0:T(8,128)S(1)} fusion(f32[1280,1280]{1,0:T(8,128)S(1)} %convolution_add_fusion.2, bf16[128,1280]{1,0:T(8,128)(2,1)S(1)} %collective-permute-done.2, bf16[128,2560]{1,0:T(8,128)(2,1)} %collective-permute-done.1), kind=kOutput, calls=%fused_computation.1 | convolution fusion | flops 421068800 | bytes 13762560 | tf_op jit(solution)/shard_map/dot_general | solution.py:149
  35.1 0.0 collective-permute-done.3
  35.1 2.5 %multiply_reduce_fusion = (f32[]{:T(128)}, f32[1280,1280]{1,0:T(8,128)S(1)}) fusion(f32[1280,1280]{1,0:T(8,128)S(1)} %convolution_add_fusion.1, bf16[128,2560]{1,0:T(8,128)(2,1)S(1)} %collective-permute-done.3), kind=kOutput, calls=%fused_computation.4 | convolution fusion | flops 425984000 | bytes 13762564 | tf_op jit(solution)/shard_map/dot_general | solution.py:149
  37.6 0.0 collective-permute-start.4
  37.6 1.5 %collective-permute-start.5 = (f32[1]{0:T(128)}, f32[1]{0:T(128)}, u32[]{:S(2)}, u32[]{:S(2)}) collective-permute-start(f32[1]{0:T(128)} %bitcast.5), channel_id=1, source_target_pairs={{0,16},{8,24},{16,0},{24,8},{1,17},{9,25},{17,1},{25,9},{2,18},{10... | collective-permute-start | bytes 20 | tf_op jit(solution)/shard_map/ppermute | solution.py:120
  39.2 0.3 collective-permute-start.6
  39.5 1.2 %fusion.1 = bf16[512,1280]{1,0:T(8,128)(2,1)S(1)} fusion(bf16[512,1280]{1,0:T(8,128)(2,1)S(1)} %fusion.2, s32[]{:T(128)S(6)} %select_n.654, bf16[1280,1280]{1,0:T(8,128)(2,1)S(1)} %copy-done, bf16[128,2560]{1,0:T(8,128)(2,1)S(1)} %collective-permute-done.3), kind=kOutput, calls=%fused_computation.6 | convolution fusion | flops 419594240 | bytes 3932164 | tf_op jit(solution)/shard_map/dot_general | solution.py:17
  40.7 0.0 copy-start.2
  40.7 0.0 collective-permute-done.4
  42.0 0.0 collective-permute-done.5
  42.0 0.4 collective-permute-done.6
  43.7 0.1 dynamic-slice_multiply_fusion.1
  43.8 1.6 %collective-permute-start.14 = (f32[80,1280]{1,0:T(8,128)S(1)}, f32[80,1280]{1,0:T(8,128)S(1)}, u32[]{:S(2)}, u32[]{:S(2)}) collective-permute-start(f32[80,1280]{1,0:T(8,128)S(1)} %get-tuple-element.41), channel_id=1, source_target_pairs={{0,2},{1,0},{3,1},{5,3},{7,5},{6,7},{4,6},{2,4},{8,10},{9,8},{11,9... | collective-permute-start | bytes 1228808 | tf_op jit(solution)/shard_map/ppermute | solution.py:84
  45.4 0.4 collective-permute-start.7
  46.0 9.3 %collective-permute-done.14 = f32[80,1280]{1,0:T(8,128)S(1)} collective-permute-done((f32[80,1280]{1,0:T(8,128)S(1)}, f32[80,1280]{1,0:T(8,128)S(1)}, u32[]{:S(2)}, u32[]{:S(2)}) %collective-permute-start.14) | collective-permute-done | bytes 409632 | tf_op jit(solution)/shard_map/ppermute | solution.py:84
  55.3 0.1 add.344
  55.4 1.6 %collective-permute-start.15 = (f32[80,1280]{1,0:T(8,128)S(1)}, f32[80,1280]{1,0:T(8,128)S(1)}, u32[]{:S(2)}, u32[]{:S(2)}) collective-permute-start(f32[80,1280]{1,0:T(8,128)S(1)} %add.344), channel_id=1, source_target_pairs={{0,2},{1,0},{3,1},{5,3},{7,5},{6,7},{4,6},{2,4},{8,10},{9,8},{11,9... | collective-permute-start | bytes 1228808 | tf_op jit(solution)/shard_map/ppermute | solution.py:84
  57.0 0.0 collective-permute-done.7
  57.0 0.1 add.317
  57.1 0.5 collective-permute-start.8
  57.6 8.4 %collective-permute-done.15 = f32[80,1280]{1,0:T(8,128)S(1)} collective-permute-done((f32[80,1280]{1,0:T(8,128)S(1)}, f32[80,1280]{1,0:T(8,128)S(1)}, u32[]{:S(2)}, u32[]{:S(2)}) %collective-permute-start.15) | collective-permute-done | bytes 409632 | tf_op jit(solution)/shard_map/ppermute | solution.py:84
  66.0 0.1 add.349
  66.1 1.6 %collective-permute-start.16 = (f32[80,1280]{1,0:T(8,128)S(1)}, f32[80,1280]{1,0:T(8,128)S(1)}, u32[]{:S(2)}, u32[]{:S(2)}) collective-permute-start(f32[80,1280]{1,0:T(8,128)S(1)} %add.349), channel_id=1, source_target_pairs={{0,2},{1,0},{3,1},{5,3},{7,5},{6,7},{4,6},{2,4},{8,10},{9,8},{11,9... | collective-permute-start | bytes 1228808 | tf_op jit(solution)/shard_map/ppermute | solution.py:84
  67.7 0.0 collective-permute-done.8
  67.8 0.5 collective-permute-start.9
  68.3 7.5 %collective-permute-done.16 = f32[80,1280]{1,0:T(8,128)S(1)} collective-permute-done((f32[80,1280]{1,0:T(8,128)S(1)}, f32[80,1280]{1,0:T(8,128)S(1)}, u32[]{:S(2)}, u32[]{:S(2)}) %collective-permute-start.16) | collective-permute-done | bytes 409632 | tf_op jit(solution)/shard_map/ppermute | solution.py:84
  75.9 1.6 %collective-permute-start.17 = (f32[80,1280]{1,0:T(8,128)S(1)}, f32[80,1280]{1,0:T(8,128)S(1)}, u32[]{:S(2)}, u32[]{:S(2)}) collective-permute-start(f32[80,1280]{1,0:T(8,128)S(1)} %add.354), channel_id=1, source_target_pairs={{0,2},{1,0},{3,1},{5,3},{7,5},{6,7},{4,6},{2,4},{8,10},{9,8},{11,9... | collective-permute-start | bytes 1228808 | tf_op jit(solution)/shard_map/ppermute | solution.py:84
  77.5 0.0 collective-permute-done.9
  77.5 0.5 collective-permute-start.10
  78.1 7.3 %collective-permute-done.17 = f32[80,1280]{1,0:T(8,128)S(1)} collective-permute-done((f32[80,1280]{1,0:T(8,128)S(1)}, f32[80,1280]{1,0:T(8,128)S(1)}, u32[]{:S(2)}, u32[]{:S(2)}) %collective-permute-start.17) | collective-permute-done | bytes 409632 | tf_op jit(solution)/shard_map/ppermute | solution.py:84
  85.5 1.6 %collective-permute-start.18 = (f32[80,1280]{1,0:T(8,128)S(1)}, f32[80,1280]{1,0:T(8,128)S(1)}, u32[]{:S(2)}, u32[]{:S(2)}) collective-permute-start(f32[80,1280]{1,0:T(8,128)S(1)} %add.359), channel_id=1, source_target_pairs={{0,2},{1,0},{3,1},{5,3},{7,5},{6,7},{4,6},{2,4},{8,10},{9,8},{11,9... | collective-permute-start | bytes 1228808 | tf_op jit(solution)/shard_map/ppermute | solution.py:84
  87.1 0.0 collective-permute-done.10
  87.2 0.5 collective-permute-start.11
  87.8 7.6 %collective-permute-done.18 = f32[80,1280]{1,0:T(8,128)S(1)} collective-permute-done((f32[80,1280]{1,0:T(8,128)S(1)}, f32[80,1280]{1,0:T(8,128)S(1)}, u32[]{:S(2)}, u32[]{:S(2)}) %collective-permute-start.18) | collective-permute-done | bytes 409632 | tf_op jit(solution)/shard_map/ppermute | solution.py:84
  95.4 1.6 %collective-permute-start.19 = (f32[80,1280]{1,0:T(8,128)S(1)}, f32[80,1280]{1,0:T(8,128)S(1)}, u32[]{:S(2)}, u32[]{:S(2)}) collective-permute-start(f32[80,1280]{1,0:T(8,128)S(1)} %add.364), channel_id=1, source_target_pairs={{0,2},{1,0},{3,1},{5,3},{7,5},{6,7},{4,6},{2,4},{8,10},{9,8},{11,9... | collective-permute-start | bytes 1228808 | tf_op jit(solution)/shard_map/ppermute | solution.py:84
  97.0 0.0 collective-permute-done.11
  97.1 0.5 collective-permute-start.12
  97.7 0.0 copy-start.3
  97.7 0.0 copy-start.4
  97.7 0.0 copy-start.5
  97.7 8.7 %collective-permute-done.19 = f32[80,1280]{1,0:T(8,128)S(1)} collective-permute-done((f32[80,1280]{1,0:T(8,128)S(1)}, f32[80,1280]{1,0:T(8,128)S(1)}, u32[]{:S(2)}, u32[]{:S(2)}) %collective-permute-start.19) | collective-permute-done | bytes 409632 | tf_op jit(solution)/shard_map/ppermute | solution.py:84
  106.4 1.6 %collective-permute-start.20 = (f32[80,1280]{1,0:T(8,128)S(1)}, f32[80,1280]{1,0:T(8,128)S(1)}, u32[]{:S(2)}, u32[]{:S(2)}) collective-permute-start(f32[80,1280]{1,0:T(8,128)S(1)} %add.369), channel_id=1, source_target_pairs={{0,2},{1,0},{3,1},{5,3},{7,5},{6,7},{4,6},{2,4},{8,10},{9,8},{11,9... | collective-permute-start | bytes 1228808 | tf_op jit(solution)/shard_map/ppermute | solution.py:84
  108.0 0.0 collective-permute-done.12
  108.1 0.5 collective-permute-start.13
  108.7 5.7 %collective-permute-done.20 = f32[80,1280]{1,0:T(8,128)S(1)} collective-permute-done((f32[80,1280]{1,0:T(8,128)S(1)}, f32[80,1280]{1,0:T(8,128)S(1)}, u32[]{:S(2)}, u32[]{:S(2)}) %collective-permute-start.20) | collective-permute-done | bytes 409632 | tf_op jit(solution)/shard_map/ppermute | solution.py:84
  114.5 1.6 %collective-permute-done.13 = f32[80,1280]{1,0:T(8,128)S(1)} collective-permute-done((f32[80,1280]{1,0:T(8,128)S(1)}, f32[80,1280]{1,0:T(8,128)S(1)}, u32[]{:S(2)}, u32[]{:S(2)}) %collective-permute-start.13) | collective-permute-done | bytes 409632 | tf_op jit(solution)/shard_map/ppermute | solution.py:83
  116.2 1.9 %add_divide_fusion = (f32[160,1280]{1,0:T(8,128)}, f32[160,1280]{1,0:T(8,128)}, f32[160,1280]{1,0:T(8,128)}, f32[160,1280]{1,0:T(8,128)}) fusion(f32[160,1280]{1,0:T(8,128)S(1)} %copy-done.3, f32[160,1280]{1,0:T(8,128)S(1)} %copy-done.4, f32[160,1280]{1,0:T(8,128)S(1)} %copy-done.5, f32[80,1280]{1,0:T(8,128)S(1)} %add.374, f32[80,1280]{1,0:T(8,128)S(1)} %add.335), kind=kLoop, calls=%fused_computation.16 | loop fusion | flops 3072000 | bytes 6553600 | tf_op jit(solution)/shard_map/div | solution.py:186
  (33 shorter events, 1.0 us)
Async XLA Ops:
  0.6 7.3 %copy-start = (bf16[1280,1280]{1,0:T(8,128)(2,1)S(1)}, bf16[1280,1280]{1,0:T(8,128)(2,1)}, u32[]{:S(2)}) copy-start(bf16[1280,1280]{1,0:T(8,128)(2,1)} %param.8) | copy-start | bytes 9830404
  4.9 20.4 %collective-permute-start = (bf16[128,2560]{1,0:T(8,128)(2,1)}, bf16[128,2560]{1,0:T(8,128)(2,1)}, u32[]{:S(2)}, u32[]{:S(2)}) collective-permute-start(bf16[128,2560]{1,0:T(8,128)(2,1)} %get-tuple-element.46), channel_id=1, source_target_pairs={{0,8},{8,0},{16,24},{24,16},{1,9},{9,1},{17,25},{25,17},{2,10},{10... | collective-permute-start | bytes 1966088 | tf_op jit(solution)/shard_map/ppermute | solution.py:104
  5.4 18.2 %collective-permute-start.1 = (bf16[128,2560]{1,0:T(8,128)(2,1)}, bf16[128,2560]{1,0:T(8,128)(2,1)}, u32[]{:S(2)}, u32[]{:S(2)}) collective-permute-start(bf16[128,2560]{1,0:T(8,128)(2,1)} %get-tuple-element.45), channel_id=1, source_target_pairs={{0,16},{8,24},{16,0},{24,8},{1,17},{9,25},{17,1},{25,9},{2,18},{10... | collective-permute-start | bytes 1966088 | tf_op jit(solution)/shard_map/ppermute | solution.py:101
  7.8 2.3 %copy-start.1 = (bf16[1,1,128,1280]{3,2,1,0:T(8,128)(2,1)S(1)}, bf16[1,1,128,1280]{3,2,1,0:T(8,128)(2,1)}, u32[]{:S(2)}) copy-start(bf16[1,1,128,1280]{3,2,1,0:T(8,128)(2,1)} %param.7) | copy-start | bytes 983044
  10.1 13.4 %copy-start.6 = (bf16[128,1280]{1,0:T(8,128)(2,1)S(1)}, bf16[128,1280]{1,0:T(8,128)(2,1)}, u32[]{:S(2)}) copy-start(bf16[128,1280]{1,0:T(8,128)(2,1)} %get-tuple-element.21) | copy-start | bytes 983044
  23.6 9.5 %collective-permute-start.2 = (bf16[128,1280]{1,0:T(8,128)(2,1)S(1)}, bf16[128,1280]{1,0:T(8,128)(2,1)S(1)}, u32[]{:S(2)}, u32[]{:S(2)}) collective-permute-start(bf16[128,1280]{1,0:T(8,128)(2,1)S(1)} %copy-done.6), channel_id=1, source_target_pairs={{0,16},{8,24},{16,0},{24,8},{1,17},{9,25},{17,1},{25,9},{2,18},{10... | collective-permute-start | bytes 983048 | tf_op jit(solution)/shard_map/ppermute | solution.py:106
  25.3 9.8 %collective-permute-start.3 = (bf16[128,2560]{1,0:T(8,128)(2,1)}, bf16[128,2560]{1,0:T(8,128)(2,1)S(1)}, u32[]{:S(2)}, u32[]{:S(2)}) collective-permute-start(bf16[128,2560]{1,0:T(8,128)(2,1)} %collective-permute-done.1), channel_id=1, source_target_pairs={{0,8},{8,0},{16,24},{24,16},{1,9},{9,1},{17,25},{25,17},{2,10},{10... | collective-permute-start | bytes 1966088 | tf_op jit(solution)/shard_map/ppermute | solution.py:107
  37.6 3.1 %collective-permute-start.4 = (f32[1]{0:T(128)}, f32[1]{0:T(128)}, u32[]{:S(2)}, u32[]{:S(2)}) collective-permute-start(f32[1]{0:T(128)} %bitcast.5), channel_id=1, source_target_pairs={{0,8},{8,0},{16,24},{24,16},{1,9},{9,1},{17,25},{25,17},{2,10},{10... | collective-permute-start | bytes 20 | tf_op jit(solution)/shard_map/ppermute | solution.py:120
  37.6 4.4 %collective-permute-start.5 = (f32[1]{0:T(128)}, f32[1]{0:T(128)}, u32[]{:S(2)}, u32[]{:S(2)}) collective-permute-start(f32[1]{0:T(128)} %bitcast.5), channel_id=1, source_target_pairs={{0,16},{8,24},{16,0},{24,8},{1,17},{9,25},{17,1},{25,9},{2,18},{10... | collective-permute-start | bytes 20 | tf_op jit(solution)/shard_map/ppermute | solution.py:120
  39.2 3.2 %collective-permute-start.6 = (f32[1]{0:T(128)}, f32[1]{0:T(128)}, u32[]{:S(2)}, u32[]{:S(2)}) collective-permute-start(f32[1]{0:T(128)} %bitcast.5), channel_id=1, source_target_pairs={{0,24},{8,16},{16,8},{24,0},{1,25},{9,17},{17,9},{25,1},{2,26},{10... | collective-permute-start | bytes 20 | tf_op jit(solution)/shard_map/ppermute | solution.py:120
  40.7 16.9 %copy-start.2 = (bf16[512,1280]{1,0:T(8,128)(2,1)}, bf16[512,1280]{1,0:T(8,128)(2,1)S(1)}, u32[]{:S(2)}) copy-start(bf16[512,1280]{1,0:T(8,128)(2,1)S(1)} %fusion.1) | copy-start | bytes 3932164
  43.8 11.5 %collective-permute-start.14 = (f32[80,1280]{1,0:T(8,128)S(1)}, f32[80,1280]{1,0:T(8,128)S(1)}, u32[]{:S(2)}, u32[]{:S(2)}) collective-permute-start(f32[80,1280]{1,0:T(8,128)S(1)} %get-tuple-element.41), channel_id=1, source_target_pairs={{0,2},{1,0},{3,1},{5,3},{7,5},{6,7},{4,6},{2,4},{8,10},{9,8},{11,9... | collective-permute-start | bytes 1228808 | tf_op jit(solution)/shard_map/ppermute | solution.py:84
  45.4 11.6 %collective-permute-start.7 = (f32[80,1280]{1,0:T(8,128)S(1)}, f32[80,1280]{1,0:T(8,128)S(1)}, u32[]{:S(2)}, u32[]{:S(2)}) collective-permute-start(f32[80,1280]{1,0:T(8,128)S(1)} %get-tuple-element.40), channel_id=1, source_target_pairs={{0,1},{1,3},{3,5},{5,7},{7,6},{6,4},{4,2},{2,0},{8,9},{9,11},{11,1... | collective-permute-start | bytes 1228808 | tf_op jit(solution)/shard_map/ppermute | solution.py:83
  55.4 10.7 %collective-permute-start.15 = (f32[80,1280]{1,0:T(8,128)S(1)}, f32[80,1280]{1,0:T(8,128)S(1)}, u32[]{:S(2)}, u32[]{:S(2)}) collective-permute-start(f32[80,1280]{1,0:T(8,128)S(1)} %add.344), channel_id=1, source_target_pairs={{0,2},{1,0},{3,1},{5,3},{7,5},{6,7},{4,6},{2,4},{8,10},{9,8},{11,9... | collective-permute-start | bytes 1228808 | tf_op jit(solution)/shard_map/ppermute | solution.py:84
  57.1 10.7 %collective-permute-start.8 = (f32[80,1280]{1,0:T(8,128)S(1)}, f32[80,1280]{1,0:T(8,128)S(1)}, u32[]{:S(2)}, u32[]{:S(2)}) collective-permute-start(f32[80,1280]{1,0:T(8,128)S(1)} %add.317), channel_id=1, source_target_pairs={{0,1},{1,3},{3,5},{5,7},{7,6},{6,4},{4,2},{2,0},{8,9},{9,11},{11,1... | collective-permute-start | bytes 1228808 | tf_op jit(solution)/shard_map/ppermute | solution.py:83
  66.1 9.7 %collective-permute-start.16 = (f32[80,1280]{1,0:T(8,128)S(1)}, f32[80,1280]{1,0:T(8,128)S(1)}, u32[]{:S(2)}, u32[]{:S(2)}) collective-permute-start(f32[80,1280]{1,0:T(8,128)S(1)} %add.349), channel_id=1, source_target_pairs={{0,2},{1,0},{3,1},{5,3},{7,5},{6,7},{4,6},{2,4},{8,10},{9,8},{11,9... | collective-permute-start | bytes 1228808 | tf_op jit(solution)/shard_map/ppermute | solution.py:84
  67.8 9.7 %collective-permute-start.9 = (f32[80,1280]{1,0:T(8,128)S(1)}, f32[80,1280]{1,0:T(8,128)S(1)}, u32[]{:S(2)}, u32[]{:S(2)}) collective-permute-start(f32[80,1280]{1,0:T(8,128)S(1)} %add.320), channel_id=1, source_target_pairs={{0,1},{1,3},{3,5},{5,7},{7,6},{6,4},{4,2},{2,0},{8,9},{9,11},{11,1... | collective-permute-start | bytes 1228808 | tf_op jit(solution)/shard_map/ppermute | solution.py:83
  75.9 9.6 %collective-permute-start.17 = (f32[80,1280]{1,0:T(8,128)S(1)}, f32[80,1280]{1,0:T(8,128)S(1)}, u32[]{:S(2)}, u32[]{:S(2)}) collective-permute-start(f32[80,1280]{1,0:T(8,128)S(1)} %add.354), channel_id=1, source_target_pairs={{0,2},{1,0},{3,1},{5,3},{7,5},{6,7},{4,6},{2,4},{8,10},{9,8},{11,9... | collective-permute-start | bytes 1228808 | tf_op jit(solution)/shard_map/ppermute | solution.py:84
  77.5 9.6 %collective-permute-start.10 = (f32[80,1280]{1,0:T(8,128)S(1)}, f32[80,1280]{1,0:T(8,128)S(1)}, u32[]{:S(2)}, u32[]{:S(2)}) collective-permute-start(f32[80,1280]{1,0:T(8,128)S(1)} %add.323), channel_id=1, source_target_pairs={{0,1},{1,3},{3,5},{5,7},{7,6},{6,4},{4,2},{2,0},{8,9},{9,11},{11,1... | collective-permute-start | bytes 1228808 | tf_op jit(solution)/shard_map/ppermute | solution.py:83
  85.5 9.9 %collective-permute-start.18 = (f32[80,1280]{1,0:T(8,128)S(1)}, f32[80,1280]{1,0:T(8,128)S(1)}, u32[]{:S(2)}, u32[]{:S(2)}) collective-permute-start(f32[80,1280]{1,0:T(8,128)S(1)} %add.359), channel_id=1, source_target_pairs={{0,2},{1,0},{3,1},{5,3},{7,5},{6,7},{4,6},{2,4},{8,10},{9,8},{11,9... | collective-permute-start | bytes 1228808 | tf_op jit(solution)/shard_map/ppermute | solution.py:84
  87.2 9.9 %collective-permute-start.11 = (f32[80,1280]{1,0:T(8,128)S(1)}, f32[80,1280]{1,0:T(8,128)S(1)}, u32[]{:S(2)}, u32[]{:S(2)}) collective-permute-start(f32[80,1280]{1,0:T(8,128)S(1)} %add.326), channel_id=1, source_target_pairs={{0,1},{1,3},{3,5},{5,7},{7,6},{6,4},{4,2},{2,0},{8,9},{9,11},{11,1... | collective-permute-start | bytes 1228808 | tf_op jit(solution)/shard_map/ppermute | solution.py:83
  95.4 11.0 %collective-permute-start.19 = (f32[80,1280]{1,0:T(8,128)S(1)}, f32[80,1280]{1,0:T(8,128)S(1)}, u32[]{:S(2)}, u32[]{:S(2)}) collective-permute-start(f32[80,1280]{1,0:T(8,128)S(1)} %add.364), channel_id=1, source_target_pairs={{0,2},{1,0},{3,1},{5,3},{7,5},{6,7},{4,6},{2,4},{8,10},{9,8},{11,9... | collective-permute-start | bytes 1228808 | tf_op jit(solution)/shard_map/ppermute | solution.py:84
  97.1 11.0 %collective-permute-start.12 = (f32[80,1280]{1,0:T(8,128)S(1)}, f32[80,1280]{1,0:T(8,128)S(1)}, u32[]{:S(2)}, u32[]{:S(2)}) collective-permute-start(f32[80,1280]{1,0:T(8,128)S(1)} %add.329), channel_id=1, source_target_pairs={{0,1},{1,3},{3,5},{5,7},{7,6},{6,4},{4,2},{2,0},{8,9},{9,11},{11,1... | collective-permute-start | bytes 1228808 | tf_op jit(solution)/shard_map/ppermute | solution.py:83
  97.7 18.5 %copy-start.3 = (f32[160,1280]{1,0:T(8,128)S(1)}, f32[160,1280]{1,0:T(8,128)}, u32[]{:S(2)}) copy-start(f32[160,1280]{1,0:T(8,128)} %param.11) | copy-start | bytes 2457604
  97.7 18.5 %copy-start.4 = (f32[160,1280]{1,0:T(8,128)S(1)}, f32[160,1280]{1,0:T(8,128)}, u32[]{:S(2)}) copy-start(f32[160,1280]{1,0:T(8,128)} %param.10) | copy-start | bytes 2457604
  97.7 18.5 %copy-start.5 = (f32[160,1280]{1,0:T(8,128)S(1)}, f32[160,1280]{1,0:T(8,128)}, u32[]{:S(2)}) copy-start(f32[160,1280]{1,0:T(8,128)} %param.9) | copy-start | bytes 2457604
  106.4 8.0 %collective-permute-start.20 = (f32[80,1280]{1,0:T(8,128)S(1)}, f32[80,1280]{1,0:T(8,128)S(1)}, u32[]{:S(2)}, u32[]{:S(2)}) collective-permute-start(f32[80,1280]{1,0:T(8,128)S(1)} %add.369), channel_id=1, source_target_pairs={{0,2},{1,0},{3,1},{5,3},{7,5},{6,7},{4,6},{2,4},{8,10},{9,8},{11,9... | collective-permute-start | bytes 1228808 | tf_op jit(solution)/shard_map/ppermute | solution.py:84
  108.1 8.0 %collective-permute-start.13 = (f32[80,1280]{1,0:T(8,128)S(1)}, f32[80,1280]{1,0:T(8,128)S(1)}, u32[]{:S(2)}, u32[]{:S(2)}) collective-permute-start(f32[80,1280]{1,0:T(8,128)S(1)} %add.332), channel_id=1, source_target_pairs={{0,1},{1,3},{3,5},{5,7},{7,6},{6,4},{4,2},{2,0},{8,9},{9,11},{11,1... | collective-permute-start | bytes 1228808 | tf_op jit(solution)/shard_map/ppermute | solution.py:83

commit v6 on v5

--- a/solution.py
+++ b/solution.py
@@ -61,7 +61,7 @@
     return out
 
 
-def ring_reduce_scatter(parts, ring, step_fn):
+def ring_reduce_scatter(parts, ring, pieces):
     n = len(ring)
     pos_of = [0] * n
     for k, d in enumerate(ring):
@@ -73,18 +73,20 @@
     def block(s, step):
         return lookup(ring, (pos - 1 - s) % n if step < 0 else (pos + 1 + s) % n)
 
-    own_r = parts(block(0, -1), 0, None)
-    own_l = parts(block(0, 1), 1, None)
-    acc_r = None
-    acc_l = None
+    chains = [(-1 if c % 2 == 0 else 1, c) for c in range(pieces)]
+    own = [parts(block(0, step), which, None) for step, which in chains]
+    acc = [None] * pieces
     for s in range(n - 1):
-        send_r = own_r if acc_r is None else acc_r + own_r
-        send_l = own_l if acc_l is None else acc_l + own_l
-        acc_r = lax.ppermute(send_r, "dp", right)
-        acc_l = lax.ppermute(send_l, "dp", left)
-        own_r = parts(block(s + 1, -1), 0, send_r)
-        own_l = parts(block(s + 1, 1), 1, send_l)
-    return jnp.concatenate([acc_r + own_r, acc_l + own_l], axis=0)
+        send = [o if x is None else x + o for x, o in zip(acc, own)]
+        acc = [
+            lax.ppermute(v, "dp", right if step < 0 else left)
+            for v, (step, _) in zip(send, chains)
+        ]
+        own = [
+            parts(block(s + 1, step), which, v)
+            for v, (step, which) in zip(send, chains)
+        ]
+    return jnp.concatenate([x + o for x, o in zip(acc, own)], axis=0)
 
 
 def exchange_four(h_rows, grad_rows):
@@ -167,7 +169,8 @@
     image_norms = jnp.sqrt(squares)
     factor = clip / jnp.maximum(image_norms, clip)
     owned_rows = slice_width // groups
-    half = owned_rows // 2
+    pieces = 4 if owned_rows % 32 == 0 else 2
+    half = owned_rows // pieces
 
     def parts(block, which, after):
         source = grads
@@ -177,7 +180,7 @@
         rows = lax.dynamic_slice_in_dim(source, start, half, axis=1)
         return lax.optimization_barrier(jnp.sum(factor[:, None, None] * rows, axis=0))
 
-    owned = ring_reduce_scatter(parts, ring, None)
+    owned = ring_reduce_scatter(parts, ring, pieces)
     clipped_mean = owned / images_all
     noisy = clipped_mean + noise_ratio * clip * noise / images_all
     new_first = beta_one * first_moment + (1.0 - beta_one) * noisy

time: 120 us -> 113 us (0.942)
  waiting for transfers between devices: 69.2 us -> 47.2 us
  starting transfers between devices: 21.4 us -> 36.2 us
    ppermute x14 -> x28, waiting for transfers between devices: 56.2 us -> 34.4 us  [ring_reduce_scatter(): lax.ppermute(v, 'dp', right if step < 0 else left)]
    ppermute x14 -> x28, starting transfers between devices: 14.9 us -> 29.7 us  [ring_reduce_scatter(): lax.ppermute(v, 'dp', right if step < 0 else left)]
  transfers between devices with their start and end apart: 21 -> 35, of which waited for: 11 -> 19; matrix products, arithmetic and copies ran while one was open for 13% -> 14% of each run, Pallas kernels for 0% -> 0%
where the time goes in v6:
time: 113 us
  waiting for transfers between devices  47.2 us (42%)
  starting transfers between devices  36.2 us (32%)
  matrix products  16.5 us (15%)
  other arithmetic  5.55 us (5%)
  between operations  4.91 us (4%)
  local copies, waits for them, and re-layouts  2.25 us (2%)
    ppermute x28, waiting for transfers between devices, ring_reduce_scatter(): lax.ppermute(v, 'dp', right if step < 0 else left)  34.4 us
    ppermute x28, starting transfers between devices, ring_reduce_scatter(): lax.ppermute(v, 'dp', right if step < 0 else left)  29.7 us
    ppermute x1, waiting for transfers between devices, exchange_four(): lax.ppermute(jnp.concatenate([cols(a ^ 3), grad_rows], axis=1), 'aug', ov...  11.3 us
    dot_general x4, matrix products, per_device(): term = jnp.dot(h_piece.T, g_piece, preferred_element_type=jnp.float32)  8.8 us
    dot_general x4, matrix products, project_back(): lax.dot_general(rows, down_weight, (((1,), (1,)), ((), ())), preferred_el...  7.72 us
    ppermute x1, starting transfers between devices, exchange_four(): lax.ppermute(jnp.concatenate([cols(a ^ 3), grad_rows], axis=1), 'aug', ov...  2.49 us
  transfers between devices with their start and end apart: 35, of which 19 were waited for; matrix products, arithmetic and copies ran while one was open for 14% of the time, Pallas kernels for 0%

profile of v6, /device:TPU:0, one launch (start us, length us, event | category | flops | bytes accessed | tf_op | source)
XLA Modules:
  0.0 112.7 jit_solution(10772153777540843750)
XLA Ops:
  0.7 2.1 %dynamic-slice_bitcast_fusion = (bf16[128,1280]{1,0:T(8,128)(2,1)}, bf16[128,1280]{1,0:T(8,128)(2,1)S(1)}, bf16[128,1280]{1,0:T(8,128)(2,1)S(1)}) fusion(bf16[1,1,128,5120]{3,2,1,0:T(8,128)(2,1)} %param.6, s32[]{:T(128)S(6)} %select_n.691, s32[]{:T(128)S(6)} %select_n.689, s32[]{:T(128)S(6)} %select_n.690), kind=kLoop, calls=%fused_computation.25 | loop fusion | bytes 1966092 | tf_op jit(solution)/shard_map/dynamic_slice | solution.py:99
  2.8 2.1 %pad_maximum_fusion = (bf16[128,2560]{1,0:T(8,128)(2,1)}, bf16[128,2560]{1,0:T(8,128)(2,1)}) fusion(bf16[128,1280]{1,0:T(8,128)(2,1)} %bitcast.107, bf16[128,1280]{1,0:T(8,128)(2,1)S(1)} %get-tuple-element.74, bf16[128,1280]{1,0:T(8,128)(2,1)S(1)} %get-tuple-element.73), kind=kLoop, calls=%fused_computation.19 | loop fusion | flops 2293760 | bytes 2293760 | tf_op jit(solution)/shard_map/concatenate | solution.py:104
  4.9 0.5 collective-permute-start
  5.4 2.5 %collective-permute-start.1 = (bf16[128,2560]{1,0:T(8,128)(2,1)}, bf16[128,2560]{1,0:T(8,128)(2,1)}, u32[]{:S(2)}, u32[]{:S(2)}) collective-permute-start(bf16[128,2560]{1,0:T(8,128)(2,1)} %get-tuple-element.75), channel_id=1, source_target_pairs={{0,16},{8,24},{16,0},{24,8},{1,17},{9,25},{17,1},{25,9},{2,18},{10... | collective-permute-start | bytes 1966088 | tf_op jit(solution)/shard_map/ppermute | solution.py:103
  7.9 2.2 %fusion.4 = bf16[512,1280]{1,0:T(8,128)(2,1)S(1)} fusion(bf16[512,1280]{1,0:T(8,128)(2,1)S(1)} %broadcast_in_dim.2, s32[]{:T(128)S(6)} %select_n.859, bf16[1280,1280]{1,0:T(8,128)(2,1)S(1)} %copy-done, bf16[1,1,128,1280]{3,2,1,0:T(8,128)(2,1)} %param.7), kind=kOutput, calls=%fused_computation.12 | convolution fusion | flops 419594240 | bytes 3932164 | tf_op jit(solution)/shard_map/dot_general | solution.py:17
  10.1 2.2 %fusion.8 = f32[1280,1280]{1,0:T(8,128)S(1)} fusion(bf16[1,1,128,5120]{3,2,1,0:T(8,128)(2,1)} %param.6, s32[]{:T(128)S(6)} %select_n.688, bf16[1,1,128,1280]{3,2,1,0:T(8,128)(2,1)} %param.7), kind=kOutput, calls=%fused_computation.23 | convolution fusion | flops 419430400 | bytes 7208964 | tf_op jit(solution)/shard_map/dot_general | solution.py:151
  12.3 11.3 %collective-permute-done.1 = bf16[128,2560]{1,0:T(8,128)(2,1)} collective-permute-done((bf16[128,2560]{1,0:T(8,128)(2,1)}, bf16[128,2560]{1,0:T(8,128)(2,1)}, u32[]{:S(2)}, u32[]{:S(2)}) %collective-permute-start.1) | collective-permute-done | bytes 655392 | tf_op jit(solution)/shard_map/ppermute | solution.py:103
  23.6 1.7 %collective-permute-start.2 = (bf16[128,1280]{1,0:T(8,128)(2,1)S(1)}, bf16[128,1280]{1,0:T(8,128)(2,1)S(1)}, u32[]{:S(2)}, u32[]{:S(2)}) collective-permute-start(bf16[128,1280]{1,0:T(8,128)(2,1)S(1)} %copy-done.5), channel_id=1, source_target_pairs={{0,16},{8,24},{16,0},{24,8},{1,17},{9,25},{17,1},{25,9},{2,18},{10... | collective-permute-start | bytes 983048 | tf_op jit(solution)/shard_map/ppermute | solution.py:108
  25.3 2.1 %convolution_add_fusion.2 = f32[1280,1280]{1,0:T(8,128)S(1)} fusion(f32[1280,1280]{1,0:T(8,128)S(1)} %fusion.8, bf16[128,2560]{1,0:T(8,128)(2,1)} %collective-permute-done), kind=kOutput, calls=%fused_computation.2 | convolution fusion | flops 421068800 | bytes 13762560 | tf_op jit(solution)/shard_map/dot_general | solution.py:151
  27.4 2.2 %fusion.3 = bf16[512,1280]{1,0:T(8,128)(2,1)S(1)} fusion(bf16[512,1280]{1,0:T(8,128)(2,1)S(1)} %fusion.4, s32[]{:T(128)S(6)} %select_n.860, bf16[1280,1280]{1,0:T(8,128)(2,1)S(1)} %copy-done, bf16[128,2560]{1,0:T(8,128)(2,1)} %collective-permute-done), kind=kOutput, calls=%fused_computation.10 | convolution fusion | flops 419594240 | bytes 3932164 | tf_op jit(solution)/shard_map/dot_general | solution.py:17
  29.6 2.2 %fusion.2 = bf16[512,1280]{1,0:T(8,128)(2,1)S(1)} fusion(bf16[512,1280]{1,0:T(8,128)(2,1)S(1)} %fusion.3, s32[]{:T(128)S(6)} %select_n.861, bf16[1280,1280]{1,0:T(8,128)(2,1)S(1)} %copy-done, bf16[128,2560]{1,0:T(8,128)(2,1)} %collective-permute-done.1), kind=kOutput, calls=%fused_computation.8 | convolution fusion | flops 419594240 | bytes 3932164 | tf_op jit(solution)/shard_map/dot_general | solution.py:17
  31.8 1.3 %collective-permute-done.2 = bf16[128,1280]{1,0:T(8,128)(2,1)S(1)} collective-permute-done((bf16[128,1280]{1,0:T(8,128)(2,1)S(1)}, bf16[128,1280]{1,0:T(8,128)(2,1)S(1)}, u32[]{:S(2)}, u32[]{:S(2)}) %collective-permute-start.2) | collective-permute-done | bytes 327712 | tf_op jit(solution)/shard_map/ppermute | solution.py:108
  33.1 2.0 %convolution_add_fusion.1 = f32[1280,1280]{1,0:T(8,128)S(1)} fusion(f32[1280,1280]{1,0:T(8,128)S(1)} %convolution_add_fusion.2, bf16[128,1280]{1,0:T(8,128)(2,1)S(1)} %collective-permute-done.2, bf16[128,2560]{1,0:T(8,128)(2,1)} %collective-permute-done.1), kind=kOutput, calls=%fused_computation.1 | convolution fusion | flops 421068800 | bytes 13762560 | tf_op jit(solution)/shard_map/dot_general | solution.py:151
  35.1 2.5 %multiply_reduce_fusion = (f32[]{:T(128)}, f32[1280,1280]{1,0:T(8,128)S(1)}) fusion(f32[1280,1280]{1,0:T(8,128)S(1)} %convolution_add_fusion.1, bf16[128,2560]{1,0:T(8,128)(2,1)S(1)} %collective-permute-done.3), kind=kOutput, calls=%fused_computation.4 | convolution fusion | flops 425984000 | bytes 13762564 | tf_op jit(solution)/shard_map/dot_general | solution.py:151
  37.6 1.5 %collective-permute-start.5 = (f32[1]{0:T(128)}, f32[1]{0:T(128)}, u32[]{:S(2)}, u32[]{:S(2)}) collective-permute-start(f32[1]{0:T(128)} %bitcast.5), channel_id=1, source_target_pairs={{0,16},{8,24},{16,0},{24,8},{1,17},{9,25},{17,1},{25,9},{2,18},{10... | collective-permute-start | bytes 20 | tf_op jit(solution)/shard_map/ppermute | solution.py:122
  39.2 0.3 collective-permute-start.6
  39.5 1.2 %fusion.1 = bf16[512,1280]{1,0:T(8,128)(2,1)S(1)} fusion(bf16[512,1280]{1,0:T(8,128)(2,1)S(1)} %fusion.2, s32[]{:T(128)S(6)} %select_n.862, bf16[1280,1280]{1,0:T(8,128)(2,1)S(1)} %copy-done, bf16[128,2560]{1,0:T(8,128)(2,1)S(1)} %collective-permute-done.3), kind=kOutput, calls=%fused_computation.6 | convolution fusion | flops 419594240 | bytes 3932164 | tf_op jit(solution)/shard_map/dot_general | solution.py:17
  42.0 0.2 collective-permute-done.6
  43.6 0.1 dynamic-slice_multiply_fusion.3
  43.7 1.6 %collective-permute-start.28 = (f32[40,1280]{1,0:T(8,128)S(1)}, f32[40,1280]{1,0:T(8,128)S(1)}, u32[]{:S(2)}, u32[]{:S(2)}) collective-permute-start(f32[40,1280]{1,0:T(8,128)S(1)} %get-tuple-element.69), channel_id=1, source_target_pairs={{0,2},{1,0},{3,1},{5,3},{7,5},{6,7},{4,6},{2,4},{8,10},{9,8},{11,9... | collective-permute-start | bytes 614408 | tf_op jit(solution)/shard_map/ppermute | solution.py:82
  45.4 0.4 collective-permute-start.21
  45.8 1.6 %collective-permute-start.14 = (f32[40,1280]{1,0:T(8,128)S(1)}, f32[40,1280]{1,0:T(8,128)S(1)}, u32[]{:S(2)}, u32[]{:S(2)}) collective-permute-start(f32[40,1280]{1,0:T(8,128)S(1)} %get-tuple-element.71), channel_id=1, source_target_pairs={{0,2},{1,0},{3,1},{5,3},{7,5},{6,7},{4,6},{2,4},{8,10},{9,8},{11,9... | collective-permute-start | bytes 614408 | tf_op jit(solution)/shard_map/ppermute | solution.py:82
  47.4 0.4 collective-permute-start.7
  48.0 3.7 %collective-permute-done.28 = f32[40,1280]{1,0:T(8,128)S(1)} collective-permute-done((f32[40,1280]{1,0:T(8,128)S(1)}, f32[40,1280]{1,0:T(8,128)S(1)}, u32[]{:S(2)}, u32[]{:S(2)}) %collective-permute-start.28) | collective-permute-done | bytes 204832 | tf_op jit(solution)/shard_map/ppermute | solution.py:82
  51.7 1.6 %collective-permute-start.29 = (f32[40,1280]{1,0:T(8,128)S(1)}, f32[40,1280]{1,0:T(8,128)S(1)}, u32[]{:S(2)}, u32[]{:S(2)}) collective-permute-start(f32[40,1280]{1,0:T(8,128)S(1)} %add.603), channel_id=1, source_target_pairs={{0,2},{1,0},{3,1},{5,3},{7,5},{6,7},{4,6},{2,4},{8,10},{9,8},{11,9... | collective-permute-start | bytes 614408 | tf_op jit(solution)/shard_map/ppermute | solution.py:82
  53.4 0.5 collective-permute-start.22
  53.9 2.2 %collective-permute-done.14 = f32[40,1280]{1,0:T(8,128)S(1)} collective-permute-done((f32[40,1280]{1,0:T(8,128)S(1)}, f32[40,1280]{1,0:T(8,128)S(1)}, u32[]{:S(2)}, u32[]{:S(2)}) %collective-permute-start.14) | collective-permute-done | bytes 204832 | tf_op jit(solution)/shard_map/ppermute | solution.py:82
  56.1 1.6 %collective-permute-start.15 = (f32[40,1280]{1,0:T(8,128)S(1)}, f32[40,1280]{1,0:T(8,128)S(1)}, u32[]{:S(2)}, u32[]{:S(2)}) collective-permute-start(f32[40,1280]{1,0:T(8,128)S(1)} %add.545), channel_id=1, source_target_pairs={{0,2},{1,0},{3,1},{5,3},{7,5},{6,7},{4,6},{2,4},{8,10},{9,8},{11,9... | collective-permute-start | bytes 614408 | tf_op jit(solution)/shard_map/ppermute | solution.py:82
  57.8 0.5 collective-permute-start.8
  58.4 2.1 %collective-permute-done.29 = f32[40,1280]{1,0:T(8,128)S(1)} collective-permute-done((f32[40,1280]{1,0:T(8,128)S(1)}, f32[40,1280]{1,0:T(8,128)S(1)}, u32[]{:S(2)}, u32[]{:S(2)}) %collective-permute-start.29) | collective-permute-done | bytes 204832 | tf_op jit(solution)/shard_map/ppermute | solution.py:82
  60.5 1.6 %collective-permute-start.30 = (f32[40,1280]{1,0:T(8,128)S(1)}, f32[40,1280]{1,0:T(8,128)S(1)}, u32[]{:S(2)}, u32[]{:S(2)}) collective-permute-start(f32[40,1280]{1,0:T(8,128)S(1)} %add.606), channel_id=1, source_target_pairs={{0,2},{1,0},{3,1},{5,3},{7,5},{6,7},{4,6},{2,4},{8,10},{9,8},{11,9... | collective-permute-start | bytes 614408 | tf_op jit(solution)/shard_map/ppermute | solution.py:82
  62.2 0.5 collective-permute-start.23
  62.7 2.2 %collective-permute-done.15 = f32[40,1280]{1,0:T(8,128)S(1)} collective-permute-done((f32[40,1280]{1,0:T(8,128)S(1)}, f32[40,1280]{1,0:T(8,128)S(1)}, u32[]{:S(2)}, u32[]{:S(2)}) %collective-permute-start.15) | collective-permute-done | bytes 204832 | tf_op jit(solution)/shard_map/ppermute | solution.py:82
  64.9 1.6 %collective-permute-start.16 = (f32[40,1280]{1,0:T(8,128)S(1)}, f32[40,1280]{1,0:T(8,128)S(1)}, u32[]{:S(2)}, u32[]{:S(2)}) collective-permute-start(f32[40,1280]{1,0:T(8,128)S(1)} %add.550), channel_id=1, source_target_pairs={{0,2},{1,0},{3,1},{5,3},{7,5},{6,7},{4,6},{2,4},{8,10},{9,8},{11,9... | collective-permute-start | bytes 614408 | tf_op jit(solution)/shard_map/ppermute | solution.py:82
  66.5 0.5 collective-permute-start.9
  67.2 2.1 %collective-permute-done.30 = f32[40,1280]{1,0:T(8,128)S(1)} collective-permute-done((f32[40,1280]{1,0:T(8,128)S(1)}, f32[40,1280]{1,0:T(8,128)S(1)}, u32[]{:S(2)}, u32[]{:S(2)}) %collective-permute-start.30) | collective-permute-done | bytes 204832 | tf_op jit(solution)/shard_map/ppermute | solution.py:82
  69.3 1.6 %collective-permute-start.31 = (f32[40,1280]{1,0:T(8,128)S(1)}, f32[40,1280]{1,0:T(8,128)S(1)}, u32[]{:S(2)}, u32[]{:S(2)}) collective-permute-start(f32[40,1280]{1,0:T(8,128)S(1)} %add.609), channel_id=1, source_target_pairs={{0,2},{1,0},{3,1},{5,3},{7,5},{6,7},{4,6},{2,4},{8,10},{9,8},{11,9... | collective-permute-start | bytes 614408 | tf_op jit(solution)/shard_map/ppermute | solution.py:82
  70.9 0.5 collective-permute-start.24
  71.4 2.2 %collective-permute-done.16 = f32[40,1280]{1,0:T(8,128)S(1)} collective-permute-done((f32[40,1280]{1,0:T(8,128)S(1)}, f32[40,1280]{1,0:T(8,128)S(1)}, u32[]{:S(2)}, u32[]{:S(2)}) %collective-permute-start.16) | collective-permute-done | bytes 204832 | tf_op jit(solution)/shard_map/ppermute | solution.py:82
  73.7 1.6 %collective-permute-start.17 = (f32[40,1280]{1,0:T(8,128)S(1)}, f32[40,1280]{1,0:T(8,128)S(1)}, u32[]{:S(2)}, u32[]{:S(2)}) collective-permute-start(f32[40,1280]{1,0:T(8,128)S(1)} %add.555), channel_id=1, source_target_pairs={{0,2},{1,0},{3,1},{5,3},{7,5},{6,7},{4,6},{2,4},{8,10},{9,8},{11,9... | collective-permute-start | bytes 614408 | tf_op jit(solution)/shard_map/ppermute | solution.py:82
  75.3 0.5 collective-permute-start.10
  75.9 2.1 %collective-permute-done.31 = f32[40,1280]{1,0:T(8,128)S(1)} collective-permute-done((f32[40,1280]{1,0:T(8,128)S(1)}, f32[40,1280]{1,0:T(8,128)S(1)}, u32[]{:S(2)}, u32[]{:S(2)}) %collective-permute-start.31) | collective-permute-done | bytes 204832 | tf_op jit(solution)/shard_map/ppermute | solution.py:82
  78.0 1.6 %collective-permute-start.32 = (f32[40,1280]{1,0:T(8,128)S(1)}, f32[40,1280]{1,0:T(8,128)S(1)}, u32[]{:S(2)}, u32[]{:S(2)}) collective-permute-start(f32[40,1280]{1,0:T(8,128)S(1)} %add.612), channel_id=1, source_target_pairs={{0,2},{1,0},{3,1},{5,3},{7,5},{6,7},{4,6},{2,4},{8,10},{9,8},{11,9... | collective-permute-start | bytes 614408 | tf_op jit(solution)/shard_map/ppermute | solution.py:82
  79.7 0.5 collective-permute-start.25
  80.2 2.2 %collective-permute-done.17 = f32[40,1280]{1,0:T(8,128)S(1)} collective-permute-done((f32[40,1280]{1,0:T(8,128)S(1)}, f32[40,1280]{1,0:T(8,128)S(1)}, u32[]{:S(2)}, u32[]{:S(2)}) %collective-permute-start.17) | collective-permute-done | bytes 204832 | tf_op jit(solution)/shard_map/ppermute | solution.py:82
  82.5 1.6 %collective-permute-start.18 = (f32[40,1280]{1,0:T(8,128)S(1)}, f32[40,1280]{1,0:T(8,128)S(1)}, u32[]{:S(2)}, u32[]{:S(2)}) collective-permute-start(f32[40,1280]{1,0:T(8,128)S(1)} %add.560), channel_id=1, source_target_pairs={{0,2},{1,0},{3,1},{5,3},{7,5},{6,7},{4,6},{2,4},{8,10},{9,8},{11,9... | collective-permute-start | bytes 614408 | tf_op jit(solution)/shard_map/ppermute | solution.py:82
  84.1 0.5 collective-permute-start.11
  84.7 2.0 %collective-permute-done.32 = f32[40,1280]{1,0:T(8,128)S(1)} collective-permute-done((f32[40,1280]{1,0:T(8,128)S(1)}, f32[40,1280]{1,0:T(8,128)S(1)}, u32[]{:S(2)}, u32[]{:S(2)}) %collective-permute-start.32) | collective-permute-done | bytes 204832 | tf_op jit(solution)/shard_map/ppermute | solution.py:82
  86.8 1.6 %collective-permute-start.33 = (f32[40,1280]{1,0:T(8,128)S(1)}, f32[40,1280]{1,0:T(8,128)S(1)}, u32[]{:S(2)}, u32[]{:S(2)}) collective-permute-start(f32[40,1280]{1,0:T(8,128)S(1)} %add.615), channel_id=1, source_target_pairs={{0,2},{1,0},{3,1},{5,3},{7,5},{6,7},{4,6},{2,4},{8,10},{9,8},{11,9... | collective-permute-start | bytes 614408 | tf_op jit(solution)/shard_map/ppermute | solution.py:82
  88.5 0.5 collective-permute-start.26
  89.0 2.2 %collective-permute-done.18 = f32[40,1280]{1,0:T(8,128)S(1)} collective-permute-done((f32[40,1280]{1,0:T(8,128)S(1)}, f32[40,1280]{1,0:T(8,128)S(1)}, u32[]{:S(2)}, u32[]{:S(2)}) %collective-permute-start.18) | collective-permute-done | bytes 204832 | tf_op jit(solution)/shard_map/ppermute | solution.py:82
  91.2 1.6 %collective-permute-start.19 = (f32[40,1280]{1,0:T(8,128)S(1)}, f32[40,1280]{1,0:T(8,128)S(1)}, u32[]{:S(2)}, u32[]{:S(2)}) collective-permute-start(f32[40,1280]{1,0:T(8,128)S(1)} %add.565), channel_id=1, source_target_pairs={{0,2},{1,0},{3,1},{5,3},{7,5},{6,7},{4,6},{2,4},{8,10},{9,8},{11,9... | collective-permute-start | bytes 614408 | tf_op jit(solution)/shard_map/ppermute | solution.py:82
  92.9 0.5 collective-permute-start.12
  93.5 2.1 %collective-permute-done.33 = f32[40,1280]{1,0:T(8,128)S(1)} collective-permute-done((f32[40,1280]{1,0:T(8,128)S(1)}, f32[40,1280]{1,0:T(8,128)S(1)}, u32[]{:S(2)}, u32[]{:S(2)}) %collective-permute-start.33) | collective-permute-done | bytes 204832 | tf_op jit(solution)/shard_map/ppermute | solution.py:82
  95.6 1.6 %collective-permute-start.34 = (f32[40,1280]{1,0:T(8,128)S(1)}, f32[40,1280]{1,0:T(8,128)S(1)}, u32[]{:S(2)}, u32[]{:S(2)}) collective-permute-start(f32[40,1280]{1,0:T(8,128)S(1)} %add.618), channel_id=1, source_target_pairs={{0,2},{1,0},{3,1},{5,3},{7,5},{6,7},{4,6},{2,4},{8,10},{9,8},{11,9... | collective-permute-start | bytes 614408 | tf_op jit(solution)/shard_map/ppermute | solution.py:82
  97.3 0.5 collective-permute-start.27
  97.8 2.2 %collective-permute-done.19 = f32[40,1280]{1,0:T(8,128)S(1)} collective-permute-done((f32[40,1280]{1,0:T(8,128)S(1)}, f32[40,1280]{1,0:T(8,128)S(1)}, u32[]{:S(2)}, u32[]{:S(2)}) %collective-permute-start.19) | collective-permute-done | bytes 204832 | tf_op jit(solution)/shard_map/ppermute | solution.py:82
  100.0 1.6 %collective-permute-start.20 = (f32[40,1280]{1,0:T(8,128)S(1)}, f32[40,1280]{1,0:T(8,128)S(1)}, u32[]{:S(2)}, u32[]{:S(2)}) collective-permute-start(f32[40,1280]{1,0:T(8,128)S(1)} %add.570), channel_id=1, source_target_pairs={{0,2},{1,0},{3,1},{5,3},{7,5},{6,7},{4,6},{2,4},{8,10},{9,8},{11,9... | collective-permute-start | bytes 614408 | tf_op jit(solution)/shard_map/ppermute | solution.py:82
  101.6 0.5 collective-permute-start.13
  102.3 2.1 %collective-permute-done.34 = f32[40,1280]{1,0:T(8,128)S(1)} collective-permute-done((f32[40,1280]{1,0:T(8,128)S(1)}, f32[40,1280]{1,0:T(8,128)S(1)}, u32[]{:S(2)}, u32[]{:S(2)}) %collective-permute-start.34) | collective-permute-done | bytes 204832 | tf_op jit(solution)/shard_map/ppermute | solution.py:82
  104.4 1.6 %collective-permute-done.27 = f32[40,1280]{1,0:T(8,128)S(1)} collective-permute-done((f32[40,1280]{1,0:T(8,128)S(1)}, f32[40,1280]{1,0:T(8,128)S(1)}, u32[]{:S(2)}, u32[]{:S(2)}) %collective-permute-start.27) | collective-permute-done | bytes 204832 | tf_op jit(solution)/shard_map/ppermute | solution.py:82
  106.0 2.2 %collective-permute-done.20 = f32[40,1280]{1,0:T(8,128)S(1)} collective-permute-done((f32[40,1280]{1,0:T(8,128)S(1)}, f32[40,1280]{1,0:T(8,128)S(1)}, u32[]{:S(2)}, u32[]{:S(2)}) %collective-permute-start.20) | collective-permute-done | bytes 204832 | tf_op jit(solution)/shard_map/ppermute | solution.py:82
  108.2 1.3 %collective-permute-done.13 = f32[40,1280]{1,0:T(8,128)S(1)} collective-permute-done((f32[40,1280]{1,0:T(8,128)S(1)}, f32[40,1280]{1,0:T(8,128)S(1)}, u32[]{:S(2)}, u32[]{:S(2)}) %collective-permute-start.13) | collective-permute-done | bytes 204832 | tf_op jit(solution)/shard_map/ppermute | solution.py:82
  109.5 2.0 %add_divide_fusion = (f32[160,1280]{1,0:T(8,128)}, f32[160,1280]{1,0:T(8,128)}, f32[160,1280]{1,0:T(8,128)}, f32[160,1280]{1,0:T(8,128)}) fusion(f32[160,1280]{1,0:T(8,128)S(1)} %copy-done.2, f32[160,1280]{1,0:T(8,128)S(1)} %copy-done.3, f32[160,1280]{1,0:T(8,128)S(1)} %copy-done.4, f32[40,1280]{1,0:T(8,128)S(1)} %add.621, f32[40,1280]{1,0:T(8,128)S(1)} %add.598, ...), kind=kLoop, calls=%fused_computation.16 | loop fusion | flops 3481600 | bytes 6553600 | tf_op jit(solution)/shard_map/div | solution.py:189
  (87 shorter events, 1.5 us)
Async XLA Ops:
  0.6 7.3 %copy-start = (bf16[1280,1280]{1,0:T(8,128)(2,1)S(1)}, bf16[1280,1280]{1,0:T(8,128)(2,1)}, u32[]{:S(2)}) copy-start(bf16[1280,1280]{1,0:T(8,128)(2,1)} %param.8) | copy-start | bytes 9830404
  4.9 20.4 %collective-permute-start = (bf16[128,2560]{1,0:T(8,128)(2,1)}, bf16[128,2560]{1,0:T(8,128)(2,1)}, u32[]{:S(2)}, u32[]{:S(2)}) collective-permute-start(bf16[128,2560]{1,0:T(8,128)(2,1)} %get-tuple-element.76), channel_id=1, source_target_pairs={{0,8},{8,0},{16,24},{24,16},{1,9},{9,1},{17,25},{25,17},{2,10},{10... | collective-permute-start | bytes 1966088 | tf_op jit(solution)/shard_map/ppermute | solution.py:106
  5.4 18.2 %collective-permute-start.1 = (bf16[128,2560]{1,0:T(8,128)(2,1)}, bf16[128,2560]{1,0:T(8,128)(2,1)}, u32[]{:S(2)}, u32[]{:S(2)}) collective-permute-start(bf16[128,2560]{1,0:T(8,128)(2,1)} %get-tuple-element.75), channel_id=1, source_target_pairs={{0,16},{8,24},{16,0},{24,8},{1,17},{9,25},{17,1},{25,9},{2,18},{10... | collective-permute-start | bytes 1966088 | tf_op jit(solution)/shard_map/ppermute | solution.py:103
  10.1 13.4 %copy-start.5 = (bf16[128,1280]{1,0:T(8,128)(2,1)S(1)}, bf16[128,1280]{1,0:T(8,128)(2,1)}, u32[]{:S(2)}) copy-start(bf16[128,1280]{1,0:T(8,128)(2,1)} %get-tuple-element.35) | copy-start | bytes 983044
  23.6 9.5 %collective-permute-start.2 = (bf16[128,1280]{1,0:T(8,128)(2,1)S(1)}, bf16[128,1280]{1,0:T(8,128)(2,1)S(1)}, u32[]{:S(2)}, u32[]{:S(2)}) collective-permute-start(bf16[128,1280]{1,0:T(8,128)(2,1)S(1)} %copy-done.5), channel_id=1, source_target_pairs={{0,16},{8,24},{16,0},{24,8},{1,17},{9,25},{17,1},{25,9},{2,18},{10... | collective-permute-start | bytes 983048 | tf_op jit(solution)/shard_map/ppermute | solution.py:108
  25.3 9.8 %collective-permute-start.3 = (bf16[128,2560]{1,0:T(8,128)(2,1)}, bf16[128,2560]{1,0:T(8,128)(2,1)S(1)}, u32[]{:S(2)}, u32[]{:S(2)}) collective-permute-start(bf16[128,2560]{1,0:T(8,128)(2,1)} %collective-permute-done.1), channel_id=1, source_target_pairs={{0,8},{8,0},{16,24},{24,16},{1,9},{9,1},{17,25},{25,17},{2,10},{10... | collective-permute-start | bytes 1966088 | tf_op jit(solution)/shard_map/ppermute | solution.py:109
  37.6 3.1 %collective-permute-start.4 = (f32[1]{0:T(128)}, f32[1]{0:T(128)}, u32[]{:S(2)}, u32[]{:S(2)}) collective-permute-start(f32[1]{0:T(128)} %bitcast.5), channel_id=1, source_target_pairs={{0,8},{8,0},{16,24},{24,16},{1,9},{9,1},{17,25},{25,17},{2,10},{10... | collective-permute-start | bytes 20 | tf_op jit(solution)/shard_map/ppermute | solution.py:122
  37.6 4.4 %collective-permute-start.5 = (f32[1]{0:T(128)}, f32[1]{0:T(128)}, u32[]{:S(2)}, u32[]{:S(2)}) collective-permute-start(f32[1]{0:T(128)} %bitcast.5), channel_id=1, source_target_pairs={{0,16},{8,24},{16,0},{24,8},{1,17},{9,25},{17,1},{25,9},{2,18},{10... | collective-permute-start | bytes 20 | tf_op jit(solution)/shard_map/ppermute | solution.py:122
  39.2 3.1 %collective-permute-start.6 = (f32[1]{0:T(128)}, f32[1]{0:T(128)}, u32[]{:S(2)}, u32[]{:S(2)}) collective-permute-start(f32[1]{0:T(128)} %bitcast.5), channel_id=1, source_target_pairs={{0,24},{8,16},{16,8},{24,0},{1,25},{9,17},{17,9},{25,1},{2,26},{10... | collective-permute-start | bytes 20 | tf_op jit(solution)/shard_map/ppermute | solution.py:122
  40.7 33.0 %copy-start.1 = (bf16[512,1280]{1,0:T(8,128)(2,1)}, bf16[512,1280]{1,0:T(8,128)(2,1)S(1)}, u32[]{:S(2)}) copy-start(bf16[512,1280]{1,0:T(8,128)(2,1)S(1)} %fusion.1) | copy-start | bytes 3932164
  43.7 8.0 %collective-permute-start.28 = (f32[40,1280]{1,0:T(8,128)S(1)}, f32[40,1280]{1,0:T(8,128)S(1)}, u32[]{:S(2)}, u32[]{:S(2)}) collective-permute-start(f32[40,1280]{1,0:T(8,128)S(1)} %get-tuple-element.69), channel_id=1, source_target_pairs={{0,2},{1,0},{3,1},{5,3},{7,5},{6,7},{4,6},{2,4},{8,10},{9,8},{11,9... | collective-permute-start | bytes 614408 | tf_op jit(solution)/shard_map/ppermute | solution.py:82
  45.4 8.0 %collective-permute-start.21 = (f32[40,1280]{1,0:T(8,128)S(1)}, f32[40,1280]{1,0:T(8,128)S(1)}, u32[]{:S(2)}, u32[]{:S(2)}) collective-permute-start(f32[40,1280]{1,0:T(8,128)S(1)} %get-tuple-element.70), channel_id=1, source_target_pairs={{0,1},{1,3},{3,5},{5,7},{7,6},{6,4},{4,2},{2,0},{8,9},{9,11},{11,1... | collective-permute-start | bytes 614408 | tf_op jit(solution)/shard_map/ppermute | solution.py:82
  45.8 10.3 %collective-permute-start.14 = (f32[40,1280]{1,0:T(8,128)S(1)}, f32[40,1280]{1,0:T(8,128)S(1)}, u32[]{:S(2)}, u32[]{:S(2)}) collective-permute-start(f32[40,1280]{1,0:T(8,128)S(1)} %get-tuple-element.71), channel_id=1, source_target_pairs={{0,2},{1,0},{3,1},{5,3},{7,5},{6,7},{4,6},{2,4},{8,10},{9,8},{11,9... | collective-permute-start | bytes 614408 | tf_op jit(solution)/shard_map/ppermute | solution.py:82
  47.4 10.3 %collective-permute-start.7 = (f32[40,1280]{1,0:T(8,128)S(1)}, f32[40,1280]{1,0:T(8,128)S(1)}, u32[]{:S(2)}, u32[]{:S(2)}) collective-permute-start(f32[40,1280]{1,0:T(8,128)S(1)} %get-tuple-element.68), channel_id=1, source_target_pairs={{0,1},{1,3},{3,5},{5,7},{7,6},{6,4},{4,2},{2,0},{8,9},{9,11},{11,1... | collective-permute-start | bytes 614408 | tf_op jit(solution)/shard_map/ppermute | solution.py:82
  51.7 8.8 %collective-permute-start.29 = (f32[40,1280]{1,0:T(8,128)S(1)}, f32[40,1280]{1,0:T(8,128)S(1)}, u32[]{:S(2)}, u32[]{:S(2)}) collective-permute-start(f32[40,1280]{1,0:T(8,128)S(1)} %add.603), channel_id=1, source_target_pairs={{0,2},{1,0},{3,1},{5,3},{7,5},{6,7},{4,6},{2,4},{8,10},{9,8},{11,9... | collective-permute-start | bytes 614408 | tf_op jit(solution)/shard_map/ppermute | solution.py:82
  53.4 8.8 %collective-permute-start.22 = (f32[40,1280]{1,0:T(8,128)S(1)}, f32[40,1280]{1,0:T(8,128)S(1)}, u32[]{:S(2)}, u32[]{:S(2)}) collective-permute-start(f32[40,1280]{1,0:T(8,128)S(1)} %add.580), channel_id=1, source_target_pairs={{0,1},{1,3},{3,5},{5,7},{7,6},{6,4},{4,2},{2,0},{8,9},{9,11},{11,1... | collective-permute-start | bytes 614408 | tf_op jit(solution)/shard_map/ppermute | solution.py:82
  56.1 8.7 %collective-permute-start.15 = (f32[40,1280]{1,0:T(8,128)S(1)}, f32[40,1280]{1,0:T(8,128)S(1)}, u32[]{:S(2)}, u32[]{:S(2)}) collective-permute-start(f32[40,1280]{1,0:T(8,128)S(1)} %add.545), channel_id=1, source_target_pairs={{0,2},{1,0},{3,1},{5,3},{7,5},{6,7},{4,6},{2,4},{8,10},{9,8},{11,9... | collective-permute-start | bytes 614408 | tf_op jit(solution)/shard_map/ppermute | solution.py:82
  57.8 8.7 %collective-permute-start.8 = (f32[40,1280]{1,0:T(8,128)S(1)}, f32[40,1280]{1,0:T(8,128)S(1)}, u32[]{:S(2)}, u32[]{:S(2)}) collective-permute-start(f32[40,1280]{1,0:T(8,128)S(1)} %add.518), channel_id=1, source_target_pairs={{0,1},{1,3},{3,5},{5,7},{7,6},{6,4},{4,2},{2,0},{8,9},{9,11},{11,1... | collective-permute-start | bytes 614408 | tf_op jit(solution)/shard_map/ppermute | solution.py:82
  60.5 8.7 %collective-permute-start.30 = (f32[40,1280]{1,0:T(8,128)S(1)}, f32[40,1280]{1,0:T(8,128)S(1)}, u32[]{:S(2)}, u32[]{:S(2)}) collective-permute-start(f32[40,1280]{1,0:T(8,128)S(1)} %add.606), channel_id=1, source_target_pairs={{0,2},{1,0},{3,1},{5,3},{7,5},{6,7},{4,6},{2,4},{8,10},{9,8},{11,9... | collective-permute-start | bytes 614408 | tf_op jit(solution)/shard_map/ppermute | solution.py:82
  62.2 8.7 %collective-permute-start.23 = (f32[40,1280]{1,0:T(8,128)S(1)}, f32[40,1280]{1,0:T(8,128)S(1)}, u32[]{:S(2)}, u32[]{:S(2)}) collective-permute-start(f32[40,1280]{1,0:T(8,128)S(1)} %add.583), channel_id=1, source_target_pairs={{0,1},{1,3},{3,5},{5,7},{7,6},{6,4},{4,2},{2,0},{8,9},{9,11},{11,1... | collective-permute-start | bytes 614408 | tf_op jit(solution)/shard_map/ppermute | solution.py:82
  64.9 8.7 %collective-permute-start.16 = (f32[40,1280]{1,0:T(8,128)S(1)}, f32[40,1280]{1,0:T(8,128)S(1)}, u32[]{:S(2)}, u32[]{:S(2)}) collective-permute-start(f32[40,1280]{1,0:T(8,128)S(1)} %add.550), channel_id=1, source_target_pairs={{0,2},{1,0},{3,1},{5,3},{7,5},{6,7},{4,6},{2,4},{8,10},{9,8},{11,9... | collective-permute-start | bytes 614408 | tf_op jit(solution)/shard_map/ppermute | solution.py:82
  66.5 8.8 %collective-permute-start.9 = (f32[40,1280]{1,0:T(8,128)S(1)}, f32[40,1280]{1,0:T(8,128)S(1)}, u32[]{:S(2)}, u32[]{:S(2)}) collective-permute-start(f32[40,1280]{1,0:T(8,128)S(1)} %add.521), channel_id=1, source_target_pairs={{0,1},{1,3},{3,5},{5,7},{7,6},{6,4},{4,2},{2,0},{8,9},{9,11},{11,1... | collective-permute-start | bytes 614408 | tf_op jit(solution)/shard_map/ppermute | solution.py:82
  69.3 8.7 %collective-permute-start.31 = (f32[40,1280]{1,0:T(8,128)S(1)}, f32[40,1280]{1,0:T(8,128)S(1)}, u32[]{:S(2)}, u32[]{:S(2)}) collective-permute-start(f32[40,1280]{1,0:T(8,128)S(1)} %add.609), channel_id=1, source_target_pairs={{0,2},{1,0},{3,1},{5,3},{7,5},{6,7},{4,6},{2,4},{8,10},{9,8},{11,9... | collective-permute-start | bytes 614408 | tf_op jit(solution)/shard_map/ppermute | solution.py:82
  70.9 8.7 %collective-permute-start.24 = (f32[40,1280]{1,0:T(8,128)S(1)}, f32[40,1280]{1,0:T(8,128)S(1)}, u32[]{:S(2)}, u32[]{:S(2)}) collective-permute-start(f32[40,1280]{1,0:T(8,128)S(1)} %add.586), channel_id=1, source_target_pairs={{0,1},{1,3},{3,5},{5,7},{7,6},{6,4},{4,2},{2,0},{8,9},{9,11},{11,1... | collective-permute-start | bytes 614408 | tf_op jit(solution)/shard_map/ppermute | solution.py:82
  73.7 8.7 %collective-permute-start.17 = (f32[40,1280]{1,0:T(8,128)S(1)}, f32[40,1280]{1,0:T(8,128)S(1)}, u32[]{:S(2)}, u32[]{:S(2)}) collective-permute-start(f32[40,1280]{1,0:T(8,128)S(1)} %add.555), channel_id=1, source_target_pairs={{0,2},{1,0},{3,1},{5,3},{7,5},{6,7},{4,6},{2,4},{8,10},{9,8},{11,9... | collective-permute-start | bytes 614408 | tf_op jit(solution)/shard_map/ppermute | solution.py:82
  75.3 8.8 %collective-permute-start.10 = (f32[40,1280]{1,0:T(8,128)S(1)}, f32[40,1280]{1,0:T(8,128)S(1)}, u32[]{:S(2)}, u32[]{:S(2)}) collective-permute-start(f32[40,1280]{1,0:T(8,128)S(1)} %add.524), channel_id=1, source_target_pairs={{0,1},{1,3},{3,5},{5,7},{7,6},{6,4},{4,2},{2,0},{8,9},{9,11},{11,1... | collective-permute-start | bytes 614408 | tf_op jit(solution)/shard_map/ppermute | solution.py:82
  78.0 8.8 %collective-permute-start.32 = (f32[40,1280]{1,0:T(8,128)S(1)}, f32[40,1280]{1,0:T(8,128)S(1)}, u32[]{:S(2)}, u32[]{:S(2)}) collective-permute-start(f32[40,1280]{1,0:T(8,128)S(1)} %add.612), channel_id=1, source_target_pairs={{0,2},{1,0},{3,1},{5,3},{7,5},{6,7},{4,6},{2,4},{8,10},{9,8},{11,9... | collective-permute-start | bytes 614408 | tf_op jit(solution)/shard_map/ppermute | solution.py:82
  79.7 8.8 %collective-permute-start.25 = (f32[40,1280]{1,0:T(8,128)S(1)}, f32[40,1280]{1,0:T(8,128)S(1)}, u32[]{:S(2)}, u32[]{:S(2)}) collective-permute-start(f32[40,1280]{1,0:T(8,128)S(1)} %add.589), channel_id=1, source_target_pairs={{0,1},{1,3},{3,5},{5,7},{7,6},{6,4},{4,2},{2,0},{8,9},{9,11},{11,1... | collective-permute-start | bytes 614408 | tf_op jit(solution)/shard_map/ppermute | solution.py:82
  82.4 27.1 %copy-start.2 = (f32[160,1280]{1,0:T(8,128)S(1)}, f32[160,1280]{1,0:T(8,128)}, u32[]{:S(2)}) copy-start(f32[160,1280]{1,0:T(8,128)} %param.11) | copy-start | bytes 2457604
  82.4 27.1 %copy-start.3 = (f32[160,1280]{1,0:T(8,128)S(1)}, f32[160,1280]{1,0:T(8,128)}, u32[]{:S(2)}) copy-start(f32[160,1280]{1,0:T(8,128)} %param.10) | copy-start | bytes 2457604
  82.5 27.1 %copy-start.4 = (f32[160,1280]{1,0:T(8,128)S(1)}, f32[160,1280]{1,0:T(8,128)}, u32[]{:S(2)}) copy-start(f32[160,1280]{1,0:T(8,128)} %param.9) | copy-start | bytes 2457604
  82.5 8.7 %collective-permute-start.18 = (f32[40,1280]{1,0:T(8,128)S(1)}, f32[40,1280]{1,0:T(8,128)S(1)}, u32[]{:S(2)}, u32[]{:S(2)}) collective-permute-start(f32[40,1280]{1,0:T(8,128)S(1)} %add.560), channel_id=1, source_target_pairs={{0,2},{1,0},{3,1},{5,3},{7,5},{6,7},{4,6},{2,4},{8,10},{9,8},{11,9... | collective-permute-start | bytes 614408 | tf_op jit(solution)/shard_map/ppermute | solution.py:82
  84.1 8.7 %collective-permute-start.11 = (f32[40,1280]{1,0:T(8,128)S(1)}, f32[40,1280]{1,0:T(8,128)S(1)}, u32[]{:S(2)}, u32[]{:S(2)}) collective-permute-start(f32[40,1280]{1,0:T(8,128)S(1)} %add.527), channel_id=1, source_target_pairs={{0,1},{1,3},{3,5},{5,7},{7,6},{6,4},{4,2},{2,0},{8,9},{9,11},{11,1... | collective-permute-start | bytes 614408 | tf_op jit(solution)/shard_map/ppermute | solution.py:82
  86.8 8.8 %collective-permute-start.33 = (f32[40,1280]{1,0:T(8,128)S(1)}, f32[40,1280]{1,0:T(8,128)S(1)}, u32[]{:S(2)}, u32[]{:S(2)}) collective-permute-start(f32[40,1280]{1,0:T(8,128)S(1)} %add.615), channel_id=1, source_target_pairs={{0,2},{1,0},{3,1},{5,3},{7,5},{6,7},{4,6},{2,4},{8,10},{9,8},{11,9... | collective-permute-start | bytes 614408 | tf_op jit(solution)/shard_map/ppermute | solution.py:82
  88.5 8.8 %collective-permute-start.26 = (f32[40,1280]{1,0:T(8,128)S(1)}, f32[40,1280]{1,0:T(8,128)S(1)}, u32[]{:S(2)}, u32[]{:S(2)}) collective-permute-start(f32[40,1280]{1,0:T(8,128)S(1)} %add.592), channel_id=1, source_target_pairs={{0,1},{1,3},{3,5},{5,7},{7,6},{6,4},{4,2},{2,0},{8,9},{9,11},{11,1... | collective-permute-start | bytes 614408 | tf_op jit(solution)/shard_map/ppermute | solution.py:82
  91.2 8.8 %collective-permute-start.19 = (f32[40,1280]{1,0:T(8,128)S(1)}, f32[40,1280]{1,0:T(8,128)S(1)}, u32[]{:S(2)}, u32[]{:S(2)}) collective-permute-start(f32[40,1280]{1,0:T(8,128)S(1)} %add.565), channel_id=1, source_target_pairs={{0,2},{1,0},{3,1},{5,3},{7,5},{6,7},{4,6},{2,4},{8,10},{9,8},{11,9... | collective-permute-start | bytes 614408 | tf_op jit(solution)/shard_map/ppermute | solution.py:82
  92.9 8.8 %collective-permute-start.12 = (f32[40,1280]{1,0:T(8,128)S(1)}, f32[40,1280]{1,0:T(8,128)S(1)}, u32[]{:S(2)}, u32[]{:S(2)}) collective-permute-start(f32[40,1280]{1,0:T(8,128)S(1)} %add.530), channel_id=1, source_target_pairs={{0,1},{1,3},{3,5},{5,7},{7,6},{6,4},{4,2},{2,0},{8,9},{9,11},{11,1... | collective-permute-start | bytes 614408 | tf_op jit(solution)/shard_map/ppermute | solution.py:82
  95.6 8.8 %collective-permute-start.34 = (f32[40,1280]{1,0:T(8,128)S(1)}, f32[40,1280]{1,0:T(8,128)S(1)}, u32[]{:S(2)}, u32[]{:S(2)}) collective-permute-start(f32[40,1280]{1,0:T(8,128)S(1)} %add.618), channel_id=1, source_target_pairs={{0,2},{1,0},{3,1},{5,3},{7,5},{6,7},{4,6},{2,4},{8,10},{9,8},{11,9... | collective-permute-start | bytes 614408 | tf_op jit(solution)/shard_map/ppermute | solution.py:82
  97.3 8.7 %collective-permute-start.27 = (f32[40,1280]{1,0:T(8,128)S(1)}, f32[40,1280]{1,0:T(8,128)S(1)}, u32[]{:S(2)}, u32[]{:S(2)}) collective-permute-start(f32[40,1280]{1,0:T(8,128)S(1)} %add.595), channel_id=1, source_target_pairs={{0,1},{1,3},{3,5},{5,7},{7,6},{6,4},{4,2},{2,0},{8,9},{9,11},{11,1... | collective-permute-start | bytes 614408 | tf_op jit(solution)/shard_map/ppermute | solution.py:82
  100.0 8.2 %collective-permute-start.20 = (f32[40,1280]{1,0:T(8,128)S(1)}, f32[40,1280]{1,0:T(8,128)S(1)}, u32[]{:S(2)}, u32[]{:S(2)}) collective-permute-start(f32[40,1280]{1,0:T(8,128)S(1)} %add.570), channel_id=1, source_target_pairs={{0,2},{1,0},{3,1},{5,3},{7,5},{6,7},{4,6},{2,4},{8,10},{9,8},{11,9... | collective-permute-start | bytes 614408 | tf_op jit(solution)/shard_map/ppermute | solution.py:82
  101.6 7.8 %collective-permute-start.13 = (f32[40,1280]{1,0:T(8,128)S(1)}, f32[40,1280]{1,0:T(8,128)S(1)}, u32[]{:S(2)}, u32[]{:S(2)}) collective-permute-start(f32[40,1280]{1,0:T(8,128)S(1)} %add.533), channel_id=1, source_target_pairs={{0,1},{1,3},{3,5},{5,7},{7,6},{6,4},{4,2},{2,0},{8,9},{9,11},{11,1... | collective-permute-start | bytes 614408 | tf_op jit(solution)/shard_map/ppermute | solution.py:82

commit v7 on v6

--- a/solution.py
+++ b/solution.py
@@ -61,7 +61,7 @@
     return out
 
 
-def ring_reduce_scatter(parts, ring, pieces):
+def ring_reduce_scatter(rows_of, factor, ring, pieces):
     n = len(ring)
     pos_of = [0] * n
     for k, d in enumerate(ring):
@@ -70,21 +70,41 @@
     pos = lookup(pos_of, me)
     right = [(ring[k], ring[(k + 1) % n]) for k in range(n)]
     left = [(ring[k], ring[(k - 1) % n]) for k in range(n)]
+    from_prev = lax.ppermute(factor, "dp", right)
+    from_next = lax.ppermute(factor, "dp", left)
+
     def block(s, step):
         return lookup(ring, (pos - 1 - s) % n if step < 0 else (pos + 1 + s) % n)
 
+    def scaled(s, step, which, after):
+        rows = rows_of(block(s, step), which, after)
+        return lax.optimization_barrier(factor * rows)
+
     chains = [(-1 if c % 2 == 0 else 1, c) for c in range(pieces)]
-    own = [parts(block(0, step), which, None) for step, which in chains]
+    own = [rows_of(block(0, step), which, None) for step, which in chains]
     acc = [None] * pieces
+    unscaled = True
     for s in range(n - 1):
-        send = [o if x is None else x + o for x, o in zip(acc, own)]
+        if s == 0:
+            send = own
+        elif unscaled:
+            send = [
+                x * (from_prev if step < 0 else from_next) + o
+                for x, o, (step, _) in zip(acc, own, chains)
+            ]
+            unscaled = False
+        else:
+            send = [x + o for x, o in zip(acc, own)]
         acc = [
             lax.ppermute(v, "dp", right if step < 0 else left)
             for v, (step, _) in zip(send, chains)
         ]
         own = [
-            parts(block(s + 1, step), which, v)
-            for v, (step, which) in zip(send, chains)
+            scaled(s + 1, step, which, v) for v, (step, which) in zip(send, chains)
+        ]
+    if unscaled:
+        acc = [
+            x * (from_prev if step < 0 else from_next) for x, (step, _) in zip(acc, chains)
         ]
     return jnp.concatenate([x + o for x, o in zip(acc, own)], axis=0)
 
@@ -172,15 +192,20 @@
     pieces = 4 if owned_rows % 32 == 0 else 2
     half = owned_rows // pieces
 
-    def parts(block, which, after):
-        source = grads
+    if images_here == 1:
+        ring_rows, ring_factor = grads[0], factor[0]
+    else:
+        ring_rows = jnp.sum(factor[:, None, None] * grads, axis=0)
+        ring_factor = jnp.float32(1.0)
+
+    def rows_of(block, which, after):
+        source = ring_rows
         if after is not None:
-            _, source = lax.optimization_barrier((after, grads))
+            _, source = lax.optimization_barrier((after, source))
         start = block * owned_rows + which * half
-        rows = lax.dynamic_slice_in_dim(source, start, half, axis=1)
-        return lax.optimization_barrier(jnp.sum(factor[:, None, None] * rows, axis=0))
-
-    owned = ring_reduce_scatter(parts, ring, pieces)
+        return lax.dynamic_slice_in_dim(source, start, half, axis=0)
+
+    owned = ring_reduce_scatter(rows_of, ring_factor, ring, pieces)
     clipped_mean = owned / images_all
     noisy = clipped_mean + noise_ratio * clip * noise / images_all
     new_first = beta_one * first_moment + (1.0 - beta_one) * noisy

time: 113 us -> 114 us (level)
  waiting for transfers between devices: 47.2 us -> 39.8 us
  starting transfers between devices: 36.2 us -> 42.1 us
  other arithmetic: 5.55 us -> 7.81 us
    ppermute x28, waiting for transfers between devices: 34.4 us -> 26.6 us  [ring_reduce_scatter(): lax.ppermute(v, 'dp', right if step < 0 else left)]
    ppermute x0 -> x2, starting transfers between devices: none -> 5.84 us  [the longest x1 2.98 us: ring_reduce_scatter(): from_next = lax.ppermute(factor, 'dp', left)]
    add x24, other arithmetic: 0.61 us -> 3 us  [the longest x4 2.46 us: ring_reduce_scatter(): x * (from_prev if step < 0 else from_next) + o]
  transfers between devices with their start and end apart: 35 -> 37, of which waited for: 19 -> 27; matrix products, arithmetic and copies ran while one was open for 14% -> 16% of each run, Pallas kernels for 0% -> 0%
where the time goes in v7:
time: 114 us; the launch traced here: 113 us
  starting transfers between devices  42.1 us (37%)
  waiting for transfers between devices  39.8 us (35%)
  matrix products  16.5 us (14%)
  other arithmetic  7.81 us (7%)
  between operations  4.75 us (4%)
  local copies, waits for them, and re-layouts  2.3 us (2%)
    ppermute x28, starting transfers between devices, ring_reduce_scatter(): lax.ppermute(v, 'dp', right if step < 0 else left)  29.7 us
    ppermute x28, waiting for transfers between devices, ring_reduce_scatter(): lax.ppermute(v, 'dp', right if step < 0 else left)  26.6 us
    ppermute x1, waiting for transfers between devices, exchange_four(): lax.ppermute(jnp.concatenate([cols(a ^ 3), grad_rows], axis=1), 'aug', ov...  11.3 us
    dot_general x4, matrix products, per_device(): term = jnp.dot(h_piece.T, g_piece, preferred_element_type=jnp.float32)  8.8 us
    dot_general x4, matrix products, project_back(): lax.dot_general(rows, down_weight, (((1,), (1,)), ((), ())), preferred_el...  7.72 us
    ppermute x1, starting transfers between devices, ring_reduce_scatter(): from_next = lax.ppermute(factor, 'dp', left)  2.98 us
    ppermute x1, starting transfers between devices, ring_reduce_scatter(): from_prev = lax.ppermute(factor, 'dp', right)  2.87 us
    ppermute x1, starting transfers between devices, exchange_four(): lax.ppermute(jnp.concatenate([cols(a ^ 3), grad_rows], axis=1), 'aug', ov...  2.49 us
  transfers between devices with their start and end apart: 37, of which 27 were waited for; matrix products, arithmetic and copies ran while one was open for 16% of the time, Pallas kernels for 0%

profile of v7, /device:TPU:0, one launch (start us, length us, event | category | flops | bytes accessed | tf_op | source)
XLA Modules:
  0.0 113.3 jit_solution(6650209566797533522)
XLA Ops:
  0.7 2.1 %dynamic-slice_bitcast_fusion = (bf16[128,1280]{1,0:T(8,128)(2,1)}, bf16[128,1280]{1,0:T(8,128)(2,1)S(1)}, bf16[128,1280]{1,0:T(8,128)(2,1)S(1)}) fusion(bf16[1,1,128,5120]{3,2,1,0:T(8,128)(2,1)} %param.6, s32[]{:T(128)S(6)} %select_n.691, s32[]{:T(128)S(6)} %select_n.689, s32[]{:T(128)S(6)} %select_n.690), kind=kLoop, calls=%fused_computation.25 | loop fusion | bytes 1966092 | tf_op jit(solution)/shard_map/dynamic_slice | solution.py:119
  2.8 2.1 %pad_maximum_fusion = (bf16[128,2560]{1,0:T(8,128)(2,1)}, bf16[128,2560]{1,0:T(8,128)(2,1)}) fusion(bf16[128,1280]{1,0:T(8,128)(2,1)} %bitcast.22, bf16[128,1280]{1,0:T(8,128)(2,1)S(1)} %get-tuple-element.74, bf16[128,1280]{1,0:T(8,128)(2,1)S(1)} %get-tuple-element.73), kind=kLoop, calls=%fused_computation.19 | loop fusion | flops 2293760 | bytes 2293760 | tf_op jit(solution)/shard_map/concatenate | solution.py:124
  5.4 2.5 %collective-permute-start.1 = (bf16[128,2560]{1,0:T(8,128)(2,1)}, bf16[128,2560]{1,0:T(8,128)(2,1)}, u32[]{:S(2)}, u32[]{:S(2)}) collective-permute-start(bf16[128,2560]{1,0:T(8,128)(2,1)} %get-tuple-element.75), channel_id=1, source_target_pairs={{0,16},{8,24},{16,0},{24,8},{1,17},{9,25},{17,1},{25,9},{2,18},{10... | collective-permute-start | bytes 1966088 | tf_op jit(solution)/shard_map/ppermute | solution.py:123
  7.9 2.2 %fusion.4 = bf16[512,1280]{1,0:T(8,128)(2,1)S(1)} fusion(bf16[512,1280]{1,0:T(8,128)(2,1)S(1)} %broadcast_in_dim.4, s32[]{:T(128)S(6)} %select_n.859, bf16[1280,1280]{1,0:T(8,128)(2,1)S(1)} %copy-done, bf16[1,1,128,1280]{3,2,1,0:T(8,128)(2,1)} %param.7), kind=kOutput, calls=%fused_computation.12 | convolution fusion | flops 419594240 | bytes 3932164 | tf_op jit(solution)/shard_map/dot_general | solution.py:17
  10.1 2.2 %fusion.8 = f32[1280,1280]{1,0:T(8,128)S(1)} fusion(bf16[1,1,128,5120]{3,2,1,0:T(8,128)(2,1)} %param.6, s32[]{:T(128)S(6)} %select_n.688, bf16[1,1,128,1280]{3,2,1,0:T(8,128)(2,1)} %param.7), kind=kOutput, calls=%fused_computation.23 | convolution fusion | flops 419430400 | bytes 7208964 | tf_op jit(solution)/shard_map/dot_general | solution.py:171
  12.3 11.3 %collective-permute-done.1 = bf16[128,2560]{1,0:T(8,128)(2,1)} collective-permute-done((bf16[128,2560]{1,0:T(8,128)(2,1)}, bf16[128,2560]{1,0:T(8,128)(2,1)}, u32[]{:S(2)}, u32[]{:S(2)}) %collective-permute-start.1) | collective-permute-done | bytes 655392 | tf_op jit(solution)/shard_map/ppermute | solution.py:123
  23.6 1.7 %collective-permute-start.2 = (bf16[128,1280]{1,0:T(8,128)(2,1)S(1)}, bf16[128,1280]{1,0:T(8,128)(2,1)S(1)}, u32[]{:S(2)}, u32[]{:S(2)}) collective-permute-start(bf16[128,1280]{1,0:T(8,128)(2,1)S(1)} %copy-done.5), channel_id=1, source_target_pairs={{0,16},{8,24},{16,0},{24,8},{1,17},{9,25},{17,1},{25,9},{2,18},{10... | collective-permute-start | bytes 983048 | tf_op jit(solution)/shard_map/ppermute | solution.py:128
  25.3 2.1 %convolution_add_fusion.2 = f32[1280,1280]{1,0:T(8,128)S(1)} fusion(f32[1280,1280]{1,0:T(8,128)S(1)} %fusion.8, bf16[128,2560]{1,0:T(8,128)(2,1)} %collective-permute-done), kind=kOutput, calls=%fused_computation.2 | convolution fusion | flops 421068800 | bytes 13762560 | tf_op jit(solution)/shard_map/dot_general | solution.py:171
  27.4 2.2 %fusion.3 = bf16[512,1280]{1,0:T(8,128)(2,1)S(1)} fusion(bf16[512,1280]{1,0:T(8,128)(2,1)S(1)} %fusion.4, s32[]{:T(128)S(6)} %select_n.860, bf16[1280,1280]{1,0:T(8,128)(2,1)S(1)} %copy-done, bf16[128,2560]{1,0:T(8,128)(2,1)} %collective-permute-done), kind=kOutput, calls=%fused_computation.10 | convolution fusion | flops 419594240 | bytes 3932164 | tf_op jit(solution)/shard_map/dot_general | solution.py:17
  29.6 2.2 %fusion.2 = bf16[512,1280]{1,0:T(8,128)(2,1)S(1)} fusion(bf16[512,1280]{1,0:T(8,128)(2,1)S(1)} %fusion.3, s32[]{:T(128)S(6)} %select_n.861, bf16[1280,1280]{1,0:T(8,128)(2,1)S(1)} %copy-done, bf16[128,2560]{1,0:T(8,128)(2,1)} %collective-permute-done.1), kind=kOutput, calls=%fused_computation.8 | convolution fusion | flops 419594240 | bytes 3932164 | tf_op jit(solution)/shard_map/dot_general | solution.py:17
  31.8 1.3 %collective-permute-done.2 = bf16[128,1280]{1,0:T(8,128)(2,1)S(1)} collective-permute-done((bf16[128,1280]{1,0:T(8,128)(2,1)S(1)}, bf16[128,1280]{1,0:T(8,128)(2,1)S(1)}, u32[]{:S(2)}, u32[]{:S(2)}) %collective-permute-start.2) | collective-permute-done | bytes 327712 | tf_op jit(solution)/shard_map/ppermute | solution.py:128
  33.1 2.0 %convolution_add_fusion.1 = f32[1280,1280]{1,0:T(8,128)S(1)} fusion(f32[1280,1280]{1,0:T(8,128)S(1)} %convolution_add_fusion.2, bf16[128,1280]{1,0:T(8,128)(2,1)S(1)} %collective-permute-done.2, bf16[128,2560]{1,0:T(8,128)(2,1)} %collective-permute-done.1), kind=kOutput, calls=%fused_computation.1 | convolution fusion | flops 421068800 | bytes 13762560 | tf_op jit(solution)/shard_map/dot_general | solution.py:171
  35.1 2.5 %multiply_reduce_fusion = (f32[]{:T(128)}, f32[1280,1280]{1,0:T(8,128)S(1)}) fusion(f32[1280,1280]{1,0:T(8,128)S(1)} %convolution_add_fusion.1, bf16[128,2560]{1,0:T(8,128)(2,1)S(1)} %collective-permute-done.3), kind=kOutput, calls=%fused_computation.4 | convolution fusion | flops 425984000 | bytes 13762564 | tf_op jit(solution)/shard_map/dot_general | solution.py:171
  37.6 1.5 %collective-permute-start.5 = (f32[1]{0:T(128)}, f32[1]{0:T(128)}, u32[]{:S(2)}, u32[]{:S(2)}) collective-permute-start(f32[1]{0:T(128)} %bitcast.5), channel_id=1, source_target_pairs={{0,16},{8,24},{16,0},{24,8},{1,17},{9,25},{17,1},{25,9},{2,18},{10... | collective-permute-start | bytes 20 | tf_op jit(solution)/shard_map/ppermute | solution.py:142
  39.6 1.7 %collective-permute-start.30 = (f32[40,1280]{1,0:T(8,128)S(1)}, f32[40,1280]{1,0:T(8,128)S(1)}, u32[]{:S(2)}, u32[]{:S(2)}) collective-permute-start(f32[40,1280]{1,0:T(8,128)S(1)} %get-tuple-element.69), channel_id=1, source_target_pairs={{0,2},{1,0},{3,1},{5,3},{7,5},{6,7},{4,6},{2,4},{8,10},{9,8},{11,9... | collective-permute-start | bytes 614408 | tf_op jit(solution)/shard_map/ppermute | solution.py:99
  41.2 1.6 %collective-permute-start.15 = (f32[40,1280]{1,0:T(8,128)S(1)}, f32[40,1280]{1,0:T(8,128)S(1)}, u32[]{:S(2)}, u32[]{:S(2)}) collective-permute-start(f32[40,1280]{1,0:T(8,128)S(1)} %get-tuple-element.71), channel_id=1, source_target_pairs={{0,2},{1,0},{3,1},{5,3},{7,5},{6,7},{4,6},{2,4},{8,10},{9,8},{11,9... | collective-permute-start | bytes 614408 | tf_op jit(solution)/shard_map/ppermute | solution.py:99
  42.8 1.2 %fusion.1 = bf16[512,1280]{1,0:T(8,128)(2,1)S(1)} fusion(bf16[512,1280]{1,0:T(8,128)(2,1)S(1)} %fusion.2, s32[]{:T(128)S(6)} %select_n.862, bf16[1280,1280]{1,0:T(8,128)(2,1)S(1)} %copy-done, bf16[128,2560]{1,0:T(8,128)(2,1)S(1)} %collective-permute-done.3), kind=kOutput, calls=%fused_computation.6 | convolution fusion | flops 419594240 | bytes 3932164 | tf_op jit(solution)/shard_map/dot_general | solution.py:17
  47.6 3.0 %collective-permute-start.16 = (f32[]{:T(128)}, f32[]{:T(128)}, u32[]{:S(2)}, u32[]{:S(2)}) collective-permute-start(f32[]{:T(128)} %bitcast.6), channel_id=1, source_target_pairs={{0,2},{1,0},{3,1},{5,3},{7,5},{6,7},{4,6},{2,4},{8,10},{9,8},{11,9... | collective-permute-start | bytes 20 | tf_op jit(solution)/shard_map/ppermute | solution.py:74
  50.7 0.6 collective-permute-done.16
  51.3 2.9 %collective-permute-start.8 = (f32[]{:T(128)}, f32[]{:T(128)}, u32[]{:S(2)}, u32[]{:S(2)}) collective-permute-start(f32[]{:T(128)} %bitcast.6), channel_id=1, source_target_pairs={{0,1},{1,3},{3,5},{5,7},{7,6},{6,4},{4,2},{2,0},{8,9},{9,11},{11,1... | collective-permute-start | bytes 20 | tf_op jit(solution)/shard_map/ppermute | solution.py:73
  54.2 0.7 multiply_add_fusion.2
  54.8 0.7 collective-permute-start.31
  55.5 0.6 multiply_add_fusion.3
  56.1 1.5 %collective-permute-start.24 = (f32[40,1280]{1,0:T(8,128)S(1)}, f32[40,1280]{1,0:T(8,128)S(1)}, u32[]{:S(2)}, u32[]{:S(2)}) collective-permute-start(f32[40,1280]{1,0:T(8,128)S(1)} %multiply_add_fusion.3), channel_id=1, source_target_pairs={{0,1},{1,3},{3,5},{5,7},{7,6},{6,4},{4,2},{2,0},{8,9},{9,11},{11,1... | collective-permute-start | bytes 614408 | tf_op jit(solution)/shard_map/ppermute | solution.py:99
  57.5 0.7 multiply_add_fusion.4
  58.2 0.7 collective-permute-start.17
  58.9 0.6 multiply_add_fusion.5
  59.5 1.5 %collective-permute-start.9 = (f32[40,1280]{1,0:T(8,128)S(1)}, f32[40,1280]{1,0:T(8,128)S(1)}, u32[]{:S(2)}, u32[]{:S(2)}) collective-permute-start(f32[40,1280]{1,0:T(8,128)S(1)} %multiply_add_fusion.5), channel_id=1, source_target_pairs={{0,1},{1,3},{3,5},{5,7},{7,6},{6,4},{4,2},{2,0},{8,9},{9,11},{11,1... | collective-permute-start | bytes 614408 | tf_op jit(solution)/shard_map/ppermute | solution.py:99
  61.0 1.5 %collective-permute-done.31 = f32[40,1280]{1,0:T(8,128)S(1)} collective-permute-done((f32[40,1280]{1,0:T(8,128)S(1)}, f32[40,1280]{1,0:T(8,128)S(1)}, u32[]{:S(2)}, u32[]{:S(2)}) %collective-permute-start.31) | collective-permute-done | bytes 204832 | tf_op jit(solution)/shard_map/ppermute | solution.py:99
  63.0 0.8 collective-permute-done.24
  63.8 1.6 %collective-permute-start.25 = (f32[40,1280]{1,0:T(8,128)S(1)}, f32[40,1280]{1,0:T(8,128)S(1)}, u32[]{:S(2)}, u32[]{:S(2)}) collective-permute-start(f32[40,1280]{1,0:T(8,128)S(1)} %add.583), channel_id=1, source_target_pairs={{0,1},{1,3},{3,5},{5,7},{7,6},{6,4},{4,2},{2,0},{8,9},{9,11},{11,1... | collective-permute-start | bytes 614408 | tf_op jit(solution)/shard_map/ppermute | solution.py:99
  65.4 1.4 %collective-permute-done.17 = f32[40,1280]{1,0:T(8,128)S(1)} collective-permute-done((f32[40,1280]{1,0:T(8,128)S(1)}, f32[40,1280]{1,0:T(8,128)S(1)}, u32[]{:S(2)}, u32[]{:S(2)}) %collective-permute-start.17) | collective-permute-done | bytes 204832 | tf_op jit(solution)/shard_map/ppermute | solution.py:99
  66.9 0.5 collective-permute-start.18
  67.4 0.8 collective-permute-done.9
  68.2 1.6 %collective-permute-start.10 = (f32[40,1280]{1,0:T(8,128)S(1)}, f32[40,1280]{1,0:T(8,128)S(1)}, u32[]{:S(2)}, u32[]{:S(2)}) collective-permute-start(f32[40,1280]{1,0:T(8,128)S(1)} %add.521), channel_id=1, source_target_pairs={{0,1},{1,3},{3,5},{5,7},{7,6},{6,4},{4,2},{2,0},{8,9},{9,11},{11,1... | collective-permute-start | bytes 614408 | tf_op jit(solution)/shard_map/ppermute | solution.py:99
  69.9 1.3 %collective-permute-done.32 = f32[40,1280]{1,0:T(8,128)S(1)} collective-permute-done((f32[40,1280]{1,0:T(8,128)S(1)}, f32[40,1280]{1,0:T(8,128)S(1)}, u32[]{:S(2)}, u32[]{:S(2)}) %collective-permute-start.32) | collective-permute-done | bytes 204832 | tf_op jit(solution)/shard_map/ppermute | solution.py:99
  71.8 0.8 collective-permute-done.25
  72.6 1.6 %collective-permute-start.26 = (f32[40,1280]{1,0:T(8,128)S(1)}, f32[40,1280]{1,0:T(8,128)S(1)}, u32[]{:S(2)}, u32[]{:S(2)}) collective-permute-start(f32[40,1280]{1,0:T(8,128)S(1)} %add.586), channel_id=1, source_target_pairs={{0,1},{1,3},{3,5},{5,7},{7,6},{6,4},{4,2},{2,0},{8,9},{9,11},{11,1... | collective-permute-start | bytes 614408 | tf_op jit(solution)/shard_map/ppermute | solution.py:99
  74.2 1.4 %collective-permute-done.18 = f32[40,1280]{1,0:T(8,128)S(1)} collective-permute-done((f32[40,1280]{1,0:T(8,128)S(1)}, f32[40,1280]{1,0:T(8,128)S(1)}, u32[]{:S(2)}, u32[]{:S(2)}) %collective-permute-start.18) | collective-permute-done | bytes 204832 | tf_op jit(solution)/shard_map/ppermute | solution.py:99
  76.2 0.8 collective-permute-done.10
  77.0 1.6 %collective-permute-start.11 = (f32[40,1280]{1,0:T(8,128)S(1)}, f32[40,1280]{1,0:T(8,128)S(1)}, u32[]{:S(2)}, u32[]{:S(2)}) collective-permute-start(f32[40,1280]{1,0:T(8,128)S(1)} %add.524), channel_id=1, source_target_pairs={{0,1},{1,3},{3,5},{5,7},{7,6},{6,4},{4,2},{2,0},{8,9},{9,11},{11,1... | collective-permute-start | bytes 614408 | tf_op jit(solution)/shard_map/ppermute | solution.py:99
  78.7 1.3 %collective-permute-done.33 = f32[40,1280]{1,0:T(8,128)S(1)} collective-permute-done((f32[40,1280]{1,0:T(8,128)S(1)}, f32[40,1280]{1,0:T(8,128)S(1)}, u32[]{:S(2)}, u32[]{:S(2)}) %collective-permute-start.33) | collective-permute-done | bytes 204832 | tf_op jit(solution)/shard_map/ppermute | solution.py:99
  80.6 0.8 collective-permute-done.26
  81.3 1.6 %collective-permute-start.27 = (f32[40,1280]{1,0:T(8,128)S(1)}, f32[40,1280]{1,0:T(8,128)S(1)}, u32[]{:S(2)}, u32[]{:S(2)}) collective-permute-start(f32[40,1280]{1,0:T(8,128)S(1)} %add.589), channel_id=1, source_target_pairs={{0,1},{1,3},{3,5},{5,7},{7,6},{6,4},{4,2},{2,0},{8,9},{9,11},{11,1... | collective-permute-start | bytes 614408 | tf_op jit(solution)/shard_map/ppermute | solution.py:99
  83.0 1.5 %collective-permute-done.19 = f32[40,1280]{1,0:T(8,128)S(1)} collective-permute-done((f32[40,1280]{1,0:T(8,128)S(1)}, f32[40,1280]{1,0:T(8,128)S(1)}, u32[]{:S(2)}, u32[]{:S(2)}) %collective-permute-start.19) | collective-permute-done | bytes 204832 | tf_op jit(solution)/shard_map/ppermute | solution.py:99
  85.0 0.7 collective-permute-done.11
  85.7 1.6 %collective-permute-start.12 = (f32[40,1280]{1,0:T(8,128)S(1)}, f32[40,1280]{1,0:T(8,128)S(1)}, u32[]{:S(2)}, u32[]{:S(2)}) collective-permute-start(f32[40,1280]{1,0:T(8,128)S(1)} %add.527), channel_id=1, source_target_pairs={{0,1},{1,3},{3,5},{5,7},{7,6},{6,4},{4,2},{2,0},{8,9},{9,11},{11,1... | collective-permute-start | bytes 614408 | tf_op jit(solution)/shard_map/ppermute | solution.py:99
  87.5 1.3 %collective-permute-done.34 = f32[40,1280]{1,0:T(8,128)S(1)} collective-permute-done((f32[40,1280]{1,0:T(8,128)S(1)}, f32[40,1280]{1,0:T(8,128)S(1)}, u32[]{:S(2)}, u32[]{:S(2)}) %collective-permute-start.34) | collective-permute-done | bytes 204832 | tf_op jit(solution)/shard_map/ppermute | solution.py:99
  89.3 0.8 collective-permute-done.27
  90.1 1.6 %collective-permute-start.28 = (f32[40,1280]{1,0:T(8,128)S(1)}, f32[40,1280]{1,0:T(8,128)S(1)}, u32[]{:S(2)}, u32[]{:S(2)}) collective-permute-start(f32[40,1280]{1,0:T(8,128)S(1)} %add.592), channel_id=1, source_target_pairs={{0,1},{1,3},{3,5},{5,7},{7,6},{6,4},{4,2},{2,0},{8,9},{9,11},{11,1... | collective-permute-start | bytes 614408 | tf_op jit(solution)/shard_map/ppermute | solution.py:99
  91.7 1.4 %collective-permute-done.20 = f32[40,1280]{1,0:T(8,128)S(1)} collective-permute-done((f32[40,1280]{1,0:T(8,128)S(1)}, f32[40,1280]{1,0:T(8,128)S(1)}, u32[]{:S(2)}, u32[]{:S(2)}) %collective-permute-start.20) | collective-permute-done | bytes 204832 | tf_op jit(solution)/shard_map/ppermute | solution.py:99
  93.7 0.8 collective-permute-done.12
  94.5 1.6 %collective-permute-start.13 = (f32[40,1280]{1,0:T(8,128)S(1)}, f32[40,1280]{1,0:T(8,128)S(1)}, u32[]{:S(2)}, u32[]{:S(2)}) collective-permute-start(f32[40,1280]{1,0:T(8,128)S(1)} %add.530), channel_id=1, source_target_pairs={{0,1},{1,3},{3,5},{5,7},{7,6},{6,4},{4,2},{2,0},{8,9},{9,11},{11,1... | collective-permute-start | bytes 614408 | tf_op jit(solution)/shard_map/ppermute | solution.py:99
  96.2 1.3 %collective-permute-done.35 = f32[40,1280]{1,0:T(8,128)S(1)} collective-permute-done((f32[40,1280]{1,0:T(8,128)S(1)}, f32[40,1280]{1,0:T(8,128)S(1)}, u32[]{:S(2)}, u32[]{:S(2)}) %collective-permute-start.35) | collective-permute-done | bytes 204832 | tf_op jit(solution)/shard_map/ppermute | solution.py:99
  98.1 0.8 collective-permute-done.28
  98.9 1.6 %collective-permute-start.29 = (f32[40,1280]{1,0:T(8,128)S(1)}, f32[40,1280]{1,0:T(8,128)S(1)}, u32[]{:S(2)}, u32[]{:S(2)}) collective-permute-start(f32[40,1280]{1,0:T(8,128)S(1)} %add.595), channel_id=1, source_target_pairs={{0,1},{1,3},{3,5},{5,7},{7,6},{6,4},{4,2},{2,0},{8,9},{9,11},{11,1... | collective-permute-start | bytes 614408 | tf_op jit(solution)/shard_map/ppermute | solution.py:99
  100.5 1.4 %collective-permute-done.21 = f32[40,1280]{1,0:T(8,128)S(1)} collective-permute-done((f32[40,1280]{1,0:T(8,128)S(1)}, f32[40,1280]{1,0:T(8,128)S(1)}, u32[]{:S(2)}, u32[]{:S(2)}) %collective-permute-start.21) | collective-permute-done | bytes 204832 | tf_op jit(solution)/shard_map/ppermute | solution.py:99
  102.5 0.8 collective-permute-done.13
  103.3 1.6 %collective-permute-start.14 = (f32[40,1280]{1,0:T(8,128)S(1)}, f32[40,1280]{1,0:T(8,128)S(1)}, u32[]{:S(2)}, u32[]{:S(2)}) collective-permute-start(f32[40,1280]{1,0:T(8,128)S(1)} %add.533), channel_id=1, source_target_pairs={{0,1},{1,3},{3,5},{5,7},{7,6},{6,4},{4,2},{2,0},{8,9},{9,11},{11,1... | collective-permute-start | bytes 614408 | tf_op jit(solution)/shard_map/ppermute | solution.py:99
  105.0 1.3 %collective-permute-done.36 = f32[40,1280]{1,0:T(8,128)S(1)} collective-permute-done((f32[40,1280]{1,0:T(8,128)S(1)}, f32[40,1280]{1,0:T(8,128)S(1)}, u32[]{:S(2)}, u32[]{:S(2)}) %collective-permute-start.36) | collective-permute-done | bytes 204832 | tf_op jit(solution)/shard_map/ppermute | solution.py:99
  106.4 1.3 %collective-permute-done.29 = f32[40,1280]{1,0:T(8,128)S(1)} collective-permute-done((f32[40,1280]{1,0:T(8,128)S(1)}, f32[40,1280]{1,0:T(8,128)S(1)}, u32[]{:S(2)}, u32[]{:S(2)}) %collective-permute-start.29) | collective-permute-done | bytes 204832 | tf_op jit(solution)/shard_map/ppermute | solution.py:99
  107.7 1.2 %collective-permute-done.22 = f32[40,1280]{1,0:T(8,128)S(1)} collective-permute-done((f32[40,1280]{1,0:T(8,128)S(1)}, f32[40,1280]{1,0:T(8,128)S(1)}, u32[]{:S(2)}, u32[]{:S(2)}) %collective-permute-start.22) | collective-permute-done | bytes 204832 | tf_op jit(solution)/shard_map/ppermute | solution.py:99
  108.9 1.2 %collective-permute-done.14 = f32[40,1280]{1,0:T(8,128)S(1)} collective-permute-done((f32[40,1280]{1,0:T(8,128)S(1)}, f32[40,1280]{1,0:T(8,128)S(1)}, u32[]{:S(2)}, u32[]{:S(2)}) %collective-permute-start.14) | collective-permute-done | bytes 204832 | tf_op jit(solution)/shard_map/ppermute | solution.py:99
  110.2 2.0 %add_divide_fusion = (f32[160,1280]{1,0:T(8,128)}, f32[160,1280]{1,0:T(8,128)}, f32[160,1280]{1,0:T(8,128)}, f32[160,1280]{1,0:T(8,128)}) fusion(f32[160,1280]{1,0:T(8,128)S(1)} %copy-done.2, f32[160,1280]{1,0:T(8,128)S(1)} %copy-done.3, f32[160,1280]{1,0:T(8,128)S(1)} %copy-done.4, f32[40,1280]{1,0:T(8,128)S(1)} %add.621, f32[40,1280]{1,0:T(8,128)S(1)} %add.598, ...), kind=kLoop, calls=%fused_computation.16 | loop fusion | flops 3481600 | bytes 6553600 | tf_op jit(solution)/shard_map/div | solution.py:214
  (89 shorter events, 7.9 us)
Async XLA Ops:
  0.6 7.3 %copy-start = (bf16[1280,1280]{1,0:T(8,128)(2,1)S(1)}, bf16[1280,1280]{1,0:T(8,128)(2,1)}, u32[]{:S(2)}) copy-start(bf16[1280,1280]{1,0:T(8,128)(2,1)} %param.8) | copy-start | bytes 9830404
  4.9 20.4 %collective-permute-start = (bf16[128,2560]{1,0:T(8,128)(2,1)}, bf16[128,2560]{1,0:T(8,128)(2,1)}, u32[]{:S(2)}, u32[]{:S(2)}) collective-permute-start(bf16[128,2560]{1,0:T(8,128)(2,1)} %get-tuple-element.76), channel_id=1, source_target_pairs={{0,8},{8,0},{16,24},{24,16},{1,9},{9,1},{17,25},{25,17},{2,10},{10... | collective-permute-start | bytes 1966088 | tf_op jit(solution)/shard_map/ppermute | solution.py:126
  5.4 18.2 %collective-permute-start.1 = (bf16[128,2560]{1,0:T(8,128)(2,1)}, bf16[128,2560]{1,0:T(8,128)(2,1)}, u32[]{:S(2)}, u32[]{:S(2)}) collective-permute-start(bf16[128,2560]{1,0:T(8,128)(2,1)} %get-tuple-element.75), channel_id=1, source_target_pairs={{0,16},{8,24},{16,0},{24,8},{1,17},{9,25},{17,1},{25,9},{2,18},{10... | collective-permute-start | bytes 1966088 | tf_op jit(solution)/shard_map/ppermute | solution.py:123
  10.1 13.4 %copy-start.5 = (bf16[128,1280]{1,0:T(8,128)(2,1)S(1)}, bf16[128,1280]{1,0:T(8,128)(2,1)}, u32[]{:S(2)}) copy-start(bf16[128,1280]{1,0:T(8,128)(2,1)} %get-tuple-element.35) | copy-start | bytes 983044
  23.6 9.5 %collective-permute-start.2 = (bf16[128,1280]{1,0:T(8,128)(2,1)S(1)}, bf16[128,1280]{1,0:T(8,128)(2,1)S(1)}, u32[]{:S(2)}, u32[]{:S(2)}) collective-permute-start(bf16[128,1280]{1,0:T(8,128)(2,1)S(1)} %copy-done.5), channel_id=1, source_target_pairs={{0,16},{8,24},{16,0},{24,8},{1,17},{9,25},{17,1},{25,9},{2,18},{10... | collective-permute-start | bytes 983048 | tf_op jit(solution)/shard_map/ppermute | solution.py:128
  25.3 9.8 %collective-permute-start.3 = (bf16[128,2560]{1,0:T(8,128)(2,1)}, bf16[128,2560]{1,0:T(8,128)(2,1)S(1)}, u32[]{:S(2)}, u32[]{:S(2)}) collective-permute-start(bf16[128,2560]{1,0:T(8,128)(2,1)} %collective-permute-done.1), channel_id=1, source_target_pairs={{0,8},{8,0},{16,24},{24,16},{1,9},{9,1},{17,25},{25,17},{2,10},{10... | collective-permute-start | bytes 1966088 | tf_op jit(solution)/shard_map/ppermute | solution.py:129
  37.6 6.4 %collective-permute-start.4 = (f32[1]{0:T(128)}, f32[1]{0:T(128)}, u32[]{:S(2)}, u32[]{:S(2)}) collective-permute-start(f32[1]{0:T(128)} %bitcast.5), channel_id=1, source_target_pairs={{0,8},{8,0},{16,24},{24,16},{1,9},{9,1},{17,25},{25,17},{2,10},{10... | collective-permute-start | bytes 20 | tf_op jit(solution)/shard_map/ppermute | solution.py:142
  37.6 8.2 %collective-permute-start.5 = (f32[1]{0:T(128)}, f32[1]{0:T(128)}, u32[]{:S(2)}, u32[]{:S(2)}) collective-permute-start(f32[1]{0:T(128)} %bitcast.5), channel_id=1, source_target_pairs={{0,16},{8,24},{16,0},{24,8},{1,17},{9,25},{17,1},{25,9},{2,18},{10... | collective-permute-start | bytes 20 | tf_op jit(solution)/shard_map/ppermute | solution.py:142
  39.2 7.1 %collective-permute-start.6 = (f32[1]{0:T(128)}, f32[1]{0:T(128)}, u32[]{:S(2)}, u32[]{:S(2)}) collective-permute-start(f32[1]{0:T(128)} %bitcast.5), channel_id=1, source_target_pairs={{0,24},{8,16},{16,8},{24,0},{1,25},{9,17},{17,9},{25,1},{2,26},{10... | collective-permute-start | bytes 20 | tf_op jit(solution)/shard_map/ppermute | solution.py:142
  39.6 14.6 %collective-permute-start.30 = (f32[40,1280]{1,0:T(8,128)S(1)}, f32[40,1280]{1,0:T(8,128)S(1)}, u32[]{:S(2)}, u32[]{:S(2)}) collective-permute-start(f32[40,1280]{1,0:T(8,128)S(1)} %get-tuple-element.69), channel_id=1, source_target_pairs={{0,2},{1,0},{3,1},{5,3},{7,5},{6,7},{4,6},{2,4},{8,10},{9,8},{11,9... | collective-permute-start | bytes 614408 | tf_op jit(solution)/shard_map/ppermute | solution.py:99
  41.2 16.3 %collective-permute-start.15 = (f32[40,1280]{1,0:T(8,128)S(1)}, f32[40,1280]{1,0:T(8,128)S(1)}, u32[]{:S(2)}, u32[]{:S(2)}) collective-permute-start(f32[40,1280]{1,0:T(8,128)S(1)} %get-tuple-element.71), channel_id=1, source_target_pairs={{0,2},{1,0},{3,1},{5,3},{7,5},{6,7},{4,6},{2,4},{8,10},{9,8},{11,9... | collective-permute-start | bytes 614408 | tf_op jit(solution)/shard_map/ppermute | solution.py:99
  44.0 34.6 %copy-start.1 = (bf16[512,1280]{1,0:T(8,128)(2,1)}, bf16[512,1280]{1,0:T(8,128)(2,1)S(1)}, u32[]{:S(2)}) copy-start(bf16[512,1280]{1,0:T(8,128)(2,1)S(1)} %fusion.1) | copy-start | bytes 3932164
  44.0 11.5 %collective-permute-start.23 = (f32[40,1280]{1,0:T(8,128)S(1)}, f32[40,1280]{1,0:T(8,128)S(1)}, u32[]{:S(2)}, u32[]{:S(2)}) collective-permute-start(f32[40,1280]{1,0:T(8,128)S(1)} %get-tuple-element.70), channel_id=1, source_target_pairs={{0,1},{1,3},{3,5},{5,7},{7,6},{6,4},{4,2},{2,0},{8,9},{9,11},{11,1... | collective-permute-start | bytes 614408 | tf_op jit(solution)/shard_map/ppermute | solution.py:99
  45.8 13.0 %collective-permute-start.7 = (f32[40,1280]{1,0:T(8,128)S(1)}, f32[40,1280]{1,0:T(8,128)S(1)}, u32[]{:S(2)}, u32[]{:S(2)}) collective-permute-start(f32[40,1280]{1,0:T(8,128)S(1)} %get-tuple-element.68), channel_id=1, source_target_pairs={{0,1},{1,3},{3,5},{5,7},{7,6},{6,4},{4,2},{2,0},{8,9},{9,11},{11,1... | collective-permute-start | bytes 614408 | tf_op jit(solution)/shard_map/ppermute | solution.py:99
  47.6 3.7 %collective-permute-start.16 = (f32[]{:T(128)}, f32[]{:T(128)}, u32[]{:S(2)}, u32[]{:S(2)}) collective-permute-start(f32[]{:T(128)} %bitcast.6), channel_id=1, source_target_pairs={{0,2},{1,0},{3,1},{5,3},{7,5},{6,7},{4,6},{2,4},{8,10},{9,8},{11,9... | collective-permute-start | bytes 20 | tf_op jit(solution)/shard_map/ppermute | solution.py:74
  51.3 4.2 %collective-permute-start.8 = (f32[]{:T(128)}, f32[]{:T(128)}, u32[]{:S(2)}, u32[]{:S(2)}) collective-permute-start(f32[]{:T(128)} %bitcast.6), channel_id=1, source_target_pairs={{0,1},{1,3},{3,5},{5,7},{7,6},{6,4},{4,2},{2,0},{8,9},{9,11},{11,1... | collective-permute-start | bytes 20 | tf_op jit(solution)/shard_map/ppermute | solution.py:73
  54.8 7.6 %collective-permute-start.31 = (f32[40,1280]{1,0:T(8,128)S(1)}, f32[40,1280]{1,0:T(8,128)S(1)}, u32[]{:S(2)}, u32[]{:S(2)}) collective-permute-start(f32[40,1280]{1,0:T(8,128)S(1)} %multiply_add_fusion.2), channel_id=1, source_target_pairs={{0,2},{1,0},{3,1},{5,3},{7,5},{6,7},{4,6},{2,4},{8,10},{9,8},{11,9... | collective-permute-start | bytes 614408 | tf_op jit(solution)/shard_map/ppermute | solution.py:99
  56.1 7.7 %collective-permute-start.24 = (f32[40,1280]{1,0:T(8,128)S(1)}, f32[40,1280]{1,0:T(8,128)S(1)}, u32[]{:S(2)}, u32[]{:S(2)}) collective-permute-start(f32[40,1280]{1,0:T(8,128)S(1)} %multiply_add_fusion.3), channel_id=1, source_target_pairs={{0,1},{1,3},{3,5},{5,7},{7,6},{6,4},{4,2},{2,0},{8,9},{9,11},{11,1... | collective-permute-start | bytes 614408 | tf_op jit(solution)/shard_map/ppermute | solution.py:99
  58.2 8.7 %collective-permute-start.17 = (f32[40,1280]{1,0:T(8,128)S(1)}, f32[40,1280]{1,0:T(8,128)S(1)}, u32[]{:S(2)}, u32[]{:S(2)}) collective-permute-start(f32[40,1280]{1,0:T(8,128)S(1)} %multiply_add_fusion.4), channel_id=1, source_target_pairs={{0,2},{1,0},{3,1},{5,3},{7,5},{6,7},{4,6},{2,4},{8,10},{9,8},{11,9... | collective-permute-start | bytes 614408 | tf_op jit(solution)/shard_map/ppermute | solution.py:99
  59.5 8.7 %collective-permute-start.9 = (f32[40,1280]{1,0:T(8,128)S(1)}, f32[40,1280]{1,0:T(8,128)S(1)}, u32[]{:S(2)}, u32[]{:S(2)}) collective-permute-start(f32[40,1280]{1,0:T(8,128)S(1)} %multiply_add_fusion.5), channel_id=1, source_target_pairs={{0,1},{1,3},{3,5},{5,7},{7,6},{6,4},{4,2},{2,0},{8,9},{9,11},{11,1... | collective-permute-start | bytes 614408 | tf_op jit(solution)/shard_map/ppermute | solution.py:99
  62.5 8.7 %collective-permute-start.32 = (f32[40,1280]{1,0:T(8,128)S(1)}, f32[40,1280]{1,0:T(8,128)S(1)}, u32[]{:S(2)}, u32[]{:S(2)}) collective-permute-start(f32[40,1280]{1,0:T(8,128)S(1)} %add.606), channel_id=1, source_target_pairs={{0,2},{1,0},{3,1},{5,3},{7,5},{6,7},{4,6},{2,4},{8,10},{9,8},{11,9... | collective-permute-start | bytes 614408 | tf_op jit(solution)/shard_map/ppermute | solution.py:99
  63.8 8.7 %collective-permute-start.25 = (f32[40,1280]{1,0:T(8,128)S(1)}, f32[40,1280]{1,0:T(8,128)S(1)}, u32[]{:S(2)}, u32[]{:S(2)}) collective-permute-start(f32[40,1280]{1,0:T(8,128)S(1)} %add.583), channel_id=1, source_target_pairs={{0,1},{1,3},{3,5},{5,7},{7,6},{6,4},{4,2},{2,0},{8,9},{9,11},{11,1... | collective-permute-start | bytes 614408 | tf_op jit(solution)/shard_map/ppermute | solution.py:99
  66.9 8.7 %collective-permute-start.18 = (f32[40,1280]{1,0:T(8,128)S(1)}, f32[40,1280]{1,0:T(8,128)S(1)}, u32[]{:S(2)}, u32[]{:S(2)}) collective-permute-start(f32[40,1280]{1,0:T(8,128)S(1)} %add.550), channel_id=1, source_target_pairs={{0,2},{1,0},{3,1},{5,3},{7,5},{6,7},{4,6},{2,4},{8,10},{9,8},{11,9... | collective-permute-start | bytes 614408 | tf_op jit(solution)/shard_map/ppermute | solution.py:99
  68.2 8.7 %collective-permute-start.10 = (f32[40,1280]{1,0:T(8,128)S(1)}, f32[40,1280]{1,0:T(8,128)S(1)}, u32[]{:S(2)}, u32[]{:S(2)}) collective-permute-start(f32[40,1280]{1,0:T(8,128)S(1)} %add.521), channel_id=1, source_target_pairs={{0,1},{1,3},{3,5},{5,7},{7,6},{6,4},{4,2},{2,0},{8,9},{9,11},{11,1... | collective-permute-start | bytes 614408 | tf_op jit(solution)/shard_map/ppermute | solution.py:99
  71.3 8.7 %collective-permute-start.33 = (f32[40,1280]{1,0:T(8,128)S(1)}, f32[40,1280]{1,0:T(8,128)S(1)}, u32[]{:S(2)}, u32[]{:S(2)}) collective-permute-start(f32[40,1280]{1,0:T(8,128)S(1)} %add.609), channel_id=1, source_target_pairs={{0,2},{1,0},{3,1},{5,3},{7,5},{6,7},{4,6},{2,4},{8,10},{9,8},{11,9... | collective-permute-start | bytes 614408 | tf_op jit(solution)/shard_map/ppermute | solution.py:99
  72.6 8.7 %collective-permute-start.26 = (f32[40,1280]{1,0:T(8,128)S(1)}, f32[40,1280]{1,0:T(8,128)S(1)}, u32[]{:S(2)}, u32[]{:S(2)}) collective-permute-start(f32[40,1280]{1,0:T(8,128)S(1)} %add.586), channel_id=1, source_target_pairs={{0,1},{1,3},{3,5},{5,7},{7,6},{6,4},{4,2},{2,0},{8,9},{9,11},{11,1... | collective-permute-start | bytes 614408 | tf_op jit(solution)/shard_map/ppermute | solution.py:99
  75.7 8.7 %collective-permute-start.19 = (f32[40,1280]{1,0:T(8,128)S(1)}, f32[40,1280]{1,0:T(8,128)S(1)}, u32[]{:S(2)}, u32[]{:S(2)}) collective-permute-start(f32[40,1280]{1,0:T(8,128)S(1)} %add.555), channel_id=1, source_target_pairs={{0,2},{1,0},{3,1},{5,3},{7,5},{6,7},{4,6},{2,4},{8,10},{9,8},{11,9... | collective-permute-start | bytes 614408 | tf_op jit(solution)/shard_map/ppermute | solution.py:99
  77.0 8.7 %collective-permute-start.11 = (f32[40,1280]{1,0:T(8,128)S(1)}, f32[40,1280]{1,0:T(8,128)S(1)}, u32[]{:S(2)}, u32[]{:S(2)}) collective-permute-start(f32[40,1280]{1,0:T(8,128)S(1)} %add.524), channel_id=1, source_target_pairs={{0,1},{1,3},{3,5},{5,7},{7,6},{6,4},{4,2},{2,0},{8,9},{9,11},{11,1... | collective-permute-start | bytes 614408 | tf_op jit(solution)/shard_map/ppermute | solution.py:99
  80.0 8.8 %collective-permute-start.34 = (f32[40,1280]{1,0:T(8,128)S(1)}, f32[40,1280]{1,0:T(8,128)S(1)}, u32[]{:S(2)}, u32[]{:S(2)}) collective-permute-start(f32[40,1280]{1,0:T(8,128)S(1)} %add.612), channel_id=1, source_target_pairs={{0,2},{1,0},{3,1},{5,3},{7,5},{6,7},{4,6},{2,4},{8,10},{9,8},{11,9... | collective-permute-start | bytes 614408 | tf_op jit(solution)/shard_map/ppermute | solution.py:99
  81.3 8.8 %collective-permute-start.27 = (f32[40,1280]{1,0:T(8,128)S(1)}, f32[40,1280]{1,0:T(8,128)S(1)}, u32[]{:S(2)}, u32[]{:S(2)}) collective-permute-start(f32[40,1280]{1,0:T(8,128)S(1)} %add.589), channel_id=1, source_target_pairs={{0,1},{1,3},{3,5},{5,7},{7,6},{6,4},{4,2},{2,0},{8,9},{9,11},{11,1... | collective-permute-start | bytes 614408 | tf_op jit(solution)/shard_map/ppermute | solution.py:99
  84.4 25.8 %copy-start.2 = (f32[160,1280]{1,0:T(8,128)S(1)}, f32[160,1280]{1,0:T(8,128)}, u32[]{:S(2)}) copy-start(f32[160,1280]{1,0:T(8,128)} %param.11) | copy-start | bytes 2457604
  84.4 25.8 %copy-start.3 = (f32[160,1280]{1,0:T(8,128)S(1)}, f32[160,1280]{1,0:T(8,128)}, u32[]{:S(2)}) copy-start(f32[160,1280]{1,0:T(8,128)} %param.10) | copy-start | bytes 2457604
  84.5 25.8 %copy-start.4 = (f32[160,1280]{1,0:T(8,128)S(1)}, f32[160,1280]{1,0:T(8,128)}, u32[]{:S(2)}) copy-start(f32[160,1280]{1,0:T(8,128)} %param.9) | copy-start | bytes 2457604
  84.5 8.7 %collective-permute-start.20 = (f32[40,1280]{1,0:T(8,128)S(1)}, f32[40,1280]{1,0:T(8,128)S(1)}, u32[]{:S(2)}, u32[]{:S(2)}) collective-permute-start(f32[40,1280]{1,0:T(8,128)S(1)} %add.560), channel_id=1, source_target_pairs={{0,2},{1,0},{3,1},{5,3},{7,5},{6,7},{4,6},{2,4},{8,10},{9,8},{11,9... | collective-permute-start | bytes 614408 | tf_op jit(solution)/shard_map/ppermute | solution.py:99
  85.7 8.7 %collective-permute-start.12 = (f32[40,1280]{1,0:T(8,128)S(1)}, f32[40,1280]{1,0:T(8,128)S(1)}, u32[]{:S(2)}, u32[]{:S(2)}) collective-permute-start(f32[40,1280]{1,0:T(8,128)S(1)} %add.527), channel_id=1, source_target_pairs={{0,1},{1,3},{3,5},{5,7},{7,6},{6,4},{4,2},{2,0},{8,9},{9,11},{11,1... | collective-permute-start | bytes 614408 | tf_op jit(solution)/shard_map/ppermute | solution.py:99
  88.8 8.7 %collective-permute-start.35 = (f32[40,1280]{1,0:T(8,128)S(1)}, f32[40,1280]{1,0:T(8,128)S(1)}, u32[]{:S(2)}, u32[]{:S(2)}) collective-permute-start(f32[40,1280]{1,0:T(8,128)S(1)} %add.615), channel_id=1, source_target_pairs={{0,2},{1,0},{3,1},{5,3},{7,5},{6,7},{4,6},{2,4},{8,10},{9,8},{11,9... | collective-permute-start | bytes 614408 | tf_op jit(solution)/shard_map/ppermute | solution.py:99
  90.1 8.7 %collective-permute-start.28 = (f32[40,1280]{1,0:T(8,128)S(1)}, f32[40,1280]{1,0:T(8,128)S(1)}, u32[]{:S(2)}, u32[]{:S(2)}) collective-permute-start(f32[40,1280]{1,0:T(8,128)S(1)} %add.592), channel_id=1, source_target_pairs={{0,1},{1,3},{3,5},{5,7},{7,6},{6,4},{4,2},{2,0},{8,9},{9,11},{11,1... | collective-permute-start | bytes 614408 | tf_op jit(solution)/shard_map/ppermute | solution.py:99
  93.2 8.7 %collective-permute-start.21 = (f32[40,1280]{1,0:T(8,128)S(1)}, f32[40,1280]{1,0:T(8,128)S(1)}, u32[]{:S(2)}, u32[]{:S(2)}) collective-permute-start(f32[40,1280]{1,0:T(8,128)S(1)} %add.565), channel_id=1, source_target_pairs={{0,2},{1,0},{3,1},{5,3},{7,5},{6,7},{4,6},{2,4},{8,10},{9,8},{11,9... | collective-permute-start | bytes 614408 | tf_op jit(solution)/shard_map/ppermute | solution.py:99
  94.5 8.7 %collective-permute-start.13 = (f32[40,1280]{1,0:T(8,128)S(1)}, f32[40,1280]{1,0:T(8,128)S(1)}, u32[]{:S(2)}, u32[]{:S(2)}) collective-permute-start(f32[40,1280]{1,0:T(8,128)S(1)} %add.530), channel_id=1, source_target_pairs={{0,1},{1,3},{3,5},{5,7},{7,6},{6,4},{4,2},{2,0},{8,9},{9,11},{11,1... | collective-permute-start | bytes 614408 | tf_op jit(solution)/shard_map/ppermute | solution.py:99
  97.6 8.7 %collective-permute-start.36 = (f32[40,1280]{1,0:T(8,128)S(1)}, f32[40,1280]{1,0:T(8,128)S(1)}, u32[]{:S(2)}, u32[]{:S(2)}) collective-permute-start(f32[40,1280]{1,0:T(8,128)S(1)} %add.618), channel_id=1, source_target_pairs={{0,2},{1,0},{3,1},{5,3},{7,5},{6,7},{4,6},{2,4},{8,10},{9,8},{11,9... | collective-permute-start | bytes 614408 | tf_op jit(solution)/shard_map/ppermute | solution.py:99
  98.9 8.7 %collective-permute-start.29 = (f32[40,1280]{1,0:T(8,128)S(1)}, f32[40,1280]{1,0:T(8,128)S(1)}, u32[]{:S(2)}, u32[]{:S(2)}) collective-permute-start(f32[40,1280]{1,0:T(8,128)S(1)} %add.595), channel_id=1, source_target_pairs={{0,1},{1,3},{3,5},{5,7},{7,6},{6,4},{4,2},{2,0},{8,9},{9,11},{11,1... | collective-permute-start | bytes 614408 | tf_op jit(solution)/shard_map/ppermute | solution.py:99
  102.0 6.9 %collective-permute-start.22 = (f32[40,1280]{1,0:T(8,128)S(1)}, f32[40,1280]{1,0:T(8,128)S(1)}, u32[]{:S(2)}, u32[]{:S(2)}) collective-permute-start(f32[40,1280]{1,0:T(8,128)S(1)} %add.570), channel_id=1, source_target_pairs={{0,2},{1,0},{3,1},{5,3},{7,5},{6,7},{4,6},{2,4},{8,10},{9,8},{11,9... | collective-permute-start | bytes 614408 | tf_op jit(solution)/shard_map/ppermute | solution.py:99
  103.3 6.9 %collective-permute-start.14 = (f32[40,1280]{1,0:T(8,128)S(1)}, f32[40,1280]{1,0:T(8,128)S(1)}, u32[]{:S(2)}, u32[]{:S(2)}) collective-permute-start(f32[40,1280]{1,0:T(8,128)S(1)} %add.533), channel_id=1, source_target_pairs={{0,1},{1,3},{3,5},{5,7},{7,6},{6,4},{4,2},{2,0},{8,9},{9,11},{11,1... | collective-permute-start | bytes 614408 | tf_op jit(solution)/shard_map/ppermute | solution.py:99

commit v8 on v6

--- a/solution.py
+++ b/solution.py
@@ -93,25 +93,25 @@
     a = lax.axis_index("aug")
     rows = h_rows.shape[0]
     sw = h_rows.shape[1] // 4
-    d = grad_rows.shape[1]
 
     def cols(b):
         return lax.dynamic_slice_in_dim(h_rows, b * sw, sw, axis=1)
 
     over_x = [(i, i ^ 2) for i in range(4)]
     over_core = [(i, i ^ 1) for i in range(4)]
-    far_first = lax.ppermute(
-        jnp.concatenate([cols(a ^ 3), grad_rows], axis=1), "aug", over_x
-    )
-    near = lax.ppermute(jnp.concatenate([cols(a ^ 1), grad_rows], axis=1), "aug", over_core)
-    _, second = lax.optimization_barrier((far_first, cols(a ^ 2)))
-    far_second = lax.ppermute(second, "aug", over_x)
-    relay = lax.ppermute(far_first, "aug", over_core)
+    g_far = lax.ppermute(grad_rows, "aug", over_x)
+    g_near = lax.ppermute(grad_rows, "aug", over_core)
+    h_far_relay = lax.ppermute(cols(a ^ 3), "aug", over_x)
+    h_near = lax.ppermute(cols(a ^ 1), "aug", over_core)
+    g_relay = lax.ppermute(g_far, "aug", over_core)
+    h_relay = lax.ppermute(h_far_relay, "aug", over_core)
+    _, second = lax.optimization_barrier((h_far_relay, cols(a ^ 2)))
+    h_far = lax.ppermute(second, "aug", over_x)
     return [
         (a * rows, cols(a), grad_rows),
-        ((a ^ 1) * rows, near[:, :sw], near[:, sw:]),
-        ((a ^ 2) * rows, far_second, far_first[:, sw:]),
-        ((a ^ 3) * rows, relay[:, :sw], relay[:, sw:]),
+        ((a ^ 1) * rows, h_near, g_near),
+        ((a ^ 2) * rows, h_far, g_far),
+        ((a ^ 3) * rows, h_relay, g_relay),
     ]
 
 

time: 113 us -> 110 us (0.973)
  waiting for transfers between devices: 47.2 us -> 40.1 us
  matrix products: 16.5 us -> 21.2 us
  other arithmetic: 5.55 us -> 3.38 us
  starting transfers between devices: 36.2 us -> 37.5 us
    ppermute x4 -> x7, waiting for transfers between devices: 12.6 us -> 5.71 us  [the longest x1 5.7 us: exchange_four(): h_far_relay = lax.ppermute(cols(a ^ 3), 'aug', over_x)]
    dot_general x4, matrix products: 8.8 us -> 13.5 us  [per_device(): term = jnp.dot(h_piece.T, g_piece, preferred_element_type=jnp.float32)]
    concatenate x1 -> x0, other arithmetic: 2.11 us -> none  [exchange_four(): jnp.concatenate([cols(a ^ 3), grad_rows], axis=1)]
    ppermute x4 -> x7, starting transfers between devices: 4.69 us -> 6.01 us  [the longest x1 2.57 us: exchange_four(): g_far = lax.ppermute(grad_rows, 'aug', over_x)]
  transfers between devices with their start and end apart: 35 -> 38, of which waited for: 19 -> 17; matrix products, arithmetic and copies ran while one was open for 14% -> 20% of each run, Pallas kernels for 0% -> 0%
where the time goes in v8:
time: 110 us; the launch traced here: 109 us
  waiting for transfers between devices  40.1 us (36%)
  starting transfers between devices  37.5 us (34%)
  matrix products  21.2 us (19%)
  between operations  4.82 us (4%)
  other arithmetic  3.38 us (3%)
  local copies, waits for them, and re-layouts  2.26 us (2%)
    ppermute x28, waiting for transfers between devices, ring_reduce_scatter(): lax.ppermute(v, 'dp', right if step < 0 else left)  34.4 us
    ppermute x28, starting transfers between devices, ring_reduce_scatter(): lax.ppermute(v, 'dp', right if step < 0 else left)  29.7 us
    dot_general x4, matrix products, per_device(): term = jnp.dot(h_piece.T, g_piece, preferred_element_type=jnp.float32)  13.5 us
    dot_general x4, matrix products, project_back(): lax.dot_general(rows, down_weight, (((1,), (1,)), ((), ())), preferred_el...  7.72 us
    ppermute x1, waiting for transfers between devices, exchange_four(): h_far_relay = lax.ppermute(cols(a ^ 3), 'aug', over_x)  5.7 us
    ppermute x1, starting transfers between devices, exchange_four(): g_far = lax.ppermute(grad_rows, 'aug', over_x)  2.57 us
  transfers between devices with their start and end apart: 38, of which 17 were waited for; matrix products, arithmetic and copies ran while one was open for 20% of the time, Pallas kernels for 0%

profile of v8, /device:TPU:0, one launch (start us, length us, event | category | flops | bytes accessed | tf_op | source)
XLA Modules:
  0.0 109.3 jit_solution(8547187543471511012)
XLA Ops:
  0.6 0.5 collective-permute-start.1
  1.2 2.6 %collective-permute-start.4 = (bf16[128,1280]{1,0:T(8,128)(2,1)}, bf16[128,1280]{1,0:T(8,128)(2,1)}, u32[]{:S(2)}, u32[]{:S(2)}) collective-permute-start(bf16[128,1280]{1,0:T(8,128)(2,1)} %bitcast.116), channel_id=1, source_target_pairs={{0,16},{8,24},{16,0},{24,8},{1,17},{9,25},{17,1},{25,9},{2,18},{10... | collective-permute-start | bytes 983048 | tf_op jit(solution)/shard_map/ppermute | solution.py:102
  3.7 2.1 %dynamic-slice_bitcast_fusion = (bf16[128,1280]{1,0:T(8,128)(2,1)}, bf16[128,1280]{1,0:T(8,128)(2,1)}, bf16[128,1280]{1,0:T(8,128)(2,1)}) fusion(bf16[1,1,128,5120]{3,2,1,0:T(8,128)(2,1)} %param.6, s32[]{:T(128)S(6)} %select_n.691, s32[]{:T(128)S(6)} %select_n.689, s32[]{:T(128)S(6)} %select_n.690), kind=kLoop, calls=%fused_computation.21 | loop fusion | bytes 1966092 | tf_op jit(solution)/shard_map/dynamic_slice | solution.py:98
  5.9 0.2 collective-permute-start
  6.0 0.5 collective-permute-start.2
  6.5 4.9 %fusion.6 = f32[1280,1280]{1,0:T(8,128)} fusion(bf16[1,1,128,5120]{3,2,1,0:T(8,128)(2,1)} %param.6, s32[]{:T(128)S(6)} %select_n.688, bf16[1,1,128,1280]{3,2,1,0:T(8,128)(2,1)} %param.7), kind=kOutput, calls=%fused_computation.19 | convolution fusion | flops 419430400 | bytes 7208964 | tf_op jit(solution)/shard_map/dot_general | solution.py:151
  11.5 2.2 %fusion.4 = bf16[512,1280]{1,0:T(8,128)(2,1)S(1)} fusion(bf16[512,1280]{1,0:T(8,128)(2,1)S(1)} %broadcast_in_dim.2, s32[]{:T(128)S(6)} %select_n.859, bf16[1280,1280]{1,0:T(8,128)(2,1)S(1)} %copy-done, bf16[1,1,128,1280]{3,2,1,0:T(8,128)(2,1)} %param.7), kind=kOutput, calls=%fused_computation.12 | convolution fusion | flops 419594240 | bytes 3932164 | tf_op jit(solution)/shard_map/dot_general | solution.py:17
  13.7 5.7 %collective-permute-done.2 = bf16[128,1280]{1,0:T(8,128)(2,1)} collective-permute-done((bf16[128,1280]{1,0:T(8,128)(2,1)}, bf16[128,1280]{1,0:T(8,128)(2,1)}, u32[]{:S(2)}, u32[]{:S(2)}) %collective-permute-start.2) | collective-permute-done | bytes 327712 | tf_op jit(solution)/shard_map/ppermute | solution.py:104
  19.4 1.8 %collective-permute-start.3 = (bf16[128,1280]{1,0:T(8,128)(2,1)}, bf16[128,1280]{1,0:T(8,128)(2,1)S(1)}, u32[]{:S(2)}, u32[]{:S(2)}) collective-permute-start(bf16[128,1280]{1,0:T(8,128)(2,1)} %get-tuple-element.35), channel_id=1, source_target_pairs={{0,16},{8,24},{16,0},{24,8},{1,17},{9,25},{17,1},{25,9},{2,18},{10... | collective-permute-start | bytes 983048 | tf_op jit(solution)/shard_map/ppermute | solution.py:109
  21.1 0.5 collective-permute-start.6
  21.7 4.1 %convolution_add_fusion.2 = f32[1280,1280]{1,0:T(8,128)S(1)} fusion(f32[1280,1280]{1,0:T(8,128)} %fusion.6, bf16[128,1280]{1,0:T(8,128)(2,1)} %collective-permute-done, bf16[128,1280]{1,0:T(8,128)(2,1)} %collective-permute-done.1), kind=kOutput, calls=%fused_computation.2 | convolution fusion | flops 421068800 | bytes 13762560 | tf_op jit(solution)/shard_map/dot_general | solution.py:151
  25.8 2.2 %fusion.3 = bf16[512,1280]{1,0:T(8,128)(2,1)S(1)} fusion(bf16[512,1280]{1,0:T(8,128)(2,1)S(1)} %fusion.4, s32[]{:T(128)S(6)} %select_n.860, bf16[128,1280]{1,0:T(8,128)(2,1)} %collective-permute-done.1, bf16[1280,1280]{1,0:T(8,128)(2,1)S(1)} %copy-done), kind=kOutput, calls=%fused_computation.10 | convolution fusion | flops 419594240 | bytes 3932164 | tf_op jit(solution)/shard_map/dot_general | solution.py:17
  28.0 2.2 %fusion.2 = bf16[512,1280]{1,0:T(8,128)(2,1)S(1)} fusion(bf16[512,1280]{1,0:T(8,128)(2,1)S(1)} %fusion.3, s32[]{:T(128)S(6)} %select_n.861, bf16[128,1280]{1,0:T(8,128)(2,1)} %collective-permute-done.4, bf16[1280,1280]{1,0:T(8,128)(2,1)S(1)} %copy-done), kind=kOutput, calls=%fused_computation.8 | convolution fusion | flops 419594240 | bytes 3932164 | tf_op jit(solution)/shard_map/dot_general | solution.py:17
  30.2 2.0 %convolution_add_fusion.1 = f32[1280,1280]{1,0:T(8,128)S(1)} fusion(f32[1280,1280]{1,0:T(8,128)S(1)} %convolution_add_fusion.2, bf16[128,1280]{1,0:T(8,128)(2,1)S(1)} %collective-permute-done.3, bf16[128,1280]{1,0:T(8,128)(2,1)} %collective-permute-done.4), kind=kOutput, calls=%fused_computation.1 | convolution fusion | flops 421068800 | bytes 13762560 | tf_op jit(solution)/shard_map/dot_general | solution.py:151
  32.2 2.5 %multiply_reduce_fusion = (f32[]{:T(128)}, f32[1280,1280]{1,0:T(8,128)S(1)}) fusion(f32[1280,1280]{1,0:T(8,128)S(1)} %convolution_add_fusion.1, bf16[128,1280]{1,0:T(8,128)(2,1)S(1)} %collective-permute-done.5, bf16[128,1280]{1,0:T(8,128)(2,1)S(1)} %collective-permute-done.6), kind=kOutput, calls=%fused_computation.4 | convolution fusion | flops 425984000 | bytes 13762564 | tf_op jit(solution)/shard_map/dot_general | solution.py:151
  34.7 0.4 collective-permute-start.8
  35.2 1.4 %collective-permute-start.9 = (f32[1]{0:T(128)}, f32[1]{0:T(128)}, u32[]{:S(2)}, u32[]{:S(2)}) collective-permute-start(f32[1]{0:T(128)} %bitcast.5), channel_id=1, source_target_pairs={{0,24},{8,16},{16,8},{24,0},{1,25},{9,17},{17,9},{25,1},{2,26},{10... | collective-permute-start | bytes 20 | tf_op jit(solution)/shard_map/ppermute | solution.py:122
  36.6 1.2 %fusion.1 = bf16[512,1280]{1,0:T(8,128)(2,1)S(1)} fusion(bf16[512,1280]{1,0:T(8,128)(2,1)S(1)} %fusion.2, s32[]{:T(128)S(6)} %select_n.862, bf16[128,1280]{1,0:T(8,128)(2,1)S(1)} %collective-permute-done.6, bf16[1280,1280]{1,0:T(8,128)(2,1)S(1)} %copy-done), kind=kOutput, calls=%fused_computation.6 | convolution fusion | flops 419594240 | bytes 3932164 | tf_op jit(solution)/shard_map/dot_general | solution.py:17
  40.4 0.1 dynamic-slice_multiply_fusion.3
  40.5 1.6 %collective-permute-start.31 = (f32[40,1280]{1,0:T(8,128)S(1)}, f32[40,1280]{1,0:T(8,128)S(1)}, u32[]{:S(2)}, u32[]{:S(2)}) collective-permute-start(f32[40,1280]{1,0:T(8,128)S(1)} %get-tuple-element.69), channel_id=1, source_target_pairs={{0,2},{1,0},{3,1},{5,3},{7,5},{6,7},{4,6},{2,4},{8,10},{9,8},{11,9... | collective-permute-start | bytes 614408 | tf_op jit(solution)/shard_map/ppermute | solution.py:82
  42.1 0.4 collective-permute-start.24
  42.6 1.6 %collective-permute-start.17 = (f32[40,1280]{1,0:T(8,128)S(1)}, f32[40,1280]{1,0:T(8,128)S(1)}, u32[]{:S(2)}, u32[]{:S(2)}) collective-permute-start(f32[40,1280]{1,0:T(8,128)S(1)} %get-tuple-element.71), channel_id=1, source_target_pairs={{0,2},{1,0},{3,1},{5,3},{7,5},{6,7},{4,6},{2,4},{8,10},{9,8},{11,9... | collective-permute-start | bytes 614408 | tf_op jit(solution)/shard_map/ppermute | solution.py:82
  44.2 0.4 collective-permute-start.10
  44.7 3.7 %collective-permute-done.31 = f32[40,1280]{1,0:T(8,128)S(1)} collective-permute-done((f32[40,1280]{1,0:T(8,128)S(1)}, f32[40,1280]{1,0:T(8,128)S(1)}, u32[]{:S(2)}, u32[]{:S(2)}) %collective-permute-start.31) | collective-permute-done | bytes 204832 | tf_op jit(solution)/shard_map/ppermute | solution.py:82
  48.5 1.6 %collective-permute-start.32 = (f32[40,1280]{1,0:T(8,128)S(1)}, f32[40,1280]{1,0:T(8,128)S(1)}, u32[]{:S(2)}, u32[]{:S(2)}) collective-permute-start(f32[40,1280]{1,0:T(8,128)S(1)} %add.603), channel_id=1, source_target_pairs={{0,2},{1,0},{3,1},{5,3},{7,5},{6,7},{4,6},{2,4},{8,10},{9,8},{11,9... | collective-permute-start | bytes 614408 | tf_op jit(solution)/shard_map/ppermute | solution.py:82
  50.1 0.5 collective-permute-start.25
  50.6 2.2 %collective-permute-done.17 = f32[40,1280]{1,0:T(8,128)S(1)} collective-permute-done((f32[40,1280]{1,0:T(8,128)S(1)}, f32[40,1280]{1,0:T(8,128)S(1)}, u32[]{:S(2)}, u32[]{:S(2)}) %collective-permute-start.17) | collective-permute-done | bytes 204832 | tf_op jit(solution)/shard_map/ppermute | solution.py:82
  52.9 1.6 %collective-permute-start.18 = (f32[40,1280]{1,0:T(8,128)S(1)}, f32[40,1280]{1,0:T(8,128)S(1)}, u32[]{:S(2)}, u32[]{:S(2)}) collective-permute-start(f32[40,1280]{1,0:T(8,128)S(1)} %add.545), channel_id=1, source_target_pairs={{0,2},{1,0},{3,1},{5,3},{7,5},{6,7},{4,6},{2,4},{8,10},{9,8},{11,9... | collective-permute-start | bytes 614408 | tf_op jit(solution)/shard_map/ppermute | solution.py:82
  54.5 0.5 collective-permute-start.11
  55.1 2.1 %collective-permute-done.32 = f32[40,1280]{1,0:T(8,128)S(1)} collective-permute-done((f32[40,1280]{1,0:T(8,128)S(1)}, f32[40,1280]{1,0:T(8,128)S(1)}, u32[]{:S(2)}, u32[]{:S(2)}) %collective-permute-start.32) | collective-permute-done | bytes 204832 | tf_op jit(solution)/shard_map/ppermute | solution.py:82
  57.3 1.6 %collective-permute-start.33 = (f32[40,1280]{1,0:T(8,128)S(1)}, f32[40,1280]{1,0:T(8,128)S(1)}, u32[]{:S(2)}, u32[]{:S(2)}) collective-permute-start(f32[40,1280]{1,0:T(8,128)S(1)} %add.606), channel_id=1, source_target_pairs={{0,2},{1,0},{3,1},{5,3},{7,5},{6,7},{4,6},{2,4},{8,10},{9,8},{11,9... | collective-permute-start | bytes 614408 | tf_op jit(solution)/shard_map/ppermute | solution.py:82
  58.9 0.5 collective-permute-start.26
  59.4 2.2 %collective-permute-done.18 = f32[40,1280]{1,0:T(8,128)S(1)} collective-permute-done((f32[40,1280]{1,0:T(8,128)S(1)}, f32[40,1280]{1,0:T(8,128)S(1)}, u32[]{:S(2)}, u32[]{:S(2)}) %collective-permute-start.18) | collective-permute-done | bytes 204832 | tf_op jit(solution)/shard_map/ppermute | solution.py:82
  61.6 1.6 %collective-permute-start.19 = (f32[40,1280]{1,0:T(8,128)S(1)}, f32[40,1280]{1,0:T(8,128)S(1)}, u32[]{:S(2)}, u32[]{:S(2)}) collective-permute-start(f32[40,1280]{1,0:T(8,128)S(1)} %add.550), channel_id=1, source_target_pairs={{0,2},{1,0},{3,1},{5,3},{7,5},{6,7},{4,6},{2,4},{8,10},{9,8},{11,9... | collective-permute-start | bytes 614408 | tf_op jit(solution)/shard_map/ppermute | solution.py:82
  63.3 0.5 collective-permute-start.12
  63.9 2.1 %collective-permute-done.33 = f32[40,1280]{1,0:T(8,128)S(1)} collective-permute-done((f32[40,1280]{1,0:T(8,128)S(1)}, f32[40,1280]{1,0:T(8,128)S(1)}, u32[]{:S(2)}, u32[]{:S(2)}) %collective-permute-start.33) | collective-permute-done | bytes 204832 | tf_op jit(solution)/shard_map/ppermute | solution.py:82
  66.0 1.6 %collective-permute-start.34 = (f32[40,1280]{1,0:T(8,128)S(1)}, f32[40,1280]{1,0:T(8,128)S(1)}, u32[]{:S(2)}, u32[]{:S(2)}) collective-permute-start(f32[40,1280]{1,0:T(8,128)S(1)} %add.609), channel_id=1, source_target_pairs={{0,2},{1,0},{3,1},{5,3},{7,5},{6,7},{4,6},{2,4},{8,10},{9,8},{11,9... | collective-permute-start | bytes 614408 | tf_op jit(solution)/shard_map/ppermute | solution.py:82
  67.7 0.5 collective-permute-start.27
  68.2 2.2 %collective-permute-done.19 = f32[40,1280]{1,0:T(8,128)S(1)} collective-permute-done((f32[40,1280]{1,0:T(8,128)S(1)}, f32[40,1280]{1,0:T(8,128)S(1)}, u32[]{:S(2)}, u32[]{:S(2)}) %collective-permute-start.19) | collective-permute-done | bytes 204832 | tf_op jit(solution)/shard_map/ppermute | solution.py:82
  70.4 1.6 %collective-permute-start.20 = (f32[40,1280]{1,0:T(8,128)S(1)}, f32[40,1280]{1,0:T(8,128)S(1)}, u32[]{:S(2)}, u32[]{:S(2)}) collective-permute-start(f32[40,1280]{1,0:T(8,128)S(1)} %add.555), channel_id=1, source_target_pairs={{0,2},{1,0},{3,1},{5,3},{7,5},{6,7},{4,6},{2,4},{8,10},{9,8},{11,9... | collective-permute-start | bytes 614408 | tf_op jit(solution)/shard_map/ppermute | solution.py:82
  72.1 0.5 collective-permute-start.13
  72.7 2.1 %collective-permute-done.34 = f32[40,1280]{1,0:T(8,128)S(1)} collective-permute-done((f32[40,1280]{1,0:T(8,128)S(1)}, f32[40,1280]{1,0:T(8,128)S(1)}, u32[]{:S(2)}, u32[]{:S(2)}) %collective-permute-start.34) | collective-permute-done | bytes 204832 | tf_op jit(solution)/shard_map/ppermute | solution.py:82
  74.8 1.6 %collective-permute-start.35 = (f32[40,1280]{1,0:T(8,128)S(1)}, f32[40,1280]{1,0:T(8,128)S(1)}, u32[]{:S(2)}, u32[]{:S(2)}) collective-permute-start(f32[40,1280]{1,0:T(8,128)S(1)} %add.612), channel_id=1, source_target_pairs={{0,2},{1,0},{3,1},{5,3},{7,5},{6,7},{4,6},{2,4},{8,10},{9,8},{11,9... | collective-permute-start | bytes 614408 | tf_op jit(solution)/shard_map/ppermute | solution.py:82
  76.5 0.5 collective-permute-start.28
  77.0 2.2 %collective-permute-done.20 = f32[40,1280]{1,0:T(8,128)S(1)} collective-permute-done((f32[40,1280]{1,0:T(8,128)S(1)}, f32[40,1280]{1,0:T(8,128)S(1)}, u32[]{:S(2)}, u32[]{:S(2)}) %collective-permute-start.20) | collective-permute-done | bytes 204832 | tf_op jit(solution)/shard_map/ppermute | solution.py:82
  79.2 1.6 %collective-permute-start.21 = (f32[40,1280]{1,0:T(8,128)S(1)}, f32[40,1280]{1,0:T(8,128)S(1)}, u32[]{:S(2)}, u32[]{:S(2)}) collective-permute-start(f32[40,1280]{1,0:T(8,128)S(1)} %add.560), channel_id=1, source_target_pairs={{0,2},{1,0},{3,1},{5,3},{7,5},{6,7},{4,6},{2,4},{8,10},{9,8},{11,9... | collective-permute-start | bytes 614408 | tf_op jit(solution)/shard_map/ppermute | solution.py:82
  80.9 0.5 collective-permute-start.14
  81.5 2.0 %collective-permute-done.35 = f32[40,1280]{1,0:T(8,128)S(1)} collective-permute-done((f32[40,1280]{1,0:T(8,128)S(1)}, f32[40,1280]{1,0:T(8,128)S(1)}, u32[]{:S(2)}, u32[]{:S(2)}) %collective-permute-start.35) | collective-permute-done | bytes 204832 | tf_op jit(solution)/shard_map/ppermute | solution.py:82
  83.6 1.6 %collective-permute-start.36 = (f32[40,1280]{1,0:T(8,128)S(1)}, f32[40,1280]{1,0:T(8,128)S(1)}, u32[]{:S(2)}, u32[]{:S(2)}) collective-permute-start(f32[40,1280]{1,0:T(8,128)S(1)} %add.615), channel_id=1, source_target_pairs={{0,2},{1,0},{3,1},{5,3},{7,5},{6,7},{4,6},{2,4},{8,10},{9,8},{11,9... | collective-permute-start | bytes 614408 | tf_op jit(solution)/shard_map/ppermute | solution.py:82
  85.2 0.5 collective-permute-start.29
  85.7 2.2 %collective-permute-done.21 = f32[40,1280]{1,0:T(8,128)S(1)} collective-permute-done((f32[40,1280]{1,0:T(8,128)S(1)}, f32[40,1280]{1,0:T(8,128)S(1)}, u32[]{:S(2)}, u32[]{:S(2)}) %collective-permute-start.21) | collective-permute-done | bytes 204832 | tf_op jit(solution)/shard_map/ppermute | solution.py:82
  88.0 1.6 %collective-permute-start.22 = (f32[40,1280]{1,0:T(8,128)S(1)}, f32[40,1280]{1,0:T(8,128)S(1)}, u32[]{:S(2)}, u32[]{:S(2)}) collective-permute-start(f32[40,1280]{1,0:T(8,128)S(1)} %add.565), channel_id=1, source_target_pairs={{0,2},{1,0},{3,1},{5,3},{7,5},{6,7},{4,6},{2,4},{8,10},{9,8},{11,9... | collective-permute-start | bytes 614408 | tf_op jit(solution)/shard_map/ppermute | solution.py:82
  89.6 0.5 collective-permute-start.15
  90.3 2.1 %collective-permute-done.36 = f32[40,1280]{1,0:T(8,128)S(1)} collective-permute-done((f32[40,1280]{1,0:T(8,128)S(1)}, f32[40,1280]{1,0:T(8,128)S(1)}, u32[]{:S(2)}, u32[]{:S(2)}) %collective-permute-start.36) | collective-permute-done | bytes 204832 | tf_op jit(solution)/shard_map/ppermute | solution.py:82
  92.4 1.6 %collective-permute-start.37 = (f32[40,1280]{1,0:T(8,128)S(1)}, f32[40,1280]{1,0:T(8,128)S(1)}, u32[]{:S(2)}, u32[]{:S(2)}) collective-permute-start(f32[40,1280]{1,0:T(8,128)S(1)} %add.618), channel_id=1, source_target_pairs={{0,2},{1,0},{3,1},{5,3},{7,5},{6,7},{4,6},{2,4},{8,10},{9,8},{11,9... | collective-permute-start | bytes 614408 | tf_op jit(solution)/shard_map/ppermute | solution.py:82
  94.0 0.5 collective-permute-start.30
  94.5 2.2 %collective-permute-done.22 = f32[40,1280]{1,0:T(8,128)S(1)} collective-permute-done((f32[40,1280]{1,0:T(8,128)S(1)}, f32[40,1280]{1,0:T(8,128)S(1)}, u32[]{:S(2)}, u32[]{:S(2)}) %collective-permute-start.22) | collective-permute-done | bytes 204832 | tf_op jit(solution)/shard_map/ppermute | solution.py:82
  96.8 1.6 %collective-permute-start.23 = (f32[40,1280]{1,0:T(8,128)S(1)}, f32[40,1280]{1,0:T(8,128)S(1)}, u32[]{:S(2)}, u32[]{:S(2)}) collective-permute-start(f32[40,1280]{1,0:T(8,128)S(1)} %add.570), channel_id=1, source_target_pairs={{0,2},{1,0},{3,1},{5,3},{7,5},{6,7},{4,6},{2,4},{8,10},{9,8},{11,9... | collective-permute-start | bytes 614408 | tf_op jit(solution)/shard_map/ppermute | solution.py:82
  98.4 0.5 collective-permute-start.16
  99.0 2.1 %collective-permute-done.37 = f32[40,1280]{1,0:T(8,128)S(1)} collective-permute-done((f32[40,1280]{1,0:T(8,128)S(1)}, f32[40,1280]{1,0:T(8,128)S(1)}, u32[]{:S(2)}, u32[]{:S(2)}) %collective-permute-start.37) | collective-permute-done | bytes 204832 | tf_op jit(solution)/shard_map/ppermute | solution.py:82
  101.1 1.6 %collective-permute-done.30 = f32[40,1280]{1,0:T(8,128)S(1)} collective-permute-done((f32[40,1280]{1,0:T(8,128)S(1)}, f32[40,1280]{1,0:T(8,128)S(1)}, u32[]{:S(2)}, u32[]{:S(2)}) %collective-permute-start.30) | collective-permute-done | bytes 204832 | tf_op jit(solution)/shard_map/ppermute | solution.py:82
  102.8 2.1 %collective-permute-done.23 = f32[40,1280]{1,0:T(8,128)S(1)} collective-permute-done((f32[40,1280]{1,0:T(8,128)S(1)}, f32[40,1280]{1,0:T(8,128)S(1)}, u32[]{:S(2)}, u32[]{:S(2)}) %collective-permute-start.23) | collective-permute-done | bytes 204832 | tf_op jit(solution)/shard_map/ppermute | solution.py:82
  104.9 1.3 %collective-permute-done.16 = f32[40,1280]{1,0:T(8,128)S(1)} collective-permute-done((f32[40,1280]{1,0:T(8,128)S(1)}, f32[40,1280]{1,0:T(8,128)S(1)}, u32[]{:S(2)}, u32[]{:S(2)}) %collective-permute-start.16) | collective-permute-done | bytes 204832 | tf_op jit(solution)/shard_map/ppermute | solution.py:82
  106.2 2.0 %add_divide_fusion = (f32[160,1280]{1,0:T(8,128)}, f32[160,1280]{1,0:T(8,128)}, f32[160,1280]{1,0:T(8,128)}, f32[160,1280]{1,0:T(8,128)}) fusion(f32[160,1280]{1,0:T(8,128)S(1)} %copy-done.2, f32[160,1280]{1,0:T(8,128)S(1)} %copy-done.3, f32[160,1280]{1,0:T(8,128)S(1)} %copy-done.4, f32[40,1280]{1,0:T(8,128)S(1)} %add.621, f32[40,1280]{1,0:T(8,128)S(1)} %add.598, ...), kind=kLoop, calls=%fused_computation.16 | loop fusion | flops 3481600 | bytes 6553600 | tf_op jit(solution)/shard_map/div | solution.py:189
  (90 shorter events, 1.5 us)
Async XLA Ops:
  0.6 10.9 %copy-start = (bf16[1280,1280]{1,0:T(8,128)(2,1)S(1)}, bf16[1280,1280]{1,0:T(8,128)(2,1)}, u32[]{:S(2)}) copy-start(bf16[1280,1280]{1,0:T(8,128)(2,1)} %param.8) | copy-start | bytes 9830404
  0.6 21.0 %collective-permute-start.1 = (bf16[128,1280]{1,0:T(8,128)(2,1)}, bf16[128,1280]{1,0:T(8,128)(2,1)}, u32[]{:S(2)}, u32[]{:S(2)}) collective-permute-start(bf16[128,1280]{1,0:T(8,128)(2,1)} %bitcast.115), channel_id=1, source_target_pairs={{0,8},{8,0},{16,24},{24,16},{1,9},{9,1},{17,25},{25,17},{2,10},{10... | collective-permute-start | bytes 983048 | tf_op jit(solution)/shard_map/ppermute | solution.py:103
  1.2 20.0 %collective-permute-start.4 = (bf16[128,1280]{1,0:T(8,128)(2,1)}, bf16[128,1280]{1,0:T(8,128)(2,1)}, u32[]{:S(2)}, u32[]{:S(2)}) collective-permute-start(bf16[128,1280]{1,0:T(8,128)(2,1)} %bitcast.116), channel_id=1, source_target_pairs={{0,16},{8,24},{16,0},{24,8},{1,17},{9,25},{17,1},{25,9},{2,18},{10... | collective-permute-start | bytes 983048 | tf_op jit(solution)/shard_map/ppermute | solution.py:102
  5.9 15.8 %collective-permute-start = (bf16[128,1280]{1,0:T(8,128)(2,1)}, bf16[128,1280]{1,0:T(8,128)(2,1)}, u32[]{:S(2)}, u32[]{:S(2)}) collective-permute-start(bf16[128,1280]{1,0:T(8,128)(2,1)} %get-tuple-element.73), channel_id=1, source_target_pairs={{0,8},{8,0},{16,24},{24,16},{1,9},{9,1},{17,25},{25,17},{2,10},{10... | collective-permute-start | bytes 983048 | tf_op jit(solution)/shard_map/ppermute | solution.py:105
  6.0 13.3 %collective-permute-start.2 = (bf16[128,1280]{1,0:T(8,128)(2,1)}, bf16[128,1280]{1,0:T(8,128)(2,1)}, u32[]{:S(2)}, u32[]{:S(2)}) collective-permute-start(bf16[128,1280]{1,0:T(8,128)(2,1)} %get-tuple-element.74), channel_id=1, source_target_pairs={{0,16},{8,24},{16,0},{24,8},{1,17},{9,25},{17,1},{25,9},{2,18},{10... | collective-permute-start | bytes 983048 | tf_op jit(solution)/shard_map/ppermute | solution.py:104
  19.4 10.8 %collective-permute-start.3 = (bf16[128,1280]{1,0:T(8,128)(2,1)}, bf16[128,1280]{1,0:T(8,128)(2,1)S(1)}, u32[]{:S(2)}, u32[]{:S(2)}) collective-permute-start(bf16[128,1280]{1,0:T(8,128)(2,1)} %get-tuple-element.35), channel_id=1, source_target_pairs={{0,16},{8,24},{16,0},{24,8},{1,17},{9,25},{17,1},{25,9},{2,18},{10... | collective-permute-start | bytes 983048 | tf_op jit(solution)/shard_map/ppermute | solution.py:109
  21.1 11.1 %collective-permute-start.5 = (bf16[128,1280]{1,0:T(8,128)(2,1)}, bf16[128,1280]{1,0:T(8,128)(2,1)S(1)}, u32[]{:S(2)}, u32[]{:S(2)}) collective-permute-start(bf16[128,1280]{1,0:T(8,128)(2,1)} %collective-permute-done.2), channel_id=1, source_target_pairs={{0,8},{8,0},{16,24},{24,16},{1,9},{9,1},{17,25},{25,17},{2,10},{10... | collective-permute-start | bytes 983048 | tf_op jit(solution)/shard_map/ppermute | solution.py:107
  21.1 11.1 %collective-permute-start.6 = (bf16[128,1280]{1,0:T(8,128)(2,1)}, bf16[128,1280]{1,0:T(8,128)(2,1)S(1)}, u32[]{:S(2)}, u32[]{:S(2)}) collective-permute-start(bf16[128,1280]{1,0:T(8,128)(2,1)} %collective-permute-done.4), channel_id=1, source_target_pairs={{0,8},{8,0},{16,24},{24,16},{1,9},{9,1},{17,25},{25,17},{2,10},{10... | collective-permute-start | bytes 983048 | tf_op jit(solution)/shard_map/ppermute | solution.py:106
  34.7 3.1 %collective-permute-start.7 = (f32[1]{0:T(128)}, f32[1]{0:T(128)}, u32[]{:S(2)}, u32[]{:S(2)}) collective-permute-start(f32[1]{0:T(128)} %bitcast.5), channel_id=1, source_target_pairs={{0,8},{8,0},{16,24},{24,16},{1,9},{9,1},{17,25},{25,17},{2,10},{10... | collective-permute-start | bytes 20 | tf_op jit(solution)/shard_map/ppermute | solution.py:122
  34.7 4.4 %collective-permute-start.8 = (f32[1]{0:T(128)}, f32[1]{0:T(128)}, u32[]{:S(2)}, u32[]{:S(2)}) collective-permute-start(f32[1]{0:T(128)} %bitcast.5), channel_id=1, source_target_pairs={{0,16},{8,24},{16,0},{24,8},{1,17},{9,25},{17,1},{25,9},{2,18},{10... | collective-permute-start | bytes 20 | tf_op jit(solution)/shard_map/ppermute | solution.py:122
  35.2 3.9 %collective-permute-start.9 = (f32[1]{0:T(128)}, f32[1]{0:T(128)}, u32[]{:S(2)}, u32[]{:S(2)}) collective-permute-start(f32[1]{0:T(128)} %bitcast.5), channel_id=1, source_target_pairs={{0,24},{8,16},{16,8},{24,0},{1,25},{9,17},{17,9},{25,1},{2,26},{10... | collective-permute-start | bytes 20 | tf_op jit(solution)/shard_map/ppermute | solution.py:122
  37.8 32.7 %copy-start.1 = (bf16[512,1280]{1,0:T(8,128)(2,1)}, bf16[512,1280]{1,0:T(8,128)(2,1)S(1)}, u32[]{:S(2)}) copy-start(bf16[512,1280]{1,0:T(8,128)(2,1)S(1)} %fusion.1) | copy-start | bytes 3932164
  40.5 7.9 %collective-permute-start.31 = (f32[40,1280]{1,0:T(8,128)S(1)}, f32[40,1280]{1,0:T(8,128)S(1)}, u32[]{:S(2)}, u32[]{:S(2)}) collective-permute-start(f32[40,1280]{1,0:T(8,128)S(1)} %get-tuple-element.69), channel_id=1, source_target_pairs={{0,2},{1,0},{3,1},{5,3},{7,5},{6,7},{4,6},{2,4},{8,10},{9,8},{11,9... | collective-permute-start | bytes 614408 | tf_op jit(solution)/shard_map/ppermute | solution.py:82
  42.1 8.0 %collective-permute-start.24 = (f32[40,1280]{1,0:T(8,128)S(1)}, f32[40,1280]{1,0:T(8,128)S(1)}, u32[]{:S(2)}, u32[]{:S(2)}) collective-permute-start(f32[40,1280]{1,0:T(8,128)S(1)} %get-tuple-element.70), channel_id=1, source_target_pairs={{0,1},{1,3},{3,5},{5,7},{7,6},{6,4},{4,2},{2,0},{8,9},{9,11},{11,1... | collective-permute-start | bytes 614408 | tf_op jit(solution)/shard_map/ppermute | solution.py:82
  42.6 10.3 %collective-permute-start.17 = (f32[40,1280]{1,0:T(8,128)S(1)}, f32[40,1280]{1,0:T(8,128)S(1)}, u32[]{:S(2)}, u32[]{:S(2)}) collective-permute-start(f32[40,1280]{1,0:T(8,128)S(1)} %get-tuple-element.71), channel_id=1, source_target_pairs={{0,2},{1,0},{3,1},{5,3},{7,5},{6,7},{4,6},{2,4},{8,10},{9,8},{11,9... | collective-permute-start | bytes 614408 | tf_op jit(solution)/shard_map/ppermute | solution.py:82
  44.2 10.3 %collective-permute-start.10 = (f32[40,1280]{1,0:T(8,128)S(1)}, f32[40,1280]{1,0:T(8,128)S(1)}, u32[]{:S(2)}, u32[]{:S(2)}) collective-permute-start(f32[40,1280]{1,0:T(8,128)S(1)} %get-tuple-element.68), channel_id=1, source_target_pairs={{0,1},{1,3},{3,5},{5,7},{7,6},{6,4},{4,2},{2,0},{8,9},{9,11},{11,1... | collective-permute-start | bytes 614408 | tf_op jit(solution)/shard_map/ppermute | solution.py:82
  48.5 8.8 %collective-permute-start.32 = (f32[40,1280]{1,0:T(8,128)S(1)}, f32[40,1280]{1,0:T(8,128)S(1)}, u32[]{:S(2)}, u32[]{:S(2)}) collective-permute-start(f32[40,1280]{1,0:T(8,128)S(1)} %add.603), channel_id=1, source_target_pairs={{0,2},{1,0},{3,1},{5,3},{7,5},{6,7},{4,6},{2,4},{8,10},{9,8},{11,9... | collective-permute-start | bytes 614408 | tf_op jit(solution)/shard_map/ppermute | solution.py:82
  50.1 8.8 %collective-permute-start.25 = (f32[40,1280]{1,0:T(8,128)S(1)}, f32[40,1280]{1,0:T(8,128)S(1)}, u32[]{:S(2)}, u32[]{:S(2)}) collective-permute-start(f32[40,1280]{1,0:T(8,128)S(1)} %add.580), channel_id=1, source_target_pairs={{0,1},{1,3},{3,5},{5,7},{7,6},{6,4},{4,2},{2,0},{8,9},{9,11},{11,1... | collective-permute-start | bytes 614408 | tf_op jit(solution)/shard_map/ppermute | solution.py:82
  52.9 8.8 %collective-permute-start.18 = (f32[40,1280]{1,0:T(8,128)S(1)}, f32[40,1280]{1,0:T(8,128)S(1)}, u32[]{:S(2)}, u32[]{:S(2)}) collective-permute-start(f32[40,1280]{1,0:T(8,128)S(1)} %add.545), channel_id=1, source_target_pairs={{0,2},{1,0},{3,1},{5,3},{7,5},{6,7},{4,6},{2,4},{8,10},{9,8},{11,9... | collective-permute-start | bytes 614408 | tf_op jit(solution)/shard_map/ppermute | solution.py:82
  54.5 8.8 %collective-permute-start.11 = (f32[40,1280]{1,0:T(8,128)S(1)}, f32[40,1280]{1,0:T(8,128)S(1)}, u32[]{:S(2)}, u32[]{:S(2)}) collective-permute-start(f32[40,1280]{1,0:T(8,128)S(1)} %add.518), channel_id=1, source_target_pairs={{0,1},{1,3},{3,5},{5,7},{7,6},{6,4},{4,2},{2,0},{8,9},{9,11},{11,1... | collective-permute-start | bytes 614408 | tf_op jit(solution)/shard_map/ppermute | solution.py:82
  57.3 8.8 %collective-permute-start.33 = (f32[40,1280]{1,0:T(8,128)S(1)}, f32[40,1280]{1,0:T(8,128)S(1)}, u32[]{:S(2)}, u32[]{:S(2)}) collective-permute-start(f32[40,1280]{1,0:T(8,128)S(1)} %add.606), channel_id=1, source_target_pairs={{0,2},{1,0},{3,1},{5,3},{7,5},{6,7},{4,6},{2,4},{8,10},{9,8},{11,9... | collective-permute-start | bytes 614408 | tf_op jit(solution)/shard_map/ppermute | solution.py:82
  58.9 8.8 %collective-permute-start.26 = (f32[40,1280]{1,0:T(8,128)S(1)}, f32[40,1280]{1,0:T(8,128)S(1)}, u32[]{:S(2)}, u32[]{:S(2)}) collective-permute-start(f32[40,1280]{1,0:T(8,128)S(1)} %add.583), channel_id=1, source_target_pairs={{0,1},{1,3},{3,5},{5,7},{7,6},{6,4},{4,2},{2,0},{8,9},{9,11},{11,1... | collective-permute-start | bytes 614408 | tf_op jit(solution)/shard_map/ppermute | solution.py:82
  61.6 8.8 %collective-permute-start.19 = (f32[40,1280]{1,0:T(8,128)S(1)}, f32[40,1280]{1,0:T(8,128)S(1)}, u32[]{:S(2)}, u32[]{:S(2)}) collective-permute-start(f32[40,1280]{1,0:T(8,128)S(1)} %add.550), channel_id=1, source_target_pairs={{0,2},{1,0},{3,1},{5,3},{7,5},{6,7},{4,6},{2,4},{8,10},{9,8},{11,9... | collective-permute-start | bytes 614408 | tf_op jit(solution)/shard_map/ppermute | solution.py:82
  63.3 8.8 %collective-permute-start.12 = (f32[40,1280]{1,0:T(8,128)S(1)}, f32[40,1280]{1,0:T(8,128)S(1)}, u32[]{:S(2)}, u32[]{:S(2)}) collective-permute-start(f32[40,1280]{1,0:T(8,128)S(1)} %add.521), channel_id=1, source_target_pairs={{0,1},{1,3},{3,5},{5,7},{7,6},{6,4},{4,2},{2,0},{8,9},{9,11},{11,1... | collective-permute-start | bytes 614408 | tf_op jit(solution)/shard_map/ppermute | solution.py:82
  66.0 8.8 %collective-permute-start.34 = (f32[40,1280]{1,0:T(8,128)S(1)}, f32[40,1280]{1,0:T(8,128)S(1)}, u32[]{:S(2)}, u32[]{:S(2)}) collective-permute-start(f32[40,1280]{1,0:T(8,128)S(1)} %add.609), channel_id=1, source_target_pairs={{0,2},{1,0},{3,1},{5,3},{7,5},{6,7},{4,6},{2,4},{8,10},{9,8},{11,9... | collective-permute-start | bytes 614408 | tf_op jit(solution)/shard_map/ppermute | solution.py:82
  67.7 8.8 %collective-permute-start.27 = (f32[40,1280]{1,0:T(8,128)S(1)}, f32[40,1280]{1,0:T(8,128)S(1)}, u32[]{:S(2)}, u32[]{:S(2)}) collective-permute-start(f32[40,1280]{1,0:T(8,128)S(1)} %add.586), channel_id=1, source_target_pairs={{0,1},{1,3},{3,5},{5,7},{7,6},{6,4},{4,2},{2,0},{8,9},{9,11},{11,1... | collective-permute-start | bytes 614408 | tf_op jit(solution)/shard_map/ppermute | solution.py:82
  70.4 8.7 %collective-permute-start.20 = (f32[40,1280]{1,0:T(8,128)S(1)}, f32[40,1280]{1,0:T(8,128)S(1)}, u32[]{:S(2)}, u32[]{:S(2)}) collective-permute-start(f32[40,1280]{1,0:T(8,128)S(1)} %add.555), channel_id=1, source_target_pairs={{0,2},{1,0},{3,1},{5,3},{7,5},{6,7},{4,6},{2,4},{8,10},{9,8},{11,9... | collective-permute-start | bytes 614408 | tf_op jit(solution)/shard_map/ppermute | solution.py:82
  72.1 8.8 %collective-permute-start.13 = (f32[40,1280]{1,0:T(8,128)S(1)}, f32[40,1280]{1,0:T(8,128)S(1)}, u32[]{:S(2)}, u32[]{:S(2)}) collective-permute-start(f32[40,1280]{1,0:T(8,128)S(1)} %add.524), channel_id=1, source_target_pairs={{0,1},{1,3},{3,5},{5,7},{7,6},{6,4},{4,2},{2,0},{8,9},{9,11},{11,1... | collective-permute-start | bytes 614408 | tf_op jit(solution)/shard_map/ppermute | solution.py:82
  74.8 8.8 %collective-permute-start.35 = (f32[40,1280]{1,0:T(8,128)S(1)}, f32[40,1280]{1,0:T(8,128)S(1)}, u32[]{:S(2)}, u32[]{:S(2)}) collective-permute-start(f32[40,1280]{1,0:T(8,128)S(1)} %add.612), channel_id=1, source_target_pairs={{0,2},{1,0},{3,1},{5,3},{7,5},{6,7},{4,6},{2,4},{8,10},{9,8},{11,9... | collective-permute-start | bytes 614408 | tf_op jit(solution)/shard_map/ppermute | solution.py:82
  76.5 8.8 %collective-permute-start.28 = (f32[40,1280]{1,0:T(8,128)S(1)}, f32[40,1280]{1,0:T(8,128)S(1)}, u32[]{:S(2)}, u32[]{:S(2)}) collective-permute-start(f32[40,1280]{1,0:T(8,128)S(1)} %add.589), channel_id=1, source_target_pairs={{0,1},{1,3},{3,5},{5,7},{7,6},{6,4},{4,2},{2,0},{8,9},{9,11},{11,1... | collective-permute-start | bytes 614408 | tf_op jit(solution)/shard_map/ppermute | solution.py:82
  79.2 27.0 %copy-start.2 = (f32[160,1280]{1,0:T(8,128)S(1)}, f32[160,1280]{1,0:T(8,128)}, u32[]{:S(2)}) copy-start(f32[160,1280]{1,0:T(8,128)} %param.11) | copy-start | bytes 2457604
  79.2 27.0 %copy-start.3 = (f32[160,1280]{1,0:T(8,128)S(1)}, f32[160,1280]{1,0:T(8,128)}, u32[]{:S(2)}) copy-start(f32[160,1280]{1,0:T(8,128)} %param.10) | copy-start | bytes 2457604
  79.2 27.0 %copy-start.4 = (f32[160,1280]{1,0:T(8,128)S(1)}, f32[160,1280]{1,0:T(8,128)}, u32[]{:S(2)}) copy-start(f32[160,1280]{1,0:T(8,128)} %param.9) | copy-start | bytes 2457604
  79.2 8.7 %collective-permute-start.21 = (f32[40,1280]{1,0:T(8,128)S(1)}, f32[40,1280]{1,0:T(8,128)S(1)}, u32[]{:S(2)}, u32[]{:S(2)}) collective-permute-start(f32[40,1280]{1,0:T(8,128)S(1)} %add.560), channel_id=1, source_target_pairs={{0,2},{1,0},{3,1},{5,3},{7,5},{6,7},{4,6},{2,4},{8,10},{9,8},{11,9... | collective-permute-start | bytes 614408 | tf_op jit(solution)/shard_map/ppermute | solution.py:82
  80.9 8.7 %collective-permute-start.14 = (f32[40,1280]{1,0:T(8,128)S(1)}, f32[40,1280]{1,0:T(8,128)S(1)}, u32[]{:S(2)}, u32[]{:S(2)}) collective-permute-start(f32[40,1280]{1,0:T(8,128)S(1)} %add.527), channel_id=1, source_target_pairs={{0,1},{1,3},{3,5},{5,7},{7,6},{6,4},{4,2},{2,0},{8,9},{9,11},{11,1... | collective-permute-start | bytes 614408 | tf_op jit(solution)/shard_map/ppermute | solution.py:82
  83.6 8.8 %collective-permute-start.36 = (f32[40,1280]{1,0:T(8,128)S(1)}, f32[40,1280]{1,0:T(8,128)S(1)}, u32[]{:S(2)}, u32[]{:S(2)}) collective-permute-start(f32[40,1280]{1,0:T(8,128)S(1)} %add.615), channel_id=1, source_target_pairs={{0,2},{1,0},{3,1},{5,3},{7,5},{6,7},{4,6},{2,4},{8,10},{9,8},{11,9... | collective-permute-start | bytes 614408 | tf_op jit(solution)/shard_map/ppermute | solution.py:82
  85.2 8.8 %collective-permute-start.29 = (f32[40,1280]{1,0:T(8,128)S(1)}, f32[40,1280]{1,0:T(8,128)S(1)}, u32[]{:S(2)}, u32[]{:S(2)}) collective-permute-start(f32[40,1280]{1,0:T(8,128)S(1)} %add.592), channel_id=1, source_target_pairs={{0,1},{1,3},{3,5},{5,7},{7,6},{6,4},{4,2},{2,0},{8,9},{9,11},{11,1... | collective-permute-start | bytes 614408 | tf_op jit(solution)/shard_map/ppermute | solution.py:82
  88.0 8.8 %collective-permute-start.22 = (f32[40,1280]{1,0:T(8,128)S(1)}, f32[40,1280]{1,0:T(8,128)S(1)}, u32[]{:S(2)}, u32[]{:S(2)}) collective-permute-start(f32[40,1280]{1,0:T(8,128)S(1)} %add.565), channel_id=1, source_target_pairs={{0,2},{1,0},{3,1},{5,3},{7,5},{6,7},{4,6},{2,4},{8,10},{9,8},{11,9... | collective-permute-start | bytes 614408 | tf_op jit(solution)/shard_map/ppermute | solution.py:82
  89.6 8.8 %collective-permute-start.15 = (f32[40,1280]{1,0:T(8,128)S(1)}, f32[40,1280]{1,0:T(8,128)S(1)}, u32[]{:S(2)}, u32[]{:S(2)}) collective-permute-start(f32[40,1280]{1,0:T(8,128)S(1)} %add.530), channel_id=1, source_target_pairs={{0,1},{1,3},{3,5},{5,7},{7,6},{6,4},{4,2},{2,0},{8,9},{9,11},{11,1... | collective-permute-start | bytes 614408 | tf_op jit(solution)/shard_map/ppermute | solution.py:82
  92.4 8.8 %collective-permute-start.37 = (f32[40,1280]{1,0:T(8,128)S(1)}, f32[40,1280]{1,0:T(8,128)S(1)}, u32[]{:S(2)}, u32[]{:S(2)}) collective-permute-start(f32[40,1280]{1,0:T(8,128)S(1)} %add.618), channel_id=1, source_target_pairs={{0,2},{1,0},{3,1},{5,3},{7,5},{6,7},{4,6},{2,4},{8,10},{9,8},{11,9... | collective-permute-start | bytes 614408 | tf_op jit(solution)/shard_map/ppermute | solution.py:82
  94.0 8.7 %collective-permute-start.30 = (f32[40,1280]{1,0:T(8,128)S(1)}, f32[40,1280]{1,0:T(8,128)S(1)}, u32[]{:S(2)}, u32[]{:S(2)}) collective-permute-start(f32[40,1280]{1,0:T(8,128)S(1)} %add.595), channel_id=1, source_target_pairs={{0,1},{1,3},{3,5},{5,7},{7,6},{6,4},{4,2},{2,0},{8,9},{9,11},{11,1... | collective-permute-start | bytes 614408 | tf_op jit(solution)/shard_map/ppermute | solution.py:82
  96.8 8.1 %collective-permute-start.23 = (f32[40,1280]{1,0:T(8,128)S(1)}, f32[40,1280]{1,0:T(8,128)S(1)}, u32[]{:S(2)}, u32[]{:S(2)}) collective-permute-start(f32[40,1280]{1,0:T(8,128)S(1)} %add.570), channel_id=1, source_target_pairs={{0,2},{1,0},{3,1},{5,3},{7,5},{6,7},{4,6},{2,4},{8,10},{9,8},{11,9... | collective-permute-start | bytes 614408 | tf_op jit(solution)/shard_map/ppermute | solution.py:82
  98.4 7.8 %collective-permute-start.16 = (f32[40,1280]{1,0:T(8,128)S(1)}, f32[40,1280]{1,0:T(8,128)S(1)}, u32[]{:S(2)}, u32[]{:S(2)}) collective-permute-start(f32[40,1280]{1,0:T(8,128)S(1)} %add.533), channel_id=1, source_target_pairs={{0,1},{1,3},{3,5},{5,7},{7,6},{6,4},{4,2},{2,0},{8,9},{9,11},{11,1... | collective-permute-start | bytes 614408 | tf_op jit(solution)/shard_map/ppermute | solution.py:82

commit v9 on v8

--- a/solution.py
+++ b/solution.py
@@ -61,7 +61,7 @@
     return out
 
 
-def ring_reduce_scatter(parts, ring, pieces):
+def ring_reduce_scatter(parts, ring, pieces, during=None):
     n = len(ring)
     pos_of = [0] * n
     for k, d in enumerate(ring):
@@ -75,6 +75,9 @@
 
     chains = [(-1 if c % 2 == 0 else 1, c) for c in range(pieces)]
     own = [parts(block(0, step), which, None) for step, which in chains]
+    extra = None
+    if during is not None:
+        extra = during(own)
     acc = [None] * pieces
     for s in range(n - 1):
         send = [o if x is None else x + o for x, o in zip(acc, own)]
@@ -86,7 +89,7 @@
             parts(block(s + 1, step), which, v)
             for v, (step, which) in zip(send, chains)
         ]
-    return jnp.concatenate([x + o for x, o in zip(acc, own)], axis=0)
+    return jnp.concatenate([x + o for x, o in zip(acc, own)], axis=0), extra
 
 
 def exchange_four(h_rows, grad_rows):
@@ -143,17 +146,23 @@
     h_rows = hidden.reshape(local_rows, width)
     grad_rows = output_grad.reshape(local_rows, model_width)
     if views == 4 and images_here == 1:
-        pieces = exchange_four(h_rows, grad_rows)
-        slice_width = pieces[0][1].shape[1]
+        blocks = exchange_four(h_rows, grad_rows)
+        slice_width = blocks[0][1].shape[1]
         summed = None
-        hidden_grad = jnp.zeros((views * local_rows, slice_width), jnp.bfloat16)
-        for at, h_piece, g_piece in pieces:
+        for at, h_piece, g_piece in blocks:
             term = jnp.dot(h_piece.T, g_piece, preferred_element_type=jnp.float32)
             summed = term if summed is None else summed + term
-            back = project_back(g_piece, down_weight).astype(jnp.bfloat16)
-            hidden_grad = lax.dynamic_update_slice_in_dim(hidden_grad, back, at, axis=0)
         summed = summed[None]
-        hidden_grad = hidden_grad.reshape(views, images_here, patches, slice_width)
+
+        def project_all(after):
+            out = jnp.zeros((views * local_rows, slice_width), jnp.bfloat16)
+            for at, _, g_piece in blocks:
+                _, g_piece = lax.optimization_barrier((after, g_piece))
+                back = project_back(g_piece, down_weight).astype(jnp.bfloat16)
+                out = lax.dynamic_update_slice_in_dim(out, back, at, axis=0)
+            return out.reshape(views, images_here, patches, slice_width)
+
+        hidden_grad = None
     else:
         swapped = lax.all_to_all(h_rows, "aug", split_axis=1, concat_axis=0, tiled=True)
         every = lax.all_gather(grad_rows, "aug", axis=0, tiled=True)
@@ -163,6 +172,7 @@
         summed = jnp.einsum("vipf,vipd->ifd", h_four, g_four, preferred_element_type=jnp.float32)
         back_rows = project_back(every, down_weight)
         hidden_grad = back_rows.astype(jnp.bfloat16).reshape(views, images_here, patches, slice_width)
+        project_all = None
     grads = summed / views
     partial_value = jnp.sum(grads * grads, axis=(1, 2))
     squares = butterfly_sum(partial_value, views)
@@ -180,7 +190,9 @@
         rows = lax.dynamic_slice_in_dim(source, start, half, axis=1)
         return lax.optimization_barrier(jnp.sum(factor[:, None, None] * rows, axis=0))
 
-    owned = ring_reduce_scatter(parts, ring, pieces)
+    owned, deferred = ring_reduce_scatter(parts, ring, pieces, project_all)
+    if hidden_grad is None:
+        hidden_grad = deferred
     clipped_mean = owned / images_all
     noisy = clipped_mean + noise_ratio * clip * noise / images_all
     new_first = beta_one * first_moment + (1.0 - beta_one) * noisy

time: 110 us -> 110 us (level)
  waiting for transfers between devices: 40.1 us -> 46 us
  matrix products: 21.2 us -> 15.5 us
    ppermute x28, waiting for transfers between devices: 34.4 us -> 28.9 us  [ring_reduce_scatter(): lax.ppermute(v, 'dp', right if step < 0 else left)]
    ppermute x1, waiting for transfers between devices: 0.01 us -> 5.06 us  [exchange_four(): h_far = lax.ppermute(second, 'aug', over_x)]
    ppermute x1, waiting for transfers between devices: 5.7 us -> 10.7 us  [exchange_four(): h_far_relay = lax.ppermute(cols(a ^ 3), 'aug', over_x)]
    dot_general x4, matrix products: 13.5 us -> 8.79 us  [per_device(): term = jnp.dot(h_piece.T, g_piece, preferred_element_type=jnp.float32)]
    ppermute x3, waiting for transfers between devices: 0.01 us -> 1.4 us  [butterfly_sum(): got[m] = lax.ppermute(value, 'aug', [(i, i ^ m) for i in range(4)])]
  transfers between devices with their start and end apart: 38 -> 38, of which waited for: 17 -> 18; matrix products, arithmetic and copies ran while one was open for 20% -> 15% of each run, Pallas kernels for 0% -> 0%
where the time goes in v9:
time: 110 us
  waiting for transfers between devices  46 us (42%)
  starting transfers between devices  37.6 us (34%)
  matrix products  15.5 us (14%)
  between operations  4.92 us (4%)
  other arithmetic  3.48 us (3%)
  local copies, waits for them, and re-layouts  2.27 us (2%)
    ppermute x28, starting transfers between devices, ring_reduce_scatter(): lax.ppermute(v, 'dp', right if step < 0 else left)  29.7 us
    ppermute x28, waiting for transfers between devices, ring_reduce_scatter(): lax.ppermute(v, 'dp', right if step < 0 else left)  28.9 us
    ppermute x1, waiting for transfers between devices, exchange_four(): h_far_relay = lax.ppermute(cols(a ^ 3), 'aug', over_x)  10.7 us
    dot_general x4, matrix products, per_device(): term = jnp.dot(h_piece.T, g_piece, preferred_element_type=jnp.float32)  8.79 us
    dot_general x4, matrix products, project_back(): lax.dot_general(rows, down_weight, (((1,), (1,)), ((), ())), preferred_el...  6.75 us
    ppermute x1, waiting for transfers between devices, exchange_four(): h_far = lax.ppermute(second, 'aug', over_x)  5.06 us
    ppermute x1, starting transfers between devices, exchange_four(): g_far = lax.ppermute(grad_rows, 'aug', over_x)  2.57 us
  transfers between devices with their start and end apart: 38, of which 18 were waited for; matrix products, arithmetic and copies ran while one was open for 15% of the time, Pallas kernels for 0%

profile of v9, /device:TPU:0, one launch (start us, length us, event | category | flops | bytes accessed | tf_op | source)
XLA Modules:
  0.0 109.8 jit_solution(9243568995467983490)
XLA Ops:
  0.6 0.5 collective-permute-start.1
  1.2 2.6 %collective-permute-start.4 = (bf16[128,1280]{1,0:T(8,128)(2,1)}, bf16[128,1280]{1,0:T(8,128)(2,1)}, u32[]{:S(2)}, u32[]{:S(2)}) collective-permute-start(bf16[128,1280]{1,0:T(8,128)(2,1)} %bitcast.115), channel_id=1, source_target_pairs={{0,16},{8,24},{16,0},{24,8},{1,17},{9,25},{17,1},{25,9},{2,18},{10... | collective-permute-start | bytes 983048 | tf_op jit(solution)/shard_map/ppermute | solution.py:105
  3.7 2.1 %dynamic-slice_bitcast_fusion = (bf16[128,1280]{1,0:T(8,128)(2,1)}, bf16[128,1280]{1,0:T(8,128)(2,1)}, bf16[128,1280]{1,0:T(8,128)(2,1)}) fusion(bf16[1,1,128,5120]{3,2,1,0:T(8,128)(2,1)} %param.6, s32[]{:T(128)S(6)} %select_n.691, s32[]{:T(128)S(6)} %select_n.689, s32[]{:T(128)S(6)} %select_n.690), kind=kLoop, calls=%fused_computation.21 | loop fusion | bytes 1966092 | tf_op jit(solution)/shard_map/dynamic_slice | solution.py:101
  5.9 0.2 collective-permute-start
  6.0 0.5 collective-permute-start.2
  6.5 2.2 %fusion.6 = f32[1280,1280]{1,0:T(8,128)S(1)} fusion(bf16[1,1,128,5120]{3,2,1,0:T(8,128)(2,1)} %param.6, s32[]{:T(128)S(6)} %select_n.688, bf16[1,1,128,1280]{3,2,1,0:T(8,128)(2,1)} %param.7), kind=kOutput, calls=%fused_computation.19 | convolution fusion | flops 419430400 | bytes 7208964 | tf_op jit(solution)/shard_map/dot_general | solution.py:153
  8.7 10.7 %collective-permute-done.2 = bf16[128,1280]{1,0:T(8,128)(2,1)} collective-permute-done((bf16[128,1280]{1,0:T(8,128)(2,1)}, bf16[128,1280]{1,0:T(8,128)(2,1)}, u32[]{:S(2)}, u32[]{:S(2)}) %collective-permute-start.2) | collective-permute-done | bytes 327712 | tf_op jit(solution)/shard_map/ppermute | solution.py:107
  19.4 1.8 %collective-permute-start.3 = (bf16[128,1280]{1,0:T(8,128)(2,1)S(1)}, bf16[128,1280]{1,0:T(8,128)(2,1)S(1)}, u32[]{:S(2)}, u32[]{:S(2)}) collective-permute-start(bf16[128,1280]{1,0:T(8,128)(2,1)S(1)} %copy-done.6), channel_id=1, source_target_pairs={{0,16},{8,24},{16,0},{24,8},{1,17},{9,25},{17,1},{25,9},{2,18},{10... | collective-permute-start | bytes 983048 | tf_op jit(solution)/shard_map/ppermute | solution.py:112
  21.1 0.5 collective-permute-start.6
  21.7 2.1 %convolution_add_fusion.2 = f32[1280,1280]{1,0:T(8,128)S(1)} fusion(f32[1280,1280]{1,0:T(8,128)S(1)} %fusion.6, bf16[128,1280]{1,0:T(8,128)(2,1)} %collective-permute-done, bf16[128,1280]{1,0:T(8,128)(2,1)} %collective-permute-done.1), kind=kOutput, calls=%fused_computation.2 | convolution fusion | flops 421068800 | bytes 13762560 | tf_op jit(solution)/shard_map/dot_general | solution.py:153
  23.8 5.1 %collective-permute-done.3 = bf16[128,1280]{1,0:T(8,128)(2,1)S(1)} collective-permute-done((bf16[128,1280]{1,0:T(8,128)(2,1)S(1)}, bf16[128,1280]{1,0:T(8,128)(2,1)S(1)}, u32[]{:S(2)}, u32[]{:S(2)}) %collective-permute-start.3) | collective-permute-done | bytes 327712 | tf_op jit(solution)/shard_map/ppermute | solution.py:112
  28.8 2.0 %convolution_add_fusion.1 = f32[1280,1280]{1,0:T(8,128)S(1)} fusion(f32[1280,1280]{1,0:T(8,128)S(1)} %convolution_add_fusion.2, bf16[128,1280]{1,0:T(8,128)(2,1)S(1)} %collective-permute-done.3, bf16[128,1280]{1,0:T(8,128)(2,1)} %collective-permute-done.4), kind=kOutput, calls=%fused_computation.1 | convolution fusion | flops 421068800 | bytes 13762560 | tf_op jit(solution)/shard_map/dot_general | solution.py:153
  30.9 2.5 %multiply_reduce_fusion = (f32[]{:T(128)}, f32[1280,1280]{1,0:T(8,128)S(1)}) fusion(f32[1280,1280]{1,0:T(8,128)S(1)} %convolution_add_fusion.1, bf16[128,1280]{1,0:T(8,128)(2,1)S(1)} %collective-permute-done.5, bf16[128,1280]{1,0:T(8,128)(2,1)S(1)} %collective-permute-done.6), kind=kOutput, calls=%fused_computation.4 | convolution fusion | flops 425984000 | bytes 13762564 | tf_op jit(solution)/shard_map/dot_general | solution.py:153
  33.4 1.6 %collective-permute-start.8 = (f32[1]{0:T(128)}, f32[1]{0:T(128)}, u32[]{:S(2)}, u32[]{:S(2)}) collective-permute-start(f32[1]{0:T(128)} %bitcast.5), channel_id=1, source_target_pairs={{0,16},{8,24},{16,0},{24,8},{1,17},{9,25},{17,1},{25,9},{2,18},{10... | collective-permute-start | bytes 20 | tf_op jit(solution)/shard_map/ppermute | solution.py:125
  35.0 0.3 collective-permute-start.9
  36.6 0.6 collective-permute-done.8
  37.2 0.8 collective-permute-done.9
  39.5 1.6 %collective-permute-start.31 = (f32[40,1280]{1,0:T(8,128)S(1)}, f32[40,1280]{1,0:T(8,128)S(1)}, u32[]{:S(2)}, u32[]{:S(2)}) collective-permute-start(f32[40,1280]{1,0:T(8,128)S(1)} %get-tuple-element.77), channel_id=1, source_target_pairs={{0,2},{1,0},{3,1},{5,3},{7,5},{6,7},{4,6},{2,4},{8,10},{9,8},{11,9... | collective-permute-start | bytes 614408 | tf_op jit(solution)/shard_map/ppermute | solution.py:85
  41.1 0.4 collective-permute-start.24
  41.6 1.6 %collective-permute-start.17 = (f32[40,1280]{1,0:T(8,128)S(1)}, f32[40,1280]{1,0:T(8,128)S(1)}, u32[]{:S(2)}, u32[]{:S(2)}) collective-permute-start(f32[40,1280]{1,0:T(8,128)S(1)} %get-tuple-element.79), channel_id=1, source_target_pairs={{0,2},{1,0},{3,1},{5,3},{7,5},{6,7},{4,6},{2,4},{8,10},{9,8},{11,9... | collective-permute-start | bytes 614408 | tf_op jit(solution)/shard_map/ppermute | solution.py:85
  43.1 0.4 collective-permute-start.10
  43.8 1.2 %fusion.4 = bf16[512,1280]{1,0:T(8,128)(2,1)S(1)} fusion(bf16[512,1280]{1,0:T(8,128)(2,1)S(1)} %broadcast_in_dim.2, s32[]{:T(128)S(6)} %select_n.859, bf16[128,1280]{1,0:T(8,128)(2,1)S(1)} %bitcast.116, bf16[1280,1280]{1,0:T(8,128)(2,1)S(1)} %copy-done), kind=kOutput, calls=%fused_computation.12 | convolution fusion | flops 419594240 | bytes 3932164 | tf_op jit(solution)/shard_map/dot_general | solution.py:17
  45.0 2.2 %fusion.3 = bf16[512,1280]{1,0:T(8,128)(2,1)S(1)} fusion(bf16[512,1280]{1,0:T(8,128)(2,1)S(1)} %fusion.4, s32[]{:T(128)S(6)} %select_n.860, bf16[128,1280]{1,0:T(8,128)(2,1)} %collective-permute-done.1, bf16[1280,1280]{1,0:T(8,128)(2,1)S(1)} %copy-done), kind=kOutput, calls=%fused_computation.10 | convolution fusion | flops 419594240 | bytes 3932164 | tf_op jit(solution)/shard_map/dot_general | solution.py:17
  47.2 2.2 %fusion.2 = bf16[512,1280]{1,0:T(8,128)(2,1)S(1)} fusion(bf16[512,1280]{1,0:T(8,128)(2,1)S(1)} %fusion.3, s32[]{:T(128)S(6)} %select_n.861, bf16[128,1280]{1,0:T(8,128)(2,1)} %collective-permute-done.4, bf16[1280,1280]{1,0:T(8,128)(2,1)S(1)} %copy-done), kind=kOutput, calls=%fused_computation.8 | convolution fusion | flops 419594240 | bytes 3932164 | tf_op jit(solution)/shard_map/dot_general | solution.py:17
  49.4 1.2 %fusion.1 = bf16[512,1280]{1,0:T(8,128)(2,1)S(1)} fusion(bf16[512,1280]{1,0:T(8,128)(2,1)S(1)} %fusion.2, s32[]{:T(128)S(6)} %select_n.862, bf16[128,1280]{1,0:T(8,128)(2,1)S(1)} %collective-permute-done.6, bf16[1280,1280]{1,0:T(8,128)(2,1)S(1)} %copy-done), kind=kOutput, calls=%fused_computation.6 | convolution fusion | flops 419594240 | bytes 3932164 | tf_op jit(solution)/shard_map/dot_general | solution.py:17
  50.7 1.6 %collective-permute-start.32 = (f32[40,1280]{1,0:T(8,128)S(1)}, f32[40,1280]{1,0:T(8,128)S(1)}, u32[]{:S(2)}, u32[]{:S(2)}) collective-permute-start(f32[40,1280]{1,0:T(8,128)S(1)} %add.603), channel_id=1, source_target_pairs={{0,2},{1,0},{3,1},{5,3},{7,5},{6,7},{4,6},{2,4},{8,10},{9,8},{11,9... | collective-permute-start | bytes 614408 | tf_op jit(solution)/shard_map/ppermute | solution.py:85
  52.3 0.5 collective-permute-start.25
  52.8 1.6 %collective-permute-start.18 = (f32[40,1280]{1,0:T(8,128)S(1)}, f32[40,1280]{1,0:T(8,128)S(1)}, u32[]{:S(2)}, u32[]{:S(2)}) collective-permute-start(f32[40,1280]{1,0:T(8,128)S(1)} %add.545), channel_id=1, source_target_pairs={{0,2},{1,0},{3,1},{5,3},{7,5},{6,7},{4,6},{2,4},{8,10},{9,8},{11,9... | collective-permute-start | bytes 614408 | tf_op jit(solution)/shard_map/ppermute | solution.py:85
  54.5 0.5 collective-permute-start.11
  55.1 3.6 %collective-permute-done.32 = f32[40,1280]{1,0:T(8,128)S(1)} collective-permute-done((f32[40,1280]{1,0:T(8,128)S(1)}, f32[40,1280]{1,0:T(8,128)S(1)}, u32[]{:S(2)}, u32[]{:S(2)}) %collective-permute-start.32) | collective-permute-done | bytes 204832 | tf_op jit(solution)/shard_map/ppermute | solution.py:85
  58.8 1.6 %collective-permute-start.33 = (f32[40,1280]{1,0:T(8,128)S(1)}, f32[40,1280]{1,0:T(8,128)S(1)}, u32[]{:S(2)}, u32[]{:S(2)}) collective-permute-start(f32[40,1280]{1,0:T(8,128)S(1)} %add.606), channel_id=1, source_target_pairs={{0,2},{1,0},{3,1},{5,3},{7,5},{6,7},{4,6},{2,4},{8,10},{9,8},{11,9... | collective-permute-start | bytes 614408 | tf_op jit(solution)/shard_map/ppermute | solution.py:85
  60.4 0.5 collective-permute-start.26
  60.9 2.2 %collective-permute-done.18 = f32[40,1280]{1,0:T(8,128)S(1)} collective-permute-done((f32[40,1280]{1,0:T(8,128)S(1)}, f32[40,1280]{1,0:T(8,128)S(1)}, u32[]{:S(2)}, u32[]{:S(2)}) %collective-permute-start.18) | collective-permute-done | bytes 204832 | tf_op jit(solution)/shard_map/ppermute | solution.py:85
  63.1 1.6 %collective-permute-start.19 = (f32[40,1280]{1,0:T(8,128)S(1)}, f32[40,1280]{1,0:T(8,128)S(1)}, u32[]{:S(2)}, u32[]{:S(2)}) collective-permute-start(f32[40,1280]{1,0:T(8,128)S(1)} %add.550), channel_id=1, source_target_pairs={{0,2},{1,0},{3,1},{5,3},{7,5},{6,7},{4,6},{2,4},{8,10},{9,8},{11,9... | collective-permute-start | bytes 614408 | tf_op jit(solution)/shard_map/ppermute | solution.py:85
  64.8 0.5 collective-permute-start.12
  65.4 2.1 %collective-permute-done.33 = f32[40,1280]{1,0:T(8,128)S(1)} collective-permute-done((f32[40,1280]{1,0:T(8,128)S(1)}, f32[40,1280]{1,0:T(8,128)S(1)}, u32[]{:S(2)}, u32[]{:S(2)}) %collective-permute-start.33) | collective-permute-done | bytes 204832 | tf_op jit(solution)/shard_map/ppermute | solution.py:85
  67.5 1.6 %collective-permute-start.34 = (f32[40,1280]{1,0:T(8,128)S(1)}, f32[40,1280]{1,0:T(8,128)S(1)}, u32[]{:S(2)}, u32[]{:S(2)}) collective-permute-start(f32[40,1280]{1,0:T(8,128)S(1)} %add.609), channel_id=1, source_target_pairs={{0,2},{1,0},{3,1},{5,3},{7,5},{6,7},{4,6},{2,4},{8,10},{9,8},{11,9... | collective-permute-start | bytes 614408 | tf_op jit(solution)/shard_map/ppermute | solution.py:85
  69.2 0.5 collective-permute-start.27
  69.7 2.2 %collective-permute-done.19 = f32[40,1280]{1,0:T(8,128)S(1)} collective-permute-done((f32[40,1280]{1,0:T(8,128)S(1)}, f32[40,1280]{1,0:T(8,128)S(1)}, u32[]{:S(2)}, u32[]{:S(2)}) %collective-permute-start.19) | collective-permute-done | bytes 204832 | tf_op jit(solution)/shard_map/ppermute | solution.py:85
  71.9 1.6 %collective-permute-start.20 = (f32[40,1280]{1,0:T(8,128)S(1)}, f32[40,1280]{1,0:T(8,128)S(1)}, u32[]{:S(2)}, u32[]{:S(2)}) collective-permute-start(f32[40,1280]{1,0:T(8,128)S(1)} %add.555), channel_id=1, source_target_pairs={{0,2},{1,0},{3,1},{5,3},{7,5},{6,7},{4,6},{2,4},{8,10},{9,8},{11,9... | collective-permute-start | bytes 614408 | tf_op jit(solution)/shard_map/ppermute | solution.py:85
  73.6 0.5 collective-permute-start.13
  74.2 2.1 %collective-permute-done.34 = f32[40,1280]{1,0:T(8,128)S(1)} collective-permute-done((f32[40,1280]{1,0:T(8,128)S(1)}, f32[40,1280]{1,0:T(8,128)S(1)}, u32[]{:S(2)}, u32[]{:S(2)}) %collective-permute-start.34) | collective-permute-done | bytes 204832 | tf_op jit(solution)/shard_map/ppermute | solution.py:85
  76.3 1.6 %collective-permute-start.35 = (f32[40,1280]{1,0:T(8,128)S(1)}, f32[40,1280]{1,0:T(8,128)S(1)}, u32[]{:S(2)}, u32[]{:S(2)}) collective-permute-start(f32[40,1280]{1,0:T(8,128)S(1)} %add.612), channel_id=1, source_target_pairs={{0,2},{1,0},{3,1},{5,3},{7,5},{6,7},{4,6},{2,4},{8,10},{9,8},{11,9... | collective-permute-start | bytes 614408 | tf_op jit(solution)/shard_map/ppermute | solution.py:85
  78.0 0.5 collective-permute-start.28
  78.5 2.2 %collective-permute-done.20 = f32[40,1280]{1,0:T(8,128)S(1)} collective-permute-done((f32[40,1280]{1,0:T(8,128)S(1)}, f32[40,1280]{1,0:T(8,128)S(1)}, u32[]{:S(2)}, u32[]{:S(2)}) %collective-permute-start.20) | collective-permute-done | bytes 204832 | tf_op jit(solution)/shard_map/ppermute | solution.py:85
  80.7 1.6 %collective-permute-start.21 = (f32[40,1280]{1,0:T(8,128)S(1)}, f32[40,1280]{1,0:T(8,128)S(1)}, u32[]{:S(2)}, u32[]{:S(2)}) collective-permute-start(f32[40,1280]{1,0:T(8,128)S(1)} %add.560), channel_id=1, source_target_pairs={{0,2},{1,0},{3,1},{5,3},{7,5},{6,7},{4,6},{2,4},{8,10},{9,8},{11,9... | collective-permute-start | bytes 614408 | tf_op jit(solution)/shard_map/ppermute | solution.py:85
  82.4 0.5 collective-permute-start.14
  83.0 2.0 %collective-permute-done.35 = f32[40,1280]{1,0:T(8,128)S(1)} collective-permute-done((f32[40,1280]{1,0:T(8,128)S(1)}, f32[40,1280]{1,0:T(8,128)S(1)}, u32[]{:S(2)}, u32[]{:S(2)}) %collective-permute-start.35) | collective-permute-done | bytes 204832 | tf_op jit(solution)/shard_map/ppermute | solution.py:85
  85.1 1.6 %collective-permute-start.36 = (f32[40,1280]{1,0:T(8,128)S(1)}, f32[40,1280]{1,0:T(8,128)S(1)}, u32[]{:S(2)}, u32[]{:S(2)}) collective-permute-start(f32[40,1280]{1,0:T(8,128)S(1)} %add.615), channel_id=1, source_target_pairs={{0,2},{1,0},{3,1},{5,3},{7,5},{6,7},{4,6},{2,4},{8,10},{9,8},{11,9... | collective-permute-start | bytes 614408 | tf_op jit(solution)/shard_map/ppermute | solution.py:85
  86.7 0.5 collective-permute-start.29
  87.2 2.2 %collective-permute-done.21 = f32[40,1280]{1,0:T(8,128)S(1)} collective-permute-done((f32[40,1280]{1,0:T(8,128)S(1)}, f32[40,1280]{1,0:T(8,128)S(1)}, u32[]{:S(2)}, u32[]{:S(2)}) %collective-permute-start.21) | collective-permute-done | bytes 204832 | tf_op jit(solution)/shard_map/ppermute | solution.py:85
  89.5 1.6 %collective-permute-start.22 = (f32[40,1280]{1,0:T(8,128)S(1)}, f32[40,1280]{1,0:T(8,128)S(1)}, u32[]{:S(2)}, u32[]{:S(2)}) collective-permute-start(f32[40,1280]{1,0:T(8,128)S(1)} %add.565), channel_id=1, source_target_pairs={{0,2},{1,0},{3,1},{5,3},{7,5},{6,7},{4,6},{2,4},{8,10},{9,8},{11,9... | collective-permute-start | bytes 614408 | tf_op jit(solution)/shard_map/ppermute | solution.py:85
  91.1 0.5 collective-permute-start.15
  91.8 2.1 %collective-permute-done.36 = f32[40,1280]{1,0:T(8,128)S(1)} collective-permute-done((f32[40,1280]{1,0:T(8,128)S(1)}, f32[40,1280]{1,0:T(8,128)S(1)}, u32[]{:S(2)}, u32[]{:S(2)}) %collective-permute-start.36) | collective-permute-done | bytes 204832 | tf_op jit(solution)/shard_map/ppermute | solution.py:85
  93.9 1.6 %collective-permute-start.37 = (f32[40,1280]{1,0:T(8,128)S(1)}, f32[40,1280]{1,0:T(8,128)S(1)}, u32[]{:S(2)}, u32[]{:S(2)}) collective-permute-start(f32[40,1280]{1,0:T(8,128)S(1)} %add.618), channel_id=1, source_target_pairs={{0,2},{1,0},{3,1},{5,3},{7,5},{6,7},{4,6},{2,4},{8,10},{9,8},{11,9... | collective-permute-start | bytes 614408 | tf_op jit(solution)/shard_map/ppermute | solution.py:85
  95.5 0.5 collective-permute-start.30
  96.0 2.2 %collective-permute-done.22 = f32[40,1280]{1,0:T(8,128)S(1)} collective-permute-done((f32[40,1280]{1,0:T(8,128)S(1)}, f32[40,1280]{1,0:T(8,128)S(1)}, u32[]{:S(2)}, u32[]{:S(2)}) %collective-permute-start.22) | collective-permute-done | bytes 204832 | tf_op jit(solution)/shard_map/ppermute | solution.py:85
  98.2 1.6 %collective-permute-start.23 = (f32[40,1280]{1,0:T(8,128)S(1)}, f32[40,1280]{1,0:T(8,128)S(1)}, u32[]{:S(2)}, u32[]{:S(2)}) collective-permute-start(f32[40,1280]{1,0:T(8,128)S(1)} %add.570), channel_id=1, source_target_pairs={{0,2},{1,0},{3,1},{5,3},{7,5},{6,7},{4,6},{2,4},{8,10},{9,8},{11,9... | collective-permute-start | bytes 614408 | tf_op jit(solution)/shard_map/ppermute | solution.py:85
  99.9 0.5 collective-permute-start.16
  100.5 2.1 %collective-permute-done.37 = f32[40,1280]{1,0:T(8,128)S(1)} collective-permute-done((f32[40,1280]{1,0:T(8,128)S(1)}, f32[40,1280]{1,0:T(8,128)S(1)}, u32[]{:S(2)}, u32[]{:S(2)}) %collective-permute-start.37) | collective-permute-done | bytes 204832 | tf_op jit(solution)/shard_map/ppermute | solution.py:85
  102.6 1.6 %collective-permute-done.30 = f32[40,1280]{1,0:T(8,128)S(1)} collective-permute-done((f32[40,1280]{1,0:T(8,128)S(1)}, f32[40,1280]{1,0:T(8,128)S(1)}, u32[]{:S(2)}, u32[]{:S(2)}) %collective-permute-start.30) | collective-permute-done | bytes 204832 | tf_op jit(solution)/shard_map/ppermute | solution.py:85
  104.3 0.9 collective-permute-done.23
  105.2 1.4 %collective-permute-done.16 = f32[40,1280]{1,0:T(8,128)S(1)} collective-permute-done((f32[40,1280]{1,0:T(8,128)S(1)}, f32[40,1280]{1,0:T(8,128)S(1)}, u32[]{:S(2)}, u32[]{:S(2)}) %collective-permute-start.16) | collective-permute-done | bytes 204832 | tf_op jit(solution)/shard_map/ppermute | solution.py:85
  106.7 2.0 %add_divide_fusion = (f32[160,1280]{1,0:T(8,128)}, f32[160,1280]{1,0:T(8,128)}, f32[160,1280]{1,0:T(8,128)}, f32[160,1280]{1,0:T(8,128)}) fusion(f32[160,1280]{1,0:T(8,128)S(1)} %copy-done.3, f32[160,1280]{1,0:T(8,128)S(1)} %copy-done.4, f32[160,1280]{1,0:T(8,128)S(1)} %copy-done.5, f32[40,1280]{1,0:T(8,128)S(1)} %add.621, f32[40,1280]{1,0:T(8,128)S(1)} %add.598, ...), kind=kLoop, calls=%fused_computation.16 | loop fusion | flops 3481600 | bytes 6553600 | tf_op jit(solution)/shard_map/div | solution.py:201
  (94 shorter events, 1.7 us)
Async XLA Ops:
  0.6 43.2 %copy-start = (bf16[1280,1280]{1,0:T(8,128)(2,1)S(1)}, bf16[1280,1280]{1,0:T(8,128)(2,1)}, u32[]{:S(2)}) copy-start(bf16[1280,1280]{1,0:T(8,128)(2,1)} %param.8) | copy-start | bytes 9830404
  0.6 21.0 %collective-permute-start.1 = (bf16[128,1280]{1,0:T(8,128)(2,1)}, bf16[128,1280]{1,0:T(8,128)(2,1)}, u32[]{:S(2)}, u32[]{:S(2)}) collective-permute-start(bf16[128,1280]{1,0:T(8,128)(2,1)} %bitcast.114), channel_id=1, source_target_pairs={{0,8},{8,0},{16,24},{24,16},{1,9},{9,1},{17,25},{25,17},{2,10},{10... | collective-permute-start | bytes 983048 | tf_op jit(solution)/shard_map/ppermute | solution.py:106
  1.2 20.0 %collective-permute-start.4 = (bf16[128,1280]{1,0:T(8,128)(2,1)}, bf16[128,1280]{1,0:T(8,128)(2,1)}, u32[]{:S(2)}, u32[]{:S(2)}) collective-permute-start(bf16[128,1280]{1,0:T(8,128)(2,1)} %bitcast.115), channel_id=1, source_target_pairs={{0,16},{8,24},{16,0},{24,8},{1,17},{9,25},{17,1},{25,9},{2,18},{10... | collective-permute-start | bytes 983048 | tf_op jit(solution)/shard_map/ppermute | solution.py:105
  5.9 15.8 %collective-permute-start = (bf16[128,1280]{1,0:T(8,128)(2,1)}, bf16[128,1280]{1,0:T(8,128)(2,1)}, u32[]{:S(2)}, u32[]{:S(2)}) collective-permute-start(bf16[128,1280]{1,0:T(8,128)(2,1)} %get-tuple-element.81), channel_id=1, source_target_pairs={{0,8},{8,0},{16,24},{24,16},{1,9},{9,1},{17,25},{25,17},{2,10},{10... | collective-permute-start | bytes 983048 | tf_op jit(solution)/shard_map/ppermute | solution.py:108
  6.0 13.3 %collective-permute-start.2 = (bf16[128,1280]{1,0:T(8,128)(2,1)}, bf16[128,1280]{1,0:T(8,128)(2,1)}, u32[]{:S(2)}, u32[]{:S(2)}) collective-permute-start(bf16[128,1280]{1,0:T(8,128)(2,1)} %get-tuple-element.82), channel_id=1, source_target_pairs={{0,16},{8,24},{16,0},{24,8},{1,17},{9,25},{17,1},{25,9},{2,18},{10... | collective-permute-start | bytes 983048 | tf_op jit(solution)/shard_map/ppermute | solution.py:107
  6.5 12.8 %copy-start.6 = (bf16[128,1280]{1,0:T(8,128)(2,1)S(1)}, bf16[128,1280]{1,0:T(8,128)(2,1)}, u32[]{:S(2)}) copy-start(bf16[128,1280]{1,0:T(8,128)(2,1)} %get-tuple-element.39) | copy-start | bytes 983044
  19.4 9.5 %collective-permute-start.3 = (bf16[128,1280]{1,0:T(8,128)(2,1)S(1)}, bf16[128,1280]{1,0:T(8,128)(2,1)S(1)}, u32[]{:S(2)}, u32[]{:S(2)}) collective-permute-start(bf16[128,1280]{1,0:T(8,128)(2,1)S(1)} %copy-done.6), channel_id=1, source_target_pairs={{0,16},{8,24},{16,0},{24,8},{1,17},{9,25},{17,1},{25,9},{2,18},{10... | collective-permute-start | bytes 983048 | tf_op jit(solution)/shard_map/ppermute | solution.py:112
  21.1 9.7 %collective-permute-start.5 = (bf16[128,1280]{1,0:T(8,128)(2,1)}, bf16[128,1280]{1,0:T(8,128)(2,1)S(1)}, u32[]{:S(2)}, u32[]{:S(2)}) collective-permute-start(bf16[128,1280]{1,0:T(8,128)(2,1)} %collective-permute-done.2), channel_id=1, source_target_pairs={{0,8},{8,0},{16,24},{24,16},{1,9},{9,1},{17,25},{25,17},{2,10},{10... | collective-permute-start | bytes 983048 | tf_op jit(solution)/shard_map/ppermute | solution.py:110
  21.1 9.8 %collective-permute-start.6 = (bf16[128,1280]{1,0:T(8,128)(2,1)}, bf16[128,1280]{1,0:T(8,128)(2,1)S(1)}, u32[]{:S(2)}, u32[]{:S(2)}) collective-permute-start(bf16[128,1280]{1,0:T(8,128)(2,1)} %collective-permute-done.4), channel_id=1, source_target_pairs={{0,8},{8,0},{16,24},{24,16},{1,9},{9,1},{17,25},{25,17},{2,10},{10... | collective-permute-start | bytes 983048 | tf_op jit(solution)/shard_map/ppermute | solution.py:109
  30.9 13.0 %copy-start.1 = (bf16[1,1,128,1280]{3,2,1,0:T(8,128)(2,1)S(1)}, bf16[1,1,128,1280]{3,2,1,0:T(8,128)(2,1)}, u32[]{:S(2)}) copy-start(bf16[1,1,128,1280]{3,2,1,0:T(8,128)(2,1)} %param.7) | copy-start | bytes 983044
  33.4 1.9 %collective-permute-start.7 = (f32[1]{0:T(128)}, f32[1]{0:T(128)}, u32[]{:S(2)}, u32[]{:S(2)}) collective-permute-start(f32[1]{0:T(128)} %bitcast.5), channel_id=1, source_target_pairs={{0,8},{8,0},{16,24},{24,16},{1,9},{9,1},{17,25},{25,17},{2,10},{10... | collective-permute-start | bytes 20 | tf_op jit(solution)/shard_map/ppermute | solution.py:125
  33.4 3.8 %collective-permute-start.8 = (f32[1]{0:T(128)}, f32[1]{0:T(128)}, u32[]{:S(2)}, u32[]{:S(2)}) collective-permute-start(f32[1]{0:T(128)} %bitcast.5), channel_id=1, source_target_pairs={{0,16},{8,24},{16,0},{24,8},{1,17},{9,25},{17,1},{25,9},{2,18},{10... | collective-permute-start | bytes 20 | tf_op jit(solution)/shard_map/ppermute | solution.py:125
  35.0 3.1 %collective-permute-start.9 = (f32[1]{0:T(128)}, f32[1]{0:T(128)}, u32[]{:S(2)}, u32[]{:S(2)}) collective-permute-start(f32[1]{0:T(128)} %bitcast.5), channel_id=1, source_target_pairs={{0,24},{8,16},{16,8},{24,0},{1,25},{9,17},{17,9},{25,1},{2,26},{10... | collective-permute-start | bytes 20 | tf_op jit(solution)/shard_map/ppermute | solution.py:125
  39.5 11.1 %collective-permute-start.31 = (f32[40,1280]{1,0:T(8,128)S(1)}, f32[40,1280]{1,0:T(8,128)S(1)}, u32[]{:S(2)}, u32[]{:S(2)}) collective-permute-start(f32[40,1280]{1,0:T(8,128)S(1)} %get-tuple-element.77), channel_id=1, source_target_pairs={{0,2},{1,0},{3,1},{5,3},{7,5},{6,7},{4,6},{2,4},{8,10},{9,8},{11,9... | collective-permute-start | bytes 614408 | tf_op jit(solution)/shard_map/ppermute | solution.py:85
  41.1 11.2 %collective-permute-start.24 = (f32[40,1280]{1,0:T(8,128)S(1)}, f32[40,1280]{1,0:T(8,128)S(1)}, u32[]{:S(2)}, u32[]{:S(2)}) collective-permute-start(f32[40,1280]{1,0:T(8,128)S(1)} %get-tuple-element.78), channel_id=1, source_target_pairs={{0,1},{1,3},{3,5},{5,7},{7,6},{6,4},{4,2},{2,0},{8,9},{9,11},{11,1... | collective-permute-start | bytes 614408 | tf_op jit(solution)/shard_map/ppermute | solution.py:85
  41.6 11.2 %collective-permute-start.17 = (f32[40,1280]{1,0:T(8,128)S(1)}, f32[40,1280]{1,0:T(8,128)S(1)}, u32[]{:S(2)}, u32[]{:S(2)}) collective-permute-start(f32[40,1280]{1,0:T(8,128)S(1)} %get-tuple-element.79), channel_id=1, source_target_pairs={{0,2},{1,0},{3,1},{5,3},{7,5},{6,7},{4,6},{2,4},{8,10},{9,8},{11,9... | collective-permute-start | bytes 614408 | tf_op jit(solution)/shard_map/ppermute | solution.py:85
  43.1 11.3 %collective-permute-start.10 = (f32[40,1280]{1,0:T(8,128)S(1)}, f32[40,1280]{1,0:T(8,128)S(1)}, u32[]{:S(2)}, u32[]{:S(2)}) collective-permute-start(f32[40,1280]{1,0:T(8,128)S(1)} %get-tuple-element.76), channel_id=1, source_target_pairs={{0,1},{1,3},{3,5},{5,7},{7,6},{6,4},{4,2},{2,0},{8,9},{9,11},{11,1... | collective-permute-start | bytes 614408 | tf_op jit(solution)/shard_map/ppermute | solution.py:85
  50.6 27.4 %copy-start.2 = (bf16[512,1280]{1,0:T(8,128)(2,1)}, bf16[512,1280]{1,0:T(8,128)(2,1)S(1)}, u32[]{:S(2)}) copy-start(bf16[512,1280]{1,0:T(8,128)(2,1)S(1)} %fusion.1) | copy-start | bytes 3932164
  50.7 8.1 %collective-permute-start.32 = (f32[40,1280]{1,0:T(8,128)S(1)}, f32[40,1280]{1,0:T(8,128)S(1)}, u32[]{:S(2)}, u32[]{:S(2)}) collective-permute-start(f32[40,1280]{1,0:T(8,128)S(1)} %add.603), channel_id=1, source_target_pairs={{0,2},{1,0},{3,1},{5,3},{7,5},{6,7},{4,6},{2,4},{8,10},{9,8},{11,9... | collective-permute-start | bytes 614408 | tf_op jit(solution)/shard_map/ppermute | solution.py:85
  52.3 8.1 %collective-permute-start.25 = (f32[40,1280]{1,0:T(8,128)S(1)}, f32[40,1280]{1,0:T(8,128)S(1)}, u32[]{:S(2)}, u32[]{:S(2)}) collective-permute-start(f32[40,1280]{1,0:T(8,128)S(1)} %add.580), channel_id=1, source_target_pairs={{0,1},{1,3},{3,5},{5,7},{7,6},{6,4},{4,2},{2,0},{8,9},{9,11},{11,1... | collective-permute-start | bytes 614408 | tf_op jit(solution)/shard_map/ppermute | solution.py:85
  52.8 10.3 %collective-permute-start.18 = (f32[40,1280]{1,0:T(8,128)S(1)}, f32[40,1280]{1,0:T(8,128)S(1)}, u32[]{:S(2)}, u32[]{:S(2)}) collective-permute-start(f32[40,1280]{1,0:T(8,128)S(1)} %add.545), channel_id=1, source_target_pairs={{0,2},{1,0},{3,1},{5,3},{7,5},{6,7},{4,6},{2,4},{8,10},{9,8},{11,9... | collective-permute-start | bytes 614408 | tf_op jit(solution)/shard_map/ppermute | solution.py:85
  54.5 10.3 %collective-permute-start.11 = (f32[40,1280]{1,0:T(8,128)S(1)}, f32[40,1280]{1,0:T(8,128)S(1)}, u32[]{:S(2)}, u32[]{:S(2)}) collective-permute-start(f32[40,1280]{1,0:T(8,128)S(1)} %add.518), channel_id=1, source_target_pairs={{0,1},{1,3},{3,5},{5,7},{7,6},{6,4},{4,2},{2,0},{8,9},{9,11},{11,1... | collective-permute-start | bytes 614408 | tf_op jit(solution)/shard_map/ppermute | solution.py:85
  58.8 8.7 %collective-permute-start.33 = (f32[40,1280]{1,0:T(8,128)S(1)}, f32[40,1280]{1,0:T(8,128)S(1)}, u32[]{:S(2)}, u32[]{:S(2)}) collective-permute-start(f32[40,1280]{1,0:T(8,128)S(1)} %add.606), channel_id=1, source_target_pairs={{0,2},{1,0},{3,1},{5,3},{7,5},{6,7},{4,6},{2,4},{8,10},{9,8},{11,9... | collective-permute-start | bytes 614408 | tf_op jit(solution)/shard_map/ppermute | solution.py:85
  60.4 8.7 %collective-permute-start.26 = (f32[40,1280]{1,0:T(8,128)S(1)}, f32[40,1280]{1,0:T(8,128)S(1)}, u32[]{:S(2)}, u32[]{:S(2)}) collective-permute-start(f32[40,1280]{1,0:T(8,128)S(1)} %add.583), channel_id=1, source_target_pairs={{0,1},{1,3},{3,5},{5,7},{7,6},{6,4},{4,2},{2,0},{8,9},{9,11},{11,1... | collective-permute-start | bytes 614408 | tf_op jit(solution)/shard_map/ppermute | solution.py:85
  63.1 8.7 %collective-permute-start.19 = (f32[40,1280]{1,0:T(8,128)S(1)}, f32[40,1280]{1,0:T(8,128)S(1)}, u32[]{:S(2)}, u32[]{:S(2)}) collective-permute-start(f32[40,1280]{1,0:T(8,128)S(1)} %add.550), channel_id=1, source_target_pairs={{0,2},{1,0},{3,1},{5,3},{7,5},{6,7},{4,6},{2,4},{8,10},{9,8},{11,9... | collective-permute-start | bytes 614408 | tf_op jit(solution)/shard_map/ppermute | solution.py:85
  64.8 8.8 %collective-permute-start.12 = (f32[40,1280]{1,0:T(8,128)S(1)}, f32[40,1280]{1,0:T(8,128)S(1)}, u32[]{:S(2)}, u32[]{:S(2)}) collective-permute-start(f32[40,1280]{1,0:T(8,128)S(1)} %add.521), channel_id=1, source_target_pairs={{0,1},{1,3},{3,5},{5,7},{7,6},{6,4},{4,2},{2,0},{8,9},{9,11},{11,1... | collective-permute-start | bytes 614408 | tf_op jit(solution)/shard_map/ppermute | solution.py:85
  67.5 8.7 %collective-permute-start.34 = (f32[40,1280]{1,0:T(8,128)S(1)}, f32[40,1280]{1,0:T(8,128)S(1)}, u32[]{:S(2)}, u32[]{:S(2)}) collective-permute-start(f32[40,1280]{1,0:T(8,128)S(1)} %add.609), channel_id=1, source_target_pairs={{0,2},{1,0},{3,1},{5,3},{7,5},{6,7},{4,6},{2,4},{8,10},{9,8},{11,9... | collective-permute-start | bytes 614408 | tf_op jit(solution)/shard_map/ppermute | solution.py:85
  69.2 8.7 %collective-permute-start.27 = (f32[40,1280]{1,0:T(8,128)S(1)}, f32[40,1280]{1,0:T(8,128)S(1)}, u32[]{:S(2)}, u32[]{:S(2)}) collective-permute-start(f32[40,1280]{1,0:T(8,128)S(1)} %add.586), channel_id=1, source_target_pairs={{0,1},{1,3},{3,5},{5,7},{7,6},{6,4},{4,2},{2,0},{8,9},{9,11},{11,1... | collective-permute-start | bytes 614408 | tf_op jit(solution)/shard_map/ppermute | solution.py:85
  71.9 8.8 %collective-permute-start.20 = (f32[40,1280]{1,0:T(8,128)S(1)}, f32[40,1280]{1,0:T(8,128)S(1)}, u32[]{:S(2)}, u32[]{:S(2)}) collective-permute-start(f32[40,1280]{1,0:T(8,128)S(1)} %add.555), channel_id=1, source_target_pairs={{0,2},{1,0},{3,1},{5,3},{7,5},{6,7},{4,6},{2,4},{8,10},{9,8},{11,9... | collective-permute-start | bytes 614408 | tf_op jit(solution)/shard_map/ppermute | solution.py:85
  73.6 8.8 %collective-permute-start.13 = (f32[40,1280]{1,0:T(8,128)S(1)}, f32[40,1280]{1,0:T(8,128)S(1)}, u32[]{:S(2)}, u32[]{:S(2)}) collective-permute-start(f32[40,1280]{1,0:T(8,128)S(1)} %add.524), channel_id=1, source_target_pairs={{0,1},{1,3},{3,5},{5,7},{7,6},{6,4},{4,2},{2,0},{8,9},{9,11},{11,1... | collective-permute-start | bytes 614408 | tf_op jit(solution)/shard_map/ppermute | solution.py:85
  76.3 8.7 %collective-permute-start.35 = (f32[40,1280]{1,0:T(8,128)S(1)}, f32[40,1280]{1,0:T(8,128)S(1)}, u32[]{:S(2)}, u32[]{:S(2)}) collective-permute-start(f32[40,1280]{1,0:T(8,128)S(1)} %add.612), channel_id=1, source_target_pairs={{0,2},{1,0},{3,1},{5,3},{7,5},{6,7},{4,6},{2,4},{8,10},{9,8},{11,9... | collective-permute-start | bytes 614408 | tf_op jit(solution)/shard_map/ppermute | solution.py:85
  78.0 8.7 %collective-permute-start.28 = (f32[40,1280]{1,0:T(8,128)S(1)}, f32[40,1280]{1,0:T(8,128)S(1)}, u32[]{:S(2)}, u32[]{:S(2)}) collective-permute-start(f32[40,1280]{1,0:T(8,128)S(1)} %add.589), channel_id=1, source_target_pairs={{0,1},{1,3},{3,5},{5,7},{7,6},{6,4},{4,2},{2,0},{8,9},{9,11},{11,1... | collective-permute-start | bytes 614408 | tf_op jit(solution)/shard_map/ppermute | solution.py:85
  80.7 25.9 %copy-start.3 = (f32[160,1280]{1,0:T(8,128)S(1)}, f32[160,1280]{1,0:T(8,128)}, u32[]{:S(2)}) copy-start(f32[160,1280]{1,0:T(8,128)} %param.11) | copy-start | bytes 2457604
  80.7 25.9 %copy-start.4 = (f32[160,1280]{1,0:T(8,128)S(1)}, f32[160,1280]{1,0:T(8,128)}, u32[]{:S(2)}) copy-start(f32[160,1280]{1,0:T(8,128)} %param.10) | copy-start | bytes 2457604
  80.7 25.9 %copy-start.5 = (f32[160,1280]{1,0:T(8,128)S(1)}, f32[160,1280]{1,0:T(8,128)}, u32[]{:S(2)}) copy-start(f32[160,1280]{1,0:T(8,128)} %param.9) | copy-start | bytes 2457604
  80.7 8.7 %collective-permute-start.21 = (f32[40,1280]{1,0:T(8,128)S(1)}, f32[40,1280]{1,0:T(8,128)S(1)}, u32[]{:S(2)}, u32[]{:S(2)}) collective-permute-start(f32[40,1280]{1,0:T(8,128)S(1)} %add.560), channel_id=1, source_target_pairs={{0,2},{1,0},{3,1},{5,3},{7,5},{6,7},{4,6},{2,4},{8,10},{9,8},{11,9... | collective-permute-start | bytes 614408 | tf_op jit(solution)/shard_map/ppermute | solution.py:85
  82.4 8.7 %collective-permute-start.14 = (f32[40,1280]{1,0:T(8,128)S(1)}, f32[40,1280]{1,0:T(8,128)S(1)}, u32[]{:S(2)}, u32[]{:S(2)}) collective-permute-start(f32[40,1280]{1,0:T(8,128)S(1)} %add.527), channel_id=1, source_target_pairs={{0,1},{1,3},{3,5},{5,7},{7,6},{6,4},{4,2},{2,0},{8,9},{9,11},{11,1... | collective-permute-start | bytes 614408 | tf_op jit(solution)/shard_map/ppermute | solution.py:85
  85.1 8.7 %collective-permute-start.36 = (f32[40,1280]{1,0:T(8,128)S(1)}, f32[40,1280]{1,0:T(8,128)S(1)}, u32[]{:S(2)}, u32[]{:S(2)}) collective-permute-start(f32[40,1280]{1,0:T(8,128)S(1)} %add.615), channel_id=1, source_target_pairs={{0,2},{1,0},{3,1},{5,3},{7,5},{6,7},{4,6},{2,4},{8,10},{9,8},{11,9... | collective-permute-start | bytes 614408 | tf_op jit(solution)/shard_map/ppermute | solution.py:85
  86.7 8.7 %collective-permute-start.29 = (f32[40,1280]{1,0:T(8,128)S(1)}, f32[40,1280]{1,0:T(8,128)S(1)}, u32[]{:S(2)}, u32[]{:S(2)}) collective-permute-start(f32[40,1280]{1,0:T(8,128)S(1)} %add.592), channel_id=1, source_target_pairs={{0,1},{1,3},{3,5},{5,7},{7,6},{6,4},{4,2},{2,0},{8,9},{9,11},{11,1... | collective-permute-start | bytes 614408 | tf_op jit(solution)/shard_map/ppermute | solution.py:85
  89.5 8.7 %collective-permute-start.22 = (f32[40,1280]{1,0:T(8,128)S(1)}, f32[40,1280]{1,0:T(8,128)S(1)}, u32[]{:S(2)}, u32[]{:S(2)}) collective-permute-start(f32[40,1280]{1,0:T(8,128)S(1)} %add.565), channel_id=1, source_target_pairs={{0,2},{1,0},{3,1},{5,3},{7,5},{6,7},{4,6},{2,4},{8,10},{9,8},{11,9... | collective-permute-start | bytes 614408 | tf_op jit(solution)/shard_map/ppermute | solution.py:85
  91.1 8.7 %collective-permute-start.15 = (f32[40,1280]{1,0:T(8,128)S(1)}, f32[40,1280]{1,0:T(8,128)S(1)}, u32[]{:S(2)}, u32[]{:S(2)}) collective-permute-start(f32[40,1280]{1,0:T(8,128)S(1)} %add.530), channel_id=1, source_target_pairs={{0,1},{1,3},{3,5},{5,7},{7,6},{6,4},{4,2},{2,0},{8,9},{9,11},{11,1... | collective-permute-start | bytes 614408 | tf_op jit(solution)/shard_map/ppermute | solution.py:85
  93.9 8.7 %collective-permute-start.37 = (f32[40,1280]{1,0:T(8,128)S(1)}, f32[40,1280]{1,0:T(8,128)S(1)}, u32[]{:S(2)}, u32[]{:S(2)}) collective-permute-start(f32[40,1280]{1,0:T(8,128)S(1)} %add.618), channel_id=1, source_target_pairs={{0,2},{1,0},{3,1},{5,3},{7,5},{6,7},{4,6},{2,4},{8,10},{9,8},{11,9... | collective-permute-start | bytes 614408 | tf_op jit(solution)/shard_map/ppermute | solution.py:85
  95.5 8.7 %collective-permute-start.30 = (f32[40,1280]{1,0:T(8,128)S(1)}, f32[40,1280]{1,0:T(8,128)S(1)}, u32[]{:S(2)}, u32[]{:S(2)}) collective-permute-start(f32[40,1280]{1,0:T(8,128)S(1)} %add.595), channel_id=1, source_target_pairs={{0,1},{1,3},{3,5},{5,7},{7,6},{6,4},{4,2},{2,0},{8,9},{9,11},{11,1... | collective-permute-start | bytes 614408 | tf_op jit(solution)/shard_map/ppermute | solution.py:85
  98.2 7.0 %collective-permute-start.23 = (f32[40,1280]{1,0:T(8,128)S(1)}, f32[40,1280]{1,0:T(8,128)S(1)}, u32[]{:S(2)}, u32[]{:S(2)}) collective-permute-start(f32[40,1280]{1,0:T(8,128)S(1)} %add.570), channel_id=1, source_target_pairs={{0,2},{1,0},{3,1},{5,3},{7,5},{6,7},{4,6},{2,4},{8,10},{9,8},{11,9... | collective-permute-start | bytes 614408 | tf_op jit(solution)/shard_map/ppermute | solution.py:85
  99.9 6.7 %collective-permute-start.16 = (f32[40,1280]{1,0:T(8,128)S(1)}, f32[40,1280]{1,0:T(8,128)S(1)}, u32[]{:S(2)}, u32[]{:S(2)}) collective-permute-start(f32[40,1280]{1,0:T(8,128)S(1)} %add.533), channel_id=1, source_target_pairs={{0,1},{1,3},{3,5},{5,7},{7,6},{6,4},{4,2},{2,0},{8,9},{9,11},{11,1... | collective-permute-start | bytes 614408 | tf_op jit(solution)/shard_map/ppermute | solution.py:85

commit v10 on v8

--- a/solution.py
+++ b/solution.py
@@ -100,9 +100,10 @@
     over_x = [(i, i ^ 2) for i in range(4)]
     over_core = [(i, i ^ 1) for i in range(4)]
     g_far = lax.ppermute(grad_rows, "aug", over_x)
-    g_near = lax.ppermute(grad_rows, "aug", over_core)
     h_far_relay = lax.ppermute(cols(a ^ 3), "aug", over_x)
-    h_near = lax.ppermute(cols(a ^ 1), "aug", over_core)
+    _, (g_mine, h_mine) = lax.optimization_barrier((h_far_relay, (grad_rows, cols(a ^ 1))))
+    g_near = lax.ppermute(g_mine, "aug", over_core)
+    h_near = lax.ppermute(h_mine, "aug", over_core)
     g_relay = lax.ppermute(g_far, "aug", over_core)
     h_relay = lax.ppermute(h_far_relay, "aug", over_core)
     _, second = lax.optimization_barrier((h_far_relay, cols(a ^ 2)))

time: 110 us -> 112 us (1.018)
  waiting for transfers between devices: 40.1 us -> 42.6 us
    ppermute x1, waiting for transfers between devices: 0.01 us -> 2.74 us  [exchange_four(): h_far = lax.ppermute(second, 'aug', over_x)]
    ppermute x1, starting transfers between devices: 2.57 us -> 0.03 us  [exchange_four(): g_far = lax.ppermute(grad_rows, 'aug', over_x)]
    ppermute x1, starting transfers between devices: 0.5 us -> 2.94 us  [exchange_four(): h_far_relay = lax.ppermute(cols(a ^ 3), 'aug', over_x)]
    ppermute x1, waiting for transfers between devices: 5.7 us -> 3.95 us  [exchange_four(): h_far_relay = lax.ppermute(cols(a ^ 3), 'aug', over_x)]
    ppermute x1, waiting for transfers between devices: 0.01 us -> 1.3 us  [exchange_four(): g_far = lax.ppermute(grad_rows, 'aug', over_x)]
  transfers between devices with their start and end apart: 38 -> 38, of which waited for: 17 -> 19; matrix products, arithmetic and copies ran while one was open for 20% -> 18% of each run, Pallas kernels for 0% -> 0%
where the time goes in v10:
time: 112 us
  waiting for transfers between devices  42.6 us (38%)
  starting transfers between devices  37.2 us (33%)
  matrix products  21.2 us (19%)
  between operations  4.85 us (4%)
  other arithmetic  3.38 us (3%)
  local copies, waits for them, and re-layouts  2.42 us (2%)
    ppermute x28, waiting for transfers between devices, ring_reduce_scatter(): lax.ppermute(v, 'dp', right if step < 0 else left)  34.6 us
    ppermute x28, starting transfers between devices, ring_reduce_scatter(): lax.ppermute(v, 'dp', right if step < 0 else left)  29.7 us
    dot_general x4, matrix products, per_device(): term = jnp.dot(h_piece.T, g_piece, preferred_element_type=jnp.float32)  13.5 us
    dot_general x4, matrix products, project_back(): lax.dot_general(rows, down_weight, (((1,), (1,)), ((), ())), preferred_el...  7.72 us
    ppermute x1, waiting for transfers between devices, exchange_four(): h_far_relay = lax.ppermute(cols(a ^ 3), 'aug', over_x)  3.95 us
    ppermute x1, starting transfers between devices, exchange_four(): h_far_relay = lax.ppermute(cols(a ^ 3), 'aug', over_x)  2.94 us
    ppermute x1, waiting for transfers between devices, exchange_four(): h_far = lax.ppermute(second, 'aug', over_x)  2.74 us
    dynamic_slice x1, local copies, waits for them, and re-layouts, cols(): return lax.dynamic_slice_in_dim(h_rows, b * sw, sw, axis=1)  2.29 us
  transfers between devices with their start and end apart: 38, of which 19 were waited for; matrix products, arithmetic and copies ran while one was open for 18% of the time, Pallas kernels for 0%

profile of v10, /device:TPU:0, one launch (start us, length us, event | category | flops | bytes accessed | tf_op | source)
XLA Modules:
  0.0 111.7 jit_solution(8656836678055203226)
XLA Ops:
  0.7 2.3 %dynamic-slice_bitcast_fusion = (bf16[128,1280]{1,0:T(8,128)(2,1)}, bf16[128,1280]{1,0:T(8,128)(2,1)}, bf16[128,1280]{1,0:T(8,128)(2,1)}) fusion(bf16[1,1,128,5120]{3,2,1,0:T(8,128)(2,1)} %param.6, s32[]{:T(128)S(6)} %select_n.691, s32[]{:T(128)S(6)} %select_n.689, s32[]{:T(128)S(6)} %select_n.690), kind=kLoop, calls=%fused_computation.21 | loop fusion | bytes 1966092 | tf_op jit(solution)/shard_map/dynamic_slice | solution.py:98
  3.0 2.9 %collective-permute-start = (bf16[128,1280]{1,0:T(8,128)(2,1)}, bf16[128,1280]{1,0:T(8,128)(2,1)}, u32[]{:S(2)}, u32[]{:S(2)}) collective-permute-start(bf16[128,1280]{1,0:T(8,128)(2,1)} %get-tuple-element.77), channel_id=1, source_target_pairs={{0,16},{8,24},{16,0},{24,8},{1,17},{9,25},{17,1},{25,9},{2,18},{10... | collective-permute-start | bytes 983048 | tf_op jit(solution)/shard_map/ppermute | solution.py:103
  5.9 4.9 %fusion.6 = f32[1280,1280]{1,0:T(8,128)} fusion(bf16[1,1,128,5120]{3,2,1,0:T(8,128)(2,1)} %param.6, s32[]{:T(128)S(6)} %select_n.688, bf16[1,1,128,1280]{3,2,1,0:T(8,128)(2,1)} %param.7), kind=kOutput, calls=%fused_computation.19 | convolution fusion | flops 419430400 | bytes 7208964 | tf_op jit(solution)/shard_map/dot_general | solution.py:152
  10.8 4.0 %collective-permute-done = bf16[128,1280]{1,0:T(8,128)(2,1)} collective-permute-done((bf16[128,1280]{1,0:T(8,128)(2,1)}, bf16[128,1280]{1,0:T(8,128)(2,1)}, u32[]{:S(2)}, u32[]{:S(2)}) %collective-permute-start) | collective-permute-done | bytes 327712 | tf_op jit(solution)/shard_map/ppermute | solution.py:103
  14.8 0.5 collective-permute-start.2
  15.3 0.1 broadcast_in_dim.2
  15.4 2.2 %fusion.4 = bf16[512,1280]{1,0:T(8,128)(2,1)S(1)} fusion(bf16[512,1280]{1,0:T(8,128)(2,1)S(1)} %broadcast_in_dim.2, s32[]{:T(128)S(6)} %select_n.859, bf16[1280,1280]{1,0:T(8,128)(2,1)S(1)} %copy-done, bf16[1,1,128,1280]{3,2,1,0:T(8,128)(2,1)} %param.7), kind=kOutput, calls=%fused_computation.12 | convolution fusion | flops 419594240 | bytes 3932164 | tf_op jit(solution)/shard_map/dot_general | solution.py:17
  17.5 2.1 %collective-permute-start.3 = (bf16[128,1280]{1,0:T(8,128)(2,1)}, bf16[128,1280]{1,0:T(8,128)(2,1)S(1)}, u32[]{:S(2)}, u32[]{:S(2)}) collective-permute-start(bf16[128,1280]{1,0:T(8,128)(2,1)} %get-tuple-element.39), channel_id=1, source_target_pairs={{0,16},{8,24},{16,0},{24,8},{1,17},{9,25},{17,1},{25,9},{2,18},{10... | collective-permute-start | bytes 983048 | tf_op jit(solution)/shard_map/ppermute | solution.py:110
  19.7 1.3 %collective-permute-done.4 = bf16[128,1280]{1,0:T(8,128)(2,1)} collective-permute-done((bf16[128,1280]{1,0:T(8,128)(2,1)}, bf16[128,1280]{1,0:T(8,128)(2,1)}, u32[]{:S(2)}, u32[]{:S(2)}) %collective-permute-start.4) | collective-permute-done | bytes 327712 | tf_op jit(solution)/shard_map/ppermute | solution.py:102
  21.0 4.1 %convolution_add_fusion.2 = f32[1280,1280]{1,0:T(8,128)S(1)} fusion(f32[1280,1280]{1,0:T(8,128)} %fusion.6, bf16[128,1280]{1,0:T(8,128)(2,1)} %collective-permute-done.1, bf16[128,1280]{1,0:T(8,128)(2,1)} %collective-permute-done.2), kind=kOutput, calls=%fused_computation.2 | convolution fusion | flops 421068800 | bytes 13762560 | tf_op jit(solution)/shard_map/dot_general | solution.py:152
  25.1 2.7 %collective-permute-done.3 = bf16[128,1280]{1,0:T(8,128)(2,1)S(1)} collective-permute-done((bf16[128,1280]{1,0:T(8,128)(2,1)}, bf16[128,1280]{1,0:T(8,128)(2,1)S(1)}, u32[]{:S(2)}, u32[]{:S(2)}) %collective-permute-start.3) | collective-permute-done | bytes 327712 | tf_op jit(solution)/shard_map/ppermute | solution.py:110
  27.9 2.0 %convolution_add_fusion.1 = f32[1280,1280]{1,0:T(8,128)S(1)} fusion(f32[1280,1280]{1,0:T(8,128)S(1)} %convolution_add_fusion.2, bf16[128,1280]{1,0:T(8,128)(2,1)S(1)} %collective-permute-done.3, bf16[128,1280]{1,0:T(8,128)(2,1)} %collective-permute-done.4), kind=kOutput, calls=%fused_computation.1 | convolution fusion | flops 421068800 | bytes 13762560 | tf_op jit(solution)/shard_map/dot_general | solution.py:152
  29.9 2.5 %multiply_reduce_fusion = (f32[]{:T(128)}, f32[1280,1280]{1,0:T(8,128)S(1)}) fusion(f32[1280,1280]{1,0:T(8,128)S(1)} %convolution_add_fusion.1, bf16[128,1280]{1,0:T(8,128)(2,1)S(1)} %collective-permute-done.5, bf16[128,1280]{1,0:T(8,128)(2,1)S(1)} %collective-permute-done.6), kind=kOutput, calls=%fused_computation.4 | convolution fusion | flops 425984000 | bytes 13762564 | tf_op jit(solution)/shard_map/dot_general | solution.py:152
  32.4 1.7 %collective-permute-start.8 = (f32[1]{0:T(128)}, f32[1]{0:T(128)}, u32[]{:S(2)}, u32[]{:S(2)}) collective-permute-start(f32[1]{0:T(128)} %bitcast.5), channel_id=1, source_target_pairs={{0,16},{8,24},{16,0},{24,8},{1,17},{9,25},{17,1},{25,9},{2,18},{10... | collective-permute-start | bytes 20 | tf_op jit(solution)/shard_map/ppermute | solution.py:123
  34.2 0.1 collective-permute-start.9
  34.3 2.2 %fusion.3 = bf16[512,1280]{1,0:T(8,128)(2,1)S(1)} fusion(bf16[512,1280]{1,0:T(8,128)(2,1)S(1)} %fusion.4, s32[]{:T(128)S(6)} %select_n.860, bf16[128,1280]{1,0:T(8,128)(2,1)} %collective-permute-done.2, bf16[1280,1280]{1,0:T(8,128)(2,1)S(1)} %copy-done), kind=kOutput, calls=%fused_computation.10 | convolution fusion | flops 419594240 | bytes 3932164 | tf_op jit(solution)/shard_map/dot_general | solution.py:17
  36.5 2.2 %fusion.2 = bf16[512,1280]{1,0:T(8,128)(2,1)S(1)} fusion(bf16[512,1280]{1,0:T(8,128)(2,1)S(1)} %fusion.3, s32[]{:T(128)S(6)} %select_n.861, bf16[128,1280]{1,0:T(8,128)(2,1)} %collective-permute-done.4, bf16[1280,1280]{1,0:T(8,128)(2,1)S(1)} %copy-done), kind=kOutput, calls=%fused_computation.8 | convolution fusion | flops 419594240 | bytes 3932164 | tf_op jit(solution)/shard_map/dot_general | solution.py:17
  38.7 1.2 %fusion.1 = bf16[512,1280]{1,0:T(8,128)(2,1)S(1)} fusion(bf16[512,1280]{1,0:T(8,128)(2,1)S(1)} %fusion.2, s32[]{:T(128)S(6)} %select_n.862, bf16[128,1280]{1,0:T(8,128)(2,1)S(1)} %collective-permute-done.6, bf16[1280,1280]{1,0:T(8,128)(2,1)S(1)} %copy-done), kind=kOutput, calls=%fused_computation.6 | convolution fusion | flops 419594240 | bytes 3932164 | tf_op jit(solution)/shard_map/dot_general | solution.py:17
  42.5 0.1 dynamic-slice_multiply_fusion.3
  42.6 1.8 %collective-permute-start.31 = (f32[40,1280]{1,0:T(8,128)S(1)}, f32[40,1280]{1,0:T(8,128)S(1)}, u32[]{:S(2)}, u32[]{:S(2)}) collective-permute-start(f32[40,1280]{1,0:T(8,128)S(1)} %get-tuple-element.73), channel_id=1, source_target_pairs={{0,2},{1,0},{3,1},{5,3},{7,5},{6,7},{4,6},{2,4},{8,10},{9,8},{11,9... | collective-permute-start | bytes 614408 | tf_op jit(solution)/shard_map/ppermute | solution.py:82
  44.4 0.2 collective-permute-start.24
  44.7 1.8 %collective-permute-start.17 = (f32[40,1280]{1,0:T(8,128)S(1)}, f32[40,1280]{1,0:T(8,128)S(1)}, u32[]{:S(2)}, u32[]{:S(2)}) collective-permute-start(f32[40,1280]{1,0:T(8,128)S(1)} %get-tuple-element.75), channel_id=1, source_target_pairs={{0,2},{1,0},{3,1},{5,3},{7,5},{6,7},{4,6},{2,4},{8,10},{9,8},{11,9... | collective-permute-start | bytes 614408 | tf_op jit(solution)/shard_map/ppermute | solution.py:82
  46.5 0.2 collective-permute-start.10
  46.8 3.7 %collective-permute-done.31 = f32[40,1280]{1,0:T(8,128)S(1)} collective-permute-done((f32[40,1280]{1,0:T(8,128)S(1)}, f32[40,1280]{1,0:T(8,128)S(1)}, u32[]{:S(2)}, u32[]{:S(2)}) %collective-permute-start.31) | collective-permute-done | bytes 204832 | tf_op jit(solution)/shard_map/ppermute | solution.py:82
  50.6 1.9 %collective-permute-start.32 = (f32[40,1280]{1,0:T(8,128)S(1)}, f32[40,1280]{1,0:T(8,128)S(1)}, u32[]{:S(2)}, u32[]{:S(2)}) collective-permute-start(f32[40,1280]{1,0:T(8,128)S(1)} %add.603), channel_id=1, source_target_pairs={{0,2},{1,0},{3,1},{5,3},{7,5},{6,7},{4,6},{2,4},{8,10},{9,8},{11,9... | collective-permute-start | bytes 614408 | tf_op jit(solution)/shard_map/ppermute | solution.py:82
  52.5 0.3 collective-permute-start.25
  52.7 2.2 %collective-permute-done.17 = f32[40,1280]{1,0:T(8,128)S(1)} collective-permute-done((f32[40,1280]{1,0:T(8,128)S(1)}, f32[40,1280]{1,0:T(8,128)S(1)}, u32[]{:S(2)}, u32[]{:S(2)}) %collective-permute-start.17) | collective-permute-done | bytes 204832 | tf_op jit(solution)/shard_map/ppermute | solution.py:82
  55.0 1.9 %collective-permute-start.18 = (f32[40,1280]{1,0:T(8,128)S(1)}, f32[40,1280]{1,0:T(8,128)S(1)}, u32[]{:S(2)}, u32[]{:S(2)}) collective-permute-start(f32[40,1280]{1,0:T(8,128)S(1)} %add.545), channel_id=1, source_target_pairs={{0,2},{1,0},{3,1},{5,3},{7,5},{6,7},{4,6},{2,4},{8,10},{9,8},{11,9... | collective-permute-start | bytes 614408 | tf_op jit(solution)/shard_map/ppermute | solution.py:82
  56.8 0.3 collective-permute-start.11
  57.2 2.1 %collective-permute-done.32 = f32[40,1280]{1,0:T(8,128)S(1)} collective-permute-done((f32[40,1280]{1,0:T(8,128)S(1)}, f32[40,1280]{1,0:T(8,128)S(1)}, u32[]{:S(2)}, u32[]{:S(2)}) %collective-permute-start.32) | collective-permute-done | bytes 204832 | tf_op jit(solution)/shard_map/ppermute | solution.py:82
  59.4 1.9 %collective-permute-start.33 = (f32[40,1280]{1,0:T(8,128)S(1)}, f32[40,1280]{1,0:T(8,128)S(1)}, u32[]{:S(2)}, u32[]{:S(2)}) collective-permute-start(f32[40,1280]{1,0:T(8,128)S(1)} %add.606), channel_id=1, source_target_pairs={{0,2},{1,0},{3,1},{5,3},{7,5},{6,7},{4,6},{2,4},{8,10},{9,8},{11,9... | collective-permute-start | bytes 614408 | tf_op jit(solution)/shard_map/ppermute | solution.py:82
  61.2 0.3 collective-permute-start.26
  61.5 2.2 %collective-permute-done.18 = f32[40,1280]{1,0:T(8,128)S(1)} collective-permute-done((f32[40,1280]{1,0:T(8,128)S(1)}, f32[40,1280]{1,0:T(8,128)S(1)}, u32[]{:S(2)}, u32[]{:S(2)}) %collective-permute-start.18) | collective-permute-done | bytes 204832 | tf_op jit(solution)/shard_map/ppermute | solution.py:82
  63.7 1.9 %collective-permute-start.19 = (f32[40,1280]{1,0:T(8,128)S(1)}, f32[40,1280]{1,0:T(8,128)S(1)}, u32[]{:S(2)}, u32[]{:S(2)}) collective-permute-start(f32[40,1280]{1,0:T(8,128)S(1)} %add.550), channel_id=1, source_target_pairs={{0,2},{1,0},{3,1},{5,3},{7,5},{6,7},{4,6},{2,4},{8,10},{9,8},{11,9... | collective-permute-start | bytes 614408 | tf_op jit(solution)/shard_map/ppermute | solution.py:82
  65.6 0.3 collective-permute-start.12
  66.0 2.1 %collective-permute-done.33 = f32[40,1280]{1,0:T(8,128)S(1)} collective-permute-done((f32[40,1280]{1,0:T(8,128)S(1)}, f32[40,1280]{1,0:T(8,128)S(1)}, u32[]{:S(2)}, u32[]{:S(2)}) %collective-permute-start.33) | collective-permute-done | bytes 204832 | tf_op jit(solution)/shard_map/ppermute | solution.py:82
  68.1 1.9 %collective-permute-start.34 = (f32[40,1280]{1,0:T(8,128)S(1)}, f32[40,1280]{1,0:T(8,128)S(1)}, u32[]{:S(2)}, u32[]{:S(2)}) collective-permute-start(f32[40,1280]{1,0:T(8,128)S(1)} %add.609), channel_id=1, source_target_pairs={{0,2},{1,0},{3,1},{5,3},{7,5},{6,7},{4,6},{2,4},{8,10},{9,8},{11,9... | collective-permute-start | bytes 614408 | tf_op jit(solution)/shard_map/ppermute | solution.py:82
  70.0 0.3 collective-permute-start.27
  70.3 2.2 %collective-permute-done.19 = f32[40,1280]{1,0:T(8,128)S(1)} collective-permute-done((f32[40,1280]{1,0:T(8,128)S(1)}, f32[40,1280]{1,0:T(8,128)S(1)}, u32[]{:S(2)}, u32[]{:S(2)}) %collective-permute-start.19) | collective-permute-done | bytes 204832 | tf_op jit(solution)/shard_map/ppermute | solution.py:82
  72.5 1.9 %collective-permute-start.20 = (f32[40,1280]{1,0:T(8,128)S(1)}, f32[40,1280]{1,0:T(8,128)S(1)}, u32[]{:S(2)}, u32[]{:S(2)}) collective-permute-start(f32[40,1280]{1,0:T(8,128)S(1)} %add.555), channel_id=1, source_target_pairs={{0,2},{1,0},{3,1},{5,3},{7,5},{6,7},{4,6},{2,4},{8,10},{9,8},{11,9... | collective-permute-start | bytes 614408 | tf_op jit(solution)/shard_map/ppermute | solution.py:82
  74.4 0.3 collective-permute-start.13
  74.8 2.1 %collective-permute-done.34 = f32[40,1280]{1,0:T(8,128)S(1)} collective-permute-done((f32[40,1280]{1,0:T(8,128)S(1)}, f32[40,1280]{1,0:T(8,128)S(1)}, u32[]{:S(2)}, u32[]{:S(2)}) %collective-permute-start.34) | collective-permute-done | bytes 204832 | tf_op jit(solution)/shard_map/ppermute | solution.py:82
  76.9 1.9 %collective-permute-start.35 = (f32[40,1280]{1,0:T(8,128)S(1)}, f32[40,1280]{1,0:T(8,128)S(1)}, u32[]{:S(2)}, u32[]{:S(2)}) collective-permute-start(f32[40,1280]{1,0:T(8,128)S(1)} %add.612), channel_id=1, source_target_pairs={{0,2},{1,0},{3,1},{5,3},{7,5},{6,7},{4,6},{2,4},{8,10},{9,8},{11,9... | collective-permute-start | bytes 614408 | tf_op jit(solution)/shard_map/ppermute | solution.py:82
  78.8 0.3 collective-permute-start.28
  79.1 2.2 %collective-permute-done.20 = f32[40,1280]{1,0:T(8,128)S(1)} collective-permute-done((f32[40,1280]{1,0:T(8,128)S(1)}, f32[40,1280]{1,0:T(8,128)S(1)}, u32[]{:S(2)}, u32[]{:S(2)}) %collective-permute-start.20) | collective-permute-done | bytes 204832 | tf_op jit(solution)/shard_map/ppermute | solution.py:82
  81.3 1.9 %collective-permute-start.21 = (f32[40,1280]{1,0:T(8,128)S(1)}, f32[40,1280]{1,0:T(8,128)S(1)}, u32[]{:S(2)}, u32[]{:S(2)}) collective-permute-start(f32[40,1280]{1,0:T(8,128)S(1)} %add.560), channel_id=1, source_target_pairs={{0,2},{1,0},{3,1},{5,3},{7,5},{6,7},{4,6},{2,4},{8,10},{9,8},{11,9... | collective-permute-start | bytes 614408 | tf_op jit(solution)/shard_map/ppermute | solution.py:82
  83.2 0.3 collective-permute-start.14
  83.6 2.0 %collective-permute-done.35 = f32[40,1280]{1,0:T(8,128)S(1)} collective-permute-done((f32[40,1280]{1,0:T(8,128)S(1)}, f32[40,1280]{1,0:T(8,128)S(1)}, u32[]{:S(2)}, u32[]{:S(2)}) %collective-permute-start.35) | collective-permute-done | bytes 204832 | tf_op jit(solution)/shard_map/ppermute | solution.py:82
  85.7 1.9 %collective-permute-start.36 = (f32[40,1280]{1,0:T(8,128)S(1)}, f32[40,1280]{1,0:T(8,128)S(1)}, u32[]{:S(2)}, u32[]{:S(2)}) collective-permute-start(f32[40,1280]{1,0:T(8,128)S(1)} %add.615), channel_id=1, source_target_pairs={{0,2},{1,0},{3,1},{5,3},{7,5},{6,7},{4,6},{2,4},{8,10},{9,8},{11,9... | collective-permute-start | bytes 614408 | tf_op jit(solution)/shard_map/ppermute | solution.py:82
  87.6 0.3 collective-permute-start.29
  87.8 2.2 %collective-permute-done.21 = f32[40,1280]{1,0:T(8,128)S(1)} collective-permute-done((f32[40,1280]{1,0:T(8,128)S(1)}, f32[40,1280]{1,0:T(8,128)S(1)}, u32[]{:S(2)}, u32[]{:S(2)}) %collective-permute-start.21) | collective-permute-done | bytes 204832 | tf_op jit(solution)/shard_map/ppermute | solution.py:82
  90.1 1.9 %collective-permute-start.22 = (f32[40,1280]{1,0:T(8,128)S(1)}, f32[40,1280]{1,0:T(8,128)S(1)}, u32[]{:S(2)}, u32[]{:S(2)}) collective-permute-start(f32[40,1280]{1,0:T(8,128)S(1)} %add.565), channel_id=1, source_target_pairs={{0,2},{1,0},{3,1},{5,3},{7,5},{6,7},{4,6},{2,4},{8,10},{9,8},{11,9... | collective-permute-start | bytes 614408 | tf_op jit(solution)/shard_map/ppermute | solution.py:82
  92.0 0.3 collective-permute-start.15
  92.4 2.1 %collective-permute-done.36 = f32[40,1280]{1,0:T(8,128)S(1)} collective-permute-done((f32[40,1280]{1,0:T(8,128)S(1)}, f32[40,1280]{1,0:T(8,128)S(1)}, u32[]{:S(2)}, u32[]{:S(2)}) %collective-permute-start.36) | collective-permute-done | bytes 204832 | tf_op jit(solution)/shard_map/ppermute | solution.py:82
  94.5 1.9 %collective-permute-start.37 = (f32[40,1280]{1,0:T(8,128)S(1)}, f32[40,1280]{1,0:T(8,128)S(1)}, u32[]{:S(2)}, u32[]{:S(2)}) collective-permute-start(f32[40,1280]{1,0:T(8,128)S(1)} %add.618), channel_id=1, source_target_pairs={{0,2},{1,0},{3,1},{5,3},{7,5},{6,7},{4,6},{2,4},{8,10},{9,8},{11,9... | collective-permute-start | bytes 614408 | tf_op jit(solution)/shard_map/ppermute | solution.py:82
  96.3 0.3 collective-permute-start.30
  96.6 2.2 %collective-permute-done.22 = f32[40,1280]{1,0:T(8,128)S(1)} collective-permute-done((f32[40,1280]{1,0:T(8,128)S(1)}, f32[40,1280]{1,0:T(8,128)S(1)}, u32[]{:S(2)}, u32[]{:S(2)}) %collective-permute-start.22) | collective-permute-done | bytes 204832 | tf_op jit(solution)/shard_map/ppermute | solution.py:82
  98.9 1.9 %collective-permute-start.23 = (f32[40,1280]{1,0:T(8,128)S(1)}, f32[40,1280]{1,0:T(8,128)S(1)}, u32[]{:S(2)}, u32[]{:S(2)}) collective-permute-start(f32[40,1280]{1,0:T(8,128)S(1)} %add.570), channel_id=1, source_target_pairs={{0,2},{1,0},{3,1},{5,3},{7,5},{6,7},{4,6},{2,4},{8,10},{9,8},{11,9... | collective-permute-start | bytes 614408 | tf_op jit(solution)/shard_map/ppermute | solution.py:82
  100.7 0.3 collective-permute-start.16
  101.1 2.1 %collective-permute-done.37 = f32[40,1280]{1,0:T(8,128)S(1)} collective-permute-done((f32[40,1280]{1,0:T(8,128)S(1)}, f32[40,1280]{1,0:T(8,128)S(1)}, u32[]{:S(2)}, u32[]{:S(2)}) %collective-permute-start.37) | collective-permute-done | bytes 204832 | tf_op jit(solution)/shard_map/ppermute | solution.py:82
  103.2 1.8 %collective-permute-done.30 = f32[40,1280]{1,0:T(8,128)S(1)} collective-permute-done((f32[40,1280]{1,0:T(8,128)S(1)}, f32[40,1280]{1,0:T(8,128)S(1)}, u32[]{:S(2)}, u32[]{:S(2)}) %collective-permute-start.30) | collective-permute-done | bytes 204832 | tf_op jit(solution)/shard_map/ppermute | solution.py:82
  105.1 1.9 %collective-permute-done.23 = f32[40,1280]{1,0:T(8,128)S(1)} collective-permute-done((f32[40,1280]{1,0:T(8,128)S(1)}, f32[40,1280]{1,0:T(8,128)S(1)}, u32[]{:S(2)}, u32[]{:S(2)}) %collective-permute-start.23) | collective-permute-done | bytes 204832 | tf_op jit(solution)/shard_map/ppermute | solution.py:82
  107.0 1.5 %collective-permute-done.16 = f32[40,1280]{1,0:T(8,128)S(1)} collective-permute-done((f32[40,1280]{1,0:T(8,128)S(1)}, f32[40,1280]{1,0:T(8,128)S(1)}, u32[]{:S(2)}, u32[]{:S(2)}) %collective-permute-start.16) | collective-permute-done | bytes 204832 | tf_op jit(solution)/shard_map/ppermute | solution.py:82
  108.5 2.0 %add_divide_fusion = (f32[160,1280]{1,0:T(8,128)}, f32[160,1280]{1,0:T(8,128)}, f32[160,1280]{1,0:T(8,128)}, f32[160,1280]{1,0:T(8,128)}) fusion(f32[160,1280]{1,0:T(8,128)S(1)} %copy-done.2, f32[160,1280]{1,0:T(8,128)S(1)} %copy-done.3, f32[160,1280]{1,0:T(8,128)S(1)} %copy-done.4, f32[40,1280]{1,0:T(8,128)S(1)} %add.621, f32[40,1280]{1,0:T(8,128)S(1)} %add.598, ...), kind=kLoop, calls=%fused_computation.16 | loop fusion | flops 3481600 | bytes 6553600 | tf_op jit(solution)/shard_map/div | solution.py:190
  (90 shorter events, 1.4 us)
Async XLA Ops:
  0.6 14.7 %copy-start = (bf16[1280,1280]{1,0:T(8,128)(2,1)S(1)}, bf16[1280,1280]{1,0:T(8,128)(2,1)}, u32[]{:S(2)}) copy-start(bf16[1280,1280]{1,0:T(8,128)(2,1)} %param.8) | copy-start | bytes 9830404
  3.0 11.8 %collective-permute-start = (bf16[128,1280]{1,0:T(8,128)(2,1)}, bf16[128,1280]{1,0:T(8,128)(2,1)}, u32[]{:S(2)}, u32[]{:S(2)}) collective-permute-start(bf16[128,1280]{1,0:T(8,128)(2,1)} %get-tuple-element.77), channel_id=1, source_target_pairs={{0,16},{8,24},{16,0},{24,8},{1,17},{9,25},{17,1},{25,9},{2,18},{10... | collective-permute-start | bytes 983048 | tf_op jit(solution)/shard_map/ppermute | solution.py:103
  5.9 15.1 %collective-permute-start.4 = (bf16[128,1280]{1,0:T(8,128)(2,1)}, bf16[128,1280]{1,0:T(8,128)(2,1)}, u32[]{:S(2)}, u32[]{:S(2)}) collective-permute-start(bf16[128,1280]{1,0:T(8,128)(2,1)} %bitcast.1), channel_id=1, source_target_pairs={{0,16},{8,24},{16,0},{24,8},{1,17},{9,25},{17,1},{25,9},{2,18},{10... | collective-permute-start | bytes 983048 | tf_op jit(solution)/shard_map/ppermute | solution.py:102
  14.8 6.2 %collective-permute-start.1 = (bf16[128,1280]{1,0:T(8,128)(2,1)}, bf16[128,1280]{1,0:T(8,128)(2,1)}, u32[]{:S(2)}, u32[]{:S(2)}) collective-permute-start(bf16[128,1280]{1,0:T(8,128)(2,1)} %get-tuple-element.37), channel_id=1, source_target_pairs={{0,8},{8,0},{16,24},{24,16},{1,9},{9,1},{17,25},{25,17},{2,10},{10... | collective-permute-start | bytes 983048 | tf_op jit(solution)/shard_map/ppermute | solution.py:106
  14.8 6.2 %collective-permute-start.2 = (bf16[128,1280]{1,0:T(8,128)(2,1)}, bf16[128,1280]{1,0:T(8,128)(2,1)}, u32[]{:S(2)}, u32[]{:S(2)}) collective-permute-start(bf16[128,1280]{1,0:T(8,128)(2,1)} %bitcast.1), channel_id=1, source_target_pairs={{0,8},{8,0},{16,24},{24,16},{1,9},{9,1},{17,25},{25,17},{2,10},{10... | collective-permute-start | bytes 983048 | tf_op jit(solution)/shard_map/ppermute | solution.py:105
  17.5 10.3 %collective-permute-start.3 = (bf16[128,1280]{1,0:T(8,128)(2,1)}, bf16[128,1280]{1,0:T(8,128)(2,1)S(1)}, u32[]{:S(2)}, u32[]{:S(2)}) collective-permute-start(bf16[128,1280]{1,0:T(8,128)(2,1)} %get-tuple-element.39), channel_id=1, source_target_pairs={{0,16},{8,24},{16,0},{24,8},{1,17},{9,25},{17,1},{25,9},{2,18},{10... | collective-permute-start | bytes 983048 | tf_op jit(solution)/shard_map/ppermute | solution.py:110
  19.7 10.2 %collective-permute-start.5 = (bf16[128,1280]{1,0:T(8,128)(2,1)}, bf16[128,1280]{1,0:T(8,128)(2,1)S(1)}, u32[]{:S(2)}, u32[]{:S(2)}) collective-permute-start(bf16[128,1280]{1,0:T(8,128)(2,1)} %collective-permute-done), channel_id=1, source_target_pairs={{0,8},{8,0},{16,24},{24,16},{1,9},{9,1},{17,25},{25,17},{2,10},{10... | collective-permute-start | bytes 983048 | tf_op jit(solution)/shard_map/ppermute | solution.py:108
  21.0 8.9 %collective-permute-start.6 = (bf16[128,1280]{1,0:T(8,128)(2,1)}, bf16[128,1280]{1,0:T(8,128)(2,1)S(1)}, u32[]{:S(2)}, u32[]{:S(2)}) collective-permute-start(bf16[128,1280]{1,0:T(8,128)(2,1)} %collective-permute-done.4), channel_id=1, source_target_pairs={{0,8},{8,0},{16,24},{24,16},{1,9},{9,1},{17,25},{25,17},{2,10},{10... | collective-permute-start | bytes 983048 | tf_op jit(solution)/shard_map/ppermute | solution.py:107
  32.4 7.5 %collective-permute-start.7 = (f32[1]{0:T(128)}, f32[1]{0:T(128)}, u32[]{:S(2)}, u32[]{:S(2)}) collective-permute-start(f32[1]{0:T(128)} %bitcast.5), channel_id=1, source_target_pairs={{0,8},{8,0},{16,24},{24,16},{1,9},{9,1},{17,25},{25,17},{2,10},{10... | collective-permute-start | bytes 20 | tf_op jit(solution)/shard_map/ppermute | solution.py:123
  32.4 8.8 %collective-permute-start.8 = (f32[1]{0:T(128)}, f32[1]{0:T(128)}, u32[]{:S(2)}, u32[]{:S(2)}) collective-permute-start(f32[1]{0:T(128)} %bitcast.5), channel_id=1, source_target_pairs={{0,16},{8,24},{16,0},{24,8},{1,17},{9,25},{17,1},{25,9},{2,18},{10... | collective-permute-start | bytes 20 | tf_op jit(solution)/shard_map/ppermute | solution.py:123
  34.2 7.0 %collective-permute-start.9 = (f32[1]{0:T(128)}, f32[1]{0:T(128)}, u32[]{:S(2)}, u32[]{:S(2)}) collective-permute-start(f32[1]{0:T(128)} %bitcast.5), channel_id=1, source_target_pairs={{0,24},{8,16},{16,8},{24,0},{1,25},{9,17},{17,9},{25,1},{2,26},{10... | collective-permute-start | bytes 20 | tf_op jit(solution)/shard_map/ppermute | solution.py:123
  39.9 32.7 %copy-start.1 = (bf16[512,1280]{1,0:T(8,128)(2,1)}, bf16[512,1280]{1,0:T(8,128)(2,1)S(1)}, u32[]{:S(2)}) copy-start(bf16[512,1280]{1,0:T(8,128)(2,1)S(1)} %fusion.1) | copy-start | bytes 3932164
  42.6 8.0 %collective-permute-start.31 = (f32[40,1280]{1,0:T(8,128)S(1)}, f32[40,1280]{1,0:T(8,128)S(1)}, u32[]{:S(2)}, u32[]{:S(2)}) collective-permute-start(f32[40,1280]{1,0:T(8,128)S(1)} %get-tuple-element.73), channel_id=1, source_target_pairs={{0,2},{1,0},{3,1},{5,3},{7,5},{6,7},{4,6},{2,4},{8,10},{9,8},{11,9... | collective-permute-start | bytes 614408 | tf_op jit(solution)/shard_map/ppermute | solution.py:82
  44.4 8.0 %collective-permute-start.24 = (f32[40,1280]{1,0:T(8,128)S(1)}, f32[40,1280]{1,0:T(8,128)S(1)}, u32[]{:S(2)}, u32[]{:S(2)}) collective-permute-start(f32[40,1280]{1,0:T(8,128)S(1)} %get-tuple-element.74), channel_id=1, source_target_pairs={{0,1},{1,3},{3,5},{5,7},{7,6},{6,4},{4,2},{2,0},{8,9},{9,11},{11,1... | collective-permute-start | bytes 614408 | tf_op jit(solution)/shard_map/ppermute | solution.py:82
  44.7 10.3 %collective-permute-start.17 = (f32[40,1280]{1,0:T(8,128)S(1)}, f32[40,1280]{1,0:T(8,128)S(1)}, u32[]{:S(2)}, u32[]{:S(2)}) collective-permute-start(f32[40,1280]{1,0:T(8,128)S(1)} %get-tuple-element.75), channel_id=1, source_target_pairs={{0,2},{1,0},{3,1},{5,3},{7,5},{6,7},{4,6},{2,4},{8,10},{9,8},{11,9... | collective-permute-start | bytes 614408 | tf_op jit(solution)/shard_map/ppermute | solution.py:82
  46.5 10.3 %collective-permute-start.10 = (f32[40,1280]{1,0:T(8,128)S(1)}, f32[40,1280]{1,0:T(8,128)S(1)}, u32[]{:S(2)}, u32[]{:S(2)}) collective-permute-start(f32[40,1280]{1,0:T(8,128)S(1)} %get-tuple-element.72), channel_id=1, source_target_pairs={{0,1},{1,3},{3,5},{5,7},{7,6},{6,4},{4,2},{2,0},{8,9},{9,11},{11,1... | collective-permute-start | bytes 614408 | tf_op jit(solution)/shard_map/ppermute | solution.py:82
  50.6 8.8 %collective-permute-start.32 = (f32[40,1280]{1,0:T(8,128)S(1)}, f32[40,1280]{1,0:T(8,128)S(1)}, u32[]{:S(2)}, u32[]{:S(2)}) collective-permute-start(f32[40,1280]{1,0:T(8,128)S(1)} %add.603), channel_id=1, source_target_pairs={{0,2},{1,0},{3,1},{5,3},{7,5},{6,7},{4,6},{2,4},{8,10},{9,8},{11,9... | collective-permute-start | bytes 614408 | tf_op jit(solution)/shard_map/ppermute | solution.py:82
  52.5 8.8 %collective-permute-start.25 = (f32[40,1280]{1,0:T(8,128)S(1)}, f32[40,1280]{1,0:T(8,128)S(1)}, u32[]{:S(2)}, u32[]{:S(2)}) collective-permute-start(f32[40,1280]{1,0:T(8,128)S(1)} %add.580), channel_id=1, source_target_pairs={{0,1},{1,3},{3,5},{5,7},{7,6},{6,4},{4,2},{2,0},{8,9},{9,11},{11,1... | collective-permute-start | bytes 614408 | tf_op jit(solution)/shard_map/ppermute | solution.py:82
  55.0 8.8 %collective-permute-start.18 = (f32[40,1280]{1,0:T(8,128)S(1)}, f32[40,1280]{1,0:T(8,128)S(1)}, u32[]{:S(2)}, u32[]{:S(2)}) collective-permute-start(f32[40,1280]{1,0:T(8,128)S(1)} %add.545), channel_id=1, source_target_pairs={{0,2},{1,0},{3,1},{5,3},{7,5},{6,7},{4,6},{2,4},{8,10},{9,8},{11,9... | collective-permute-start | bytes 614408 | tf_op jit(solution)/shard_map/ppermute | solution.py:82
  56.8 8.8 %collective-permute-start.11 = (f32[40,1280]{1,0:T(8,128)S(1)}, f32[40,1280]{1,0:T(8,128)S(1)}, u32[]{:S(2)}, u32[]{:S(2)}) collective-permute-start(f32[40,1280]{1,0:T(8,128)S(1)} %add.518), channel_id=1, source_target_pairs={{0,1},{1,3},{3,5},{5,7},{7,6},{6,4},{4,2},{2,0},{8,9},{9,11},{11,1... | collective-permute-start | bytes 614408 | tf_op jit(solution)/shard_map/ppermute | solution.py:82
  59.4 8.8 %collective-permute-start.33 = (f32[40,1280]{1,0:T(8,128)S(1)}, f32[40,1280]{1,0:T(8,128)S(1)}, u32[]{:S(2)}, u32[]{:S(2)}) collective-permute-start(f32[40,1280]{1,0:T(8,128)S(1)} %add.606), channel_id=1, source_target_pairs={{0,2},{1,0},{3,1},{5,3},{7,5},{6,7},{4,6},{2,4},{8,10},{9,8},{11,9... | collective-permute-start | bytes 614408 | tf_op jit(solution)/shard_map/ppermute | solution.py:82
  61.2 8.8 %collective-permute-start.26 = (f32[40,1280]{1,0:T(8,128)S(1)}, f32[40,1280]{1,0:T(8,128)S(1)}, u32[]{:S(2)}, u32[]{:S(2)}) collective-permute-start(f32[40,1280]{1,0:T(8,128)S(1)} %add.583), channel_id=1, source_target_pairs={{0,1},{1,3},{3,5},{5,7},{7,6},{6,4},{4,2},{2,0},{8,9},{9,11},{11,1... | collective-permute-start | bytes 614408 | tf_op jit(solution)/shard_map/ppermute | solution.py:82
  63.7 8.8 %collective-permute-start.19 = (f32[40,1280]{1,0:T(8,128)S(1)}, f32[40,1280]{1,0:T(8,128)S(1)}, u32[]{:S(2)}, u32[]{:S(2)}) collective-permute-start(f32[40,1280]{1,0:T(8,128)S(1)} %add.550), channel_id=1, source_target_pairs={{0,2},{1,0},{3,1},{5,3},{7,5},{6,7},{4,6},{2,4},{8,10},{9,8},{11,9... | collective-permute-start | bytes 614408 | tf_op jit(solution)/shard_map/ppermute | solution.py:82
  65.6 8.8 %collective-permute-start.12 = (f32[40,1280]{1,0:T(8,128)S(1)}, f32[40,1280]{1,0:T(8,128)S(1)}, u32[]{:S(2)}, u32[]{:S(2)}) collective-permute-start(f32[40,1280]{1,0:T(8,128)S(1)} %add.521), channel_id=1, source_target_pairs={{0,1},{1,3},{3,5},{5,7},{7,6},{6,4},{4,2},{2,0},{8,9},{9,11},{11,1... | collective-permute-start | bytes 614408 | tf_op jit(solution)/shard_map/ppermute | solution.py:82
  68.1 8.8 %collective-permute-start.34 = (f32[40,1280]{1,0:T(8,128)S(1)}, f32[40,1280]{1,0:T(8,128)S(1)}, u32[]{:S(2)}, u32[]{:S(2)}) collective-permute-start(f32[40,1280]{1,0:T(8,128)S(1)} %add.609), channel_id=1, source_target_pairs={{0,2},{1,0},{3,1},{5,3},{7,5},{6,7},{4,6},{2,4},{8,10},{9,8},{11,9... | collective-permute-start | bytes 614408 | tf_op jit(solution)/shard_map/ppermute | solution.py:82
  70.0 8.8 %collective-permute-start.27 = (f32[40,1280]{1,0:T(8,128)S(1)}, f32[40,1280]{1,0:T(8,128)S(1)}, u32[]{:S(2)}, u32[]{:S(2)}) collective-permute-start(f32[40,1280]{1,0:T(8,128)S(1)} %add.586), channel_id=1, source_target_pairs={{0,1},{1,3},{3,5},{5,7},{7,6},{6,4},{4,2},{2,0},{8,9},{9,11},{11,1... | collective-permute-start | bytes 614408 | tf_op jit(solution)/shard_map/ppermute | solution.py:82
  72.5 8.7 %collective-permute-start.20 = (f32[40,1280]{1,0:T(8,128)S(1)}, f32[40,1280]{1,0:T(8,128)S(1)}, u32[]{:S(2)}, u32[]{:S(2)}) collective-permute-start(f32[40,1280]{1,0:T(8,128)S(1)} %add.555), channel_id=1, source_target_pairs={{0,2},{1,0},{3,1},{5,3},{7,5},{6,7},{4,6},{2,4},{8,10},{9,8},{11,9... | collective-permute-start | bytes 614408 | tf_op jit(solution)/shard_map/ppermute | solution.py:82
  74.4 8.8 %collective-permute-start.13 = (f32[40,1280]{1,0:T(8,128)S(1)}, f32[40,1280]{1,0:T(8,128)S(1)}, u32[]{:S(2)}, u32[]{:S(2)}) collective-permute-start(f32[40,1280]{1,0:T(8,128)S(1)} %add.524), channel_id=1, source_target_pairs={{0,1},{1,3},{3,5},{5,7},{7,6},{6,4},{4,2},{2,0},{8,9},{9,11},{11,1... | collective-permute-start | bytes 614408 | tf_op jit(solution)/shard_map/ppermute | solution.py:82
  76.9 8.8 %collective-permute-start.35 = (f32[40,1280]{1,0:T(8,128)S(1)}, f32[40,1280]{1,0:T(8,128)S(1)}, u32[]{:S(2)}, u32[]{:S(2)}) collective-permute-start(f32[40,1280]{1,0:T(8,128)S(1)} %add.612), channel_id=1, source_target_pairs={{0,2},{1,0},{3,1},{5,3},{7,5},{6,7},{4,6},{2,4},{8,10},{9,8},{11,9... | collective-permute-start | bytes 614408 | tf_op jit(solution)/shard_map/ppermute | solution.py:82
  78.8 8.8 %collective-permute-start.28 = (f32[40,1280]{1,0:T(8,128)S(1)}, f32[40,1280]{1,0:T(8,128)S(1)}, u32[]{:S(2)}, u32[]{:S(2)}) collective-permute-start(f32[40,1280]{1,0:T(8,128)S(1)} %add.589), channel_id=1, source_target_pairs={{0,1},{1,3},{3,5},{5,7},{7,6},{6,4},{4,2},{2,0},{8,9},{9,11},{11,1... | collective-permute-start | bytes 614408 | tf_op jit(solution)/shard_map/ppermute | solution.py:82
  81.3 27.2 %copy-start.2 = (f32[160,1280]{1,0:T(8,128)S(1)}, f32[160,1280]{1,0:T(8,128)}, u32[]{:S(2)}) copy-start(f32[160,1280]{1,0:T(8,128)} %param.11) | copy-start | bytes 2457604
  81.3 27.2 %copy-start.3 = (f32[160,1280]{1,0:T(8,128)S(1)}, f32[160,1280]{1,0:T(8,128)}, u32[]{:S(2)}) copy-start(f32[160,1280]{1,0:T(8,128)} %param.10) | copy-start | bytes 2457604
  81.3 27.2 %copy-start.4 = (f32[160,1280]{1,0:T(8,128)S(1)}, f32[160,1280]{1,0:T(8,128)}, u32[]{:S(2)}) copy-start(f32[160,1280]{1,0:T(8,128)} %param.9) | copy-start | bytes 2457604
  81.3 8.7 %collective-permute-start.21 = (f32[40,1280]{1,0:T(8,128)S(1)}, f32[40,1280]{1,0:T(8,128)S(1)}, u32[]{:S(2)}, u32[]{:S(2)}) collective-permute-start(f32[40,1280]{1,0:T(8,128)S(1)} %add.560), channel_id=1, source_target_pairs={{0,2},{1,0},{3,1},{5,3},{7,5},{6,7},{4,6},{2,4},{8,10},{9,8},{11,9... | collective-permute-start | bytes 614408 | tf_op jit(solution)/shard_map/ppermute | solution.py:82
  83.2 8.7 %collective-permute-start.14 = (f32[40,1280]{1,0:T(8,128)S(1)}, f32[40,1280]{1,0:T(8,128)S(1)}, u32[]{:S(2)}, u32[]{:S(2)}) collective-permute-start(f32[40,1280]{1,0:T(8,128)S(1)} %add.527), channel_id=1, source_target_pairs={{0,1},{1,3},{3,5},{5,7},{7,6},{6,4},{4,2},{2,0},{8,9},{9,11},{11,1... | collective-permute-start | bytes 614408 | tf_op jit(solution)/shard_map/ppermute | solution.py:82
  85.7 8.8 %collective-permute-start.36 = (f32[40,1280]{1,0:T(8,128)S(1)}, f32[40,1280]{1,0:T(8,128)S(1)}, u32[]{:S(2)}, u32[]{:S(2)}) collective-permute-start(f32[40,1280]{1,0:T(8,128)S(1)} %add.615), channel_id=1, source_target_pairs={{0,2},{1,0},{3,1},{5,3},{7,5},{6,7},{4,6},{2,4},{8,10},{9,8},{11,9... | collective-permute-start | bytes 614408 | tf_op jit(solution)/shard_map/ppermute | solution.py:82
  87.6 8.8 %collective-permute-start.29 = (f32[40,1280]{1,0:T(8,128)S(1)}, f32[40,1280]{1,0:T(8,128)S(1)}, u32[]{:S(2)}, u32[]{:S(2)}) collective-permute-start(f32[40,1280]{1,0:T(8,128)S(1)} %add.592), channel_id=1, source_target_pairs={{0,1},{1,3},{3,5},{5,7},{7,6},{6,4},{4,2},{2,0},{8,9},{9,11},{11,1... | collective-permute-start | bytes 614408 | tf_op jit(solution)/shard_map/ppermute | solution.py:82
  90.1 8.8 %collective-permute-start.22 = (f32[40,1280]{1,0:T(8,128)S(1)}, f32[40,1280]{1,0:T(8,128)S(1)}, u32[]{:S(2)}, u32[]{:S(2)}) collective-permute-start(f32[40,1280]{1,0:T(8,128)S(1)} %add.565), channel_id=1, source_target_pairs={{0,2},{1,0},{3,1},{5,3},{7,5},{6,7},{4,6},{2,4},{8,10},{9,8},{11,9... | collective-permute-start | bytes 614408 | tf_op jit(solution)/shard_map/ppermute | solution.py:82
  92.0 8.8 %collective-permute-start.15 = (f32[40,1280]{1,0:T(8,128)S(1)}, f32[40,1280]{1,0:T(8,128)S(1)}, u32[]{:S(2)}, u32[]{:S(2)}) collective-permute-start(f32[40,1280]{1,0:T(8,128)S(1)} %add.530), channel_id=1, source_target_pairs={{0,1},{1,3},{3,5},{5,7},{7,6},{6,4},{4,2},{2,0},{8,9},{9,11},{11,1... | collective-permute-start | bytes 614408 | tf_op jit(solution)/shard_map/ppermute | solution.py:82
  94.5 8.8 %collective-permute-start.37 = (f32[40,1280]{1,0:T(8,128)S(1)}, f32[40,1280]{1,0:T(8,128)S(1)}, u32[]{:S(2)}, u32[]{:S(2)}) collective-permute-start(f32[40,1280]{1,0:T(8,128)S(1)} %add.618), channel_id=1, source_target_pairs={{0,2},{1,0},{3,1},{5,3},{7,5},{6,7},{4,6},{2,4},{8,10},{9,8},{11,9... | collective-permute-start | bytes 614408 | tf_op jit(solution)/shard_map/ppermute | solution.py:82
  96.3 8.7 %collective-permute-start.30 = (f32[40,1280]{1,0:T(8,128)S(1)}, f32[40,1280]{1,0:T(8,128)S(1)}, u32[]{:S(2)}, u32[]{:S(2)}) collective-permute-start(f32[40,1280]{1,0:T(8,128)S(1)} %add.595), channel_id=1, source_target_pairs={{0,1},{1,3},{3,5},{5,7},{7,6},{6,4},{4,2},{2,0},{8,9},{9,11},{11,1... | collective-permute-start | bytes 614408 | tf_op jit(solution)/shard_map/ppermute | solution.py:82
  98.9 8.1 %collective-permute-start.23 = (f32[40,1280]{1,0:T(8,128)S(1)}, f32[40,1280]{1,0:T(8,128)S(1)}, u32[]{:S(2)}, u32[]{:S(2)}) collective-permute-start(f32[40,1280]{1,0:T(8,128)S(1)} %add.570), channel_id=1, source_target_pairs={{0,2},{1,0},{3,1},{5,3},{7,5},{6,7},{4,6},{2,4},{8,10},{9,8},{11,9... | collective-permute-start | bytes 614408 | tf_op jit(solution)/shard_map/ppermute | solution.py:82
  100.7 7.7 %collective-permute-start.16 = (f32[40,1280]{1,0:T(8,128)S(1)}, f32[40,1280]{1,0:T(8,128)S(1)}, u32[]{:S(2)}, u32[]{:S(2)}) collective-permute-start(f32[40,1280]{1,0:T(8,128)S(1)} %add.533), channel_id=1, source_target_pairs={{0,1},{1,3},{3,5},{5,7},{7,6},{6,4},{4,2},{2,0},{8,9},{9,11},{11,1... | collective-permute-start | bytes 614408 | tf_op jit(solution)/shard_map/ppermute | solution.py:82

commit v11 on v9

--- a/solution.py
+++ b/solution.py
@@ -103,13 +103,15 @@
     over_x = [(i, i ^ 2) for i in range(4)]
     over_core = [(i, i ^ 1) for i in range(4)]
     g_far = lax.ppermute(grad_rows, "aug", over_x)
-    g_near = lax.ppermute(grad_rows, "aug", over_core)
     h_far_relay = lax.ppermute(cols(a ^ 3), "aug", over_x)
-    h_near = lax.ppermute(cols(a ^ 1), "aug", over_core)
-    g_relay = lax.ppermute(g_far, "aug", over_core)
-    h_relay = lax.ppermute(h_far_relay, "aug", over_core)
-    _, second = lax.optimization_barrier((h_far_relay, cols(a ^ 2)))
-    h_far = lax.ppermute(second, "aug", over_x)
+    h_far = lax.ppermute(cols(a ^ 2), "aug", over_x)
+    _, (g_mine, h_mine, g_fwd, h_fwd) = lax.optimization_barrier(
+        ((g_far, h_far_relay, h_far), (grad_rows, cols(a ^ 1), g_far, h_far_relay))
+    )
+    g_near = lax.ppermute(g_mine, "aug", over_core)
+    h_near = lax.ppermute(h_mine, "aug", over_core)
+    g_relay = lax.ppermute(g_fwd, "aug", over_core)
+    h_relay = lax.ppermute(h_fwd, "aug", over_core)
     return [
         (a * rows, cols(a), grad_rows),
         ((a ^ 1) * rows, h_near, g_near),

time: 110 us -> 113 us (1.027)
  waiting for transfers between devices: 46 us -> 50.5 us
  matrix products: 15.5 us -> 13.9 us
    ppermute x1, waiting for transfers between devices: 0.01 us -> 6.19 us  [exchange_four(): g_far = lax.ppermute(grad_rows, 'aug', over_x)]
    ppermute x1, waiting for transfers between devices: 10.7 us -> 7.02 us  [exchange_four(): h_far_relay = lax.ppermute(cols(a ^ 3), 'aug', over_x)]
    ppermute x5, waiting for transfers between devices: 5.07 us -> 7.36 us  [the longest x1 6.82 us: exchange_four(): h_far = lax.ppermute(cols(a ^ 2), 'aug', over_x)]
  transfers between devices with their start and end apart: 38 -> 38, of which waited for: 18 -> 21; matrix products, arithmetic and copies ran while one was open for 15% -> 9% of each run, Pallas kernels for 0% -> 0%
where the time goes in v11:
time: 113 us
  waiting for transfers between devices  50.5 us (45%)
  starting transfers between devices  37.8 us (33%)
  matrix products  13.9 us (12%)
  between operations  4.86 us (4%)
  other arithmetic  3.49 us (3%)
  local copies, waits for them, and re-layouts  2.42 us (2%)
    ppermute x28, starting transfers between devices, ring_reduce_scatter(): lax.ppermute(v, 'dp', right if step < 0 else left)  29.7 us
    ppermute x28, waiting for transfers between devices, ring_reduce_scatter(): lax.ppermute(v, 'dp', right if step < 0 else left)  28.4 us
    dot_general x4, matrix products, per_device(): term = jnp.dot(h_piece.T, g_piece, preferred_element_type=jnp.float32)  8.15 us
    ppermute x1, waiting for transfers between devices, exchange_four(): h_far_relay = lax.ppermute(cols(a ^ 3), 'aug', over_x)  7.02 us
    ppermute x1, waiting for transfers between devices, exchange_four(): h_far = lax.ppermute(cols(a ^ 2), 'aug', over_x)  6.82 us
    ppermute x1, waiting for transfers between devices, exchange_four(): g_far = lax.ppermute(grad_rows, 'aug', over_x)  6.19 us
    dot_general x4, matrix products, project_back(): lax.dot_general(rows, down_weight, (((1,), (1,)), ((), ())), preferred_el...  5.78 us
    ppermute x1, starting transfers between devices, exchange_four(): h_far = lax.ppermute(cols(a ^ 2), 'aug', over_x)  2.94 us
  transfers between devices with their start and end apart: 38, of which 21 were waited for; matrix products, arithmetic and copies ran while one was open for 9% of the time, Pallas kernels for 0%

profile of v11, /device:TPU:0, one launch (start us, length us, event | category | flops | bytes accessed | tf_op | source)
XLA Modules:
  0.0 113.0 jit_solution(4114690295533403228)
XLA Ops:
  0.7 2.3 %dynamic-slice_bitcast_fusion = (bf16[128,1280]{1,0:T(8,128)(2,1)}, bf16[128,1280]{1,0:T(8,128)(2,1)}, bf16[128,1280]{1,0:T(8,128)(2,1)}) fusion(bf16[1,1,128,5120]{3,2,1,0:T(8,128)(2,1)} %param.6, s32[]{:T(128)S(6)} %select_n.691, s32[]{:T(128)S(6)} %select_n.689, s32[]{:T(128)S(6)} %select_n.690), kind=kLoop, calls=%fused_computation.21 | loop fusion | bytes 1966092 | tf_op jit(solution)/shard_map/dynamic_slice | solution.py:101
  3.0 2.9 %collective-permute-start.1 = (bf16[128,1280]{1,0:T(8,128)(2,1)}, bf16[128,1280]{1,0:T(8,128)(2,1)}, u32[]{:S(2)}, u32[]{:S(2)}) collective-permute-start(bf16[128,1280]{1,0:T(8,128)(2,1)} %get-tuple-element.87), channel_id=1, source_target_pairs={{0,16},{8,24},{16,0},{24,8},{1,17},{9,25},{17,1},{25,9},{2,18},{10... | collective-permute-start | bytes 983048 | tf_op jit(solution)/shard_map/ppermute | solution.py:107
  5.9 2.0 %collective-permute-start = (bf16[128,1280]{1,0:T(8,128)(2,1)}, bf16[128,1280]{1,0:T(8,128)(2,1)}, u32[]{:S(2)}, u32[]{:S(2)}) collective-permute-start(bf16[128,1280]{1,0:T(8,128)(2,1)} %bitcast.114), channel_id=1, source_target_pairs={{0,16},{8,24},{16,0},{24,8},{1,17},{9,25},{17,1},{25,9},{2,18},{10... | collective-permute-start | bytes 983048 | tf_op jit(solution)/shard_map/ppermute | solution.py:105
  7.9 6.8 %collective-permute-done.1 = bf16[128,1280]{1,0:T(8,128)(2,1)} collective-permute-done((bf16[128,1280]{1,0:T(8,128)(2,1)}, bf16[128,1280]{1,0:T(8,128)(2,1)}, u32[]{:S(2)}, u32[]{:S(2)}) %collective-permute-start.1) | collective-permute-done | bytes 327712 | tf_op jit(solution)/shard_map/ppermute | solution.py:107
  14.8 7.0 %collective-permute-done.2 = bf16[128,1280]{1,0:T(8,128)(2,1)} collective-permute-done((bf16[128,1280]{1,0:T(8,128)(2,1)}, bf16[128,1280]{1,0:T(8,128)(2,1)}, u32[]{:S(2)}, u32[]{:S(2)}) %collective-permute-start.2) | collective-permute-done | bytes 327712 | tf_op jit(solution)/shard_map/ppermute | solution.py:106
  21.8 6.2 %collective-permute-done = bf16[128,1280]{1,0:T(8,128)(2,1)} collective-permute-done((bf16[128,1280]{1,0:T(8,128)(2,1)}, bf16[128,1280]{1,0:T(8,128)(2,1)}, u32[]{:S(2)}, u32[]{:S(2)}) %collective-permute-start) | collective-permute-done | bytes 327712 | tf_op jit(solution)/shard_map/ppermute | solution.py:105
  28.0 0.5 collective-permute-start.5
  28.5 2.1 %fusion.7 = f32[1280,1280]{1,0:T(8,128)S(1)} fusion(bf16[1,1,128,5120]{3,2,1,0:T(8,128)(2,1)} %param.6, s32[]{:T(128)S(6)} %select_n.688, bf16[1,1,128,1280]{3,2,1,0:T(8,128)(2,1)} %param.7), kind=kOutput, calls=%fused_computation.19 | convolution fusion | flops 419430400 | bytes 7208964 | tf_op jit(solution)/shard_map/dot_general | solution.py:155
  30.7 0.5 collective-permute-start.3
  31.2 1.0 fusion.13
  32.3 0.5 collective-permute-done.3
  32.8 1.1 convolution_add_fusion.1
  33.8 3.9 %multiply_reduce_fusion = (f32[]{:T(128)}, f32[1280,1280]{1,0:T(8,128)S(1)}) fusion(f32[1280,1280]{1,0:T(8,128)S(1)} %fusion.13, f32[1280,1280]{1,0:T(8,128)S(1)} %convolution_add_fusion.1, bf16[128,1280]{1,0:T(8,128)(2,1)} %collective-permute-done.1, bf16[128,1280]{1,0:T(8,128)(2,1)} %collective-permute-done), kind=kOutput, calls=%fused_computation.4 | convolution fusion | flops 427622400 | bytes 20316164 | tf_op jit(solution)/shard_map/dot_general | solution.py:155
  37.8 1.7 %collective-permute-start.8 = (f32[1]{0:T(128)}, f32[1]{0:T(128)}, u32[]{:S(2)}, u32[]{:S(2)}) collective-permute-start(f32[1]{0:T(128)} %bitcast.5), channel_id=1, source_target_pairs={{0,16},{8,24},{16,0},{24,8},{1,17},{9,25},{17,1},{25,9},{2,18},{10... | collective-permute-start | bytes 20 | tf_op jit(solution)/shard_map/ppermute | solution.py:127
  39.5 0.4 collective-permute-start.7
  39.9 1.0 collective-permute-done.7
  42.2 0.5 collective-permute-done.9
  44.1 1.6 %collective-permute-start.10 = (f32[40,1280]{1,0:T(8,128)S(1)}, f32[40,1280]{1,0:T(8,128)S(1)}, u32[]{:S(2)}, u32[]{:S(2)}) collective-permute-start(f32[40,1280]{1,0:T(8,128)S(1)} %get-tuple-element.82), channel_id=1, source_target_pairs={{0,1},{1,3},{3,5},{5,7},{7,6},{6,4},{4,2},{2,0},{8,9},{9,11},{11,1... | collective-permute-start | bytes 614408 | tf_op jit(solution)/shard_map/ppermute | solution.py:85
  45.7 0.5 collective-permute-start.17
  46.2 1.6 %collective-permute-start.24 = (f32[40,1280]{1,0:T(8,128)S(1)}, f32[40,1280]{1,0:T(8,128)S(1)}, u32[]{:S(2)}, u32[]{:S(2)}) collective-permute-start(f32[40,1280]{1,0:T(8,128)S(1)} %get-tuple-element.84), channel_id=1, source_target_pairs={{0,1},{1,3},{3,5},{5,7},{7,6},{6,4},{4,2},{2,0},{8,9},{9,11},{11,1... | collective-permute-start | bytes 614408 | tf_op jit(solution)/shard_map/ppermute | solution.py:85
  47.7 0.5 collective-permute-start.31
  48.4 1.2 %fusion.5 = bf16[512,1280]{1,0:T(8,128)(2,1)S(1)} fusion(bf16[512,1280]{1,0:T(8,128)(2,1)S(1)} %broadcast_in_dim.2, s32[]{:T(128)S(6)} %select_n.859, bf16[128,1280]{1,0:T(8,128)(2,1)S(1)} %bitcast.116, bf16[1280,1280]{1,0:T(8,128)(2,1)S(1)} %copy-done), kind=kOutput, calls=%fused_computation.12 | convolution fusion | flops 419594240 | bytes 3932164 | tf_op jit(solution)/shard_map/dot_general | solution.py:17
  49.7 1.2 %fusion.4 = bf16[512,1280]{1,0:T(8,128)(2,1)S(1)} fusion(bf16[512,1280]{1,0:T(8,128)(2,1)S(1)} %fusion.5, s32[]{:T(128)S(6)} %select_n.860, bf16[128,1280]{1,0:T(8,128)(2,1)S(1)} %collective-permute-done.4, bf16[1280,1280]{1,0:T(8,128)(2,1)S(1)} %copy-done), kind=kOutput, calls=%fused_computation.10 | convolution fusion | flops 419594240 | bytes 3932164 | tf_op jit(solution)/shard_map/dot_general | solution.py:17
  50.9 2.2 %fusion.3 = bf16[512,1280]{1,0:T(8,128)(2,1)S(1)} fusion(bf16[512,1280]{1,0:T(8,128)(2,1)S(1)} %fusion.4, s32[]{:T(128)S(6)} %select_n.861, bf16[128,1280]{1,0:T(8,128)(2,1)} %collective-permute-done, bf16[1280,1280]{1,0:T(8,128)(2,1)S(1)} %copy-done), kind=kOutput, calls=%fused_computation.8 | convolution fusion | flops 419594240 | bytes 3932164 | tf_op jit(solution)/shard_map/dot_general | solution.py:17
  53.0 1.2 %fusion.2 = bf16[512,1280]{1,0:T(8,128)(2,1)S(1)} fusion(bf16[512,1280]{1,0:T(8,128)(2,1)S(1)} %fusion.3, s32[]{:T(128)S(6)} %select_n.862, bf16[128,1280]{1,0:T(8,128)(2,1)S(1)} %collective-permute-done.6, bf16[1280,1280]{1,0:T(8,128)(2,1)S(1)} %copy-done), kind=kOutput, calls=%fused_computation.6 | convolution fusion | flops 419594240 | bytes 3932164 | tf_op jit(solution)/shard_map/dot_general | solution.py:17
  54.3 1.6 %collective-permute-start.11 = (f32[40,1280]{1,0:T(8,128)S(1)}, f32[40,1280]{1,0:T(8,128)S(1)}, u32[]{:S(2)}, u32[]{:S(2)}) collective-permute-start(f32[40,1280]{1,0:T(8,128)S(1)} %add.518), channel_id=1, source_target_pairs={{0,1},{1,3},{3,5},{5,7},{7,6},{6,4},{4,2},{2,0},{8,9},{9,11},{11,1... | collective-permute-start | bytes 614408 | tf_op jit(solution)/shard_map/ppermute | solution.py:85
  55.9 0.5 collective-permute-start.18
  56.5 1.6 %collective-permute-start.25 = (f32[40,1280]{1,0:T(8,128)S(1)}, f32[40,1280]{1,0:T(8,128)S(1)}, u32[]{:S(2)}, u32[]{:S(2)}) collective-permute-start(f32[40,1280]{1,0:T(8,128)S(1)} %add.580), channel_id=1, source_target_pairs={{0,1},{1,3},{3,5},{5,7},{7,6},{6,4},{4,2},{2,0},{8,9},{9,11},{11,1... | collective-permute-start | bytes 614408 | tf_op jit(solution)/shard_map/ppermute | solution.py:85
  58.1 0.5 collective-permute-start.32
  58.8 3.6 %collective-permute-done.11 = f32[40,1280]{1,0:T(8,128)S(1)} collective-permute-done((f32[40,1280]{1,0:T(8,128)S(1)}, f32[40,1280]{1,0:T(8,128)S(1)}, u32[]{:S(2)}, u32[]{:S(2)}) %collective-permute-start.11) | collective-permute-done | bytes 204832 | tf_op jit(solution)/shard_map/ppermute | solution.py:85
  62.4 1.6 %collective-permute-start.12 = (f32[40,1280]{1,0:T(8,128)S(1)}, f32[40,1280]{1,0:T(8,128)S(1)}, u32[]{:S(2)}, u32[]{:S(2)}) collective-permute-start(f32[40,1280]{1,0:T(8,128)S(1)} %add.521), channel_id=1, source_target_pairs={{0,1},{1,3},{3,5},{5,7},{7,6},{6,4},{4,2},{2,0},{8,9},{9,11},{11,1... | collective-permute-start | bytes 614408 | tf_op jit(solution)/shard_map/ppermute | solution.py:85
  64.0 0.5 collective-permute-start.19
  64.6 2.2 %collective-permute-done.25 = f32[40,1280]{1,0:T(8,128)S(1)} collective-permute-done((f32[40,1280]{1,0:T(8,128)S(1)}, f32[40,1280]{1,0:T(8,128)S(1)}, u32[]{:S(2)}, u32[]{:S(2)}) %collective-permute-start.25) | collective-permute-done | bytes 204832 | tf_op jit(solution)/shard_map/ppermute | solution.py:85
  66.8 1.6 %collective-permute-start.26 = (f32[40,1280]{1,0:T(8,128)S(1)}, f32[40,1280]{1,0:T(8,128)S(1)}, u32[]{:S(2)}, u32[]{:S(2)}) collective-permute-start(f32[40,1280]{1,0:T(8,128)S(1)} %add.583), channel_id=1, source_target_pairs={{0,1},{1,3},{3,5},{5,7},{7,6},{6,4},{4,2},{2,0},{8,9},{9,11},{11,1... | collective-permute-start | bytes 614408 | tf_op jit(solution)/shard_map/ppermute | solution.py:85
  68.4 0.5 collective-permute-start.33
  69.1 2.1 %collective-permute-done.12 = f32[40,1280]{1,0:T(8,128)S(1)} collective-permute-done((f32[40,1280]{1,0:T(8,128)S(1)}, f32[40,1280]{1,0:T(8,128)S(1)}, u32[]{:S(2)}, u32[]{:S(2)}) %collective-permute-start.12) | collective-permute-done | bytes 204832 | tf_op jit(solution)/shard_map/ppermute | solution.py:85
  71.2 1.6 %collective-permute-start.13 = (f32[40,1280]{1,0:T(8,128)S(1)}, f32[40,1280]{1,0:T(8,128)S(1)}, u32[]{:S(2)}, u32[]{:S(2)}) collective-permute-start(f32[40,1280]{1,0:T(8,128)S(1)} %add.524), channel_id=1, source_target_pairs={{0,1},{1,3},{3,5},{5,7},{7,6},{6,4},{4,2},{2,0},{8,9},{9,11},{11,1... | collective-permute-start | bytes 614408 | tf_op jit(solution)/shard_map/ppermute | solution.py:85
  72.8 0.5 collective-permute-start.20
  73.3 2.2 %collective-permute-done.26 = f32[40,1280]{1,0:T(8,128)S(1)} collective-permute-done((f32[40,1280]{1,0:T(8,128)S(1)}, f32[40,1280]{1,0:T(8,128)S(1)}, u32[]{:S(2)}, u32[]{:S(2)}) %collective-permute-start.26) | collective-permute-done | bytes 204832 | tf_op jit(solution)/shard_map/ppermute | solution.py:85
  75.6 1.6 %collective-permute-start.27 = (f32[40,1280]{1,0:T(8,128)S(1)}, f32[40,1280]{1,0:T(8,128)S(1)}, u32[]{:S(2)}, u32[]{:S(2)}) collective-permute-start(f32[40,1280]{1,0:T(8,128)S(1)} %add.586), channel_id=1, source_target_pairs={{0,1},{1,3},{3,5},{5,7},{7,6},{6,4},{4,2},{2,0},{8,9},{9,11},{11,1... | collective-permute-start | bytes 614408 | tf_op jit(solution)/shard_map/ppermute | solution.py:85
  77.2 0.5 collective-permute-start.34
  77.8 2.1 %collective-permute-done.13 = f32[40,1280]{1,0:T(8,128)S(1)} collective-permute-done((f32[40,1280]{1,0:T(8,128)S(1)}, f32[40,1280]{1,0:T(8,128)S(1)}, u32[]{:S(2)}, u32[]{:S(2)}) %collective-permute-start.13) | collective-permute-done | bytes 204832 | tf_op jit(solution)/shard_map/ppermute | solution.py:85
  79.9 1.6 %collective-permute-start.14 = (f32[40,1280]{1,0:T(8,128)S(1)}, f32[40,1280]{1,0:T(8,128)S(1)}, u32[]{:S(2)}, u32[]{:S(2)}) collective-permute-start(f32[40,1280]{1,0:T(8,128)S(1)} %add.527), channel_id=1, source_target_pairs={{0,1},{1,3},{3,5},{5,7},{7,6},{6,4},{4,2},{2,0},{8,9},{9,11},{11,1... | collective-permute-start | bytes 614408 | tf_op jit(solution)/shard_map/ppermute | solution.py:85
  81.6 0.5 collective-permute-start.21
  82.1 2.2 %collective-permute-done.27 = f32[40,1280]{1,0:T(8,128)S(1)} collective-permute-done((f32[40,1280]{1,0:T(8,128)S(1)}, f32[40,1280]{1,0:T(8,128)S(1)}, u32[]{:S(2)}, u32[]{:S(2)}) %collective-permute-start.27) | collective-permute-done | bytes 204832 | tf_op jit(solution)/shard_map/ppermute | solution.py:85
  84.4 1.6 %collective-permute-start.28 = (f32[40,1280]{1,0:T(8,128)S(1)}, f32[40,1280]{1,0:T(8,128)S(1)}, u32[]{:S(2)}, u32[]{:S(2)}) collective-permute-start(f32[40,1280]{1,0:T(8,128)S(1)} %add.589), channel_id=1, source_target_pairs={{0,1},{1,3},{3,5},{5,7},{7,6},{6,4},{4,2},{2,0},{8,9},{9,11},{11,1... | collective-permute-start | bytes 614408 | tf_op jit(solution)/shard_map/ppermute | solution.py:85
  86.0 0.5 collective-permute-start.35
  86.7 2.0 %collective-permute-done.14 = f32[40,1280]{1,0:T(8,128)S(1)} collective-permute-done((f32[40,1280]{1,0:T(8,128)S(1)}, f32[40,1280]{1,0:T(8,128)S(1)}, u32[]{:S(2)}, u32[]{:S(2)}) %collective-permute-start.14) | collective-permute-done | bytes 204832 | tf_op jit(solution)/shard_map/ppermute | solution.py:85
  88.7 1.6 %collective-permute-start.15 = (f32[40,1280]{1,0:T(8,128)S(1)}, f32[40,1280]{1,0:T(8,128)S(1)}, u32[]{:S(2)}, u32[]{:S(2)}) collective-permute-start(f32[40,1280]{1,0:T(8,128)S(1)} %add.530), channel_id=1, source_target_pairs={{0,1},{1,3},{3,5},{5,7},{7,6},{6,4},{4,2},{2,0},{8,9},{9,11},{11,1... | collective-permute-start | bytes 614408 | tf_op jit(solution)/shard_map/ppermute | solution.py:85
  90.4 0.5 collective-permute-start.22
  90.9 2.2 %collective-permute-done.28 = f32[40,1280]{1,0:T(8,128)S(1)} collective-permute-done((f32[40,1280]{1,0:T(8,128)S(1)}, f32[40,1280]{1,0:T(8,128)S(1)}, u32[]{:S(2)}, u32[]{:S(2)}) %collective-permute-start.28) | collective-permute-done | bytes 204832 | tf_op jit(solution)/shard_map/ppermute | solution.py:85
  93.1 1.6 %collective-permute-start.29 = (f32[40,1280]{1,0:T(8,128)S(1)}, f32[40,1280]{1,0:T(8,128)S(1)}, u32[]{:S(2)}, u32[]{:S(2)}) collective-permute-start(f32[40,1280]{1,0:T(8,128)S(1)} %add.592), channel_id=1, source_target_pairs={{0,1},{1,3},{3,5},{5,7},{7,6},{6,4},{4,2},{2,0},{8,9},{9,11},{11,1... | collective-permute-start | bytes 614408 | tf_op jit(solution)/shard_map/ppermute | solution.py:85
  94.7 0.5 collective-permute-start.36
  95.4 2.1 %collective-permute-done.15 = f32[40,1280]{1,0:T(8,128)S(1)} collective-permute-done((f32[40,1280]{1,0:T(8,128)S(1)}, f32[40,1280]{1,0:T(8,128)S(1)}, u32[]{:S(2)}, u32[]{:S(2)}) %collective-permute-start.15) | collective-permute-done | bytes 204832 | tf_op jit(solution)/shard_map/ppermute | solution.py:85
  97.5 1.6 %collective-permute-start.16 = (f32[40,1280]{1,0:T(8,128)S(1)}, f32[40,1280]{1,0:T(8,128)S(1)}, u32[]{:S(2)}, u32[]{:S(2)}) collective-permute-start(f32[40,1280]{1,0:T(8,128)S(1)} %add.533), channel_id=1, source_target_pairs={{0,1},{1,3},{3,5},{5,7},{7,6},{6,4},{4,2},{2,0},{8,9},{9,11},{11,1... | collective-permute-start | bytes 614408 | tf_op jit(solution)/shard_map/ppermute | solution.py:85
  99.1 0.5 collective-permute-start.23
  99.7 2.2 %collective-permute-done.29 = f32[40,1280]{1,0:T(8,128)S(1)} collective-permute-done((f32[40,1280]{1,0:T(8,128)S(1)}, f32[40,1280]{1,0:T(8,128)S(1)}, u32[]{:S(2)}, u32[]{:S(2)}) %collective-permute-start.29) | collective-permute-done | bytes 204832 | tf_op jit(solution)/shard_map/ppermute | solution.py:85
  101.9 1.6 %collective-permute-start.30 = (f32[40,1280]{1,0:T(8,128)S(1)}, f32[40,1280]{1,0:T(8,128)S(1)}, u32[]{:S(2)}, u32[]{:S(2)}) collective-permute-start(f32[40,1280]{1,0:T(8,128)S(1)} %add.595), channel_id=1, source_target_pairs={{0,1},{1,3},{3,5},{5,7},{7,6},{6,4},{4,2},{2,0},{8,9},{9,11},{11,1... | collective-permute-start | bytes 614408 | tf_op jit(solution)/shard_map/ppermute | solution.py:85
  103.5 0.5 collective-permute-start.37
  104.2 2.0 %collective-permute-done.16 = f32[40,1280]{1,0:T(8,128)S(1)} collective-permute-done((f32[40,1280]{1,0:T(8,128)S(1)}, f32[40,1280]{1,0:T(8,128)S(1)}, u32[]{:S(2)}, u32[]{:S(2)}) %collective-permute-start.16) | collective-permute-done | bytes 204832 | tf_op jit(solution)/shard_map/ppermute | solution.py:85
  106.2 1.4 %collective-permute-done.23 = f32[40,1280]{1,0:T(8,128)S(1)} collective-permute-done((f32[40,1280]{1,0:T(8,128)S(1)}, f32[40,1280]{1,0:T(8,128)S(1)}, u32[]{:S(2)}, u32[]{:S(2)}) %collective-permute-start.23) | collective-permute-done | bytes 204832 | tf_op jit(solution)/shard_map/ppermute | solution.py:85
  107.7 0.7 collective-permute-done.30
  108.4 1.4 %collective-permute-done.37 = f32[40,1280]{1,0:T(8,128)S(1)} collective-permute-done((f32[40,1280]{1,0:T(8,128)S(1)}, f32[40,1280]{1,0:T(8,128)S(1)}, u32[]{:S(2)}, u32[]{:S(2)}) %collective-permute-start.37) | collective-permute-done | bytes 204832 | tf_op jit(solution)/shard_map/ppermute | solution.py:85
  109.9 2.0 %add_divide_fusion = (f32[160,1280]{1,0:T(8,128)}, f32[160,1280]{1,0:T(8,128)}, f32[160,1280]{1,0:T(8,128)}, f32[160,1280]{1,0:T(8,128)}) fusion(f32[160,1280]{1,0:T(8,128)S(1)} %copy-done.3, f32[160,1280]{1,0:T(8,128)S(1)} %copy-done.4, f32[160,1280]{1,0:T(8,128)S(1)} %copy-done.5, f32[40,1280]{1,0:T(8,128)S(1)} %add.621, f32[40,1280]{1,0:T(8,128)S(1)} %add.598, ...), kind=kLoop, calls=%fused_computation.16 | loop fusion | flops 3481600 | bytes 6553600 | tf_op jit(solution)/shard_map/div | solution.py:203
  (94 shorter events, 1.8 us)
Async XLA Ops:
  0.6 47.8 %copy-start = (bf16[1280,1280]{1,0:T(8,128)(2,1)S(1)}, bf16[1280,1280]{1,0:T(8,128)(2,1)}, u32[]{:S(2)}) copy-start(bf16[1280,1280]{1,0:T(8,128)(2,1)} %param.8) | copy-start | bytes 9830404
  3.0 11.8 %collective-permute-start.1 = (bf16[128,1280]{1,0:T(8,128)(2,1)}, bf16[128,1280]{1,0:T(8,128)(2,1)}, u32[]{:S(2)}, u32[]{:S(2)}) collective-permute-start(bf16[128,1280]{1,0:T(8,128)(2,1)} %get-tuple-element.87), channel_id=1, source_target_pairs={{0,16},{8,24},{16,0},{24,8},{1,17},{9,25},{17,1},{25,9},{2,18},{10... | collective-permute-start | bytes 983048 | tf_op jit(solution)/shard_map/ppermute | solution.py:107
  5.9 15.9 %collective-permute-start.2 = (bf16[128,1280]{1,0:T(8,128)(2,1)}, bf16[128,1280]{1,0:T(8,128)(2,1)}, u32[]{:S(2)}, u32[]{:S(2)}) collective-permute-start(bf16[128,1280]{1,0:T(8,128)(2,1)} %get-tuple-element.86), channel_id=1, source_target_pairs={{0,16},{8,24},{16,0},{24,8},{1,17},{9,25},{17,1},{25,9},{2,18},{10... | collective-permute-start | bytes 983048 | tf_op jit(solution)/shard_map/ppermute | solution.py:106
  5.9 22.0 %collective-permute-start = (bf16[128,1280]{1,0:T(8,128)(2,1)}, bf16[128,1280]{1,0:T(8,128)(2,1)}, u32[]{:S(2)}, u32[]{:S(2)}) collective-permute-start(bf16[128,1280]{1,0:T(8,128)(2,1)} %bitcast.114), channel_id=1, source_target_pairs={{0,16},{8,24},{16,0},{24,8},{1,17},{9,25},{17,1},{25,9},{2,18},{10... | collective-permute-start | bytes 983048 | tf_op jit(solution)/shard_map/ppermute | solution.py:105
  7.9 22.7 %copy-start.1 = (bf16[1,1,128,1280]{3,2,1,0:T(8,128)(2,1)S(1)}, bf16[1,1,128,1280]{3,2,1,0:T(8,128)(2,1)}, u32[]{:S(2)}) copy-start(bf16[1,1,128,1280]{3,2,1,0:T(8,128)(2,1)} %param.7) | copy-start | bytes 983044
  7.9 22.8 %copy-start.6 = (bf16[128,1280]{1,0:T(8,128)(2,1)S(1)}, bf16[128,1280]{1,0:T(8,128)(2,1)}, u32[]{:S(2)}) copy-start(bf16[128,1280]{1,0:T(8,128)(2,1)} %get-tuple-element.42) | copy-start | bytes 983044
  28.0 3.2 %collective-permute-start.6 = (bf16[128,1280]{1,0:T(8,128)(2,1)}, bf16[128,1280]{1,0:T(8,128)(2,1)S(1)}, u32[]{:S(2)}, u32[]{:S(2)}) collective-permute-start(bf16[128,1280]{1,0:T(8,128)(2,1)} %collective-permute-done), channel_id=1, source_target_pairs={{0,8},{8,0},{16,24},{24,16},{1,9},{9,1},{17,25},{25,17},{2,10},{10... | collective-permute-start | bytes 983048 | tf_op jit(solution)/shard_map/ppermute | solution.py:113
  28.0 3.2 %collective-permute-start.5 = (bf16[128,1280]{1,0:T(8,128)(2,1)}, bf16[128,1280]{1,0:T(8,128)(2,1)S(1)}, u32[]{:S(2)}, u32[]{:S(2)}) collective-permute-start(bf16[128,1280]{1,0:T(8,128)(2,1)} %collective-permute-done.2), channel_id=1, source_target_pairs={{0,8},{8,0},{16,24},{24,16},{1,9},{9,1},{17,25},{25,17},{2,10},{10... | collective-permute-start | bytes 983048 | tf_op jit(solution)/shard_map/ppermute | solution.py:114
  30.6 1.7 %collective-permute-start.4 = (bf16[128,1280]{1,0:T(8,128)(2,1)S(1)}, bf16[128,1280]{1,0:T(8,128)(2,1)S(1)}, u32[]{:S(2)}, u32[]{:S(2)}) collective-permute-start(bf16[128,1280]{1,0:T(8,128)(2,1)S(1)} %bitcast.115), channel_id=1, source_target_pairs={{0,8},{8,0},{16,24},{24,16},{1,9},{9,1},{17,25},{25,17},{2,10},{10... | collective-permute-start | bytes 983048 | tf_op jit(solution)/shard_map/ppermute | solution.py:111
  30.7 2.1 %collective-permute-start.3 = (bf16[128,1280]{1,0:T(8,128)(2,1)S(1)}, bf16[128,1280]{1,0:T(8,128)(2,1)S(1)}, u32[]{:S(2)}, u32[]{:S(2)}) collective-permute-start(bf16[128,1280]{1,0:T(8,128)(2,1)S(1)} %copy-done.6), channel_id=1, source_target_pairs={{0,8},{8,0},{16,24},{24,16},{1,9},{9,1},{17,25},{25,17},{2,10},{10... | collective-permute-start | bytes 983048 | tf_op jit(solution)/shard_map/ppermute | solution.py:112
  37.8 4.4 %collective-permute-start.8 = (f32[1]{0:T(128)}, f32[1]{0:T(128)}, u32[]{:S(2)}, u32[]{:S(2)}) collective-permute-start(f32[1]{0:T(128)} %bitcast.5), channel_id=1, source_target_pairs={{0,16},{8,24},{16,0},{24,8},{1,17},{9,25},{17,1},{25,9},{2,18},{10... | collective-permute-start | bytes 20 | tf_op jit(solution)/shard_map/ppermute | solution.py:127
  39.5 3.2 %collective-permute-start.9 = (f32[1]{0:T(128)}, f32[1]{0:T(128)}, u32[]{:S(2)}, u32[]{:S(2)}) collective-permute-start(f32[1]{0:T(128)} %bitcast.5), channel_id=1, source_target_pairs={{0,24},{8,16},{16,8},{24,0},{1,25},{9,17},{17,9},{25,1},{2,26},{10... | collective-permute-start | bytes 20 | tf_op jit(solution)/shard_map/ppermute | solution.py:127
  39.5 1.4 %collective-permute-start.7 = (f32[1]{0:T(128)}, f32[1]{0:T(128)}, u32[]{:S(2)}, u32[]{:S(2)}) collective-permute-start(f32[1]{0:T(128)} %bitcast.5), channel_id=1, source_target_pairs={{0,8},{8,0},{16,24},{24,16},{1,9},{9,1},{17,25},{25,17},{2,10},{10... | collective-permute-start | bytes 20 | tf_op jit(solution)/shard_map/ppermute | solution.py:127
  44.1 10.1 %collective-permute-start.10 = (f32[40,1280]{1,0:T(8,128)S(1)}, f32[40,1280]{1,0:T(8,128)S(1)}, u32[]{:S(2)}, u32[]{:S(2)}) collective-permute-start(f32[40,1280]{1,0:T(8,128)S(1)} %get-tuple-element.82), channel_id=1, source_target_pairs={{0,1},{1,3},{3,5},{5,7},{7,6},{6,4},{4,2},{2,0},{8,9},{9,11},{11,1... | collective-permute-start | bytes 614408 | tf_op jit(solution)/shard_map/ppermute | solution.py:85
  45.7 10.2 %collective-permute-start.17 = (f32[40,1280]{1,0:T(8,128)S(1)}, f32[40,1280]{1,0:T(8,128)S(1)}, u32[]{:S(2)}, u32[]{:S(2)}) collective-permute-start(f32[40,1280]{1,0:T(8,128)S(1)} %get-tuple-element.85), channel_id=1, source_target_pairs={{0,2},{1,0},{3,1},{5,3},{7,5},{6,7},{4,6},{2,4},{8,10},{9,8},{11,9... | collective-permute-start | bytes 614408 | tf_op jit(solution)/shard_map/ppermute | solution.py:85
  46.2 10.3 %collective-permute-start.24 = (f32[40,1280]{1,0:T(8,128)S(1)}, f32[40,1280]{1,0:T(8,128)S(1)}, u32[]{:S(2)}, u32[]{:S(2)}) collective-permute-start(f32[40,1280]{1,0:T(8,128)S(1)} %get-tuple-element.84), channel_id=1, source_target_pairs={{0,1},{1,3},{3,5},{5,7},{7,6},{6,4},{4,2},{2,0},{8,9},{9,11},{11,1... | collective-permute-start | bytes 614408 | tf_op jit(solution)/shard_map/ppermute | solution.py:85
  47.7 10.3 %collective-permute-start.31 = (f32[40,1280]{1,0:T(8,128)S(1)}, f32[40,1280]{1,0:T(8,128)S(1)}, u32[]{:S(2)}, u32[]{:S(2)}) collective-permute-start(f32[40,1280]{1,0:T(8,128)S(1)} %get-tuple-element.83), channel_id=1, source_target_pairs={{0,2},{1,0},{3,1},{5,3},{7,5},{6,7},{4,6},{2,4},{8,10},{9,8},{11,9... | collective-permute-start | bytes 614408 | tf_op jit(solution)/shard_map/ppermute | solution.py:85
  54.2 27.3 %copy-start.2 = (bf16[512,1280]{1,0:T(8,128)(2,1)}, bf16[512,1280]{1,0:T(8,128)(2,1)S(1)}, u32[]{:S(2)}) copy-start(bf16[512,1280]{1,0:T(8,128)(2,1)S(1)} %fusion.2) | copy-start | bytes 3932164
  54.3 8.1 %collective-permute-start.11 = (f32[40,1280]{1,0:T(8,128)S(1)}, f32[40,1280]{1,0:T(8,128)S(1)}, u32[]{:S(2)}, u32[]{:S(2)}) collective-permute-start(f32[40,1280]{1,0:T(8,128)S(1)} %add.518), channel_id=1, source_target_pairs={{0,1},{1,3},{3,5},{5,7},{7,6},{6,4},{4,2},{2,0},{8,9},{9,11},{11,1... | collective-permute-start | bytes 614408 | tf_op jit(solution)/shard_map/ppermute | solution.py:85
  55.9 8.1 %collective-permute-start.18 = (f32[40,1280]{1,0:T(8,128)S(1)}, f32[40,1280]{1,0:T(8,128)S(1)}, u32[]{:S(2)}, u32[]{:S(2)}) collective-permute-start(f32[40,1280]{1,0:T(8,128)S(1)} %add.545), channel_id=1, source_target_pairs={{0,2},{1,0},{3,1},{5,3},{7,5},{6,7},{4,6},{2,4},{8,10},{9,8},{11,9... | collective-permute-start | bytes 614408 | tf_op jit(solution)/shard_map/ppermute | solution.py:85
  56.5 10.3 %collective-permute-start.25 = (f32[40,1280]{1,0:T(8,128)S(1)}, f32[40,1280]{1,0:T(8,128)S(1)}, u32[]{:S(2)}, u32[]{:S(2)}) collective-permute-start(f32[40,1280]{1,0:T(8,128)S(1)} %add.580), channel_id=1, source_target_pairs={{0,1},{1,3},{3,5},{5,7},{7,6},{6,4},{4,2},{2,0},{8,9},{9,11},{11,1... | collective-permute-start | bytes 614408 | tf_op jit(solution)/shard_map/ppermute | solution.py:85
  58.1 10.3 %collective-permute-start.32 = (f32[40,1280]{1,0:T(8,128)S(1)}, f32[40,1280]{1,0:T(8,128)S(1)}, u32[]{:S(2)}, u32[]{:S(2)}) collective-permute-start(f32[40,1280]{1,0:T(8,128)S(1)} %add.603), channel_id=1, source_target_pairs={{0,2},{1,0},{3,1},{5,3},{7,5},{6,7},{4,6},{2,4},{8,10},{9,8},{11,9... | collective-permute-start | bytes 614408 | tf_op jit(solution)/shard_map/ppermute | solution.py:85
  62.4 8.7 %collective-permute-start.12 = (f32[40,1280]{1,0:T(8,128)S(1)}, f32[40,1280]{1,0:T(8,128)S(1)}, u32[]{:S(2)}, u32[]{:S(2)}) collective-permute-start(f32[40,1280]{1,0:T(8,128)S(1)} %add.521), channel_id=1, source_target_pairs={{0,1},{1,3},{3,5},{5,7},{7,6},{6,4},{4,2},{2,0},{8,9},{9,11},{11,1... | collective-permute-start | bytes 614408 | tf_op jit(solution)/shard_map/ppermute | solution.py:85
  64.0 8.7 %collective-permute-start.19 = (f32[40,1280]{1,0:T(8,128)S(1)}, f32[40,1280]{1,0:T(8,128)S(1)}, u32[]{:S(2)}, u32[]{:S(2)}) collective-permute-start(f32[40,1280]{1,0:T(8,128)S(1)} %add.550), channel_id=1, source_target_pairs={{0,2},{1,0},{3,1},{5,3},{7,5},{6,7},{4,6},{2,4},{8,10},{9,8},{11,9... | collective-permute-start | bytes 614408 | tf_op jit(solution)/shard_map/ppermute | solution.py:85
  66.8 8.7 %collective-permute-start.26 = (f32[40,1280]{1,0:T(8,128)S(1)}, f32[40,1280]{1,0:T(8,128)S(1)}, u32[]{:S(2)}, u32[]{:S(2)}) collective-permute-start(f32[40,1280]{1,0:T(8,128)S(1)} %add.583), channel_id=1, source_target_pairs={{0,1},{1,3},{3,5},{5,7},{7,6},{6,4},{4,2},{2,0},{8,9},{9,11},{11,1... | collective-permute-start | bytes 614408 | tf_op jit(solution)/shard_map/ppermute | solution.py:85
  68.4 8.7 %collective-permute-start.33 = (f32[40,1280]{1,0:T(8,128)S(1)}, f32[40,1280]{1,0:T(8,128)S(1)}, u32[]{:S(2)}, u32[]{:S(2)}) collective-permute-start(f32[40,1280]{1,0:T(8,128)S(1)} %add.606), channel_id=1, source_target_pairs={{0,2},{1,0},{3,1},{5,3},{7,5},{6,7},{4,6},{2,4},{8,10},{9,8},{11,9... | collective-permute-start | bytes 614408 | tf_op jit(solution)/shard_map/ppermute | solution.py:85
  71.2 8.7 %collective-permute-start.13 = (f32[40,1280]{1,0:T(8,128)S(1)}, f32[40,1280]{1,0:T(8,128)S(1)}, u32[]{:S(2)}, u32[]{:S(2)}) collective-permute-start(f32[40,1280]{1,0:T(8,128)S(1)} %add.524), channel_id=1, source_target_pairs={{0,1},{1,3},{3,5},{5,7},{7,6},{6,4},{4,2},{2,0},{8,9},{9,11},{11,1... | collective-permute-start | bytes 614408 | tf_op jit(solution)/shard_map/ppermute | solution.py:85
  72.8 8.7 %collective-permute-start.20 = (f32[40,1280]{1,0:T(8,128)S(1)}, f32[40,1280]{1,0:T(8,128)S(1)}, u32[]{:S(2)}, u32[]{:S(2)}) collective-permute-start(f32[40,1280]{1,0:T(8,128)S(1)} %add.555), channel_id=1, source_target_pairs={{0,2},{1,0},{3,1},{5,3},{7,5},{6,7},{4,6},{2,4},{8,10},{9,8},{11,9... | collective-permute-start | bytes 614408 | tf_op jit(solution)/shard_map/ppermute | solution.py:85
  75.6 8.7 %collective-permute-start.27 = (f32[40,1280]{1,0:T(8,128)S(1)}, f32[40,1280]{1,0:T(8,128)S(1)}, u32[]{:S(2)}, u32[]{:S(2)}) collective-permute-start(f32[40,1280]{1,0:T(8,128)S(1)} %add.586), channel_id=1, source_target_pairs={{0,1},{1,3},{3,5},{5,7},{7,6},{6,4},{4,2},{2,0},{8,9},{9,11},{11,1... | collective-permute-start | bytes 614408 | tf_op jit(solution)/shard_map/ppermute | solution.py:85
  77.2 8.8 %collective-permute-start.34 = (f32[40,1280]{1,0:T(8,128)S(1)}, f32[40,1280]{1,0:T(8,128)S(1)}, u32[]{:S(2)}, u32[]{:S(2)}) collective-permute-start(f32[40,1280]{1,0:T(8,128)S(1)} %add.609), channel_id=1, source_target_pairs={{0,2},{1,0},{3,1},{5,3},{7,5},{6,7},{4,6},{2,4},{8,10},{9,8},{11,9... | collective-permute-start | bytes 614408 | tf_op jit(solution)/shard_map/ppermute | solution.py:85
  79.9 8.7 %collective-permute-start.14 = (f32[40,1280]{1,0:T(8,128)S(1)}, f32[40,1280]{1,0:T(8,128)S(1)}, u32[]{:S(2)}, u32[]{:S(2)}) collective-permute-start(f32[40,1280]{1,0:T(8,128)S(1)} %add.527), channel_id=1, source_target_pairs={{0,1},{1,3},{3,5},{5,7},{7,6},{6,4},{4,2},{2,0},{8,9},{9,11},{11,1... | collective-permute-start | bytes 614408 | tf_op jit(solution)/shard_map/ppermute | solution.py:85
  81.6 8.7 %collective-permute-start.21 = (f32[40,1280]{1,0:T(8,128)S(1)}, f32[40,1280]{1,0:T(8,128)S(1)}, u32[]{:S(2)}, u32[]{:S(2)}) collective-permute-start(f32[40,1280]{1,0:T(8,128)S(1)} %add.560), channel_id=1, source_target_pairs={{0,2},{1,0},{3,1},{5,3},{7,5},{6,7},{4,6},{2,4},{8,10},{9,8},{11,9... | collective-permute-start | bytes 614408 | tf_op jit(solution)/shard_map/ppermute | solution.py:85
  84.3 25.5 %copy-start.3 = (f32[160,1280]{1,0:T(8,128)S(1)}, f32[160,1280]{1,0:T(8,128)}, u32[]{:S(2)}) copy-start(f32[160,1280]{1,0:T(8,128)} %param.11) | copy-start | bytes 2457604
  84.3 25.5 %copy-start.4 = (f32[160,1280]{1,0:T(8,128)S(1)}, f32[160,1280]{1,0:T(8,128)}, u32[]{:S(2)}) copy-start(f32[160,1280]{1,0:T(8,128)} %param.10) | copy-start | bytes 2457604
  84.4 25.5 %copy-start.5 = (f32[160,1280]{1,0:T(8,128)S(1)}, f32[160,1280]{1,0:T(8,128)}, u32[]{:S(2)}) copy-start(f32[160,1280]{1,0:T(8,128)} %param.9) | copy-start | bytes 2457604
  84.4 8.7 %collective-permute-start.28 = (f32[40,1280]{1,0:T(8,128)S(1)}, f32[40,1280]{1,0:T(8,128)S(1)}, u32[]{:S(2)}, u32[]{:S(2)}) collective-permute-start(f32[40,1280]{1,0:T(8,128)S(1)} %add.589), channel_id=1, source_target_pairs={{0,1},{1,3},{3,5},{5,7},{7,6},{6,4},{4,2},{2,0},{8,9},{9,11},{11,1... | collective-permute-start | bytes 614408 | tf_op jit(solution)/shard_map/ppermute | solution.py:85
  86.0 8.7 %collective-permute-start.35 = (f32[40,1280]{1,0:T(8,128)S(1)}, f32[40,1280]{1,0:T(8,128)S(1)}, u32[]{:S(2)}, u32[]{:S(2)}) collective-permute-start(f32[40,1280]{1,0:T(8,128)S(1)} %add.612), channel_id=1, source_target_pairs={{0,2},{1,0},{3,1},{5,3},{7,5},{6,7},{4,6},{2,4},{8,10},{9,8},{11,9... | collective-permute-start | bytes 614408 | tf_op jit(solution)/shard_map/ppermute | solution.py:85
  88.7 8.7 %collective-permute-start.15 = (f32[40,1280]{1,0:T(8,128)S(1)}, f32[40,1280]{1,0:T(8,128)S(1)}, u32[]{:S(2)}, u32[]{:S(2)}) collective-permute-start(f32[40,1280]{1,0:T(8,128)S(1)} %add.530), channel_id=1, source_target_pairs={{0,1},{1,3},{3,5},{5,7},{7,6},{6,4},{4,2},{2,0},{8,9},{9,11},{11,1... | collective-permute-start | bytes 614408 | tf_op jit(solution)/shard_map/ppermute | solution.py:85
  90.4 8.7 %collective-permute-start.22 = (f32[40,1280]{1,0:T(8,128)S(1)}, f32[40,1280]{1,0:T(8,128)S(1)}, u32[]{:S(2)}, u32[]{:S(2)}) collective-permute-start(f32[40,1280]{1,0:T(8,128)S(1)} %add.565), channel_id=1, source_target_pairs={{0,2},{1,0},{3,1},{5,3},{7,5},{6,7},{4,6},{2,4},{8,10},{9,8},{11,9... | collective-permute-start | bytes 614408 | tf_op jit(solution)/shard_map/ppermute | solution.py:85
  93.1 8.7 %collective-permute-start.29 = (f32[40,1280]{1,0:T(8,128)S(1)}, f32[40,1280]{1,0:T(8,128)S(1)}, u32[]{:S(2)}, u32[]{:S(2)}) collective-permute-start(f32[40,1280]{1,0:T(8,128)S(1)} %add.592), channel_id=1, source_target_pairs={{0,1},{1,3},{3,5},{5,7},{7,6},{6,4},{4,2},{2,0},{8,9},{9,11},{11,1... | collective-permute-start | bytes 614408 | tf_op jit(solution)/shard_map/ppermute | solution.py:85
  94.7 8.7 %collective-permute-start.36 = (f32[40,1280]{1,0:T(8,128)S(1)}, f32[40,1280]{1,0:T(8,128)S(1)}, u32[]{:S(2)}, u32[]{:S(2)}) collective-permute-start(f32[40,1280]{1,0:T(8,128)S(1)} %add.615), channel_id=1, source_target_pairs={{0,2},{1,0},{3,1},{5,3},{7,5},{6,7},{4,6},{2,4},{8,10},{9,8},{11,9... | collective-permute-start | bytes 614408 | tf_op jit(solution)/shard_map/ppermute | solution.py:85
  97.5 8.7 %collective-permute-start.16 = (f32[40,1280]{1,0:T(8,128)S(1)}, f32[40,1280]{1,0:T(8,128)S(1)}, u32[]{:S(2)}, u32[]{:S(2)}) collective-permute-start(f32[40,1280]{1,0:T(8,128)S(1)} %add.533), channel_id=1, source_target_pairs={{0,1},{1,3},{3,5},{5,7},{7,6},{6,4},{4,2},{2,0},{8,9},{9,11},{11,1... | collective-permute-start | bytes 614408 | tf_op jit(solution)/shard_map/ppermute | solution.py:85
  99.1 8.5 %collective-permute-start.23 = (f32[40,1280]{1,0:T(8,128)S(1)}, f32[40,1280]{1,0:T(8,128)S(1)}, u32[]{:S(2)}, u32[]{:S(2)}) collective-permute-start(f32[40,1280]{1,0:T(8,128)S(1)} %add.570), channel_id=1, source_target_pairs={{0,2},{1,0},{3,1},{5,3},{7,5},{6,7},{4,6},{2,4},{8,10},{9,8},{11,9... | collective-permute-start | bytes 614408 | tf_op jit(solution)/shard_map/ppermute | solution.py:85
  101.9 6.5 %collective-permute-start.30 = (f32[40,1280]{1,0:T(8,128)S(1)}, f32[40,1280]{1,0:T(8,128)S(1)}, u32[]{:S(2)}, u32[]{:S(2)}) collective-permute-start(f32[40,1280]{1,0:T(8,128)S(1)} %add.595), channel_id=1, source_target_pairs={{0,1},{1,3},{3,5},{5,7},{7,6},{6,4},{4,2},{2,0},{8,9},{9,11},{11,1... | collective-permute-start | bytes 614408 | tf_op jit(solution)/shard_map/ppermute | solution.py:85
  103.5 6.3 %collective-permute-start.37 = (f32[40,1280]{1,0:T(8,128)S(1)}, f32[40,1280]{1,0:T(8,128)S(1)}, u32[]{:S(2)}, u32[]{:S(2)}) collective-permute-start(f32[40,1280]{1,0:T(8,128)S(1)} %add.618), channel_id=1, source_target_pairs={{0,2},{1,0},{3,1},{5,3},{7,5},{6,7},{4,6},{2,4},{8,10},{9,8},{11,9... | collective-permute-start | bytes 614408 | tf_op jit(solution)/shard_map/ppermute | solution.py:85

commit v12 on v9

--- a/solution.py
+++ b/solution.py
@@ -103,13 +103,14 @@
     over_x = [(i, i ^ 2) for i in range(4)]
     over_core = [(i, i ^ 1) for i in range(4)]
     g_far = lax.ppermute(grad_rows, "aug", over_x)
-    g_near = lax.ppermute(grad_rows, "aug", over_core)
     h_far_relay = lax.ppermute(cols(a ^ 3), "aug", over_x)
-    h_near = lax.ppermute(cols(a ^ 1), "aug", over_core)
+    _, second = lax.optimization_barrier(((g_far, h_far_relay), cols(a ^ 2)))
+    h_far = lax.ppermute(second, "aug", over_x)
     g_relay = lax.ppermute(g_far, "aug", over_core)
     h_relay = lax.ppermute(h_far_relay, "aug", over_core)
-    _, second = lax.optimization_barrier((h_far_relay, cols(a ^ 2)))
-    h_far = lax.ppermute(second, "aug", over_x)
+    _, (g_mine, h_mine) = lax.optimization_barrier((h_far, (grad_rows, cols(a ^ 1))))
+    g_near = lax.ppermute(g_mine, "aug", over_core)
+    h_near = lax.ppermute(h_mine, "aug", over_core)
     return [
         (a * rows, cols(a), grad_rows),
         ((a ^ 1) * rows, h_near, g_near),

time: 110 us -> 113 us (1.027)
  waiting for transfers between devices: 46 us -> 50.4 us
  matrix products: 15.5 us -> 13.5 us
    ppermute x1, waiting for transfers between devices: 0.01 us -> 6.59 us  [exchange_four(): g_far = lax.ppermute(grad_rows, 'aug', over_x)]
    ppermute x1, waiting for transfers between devices: 10.7 us -> 6.09 us  [exchange_four(): h_far_relay = lax.ppermute(cols(a ^ 3), 'aug', over_x)]
    ppermute x1, waiting for transfers between devices: 5.06 us -> 7.47 us  [exchange_four(): h_far = lax.ppermute(second, 'aug', over_x)]
  transfers between devices with their start and end apart: 38 -> 38, of which waited for: 18 -> 19; matrix products, arithmetic and copies ran while one was open for 15% -> 13% of each run, Pallas kernels for 0% -> 0%
where the time goes in v12:
time: 113 us
  waiting for transfers between devices  50.4 us (45%)
  starting transfers between devices  37.6 us (33%)
  matrix products  13.5 us (12%)
  between operations  4.88 us (4%)
  other arithmetic  3.46 us (3%)
  local copies, waits for them, and re-layouts  2.92 us (3%)
    ppermute x28, starting transfers between devices, ring_reduce_scatter(): lax.ppermute(v, 'dp', right if step < 0 else left)  29.7 us
    ppermute x28, waiting for transfers between devices, ring_reduce_scatter(): lax.ppermute(v, 'dp', right if step < 0 else left)  28.8 us
    dot_general x4, matrix products, per_device(): term = jnp.dot(h_piece.T, g_piece, preferred_element_type=jnp.float32)  7.77 us
    ppermute x1, waiting for transfers between devices, exchange_four(): h_far = lax.ppermute(second, 'aug', over_x)  7.47 us
    ppermute x1, waiting for transfers between devices, exchange_four(): g_far = lax.ppermute(grad_rows, 'aug', over_x)  6.59 us
    ppermute x1, waiting for transfers between devices, exchange_four(): h_far_relay = lax.ppermute(cols(a ^ 3), 'aug', over_x)  6.09 us
    dot_general x4, matrix products, project_back(): lax.dot_general(rows, down_weight, (((1,), (1,)), ((), ())), preferred_el...  5.77 us
    ppermute x1, starting transfers between devices, exchange_four(): g_far = lax.ppermute(grad_rows, 'aug', over_x)  3 us
  transfers between devices with their start and end apart: 38, of which 19 were waited for; matrix products, arithmetic and copies ran while one was open for 13% of the time, Pallas kernels for 0%

profile of v12, /device:TPU:0, one launch (start us, length us, event | category | flops | bytes accessed | tf_op | source)
XLA Modules:
  0.0 112.7 jit_solution(10490582500577026648)
XLA Ops:
  0.6 3.0 %collective-permute-start = (bf16[128,1280]{1,0:T(8,128)(2,1)}, bf16[128,1280]{1,0:T(8,128)(2,1)}, u32[]{:S(2)}, u32[]{:S(2)}) collective-permute-start(bf16[128,1280]{1,0:T(8,128)(2,1)} %bitcast.114), channel_id=1, source_target_pairs={{0,16},{8,24},{16,0},{24,8},{1,17},{9,25},{17,1},{25,9},{2,18},{10... | collective-permute-start | bytes 983048 | tf_op jit(solution)/shard_map/ppermute | solution.py:105
  3.7 2.1 %dynamic-slice_bitcast_fusion = (bf16[128,1280]{1,0:T(8,128)(2,1)}, bf16[128,1280]{1,0:T(8,128)(2,1)S(1)}, bf16[128,1280]{1,0:T(8,128)(2,1)}) fusion(bf16[1,1,128,5120]{3,2,1,0:T(8,128)(2,1)} %param.6, s32[]{:T(128)S(6)} %select_n.691, s32[]{:T(128)S(6)} %select_n.689, s32[]{:T(128)S(6)} %select_n.690), kind=kLoop, calls=%fused_computation.21 | loop fusion | bytes 1966092 | tf_op jit(solution)/shard_map/dynamic_slice | solution.py:101
  5.9 6.6 %collective-permute-done = bf16[128,1280]{1,0:T(8,128)(2,1)} collective-permute-done((bf16[128,1280]{1,0:T(8,128)(2,1)}, bf16[128,1280]{1,0:T(8,128)(2,1)}, u32[]{:S(2)}, u32[]{:S(2)}) %collective-permute-start) | collective-permute-done | bytes 327712 | tf_op jit(solution)/shard_map/ppermute | solution.py:105
  12.5 6.1 %collective-permute-done.1 = bf16[128,1280]{1,0:T(8,128)(2,1)S(1)} collective-permute-done((bf16[128,1280]{1,0:T(8,128)(2,1)S(1)}, bf16[128,1280]{1,0:T(8,128)(2,1)S(1)}, u32[]{:S(2)}, u32[]{:S(2)}) %collective-permute-start.1) | collective-permute-done | bytes 327712 | tf_op jit(solution)/shard_map/ppermute | solution.py:106
  18.6 0.7 copy-done.6
  19.3 1.7 %collective-permute-start.2 = (bf16[128,1280]{1,0:T(8,128)(2,1)}, bf16[128,1280]{1,0:T(8,128)(2,1)}, u32[]{:S(2)}, u32[]{:S(2)}) collective-permute-start(bf16[128,1280]{1,0:T(8,128)(2,1)} %get-tuple-element.41), channel_id=1, source_target_pairs={{0,16},{8,24},{16,0},{24,8},{1,17},{9,25},{17,1},{25,9},{2,18},{10... | collective-permute-start | bytes 983048 | tf_op jit(solution)/shard_map/ppermute | solution.py:108
  21.1 7.5 %collective-permute-done.2 = bf16[128,1280]{1,0:T(8,128)(2,1)} collective-permute-done((bf16[128,1280]{1,0:T(8,128)(2,1)}, bf16[128,1280]{1,0:T(8,128)(2,1)}, u32[]{:S(2)}, u32[]{:S(2)}) %collective-permute-start.2) | collective-permute-done | bytes 327712 | tf_op jit(solution)/shard_map/ppermute | solution.py:108
  28.5 0.5 collective-permute-start.4
  29.0 2.1 %fusion.6 = f32[1280,1280]{1,0:T(8,128)S(1)} fusion(bf16[1,1,128,5120]{3,2,1,0:T(8,128)(2,1)} %param.6, s32[]{:T(128)S(6)} %select_n.688, bf16[1,1,128,1280]{3,2,1,0:T(8,128)(2,1)} %param.7), kind=kOutput, calls=%fused_computation.19 | convolution fusion | flops 419430400 | bytes 7208964 | tf_op jit(solution)/shard_map/dot_general | solution.py:154
  31.2 0.5 collective-permute-start.6
  31.8 1.0 convolution_add_fusion.2
  32.8 2.1 %convolution_add_fusion.1 = f32[1280,1280]{1,0:T(8,128)S(1)} fusion(f32[1280,1280]{1,0:T(8,128)S(1)} %convolution_add_fusion.2, bf16[128,1280]{1,0:T(8,128)(2,1)} %collective-permute-done.2, bf16[128,1280]{1,0:T(8,128)(2,1)} %collective-permute-done), kind=kOutput, calls=%fused_computation.1 | convolution fusion | flops 421068800 | bytes 13762560 | tf_op jit(solution)/shard_map/dot_general | solution.py:154
  35.0 2.5 %multiply_reduce_fusion = (f32[]{:T(128)}, f32[1280,1280]{1,0:T(8,128)S(1)}) fusion(f32[1280,1280]{1,0:T(8,128)S(1)} %convolution_add_fusion.1, bf16[128,1280]{1,0:T(8,128)(2,1)S(1)} %collective-permute-done.5, bf16[128,1280]{1,0:T(8,128)(2,1)S(1)} %collective-permute-done.6), kind=kOutput, calls=%fused_computation.4 | convolution fusion | flops 425984000 | bytes 13762564 | tf_op jit(solution)/shard_map/dot_general | solution.py:154
  37.5 1.4 %collective-permute-start.8 = (f32[1]{0:T(128)}, f32[1]{0:T(128)}, u32[]{:S(2)}, u32[]{:S(2)}) collective-permute-start(f32[1]{0:T(128)} %bitcast.5), channel_id=1, source_target_pairs={{0,16},{8,24},{16,0},{24,8},{1,17},{9,25},{17,1},{25,9},{2,18},{10... | collective-permute-start | bytes 20 | tf_op jit(solution)/shard_map/ppermute | solution.py:126
  39.0 0.4 collective-permute-start.9
  40.6 0.6 collective-permute-done.8
  41.2 0.8 collective-permute-done.9
  43.5 1.6 %collective-permute-start.31 = (f32[40,1280]{1,0:T(8,128)S(1)}, f32[40,1280]{1,0:T(8,128)S(1)}, u32[]{:S(2)}, u32[]{:S(2)}) collective-permute-start(f32[40,1280]{1,0:T(8,128)S(1)} %get-tuple-element.81), channel_id=1, source_target_pairs={{0,2},{1,0},{3,1},{5,3},{7,5},{6,7},{4,6},{2,4},{8,10},{9,8},{11,9... | collective-permute-start | bytes 614408 | tf_op jit(solution)/shard_map/ppermute | solution.py:85
  45.1 0.4 collective-permute-start.24
  45.6 1.6 %collective-permute-start.17 = (f32[40,1280]{1,0:T(8,128)S(1)}, f32[40,1280]{1,0:T(8,128)S(1)}, u32[]{:S(2)}, u32[]{:S(2)}) collective-permute-start(f32[40,1280]{1,0:T(8,128)S(1)} %get-tuple-element.83), channel_id=1, source_target_pairs={{0,2},{1,0},{3,1},{5,3},{7,5},{6,7},{4,6},{2,4},{8,10},{9,8},{11,9... | collective-permute-start | bytes 614408 | tf_op jit(solution)/shard_map/ppermute | solution.py:85
  47.2 0.4 collective-permute-start.10
  47.8 1.2 %fusion.4 = bf16[512,1280]{1,0:T(8,128)(2,1)S(1)} fusion(bf16[512,1280]{1,0:T(8,128)(2,1)S(1)} %broadcast_in_dim.2, s32[]{:T(128)S(6)} %select_n.859, bf16[128,1280]{1,0:T(8,128)(2,1)S(1)} %bitcast.116, bf16[1280,1280]{1,0:T(8,128)(2,1)S(1)} %copy-done), kind=kOutput, calls=%fused_computation.12 | convolution fusion | flops 419594240 | bytes 3932164 | tf_op jit(solution)/shard_map/dot_general | solution.py:17
  49.0 1.2 %fusion.3 = bf16[512,1280]{1,0:T(8,128)(2,1)S(1)} fusion(bf16[512,1280]{1,0:T(8,128)(2,1)S(1)} %fusion.4, s32[]{:T(128)S(6)} %select_n.860, bf16[128,1280]{1,0:T(8,128)(2,1)S(1)} %collective-permute-done.4, bf16[1280,1280]{1,0:T(8,128)(2,1)S(1)} %copy-done), kind=kOutput, calls=%fused_computation.10 | convolution fusion | flops 419594240 | bytes 3932164 | tf_op jit(solution)/shard_map/dot_general | solution.py:17
  50.3 2.2 %fusion.2 = bf16[512,1280]{1,0:T(8,128)(2,1)S(1)} fusion(bf16[512,1280]{1,0:T(8,128)(2,1)S(1)} %fusion.3, s32[]{:T(128)S(6)} %select_n.861, bf16[128,1280]{1,0:T(8,128)(2,1)} %collective-permute-done, bf16[1280,1280]{1,0:T(8,128)(2,1)S(1)} %copy-done), kind=kOutput, calls=%fused_computation.8 | convolution fusion | flops 419594240 | bytes 3932164 | tf_op jit(solution)/shard_map/dot_general | solution.py:17
  52.4 1.2 %fusion.1 = bf16[512,1280]{1,0:T(8,128)(2,1)S(1)} fusion(bf16[512,1280]{1,0:T(8,128)(2,1)S(1)} %fusion.2, s32[]{:T(128)S(6)} %select_n.862, bf16[128,1280]{1,0:T(8,128)(2,1)S(1)} %collective-permute-done.6, bf16[1280,1280]{1,0:T(8,128)(2,1)S(1)} %copy-done), kind=kOutput, calls=%fused_computation.6 | convolution fusion | flops 419594240 | bytes 3932164 | tf_op jit(solution)/shard_map/dot_general | solution.py:17
  53.7 1.6 %collective-permute-start.32 = (f32[40,1280]{1,0:T(8,128)S(1)}, f32[40,1280]{1,0:T(8,128)S(1)}, u32[]{:S(2)}, u32[]{:S(2)}) collective-permute-start(f32[40,1280]{1,0:T(8,128)S(1)} %add.603), channel_id=1, source_target_pairs={{0,2},{1,0},{3,1},{5,3},{7,5},{6,7},{4,6},{2,4},{8,10},{9,8},{11,9... | collective-permute-start | bytes 614408 | tf_op jit(solution)/shard_map/ppermute | solution.py:85
  55.4 0.5 collective-permute-start.25
  55.9 1.6 %collective-permute-start.18 = (f32[40,1280]{1,0:T(8,128)S(1)}, f32[40,1280]{1,0:T(8,128)S(1)}, u32[]{:S(2)}, u32[]{:S(2)}) collective-permute-start(f32[40,1280]{1,0:T(8,128)S(1)} %add.545), channel_id=1, source_target_pairs={{0,2},{1,0},{3,1},{5,3},{7,5},{6,7},{4,6},{2,4},{8,10},{9,8},{11,9... | collective-permute-start | bytes 614408 | tf_op jit(solution)/shard_map/ppermute | solution.py:85
  57.5 0.5 collective-permute-start.11
  58.2 3.6 %collective-permute-done.32 = f32[40,1280]{1,0:T(8,128)S(1)} collective-permute-done((f32[40,1280]{1,0:T(8,128)S(1)}, f32[40,1280]{1,0:T(8,128)S(1)}, u32[]{:S(2)}, u32[]{:S(2)}) %collective-permute-start.32) | collective-permute-done | bytes 204832 | tf_op jit(solution)/shard_map/ppermute | solution.py:85
  61.8 1.6 %collective-permute-start.33 = (f32[40,1280]{1,0:T(8,128)S(1)}, f32[40,1280]{1,0:T(8,128)S(1)}, u32[]{:S(2)}, u32[]{:S(2)}) collective-permute-start(f32[40,1280]{1,0:T(8,128)S(1)} %add.606), channel_id=1, source_target_pairs={{0,2},{1,0},{3,1},{5,3},{7,5},{6,7},{4,6},{2,4},{8,10},{9,8},{11,9... | collective-permute-start | bytes 614408 | tf_op jit(solution)/shard_map/ppermute | solution.py:85
  63.4 0.5 collective-permute-start.26
  64.0 2.2 %collective-permute-done.18 = f32[40,1280]{1,0:T(8,128)S(1)} collective-permute-done((f32[40,1280]{1,0:T(8,128)S(1)}, f32[40,1280]{1,0:T(8,128)S(1)}, u32[]{:S(2)}, u32[]{:S(2)}) %collective-permute-start.18) | collective-permute-done | bytes 204832 | tf_op jit(solution)/shard_map/ppermute | solution.py:85
  66.2 1.6 %collective-permute-start.19 = (f32[40,1280]{1,0:T(8,128)S(1)}, f32[40,1280]{1,0:T(8,128)S(1)}, u32[]{:S(2)}, u32[]{:S(2)}) collective-permute-start(f32[40,1280]{1,0:T(8,128)S(1)} %add.550), channel_id=1, source_target_pairs={{0,2},{1,0},{3,1},{5,3},{7,5},{6,7},{4,6},{2,4},{8,10},{9,8},{11,9... | collective-permute-start | bytes 614408 | tf_op jit(solution)/shard_map/ppermute | solution.py:85
  67.8 0.5 collective-permute-start.12
  68.5 2.1 %collective-permute-done.33 = f32[40,1280]{1,0:T(8,128)S(1)} collective-permute-done((f32[40,1280]{1,0:T(8,128)S(1)}, f32[40,1280]{1,0:T(8,128)S(1)}, u32[]{:S(2)}, u32[]{:S(2)}) %collective-permute-start.33) | collective-permute-done | bytes 204832 | tf_op jit(solution)/shard_map/ppermute | solution.py:85
  70.6 1.6 %collective-permute-start.34 = (f32[40,1280]{1,0:T(8,128)S(1)}, f32[40,1280]{1,0:T(8,128)S(1)}, u32[]{:S(2)}, u32[]{:S(2)}) collective-permute-start(f32[40,1280]{1,0:T(8,128)S(1)} %add.609), channel_id=1, source_target_pairs={{0,2},{1,0},{3,1},{5,3},{7,5},{6,7},{4,6},{2,4},{8,10},{9,8},{11,9... | collective-permute-start | bytes 614408 | tf_op jit(solution)/shard_map/ppermute | solution.py:85
  72.2 0.5 collective-permute-start.27
  72.7 2.2 %collective-permute-done.19 = f32[40,1280]{1,0:T(8,128)S(1)} collective-permute-done((f32[40,1280]{1,0:T(8,128)S(1)}, f32[40,1280]{1,0:T(8,128)S(1)}, u32[]{:S(2)}, u32[]{:S(2)}) %collective-permute-start.19) | collective-permute-done | bytes 204832 | tf_op jit(solution)/shard_map/ppermute | solution.py:85
  75.0 1.6 %collective-permute-start.20 = (f32[40,1280]{1,0:T(8,128)S(1)}, f32[40,1280]{1,0:T(8,128)S(1)}, u32[]{:S(2)}, u32[]{:S(2)}) collective-permute-start(f32[40,1280]{1,0:T(8,128)S(1)} %add.555), channel_id=1, source_target_pairs={{0,2},{1,0},{3,1},{5,3},{7,5},{6,7},{4,6},{2,4},{8,10},{9,8},{11,9... | collective-permute-start | bytes 614408 | tf_op jit(solution)/shard_map/ppermute | solution.py:85
  76.6 0.5 collective-permute-start.13
  77.2 2.1 %collective-permute-done.34 = f32[40,1280]{1,0:T(8,128)S(1)} collective-permute-done((f32[40,1280]{1,0:T(8,128)S(1)}, f32[40,1280]{1,0:T(8,128)S(1)}, u32[]{:S(2)}, u32[]{:S(2)}) %collective-permute-start.34) | collective-permute-done | bytes 204832 | tf_op jit(solution)/shard_map/ppermute | solution.py:85
  79.3 1.6 %collective-permute-start.35 = (f32[40,1280]{1,0:T(8,128)S(1)}, f32[40,1280]{1,0:T(8,128)S(1)}, u32[]{:S(2)}, u32[]{:S(2)}) collective-permute-start(f32[40,1280]{1,0:T(8,128)S(1)} %add.612), channel_id=1, source_target_pairs={{0,2},{1,0},{3,1},{5,3},{7,5},{6,7},{4,6},{2,4},{8,10},{9,8},{11,9... | collective-permute-start | bytes 614408 | tf_op jit(solution)/shard_map/ppermute | solution.py:85
  81.0 0.5 collective-permute-start.28
  81.5 2.2 %collective-permute-done.20 = f32[40,1280]{1,0:T(8,128)S(1)} collective-permute-done((f32[40,1280]{1,0:T(8,128)S(1)}, f32[40,1280]{1,0:T(8,128)S(1)}, u32[]{:S(2)}, u32[]{:S(2)}) %collective-permute-start.20) | collective-permute-done | bytes 204832 | tf_op jit(solution)/shard_map/ppermute | solution.py:85
  83.8 1.6 %collective-permute-start.21 = (f32[40,1280]{1,0:T(8,128)S(1)}, f32[40,1280]{1,0:T(8,128)S(1)}, u32[]{:S(2)}, u32[]{:S(2)}) collective-permute-start(f32[40,1280]{1,0:T(8,128)S(1)} %add.560), channel_id=1, source_target_pairs={{0,2},{1,0},{3,1},{5,3},{7,5},{6,7},{4,6},{2,4},{8,10},{9,8},{11,9... | collective-permute-start | bytes 614408 | tf_op jit(solution)/shard_map/ppermute | solution.py:85
  85.4 0.5 collective-permute-start.14
  86.0 2.0 %collective-permute-done.35 = f32[40,1280]{1,0:T(8,128)S(1)} collective-permute-done((f32[40,1280]{1,0:T(8,128)S(1)}, f32[40,1280]{1,0:T(8,128)S(1)}, u32[]{:S(2)}, u32[]{:S(2)}) %collective-permute-start.35) | collective-permute-done | bytes 204832 | tf_op jit(solution)/shard_map/ppermute | solution.py:85
  88.1 1.6 %collective-permute-start.36 = (f32[40,1280]{1,0:T(8,128)S(1)}, f32[40,1280]{1,0:T(8,128)S(1)}, u32[]{:S(2)}, u32[]{:S(2)}) collective-permute-start(f32[40,1280]{1,0:T(8,128)S(1)} %add.615), channel_id=1, source_target_pairs={{0,2},{1,0},{3,1},{5,3},{7,5},{6,7},{4,6},{2,4},{8,10},{9,8},{11,9... | collective-permute-start | bytes 614408 | tf_op jit(solution)/shard_map/ppermute | solution.py:85
  89.8 0.5 collective-permute-start.29
  90.3 2.2 %collective-permute-done.21 = f32[40,1280]{1,0:T(8,128)S(1)} collective-permute-done((f32[40,1280]{1,0:T(8,128)S(1)}, f32[40,1280]{1,0:T(8,128)S(1)}, u32[]{:S(2)}, u32[]{:S(2)}) %collective-permute-start.21) | collective-permute-done | bytes 204832 | tf_op jit(solution)/shard_map/ppermute | solution.py:85
  92.5 1.6 %collective-permute-start.22 = (f32[40,1280]{1,0:T(8,128)S(1)}, f32[40,1280]{1,0:T(8,128)S(1)}, u32[]{:S(2)}, u32[]{:S(2)}) collective-permute-start(f32[40,1280]{1,0:T(8,128)S(1)} %add.565), channel_id=1, source_target_pairs={{0,2},{1,0},{3,1},{5,3},{7,5},{6,7},{4,6},{2,4},{8,10},{9,8},{11,9... | collective-permute-start | bytes 614408 | tf_op jit(solution)/shard_map/ppermute | solution.py:85
  94.2 0.5 collective-permute-start.15
  94.8 2.1 %collective-permute-done.36 = f32[40,1280]{1,0:T(8,128)S(1)} collective-permute-done((f32[40,1280]{1,0:T(8,128)S(1)}, f32[40,1280]{1,0:T(8,128)S(1)}, u32[]{:S(2)}, u32[]{:S(2)}) %collective-permute-start.36) | collective-permute-done | bytes 204832 | tf_op jit(solution)/shard_map/ppermute | solution.py:85
  96.9 1.6 %collective-permute-start.37 = (f32[40,1280]{1,0:T(8,128)S(1)}, f32[40,1280]{1,0:T(8,128)S(1)}, u32[]{:S(2)}, u32[]{:S(2)}) collective-permute-start(f32[40,1280]{1,0:T(8,128)S(1)} %add.618), channel_id=1, source_target_pairs={{0,2},{1,0},{3,1},{5,3},{7,5},{6,7},{4,6},{2,4},{8,10},{9,8},{11,9... | collective-permute-start | bytes 614408 | tf_op jit(solution)/shard_map/ppermute | solution.py:85
  98.6 0.5 collective-permute-start.30
  99.1 2.2 %collective-permute-done.22 = f32[40,1280]{1,0:T(8,128)S(1)} collective-permute-done((f32[40,1280]{1,0:T(8,128)S(1)}, f32[40,1280]{1,0:T(8,128)S(1)}, u32[]{:S(2)}, u32[]{:S(2)}) %collective-permute-start.22) | collective-permute-done | bytes 204832 | tf_op jit(solution)/shard_map/ppermute | solution.py:85
  101.3 1.6 %collective-permute-start.23 = (f32[40,1280]{1,0:T(8,128)S(1)}, f32[40,1280]{1,0:T(8,128)S(1)}, u32[]{:S(2)}, u32[]{:S(2)}) collective-permute-start(f32[40,1280]{1,0:T(8,128)S(1)} %add.570), channel_id=1, source_target_pairs={{0,2},{1,0},{3,1},{5,3},{7,5},{6,7},{4,6},{2,4},{8,10},{9,8},{11,9... | collective-permute-start | bytes 614408 | tf_op jit(solution)/shard_map/ppermute | solution.py:85
  103.0 0.5 collective-permute-start.16
  103.6 2.1 %collective-permute-done.37 = f32[40,1280]{1,0:T(8,128)S(1)} collective-permute-done((f32[40,1280]{1,0:T(8,128)S(1)}, f32[40,1280]{1,0:T(8,128)S(1)}, u32[]{:S(2)}, u32[]{:S(2)}) %collective-permute-start.37) | collective-permute-done | bytes 204832 | tf_op jit(solution)/shard_map/ppermute | solution.py:85
  105.7 1.6 %collective-permute-done.30 = f32[40,1280]{1,0:T(8,128)S(1)} collective-permute-done((f32[40,1280]{1,0:T(8,128)S(1)}, f32[40,1280]{1,0:T(8,128)S(1)}, u32[]{:S(2)}, u32[]{:S(2)}) %collective-permute-start.30) | collective-permute-done | bytes 204832 | tf_op jit(solution)/shard_map/ppermute | solution.py:85
  107.3 0.9 collective-permute-done.23
  108.2 1.4 %collective-permute-done.16 = f32[40,1280]{1,0:T(8,128)S(1)} collective-permute-done((f32[40,1280]{1,0:T(8,128)S(1)}, f32[40,1280]{1,0:T(8,128)S(1)}, u32[]{:S(2)}, u32[]{:S(2)}) %collective-permute-start.16) | collective-permute-done | bytes 204832 | tf_op jit(solution)/shard_map/ppermute | solution.py:85
  109.6 2.0 %add_divide_fusion = (f32[160,1280]{1,0:T(8,128)}, f32[160,1280]{1,0:T(8,128)}, f32[160,1280]{1,0:T(8,128)}, f32[160,1280]{1,0:T(8,128)}) fusion(f32[160,1280]{1,0:T(8,128)S(1)} %copy-done.3, f32[160,1280]{1,0:T(8,128)S(1)} %copy-done.4, f32[160,1280]{1,0:T(8,128)S(1)} %copy-done.5, f32[40,1280]{1,0:T(8,128)S(1)} %add.621, f32[40,1280]{1,0:T(8,128)S(1)} %add.598, ...), kind=kLoop, calls=%fused_computation.16 | loop fusion | flops 3481600 | bytes 6553600 | tf_op jit(solution)/shard_map/div | solution.py:202
  (96 shorter events, 2.0 us)
Async XLA Ops:
  0.6 47.2 %copy-start = (bf16[1280,1280]{1,0:T(8,128)(2,1)S(1)}, bf16[1280,1280]{1,0:T(8,128)(2,1)}, u32[]{:S(2)}) copy-start(bf16[1280,1280]{1,0:T(8,128)(2,1)} %param.8) | copy-start | bytes 9830404
  0.6 11.9 %collective-permute-start = (bf16[128,1280]{1,0:T(8,128)(2,1)}, bf16[128,1280]{1,0:T(8,128)(2,1)}, u32[]{:S(2)}, u32[]{:S(2)}) collective-permute-start(bf16[128,1280]{1,0:T(8,128)(2,1)} %bitcast.114), channel_id=1, source_target_pairs={{0,16},{8,24},{16,0},{24,8},{1,17},{9,25},{17,1},{25,9},{2,18},{10... | collective-permute-start | bytes 983048 | tf_op jit(solution)/shard_map/ppermute | solution.py:105
  5.7 12.9 %collective-permute-start.1 = (bf16[128,1280]{1,0:T(8,128)(2,1)S(1)}, bf16[128,1280]{1,0:T(8,128)(2,1)S(1)}, u32[]{:S(2)}, u32[]{:S(2)}) collective-permute-start(bf16[128,1280]{1,0:T(8,128)(2,1)S(1)} %get-tuple-element.85), channel_id=1, source_target_pairs={{0,16},{8,24},{16,0},{24,8},{1,17},{9,25},{17,1},{25,9},{2,18},{10... | collective-permute-start | bytes 983048 | tf_op jit(solution)/shard_map/ppermute | solution.py:106
  18.6 0.7 copy-start.6
  19.3 9.2 %collective-permute-start.2 = (bf16[128,1280]{1,0:T(8,128)(2,1)}, bf16[128,1280]{1,0:T(8,128)(2,1)}, u32[]{:S(2)}, u32[]{:S(2)}) collective-permute-start(bf16[128,1280]{1,0:T(8,128)(2,1)} %get-tuple-element.41), channel_id=1, source_target_pairs={{0,16},{8,24},{16,0},{24,8},{1,17},{9,25},{17,1},{25,9},{2,18},{10... | collective-permute-start | bytes 983048 | tf_op jit(solution)/shard_map/ppermute | solution.py:108
  21.1 10.1 %copy-start.7 = (bf16[128,1280]{1,0:T(8,128)(2,1)S(1)}, bf16[128,1280]{1,0:T(8,128)(2,1)}, u32[]{:S(2)}) copy-start(bf16[128,1280]{1,0:T(8,128)(2,1)} %copy-done.6) | copy-start | bytes 983044
  28.5 3.2 %collective-permute-start.3 = (bf16[128,1280]{1,0:T(8,128)(2,1)}, bf16[128,1280]{1,0:T(8,128)(2,1)S(1)}, u32[]{:S(2)}, u32[]{:S(2)}) collective-permute-start(bf16[128,1280]{1,0:T(8,128)(2,1)} %get-tuple-element.42), channel_id=1, source_target_pairs={{0,8},{8,0},{16,24},{24,16},{1,9},{9,1},{17,25},{25,17},{2,10},{10... | collective-permute-start | bytes 983048 | tf_op jit(solution)/shard_map/ppermute | solution.py:113
  28.5 3.2 %collective-permute-start.4 = (bf16[128,1280]{1,0:T(8,128)(2,1)}, bf16[128,1280]{1,0:T(8,128)(2,1)S(1)}, u32[]{:S(2)}, u32[]{:S(2)}) collective-permute-start(bf16[128,1280]{1,0:T(8,128)(2,1)} %bitcast.115), channel_id=1, source_target_pairs={{0,8},{8,0},{16,24},{24,16},{1,9},{9,1},{17,25},{25,17},{2,10},{10... | collective-permute-start | bytes 983048 | tf_op jit(solution)/shard_map/ppermute | solution.py:112
  31.2 3.8 %collective-permute-start.5 = (bf16[128,1280]{1,0:T(8,128)(2,1)S(1)}, bf16[128,1280]{1,0:T(8,128)(2,1)S(1)}, u32[]{:S(2)}, u32[]{:S(2)}) collective-permute-start(bf16[128,1280]{1,0:T(8,128)(2,1)S(1)} %copy-done.7), channel_id=1, source_target_pairs={{0,8},{8,0},{16,24},{24,16},{1,9},{9,1},{17,25},{25,17},{2,10},{10... | collective-permute-start | bytes 983048 | tf_op jit(solution)/shard_map/ppermute | solution.py:110
  31.2 3.7 %collective-permute-start.6 = (bf16[128,1280]{1,0:T(8,128)(2,1)}, bf16[128,1280]{1,0:T(8,128)(2,1)S(1)}, u32[]{:S(2)}, u32[]{:S(2)}) collective-permute-start(bf16[128,1280]{1,0:T(8,128)(2,1)} %collective-permute-done), channel_id=1, source_target_pairs={{0,8},{8,0},{16,24},{24,16},{1,9},{9,1},{17,25},{25,17},{2,10},{10... | collective-permute-start | bytes 983048 | tf_op jit(solution)/shard_map/ppermute | solution.py:109
  34.9 12.9 %copy-start.1 = (bf16[1,1,128,1280]{3,2,1,0:T(8,128)(2,1)S(1)}, bf16[1,1,128,1280]{3,2,1,0:T(8,128)(2,1)}, u32[]{:S(2)}) copy-start(bf16[1,1,128,1280]{3,2,1,0:T(8,128)(2,1)} %param.7) | copy-start | bytes 983044
  37.5 1.9 %collective-permute-start.7 = (f32[1]{0:T(128)}, f32[1]{0:T(128)}, u32[]{:S(2)}, u32[]{:S(2)}) collective-permute-start(f32[1]{0:T(128)} %bitcast.5), channel_id=1, source_target_pairs={{0,8},{8,0},{16,24},{24,16},{1,9},{9,1},{17,25},{25,17},{2,10},{10... | collective-permute-start | bytes 20 | tf_op jit(solution)/shard_map/ppermute | solution.py:126
  37.5 3.6 %collective-permute-start.8 = (f32[1]{0:T(128)}, f32[1]{0:T(128)}, u32[]{:S(2)}, u32[]{:S(2)}) collective-permute-start(f32[1]{0:T(128)} %bitcast.5), channel_id=1, source_target_pairs={{0,16},{8,24},{16,0},{24,8},{1,17},{9,25},{17,1},{25,9},{2,18},{10... | collective-permute-start | bytes 20 | tf_op jit(solution)/shard_map/ppermute | solution.py:126
  39.0 3.1 %collective-permute-start.9 = (f32[1]{0:T(128)}, f32[1]{0:T(128)}, u32[]{:S(2)}, u32[]{:S(2)}) collective-permute-start(f32[1]{0:T(128)} %bitcast.5), channel_id=1, source_target_pairs={{0,24},{8,16},{16,8},{24,0},{1,25},{9,17},{17,9},{25,1},{2,26},{10... | collective-permute-start | bytes 20 | tf_op jit(solution)/shard_map/ppermute | solution.py:126
  43.5 10.1 %collective-permute-start.31 = (f32[40,1280]{1,0:T(8,128)S(1)}, f32[40,1280]{1,0:T(8,128)S(1)}, u32[]{:S(2)}, u32[]{:S(2)}) collective-permute-start(f32[40,1280]{1,0:T(8,128)S(1)} %get-tuple-element.81), channel_id=1, source_target_pairs={{0,2},{1,0},{3,1},{5,3},{7,5},{6,7},{4,6},{2,4},{8,10},{9,8},{11,9... | collective-permute-start | bytes 614408 | tf_op jit(solution)/shard_map/ppermute | solution.py:85
  45.1 10.2 %collective-permute-start.24 = (f32[40,1280]{1,0:T(8,128)S(1)}, f32[40,1280]{1,0:T(8,128)S(1)}, u32[]{:S(2)}, u32[]{:S(2)}) collective-permute-start(f32[40,1280]{1,0:T(8,128)S(1)} %get-tuple-element.82), channel_id=1, source_target_pairs={{0,1},{1,3},{3,5},{5,7},{7,6},{6,4},{4,2},{2,0},{8,9},{9,11},{11,1... | collective-permute-start | bytes 614408 | tf_op jit(solution)/shard_map/ppermute | solution.py:85
  45.6 10.3 %collective-permute-start.17 = (f32[40,1280]{1,0:T(8,128)S(1)}, f32[40,1280]{1,0:T(8,128)S(1)}, u32[]{:S(2)}, u32[]{:S(2)}) collective-permute-start(f32[40,1280]{1,0:T(8,128)S(1)} %get-tuple-element.83), channel_id=1, source_target_pairs={{0,2},{1,0},{3,1},{5,3},{7,5},{6,7},{4,6},{2,4},{8,10},{9,8},{11,9... | collective-permute-start | bytes 614408 | tf_op jit(solution)/shard_map/ppermute | solution.py:85
  47.2 10.4 %collective-permute-start.10 = (f32[40,1280]{1,0:T(8,128)S(1)}, f32[40,1280]{1,0:T(8,128)S(1)}, u32[]{:S(2)}, u32[]{:S(2)}) collective-permute-start(f32[40,1280]{1,0:T(8,128)S(1)} %get-tuple-element.80), channel_id=1, source_target_pairs={{0,1},{1,3},{3,5},{5,7},{7,6},{6,4},{4,2},{2,0},{8,9},{9,11},{11,1... | collective-permute-start | bytes 614408 | tf_op jit(solution)/shard_map/ppermute | solution.py:85
  53.6 27.4 %copy-start.2 = (bf16[512,1280]{1,0:T(8,128)(2,1)}, bf16[512,1280]{1,0:T(8,128)(2,1)S(1)}, u32[]{:S(2)}) copy-start(bf16[512,1280]{1,0:T(8,128)(2,1)S(1)} %fusion.1) | copy-start | bytes 3932164
  53.7 8.1 %collective-permute-start.32 = (f32[40,1280]{1,0:T(8,128)S(1)}, f32[40,1280]{1,0:T(8,128)S(1)}, u32[]{:S(2)}, u32[]{:S(2)}) collective-permute-start(f32[40,1280]{1,0:T(8,128)S(1)} %add.603), channel_id=1, source_target_pairs={{0,2},{1,0},{3,1},{5,3},{7,5},{6,7},{4,6},{2,4},{8,10},{9,8},{11,9... | collective-permute-start | bytes 614408 | tf_op jit(solution)/shard_map/ppermute | solution.py:85
  55.4 8.1 %collective-permute-start.25 = (f32[40,1280]{1,0:T(8,128)S(1)}, f32[40,1280]{1,0:T(8,128)S(1)}, u32[]{:S(2)}, u32[]{:S(2)}) collective-permute-start(f32[40,1280]{1,0:T(8,128)S(1)} %add.580), channel_id=1, source_target_pairs={{0,1},{1,3},{3,5},{5,7},{7,6},{6,4},{4,2},{2,0},{8,9},{9,11},{11,1... | collective-permute-start | bytes 614408 | tf_op jit(solution)/shard_map/ppermute | solution.py:85
  55.9 10.3 %collective-permute-start.18 = (f32[40,1280]{1,0:T(8,128)S(1)}, f32[40,1280]{1,0:T(8,128)S(1)}, u32[]{:S(2)}, u32[]{:S(2)}) collective-permute-start(f32[40,1280]{1,0:T(8,128)S(1)} %add.545), channel_id=1, source_target_pairs={{0,2},{1,0},{3,1},{5,3},{7,5},{6,7},{4,6},{2,4},{8,10},{9,8},{11,9... | collective-permute-start | bytes 614408 | tf_op jit(solution)/shard_map/ppermute | solution.py:85
  57.5 10.3 %collective-permute-start.11 = (f32[40,1280]{1,0:T(8,128)S(1)}, f32[40,1280]{1,0:T(8,128)S(1)}, u32[]{:S(2)}, u32[]{:S(2)}) collective-permute-start(f32[40,1280]{1,0:T(8,128)S(1)} %add.518), channel_id=1, source_target_pairs={{0,1},{1,3},{3,5},{5,7},{7,6},{6,4},{4,2},{2,0},{8,9},{9,11},{11,1... | collective-permute-start | bytes 614408 | tf_op jit(solution)/shard_map/ppermute | solution.py:85
  61.8 8.7 %collective-permute-start.33 = (f32[40,1280]{1,0:T(8,128)S(1)}, f32[40,1280]{1,0:T(8,128)S(1)}, u32[]{:S(2)}, u32[]{:S(2)}) collective-permute-start(f32[40,1280]{1,0:T(8,128)S(1)} %add.606), channel_id=1, source_target_pairs={{0,2},{1,0},{3,1},{5,3},{7,5},{6,7},{4,6},{2,4},{8,10},{9,8},{11,9... | collective-permute-start | bytes 614408 | tf_op jit(solution)/shard_map/ppermute | solution.py:85
  63.4 8.7 %collective-permute-start.26 = (f32[40,1280]{1,0:T(8,128)S(1)}, f32[40,1280]{1,0:T(8,128)S(1)}, u32[]{:S(2)}, u32[]{:S(2)}) collective-permute-start(f32[40,1280]{1,0:T(8,128)S(1)} %add.583), channel_id=1, source_target_pairs={{0,1},{1,3},{3,5},{5,7},{7,6},{6,4},{4,2},{2,0},{8,9},{9,11},{11,1... | collective-permute-start | bytes 614408 | tf_op jit(solution)/shard_map/ppermute | solution.py:85
  66.2 8.8 %collective-permute-start.19 = (f32[40,1280]{1,0:T(8,128)S(1)}, f32[40,1280]{1,0:T(8,128)S(1)}, u32[]{:S(2)}, u32[]{:S(2)}) collective-permute-start(f32[40,1280]{1,0:T(8,128)S(1)} %add.550), channel_id=1, source_target_pairs={{0,2},{1,0},{3,1},{5,3},{7,5},{6,7},{4,6},{2,4},{8,10},{9,8},{11,9... | collective-permute-start | bytes 614408 | tf_op jit(solution)/shard_map/ppermute | solution.py:85
  67.8 8.8 %collective-permute-start.12 = (f32[40,1280]{1,0:T(8,128)S(1)}, f32[40,1280]{1,0:T(8,128)S(1)}, u32[]{:S(2)}, u32[]{:S(2)}) collective-permute-start(f32[40,1280]{1,0:T(8,128)S(1)} %add.521), channel_id=1, source_target_pairs={{0,1},{1,3},{3,5},{5,7},{7,6},{6,4},{4,2},{2,0},{8,9},{9,11},{11,1... | collective-permute-start | bytes 614408 | tf_op jit(solution)/shard_map/ppermute | solution.py:85
  70.6 8.8 %collective-permute-start.34 = (f32[40,1280]{1,0:T(8,128)S(1)}, f32[40,1280]{1,0:T(8,128)S(1)}, u32[]{:S(2)}, u32[]{:S(2)}) collective-permute-start(f32[40,1280]{1,0:T(8,128)S(1)} %add.609), channel_id=1, source_target_pairs={{0,2},{1,0},{3,1},{5,3},{7,5},{6,7},{4,6},{2,4},{8,10},{9,8},{11,9... | collective-permute-start | bytes 614408 | tf_op jit(solution)/shard_map/ppermute | solution.py:85
  72.2 8.7 %collective-permute-start.27 = (f32[40,1280]{1,0:T(8,128)S(1)}, f32[40,1280]{1,0:T(8,128)S(1)}, u32[]{:S(2)}, u32[]{:S(2)}) collective-permute-start(f32[40,1280]{1,0:T(8,128)S(1)} %add.586), channel_id=1, source_target_pairs={{0,1},{1,3},{3,5},{5,7},{7,6},{6,4},{4,2},{2,0},{8,9},{9,11},{11,1... | collective-permute-start | bytes 614408 | tf_op jit(solution)/shard_map/ppermute | solution.py:85
  75.0 8.7 %collective-permute-start.20 = (f32[40,1280]{1,0:T(8,128)S(1)}, f32[40,1280]{1,0:T(8,128)S(1)}, u32[]{:S(2)}, u32[]{:S(2)}) collective-permute-start(f32[40,1280]{1,0:T(8,128)S(1)} %add.555), channel_id=1, source_target_pairs={{0,2},{1,0},{3,1},{5,3},{7,5},{6,7},{4,6},{2,4},{8,10},{9,8},{11,9... | collective-permute-start | bytes 614408 | tf_op jit(solution)/shard_map/ppermute | solution.py:85
  76.6 8.8 %collective-permute-start.13 = (f32[40,1280]{1,0:T(8,128)S(1)}, f32[40,1280]{1,0:T(8,128)S(1)}, u32[]{:S(2)}, u32[]{:S(2)}) collective-permute-start(f32[40,1280]{1,0:T(8,128)S(1)} %add.524), channel_id=1, source_target_pairs={{0,1},{1,3},{3,5},{5,7},{7,6},{6,4},{4,2},{2,0},{8,9},{9,11},{11,1... | collective-permute-start | bytes 614408 | tf_op jit(solution)/shard_map/ppermute | solution.py:85
  79.3 8.8 %collective-permute-start.35 = (f32[40,1280]{1,0:T(8,128)S(1)}, f32[40,1280]{1,0:T(8,128)S(1)}, u32[]{:S(2)}, u32[]{:S(2)}) collective-permute-start(f32[40,1280]{1,0:T(8,128)S(1)} %add.612), channel_id=1, source_target_pairs={{0,2},{1,0},{3,1},{5,3},{7,5},{6,7},{4,6},{2,4},{8,10},{9,8},{11,9... | collective-permute-start | bytes 614408 | tf_op jit(solution)/shard_map/ppermute | solution.py:85
  81.0 8.7 %collective-permute-start.28 = (f32[40,1280]{1,0:T(8,128)S(1)}, f32[40,1280]{1,0:T(8,128)S(1)}, u32[]{:S(2)}, u32[]{:S(2)}) collective-permute-start(f32[40,1280]{1,0:T(8,128)S(1)} %add.589), channel_id=1, source_target_pairs={{0,1},{1,3},{3,5},{5,7},{7,6},{6,4},{4,2},{2,0},{8,9},{9,11},{11,1... | collective-permute-start | bytes 614408 | tf_op jit(solution)/shard_map/ppermute | solution.py:85
  83.7 25.9 %copy-start.3 = (f32[160,1280]{1,0:T(8,128)S(1)}, f32[160,1280]{1,0:T(8,128)}, u32[]{:S(2)}) copy-start(f32[160,1280]{1,0:T(8,128)} %param.11) | copy-start | bytes 2457604
  83.7 25.9 %copy-start.4 = (f32[160,1280]{1,0:T(8,128)S(1)}, f32[160,1280]{1,0:T(8,128)}, u32[]{:S(2)}) copy-start(f32[160,1280]{1,0:T(8,128)} %param.10) | copy-start | bytes 2457604
  83.8 25.9 %copy-start.5 = (f32[160,1280]{1,0:T(8,128)S(1)}, f32[160,1280]{1,0:T(8,128)}, u32[]{:S(2)}) copy-start(f32[160,1280]{1,0:T(8,128)} %param.9) | copy-start | bytes 2457604
  83.8 8.7 %collective-permute-start.21 = (f32[40,1280]{1,0:T(8,128)S(1)}, f32[40,1280]{1,0:T(8,128)S(1)}, u32[]{:S(2)}, u32[]{:S(2)}) collective-permute-start(f32[40,1280]{1,0:T(8,128)S(1)} %add.560), channel_id=1, source_target_pairs={{0,2},{1,0},{3,1},{5,3},{7,5},{6,7},{4,6},{2,4},{8,10},{9,8},{11,9... | collective-permute-start | bytes 614408 | tf_op jit(solution)/shard_map/ppermute | solution.py:85
  85.4 8.7 %collective-permute-start.14 = (f32[40,1280]{1,0:T(8,128)S(1)}, f32[40,1280]{1,0:T(8,128)S(1)}, u32[]{:S(2)}, u32[]{:S(2)}) collective-permute-start(f32[40,1280]{1,0:T(8,128)S(1)} %add.527), channel_id=1, source_target_pairs={{0,1},{1,3},{3,5},{5,7},{7,6},{6,4},{4,2},{2,0},{8,9},{9,11},{11,1... | collective-permute-start | bytes 614408 | tf_op jit(solution)/shard_map/ppermute | solution.py:85
  88.1 8.7 %collective-permute-start.36 = (f32[40,1280]{1,0:T(8,128)S(1)}, f32[40,1280]{1,0:T(8,128)S(1)}, u32[]{:S(2)}, u32[]{:S(2)}) collective-permute-start(f32[40,1280]{1,0:T(8,128)S(1)} %add.615), channel_id=1, source_target_pairs={{0,2},{1,0},{3,1},{5,3},{7,5},{6,7},{4,6},{2,4},{8,10},{9,8},{11,9... | collective-permute-start | bytes 614408 | tf_op jit(solution)/shard_map/ppermute | solution.py:85
  89.8 8.7 %collective-permute-start.29 = (f32[40,1280]{1,0:T(8,128)S(1)}, f32[40,1280]{1,0:T(8,128)S(1)}, u32[]{:S(2)}, u32[]{:S(2)}) collective-permute-start(f32[40,1280]{1,0:T(8,128)S(1)} %add.592), channel_id=1, source_target_pairs={{0,1},{1,3},{3,5},{5,7},{7,6},{6,4},{4,2},{2,0},{8,9},{9,11},{11,1... | collective-permute-start | bytes 614408 | tf_op jit(solution)/shard_map/ppermute | solution.py:85
  92.5 8.7 %collective-permute-start.22 = (f32[40,1280]{1,0:T(8,128)S(1)}, f32[40,1280]{1,0:T(8,128)S(1)}, u32[]{:S(2)}, u32[]{:S(2)}) collective-permute-start(f32[40,1280]{1,0:T(8,128)S(1)} %add.565), channel_id=1, source_target_pairs={{0,2},{1,0},{3,1},{5,3},{7,5},{6,7},{4,6},{2,4},{8,10},{9,8},{11,9... | collective-permute-start | bytes 614408 | tf_op jit(solution)/shard_map/ppermute | solution.py:85
  94.2 8.7 %collective-permute-start.15 = (f32[40,1280]{1,0:T(8,128)S(1)}, f32[40,1280]{1,0:T(8,128)S(1)}, u32[]{:S(2)}, u32[]{:S(2)}) collective-permute-start(f32[40,1280]{1,0:T(8,128)S(1)} %add.530), channel_id=1, source_target_pairs={{0,1},{1,3},{3,5},{5,7},{7,6},{6,4},{4,2},{2,0},{8,9},{9,11},{11,1... | collective-permute-start | bytes 614408 | tf_op jit(solution)/shard_map/ppermute | solution.py:85
  96.9 8.7 %collective-permute-start.37 = (f32[40,1280]{1,0:T(8,128)S(1)}, f32[40,1280]{1,0:T(8,128)S(1)}, u32[]{:S(2)}, u32[]{:S(2)}) collective-permute-start(f32[40,1280]{1,0:T(8,128)S(1)} %add.618), channel_id=1, source_target_pairs={{0,2},{1,0},{3,1},{5,3},{7,5},{6,7},{4,6},{2,4},{8,10},{9,8},{11,9... | collective-permute-start | bytes 614408 | tf_op jit(solution)/shard_map/ppermute | solution.py:85
  98.6 8.7 %collective-permute-start.30 = (f32[40,1280]{1,0:T(8,128)S(1)}, f32[40,1280]{1,0:T(8,128)S(1)}, u32[]{:S(2)}, u32[]{:S(2)}) collective-permute-start(f32[40,1280]{1,0:T(8,128)S(1)} %add.595), channel_id=1, source_target_pairs={{0,1},{1,3},{3,5},{5,7},{7,6},{6,4},{4,2},{2,0},{8,9},{9,11},{11,1... | collective-permute-start | bytes 614408 | tf_op jit(solution)/shard_map/ppermute | solution.py:85
  101.3 6.9 %collective-permute-start.23 = (f32[40,1280]{1,0:T(8,128)S(1)}, f32[40,1280]{1,0:T(8,128)S(1)}, u32[]{:S(2)}, u32[]{:S(2)}) collective-permute-start(f32[40,1280]{1,0:T(8,128)S(1)} %add.570), channel_id=1, source_target_pairs={{0,2},{1,0},{3,1},{5,3},{7,5},{6,7},{4,6},{2,4},{8,10},{9,8},{11,9... | collective-permute-start | bytes 614408 | tf_op jit(solution)/shard_map/ppermute | solution.py:85
  103.0 6.6 %collective-permute-start.16 = (f32[40,1280]{1,0:T(8,128)S(1)}, f32[40,1280]{1,0:T(8,128)S(1)}, u32[]{:S(2)}, u32[]{:S(2)}) collective-permute-start(f32[40,1280]{1,0:T(8,128)S(1)} %add.533), channel_id=1, source_target_pairs={{0,1},{1,3},{3,5},{5,7},{7,6},{6,4},{4,2},{2,0},{8,9},{9,11},{11,1... | collective-permute-start | bytes 614408 | tf_op jit(solution)/shard_map/ppermute | solution.py:85

commit v13 on v9

--- a/solution.py
+++ b/solution.py
@@ -103,9 +103,10 @@
     over_x = [(i, i ^ 2) for i in range(4)]
     over_core = [(i, i ^ 1) for i in range(4)]
     g_far = lax.ppermute(grad_rows, "aug", over_x)
-    g_near = lax.ppermute(grad_rows, "aug", over_core)
     h_far_relay = lax.ppermute(cols(a ^ 3), "aug", over_x)
-    h_near = lax.ppermute(cols(a ^ 1), "aug", over_core)
+    _, (g_mine, h_mine) = lax.optimization_barrier((h_far_relay, (grad_rows, cols(a ^ 1))))
+    g_near = lax.ppermute(g_mine, "aug", over_core)
+    h_near = lax.ppermute(h_mine, "aug", over_core)
     g_relay = lax.ppermute(g_far, "aug", over_core)
     h_relay = lax.ppermute(h_far_relay, "aug", over_core)
     _, second = lax.optimization_barrier((h_far_relay, cols(a ^ 2)))

time: 110 us -> 108 us (0.982)
  matrix products: 15.5 us -> 13.4 us
    ppermute x1, starting transfers between devices: 2.57 us -> 0.03 us  [exchange_four(): g_far = lax.ppermute(grad_rows, 'aug', over_x)]
    ppermute x1, starting transfers between devices: 0.5 us -> 2.94 us  [exchange_four(): h_far_relay = lax.ppermute(cols(a ^ 3), 'aug', over_x)]
    ppermute x1, waiting for transfers between devices: 10.7 us -> 8.81 us  [exchange_four(): h_far_relay = lax.ppermute(cols(a ^ 3), 'aug', over_x)]
    ppermute x1, waiting for transfers between devices: 0.01 us -> 1.83 us  [exchange_four(): g_far = lax.ppermute(grad_rows, 'aug', over_x)]
    dot_general x4, matrix products: 8.79 us -> 7.67 us  [per_device(): term = jnp.dot(h_piece.T, g_piece, preferred_element_type=jnp.float32)]
  transfers between devices with their start and end apart: 38 -> 38, of which waited for: 18 -> 19; matrix products, arithmetic and copies ran while one was open for 15% -> 11% of each run, Pallas kernels for 0% -> 0%
where the time goes in v13:
time: 108 us
  waiting for transfers between devices  46.6 us (43%)
  starting transfers between devices  37.2 us (34%)
  matrix products  13.4 us (12%)
  between operations  4.91 us (5%)
  other arithmetic  3.46 us (3%)
  local copies, waits for them, and re-layouts  2.43 us (2%)
    ppermute x28, starting transfers between devices, ring_reduce_scatter(): lax.ppermute(v, 'dp', right if step < 0 else left)  29.7 us
    ppermute x28, waiting for transfers between devices, ring_reduce_scatter(): lax.ppermute(v, 'dp', right if step < 0 else left)  28.9 us
    ppermute x1, waiting for transfers between devices, exchange_four(): h_far_relay = lax.ppermute(cols(a ^ 3), 'aug', over_x)  8.81 us
    dot_general x4, matrix products, per_device(): term = jnp.dot(h_piece.T, g_piece, preferred_element_type=jnp.float32)  7.67 us
    dot_general x4, matrix products, project_back(): lax.dot_general(rows, down_weight, (((1,), (1,)), ((), ())), preferred_el...  5.77 us
    ppermute x1, waiting for transfers between devices, exchange_four(): h_far = lax.ppermute(second, 'aug', over_x)  5.45 us
    ppermute x1, starting transfers between devices, exchange_four(): h_far_relay = lax.ppermute(cols(a ^ 3), 'aug', over_x)  2.94 us
    dynamic_slice x1, local copies, waits for them, and re-layouts, cols(): return lax.dynamic_slice_in_dim(h_rows, b * sw, sw, axis=1)  2.29 us
  transfers between devices with their start and end apart: 38, of which 19 were waited for; matrix products, arithmetic and copies ran while one was open for 11% of the time, Pallas kernels for 0%

profile of v13, /device:TPU:0, one launch (start us, length us, event | category | flops | bytes accessed | tf_op | source)
XLA Modules:
  0.0 108.0 jit_solution(157743380067487111)
XLA Ops:
  0.7 2.3 %dynamic-slice_bitcast_fusion = (bf16[128,1280]{1,0:T(8,128)(2,1)}, bf16[128,1280]{1,0:T(8,128)(2,1)}, bf16[128,1280]{1,0:T(8,128)(2,1)}) fusion(bf16[1,1,128,5120]{3,2,1,0:T(8,128)(2,1)} %param.6, s32[]{:T(128)S(6)} %select_n.691, s32[]{:T(128)S(6)} %select_n.689, s32[]{:T(128)S(6)} %select_n.690), kind=kLoop, calls=%fused_computation.21 | loop fusion | bytes 1966092 | tf_op jit(solution)/shard_map/dynamic_slice | solution.py:101
  3.0 2.9 %collective-permute-start = (bf16[128,1280]{1,0:T(8,128)(2,1)}, bf16[128,1280]{1,0:T(8,128)(2,1)}, u32[]{:S(2)}, u32[]{:S(2)}) collective-permute-start(bf16[128,1280]{1,0:T(8,128)(2,1)} %get-tuple-element.85), channel_id=1, source_target_pairs={{0,16},{8,24},{16,0},{24,8},{1,17},{9,25},{17,1},{25,9},{2,18},{10... | collective-permute-start | bytes 983048 | tf_op jit(solution)/shard_map/ppermute | solution.py:106
  5.9 8.8 %collective-permute-done = bf16[128,1280]{1,0:T(8,128)(2,1)} collective-permute-done((bf16[128,1280]{1,0:T(8,128)(2,1)}, bf16[128,1280]{1,0:T(8,128)(2,1)}, u32[]{:S(2)}, u32[]{:S(2)}) %collective-permute-start) | collective-permute-done | bytes 327712 | tf_op jit(solution)/shard_map/ppermute | solution.py:106
  14.8 0.5 collective-permute-start.2
  15.3 2.1 %fusion.6 = f32[1280,1280]{1,0:T(8,128)S(1)} fusion(bf16[1,1,128,5120]{3,2,1,0:T(8,128)(2,1)} %param.6, s32[]{:T(128)S(6)} %select_n.688, bf16[1,1,128,1280]{3,2,1,0:T(8,128)(2,1)} %param.7), kind=kOutput, calls=%fused_computation.19 | convolution fusion | flops 419430400 | bytes 7208964 | tf_op jit(solution)/shard_map/dot_general | solution.py:154
  17.4 2.1 %collective-permute-start.3 = (bf16[128,1280]{1,0:T(8,128)(2,1)S(1)}, bf16[128,1280]{1,0:T(8,128)(2,1)S(1)}, u32[]{:S(2)}, u32[]{:S(2)}) collective-permute-start(bf16[128,1280]{1,0:T(8,128)(2,1)S(1)} %copy-done.6), channel_id=1, source_target_pairs={{0,16},{8,24},{16,0},{24,8},{1,17},{9,25},{17,1},{25,9},{2,18},{10... | collective-permute-start | bytes 983048 | tf_op jit(solution)/shard_map/ppermute | solution.py:113
  19.5 1.8 %collective-permute-done.4 = bf16[128,1280]{1,0:T(8,128)(2,1)} collective-permute-done((bf16[128,1280]{1,0:T(8,128)(2,1)}, bf16[128,1280]{1,0:T(8,128)(2,1)}, u32[]{:S(2)}, u32[]{:S(2)}) %collective-permute-start.4) | collective-permute-done | bytes 327712 | tf_op jit(solution)/shard_map/ppermute | solution.py:105
  21.4 1.0 convolution_add_fusion.2
  22.4 5.5 %collective-permute-done.3 = bf16[128,1280]{1,0:T(8,128)(2,1)S(1)} collective-permute-done((bf16[128,1280]{1,0:T(8,128)(2,1)S(1)}, bf16[128,1280]{1,0:T(8,128)(2,1)S(1)}, u32[]{:S(2)}, u32[]{:S(2)}) %collective-permute-start.3) | collective-permute-done | bytes 327712 | tf_op jit(solution)/shard_map/ppermute | solution.py:113
  27.9 2.0 %convolution_add_fusion.1 = f32[1280,1280]{1,0:T(8,128)S(1)} fusion(f32[1280,1280]{1,0:T(8,128)S(1)} %convolution_add_fusion.2, bf16[128,1280]{1,0:T(8,128)(2,1)S(1)} %collective-permute-done.3, bf16[128,1280]{1,0:T(8,128)(2,1)} %collective-permute-done.4), kind=kOutput, calls=%fused_computation.1 | convolution fusion | flops 421068800 | bytes 13762560 | tf_op jit(solution)/shard_map/dot_general | solution.py:154
  29.9 2.5 %multiply_reduce_fusion = (f32[]{:T(128)}, f32[1280,1280]{1,0:T(8,128)S(1)}) fusion(f32[1280,1280]{1,0:T(8,128)S(1)} %convolution_add_fusion.1, bf16[128,1280]{1,0:T(8,128)(2,1)S(1)} %collective-permute-done.5, bf16[128,1280]{1,0:T(8,128)(2,1)S(1)} %collective-permute-done.6), kind=kOutput, calls=%fused_computation.4 | convolution fusion | flops 425984000 | bytes 13762564 | tf_op jit(solution)/shard_map/dot_general | solution.py:154
  32.4 1.7 %collective-permute-start.8 = (f32[1]{0:T(128)}, f32[1]{0:T(128)}, u32[]{:S(2)}, u32[]{:S(2)}) collective-permute-start(f32[1]{0:T(128)} %bitcast.5), channel_id=1, source_target_pairs={{0,16},{8,24},{16,0},{24,8},{1,17},{9,25},{17,1},{25,9},{2,18},{10... | collective-permute-start | bytes 20 | tf_op jit(solution)/shard_map/ppermute | solution.py:126
  34.2 0.1 collective-permute-start.9
  35.6 0.6 collective-permute-done.8
  36.2 1.0 collective-permute-done.9
  38.6 0.1 dynamic-slice_multiply_fusion.3
  38.7 1.6 %collective-permute-start.31 = (f32[40,1280]{1,0:T(8,128)S(1)}, f32[40,1280]{1,0:T(8,128)S(1)}, u32[]{:S(2)}, u32[]{:S(2)}) collective-permute-start(f32[40,1280]{1,0:T(8,128)S(1)} %get-tuple-element.81), channel_id=1, source_target_pairs={{0,2},{1,0},{3,1},{5,3},{7,5},{6,7},{4,6},{2,4},{8,10},{9,8},{11,9... | collective-permute-start | bytes 614408 | tf_op jit(solution)/shard_map/ppermute | solution.py:85
  40.3 0.4 collective-permute-start.24
  40.8 1.6 %collective-permute-start.17 = (f32[40,1280]{1,0:T(8,128)S(1)}, f32[40,1280]{1,0:T(8,128)S(1)}, u32[]{:S(2)}, u32[]{:S(2)}) collective-permute-start(f32[40,1280]{1,0:T(8,128)S(1)} %get-tuple-element.83), channel_id=1, source_target_pairs={{0,2},{1,0},{3,1},{5,3},{7,5},{6,7},{4,6},{2,4},{8,10},{9,8},{11,9... | collective-permute-start | bytes 614408 | tf_op jit(solution)/shard_map/ppermute | solution.py:85
  42.3 0.4 collective-permute-start.10
  42.9 0.1 broadcast_in_dim.2
  43.0 1.2 %fusion.4 = bf16[512,1280]{1,0:T(8,128)(2,1)S(1)} fusion(bf16[512,1280]{1,0:T(8,128)(2,1)S(1)} %broadcast_in_dim.2, s32[]{:T(128)S(6)} %select_n.859, bf16[128,1280]{1,0:T(8,128)(2,1)S(1)} %bitcast.116, bf16[1280,1280]{1,0:T(8,128)(2,1)S(1)} %copy-done), kind=kOutput, calls=%fused_computation.12 | convolution fusion | flops 419594240 | bytes 3932164 | tf_op jit(solution)/shard_map/dot_general | solution.py:17
  44.2 1.2 %fusion.3 = bf16[512,1280]{1,0:T(8,128)(2,1)S(1)} fusion(bf16[512,1280]{1,0:T(8,128)(2,1)S(1)} %fusion.4, s32[]{:T(128)S(6)} %select_n.860, bf16[128,1280]{1,0:T(8,128)(2,1)S(1)} %collective-permute-done.2, bf16[1280,1280]{1,0:T(8,128)(2,1)S(1)} %copy-done), kind=kOutput, calls=%fused_computation.10 | convolution fusion | flops 419594240 | bytes 3932164 | tf_op jit(solution)/shard_map/dot_general | solution.py:17
  45.4 2.2 %fusion.2 = bf16[512,1280]{1,0:T(8,128)(2,1)S(1)} fusion(bf16[512,1280]{1,0:T(8,128)(2,1)S(1)} %fusion.3, s32[]{:T(128)S(6)} %select_n.861, bf16[128,1280]{1,0:T(8,128)(2,1)} %collective-permute-done.4, bf16[1280,1280]{1,0:T(8,128)(2,1)S(1)} %copy-done), kind=kOutput, calls=%fused_computation.8 | convolution fusion | flops 419594240 | bytes 3932164 | tf_op jit(solution)/shard_map/dot_general | solution.py:17
  47.6 1.2 %fusion.1 = bf16[512,1280]{1,0:T(8,128)(2,1)S(1)} fusion(bf16[512,1280]{1,0:T(8,128)(2,1)S(1)} %fusion.2, s32[]{:T(128)S(6)} %select_n.862, bf16[128,1280]{1,0:T(8,128)(2,1)S(1)} %collective-permute-done.6, bf16[1280,1280]{1,0:T(8,128)(2,1)S(1)} %copy-done), kind=kOutput, calls=%fused_computation.6 | convolution fusion | flops 419594240 | bytes 3932164 | tf_op jit(solution)/shard_map/dot_general | solution.py:17
  48.9 1.6 %collective-permute-start.32 = (f32[40,1280]{1,0:T(8,128)S(1)}, f32[40,1280]{1,0:T(8,128)S(1)}, u32[]{:S(2)}, u32[]{:S(2)}) collective-permute-start(f32[40,1280]{1,0:T(8,128)S(1)} %add.603), channel_id=1, source_target_pairs={{0,2},{1,0},{3,1},{5,3},{7,5},{6,7},{4,6},{2,4},{8,10},{9,8},{11,9... | collective-permute-start | bytes 614408 | tf_op jit(solution)/shard_map/ppermute | solution.py:85
  50.5 0.5 collective-permute-start.25
  51.1 1.6 %collective-permute-start.18 = (f32[40,1280]{1,0:T(8,128)S(1)}, f32[40,1280]{1,0:T(8,128)S(1)}, u32[]{:S(2)}, u32[]{:S(2)}) collective-permute-start(f32[40,1280]{1,0:T(8,128)S(1)} %add.545), channel_id=1, source_target_pairs={{0,2},{1,0},{3,1},{5,3},{7,5},{6,7},{4,6},{2,4},{8,10},{9,8},{11,9... | collective-permute-start | bytes 614408 | tf_op jit(solution)/shard_map/ppermute | solution.py:85
  52.7 0.5 collective-permute-start.11
  53.3 3.6 %collective-permute-done.32 = f32[40,1280]{1,0:T(8,128)S(1)} collective-permute-done((f32[40,1280]{1,0:T(8,128)S(1)}, f32[40,1280]{1,0:T(8,128)S(1)}, u32[]{:S(2)}, u32[]{:S(2)}) %collective-permute-start.32) | collective-permute-done | bytes 204832 | tf_op jit(solution)/shard_map/ppermute | solution.py:85
  57.0 1.6 %collective-permute-start.33 = (f32[40,1280]{1,0:T(8,128)S(1)}, f32[40,1280]{1,0:T(8,128)S(1)}, u32[]{:S(2)}, u32[]{:S(2)}) collective-permute-start(f32[40,1280]{1,0:T(8,128)S(1)} %add.606), channel_id=1, source_target_pairs={{0,2},{1,0},{3,1},{5,3},{7,5},{6,7},{4,6},{2,4},{8,10},{9,8},{11,9... | collective-permute-start | bytes 614408 | tf_op jit(solution)/shard_map/ppermute | solution.py:85
  58.6 0.5 collective-permute-start.26
  59.1 2.2 %collective-permute-done.18 = f32[40,1280]{1,0:T(8,128)S(1)} collective-permute-done((f32[40,1280]{1,0:T(8,128)S(1)}, f32[40,1280]{1,0:T(8,128)S(1)}, u32[]{:S(2)}, u32[]{:S(2)}) %collective-permute-start.18) | collective-permute-done | bytes 204832 | tf_op jit(solution)/shard_map/ppermute | solution.py:85
  61.4 1.6 %collective-permute-start.19 = (f32[40,1280]{1,0:T(8,128)S(1)}, f32[40,1280]{1,0:T(8,128)S(1)}, u32[]{:S(2)}, u32[]{:S(2)}) collective-permute-start(f32[40,1280]{1,0:T(8,128)S(1)} %add.550), channel_id=1, source_target_pairs={{0,2},{1,0},{3,1},{5,3},{7,5},{6,7},{4,6},{2,4},{8,10},{9,8},{11,9... | collective-permute-start | bytes 614408 | tf_op jit(solution)/shard_map/ppermute | solution.py:85
  63.0 0.5 collective-permute-start.12
  63.6 2.1 %collective-permute-done.33 = f32[40,1280]{1,0:T(8,128)S(1)} collective-permute-done((f32[40,1280]{1,0:T(8,128)S(1)}, f32[40,1280]{1,0:T(8,128)S(1)}, u32[]{:S(2)}, u32[]{:S(2)}) %collective-permute-start.33) | collective-permute-done | bytes 204832 | tf_op jit(solution)/shard_map/ppermute | solution.py:85
  65.7 1.6 %collective-permute-start.34 = (f32[40,1280]{1,0:T(8,128)S(1)}, f32[40,1280]{1,0:T(8,128)S(1)}, u32[]{:S(2)}, u32[]{:S(2)}) collective-permute-start(f32[40,1280]{1,0:T(8,128)S(1)} %add.609), channel_id=1, source_target_pairs={{0,2},{1,0},{3,1},{5,3},{7,5},{6,7},{4,6},{2,4},{8,10},{9,8},{11,9... | collective-permute-start | bytes 614408 | tf_op jit(solution)/shard_map/ppermute | solution.py:85
  67.4 0.5 collective-permute-start.27
  67.9 2.2 %collective-permute-done.19 = f32[40,1280]{1,0:T(8,128)S(1)} collective-permute-done((f32[40,1280]{1,0:T(8,128)S(1)}, f32[40,1280]{1,0:T(8,128)S(1)}, u32[]{:S(2)}, u32[]{:S(2)}) %collective-permute-start.19) | collective-permute-done | bytes 204832 | tf_op jit(solution)/shard_map/ppermute | solution.py:85
  70.1 1.6 %collective-permute-start.20 = (f32[40,1280]{1,0:T(8,128)S(1)}, f32[40,1280]{1,0:T(8,128)S(1)}, u32[]{:S(2)}, u32[]{:S(2)}) collective-permute-start(f32[40,1280]{1,0:T(8,128)S(1)} %add.555), channel_id=1, source_target_pairs={{0,2},{1,0},{3,1},{5,3},{7,5},{6,7},{4,6},{2,4},{8,10},{9,8},{11,9... | collective-permute-start | bytes 614408 | tf_op jit(solution)/shard_map/ppermute | solution.py:85
  71.8 0.5 collective-permute-start.13
  72.4 2.1 %collective-permute-done.34 = f32[40,1280]{1,0:T(8,128)S(1)} collective-permute-done((f32[40,1280]{1,0:T(8,128)S(1)}, f32[40,1280]{1,0:T(8,128)S(1)}, u32[]{:S(2)}, u32[]{:S(2)}) %collective-permute-start.34) | collective-permute-done | bytes 204832 | tf_op jit(solution)/shard_map/ppermute | solution.py:85
  74.5 1.6 %collective-permute-start.35 = (f32[40,1280]{1,0:T(8,128)S(1)}, f32[40,1280]{1,0:T(8,128)S(1)}, u32[]{:S(2)}, u32[]{:S(2)}) collective-permute-start(f32[40,1280]{1,0:T(8,128)S(1)} %add.612), channel_id=1, source_target_pairs={{0,2},{1,0},{3,1},{5,3},{7,5},{6,7},{4,6},{2,4},{8,10},{9,8},{11,9... | collective-permute-start | bytes 614408 | tf_op jit(solution)/shard_map/ppermute | solution.py:85
  76.2 0.5 collective-permute-start.28
  76.7 2.2 %collective-permute-done.20 = f32[40,1280]{1,0:T(8,128)S(1)} collective-permute-done((f32[40,1280]{1,0:T(8,128)S(1)}, f32[40,1280]{1,0:T(8,128)S(1)}, u32[]{:S(2)}, u32[]{:S(2)}) %collective-permute-start.20) | collective-permute-done | bytes 204832 | tf_op jit(solution)/shard_map/ppermute | solution.py:85
  78.9 1.6 %collective-permute-start.21 = (f32[40,1280]{1,0:T(8,128)S(1)}, f32[40,1280]{1,0:T(8,128)S(1)}, u32[]{:S(2)}, u32[]{:S(2)}) collective-permute-start(f32[40,1280]{1,0:T(8,128)S(1)} %add.560), channel_id=1, source_target_pairs={{0,2},{1,0},{3,1},{5,3},{7,5},{6,7},{4,6},{2,4},{8,10},{9,8},{11,9... | collective-permute-start | bytes 614408 | tf_op jit(solution)/shard_map/ppermute | solution.py:85
  80.6 0.5 collective-permute-start.14
  81.2 2.0 %collective-permute-done.35 = f32[40,1280]{1,0:T(8,128)S(1)} collective-permute-done((f32[40,1280]{1,0:T(8,128)S(1)}, f32[40,1280]{1,0:T(8,128)S(1)}, u32[]{:S(2)}, u32[]{:S(2)}) %collective-permute-start.35) | collective-permute-done | bytes 204832 | tf_op jit(solution)/shard_map/ppermute | solution.py:85
  83.3 1.6 %collective-permute-start.36 = (f32[40,1280]{1,0:T(8,128)S(1)}, f32[40,1280]{1,0:T(8,128)S(1)}, u32[]{:S(2)}, u32[]{:S(2)}) collective-permute-start(f32[40,1280]{1,0:T(8,128)S(1)} %add.615), channel_id=1, source_target_pairs={{0,2},{1,0},{3,1},{5,3},{7,5},{6,7},{4,6},{2,4},{8,10},{9,8},{11,9... | collective-permute-start | bytes 614408 | tf_op jit(solution)/shard_map/ppermute | solution.py:85
  85.0 0.5 collective-permute-start.29
  85.5 2.2 %collective-permute-done.21 = f32[40,1280]{1,0:T(8,128)S(1)} collective-permute-done((f32[40,1280]{1,0:T(8,128)S(1)}, f32[40,1280]{1,0:T(8,128)S(1)}, u32[]{:S(2)}, u32[]{:S(2)}) %collective-permute-start.21) | collective-permute-done | bytes 204832 | tf_op jit(solution)/shard_map/ppermute | solution.py:85
  87.7 1.6 %collective-permute-start.22 = (f32[40,1280]{1,0:T(8,128)S(1)}, f32[40,1280]{1,0:T(8,128)S(1)}, u32[]{:S(2)}, u32[]{:S(2)}) collective-permute-start(f32[40,1280]{1,0:T(8,128)S(1)} %add.565), channel_id=1, source_target_pairs={{0,2},{1,0},{3,1},{5,3},{7,5},{6,7},{4,6},{2,4},{8,10},{9,8},{11,9... | collective-permute-start | bytes 614408 | tf_op jit(solution)/shard_map/ppermute | solution.py:85
  89.4 0.5 collective-permute-start.15
  90.0 2.1 %collective-permute-done.36 = f32[40,1280]{1,0:T(8,128)S(1)} collective-permute-done((f32[40,1280]{1,0:T(8,128)S(1)}, f32[40,1280]{1,0:T(8,128)S(1)}, u32[]{:S(2)}, u32[]{:S(2)}) %collective-permute-start.36) | collective-permute-done | bytes 204832 | tf_op jit(solution)/shard_map/ppermute | solution.py:85
  92.1 1.6 %collective-permute-start.37 = (f32[40,1280]{1,0:T(8,128)S(1)}, f32[40,1280]{1,0:T(8,128)S(1)}, u32[]{:S(2)}, u32[]{:S(2)}) collective-permute-start(f32[40,1280]{1,0:T(8,128)S(1)} %add.618), channel_id=1, source_target_pairs={{0,2},{1,0},{3,1},{5,3},{7,5},{6,7},{4,6},{2,4},{8,10},{9,8},{11,9... | collective-permute-start | bytes 614408 | tf_op jit(solution)/shard_map/ppermute | solution.py:85
  93.7 0.5 collective-permute-start.30
  94.2 2.2 %collective-permute-done.22 = f32[40,1280]{1,0:T(8,128)S(1)} collective-permute-done((f32[40,1280]{1,0:T(8,128)S(1)}, f32[40,1280]{1,0:T(8,128)S(1)}, u32[]{:S(2)}, u32[]{:S(2)}) %collective-permute-start.22) | collective-permute-done | bytes 204832 | tf_op jit(solution)/shard_map/ppermute | solution.py:85
  96.5 1.6 %collective-permute-start.23 = (f32[40,1280]{1,0:T(8,128)S(1)}, f32[40,1280]{1,0:T(8,128)S(1)}, u32[]{:S(2)}, u32[]{:S(2)}) collective-permute-start(f32[40,1280]{1,0:T(8,128)S(1)} %add.570), channel_id=1, source_target_pairs={{0,2},{1,0},{3,1},{5,3},{7,5},{6,7},{4,6},{2,4},{8,10},{9,8},{11,9... | collective-permute-start | bytes 614408 | tf_op jit(solution)/shard_map/ppermute | solution.py:85
  98.1 0.5 collective-permute-start.16
  98.7 2.1 %collective-permute-done.37 = f32[40,1280]{1,0:T(8,128)S(1)} collective-permute-done((f32[40,1280]{1,0:T(8,128)S(1)}, f32[40,1280]{1,0:T(8,128)S(1)}, u32[]{:S(2)}, u32[]{:S(2)}) %collective-permute-start.37) | collective-permute-done | bytes 204832 | tf_op jit(solution)/shard_map/ppermute | solution.py:85
  100.8 1.6 %collective-permute-done.30 = f32[40,1280]{1,0:T(8,128)S(1)} collective-permute-done((f32[40,1280]{1,0:T(8,128)S(1)}, f32[40,1280]{1,0:T(8,128)S(1)}, u32[]{:S(2)}, u32[]{:S(2)}) %collective-permute-start.30) | collective-permute-done | bytes 204832 | tf_op jit(solution)/shard_map/ppermute | solution.py:85
  102.5 0.9 collective-permute-done.23
  103.5 1.4 %collective-permute-done.16 = f32[40,1280]{1,0:T(8,128)S(1)} collective-permute-done((f32[40,1280]{1,0:T(8,128)S(1)}, f32[40,1280]{1,0:T(8,128)S(1)}, u32[]{:S(2)}, u32[]{:S(2)}) %collective-permute-start.16) | collective-permute-done | bytes 204832 | tf_op jit(solution)/shard_map/ppermute | solution.py:85
  104.9 2.0 %add_divide_fusion = (f32[160,1280]{1,0:T(8,128)}, f32[160,1280]{1,0:T(8,128)}, f32[160,1280]{1,0:T(8,128)}, f32[160,1280]{1,0:T(8,128)}) fusion(f32[160,1280]{1,0:T(8,128)S(1)} %copy-done.3, f32[160,1280]{1,0:T(8,128)S(1)} %copy-done.4, f32[160,1280]{1,0:T(8,128)S(1)} %copy-done.5, f32[40,1280]{1,0:T(8,128)S(1)} %add.621, f32[40,1280]{1,0:T(8,128)S(1)} %add.598, ...), kind=kLoop, calls=%fused_computation.16 | loop fusion | flops 3481600 | bytes 6553600 | tf_op jit(solution)/shard_map/div | solution.py:202
  (94 shorter events, 1.5 us)
Async XLA Ops:
  0.6 42.4 %copy-start = (bf16[1280,1280]{1,0:T(8,128)(2,1)S(1)}, bf16[1280,1280]{1,0:T(8,128)(2,1)}, u32[]{:S(2)}) copy-start(bf16[1280,1280]{1,0:T(8,128)(2,1)} %param.8) | copy-start | bytes 9830404
  3.0 11.8 %collective-permute-start = (bf16[128,1280]{1,0:T(8,128)(2,1)}, bf16[128,1280]{1,0:T(8,128)(2,1)}, u32[]{:S(2)}, u32[]{:S(2)}) collective-permute-start(bf16[128,1280]{1,0:T(8,128)(2,1)} %get-tuple-element.85), channel_id=1, source_target_pairs={{0,16},{8,24},{16,0},{24,8},{1,17},{9,25},{17,1},{25,9},{2,18},{10... | collective-permute-start | bytes 983048 | tf_op jit(solution)/shard_map/ppermute | solution.py:106
  5.9 15.4 %collective-permute-start.4 = (bf16[128,1280]{1,0:T(8,128)(2,1)}, bf16[128,1280]{1,0:T(8,128)(2,1)}, u32[]{:S(2)}, u32[]{:S(2)}) collective-permute-start(bf16[128,1280]{1,0:T(8,128)(2,1)} %bitcast.114), channel_id=1, source_target_pairs={{0,16},{8,24},{16,0},{24,8},{1,17},{9,25},{17,1},{25,9},{2,18},{10... | collective-permute-start | bytes 983048 | tf_op jit(solution)/shard_map/ppermute | solution.py:105
  5.9 11.4 %copy-start.6 = (bf16[128,1280]{1,0:T(8,128)(2,1)S(1)}, bf16[128,1280]{1,0:T(8,128)(2,1)}, u32[]{:S(2)}) copy-start(bf16[128,1280]{1,0:T(8,128)(2,1)} %get-tuple-element.43) | copy-start | bytes 983044
  14.8 6.6 %collective-permute-start.1 = (bf16[128,1280]{1,0:T(8,128)(2,1)}, bf16[128,1280]{1,0:T(8,128)(2,1)S(1)}, u32[]{:S(2)}, u32[]{:S(2)}) collective-permute-start(bf16[128,1280]{1,0:T(8,128)(2,1)} %get-tuple-element.41), channel_id=1, source_target_pairs={{0,8},{8,0},{16,24},{24,16},{1,9},{9,1},{17,25},{25,17},{2,10},{10... | collective-permute-start | bytes 983048 | tf_op jit(solution)/shard_map/ppermute | solution.py:109
  14.8 6.6 %collective-permute-start.2 = (bf16[128,1280]{1,0:T(8,128)(2,1)}, bf16[128,1280]{1,0:T(8,128)(2,1)S(1)}, u32[]{:S(2)}, u32[]{:S(2)}) collective-permute-start(bf16[128,1280]{1,0:T(8,128)(2,1)} %bitcast.115), channel_id=1, source_target_pairs={{0,8},{8,0},{16,24},{24,16},{1,9},{9,1},{17,25},{25,17},{2,10},{10... | collective-permute-start | bytes 983048 | tf_op jit(solution)/shard_map/ppermute | solution.py:108
  17.4 10.5 %collective-permute-start.3 = (bf16[128,1280]{1,0:T(8,128)(2,1)S(1)}, bf16[128,1280]{1,0:T(8,128)(2,1)S(1)}, u32[]{:S(2)}, u32[]{:S(2)}) collective-permute-start(bf16[128,1280]{1,0:T(8,128)(2,1)S(1)} %copy-done.6), channel_id=1, source_target_pairs={{0,16},{8,24},{16,0},{24,8},{1,17},{9,25},{17,1},{25,9},{2,18},{10... | collective-permute-start | bytes 983048 | tf_op jit(solution)/shard_map/ppermute | solution.py:113
  19.5 10.4 %collective-permute-start.5 = (bf16[128,1280]{1,0:T(8,128)(2,1)}, bf16[128,1280]{1,0:T(8,128)(2,1)S(1)}, u32[]{:S(2)}, u32[]{:S(2)}) collective-permute-start(bf16[128,1280]{1,0:T(8,128)(2,1)} %collective-permute-done), channel_id=1, source_target_pairs={{0,8},{8,0},{16,24},{24,16},{1,9},{9,1},{17,25},{25,17},{2,10},{10... | collective-permute-start | bytes 983048 | tf_op jit(solution)/shard_map/ppermute | solution.py:111
  21.3 8.6 %collective-permute-start.6 = (bf16[128,1280]{1,0:T(8,128)(2,1)}, bf16[128,1280]{1,0:T(8,128)(2,1)S(1)}, u32[]{:S(2)}, u32[]{:S(2)}) collective-permute-start(bf16[128,1280]{1,0:T(8,128)(2,1)} %collective-permute-done.4), channel_id=1, source_target_pairs={{0,8},{8,0},{16,24},{24,16},{1,9},{9,1},{17,25},{25,17},{2,10},{10... | collective-permute-start | bytes 983048 | tf_op jit(solution)/shard_map/ppermute | solution.py:110
  29.9 13.1 %copy-start.1 = (bf16[1,1,128,1280]{3,2,1,0:T(8,128)(2,1)S(1)}, bf16[1,1,128,1280]{3,2,1,0:T(8,128)(2,1)}, u32[]{:S(2)}) copy-start(bf16[1,1,128,1280]{3,2,1,0:T(8,128)(2,1)} %param.7) | copy-start | bytes 983044
  32.4 1.9 %collective-permute-start.7 = (f32[1]{0:T(128)}, f32[1]{0:T(128)}, u32[]{:S(2)}, u32[]{:S(2)}) collective-permute-start(f32[1]{0:T(128)} %bitcast.5), channel_id=1, source_target_pairs={{0,8},{8,0},{16,24},{24,16},{1,9},{9,1},{17,25},{25,17},{2,10},{10... | collective-permute-start | bytes 20 | tf_op jit(solution)/shard_map/ppermute | solution.py:126
  32.4 3.8 %collective-permute-start.8 = (f32[1]{0:T(128)}, f32[1]{0:T(128)}, u32[]{:S(2)}, u32[]{:S(2)}) collective-permute-start(f32[1]{0:T(128)} %bitcast.5), channel_id=1, source_target_pairs={{0,16},{8,24},{16,0},{24,8},{1,17},{9,25},{17,1},{25,9},{2,18},{10... | collective-permute-start | bytes 20 | tf_op jit(solution)/shard_map/ppermute | solution.py:126
  34.2 3.1 %collective-permute-start.9 = (f32[1]{0:T(128)}, f32[1]{0:T(128)}, u32[]{:S(2)}, u32[]{:S(2)}) collective-permute-start(f32[1]{0:T(128)} %bitcast.5), channel_id=1, source_target_pairs={{0,24},{8,16},{16,8},{24,0},{1,25},{9,17},{17,9},{25,1},{2,26},{10... | collective-permute-start | bytes 20 | tf_op jit(solution)/shard_map/ppermute | solution.py:126
  38.7 10.2 %collective-permute-start.31 = (f32[40,1280]{1,0:T(8,128)S(1)}, f32[40,1280]{1,0:T(8,128)S(1)}, u32[]{:S(2)}, u32[]{:S(2)}) collective-permute-start(f32[40,1280]{1,0:T(8,128)S(1)} %get-tuple-element.81), channel_id=1, source_target_pairs={{0,2},{1,0},{3,1},{5,3},{7,5},{6,7},{4,6},{2,4},{8,10},{9,8},{11,9... | collective-permute-start | bytes 614408 | tf_op jit(solution)/shard_map/ppermute | solution.py:85
  40.3 10.2 %collective-permute-start.24 = (f32[40,1280]{1,0:T(8,128)S(1)}, f32[40,1280]{1,0:T(8,128)S(1)}, u32[]{:S(2)}, u32[]{:S(2)}) collective-permute-start(f32[40,1280]{1,0:T(8,128)S(1)} %get-tuple-element.82), channel_id=1, source_target_pairs={{0,1},{1,3},{3,5},{5,7},{7,6},{6,4},{4,2},{2,0},{8,9},{9,11},{11,1... | collective-permute-start | bytes 614408 | tf_op jit(solution)/shard_map/ppermute | solution.py:85
  40.8 10.3 %collective-permute-start.17 = (f32[40,1280]{1,0:T(8,128)S(1)}, f32[40,1280]{1,0:T(8,128)S(1)}, u32[]{:S(2)}, u32[]{:S(2)}) collective-permute-start(f32[40,1280]{1,0:T(8,128)S(1)} %get-tuple-element.83), channel_id=1, source_target_pairs={{0,2},{1,0},{3,1},{5,3},{7,5},{6,7},{4,6},{2,4},{8,10},{9,8},{11,9... | collective-permute-start | bytes 614408 | tf_op jit(solution)/shard_map/ppermute | solution.py:85
  42.3 10.4 %collective-permute-start.10 = (f32[40,1280]{1,0:T(8,128)S(1)}, f32[40,1280]{1,0:T(8,128)S(1)}, u32[]{:S(2)}, u32[]{:S(2)}) collective-permute-start(f32[40,1280]{1,0:T(8,128)S(1)} %get-tuple-element.80), channel_id=1, source_target_pairs={{0,1},{1,3},{3,5},{5,7},{7,6},{6,4},{4,2},{2,0},{8,9},{9,11},{11,1... | collective-permute-start | bytes 614408 | tf_op jit(solution)/shard_map/ppermute | solution.py:85
  48.8 27.4 %copy-start.2 = (bf16[512,1280]{1,0:T(8,128)(2,1)}, bf16[512,1280]{1,0:T(8,128)(2,1)S(1)}, u32[]{:S(2)}) copy-start(bf16[512,1280]{1,0:T(8,128)(2,1)S(1)} %fusion.1) | copy-start | bytes 3932164
  48.9 8.1 %collective-permute-start.32 = (f32[40,1280]{1,0:T(8,128)S(1)}, f32[40,1280]{1,0:T(8,128)S(1)}, u32[]{:S(2)}, u32[]{:S(2)}) collective-permute-start(f32[40,1280]{1,0:T(8,128)S(1)} %add.603), channel_id=1, source_target_pairs={{0,2},{1,0},{3,1},{5,3},{7,5},{6,7},{4,6},{2,4},{8,10},{9,8},{11,9... | collective-permute-start | bytes 614408 | tf_op jit(solution)/shard_map/ppermute | solution.py:85
  50.5 8.1 %collective-permute-start.25 = (f32[40,1280]{1,0:T(8,128)S(1)}, f32[40,1280]{1,0:T(8,128)S(1)}, u32[]{:S(2)}, u32[]{:S(2)}) collective-permute-start(f32[40,1280]{1,0:T(8,128)S(1)} %add.580), channel_id=1, source_target_pairs={{0,1},{1,3},{3,5},{5,7},{7,6},{6,4},{4,2},{2,0},{8,9},{9,11},{11,1... | collective-permute-start | bytes 614408 | tf_op jit(solution)/shard_map/ppermute | solution.py:85
  51.1 10.3 %collective-permute-start.18 = (f32[40,1280]{1,0:T(8,128)S(1)}, f32[40,1280]{1,0:T(8,128)S(1)}, u32[]{:S(2)}, u32[]{:S(2)}) collective-permute-start(f32[40,1280]{1,0:T(8,128)S(1)} %add.545), channel_id=1, source_target_pairs={{0,2},{1,0},{3,1},{5,3},{7,5},{6,7},{4,6},{2,4},{8,10},{9,8},{11,9... | collective-permute-start | bytes 614408 | tf_op jit(solution)/shard_map/ppermute | solution.py:85
  52.7 10.3 %collective-permute-start.11 = (f32[40,1280]{1,0:T(8,128)S(1)}, f32[40,1280]{1,0:T(8,128)S(1)}, u32[]{:S(2)}, u32[]{:S(2)}) collective-permute-start(f32[40,1280]{1,0:T(8,128)S(1)} %add.518), channel_id=1, source_target_pairs={{0,1},{1,3},{3,5},{5,7},{7,6},{6,4},{4,2},{2,0},{8,9},{9,11},{11,1... | collective-permute-start | bytes 614408 | tf_op jit(solution)/shard_map/ppermute | solution.py:85
  57.0 8.7 %collective-permute-start.33 = (f32[40,1280]{1,0:T(8,128)S(1)}, f32[40,1280]{1,0:T(8,128)S(1)}, u32[]{:S(2)}, u32[]{:S(2)}) collective-permute-start(f32[40,1280]{1,0:T(8,128)S(1)} %add.606), channel_id=1, source_target_pairs={{0,2},{1,0},{3,1},{5,3},{7,5},{6,7},{4,6},{2,4},{8,10},{9,8},{11,9... | collective-permute-start | bytes 614408 | tf_op jit(solution)/shard_map/ppermute | solution.py:85
  58.6 8.7 %collective-permute-start.26 = (f32[40,1280]{1,0:T(8,128)S(1)}, f32[40,1280]{1,0:T(8,128)S(1)}, u32[]{:S(2)}, u32[]{:S(2)}) collective-permute-start(f32[40,1280]{1,0:T(8,128)S(1)} %add.583), channel_id=1, source_target_pairs={{0,1},{1,3},{3,5},{5,7},{7,6},{6,4},{4,2},{2,0},{8,9},{9,11},{11,1... | collective-permute-start | bytes 614408 | tf_op jit(solution)/shard_map/ppermute | solution.py:85
  61.4 8.8 %collective-permute-start.19 = (f32[40,1280]{1,0:T(8,128)S(1)}, f32[40,1280]{1,0:T(8,128)S(1)}, u32[]{:S(2)}, u32[]{:S(2)}) collective-permute-start(f32[40,1280]{1,0:T(8,128)S(1)} %add.550), channel_id=1, source_target_pairs={{0,2},{1,0},{3,1},{5,3},{7,5},{6,7},{4,6},{2,4},{8,10},{9,8},{11,9... | collective-permute-start | bytes 614408 | tf_op jit(solution)/shard_map/ppermute | solution.py:85
  63.0 8.8 %collective-permute-start.12 = (f32[40,1280]{1,0:T(8,128)S(1)}, f32[40,1280]{1,0:T(8,128)S(1)}, u32[]{:S(2)}, u32[]{:S(2)}) collective-permute-start(f32[40,1280]{1,0:T(8,128)S(1)} %add.521), channel_id=1, source_target_pairs={{0,1},{1,3},{3,5},{5,7},{7,6},{6,4},{4,2},{2,0},{8,9},{9,11},{11,1... | collective-permute-start | bytes 614408 | tf_op jit(solution)/shard_map/ppermute | solution.py:85
  65.7 8.8 %collective-permute-start.34 = (f32[40,1280]{1,0:T(8,128)S(1)}, f32[40,1280]{1,0:T(8,128)S(1)}, u32[]{:S(2)}, u32[]{:S(2)}) collective-permute-start(f32[40,1280]{1,0:T(8,128)S(1)} %add.609), channel_id=1, source_target_pairs={{0,2},{1,0},{3,1},{5,3},{7,5},{6,7},{4,6},{2,4},{8,10},{9,8},{11,9... | collective-permute-start | bytes 614408 | tf_op jit(solution)/shard_map/ppermute | solution.py:85
  67.4 8.7 %collective-permute-start.27 = (f32[40,1280]{1,0:T(8,128)S(1)}, f32[40,1280]{1,0:T(8,128)S(1)}, u32[]{:S(2)}, u32[]{:S(2)}) collective-permute-start(f32[40,1280]{1,0:T(8,128)S(1)} %add.586), channel_id=1, source_target_pairs={{0,1},{1,3},{3,5},{5,7},{7,6},{6,4},{4,2},{2,0},{8,9},{9,11},{11,1... | collective-permute-start | bytes 614408 | tf_op jit(solution)/shard_map/ppermute | solution.py:85
  70.1 8.7 %collective-permute-start.20 = (f32[40,1280]{1,0:T(8,128)S(1)}, f32[40,1280]{1,0:T(8,128)S(1)}, u32[]{:S(2)}, u32[]{:S(2)}) collective-permute-start(f32[40,1280]{1,0:T(8,128)S(1)} %add.555), channel_id=1, source_target_pairs={{0,2},{1,0},{3,1},{5,3},{7,5},{6,7},{4,6},{2,4},{8,10},{9,8},{11,9... | collective-permute-start | bytes 614408 | tf_op jit(solution)/shard_map/ppermute | solution.py:85
  71.8 8.8 %collective-permute-start.13 = (f32[40,1280]{1,0:T(8,128)S(1)}, f32[40,1280]{1,0:T(8,128)S(1)}, u32[]{:S(2)}, u32[]{:S(2)}) collective-permute-start(f32[40,1280]{1,0:T(8,128)S(1)} %add.524), channel_id=1, source_target_pairs={{0,1},{1,3},{3,5},{5,7},{7,6},{6,4},{4,2},{2,0},{8,9},{9,11},{11,1... | collective-permute-start | bytes 614408 | tf_op jit(solution)/shard_map/ppermute | solution.py:85
  74.5 8.8 %collective-permute-start.35 = (f32[40,1280]{1,0:T(8,128)S(1)}, f32[40,1280]{1,0:T(8,128)S(1)}, u32[]{:S(2)}, u32[]{:S(2)}) collective-permute-start(f32[40,1280]{1,0:T(8,128)S(1)} %add.612), channel_id=1, source_target_pairs={{0,2},{1,0},{3,1},{5,3},{7,5},{6,7},{4,6},{2,4},{8,10},{9,8},{11,9... | collective-permute-start | bytes 614408 | tf_op jit(solution)/shard_map/ppermute | solution.py:85
  76.2 8.7 %collective-permute-start.28 = (f32[40,1280]{1,0:T(8,128)S(1)}, f32[40,1280]{1,0:T(8,128)S(1)}, u32[]{:S(2)}, u32[]{:S(2)}) collective-permute-start(f32[40,1280]{1,0:T(8,128)S(1)} %add.589), channel_id=1, source_target_pairs={{0,1},{1,3},{3,5},{5,7},{7,6},{6,4},{4,2},{2,0},{8,9},{9,11},{11,1... | collective-permute-start | bytes 614408 | tf_op jit(solution)/shard_map/ppermute | solution.py:85
  78.9 25.9 %copy-start.3 = (f32[160,1280]{1,0:T(8,128)S(1)}, f32[160,1280]{1,0:T(8,128)}, u32[]{:S(2)}) copy-start(f32[160,1280]{1,0:T(8,128)} %param.11) | copy-start | bytes 2457604
  78.9 25.9 %copy-start.4 = (f32[160,1280]{1,0:T(8,128)S(1)}, f32[160,1280]{1,0:T(8,128)}, u32[]{:S(2)}) copy-start(f32[160,1280]{1,0:T(8,128)} %param.10) | copy-start | bytes 2457604
  78.9 25.9 %copy-start.5 = (f32[160,1280]{1,0:T(8,128)S(1)}, f32[160,1280]{1,0:T(8,128)}, u32[]{:S(2)}) copy-start(f32[160,1280]{1,0:T(8,128)} %param.9) | copy-start | bytes 2457604
  78.9 8.7 %collective-permute-start.21 = (f32[40,1280]{1,0:T(8,128)S(1)}, f32[40,1280]{1,0:T(8,128)S(1)}, u32[]{:S(2)}, u32[]{:S(2)}) collective-permute-start(f32[40,1280]{1,0:T(8,128)S(1)} %add.560), channel_id=1, source_target_pairs={{0,2},{1,0},{3,1},{5,3},{7,5},{6,7},{4,6},{2,4},{8,10},{9,8},{11,9... | collective-permute-start | bytes 614408 | tf_op jit(solution)/shard_map/ppermute | solution.py:85
  80.6 8.7 %collective-permute-start.14 = (f32[40,1280]{1,0:T(8,128)S(1)}, f32[40,1280]{1,0:T(8,128)S(1)}, u32[]{:S(2)}, u32[]{:S(2)}) collective-permute-start(f32[40,1280]{1,0:T(8,128)S(1)} %add.527), channel_id=1, source_target_pairs={{0,1},{1,3},{3,5},{5,7},{7,6},{6,4},{4,2},{2,0},{8,9},{9,11},{11,1... | collective-permute-start | bytes 614408 | tf_op jit(solution)/shard_map/ppermute | solution.py:85
  83.3 8.7 %collective-permute-start.36 = (f32[40,1280]{1,0:T(8,128)S(1)}, f32[40,1280]{1,0:T(8,128)S(1)}, u32[]{:S(2)}, u32[]{:S(2)}) collective-permute-start(f32[40,1280]{1,0:T(8,128)S(1)} %add.615), channel_id=1, source_target_pairs={{0,2},{1,0},{3,1},{5,3},{7,5},{6,7},{4,6},{2,4},{8,10},{9,8},{11,9... | collective-permute-start | bytes 614408 | tf_op jit(solution)/shard_map/ppermute | solution.py:85
  85.0 8.7 %collective-permute-start.29 = (f32[40,1280]{1,0:T(8,128)S(1)}, f32[40,1280]{1,0:T(8,128)S(1)}, u32[]{:S(2)}, u32[]{:S(2)}) collective-permute-start(f32[40,1280]{1,0:T(8,128)S(1)} %add.592), channel_id=1, source_target_pairs={{0,1},{1,3},{3,5},{5,7},{7,6},{6,4},{4,2},{2,0},{8,9},{9,11},{11,1... | collective-permute-start | bytes 614408 | tf_op jit(solution)/shard_map/ppermute | solution.py:85
  87.7 8.7 %collective-permute-start.22 = (f32[40,1280]{1,0:T(8,128)S(1)}, f32[40,1280]{1,0:T(8,128)S(1)}, u32[]{:S(2)}, u32[]{:S(2)}) collective-permute-start(f32[40,1280]{1,0:T(8,128)S(1)} %add.565), channel_id=1, source_target_pairs={{0,2},{1,0},{3,1},{5,3},{7,5},{6,7},{4,6},{2,4},{8,10},{9,8},{11,9... | collective-permute-start | bytes 614408 | tf_op jit(solution)/shard_map/ppermute | solution.py:85
  89.4 8.7 %collective-permute-start.15 = (f32[40,1280]{1,0:T(8,128)S(1)}, f32[40,1280]{1,0:T(8,128)S(1)}, u32[]{:S(2)}, u32[]{:S(2)}) collective-permute-start(f32[40,1280]{1,0:T(8,128)S(1)} %add.530), channel_id=1, source_target_pairs={{0,1},{1,3},{3,5},{5,7},{7,6},{6,4},{4,2},{2,0},{8,9},{9,11},{11,1... | collective-permute-start | bytes 614408 | tf_op jit(solution)/shard_map/ppermute | solution.py:85
  92.1 8.7 %collective-permute-start.37 = (f32[40,1280]{1,0:T(8,128)S(1)}, f32[40,1280]{1,0:T(8,128)S(1)}, u32[]{:S(2)}, u32[]{:S(2)}) collective-permute-start(f32[40,1280]{1,0:T(8,128)S(1)} %add.618), channel_id=1, source_target_pairs={{0,2},{1,0},{3,1},{5,3},{7,5},{6,7},{4,6},{2,4},{8,10},{9,8},{11,9... | collective-permute-start | bytes 614408 | tf_op jit(solution)/shard_map/ppermute | solution.py:85
  93.7 8.7 %collective-permute-start.30 = (f32[40,1280]{1,0:T(8,128)S(1)}, f32[40,1280]{1,0:T(8,128)S(1)}, u32[]{:S(2)}, u32[]{:S(2)}) collective-permute-start(f32[40,1280]{1,0:T(8,128)S(1)} %add.595), channel_id=1, source_target_pairs={{0,1},{1,3},{3,5},{5,7},{7,6},{6,4},{4,2},{2,0},{8,9},{9,11},{11,1... | collective-permute-start | bytes 614408 | tf_op jit(solution)/shard_map/ppermute | solution.py:85
  96.5 7.0 %collective-permute-start.23 = (f32[40,1280]{1,0:T(8,128)S(1)}, f32[40,1280]{1,0:T(8,128)S(1)}, u32[]{:S(2)}, u32[]{:S(2)}) collective-permute-start(f32[40,1280]{1,0:T(8,128)S(1)} %add.570), channel_id=1, source_target_pairs={{0,2},{1,0},{3,1},{5,3},{7,5},{6,7},{4,6},{2,4},{8,10},{9,8},{11,9... | collective-permute-start | bytes 614408 | tf_op jit(solution)/shard_map/ppermute | solution.py:85
  98.1 6.7 %collective-permute-start.16 = (f32[40,1280]{1,0:T(8,128)S(1)}, f32[40,1280]{1,0:T(8,128)S(1)}, u32[]{:S(2)}, u32[]{:S(2)}) collective-permute-start(f32[40,1280]{1,0:T(8,128)S(1)} %add.533), channel_id=1, source_target_pairs={{0,1},{1,3},{3,5},{5,7},{7,6},{6,4},{4,2},{2,0},{8,9},{9,11},{11,1... | collective-permute-start | bytes 614408 | tf_op jit(solution)/shard_map/ppermute | solution.py:85

commit v14 on v13

--- a/solution.py
+++ b/solution.py
@@ -75,12 +75,12 @@
 
     chains = [(-1 if c % 2 == 0 else 1, c) for c in range(pieces)]
     own = [parts(block(0, step), which, None) for step, which in chains]
-    extra = None
-    if during is not None:
-        extra = during(own)
+    extra = []
     acc = [None] * pieces
     for s in range(n - 1):
         send = [o if x is None else x + o for x, o in zip(acc, own)]
+        if during is not None:
+            extra.append(during(s, send))
         acc = [
             lax.ppermute(v, "dp", right if step < 0 else left)
             for v, (step, _) in zip(send, chains)
@@ -155,13 +155,12 @@
             summed = term if summed is None else summed + term
         summed = summed[None]
 
-        def project_all(after):
-            out = jnp.zeros((views * local_rows, slice_width), jnp.bfloat16)
-            for at, _, g_piece in blocks:
-                _, g_piece = lax.optimization_barrier((after, g_piece))
-                back = project_back(g_piece, down_weight).astype(jnp.bfloat16)
-                out = lax.dynamic_update_slice_in_dim(out, back, at, axis=0)
-            return out.reshape(views, images_here, patches, slice_width)
+        def project_all(step, after):
+            if step >= len(blocks):
+                return None
+            at, _, g_piece = blocks[step]
+            _, g_piece = lax.optimization_barrier((after, g_piece))
+            return at, project_back(g_piece, down_weight).astype(jnp.bfloat16)
 
         hidden_grad = None
     else:
@@ -193,7 +192,11 @@
 
     owned, deferred = ring_reduce_scatter(parts, ring, pieces, project_all)
     if hidden_grad is None:
-        hidden_grad = deferred
+        out = jnp.zeros((views * local_rows, slice_width), jnp.bfloat16)
+        for item in deferred:
+            if item is not None:
+                out = lax.dynamic_update_slice_in_dim(out, item[1], item[0], axis=0)
+        hidden_grad = out.reshape(views, images_here, patches, slice_width)
     clipped_mean = owned / images_all
     noisy = clipped_mean + noise_ratio * clip * noise / images_all
     new_first = beta_one * first_moment + (1.0 - beta_one) * noisy

time: 108 us -> 108 us (level)
  transfers between devices with their start and end apart: 38 -> 38, of which waited for: 19 -> 20; matrix products, arithmetic and copies ran while one was open for 11% -> 12% of each run, Pallas kernels for 0% -> 0%
where the time goes in v14:
time: 108 us; the launch traced here: 107 us
  waiting for transfers between devices  45.7 us (42%)
  starting transfers between devices  37.4 us (35%)
  matrix products  13.4 us (12%)
  between operations  4.89 us (5%)
  other arithmetic  3.47 us (3%)
  local copies, waits for them, and re-layouts  2.43 us (2%)
    ppermute x28, starting transfers between devices, ring_reduce_scatter(): lax.ppermute(v, 'dp', right if step < 0 else left)  29.7 us
    ppermute x28, waiting for transfers between devices, ring_reduce_scatter(): lax.ppermute(v, 'dp', right if step < 0 else left)  28.1 us
    ppermute x1, waiting for transfers between devices, exchange_four(): h_far_relay = lax.ppermute(cols(a ^ 3), 'aug', over_x)  8.81 us
    dot_general x4, matrix products, per_device(): term = jnp.dot(h_piece.T, g_piece, preferred_element_type=jnp.float32)  7.67 us
    dot_general x4, matrix products, project_back(): lax.dot_general(rows, down_weight, (((1,), (1,)), ((), ())), preferred_el...  5.78 us
    ppermute x1, waiting for transfers between devices, exchange_four(): h_far = lax.ppermute(second, 'aug', over_x)  5.45 us
    ppermute x1, starting transfers between devices, exchange_four(): h_far_relay = lax.ppermute(cols(a ^ 3), 'aug', over_x)  2.94 us
    dynamic_slice x1, local copies, waits for them, and re-layouts, cols(): return lax.dynamic_slice_in_dim(h_rows, b * sw, sw, axis=1)  2.29 us
  transfers between devices with their start and end apart: 38, of which 20 were waited for; matrix products, arithmetic and copies ran while one was open for 12% of the time, Pallas kernels for 0%

profile of v14, /device:TPU:0, one launch (start us, length us, event | category | flops | bytes accessed | tf_op | source)
XLA Modules:
  0.0 107.3 jit_solution(16975783166588490753)
XLA Ops:
  0.7 2.3 %dynamic-slice_bitcast_fusion = (bf16[128,1280]{1,0:T(8,128)(2,1)}, bf16[128,1280]{1,0:T(8,128)(2,1)}, bf16[128,1280]{1,0:T(8,128)(2,1)}) fusion(bf16[1,1,128,5120]{3,2,1,0:T(8,128)(2,1)} %param.6, s32[]{:T(128)S(6)} %select_n.691, s32[]{:T(128)S(6)} %select_n.689, s32[]{:T(128)S(6)} %select_n.690), kind=kLoop, calls=%fused_computation.21 | loop fusion | bytes 1966092 | tf_op jit(solution)/shard_map/dynamic_slice | solution.py:101
  3.0 2.9 %collective-permute-start = (bf16[128,1280]{1,0:T(8,128)(2,1)}, bf16[128,1280]{1,0:T(8,128)(2,1)}, u32[]{:S(2)}, u32[]{:S(2)}) collective-permute-start(bf16[128,1280]{1,0:T(8,128)(2,1)} %get-tuple-element.85), channel_id=1, source_target_pairs={{0,16},{8,24},{16,0},{24,8},{1,17},{9,25},{17,1},{25,9},{2,18},{10... | collective-permute-start | bytes 983048 | tf_op jit(solution)/shard_map/ppermute | solution.py:106
  5.9 8.8 %collective-permute-done = bf16[128,1280]{1,0:T(8,128)(2,1)} collective-permute-done((bf16[128,1280]{1,0:T(8,128)(2,1)}, bf16[128,1280]{1,0:T(8,128)(2,1)}, u32[]{:S(2)}, u32[]{:S(2)}) %collective-permute-start) | collective-permute-done | bytes 327712 | tf_op jit(solution)/shard_map/ppermute | solution.py:106
  14.8 0.5 collective-permute-start.1
  15.3 2.1 %fusion.6 = f32[1280,1280]{1,0:T(8,128)S(1)} fusion(bf16[1,1,128,5120]{3,2,1,0:T(8,128)(2,1)} %param.6, s32[]{:T(128)S(6)} %select_n.688, bf16[1,1,128,1280]{3,2,1,0:T(8,128)(2,1)} %param.7), kind=kOutput, calls=%fused_computation.19 | convolution fusion | flops 419430400 | bytes 7208964 | tf_op jit(solution)/shard_map/dot_general | solution.py:154
  17.4 2.1 %collective-permute-start.3 = (bf16[128,1280]{1,0:T(8,128)(2,1)S(1)}, bf16[128,1280]{1,0:T(8,128)(2,1)S(1)}, u32[]{:S(2)}, u32[]{:S(2)}) collective-permute-start(bf16[128,1280]{1,0:T(8,128)(2,1)S(1)} %copy-done.6), channel_id=1, source_target_pairs={{0,16},{8,24},{16,0},{24,8},{1,17},{9,25},{17,1},{25,9},{2,18},{10... | collective-permute-start | bytes 983048 | tf_op jit(solution)/shard_map/ppermute | solution.py:113
  19.5 1.8 %collective-permute-done.4 = bf16[128,1280]{1,0:T(8,128)(2,1)} collective-permute-done((bf16[128,1280]{1,0:T(8,128)(2,1)}, bf16[128,1280]{1,0:T(8,128)(2,1)}, u32[]{:S(2)}, u32[]{:S(2)}) %collective-permute-start.4) | collective-permute-done | bytes 327712 | tf_op jit(solution)/shard_map/ppermute | solution.py:105
  21.4 1.0 convolution_add_fusion.2
  22.4 5.5 %collective-permute-done.3 = bf16[128,1280]{1,0:T(8,128)(2,1)S(1)} collective-permute-done((bf16[128,1280]{1,0:T(8,128)(2,1)S(1)}, bf16[128,1280]{1,0:T(8,128)(2,1)S(1)}, u32[]{:S(2)}, u32[]{:S(2)}) %collective-permute-start.3) | collective-permute-done | bytes 327712 | tf_op jit(solution)/shard_map/ppermute | solution.py:113
  27.9 2.0 %convolution_add_fusion.1 = f32[1280,1280]{1,0:T(8,128)S(1)} fusion(f32[1280,1280]{1,0:T(8,128)S(1)} %convolution_add_fusion.2, bf16[128,1280]{1,0:T(8,128)(2,1)S(1)} %collective-permute-done.3, bf16[128,1280]{1,0:T(8,128)(2,1)} %collective-permute-done.4), kind=kOutput, calls=%fused_computation.1 | convolution fusion | flops 421068800 | bytes 13762560 | tf_op jit(solution)/shard_map/dot_general | solution.py:154
  29.9 2.5 %multiply_reduce_fusion = (f32[]{:T(128)}, f32[1280,1280]{1,0:T(8,128)S(1)}) fusion(f32[1280,1280]{1,0:T(8,128)S(1)} %convolution_add_fusion.1, bf16[128,1280]{1,0:T(8,128)(2,1)S(1)} %collective-permute-done.5, bf16[128,1280]{1,0:T(8,128)(2,1)S(1)} %collective-permute-done.6), kind=kOutput, calls=%fused_computation.4 | convolution fusion | flops 425984000 | bytes 13762564 | tf_op jit(solution)/shard_map/dot_general | solution.py:154
  32.4 1.7 %collective-permute-start.8 = (f32[1]{0:T(128)}, f32[1]{0:T(128)}, u32[]{:S(2)}, u32[]{:S(2)}) collective-permute-start(f32[1]{0:T(128)} %bitcast.5), channel_id=1, source_target_pairs={{0,16},{8,24},{16,0},{24,8},{1,17},{9,25},{17,1},{25,9},{2,18},{10... | collective-permute-start | bytes 20 | tf_op jit(solution)/shard_map/ppermute | solution.py:126
  34.2 0.4 collective-permute-start.7
  34.6 1.0 collective-permute-done.7
  36.9 0.5 collective-permute-done.9
  38.7 0.1 dynamic-slice_multiply_fusion.3
  38.8 1.6 %collective-permute-start.10 = (f32[40,1280]{1,0:T(8,128)S(1)}, f32[40,1280]{1,0:T(8,128)S(1)}, u32[]{:S(2)}, u32[]{:S(2)}) collective-permute-start(f32[40,1280]{1,0:T(8,128)S(1)} %get-tuple-element.80), channel_id=1, source_target_pairs={{0,1},{1,3},{3,5},{5,7},{7,6},{6,4},{4,2},{2,0},{8,9},{9,11},{11,1... | collective-permute-start | bytes 614408 | tf_op jit(solution)/shard_map/ppermute | solution.py:85
  40.3 0.5 collective-permute-start.17
  40.8 1.5 %collective-permute-start.24 = (f32[40,1280]{1,0:T(8,128)S(1)}, f32[40,1280]{1,0:T(8,128)S(1)}, u32[]{:S(2)}, u32[]{:S(2)}) collective-permute-start(f32[40,1280]{1,0:T(8,128)S(1)} %get-tuple-element.82), channel_id=1, source_target_pairs={{0,1},{1,3},{3,5},{5,7},{7,6},{6,4},{4,2},{2,0},{8,9},{9,11},{11,1... | collective-permute-start | bytes 614408 | tf_op jit(solution)/shard_map/ppermute | solution.py:85
  42.4 0.5 collective-permute-start.31
  43.1 1.2 %fusion.4 = bf16[512,1280]{1,0:T(8,128)(2,1)S(1)} fusion(bf16[512,1280]{1,0:T(8,128)(2,1)S(1)} %broadcast_in_dim.2, s32[]{:T(128)S(6)} %select_n.859, bf16[128,1280]{1,0:T(8,128)(2,1)S(1)} %bitcast.116, bf16[1280,1280]{1,0:T(8,128)(2,1)S(1)} %copy-done), kind=kOutput, calls=%fused_computation.12 | convolution fusion | flops 419594240 | bytes 3932164 | tf_op jit(solution)/shard_map/dot_general | solution.py:17
  44.3 2.5 %collective-permute-done.10 = f32[40,1280]{1,0:T(8,128)S(1)} collective-permute-done((f32[40,1280]{1,0:T(8,128)S(1)}, f32[40,1280]{1,0:T(8,128)S(1)}, u32[]{:S(2)}, u32[]{:S(2)}) %collective-permute-start.10) | collective-permute-done | bytes 204832 | tf_op jit(solution)/shard_map/ppermute | solution.py:85
  46.8 1.5 %collective-permute-start.11 = (f32[40,1280]{1,0:T(8,128)S(1)}, f32[40,1280]{1,0:T(8,128)S(1)}, u32[]{:S(2)}, u32[]{:S(2)}) collective-permute-start(f32[40,1280]{1,0:T(8,128)S(1)} %add.518), channel_id=1, source_target_pairs={{0,1},{1,3},{3,5},{5,7},{7,6},{6,4},{4,2},{2,0},{8,9},{9,11},{11,1... | collective-permute-start | bytes 614408 | tf_op jit(solution)/shard_map/ppermute | solution.py:85
  48.4 0.6 collective-permute-start.18
  49.0 2.2 %collective-permute-done.24 = f32[40,1280]{1,0:T(8,128)S(1)} collective-permute-done((f32[40,1280]{1,0:T(8,128)S(1)}, f32[40,1280]{1,0:T(8,128)S(1)}, u32[]{:S(2)}, u32[]{:S(2)}) %collective-permute-start.24) | collective-permute-done | bytes 204832 | tf_op jit(solution)/shard_map/ppermute | solution.py:85
  51.2 1.5 %collective-permute-start.25 = (f32[40,1280]{1,0:T(8,128)S(1)}, f32[40,1280]{1,0:T(8,128)S(1)}, u32[]{:S(2)}, u32[]{:S(2)}) collective-permute-start(f32[40,1280]{1,0:T(8,128)S(1)} %add.580), channel_id=1, source_target_pairs={{0,1},{1,3},{3,5},{5,7},{7,6},{6,4},{4,2},{2,0},{8,9},{9,11},{11,1... | collective-permute-start | bytes 614408 | tf_op jit(solution)/shard_map/ppermute | solution.py:85
  52.8 0.6 collective-permute-start.32
  53.5 1.2 %fusion.3 = bf16[512,1280]{1,0:T(8,128)(2,1)S(1)} fusion(bf16[512,1280]{1,0:T(8,128)(2,1)S(1)} %fusion.4, s32[]{:T(128)S(6)} %select_n.860, bf16[128,1280]{1,0:T(8,128)(2,1)S(1)} %collective-permute-done.2, bf16[1280,1280]{1,0:T(8,128)(2,1)S(1)} %copy-done), kind=kOutput, calls=%fused_computation.10 | convolution fusion | flops 419594240 | bytes 3932164 | tf_op jit(solution)/shard_map/dot_general | solution.py:17
  54.7 0.9 collective-permute-done.11
  55.6 1.5 %collective-permute-start.12 = (f32[40,1280]{1,0:T(8,128)S(1)}, f32[40,1280]{1,0:T(8,128)S(1)}, u32[]{:S(2)}, u32[]{:S(2)}) collective-permute-start(f32[40,1280]{1,0:T(8,128)S(1)} %add.521), channel_id=1, source_target_pairs={{0,1},{1,3},{3,5},{5,7},{7,6},{6,4},{4,2},{2,0},{8,9},{9,11},{11,1... | collective-permute-start | bytes 614408 | tf_op jit(solution)/shard_map/ppermute | solution.py:85
  57.2 0.6 collective-permute-start.19
  57.7 2.2 %collective-permute-done.25 = f32[40,1280]{1,0:T(8,128)S(1)} collective-permute-done((f32[40,1280]{1,0:T(8,128)S(1)}, f32[40,1280]{1,0:T(8,128)S(1)}, u32[]{:S(2)}, u32[]{:S(2)}) %collective-permute-start.25) | collective-permute-done | bytes 204832 | tf_op jit(solution)/shard_map/ppermute | solution.py:85
  60.0 1.5 %collective-permute-start.26 = (f32[40,1280]{1,0:T(8,128)S(1)}, f32[40,1280]{1,0:T(8,128)S(1)}, u32[]{:S(2)}, u32[]{:S(2)}) collective-permute-start(f32[40,1280]{1,0:T(8,128)S(1)} %add.583), channel_id=1, source_target_pairs={{0,1},{1,3},{3,5},{5,7},{7,6},{6,4},{4,2},{2,0},{8,9},{9,11},{11,1... | collective-permute-start | bytes 614408 | tf_op jit(solution)/shard_map/ppermute | solution.py:85
  61.5 0.6 collective-permute-start.33
  62.3 2.2 %fusion.2 = bf16[512,1280]{1,0:T(8,128)(2,1)S(1)} fusion(bf16[512,1280]{1,0:T(8,128)(2,1)S(1)} %fusion.3, s32[]{:T(128)S(6)} %select_n.861, bf16[128,1280]{1,0:T(8,128)(2,1)} %collective-permute-done.4, bf16[1280,1280]{1,0:T(8,128)(2,1)S(1)} %copy-done), kind=kOutput, calls=%fused_computation.8 | convolution fusion | flops 419594240 | bytes 3932164 | tf_op jit(solution)/shard_map/dot_general | solution.py:17
  64.5 1.5 %collective-permute-start.13 = (f32[40,1280]{1,0:T(8,128)S(1)}, f32[40,1280]{1,0:T(8,128)S(1)}, u32[]{:S(2)}, u32[]{:S(2)}) collective-permute-start(f32[40,1280]{1,0:T(8,128)S(1)} %add.524), channel_id=1, source_target_pairs={{0,1},{1,3},{3,5},{5,7},{7,6},{6,4},{4,2},{2,0},{8,9},{9,11},{11,1... | collective-permute-start | bytes 614408 | tf_op jit(solution)/shard_map/ppermute | solution.py:85
  66.1 0.6 collective-permute-start.20
  66.6 2.1 %collective-permute-done.26 = f32[40,1280]{1,0:T(8,128)S(1)} collective-permute-done((f32[40,1280]{1,0:T(8,128)S(1)}, f32[40,1280]{1,0:T(8,128)S(1)}, u32[]{:S(2)}, u32[]{:S(2)}) %collective-permute-start.26) | collective-permute-done | bytes 204832 | tf_op jit(solution)/shard_map/ppermute | solution.py:85
  68.7 1.5 %collective-permute-start.27 = (f32[40,1280]{1,0:T(8,128)S(1)}, f32[40,1280]{1,0:T(8,128)S(1)}, u32[]{:S(2)}, u32[]{:S(2)}) collective-permute-start(f32[40,1280]{1,0:T(8,128)S(1)} %add.586), channel_id=1, source_target_pairs={{0,1},{1,3},{3,5},{5,7},{7,6},{6,4},{4,2},{2,0},{8,9},{9,11},{11,1... | collective-permute-start | bytes 614408 | tf_op jit(solution)/shard_map/ppermute | solution.py:85
  70.3 0.6 collective-permute-start.34
  71.0 1.2 %fusion.1 = bf16[512,1280]{1,0:T(8,128)(2,1)S(1)} fusion(bf16[512,1280]{1,0:T(8,128)(2,1)S(1)} %fusion.2, s32[]{:T(128)S(6)} %select_n.862, bf16[128,1280]{1,0:T(8,128)(2,1)S(1)} %collective-permute-done.6, bf16[1280,1280]{1,0:T(8,128)(2,1)S(1)} %copy-done), kind=kOutput, calls=%fused_computation.6 | convolution fusion | flops 419594240 | bytes 3932164 | tf_op jit(solution)/shard_map/dot_general | solution.py:17
  72.3 0.9 collective-permute-done.13
  73.1 1.5 %collective-permute-start.14 = (f32[40,1280]{1,0:T(8,128)S(1)}, f32[40,1280]{1,0:T(8,128)S(1)}, u32[]{:S(2)}, u32[]{:S(2)}) collective-permute-start(f32[40,1280]{1,0:T(8,128)S(1)} %add.527), channel_id=1, source_target_pairs={{0,1},{1,3},{3,5},{5,7},{7,6},{6,4},{4,2},{2,0},{8,9},{9,11},{11,1... | collective-permute-start | bytes 614408 | tf_op jit(solution)/shard_map/ppermute | solution.py:85
  74.7 0.6 collective-permute-start.21
  75.3 2.2 %collective-permute-done.27 = f32[40,1280]{1,0:T(8,128)S(1)} collective-permute-done((f32[40,1280]{1,0:T(8,128)S(1)}, f32[40,1280]{1,0:T(8,128)S(1)}, u32[]{:S(2)}, u32[]{:S(2)}) %collective-permute-start.27) | collective-permute-done | bytes 204832 | tf_op jit(solution)/shard_map/ppermute | solution.py:85
  77.6 1.5 %collective-permute-start.28 = (f32[40,1280]{1,0:T(8,128)S(1)}, f32[40,1280]{1,0:T(8,128)S(1)}, u32[]{:S(2)}, u32[]{:S(2)}) collective-permute-start(f32[40,1280]{1,0:T(8,128)S(1)} %add.589), channel_id=1, source_target_pairs={{0,1},{1,3},{3,5},{5,7},{7,6},{6,4},{4,2},{2,0},{8,9},{9,11},{11,1... | collective-permute-start | bytes 614408 | tf_op jit(solution)/shard_map/ppermute | solution.py:85
  79.1 0.6 collective-permute-start.35
  79.8 2.0 %collective-permute-done.14 = f32[40,1280]{1,0:T(8,128)S(1)} collective-permute-done((f32[40,1280]{1,0:T(8,128)S(1)}, f32[40,1280]{1,0:T(8,128)S(1)}, u32[]{:S(2)}, u32[]{:S(2)}) %collective-permute-start.14) | collective-permute-done | bytes 204832 | tf_op jit(solution)/shard_map/ppermute | solution.py:85
  81.9 1.5 %collective-permute-start.15 = (f32[40,1280]{1,0:T(8,128)S(1)}, f32[40,1280]{1,0:T(8,128)S(1)}, u32[]{:S(2)}, u32[]{:S(2)}) collective-permute-start(f32[40,1280]{1,0:T(8,128)S(1)} %add.530), channel_id=1, source_target_pairs={{0,1},{1,3},{3,5},{5,7},{7,6},{6,4},{4,2},{2,0},{8,9},{9,11},{11,1... | collective-permute-start | bytes 614408 | tf_op jit(solution)/shard_map/ppermute | solution.py:85
  83.5 0.6 collective-permute-start.22
  84.1 2.2 %collective-permute-done.28 = f32[40,1280]{1,0:T(8,128)S(1)} collective-permute-done((f32[40,1280]{1,0:T(8,128)S(1)}, f32[40,1280]{1,0:T(8,128)S(1)}, u32[]{:S(2)}, u32[]{:S(2)}) %collective-permute-start.28) | collective-permute-done | bytes 204832 | tf_op jit(solution)/shard_map/ppermute | solution.py:85
  86.3 1.5 %collective-permute-start.29 = (f32[40,1280]{1,0:T(8,128)S(1)}, f32[40,1280]{1,0:T(8,128)S(1)}, u32[]{:S(2)}, u32[]{:S(2)}) collective-permute-start(f32[40,1280]{1,0:T(8,128)S(1)} %add.592), channel_id=1, source_target_pairs={{0,1},{1,3},{3,5},{5,7},{7,6},{6,4},{4,2},{2,0},{8,9},{9,11},{11,1... | collective-permute-start | bytes 614408 | tf_op jit(solution)/shard_map/ppermute | solution.py:85
  87.9 0.6 collective-permute-start.36
  88.6 2.1 %collective-permute-done.15 = f32[40,1280]{1,0:T(8,128)S(1)} collective-permute-done((f32[40,1280]{1,0:T(8,128)S(1)}, f32[40,1280]{1,0:T(8,128)S(1)}, u32[]{:S(2)}, u32[]{:S(2)}) %collective-permute-start.15) | collective-permute-done | bytes 204832 | tf_op jit(solution)/shard_map/ppermute | solution.py:85
  90.7 1.5 %collective-permute-start.16 = (f32[40,1280]{1,0:T(8,128)S(1)}, f32[40,1280]{1,0:T(8,128)S(1)}, u32[]{:S(2)}, u32[]{:S(2)}) collective-permute-start(f32[40,1280]{1,0:T(8,128)S(1)} %add.533), channel_id=1, source_target_pairs={{0,1},{1,3},{3,5},{5,7},{7,6},{6,4},{4,2},{2,0},{8,9},{9,11},{11,1... | collective-permute-start | bytes 614408 | tf_op jit(solution)/shard_map/ppermute | solution.py:85
  92.3 0.6 collective-permute-start.23
  92.9 2.2 %collective-permute-done.29 = f32[40,1280]{1,0:T(8,128)S(1)} collective-permute-done((f32[40,1280]{1,0:T(8,128)S(1)}, f32[40,1280]{1,0:T(8,128)S(1)}, u32[]{:S(2)}, u32[]{:S(2)}) %collective-permute-start.29) | collective-permute-done | bytes 204832 | tf_op jit(solution)/shard_map/ppermute | solution.py:85
  95.1 1.5 %collective-permute-start.30 = (f32[40,1280]{1,0:T(8,128)S(1)}, f32[40,1280]{1,0:T(8,128)S(1)}, u32[]{:S(2)}, u32[]{:S(2)}) collective-permute-start(f32[40,1280]{1,0:T(8,128)S(1)} %add.595), channel_id=1, source_target_pairs={{0,1},{1,3},{3,5},{5,7},{7,6},{6,4},{4,2},{2,0},{8,9},{9,11},{11,1... | collective-permute-start | bytes 614408 | tf_op jit(solution)/shard_map/ppermute | solution.py:85
  96.7 0.6 collective-permute-start.37
  97.4 2.1 %collective-permute-done.16 = f32[40,1280]{1,0:T(8,128)S(1)} collective-permute-done((f32[40,1280]{1,0:T(8,128)S(1)}, f32[40,1280]{1,0:T(8,128)S(1)}, u32[]{:S(2)}, u32[]{:S(2)}) %collective-permute-start.16) | collective-permute-done | bytes 204832 | tf_op jit(solution)/shard_map/ppermute | solution.py:85
  99.5 1.5 %collective-permute-done.23 = f32[40,1280]{1,0:T(8,128)S(1)} collective-permute-done((f32[40,1280]{1,0:T(8,128)S(1)}, f32[40,1280]{1,0:T(8,128)S(1)}, u32[]{:S(2)}, u32[]{:S(2)}) %collective-permute-start.23) | collective-permute-done | bytes 204832 | tf_op jit(solution)/shard_map/ppermute | solution.py:85
  101.0 1.7 %collective-permute-done.30 = f32[40,1280]{1,0:T(8,128)S(1)} collective-permute-done((f32[40,1280]{1,0:T(8,128)S(1)}, f32[40,1280]{1,0:T(8,128)S(1)}, u32[]{:S(2)}, u32[]{:S(2)}) %collective-permute-start.30) | collective-permute-done | bytes 204832 | tf_op jit(solution)/shard_map/ppermute | solution.py:85
  102.7 1.4 %collective-permute-done.37 = f32[40,1280]{1,0:T(8,128)S(1)} collective-permute-done((f32[40,1280]{1,0:T(8,128)S(1)}, f32[40,1280]{1,0:T(8,128)S(1)}, u32[]{:S(2)}, u32[]{:S(2)}) %collective-permute-start.37) | collective-permute-done | bytes 204832 | tf_op jit(solution)/shard_map/ppermute | solution.py:85
  104.2 2.0 %add_divide_fusion = (f32[160,1280]{1,0:T(8,128)}, f32[160,1280]{1,0:T(8,128)}, f32[160,1280]{1,0:T(8,128)}, f32[160,1280]{1,0:T(8,128)}) fusion(f32[160,1280]{1,0:T(8,128)S(1)} %copy-done.3, f32[160,1280]{1,0:T(8,128)S(1)} %copy-done.4, f32[160,1280]{1,0:T(8,128)S(1)} %copy-done.5, f32[40,1280]{1,0:T(8,128)S(1)} %add.621, f32[40,1280]{1,0:T(8,128)S(1)} %add.598, ...), kind=kLoop, calls=%fused_computation.16 | loop fusion | flops 3481600 | bytes 6553600 | tf_op jit(solution)/shard_map/div | solution.py:205
  (94 shorter events, 1.6 us)
Async XLA Ops:
  0.6 42.5 %copy-start = (bf16[1280,1280]{1,0:T(8,128)(2,1)S(1)}, bf16[1280,1280]{1,0:T(8,128)(2,1)}, u32[]{:S(2)}) copy-start(bf16[1280,1280]{1,0:T(8,128)(2,1)} %param.8) | copy-start | bytes 9830404
  3.0 11.8 %collective-permute-start = (bf16[128,1280]{1,0:T(8,128)(2,1)}, bf16[128,1280]{1,0:T(8,128)(2,1)}, u32[]{:S(2)}, u32[]{:S(2)}) collective-permute-start(bf16[128,1280]{1,0:T(8,128)(2,1)} %get-tuple-element.85), channel_id=1, source_target_pairs={{0,16},{8,24},{16,0},{24,8},{1,17},{9,25},{17,1},{25,9},{2,18},{10... | collective-permute-start | bytes 983048 | tf_op jit(solution)/shard_map/ppermute | solution.py:106
  5.9 15.4 %collective-permute-start.4 = (bf16[128,1280]{1,0:T(8,128)(2,1)}, bf16[128,1280]{1,0:T(8,128)(2,1)}, u32[]{:S(2)}, u32[]{:S(2)}) collective-permute-start(bf16[128,1280]{1,0:T(8,128)(2,1)} %bitcast.114), channel_id=1, source_target_pairs={{0,16},{8,24},{16,0},{24,8},{1,17},{9,25},{17,1},{25,9},{2,18},{10... | collective-permute-start | bytes 983048 | tf_op jit(solution)/shard_map/ppermute | solution.py:105
  5.9 11.4 %copy-start.6 = (bf16[128,1280]{1,0:T(8,128)(2,1)S(1)}, bf16[128,1280]{1,0:T(8,128)(2,1)}, u32[]{:S(2)}) copy-start(bf16[128,1280]{1,0:T(8,128)(2,1)} %get-tuple-element.43) | copy-start | bytes 983044
  14.8 6.6 %collective-permute-start.2 = (bf16[128,1280]{1,0:T(8,128)(2,1)}, bf16[128,1280]{1,0:T(8,128)(2,1)S(1)}, u32[]{:S(2)}, u32[]{:S(2)}) collective-permute-start(bf16[128,1280]{1,0:T(8,128)(2,1)} %bitcast.115), channel_id=1, source_target_pairs={{0,8},{8,0},{16,24},{24,16},{1,9},{9,1},{17,25},{25,17},{2,10},{10... | collective-permute-start | bytes 983048 | tf_op jit(solution)/shard_map/ppermute | solution.py:108
  14.8 6.6 %collective-permute-start.1 = (bf16[128,1280]{1,0:T(8,128)(2,1)}, bf16[128,1280]{1,0:T(8,128)(2,1)S(1)}, u32[]{:S(2)}, u32[]{:S(2)}) collective-permute-start(bf16[128,1280]{1,0:T(8,128)(2,1)} %get-tuple-element.41), channel_id=1, source_target_pairs={{0,8},{8,0},{16,24},{24,16},{1,9},{9,1},{17,25},{25,17},{2,10},{10... | collective-permute-start | bytes 983048 | tf_op jit(solution)/shard_map/ppermute | solution.py:109
  17.4 10.5 %collective-permute-start.3 = (bf16[128,1280]{1,0:T(8,128)(2,1)S(1)}, bf16[128,1280]{1,0:T(8,128)(2,1)S(1)}, u32[]{:S(2)}, u32[]{:S(2)}) collective-permute-start(bf16[128,1280]{1,0:T(8,128)(2,1)S(1)} %copy-done.6), channel_id=1, source_target_pairs={{0,16},{8,24},{16,0},{24,8},{1,17},{9,25},{17,1},{25,9},{2,18},{10... | collective-permute-start | bytes 983048 | tf_op jit(solution)/shard_map/ppermute | solution.py:113
  19.5 10.4 %collective-permute-start.5 = (bf16[128,1280]{1,0:T(8,128)(2,1)}, bf16[128,1280]{1,0:T(8,128)(2,1)S(1)}, u32[]{:S(2)}, u32[]{:S(2)}) collective-permute-start(bf16[128,1280]{1,0:T(8,128)(2,1)} %collective-permute-done), channel_id=1, source_target_pairs={{0,8},{8,0},{16,24},{24,16},{1,9},{9,1},{17,25},{25,17},{2,10},{10... | collective-permute-start | bytes 983048 | tf_op jit(solution)/shard_map/ppermute | solution.py:111
  21.3 8.6 %collective-permute-start.6 = (bf16[128,1280]{1,0:T(8,128)(2,1)}, bf16[128,1280]{1,0:T(8,128)(2,1)S(1)}, u32[]{:S(2)}, u32[]{:S(2)}) collective-permute-start(bf16[128,1280]{1,0:T(8,128)(2,1)} %collective-permute-done.4), channel_id=1, source_target_pairs={{0,8},{8,0},{16,24},{24,16},{1,9},{9,1},{17,25},{25,17},{2,10},{10... | collective-permute-start | bytes 983048 | tf_op jit(solution)/shard_map/ppermute | solution.py:110
  29.9 13.2 %copy-start.1 = (bf16[1,1,128,1280]{3,2,1,0:T(8,128)(2,1)S(1)}, bf16[1,1,128,1280]{3,2,1,0:T(8,128)(2,1)}, u32[]{:S(2)}) copy-start(bf16[1,1,128,1280]{3,2,1,0:T(8,128)(2,1)} %param.7) | copy-start | bytes 983044
  32.4 4.4 %collective-permute-start.8 = (f32[1]{0:T(128)}, f32[1]{0:T(128)}, u32[]{:S(2)}, u32[]{:S(2)}) collective-permute-start(f32[1]{0:T(128)} %bitcast.5), channel_id=1, source_target_pairs={{0,16},{8,24},{16,0},{24,8},{1,17},{9,25},{17,1},{25,9},{2,18},{10... | collective-permute-start | bytes 20 | tf_op jit(solution)/shard_map/ppermute | solution.py:126
  34.2 3.2 %collective-permute-start.9 = (f32[1]{0:T(128)}, f32[1]{0:T(128)}, u32[]{:S(2)}, u32[]{:S(2)}) collective-permute-start(f32[1]{0:T(128)} %bitcast.5), channel_id=1, source_target_pairs={{0,24},{8,16},{16,8},{24,0},{1,25},{9,17},{17,9},{25,1},{2,26},{10... | collective-permute-start | bytes 20 | tf_op jit(solution)/shard_map/ppermute | solution.py:126
  34.2 1.3 %collective-permute-start.7 = (f32[1]{0:T(128)}, f32[1]{0:T(128)}, u32[]{:S(2)}, u32[]{:S(2)}) collective-permute-start(f32[1]{0:T(128)} %bitcast.5), channel_id=1, source_target_pairs={{0,8},{8,0},{16,24},{24,16},{1,9},{9,1},{17,25},{25,17},{2,10},{10... | collective-permute-start | bytes 20 | tf_op jit(solution)/shard_map/ppermute | solution.py:126
  38.8 8.0 %collective-permute-start.10 = (f32[40,1280]{1,0:T(8,128)S(1)}, f32[40,1280]{1,0:T(8,128)S(1)}, u32[]{:S(2)}, u32[]{:S(2)}) collective-permute-start(f32[40,1280]{1,0:T(8,128)S(1)} %get-tuple-element.80), channel_id=1, source_target_pairs={{0,1},{1,3},{3,5},{5,7},{7,6},{6,4},{4,2},{2,0},{8,9},{9,11},{11,1... | collective-permute-start | bytes 614408 | tf_op jit(solution)/shard_map/ppermute | solution.py:85
  40.3 8.0 %collective-permute-start.17 = (f32[40,1280]{1,0:T(8,128)S(1)}, f32[40,1280]{1,0:T(8,128)S(1)}, u32[]{:S(2)}, u32[]{:S(2)}) collective-permute-start(f32[40,1280]{1,0:T(8,128)S(1)} %get-tuple-element.83), channel_id=1, source_target_pairs={{0,2},{1,0},{3,1},{5,3},{7,5},{6,7},{4,6},{2,4},{8,10},{9,8},{11,9... | collective-permute-start | bytes 614408 | tf_op jit(solution)/shard_map/ppermute | solution.py:85
  40.8 10.3 %collective-permute-start.24 = (f32[40,1280]{1,0:T(8,128)S(1)}, f32[40,1280]{1,0:T(8,128)S(1)}, u32[]{:S(2)}, u32[]{:S(2)}) collective-permute-start(f32[40,1280]{1,0:T(8,128)S(1)} %get-tuple-element.82), channel_id=1, source_target_pairs={{0,1},{1,3},{3,5},{5,7},{7,6},{6,4},{4,2},{2,0},{8,9},{9,11},{11,1... | collective-permute-start | bytes 614408 | tf_op jit(solution)/shard_map/ppermute | solution.py:85
  42.4 10.4 %collective-permute-start.31 = (f32[40,1280]{1,0:T(8,128)S(1)}, f32[40,1280]{1,0:T(8,128)S(1)}, u32[]{:S(2)}, u32[]{:S(2)}) collective-permute-start(f32[40,1280]{1,0:T(8,128)S(1)} %get-tuple-element.81), channel_id=1, source_target_pairs={{0,2},{1,0},{3,1},{5,3},{7,5},{6,7},{4,6},{2,4},{8,10},{9,8},{11,9... | collective-permute-start | bytes 614408 | tf_op jit(solution)/shard_map/ppermute | solution.py:85
  46.8 8.8 %collective-permute-start.11 = (f32[40,1280]{1,0:T(8,128)S(1)}, f32[40,1280]{1,0:T(8,128)S(1)}, u32[]{:S(2)}, u32[]{:S(2)}) collective-permute-start(f32[40,1280]{1,0:T(8,128)S(1)} %add.518), channel_id=1, source_target_pairs={{0,1},{1,3},{3,5},{5,7},{7,6},{6,4},{4,2},{2,0},{8,9},{9,11},{11,1... | collective-permute-start | bytes 614408 | tf_op jit(solution)/shard_map/ppermute | solution.py:85
  48.4 8.8 %collective-permute-start.18 = (f32[40,1280]{1,0:T(8,128)S(1)}, f32[40,1280]{1,0:T(8,128)S(1)}, u32[]{:S(2)}, u32[]{:S(2)}) collective-permute-start(f32[40,1280]{1,0:T(8,128)S(1)} %add.545), channel_id=1, source_target_pairs={{0,2},{1,0},{3,1},{5,3},{7,5},{6,7},{4,6},{2,4},{8,10},{9,8},{11,9... | collective-permute-start | bytes 614408 | tf_op jit(solution)/shard_map/ppermute | solution.py:85
  51.2 8.8 %collective-permute-start.25 = (f32[40,1280]{1,0:T(8,128)S(1)}, f32[40,1280]{1,0:T(8,128)S(1)}, u32[]{:S(2)}, u32[]{:S(2)}) collective-permute-start(f32[40,1280]{1,0:T(8,128)S(1)} %add.580), channel_id=1, source_target_pairs={{0,1},{1,3},{3,5},{5,7},{7,6},{6,4},{4,2},{2,0},{8,9},{9,11},{11,1... | collective-permute-start | bytes 614408 | tf_op jit(solution)/shard_map/ppermute | solution.py:85
  52.8 8.7 %collective-permute-start.32 = (f32[40,1280]{1,0:T(8,128)S(1)}, f32[40,1280]{1,0:T(8,128)S(1)}, u32[]{:S(2)}, u32[]{:S(2)}) collective-permute-start(f32[40,1280]{1,0:T(8,128)S(1)} %add.603), channel_id=1, source_target_pairs={{0,2},{1,0},{3,1},{5,3},{7,5},{6,7},{4,6},{2,4},{8,10},{9,8},{11,9... | collective-permute-start | bytes 614408 | tf_op jit(solution)/shard_map/ppermute | solution.py:85
  55.6 8.9 %collective-permute-start.12 = (f32[40,1280]{1,0:T(8,128)S(1)}, f32[40,1280]{1,0:T(8,128)S(1)}, u32[]{:S(2)}, u32[]{:S(2)}) collective-permute-start(f32[40,1280]{1,0:T(8,128)S(1)} %add.521), channel_id=1, source_target_pairs={{0,1},{1,3},{3,5},{5,7},{7,6},{6,4},{4,2},{2,0},{8,9},{9,11},{11,1... | collective-permute-start | bytes 614408 | tf_op jit(solution)/shard_map/ppermute | solution.py:85
  57.2 8.9 %collective-permute-start.19 = (f32[40,1280]{1,0:T(8,128)S(1)}, f32[40,1280]{1,0:T(8,128)S(1)}, u32[]{:S(2)}, u32[]{:S(2)}) collective-permute-start(f32[40,1280]{1,0:T(8,128)S(1)} %add.550), channel_id=1, source_target_pairs={{0,2},{1,0},{3,1},{5,3},{7,5},{6,7},{4,6},{2,4},{8,10},{9,8},{11,9... | collective-permute-start | bytes 614408 | tf_op jit(solution)/shard_map/ppermute | solution.py:85
  60.0 8.8 %collective-permute-start.26 = (f32[40,1280]{1,0:T(8,128)S(1)}, f32[40,1280]{1,0:T(8,128)S(1)}, u32[]{:S(2)}, u32[]{:S(2)}) collective-permute-start(f32[40,1280]{1,0:T(8,128)S(1)} %add.583), channel_id=1, source_target_pairs={{0,1},{1,3},{3,5},{5,7},{7,6},{6,4},{4,2},{2,0},{8,9},{9,11},{11,1... | collective-permute-start | bytes 614408 | tf_op jit(solution)/shard_map/ppermute | solution.py:85
  61.5 8.8 %collective-permute-start.33 = (f32[40,1280]{1,0:T(8,128)S(1)}, f32[40,1280]{1,0:T(8,128)S(1)}, u32[]{:S(2)}, u32[]{:S(2)}) collective-permute-start(f32[40,1280]{1,0:T(8,128)S(1)} %add.606), channel_id=1, source_target_pairs={{0,2},{1,0},{3,1},{5,3},{7,5},{6,7},{4,6},{2,4},{8,10},{9,8},{11,9... | collective-permute-start | bytes 614408 | tf_op jit(solution)/shard_map/ppermute | solution.py:85
  64.5 8.6 %collective-permute-start.13 = (f32[40,1280]{1,0:T(8,128)S(1)}, f32[40,1280]{1,0:T(8,128)S(1)}, u32[]{:S(2)}, u32[]{:S(2)}) collective-permute-start(f32[40,1280]{1,0:T(8,128)S(1)} %add.524), channel_id=1, source_target_pairs={{0,1},{1,3},{3,5},{5,7},{7,6},{6,4},{4,2},{2,0},{8,9},{9,11},{11,1... | collective-permute-start | bytes 614408 | tf_op jit(solution)/shard_map/ppermute | solution.py:85
  66.1 8.6 %collective-permute-start.20 = (f32[40,1280]{1,0:T(8,128)S(1)}, f32[40,1280]{1,0:T(8,128)S(1)}, u32[]{:S(2)}, u32[]{:S(2)}) collective-permute-start(f32[40,1280]{1,0:T(8,128)S(1)} %add.555), channel_id=1, source_target_pairs={{0,2},{1,0},{3,1},{5,3},{7,5},{6,7},{4,6},{2,4},{8,10},{9,8},{11,9... | collective-permute-start | bytes 614408 | tf_op jit(solution)/shard_map/ppermute | solution.py:85
  68.7 8.7 %collective-permute-start.27 = (f32[40,1280]{1,0:T(8,128)S(1)}, f32[40,1280]{1,0:T(8,128)S(1)}, u32[]{:S(2)}, u32[]{:S(2)}) collective-permute-start(f32[40,1280]{1,0:T(8,128)S(1)} %add.586), channel_id=1, source_target_pairs={{0,1},{1,3},{3,5},{5,7},{7,6},{6,4},{4,2},{2,0},{8,9},{9,11},{11,1... | collective-permute-start | bytes 614408 | tf_op jit(solution)/shard_map/ppermute | solution.py:85
  70.3 8.8 %collective-permute-start.34 = (f32[40,1280]{1,0:T(8,128)S(1)}, f32[40,1280]{1,0:T(8,128)S(1)}, u32[]{:S(2)}, u32[]{:S(2)}) collective-permute-start(f32[40,1280]{1,0:T(8,128)S(1)} %add.609), channel_id=1, source_target_pairs={{0,2},{1,0},{3,1},{5,3},{7,5},{6,7},{4,6},{2,4},{8,10},{9,8},{11,9... | collective-permute-start | bytes 614408 | tf_op jit(solution)/shard_map/ppermute | solution.py:85
  72.2 28.8 %copy-start.2 = (bf16[512,1280]{1,0:T(8,128)(2,1)}, bf16[512,1280]{1,0:T(8,128)(2,1)S(1)}, u32[]{:S(2)}) copy-start(bf16[512,1280]{1,0:T(8,128)(2,1)S(1)} %fusion.1) | copy-start | bytes 3932164
  73.1 8.7 %collective-permute-start.14 = (f32[40,1280]{1,0:T(8,128)S(1)}, f32[40,1280]{1,0:T(8,128)S(1)}, u32[]{:S(2)}, u32[]{:S(2)}) collective-permute-start(f32[40,1280]{1,0:T(8,128)S(1)} %add.527), channel_id=1, source_target_pairs={{0,1},{1,3},{3,5},{5,7},{7,6},{6,4},{4,2},{2,0},{8,9},{9,11},{11,1... | collective-permute-start | bytes 614408 | tf_op jit(solution)/shard_map/ppermute | solution.py:85
  74.7 8.7 %collective-permute-start.21 = (f32[40,1280]{1,0:T(8,128)S(1)}, f32[40,1280]{1,0:T(8,128)S(1)}, u32[]{:S(2)}, u32[]{:S(2)}) collective-permute-start(f32[40,1280]{1,0:T(8,128)S(1)} %add.560), channel_id=1, source_target_pairs={{0,2},{1,0},{3,1},{5,3},{7,5},{6,7},{4,6},{2,4},{8,10},{9,8},{11,9... | collective-permute-start | bytes 614408 | tf_op jit(solution)/shard_map/ppermute | solution.py:85
  77.5 26.6 %copy-start.3 = (f32[160,1280]{1,0:T(8,128)S(1)}, f32[160,1280]{1,0:T(8,128)}, u32[]{:S(2)}) copy-start(f32[160,1280]{1,0:T(8,128)} %param.11) | copy-start | bytes 2457604
  77.5 26.6 %copy-start.4 = (f32[160,1280]{1,0:T(8,128)S(1)}, f32[160,1280]{1,0:T(8,128)}, u32[]{:S(2)}) copy-start(f32[160,1280]{1,0:T(8,128)} %param.10) | copy-start | bytes 2457604
  77.6 26.6 %copy-start.5 = (f32[160,1280]{1,0:T(8,128)S(1)}, f32[160,1280]{1,0:T(8,128)}, u32[]{:S(2)}) copy-start(f32[160,1280]{1,0:T(8,128)} %param.9) | copy-start | bytes 2457604
  77.6 8.7 %collective-permute-start.28 = (f32[40,1280]{1,0:T(8,128)S(1)}, f32[40,1280]{1,0:T(8,128)S(1)}, u32[]{:S(2)}, u32[]{:S(2)}) collective-permute-start(f32[40,1280]{1,0:T(8,128)S(1)} %add.589), channel_id=1, source_target_pairs={{0,1},{1,3},{3,5},{5,7},{7,6},{6,4},{4,2},{2,0},{8,9},{9,11},{11,1... | collective-permute-start | bytes 614408 | tf_op jit(solution)/shard_map/ppermute | solution.py:85
  79.1 8.7 %collective-permute-start.35 = (f32[40,1280]{1,0:T(8,128)S(1)}, f32[40,1280]{1,0:T(8,128)S(1)}, u32[]{:S(2)}, u32[]{:S(2)}) collective-permute-start(f32[40,1280]{1,0:T(8,128)S(1)} %add.612), channel_id=1, source_target_pairs={{0,2},{1,0},{3,1},{5,3},{7,5},{6,7},{4,6},{2,4},{8,10},{9,8},{11,9... | collective-permute-start | bytes 614408 | tf_op jit(solution)/shard_map/ppermute | solution.py:85
  81.9 8.8 %collective-permute-start.15 = (f32[40,1280]{1,0:T(8,128)S(1)}, f32[40,1280]{1,0:T(8,128)S(1)}, u32[]{:S(2)}, u32[]{:S(2)}) collective-permute-start(f32[40,1280]{1,0:T(8,128)S(1)} %add.530), channel_id=1, source_target_pairs={{0,1},{1,3},{3,5},{5,7},{7,6},{6,4},{4,2},{2,0},{8,9},{9,11},{11,1... | collective-permute-start | bytes 614408 | tf_op jit(solution)/shard_map/ppermute | solution.py:85
  83.5 8.8 %collective-permute-start.22 = (f32[40,1280]{1,0:T(8,128)S(1)}, f32[40,1280]{1,0:T(8,128)S(1)}, u32[]{:S(2)}, u32[]{:S(2)}) collective-permute-start(f32[40,1280]{1,0:T(8,128)S(1)} %add.565), channel_id=1, source_target_pairs={{0,2},{1,0},{3,1},{5,3},{7,5},{6,7},{4,6},{2,4},{8,10},{9,8},{11,9... | collective-permute-start | bytes 614408 | tf_op jit(solution)/shard_map/ppermute | solution.py:85
  86.3 8.7 %collective-permute-start.29 = (f32[40,1280]{1,0:T(8,128)S(1)}, f32[40,1280]{1,0:T(8,128)S(1)}, u32[]{:S(2)}, u32[]{:S(2)}) collective-permute-start(f32[40,1280]{1,0:T(8,128)S(1)} %add.592), channel_id=1, source_target_pairs={{0,1},{1,3},{3,5},{5,7},{7,6},{6,4},{4,2},{2,0},{8,9},{9,11},{11,1... | collective-permute-start | bytes 614408 | tf_op jit(solution)/shard_map/ppermute | solution.py:85
  87.9 8.7 %collective-permute-start.36 = (f32[40,1280]{1,0:T(8,128)S(1)}, f32[40,1280]{1,0:T(8,128)S(1)}, u32[]{:S(2)}, u32[]{:S(2)}) collective-permute-start(f32[40,1280]{1,0:T(8,128)S(1)} %add.615), channel_id=1, source_target_pairs={{0,2},{1,0},{3,1},{5,3},{7,5},{6,7},{4,6},{2,4},{8,10},{9,8},{11,9... | collective-permute-start | bytes 614408 | tf_op jit(solution)/shard_map/ppermute | solution.py:85
  90.7 8.7 %collective-permute-start.16 = (f32[40,1280]{1,0:T(8,128)S(1)}, f32[40,1280]{1,0:T(8,128)S(1)}, u32[]{:S(2)}, u32[]{:S(2)}) collective-permute-start(f32[40,1280]{1,0:T(8,128)S(1)} %add.533), channel_id=1, source_target_pairs={{0,1},{1,3},{3,5},{5,7},{7,6},{6,4},{4,2},{2,0},{8,9},{9,11},{11,1... | collective-permute-start | bytes 614408 | tf_op jit(solution)/shard_map/ppermute | solution.py:85
  92.3 8.7 %collective-permute-start.23 = (f32[40,1280]{1,0:T(8,128)S(1)}, f32[40,1280]{1,0:T(8,128)S(1)}, u32[]{:S(2)}, u32[]{:S(2)}) collective-permute-start(f32[40,1280]{1,0:T(8,128)S(1)} %add.570), channel_id=1, source_target_pairs={{0,2},{1,0},{3,1},{5,3},{7,5},{6,7},{4,6},{2,4},{8,10},{9,8},{11,9... | collective-permute-start | bytes 614408 | tf_op jit(solution)/shard_map/ppermute | solution.py:85
  95.1 7.6 %collective-permute-start.30 = (f32[40,1280]{1,0:T(8,128)S(1)}, f32[40,1280]{1,0:T(8,128)S(1)}, u32[]{:S(2)}, u32[]{:S(2)}) collective-permute-start(f32[40,1280]{1,0:T(8,128)S(1)} %add.595), channel_id=1, source_target_pairs={{0,1},{1,3},{3,5},{5,7},{7,6},{6,4},{4,2},{2,0},{8,9},{9,11},{11,1... | collective-permute-start | bytes 614408 | tf_op jit(solution)/shard_map/ppermute | solution.py:85
  96.7 7.5 %collective-permute-start.37 = (f32[40,1280]{1,0:T(8,128)S(1)}, f32[40,1280]{1,0:T(8,128)S(1)}, u32[]{:S(2)}, u32[]{:S(2)}) collective-permute-start(f32[40,1280]{1,0:T(8,128)S(1)} %add.618), channel_id=1, source_target_pairs={{0,2},{1,0},{3,1},{5,3},{7,5},{6,7},{4,6},{2,4},{8,10},{9,8},{11,9... | collective-permute-start | bytes 614408 | tf_op jit(solution)/shard_map/ppermute | solution.py:85

commit v15 on v14

--- a/solution.py
+++ b/solution.py
@@ -103,14 +103,15 @@
     over_x = [(i, i ^ 2) for i in range(4)]
     over_core = [(i, i ^ 1) for i in range(4)]
     g_far = lax.ppermute(grad_rows, "aug", over_x)
-    h_far_relay = lax.ppermute(cols(a ^ 3), "aug", over_x)
-    _, (g_mine, h_mine) = lax.optimization_barrier((h_far_relay, (grad_rows, cols(a ^ 1))))
+    other = lax.dynamic_slice_in_dim(h_rows, ((a ^ 2) & ~1) * sw, 2 * sw, axis=1)
+    h_pair = lax.ppermute(other, "aug", over_x)
+    h_far = lax.dynamic_slice_in_dim(h_pair, (a & 1) * sw, sw, axis=1)
+    h_fwd = lax.dynamic_slice_in_dim(h_pair, ((a & 1) ^ 1) * sw, sw, axis=1)
+    _, (g_mine, h_mine) = lax.optimization_barrier((h_pair, (grad_rows, cols(a ^ 1))))
     g_near = lax.ppermute(g_mine, "aug", over_core)
     h_near = lax.ppermute(h_mine, "aug", over_core)
     g_relay = lax.ppermute(g_far, "aug", over_core)
-    h_relay = lax.ppermute(h_far_relay, "aug", over_core)
-    _, second = lax.optimization_barrier((h_far_relay, cols(a ^ 2)))
-    h_far = lax.ppermute(second, "aug", over_x)
+    h_relay = lax.ppermute(h_fwd, "aug", over_core)
     return [
         (a * rows, cols(a), grad_rows),
         ((a ^ 1) * rows, h_near, g_near),

time: 108 us -> 113 us (1.046)
  matrix products: 13.4 us -> 20.4 us
  local copies, waits for them, and re-layouts: 2.43 us -> 4.96 us
  waiting for transfers between devices: 45.7 us -> 43.5 us
  starting transfers between devices: 37.4 us -> 35.9 us
    dot_general x4, matrix products: 7.67 us -> 13.6 us  [per_device(): term = jnp.dot(h_piece.T, g_piece, preferred_element_type=jnp.float32)]
    dynamic_slice x0 -> x2, local copies, waits for them, and re-layouts: none -> 3.12 us  [the longest x1 2.12 us: exchange_four(): lax.dynamic_slice_in_dim(h_rows, ((a ^ 2) & ~1) * sw, 2 * sw, axis=1)]
    ppermute x3 -> x2, starting transfers between devices: 5.07 us -> 3.51 us  [the longest x1 2.94 us: exchange_four(): h_pair = lax.ppermute(other, 'aug', over_x)]
    ppermute x3 -> x2, waiting for transfers between devices: 14.3 us -> 14.1 us  [the longest x1 14.1 us: exchange_four(): h_pair = lax.ppermute(other, 'aug', over_x)]
  transfers between devices with their start and end apart: 38 -> 37, of which waited for: 20 -> 18; matrix products, arithmetic and copies ran while one was open for 12% -> 19% of each run, Pallas kernels for 0% -> 0%
where the time goes in v15:
time: 113 us
  waiting for transfers between devices  43.5 us (38%)
  starting transfers between devices  35.9 us (32%)
  matrix products  20.4 us (18%)
  local copies, waits for them, and re-layouts  4.96 us (4%)
  between operations  4.89 us (4%)
  other arithmetic  3.48 us (3%)
    ppermute x28, starting transfers between devices, ring_reduce_scatter(): lax.ppermute(v, 'dp', right if step < 0 else left)  29.7 us
    ppermute x28, waiting for transfers between devices, ring_reduce_scatter(): lax.ppermute(v, 'dp', right if step < 0 else left)  27.1 us
    ppermute x1, waiting for transfers between devices, exchange_four(): h_pair = lax.ppermute(other, 'aug', over_x)  14.1 us
    dot_general x4, matrix products, per_device(): term = jnp.dot(h_piece.T, g_piece, preferred_element_type=jnp.float32)  13.6 us
    dot_general x4, matrix products, project_back(): lax.dot_general(rows, down_weight, (((1,), (1,)), ((), ())), preferred_el...  6.75 us
    ppermute x1, starting transfers between devices, exchange_four(): h_pair = lax.ppermute(other, 'aug', over_x)  2.94 us
  transfers between devices with their start and end apart: 37, of which 18 were waited for; matrix products, arithmetic and copies ran while one was open for 19% of the time, Pallas kernels for 0%

profile of v15, /device:TPU:0, one launch (start us, length us, event | category | flops | bytes accessed | tf_op | source)
XLA Modules:
  0.0 113.1 jit_solution(12438303233361297575)
XLA Ops:
  0.7 2.1 %dynamic-slice_bitcast_fusion = bf16[128,2560]{1,0:T(8,128)(2,1)} fusion(bf16[1,1,128,5120]{3,2,1,0:T(8,128)(2,1)} %param.6, s32[]{:T(128)S(6)} %select_n.692), kind=kLoop, calls=%fused_computation.19 | loop fusion | bytes 1310724 | tf_op jit(solution)/shard_map/dynamic_slice | solution.py:106
  2.8 2.9 %collective-permute-start = (bf16[128,2560]{1,0:T(8,128)(2,1)}, bf16[128,2560]{1,0:T(8,128)(2,1)}, u32[]{:S(2)}, u32[]{:S(2)}) collective-permute-start(bf16[128,2560]{1,0:T(8,128)(2,1)} %dynamic-slice_bitcast_fusion), channel_id=1, source_target_pairs={{0,16},{8,24},{16,0},{24,8},{1,17},{9,25},{17,1},{25,9},{2,18},{10... | collective-permute-start | bytes 1966088 | tf_op jit(solution)/shard_map/ppermute | solution.py:107
  5.8 1.7 %dynamic-slice_bitcast_fusion.1 = bf16[128,1280]{1,0:T(8,128)(2,1)} fusion(bf16[1,1,128,5120]{3,2,1,0:T(8,128)(2,1)} %param.6, s32[]{:T(128)S(6)} %select_n.693), kind=kLoop, calls=%fused_computation.23 | loop fusion | bytes 655364 | tf_op jit(solution)/shard_map/dynamic_slice | solution.py:101
  7.5 14.1 %collective-permute-done = bf16[128,2560]{1,0:T(8,128)(2,1)} collective-permute-done((bf16[128,2560]{1,0:T(8,128)(2,1)}, bf16[128,2560]{1,0:T(8,128)(2,1)}, u32[]{:S(2)}, u32[]{:S(2)}) %collective-permute-start) | collective-permute-done | bytes 655392 | tf_op jit(solution)/shard_map/ppermute | solution.py:107
  21.6 0.5 collective-permute-start.1
  22.1 4.9 %fusion.6 = f32[1280,1280]{1,0:T(8,128)} fusion(bf16[1,1,128,5120]{3,2,1,0:T(8,128)(2,1)} %param.6, s32[]{:T(128)S(6)} %select_n.691, bf16[1,1,128,1280]{3,2,1,0:T(8,128)(2,1)} %param.7), kind=kOutput, calls=%fused_computation.20 | convolution fusion | flops 419430400 | bytes 7208964 | tf_op jit(solution)/shard_map/dot_general | solution.py:155
  27.0 0.8 collective-permute-done.3
  27.8 1.0 constant_dynamic-slice_fusion
  28.8 0.6 collective-permute-start.4
  29.4 4.1 %convolution_add_fusion.2 = f32[1280,1280]{1,0:T(8,128)S(1)} fusion(f32[1280,1280]{1,0:T(8,128)} %fusion.6, bf16[128,1280]{1,0:T(8,128)(2,1)} %collective-permute-done.1, bf16[128,1280]{1,0:T(8,128)(2,1)} %collective-permute-done.2), kind=kOutput, calls=%fused_computation.2 | convolution fusion | flops 421068800 | bytes 13762560 | tf_op jit(solution)/shard_map/dot_general | solution.py:155
  33.5 2.1 %convolution_add_fusion.1 = f32[1280,1280]{1,0:T(8,128)S(1)} fusion(f32[1280,1280]{1,0:T(8,128)S(1)} %convolution_add_fusion.2, bf16[128,1280]{1,0:T(8,128)(2,1)} %collective-permute-done.3, bf16[128,2560]{1,0:T(8,128)(2,1)} %collective-permute-done, s32[]{:T(128)S(6)} %select_n.694), kind=kOutput, calls=%fused_computation.1 | convolution fusion | flops 421068800 | bytes 13762564 | tf_op jit(solution)/shard_map/dot_general | solution.py:155
  35.7 2.5 %multiply_reduce_fusion = (f32[]{:T(128)}, f32[1280,1280]{1,0:T(8,128)S(1)}) fusion(f32[1280,1280]{1,0:T(8,128)S(1)} %convolution_add_fusion.1, bf16[128,1280]{1,0:T(8,128)(2,1)S(1)} %collective-permute-done.4, bf16[128,1280]{1,0:T(8,128)(2,1)S(1)} %collective-permute-done.5), kind=kOutput, calls=%fused_computation.4 | convolution fusion | flops 425984000 | bytes 13762564 | tf_op jit(solution)/shard_map/dot_general | solution.py:155
  38.2 1.7 %collective-permute-start.7 = (f32[1]{0:T(128)}, f32[1]{0:T(128)}, u32[]{:S(2)}, u32[]{:S(2)}) collective-permute-start(f32[1]{0:T(128)} %bitcast.4), channel_id=1, source_target_pairs={{0,16},{8,24},{16,0},{24,8},{1,17},{9,25},{17,1},{25,9},{2,18},{10... | collective-permute-start | bytes 20 | tf_op jit(solution)/shard_map/ppermute | solution.py:127
  39.9 0.4 collective-permute-start.6
  40.3 1.0 collective-permute-done.6
  42.6 0.5 collective-permute-done.8
  44.4 0.1 dynamic-slice_multiply_fusion.3
  44.5 1.6 %collective-permute-start.9 = (f32[40,1280]{1,0:T(8,128)S(1)}, f32[40,1280]{1,0:T(8,128)S(1)}, u32[]{:S(2)}, u32[]{:S(2)}) collective-permute-start(f32[40,1280]{1,0:T(8,128)S(1)} %get-tuple-element.78), channel_id=1, source_target_pairs={{0,1},{1,3},{3,5},{5,7},{7,6},{6,4},{4,2},{2,0},{8,9},{9,11},{11,1... | collective-permute-start | bytes 614408 | tf_op jit(solution)/shard_map/ppermute | solution.py:85
  46.1 0.5 collective-permute-start.16
  46.6 1.5 %collective-permute-start.23 = (f32[40,1280]{1,0:T(8,128)S(1)}, f32[40,1280]{1,0:T(8,128)S(1)}, u32[]{:S(2)}, u32[]{:S(2)}) collective-permute-start(f32[40,1280]{1,0:T(8,128)S(1)} %get-tuple-element.80), channel_id=1, source_target_pairs={{0,1},{1,3},{3,5},{5,7},{7,6},{6,4},{4,2},{2,0},{8,9},{9,11},{11,1... | collective-permute-start | bytes 614408 | tf_op jit(solution)/shard_map/ppermute | solution.py:85
  48.1 0.5 collective-permute-start.30
  48.9 1.2 %fusion.4 = bf16[512,1280]{1,0:T(8,128)(2,1)S(1)} fusion(bf16[512,1280]{1,0:T(8,128)(2,1)S(1)} %broadcast_in_dim.2, s32[]{:T(128)S(6)} %select_n.863, bf16[128,1280]{1,0:T(8,128)(2,1)S(1)} %bitcast.113, bf16[1280,1280]{1,0:T(8,128)(2,1)S(1)} %copy-done), kind=kOutput, calls=%fused_computation.12 | convolution fusion | flops 419594240 | bytes 3932164 | tf_op jit(solution)/shard_map/dot_general | solution.py:17
  50.1 2.5 %collective-permute-done.9 = f32[40,1280]{1,0:T(8,128)S(1)} collective-permute-done((f32[40,1280]{1,0:T(8,128)S(1)}, f32[40,1280]{1,0:T(8,128)S(1)}, u32[]{:S(2)}, u32[]{:S(2)}) %collective-permute-start.9) | collective-permute-done | bytes 204832 | tf_op jit(solution)/shard_map/ppermute | solution.py:85
  52.6 1.5 %collective-permute-start.10 = (f32[40,1280]{1,0:T(8,128)S(1)}, f32[40,1280]{1,0:T(8,128)S(1)}, u32[]{:S(2)}, u32[]{:S(2)}) collective-permute-start(f32[40,1280]{1,0:T(8,128)S(1)} %add.522), channel_id=1, source_target_pairs={{0,1},{1,3},{3,5},{5,7},{7,6},{6,4},{4,2},{2,0},{8,9},{9,11},{11,1... | collective-permute-start | bytes 614408 | tf_op jit(solution)/shard_map/ppermute | solution.py:85
  54.2 0.6 collective-permute-start.17
  54.8 2.2 %collective-permute-done.23 = f32[40,1280]{1,0:T(8,128)S(1)} collective-permute-done((f32[40,1280]{1,0:T(8,128)S(1)}, f32[40,1280]{1,0:T(8,128)S(1)}, u32[]{:S(2)}, u32[]{:S(2)}) %collective-permute-start.23) | collective-permute-done | bytes 204832 | tf_op jit(solution)/shard_map/ppermute | solution.py:85
  57.0 1.5 %collective-permute-start.24 = (f32[40,1280]{1,0:T(8,128)S(1)}, f32[40,1280]{1,0:T(8,128)S(1)}, u32[]{:S(2)}, u32[]{:S(2)}) collective-permute-start(f32[40,1280]{1,0:T(8,128)S(1)} %add.584), channel_id=1, source_target_pairs={{0,1},{1,3},{3,5},{5,7},{7,6},{6,4},{4,2},{2,0},{8,9},{9,11},{11,1... | collective-permute-start | bytes 614408 | tf_op jit(solution)/shard_map/ppermute | solution.py:85
  58.6 0.6 collective-permute-start.31
  59.3 2.2 %fusion.3 = bf16[512,1280]{1,0:T(8,128)(2,1)S(1)} fusion(bf16[512,1280]{1,0:T(8,128)(2,1)S(1)} %fusion.4, s32[]{:T(128)S(6)} %select_n.864, bf16[128,1280]{1,0:T(8,128)(2,1)} %collective-permute-done.2, bf16[1280,1280]{1,0:T(8,128)(2,1)S(1)} %copy-done), kind=kOutput, calls=%fused_computation.10 | convolution fusion | flops 419594240 | bytes 3932164 | tf_op jit(solution)/shard_map/dot_general | solution.py:17
  61.5 1.5 %collective-permute-start.11 = (f32[40,1280]{1,0:T(8,128)S(1)}, f32[40,1280]{1,0:T(8,128)S(1)}, u32[]{:S(2)}, u32[]{:S(2)}) collective-permute-start(f32[40,1280]{1,0:T(8,128)S(1)} %add.525), channel_id=1, source_target_pairs={{0,1},{1,3},{3,5},{5,7},{7,6},{6,4},{4,2},{2,0},{8,9},{9,11},{11,1... | collective-permute-start | bytes 614408 | tf_op jit(solution)/shard_map/ppermute | solution.py:85
  63.1 0.6 collective-permute-start.18
  63.6 2.1 %collective-permute-done.24 = f32[40,1280]{1,0:T(8,128)S(1)} collective-permute-done((f32[40,1280]{1,0:T(8,128)S(1)}, f32[40,1280]{1,0:T(8,128)S(1)}, u32[]{:S(2)}, u32[]{:S(2)}) %collective-permute-start.24) | collective-permute-done | bytes 204832 | tf_op jit(solution)/shard_map/ppermute | solution.py:85
  65.8 1.5 %collective-permute-start.25 = (f32[40,1280]{1,0:T(8,128)S(1)}, f32[40,1280]{1,0:T(8,128)S(1)}, u32[]{:S(2)}, u32[]{:S(2)}) collective-permute-start(f32[40,1280]{1,0:T(8,128)S(1)} %add.587), channel_id=1, source_target_pairs={{0,1},{1,3},{3,5},{5,7},{7,6},{6,4},{4,2},{2,0},{8,9},{9,11},{11,1... | collective-permute-start | bytes 614408 | tf_op jit(solution)/shard_map/ppermute | solution.py:85
  67.3 0.6 collective-permute-start.32
  68.0 2.2 %fusion.2 = bf16[512,1280]{1,0:T(8,128)(2,1)S(1)} fusion(bf16[512,1280]{1,0:T(8,128)(2,1)S(1)} %fusion.3, s32[]{:T(128)S(6)} %select_n.865, bf16[128,1280]{1,0:T(8,128)(2,1)} %collective-permute-done.3, bf16[1280,1280]{1,0:T(8,128)(2,1)S(1)} %copy-done), kind=kOutput, calls=%fused_computation.8 | convolution fusion | flops 419594240 | bytes 3932164 | tf_op jit(solution)/shard_map/dot_general | solution.py:17
  70.3 1.6 %collective-permute-start.12 = (f32[40,1280]{1,0:T(8,128)S(1)}, f32[40,1280]{1,0:T(8,128)S(1)}, u32[]{:S(2)}, u32[]{:S(2)}) collective-permute-start(f32[40,1280]{1,0:T(8,128)S(1)} %add.528), channel_id=1, source_target_pairs={{0,1},{1,3},{3,5},{5,7},{7,6},{6,4},{4,2},{2,0},{8,9},{9,11},{11,1... | collective-permute-start | bytes 614408 | tf_op jit(solution)/shard_map/ppermute | solution.py:85
  71.8 0.6 collective-permute-start.19
  72.4 2.1 %collective-permute-done.25 = f32[40,1280]{1,0:T(8,128)S(1)} collective-permute-done((f32[40,1280]{1,0:T(8,128)S(1)}, f32[40,1280]{1,0:T(8,128)S(1)}, u32[]{:S(2)}, u32[]{:S(2)}) %collective-permute-start.25) | collective-permute-done | bytes 204832 | tf_op jit(solution)/shard_map/ppermute | solution.py:85
  74.5 1.5 %collective-permute-start.26 = (f32[40,1280]{1,0:T(8,128)S(1)}, f32[40,1280]{1,0:T(8,128)S(1)}, u32[]{:S(2)}, u32[]{:S(2)}) collective-permute-start(f32[40,1280]{1,0:T(8,128)S(1)} %add.590), channel_id=1, source_target_pairs={{0,1},{1,3},{3,5},{5,7},{7,6},{6,4},{4,2},{2,0},{8,9},{9,11},{11,1... | collective-permute-start | bytes 614408 | tf_op jit(solution)/shard_map/ppermute | solution.py:85
  76.1 0.6 collective-permute-start.33
  76.8 1.2 %fusion.1 = bf16[512,1280]{1,0:T(8,128)(2,1)S(1)} fusion(bf16[512,1280]{1,0:T(8,128)(2,1)S(1)} %fusion.2, s32[]{:T(128)S(6)} %select_n.866, bf16[128,1280]{1,0:T(8,128)(2,1)S(1)} %collective-permute-done.5, bf16[1280,1280]{1,0:T(8,128)(2,1)S(1)} %copy-done), kind=kOutput, calls=%fused_computation.6 | convolution fusion | flops 419594240 | bytes 3932164 | tf_op jit(solution)/shard_map/dot_general | solution.py:17
  78.0 0.9 collective-permute-done.12
  78.9 1.5 %collective-permute-start.13 = (f32[40,1280]{1,0:T(8,128)S(1)}, f32[40,1280]{1,0:T(8,128)S(1)}, u32[]{:S(2)}, u32[]{:S(2)}) collective-permute-start(f32[40,1280]{1,0:T(8,128)S(1)} %add.531), channel_id=1, source_target_pairs={{0,1},{1,3},{3,5},{5,7},{7,6},{6,4},{4,2},{2,0},{8,9},{9,11},{11,1... | collective-permute-start | bytes 614408 | tf_op jit(solution)/shard_map/ppermute | solution.py:85
  80.5 0.6 collective-permute-start.20
  81.1 2.2 %collective-permute-done.26 = f32[40,1280]{1,0:T(8,128)S(1)} collective-permute-done((f32[40,1280]{1,0:T(8,128)S(1)}, f32[40,1280]{1,0:T(8,128)S(1)}, u32[]{:S(2)}, u32[]{:S(2)}) %collective-permute-start.26) | collective-permute-done | bytes 204832 | tf_op jit(solution)/shard_map/ppermute | solution.py:85
  83.3 1.5 %collective-permute-start.27 = (f32[40,1280]{1,0:T(8,128)S(1)}, f32[40,1280]{1,0:T(8,128)S(1)}, u32[]{:S(2)}, u32[]{:S(2)}) collective-permute-start(f32[40,1280]{1,0:T(8,128)S(1)} %add.593), channel_id=1, source_target_pairs={{0,1},{1,3},{3,5},{5,7},{7,6},{6,4},{4,2},{2,0},{8,9},{9,11},{11,1... | collective-permute-start | bytes 614408 | tf_op jit(solution)/shard_map/ppermute | solution.py:85
  84.9 0.6 collective-permute-start.34
  85.6 2.0 %collective-permute-done.13 = f32[40,1280]{1,0:T(8,128)S(1)} collective-permute-done((f32[40,1280]{1,0:T(8,128)S(1)}, f32[40,1280]{1,0:T(8,128)S(1)}, u32[]{:S(2)}, u32[]{:S(2)}) %collective-permute-start.13) | collective-permute-done | bytes 204832 | tf_op jit(solution)/shard_map/ppermute | solution.py:85
  87.7 1.5 %collective-permute-start.14 = (f32[40,1280]{1,0:T(8,128)S(1)}, f32[40,1280]{1,0:T(8,128)S(1)}, u32[]{:S(2)}, u32[]{:S(2)}) collective-permute-start(f32[40,1280]{1,0:T(8,128)S(1)} %add.534), channel_id=1, source_target_pairs={{0,1},{1,3},{3,5},{5,7},{7,6},{6,4},{4,2},{2,0},{8,9},{9,11},{11,1... | collective-permute-start | bytes 614408 | tf_op jit(solution)/shard_map/ppermute | solution.py:85
  89.3 0.6 collective-permute-start.21
  89.9 2.2 %collective-permute-done.27 = f32[40,1280]{1,0:T(8,128)S(1)} collective-permute-done((f32[40,1280]{1,0:T(8,128)S(1)}, f32[40,1280]{1,0:T(8,128)S(1)}, u32[]{:S(2)}, u32[]{:S(2)}) %collective-permute-start.27) | collective-permute-done | bytes 204832 | tf_op jit(solution)/shard_map/ppermute | solution.py:85
  92.1 1.5 %collective-permute-start.28 = (f32[40,1280]{1,0:T(8,128)S(1)}, f32[40,1280]{1,0:T(8,128)S(1)}, u32[]{:S(2)}, u32[]{:S(2)}) collective-permute-start(f32[40,1280]{1,0:T(8,128)S(1)} %add.596), channel_id=1, source_target_pairs={{0,1},{1,3},{3,5},{5,7},{7,6},{6,4},{4,2},{2,0},{8,9},{9,11},{11,1... | collective-permute-start | bytes 614408 | tf_op jit(solution)/shard_map/ppermute | solution.py:85
  93.7 0.6 collective-permute-start.35
  94.4 2.1 %collective-permute-done.14 = f32[40,1280]{1,0:T(8,128)S(1)} collective-permute-done((f32[40,1280]{1,0:T(8,128)S(1)}, f32[40,1280]{1,0:T(8,128)S(1)}, u32[]{:S(2)}, u32[]{:S(2)}) %collective-permute-start.14) | collective-permute-done | bytes 204832 | tf_op jit(solution)/shard_map/ppermute | solution.py:85
  96.5 1.5 %collective-permute-start.15 = (f32[40,1280]{1,0:T(8,128)S(1)}, f32[40,1280]{1,0:T(8,128)S(1)}, u32[]{:S(2)}, u32[]{:S(2)}) collective-permute-start(f32[40,1280]{1,0:T(8,128)S(1)} %add.537), channel_id=1, source_target_pairs={{0,1},{1,3},{3,5},{5,7},{7,6},{6,4},{4,2},{2,0},{8,9},{9,11},{11,1... | collective-permute-start | bytes 614408 | tf_op jit(solution)/shard_map/ppermute | solution.py:85
  98.1 0.6 collective-permute-start.22
  98.6 2.2 %collective-permute-done.28 = f32[40,1280]{1,0:T(8,128)S(1)} collective-permute-done((f32[40,1280]{1,0:T(8,128)S(1)}, f32[40,1280]{1,0:T(8,128)S(1)}, u32[]{:S(2)}, u32[]{:S(2)}) %collective-permute-start.28) | collective-permute-done | bytes 204832 | tf_op jit(solution)/shard_map/ppermute | solution.py:85
  100.9 1.5 %collective-permute-start.29 = (f32[40,1280]{1,0:T(8,128)S(1)}, f32[40,1280]{1,0:T(8,128)S(1)}, u32[]{:S(2)}, u32[]{:S(2)}) collective-permute-start(f32[40,1280]{1,0:T(8,128)S(1)} %add.599), channel_id=1, source_target_pairs={{0,1},{1,3},{3,5},{5,7},{7,6},{6,4},{4,2},{2,0},{8,9},{9,11},{11,1... | collective-permute-start | bytes 614408 | tf_op jit(solution)/shard_map/ppermute | solution.py:85
  102.4 0.6 collective-permute-start.36
  103.1 2.1 %collective-permute-done.15 = f32[40,1280]{1,0:T(8,128)S(1)} collective-permute-done((f32[40,1280]{1,0:T(8,128)S(1)}, f32[40,1280]{1,0:T(8,128)S(1)}, u32[]{:S(2)}, u32[]{:S(2)}) %collective-permute-start.15) | collective-permute-done | bytes 204832 | tf_op jit(solution)/shard_map/ppermute | solution.py:85
  105.3 1.5 %collective-permute-done.22 = f32[40,1280]{1,0:T(8,128)S(1)} collective-permute-done((f32[40,1280]{1,0:T(8,128)S(1)}, f32[40,1280]{1,0:T(8,128)S(1)}, u32[]{:S(2)}, u32[]{:S(2)}) %collective-permute-start.22) | collective-permute-done | bytes 204832 | tf_op jit(solution)/shard_map/ppermute | solution.py:85
  106.8 1.7 %collective-permute-done.29 = f32[40,1280]{1,0:T(8,128)S(1)} collective-permute-done((f32[40,1280]{1,0:T(8,128)S(1)}, f32[40,1280]{1,0:T(8,128)S(1)}, u32[]{:S(2)}, u32[]{:S(2)}) %collective-permute-start.29) | collective-permute-done | bytes 204832 | tf_op jit(solution)/shard_map/ppermute | solution.py:85
  108.5 1.4 %collective-permute-done.36 = f32[40,1280]{1,0:T(8,128)S(1)} collective-permute-done((f32[40,1280]{1,0:T(8,128)S(1)}, f32[40,1280]{1,0:T(8,128)S(1)}, u32[]{:S(2)}, u32[]{:S(2)}) %collective-permute-start.36) | collective-permute-done | bytes 204832 | tf_op jit(solution)/shard_map/ppermute | solution.py:85
  110.0 2.0 %add_divide_fusion = (f32[160,1280]{1,0:T(8,128)}, f32[160,1280]{1,0:T(8,128)}, f32[160,1280]{1,0:T(8,128)}, f32[160,1280]{1,0:T(8,128)}) fusion(f32[160,1280]{1,0:T(8,128)S(1)} %copy-done.3, f32[160,1280]{1,0:T(8,128)S(1)} %copy-done.4, f32[160,1280]{1,0:T(8,128)S(1)} %copy-done.5, f32[40,1280]{1,0:T(8,128)S(1)} %add.625, f32[40,1280]{1,0:T(8,128)S(1)} %add.602, ...), kind=kLoop, calls=%fused_computation.16 | loop fusion | flops 3481600 | bytes 6553600 | tf_op jit(solution)/shard_map/div | solution.py:206
  (92 shorter events, 1.6 us)
Async XLA Ops:
  0.6 48.2 %copy-start = (bf16[1280,1280]{1,0:T(8,128)(2,1)S(1)}, bf16[1280,1280]{1,0:T(8,128)(2,1)}, u32[]{:S(2)}) copy-start(bf16[1280,1280]{1,0:T(8,128)(2,1)} %param.8) | copy-start | bytes 9830404
  2.8 18.8 %collective-permute-start = (bf16[128,2560]{1,0:T(8,128)(2,1)}, bf16[128,2560]{1,0:T(8,128)(2,1)}, u32[]{:S(2)}, u32[]{:S(2)}) collective-permute-start(bf16[128,2560]{1,0:T(8,128)(2,1)} %dynamic-slice_bitcast_fusion), channel_id=1, source_target_pairs={{0,16},{8,24},{16,0},{24,8},{1,17},{9,25},{17,1},{25,9},{2,18},{10... | collective-permute-start | bytes 1966088 | tf_op jit(solution)/shard_map/ppermute | solution.py:107
  5.7 22.1 %collective-permute-start.3 = (bf16[128,1280]{1,0:T(8,128)(2,1)}, bf16[128,1280]{1,0:T(8,128)(2,1)}, u32[]{:S(2)}, u32[]{:S(2)}) collective-permute-start(bf16[128,1280]{1,0:T(8,128)(2,1)} %bitcast.111), channel_id=1, source_target_pairs={{0,16},{8,24},{16,0},{24,8},{1,17},{9,25},{17,1},{25,9},{2,18},{10... | collective-permute-start | bytes 983048 | tf_op jit(solution)/shard_map/ppermute | solution.py:105
  21.6 7.8 %collective-permute-start.2 = (bf16[128,1280]{1,0:T(8,128)(2,1)}, bf16[128,1280]{1,0:T(8,128)(2,1)}, u32[]{:S(2)}, u32[]{:S(2)}) collective-permute-start(bf16[128,1280]{1,0:T(8,128)(2,1)} %bitcast.112), channel_id=1, source_target_pairs={{0,8},{8,0},{16,24},{24,16},{1,9},{9,1},{17,25},{25,17},{2,10},{10... | collective-permute-start | bytes 983048 | tf_op jit(solution)/shard_map/ppermute | solution.py:111
  21.6 7.8 %collective-permute-start.1 = (bf16[128,1280]{1,0:T(8,128)(2,1)}, bf16[128,1280]{1,0:T(8,128)(2,1)}, u32[]{:S(2)}, u32[]{:S(2)}) collective-permute-start(bf16[128,1280]{1,0:T(8,128)(2,1)} %dynamic-slice_bitcast_fusion.1), channel_id=1, source_target_pairs={{0,8},{8,0},{16,24},{24,16},{1,9},{9,1},{17,25},{25,17},{2,10},{10... | collective-permute-start | bytes 983048 | tf_op jit(solution)/shard_map/ppermute | solution.py:112
  27.8 7.9 %collective-permute-start.5 = (bf16[128,1280]{1,0:T(8,128)(2,1)}, bf16[128,1280]{1,0:T(8,128)(2,1)S(1)}, u32[]{:S(2)}, u32[]{:S(2)}) collective-permute-start(bf16[128,1280]{1,0:T(8,128)(2,1)} %collective-permute-done.3), channel_id=1, source_target_pairs={{0,8},{8,0},{16,24},{24,16},{1,9},{9,1},{17,25},{25,17},{2,10},{10... | collective-permute-start | bytes 983048 | tf_op jit(solution)/shard_map/ppermute | solution.py:113
  28.8 6.9 %collective-permute-start.4 = (bf16[128,1280]{1,0:T(8,128)(2,1)S(1)}, bf16[128,1280]{1,0:T(8,128)(2,1)S(1)}, u32[]{:S(2)}, u32[]{:S(2)}) collective-permute-start(bf16[128,1280]{1,0:T(8,128)(2,1)S(1)} %constant_dynamic-slice_fusion), channel_id=1, source_target_pairs={{0,8},{8,0},{16,24},{24,16},{1,9},{9,1},{17,25},{25,17},{2,10},{10... | collective-permute-start | bytes 983048 | tf_op jit(solution)/shard_map/ppermute | solution.py:114
  35.6 13.2 %copy-start.1 = (bf16[1,1,128,1280]{3,2,1,0:T(8,128)(2,1)S(1)}, bf16[1,1,128,1280]{3,2,1,0:T(8,128)(2,1)}, u32[]{:S(2)}) copy-start(bf16[1,1,128,1280]{3,2,1,0:T(8,128)(2,1)} %param.7) | copy-start | bytes 983044
  38.2 4.4 %collective-permute-start.7 = (f32[1]{0:T(128)}, f32[1]{0:T(128)}, u32[]{:S(2)}, u32[]{:S(2)}) collective-permute-start(f32[1]{0:T(128)} %bitcast.4), channel_id=1, source_target_pairs={{0,16},{8,24},{16,0},{24,8},{1,17},{9,25},{17,1},{25,9},{2,18},{10... | collective-permute-start | bytes 20 | tf_op jit(solution)/shard_map/ppermute | solution.py:127
  39.9 3.2 %collective-permute-start.8 = (f32[1]{0:T(128)}, f32[1]{0:T(128)}, u32[]{:S(2)}, u32[]{:S(2)}) collective-permute-start(f32[1]{0:T(128)} %bitcast.4), channel_id=1, source_target_pairs={{0,24},{8,16},{16,8},{24,0},{1,25},{9,17},{17,9},{25,1},{2,26},{10... | collective-permute-start | bytes 20 | tf_op jit(solution)/shard_map/ppermute | solution.py:127
  39.9 1.4 %collective-permute-start.6 = (f32[1]{0:T(128)}, f32[1]{0:T(128)}, u32[]{:S(2)}, u32[]{:S(2)}) collective-permute-start(f32[1]{0:T(128)} %bitcast.4), channel_id=1, source_target_pairs={{0,8},{8,0},{16,24},{24,16},{1,9},{9,1},{17,25},{25,17},{2,10},{10... | collective-permute-start | bytes 20 | tf_op jit(solution)/shard_map/ppermute | solution.py:127
  44.5 8.0 %collective-permute-start.9 = (f32[40,1280]{1,0:T(8,128)S(1)}, f32[40,1280]{1,0:T(8,128)S(1)}, u32[]{:S(2)}, u32[]{:S(2)}) collective-permute-start(f32[40,1280]{1,0:T(8,128)S(1)} %get-tuple-element.78), channel_id=1, source_target_pairs={{0,1},{1,3},{3,5},{5,7},{7,6},{6,4},{4,2},{2,0},{8,9},{9,11},{11,1... | collective-permute-start | bytes 614408 | tf_op jit(solution)/shard_map/ppermute | solution.py:85
  46.1 8.0 %collective-permute-start.16 = (f32[40,1280]{1,0:T(8,128)S(1)}, f32[40,1280]{1,0:T(8,128)S(1)}, u32[]{:S(2)}, u32[]{:S(2)}) collective-permute-start(f32[40,1280]{1,0:T(8,128)S(1)} %get-tuple-element.81), channel_id=1, source_target_pairs={{0,2},{1,0},{3,1},{5,3},{7,5},{6,7},{4,6},{2,4},{8,10},{9,8},{11,9... | collective-permute-start | bytes 614408 | tf_op jit(solution)/shard_map/ppermute | solution.py:85
  46.6 10.3 %collective-permute-start.23 = (f32[40,1280]{1,0:T(8,128)S(1)}, f32[40,1280]{1,0:T(8,128)S(1)}, u32[]{:S(2)}, u32[]{:S(2)}) collective-permute-start(f32[40,1280]{1,0:T(8,128)S(1)} %get-tuple-element.80), channel_id=1, source_target_pairs={{0,1},{1,3},{3,5},{5,7},{7,6},{6,4},{4,2},{2,0},{8,9},{9,11},{11,1... | collective-permute-start | bytes 614408 | tf_op jit(solution)/shard_map/ppermute | solution.py:85
  48.1 10.4 %collective-permute-start.30 = (f32[40,1280]{1,0:T(8,128)S(1)}, f32[40,1280]{1,0:T(8,128)S(1)}, u32[]{:S(2)}, u32[]{:S(2)}) collective-permute-start(f32[40,1280]{1,0:T(8,128)S(1)} %get-tuple-element.79), channel_id=1, source_target_pairs={{0,2},{1,0},{3,1},{5,3},{7,5},{6,7},{4,6},{2,4},{8,10},{9,8},{11,9... | collective-permute-start | bytes 614408 | tf_op jit(solution)/shard_map/ppermute | solution.py:85
  52.6 8.9 %collective-permute-start.10 = (f32[40,1280]{1,0:T(8,128)S(1)}, f32[40,1280]{1,0:T(8,128)S(1)}, u32[]{:S(2)}, u32[]{:S(2)}) collective-permute-start(f32[40,1280]{1,0:T(8,128)S(1)} %add.522), channel_id=1, source_target_pairs={{0,1},{1,3},{3,5},{5,7},{7,6},{6,4},{4,2},{2,0},{8,9},{9,11},{11,1... | collective-permute-start | bytes 614408 | tf_op jit(solution)/shard_map/ppermute | solution.py:85
  54.2 8.9 %collective-permute-start.17 = (f32[40,1280]{1,0:T(8,128)S(1)}, f32[40,1280]{1,0:T(8,128)S(1)}, u32[]{:S(2)}, u32[]{:S(2)}) collective-permute-start(f32[40,1280]{1,0:T(8,128)S(1)} %add.549), channel_id=1, source_target_pairs={{0,2},{1,0},{3,1},{5,3},{7,5},{6,7},{4,6},{2,4},{8,10},{9,8},{11,9... | collective-permute-start | bytes 614408 | tf_op jit(solution)/shard_map/ppermute | solution.py:85
  57.0 8.7 %collective-permute-start.24 = (f32[40,1280]{1,0:T(8,128)S(1)}, f32[40,1280]{1,0:T(8,128)S(1)}, u32[]{:S(2)}, u32[]{:S(2)}) collective-permute-start(f32[40,1280]{1,0:T(8,128)S(1)} %add.584), channel_id=1, source_target_pairs={{0,1},{1,3},{3,5},{5,7},{7,6},{6,4},{4,2},{2,0},{8,9},{9,11},{11,1... | collective-permute-start | bytes 614408 | tf_op jit(solution)/shard_map/ppermute | solution.py:85
  58.6 8.7 %collective-permute-start.31 = (f32[40,1280]{1,0:T(8,128)S(1)}, f32[40,1280]{1,0:T(8,128)S(1)}, u32[]{:S(2)}, u32[]{:S(2)}) collective-permute-start(f32[40,1280]{1,0:T(8,128)S(1)} %add.607), channel_id=1, source_target_pairs={{0,2},{1,0},{3,1},{5,3},{7,5},{6,7},{4,6},{2,4},{8,10},{9,8},{11,9... | collective-permute-start | bytes 614408 | tf_op jit(solution)/shard_map/ppermute | solution.py:85
  61.5 8.7 %collective-permute-start.11 = (f32[40,1280]{1,0:T(8,128)S(1)}, f32[40,1280]{1,0:T(8,128)S(1)}, u32[]{:S(2)}, u32[]{:S(2)}) collective-permute-start(f32[40,1280]{1,0:T(8,128)S(1)} %add.525), channel_id=1, source_target_pairs={{0,1},{1,3},{3,5},{5,7},{7,6},{6,4},{4,2},{2,0},{8,9},{9,11},{11,1... | collective-permute-start | bytes 614408 | tf_op jit(solution)/shard_map/ppermute | solution.py:85
  63.1 8.8 %collective-permute-start.18 = (f32[40,1280]{1,0:T(8,128)S(1)}, f32[40,1280]{1,0:T(8,128)S(1)}, u32[]{:S(2)}, u32[]{:S(2)}) collective-permute-start(f32[40,1280]{1,0:T(8,128)S(1)} %add.554), channel_id=1, source_target_pairs={{0,2},{1,0},{3,1},{5,3},{7,5},{6,7},{4,6},{2,4},{8,10},{9,8},{11,9... | collective-permute-start | bytes 614408 | tf_op jit(solution)/shard_map/ppermute | solution.py:85
  65.8 8.7 %collective-permute-start.25 = (f32[40,1280]{1,0:T(8,128)S(1)}, f32[40,1280]{1,0:T(8,128)S(1)}, u32[]{:S(2)}, u32[]{:S(2)}) collective-permute-start(f32[40,1280]{1,0:T(8,128)S(1)} %add.587), channel_id=1, source_target_pairs={{0,1},{1,3},{3,5},{5,7},{7,6},{6,4},{4,2},{2,0},{8,9},{9,11},{11,1... | collective-permute-start | bytes 614408 | tf_op jit(solution)/shard_map/ppermute | solution.py:85
  67.3 8.7 %collective-permute-start.32 = (f32[40,1280]{1,0:T(8,128)S(1)}, f32[40,1280]{1,0:T(8,128)S(1)}, u32[]{:S(2)}, u32[]{:S(2)}) collective-permute-start(f32[40,1280]{1,0:T(8,128)S(1)} %add.610), channel_id=1, source_target_pairs={{0,2},{1,0},{3,1},{5,3},{7,5},{6,7},{4,6},{2,4},{8,10},{9,8},{11,9... | collective-permute-start | bytes 614408 | tf_op jit(solution)/shard_map/ppermute | solution.py:85
  70.3 8.6 %collective-permute-start.12 = (f32[40,1280]{1,0:T(8,128)S(1)}, f32[40,1280]{1,0:T(8,128)S(1)}, u32[]{:S(2)}, u32[]{:S(2)}) collective-permute-start(f32[40,1280]{1,0:T(8,128)S(1)} %add.528), channel_id=1, source_target_pairs={{0,1},{1,3},{3,5},{5,7},{7,6},{6,4},{4,2},{2,0},{8,9},{9,11},{11,1... | collective-permute-start | bytes 614408 | tf_op jit(solution)/shard_map/ppermute | solution.py:85
  71.8 8.6 %collective-permute-start.19 = (f32[40,1280]{1,0:T(8,128)S(1)}, f32[40,1280]{1,0:T(8,128)S(1)}, u32[]{:S(2)}, u32[]{:S(2)}) collective-permute-start(f32[40,1280]{1,0:T(8,128)S(1)} %add.559), channel_id=1, source_target_pairs={{0,2},{1,0},{3,1},{5,3},{7,5},{6,7},{4,6},{2,4},{8,10},{9,8},{11,9... | collective-permute-start | bytes 614408 | tf_op jit(solution)/shard_map/ppermute | solution.py:85
  74.5 8.7 %collective-permute-start.26 = (f32[40,1280]{1,0:T(8,128)S(1)}, f32[40,1280]{1,0:T(8,128)S(1)}, u32[]{:S(2)}, u32[]{:S(2)}) collective-permute-start(f32[40,1280]{1,0:T(8,128)S(1)} %add.590), channel_id=1, source_target_pairs={{0,1},{1,3},{3,5},{5,7},{7,6},{6,4},{4,2},{2,0},{8,9},{9,11},{11,1... | collective-permute-start | bytes 614408 | tf_op jit(solution)/shard_map/ppermute | solution.py:85
  76.1 8.8 %collective-permute-start.33 = (f32[40,1280]{1,0:T(8,128)S(1)}, f32[40,1280]{1,0:T(8,128)S(1)}, u32[]{:S(2)}, u32[]{:S(2)}) collective-permute-start(f32[40,1280]{1,0:T(8,128)S(1)} %add.613), channel_id=1, source_target_pairs={{0,2},{1,0},{3,1},{5,3},{7,5},{6,7},{4,6},{2,4},{8,10},{9,8},{11,9... | collective-permute-start | bytes 614408 | tf_op jit(solution)/shard_map/ppermute | solution.py:85
  78.0 28.8 %copy-start.2 = (bf16[512,1280]{1,0:T(8,128)(2,1)}, bf16[512,1280]{1,0:T(8,128)(2,1)S(1)}, u32[]{:S(2)}) copy-start(bf16[512,1280]{1,0:T(8,128)(2,1)S(1)} %fusion.1) | copy-start | bytes 3932164
  78.9 8.7 %collective-permute-start.13 = (f32[40,1280]{1,0:T(8,128)S(1)}, f32[40,1280]{1,0:T(8,128)S(1)}, u32[]{:S(2)}, u32[]{:S(2)}) collective-permute-start(f32[40,1280]{1,0:T(8,128)S(1)} %add.531), channel_id=1, source_target_pairs={{0,1},{1,3},{3,5},{5,7},{7,6},{6,4},{4,2},{2,0},{8,9},{9,11},{11,1... | collective-permute-start | bytes 614408 | tf_op jit(solution)/shard_map/ppermute | solution.py:85
  80.5 8.8 %collective-permute-start.20 = (f32[40,1280]{1,0:T(8,128)S(1)}, f32[40,1280]{1,0:T(8,128)S(1)}, u32[]{:S(2)}, u32[]{:S(2)}) collective-permute-start(f32[40,1280]{1,0:T(8,128)S(1)} %add.564), channel_id=1, source_target_pairs={{0,2},{1,0},{3,1},{5,3},{7,5},{6,7},{4,6},{2,4},{8,10},{9,8},{11,9... | collective-permute-start | bytes 614408 | tf_op jit(solution)/shard_map/ppermute | solution.py:85
  83.3 26.6 %copy-start.3 = (f32[160,1280]{1,0:T(8,128)S(1)}, f32[160,1280]{1,0:T(8,128)}, u32[]{:S(2)}) copy-start(f32[160,1280]{1,0:T(8,128)} %param.11) | copy-start | bytes 2457604
  83.3 26.6 %copy-start.4 = (f32[160,1280]{1,0:T(8,128)S(1)}, f32[160,1280]{1,0:T(8,128)}, u32[]{:S(2)}) copy-start(f32[160,1280]{1,0:T(8,128)} %param.10) | copy-start | bytes 2457604
  83.3 26.6 %copy-start.5 = (f32[160,1280]{1,0:T(8,128)S(1)}, f32[160,1280]{1,0:T(8,128)}, u32[]{:S(2)}) copy-start(f32[160,1280]{1,0:T(8,128)} %param.9) | copy-start | bytes 2457604
  83.3 8.7 %collective-permute-start.27 = (f32[40,1280]{1,0:T(8,128)S(1)}, f32[40,1280]{1,0:T(8,128)S(1)}, u32[]{:S(2)}, u32[]{:S(2)}) collective-permute-start(f32[40,1280]{1,0:T(8,128)S(1)} %add.593), channel_id=1, source_target_pairs={{0,1},{1,3},{3,5},{5,7},{7,6},{6,4},{4,2},{2,0},{8,9},{9,11},{11,1... | collective-permute-start | bytes 614408 | tf_op jit(solution)/shard_map/ppermute | solution.py:85
  84.9 8.7 %collective-permute-start.34 = (f32[40,1280]{1,0:T(8,128)S(1)}, f32[40,1280]{1,0:T(8,128)S(1)}, u32[]{:S(2)}, u32[]{:S(2)}) collective-permute-start(f32[40,1280]{1,0:T(8,128)S(1)} %add.616), channel_id=1, source_target_pairs={{0,2},{1,0},{3,1},{5,3},{7,5},{6,7},{4,6},{2,4},{8,10},{9,8},{11,9... | collective-permute-start | bytes 614408 | tf_op jit(solution)/shard_map/ppermute | solution.py:85
  87.7 8.7 %collective-permute-start.14 = (f32[40,1280]{1,0:T(8,128)S(1)}, f32[40,1280]{1,0:T(8,128)S(1)}, u32[]{:S(2)}, u32[]{:S(2)}) collective-permute-start(f32[40,1280]{1,0:T(8,128)S(1)} %add.534), channel_id=1, source_target_pairs={{0,1},{1,3},{3,5},{5,7},{7,6},{6,4},{4,2},{2,0},{8,9},{9,11},{11,1... | collective-permute-start | bytes 614408 | tf_op jit(solution)/shard_map/ppermute | solution.py:85
  89.3 8.7 %collective-permute-start.21 = (f32[40,1280]{1,0:T(8,128)S(1)}, f32[40,1280]{1,0:T(8,128)S(1)}, u32[]{:S(2)}, u32[]{:S(2)}) collective-permute-start(f32[40,1280]{1,0:T(8,128)S(1)} %add.569), channel_id=1, source_target_pairs={{0,2},{1,0},{3,1},{5,3},{7,5},{6,7},{4,6},{2,4},{8,10},{9,8},{11,9... | collective-permute-start | bytes 614408 | tf_op jit(solution)/shard_map/ppermute | solution.py:85
  92.1 8.8 %collective-permute-start.28 = (f32[40,1280]{1,0:T(8,128)S(1)}, f32[40,1280]{1,0:T(8,128)S(1)}, u32[]{:S(2)}, u32[]{:S(2)}) collective-permute-start(f32[40,1280]{1,0:T(8,128)S(1)} %add.596), channel_id=1, source_target_pairs={{0,1},{1,3},{3,5},{5,7},{7,6},{6,4},{4,2},{2,0},{8,9},{9,11},{11,1... | collective-permute-start | bytes 614408 | tf_op jit(solution)/shard_map/ppermute | solution.py:85
  93.7 8.8 %collective-permute-start.35 = (f32[40,1280]{1,0:T(8,128)S(1)}, f32[40,1280]{1,0:T(8,128)S(1)}, u32[]{:S(2)}, u32[]{:S(2)}) collective-permute-start(f32[40,1280]{1,0:T(8,128)S(1)} %add.619), channel_id=1, source_target_pairs={{0,2},{1,0},{3,1},{5,3},{7,5},{6,7},{4,6},{2,4},{8,10},{9,8},{11,9... | collective-permute-start | bytes 614408 | tf_op jit(solution)/shard_map/ppermute | solution.py:85
  96.5 8.7 %collective-permute-start.15 = (f32[40,1280]{1,0:T(8,128)S(1)}, f32[40,1280]{1,0:T(8,128)S(1)}, u32[]{:S(2)}, u32[]{:S(2)}) collective-permute-start(f32[40,1280]{1,0:T(8,128)S(1)} %add.537), channel_id=1, source_target_pairs={{0,1},{1,3},{3,5},{5,7},{7,6},{6,4},{4,2},{2,0},{8,9},{9,11},{11,1... | collective-permute-start | bytes 614408 | tf_op jit(solution)/shard_map/ppermute | solution.py:85
  98.1 8.7 %collective-permute-start.22 = (f32[40,1280]{1,0:T(8,128)S(1)}, f32[40,1280]{1,0:T(8,128)S(1)}, u32[]{:S(2)}, u32[]{:S(2)}) collective-permute-start(f32[40,1280]{1,0:T(8,128)S(1)} %add.574), channel_id=1, source_target_pairs={{0,2},{1,0},{3,1},{5,3},{7,5},{6,7},{4,6},{2,4},{8,10},{9,8},{11,9... | collective-permute-start | bytes 614408 | tf_op jit(solution)/shard_map/ppermute | solution.py:85
  100.9 7.6 %collective-permute-start.29 = (f32[40,1280]{1,0:T(8,128)S(1)}, f32[40,1280]{1,0:T(8,128)S(1)}, u32[]{:S(2)}, u32[]{:S(2)}) collective-permute-start(f32[40,1280]{1,0:T(8,128)S(1)} %add.599), channel_id=1, source_target_pairs={{0,1},{1,3},{3,5},{5,7},{7,6},{6,4},{4,2},{2,0},{8,9},{9,11},{11,1... | collective-permute-start | bytes 614408 | tf_op jit(solution)/shard_map/ppermute | solution.py:85
  102.4 7.5 %collective-permute-start.36 = (f32[40,1280]{1,0:T(8,128)S(1)}, f32[40,1280]{1,0:T(8,128)S(1)}, u32[]{:S(2)}, u32[]{:S(2)}) collective-permute-start(f32[40,1280]{1,0:T(8,128)S(1)} %add.622), channel_id=1, source_target_pairs={{0,2},{1,0},{3,1},{5,3},{7,5},{6,7},{4,6},{2,4},{8,10},{9,8},{11,9... | collective-permute-start | bytes 614408 | tf_op jit(solution)/shard_map/ppermute | solution.py:85

commit v16 on v14

--- a/solution.py
+++ b/solution.py
@@ -104,13 +104,13 @@
     over_core = [(i, i ^ 1) for i in range(4)]
     g_far = lax.ppermute(grad_rows, "aug", over_x)
     h_far_relay = lax.ppermute(cols(a ^ 3), "aug", over_x)
-    _, (g_mine, h_mine) = lax.optimization_barrier((h_far_relay, (grad_rows, cols(a ^ 1))))
-    g_near = lax.ppermute(g_mine, "aug", over_core)
-    h_near = lax.ppermute(h_mine, "aug", over_core)
     g_relay = lax.ppermute(g_far, "aug", over_core)
     h_relay = lax.ppermute(h_far_relay, "aug", over_core)
     _, second = lax.optimization_barrier((h_far_relay, cols(a ^ 2)))
     h_far = lax.ppermute(second, "aug", over_x)
+    _, (g_mine, h_mine) = lax.optimization_barrier((h_far, (grad_rows, cols(a ^ 1))))
+    g_near = lax.ppermute(g_mine, "aug", over_core)
+    h_near = lax.ppermute(h_mine, "aug", over_core)
     return [
         (a * rows, cols(a), grad_rows),
         ((a ^ 1) * rows, h_near, g_near),

time: 108 us -> 111 us (1.028)
  waiting for transfers between devices: 45.7 us -> 48.7 us
    ppermute x1, waiting for transfers between devices: 5.45 us -> 8.93 us  [exchange_four(): h_far = lax.ppermute(second, 'aug', over_x)]
  transfers between devices with their start and end apart: 38 -> 38, of which waited for: 20 -> 20; matrix products, arithmetic and copies ran while one was open for 12% -> 11% of each run, Pallas kernels for 0% -> 0%
where the time goes in v16:
time: 111 us
  waiting for transfers between devices  48.7 us (44%)
  starting transfers between devices  37.4 us (34%)
  matrix products  13.5 us (12%)
  between operations  4.88 us (4%)
  other arithmetic  3.47 us (3%)
  local copies, waits for them, and re-layouts  3.08 us (3%)
    ppermute x28, starting transfers between devices, ring_reduce_scatter(): lax.ppermute(v, 'dp', right if step < 0 else left)  29.7 us
    ppermute x28, waiting for transfers between devices, ring_reduce_scatter(): lax.ppermute(v, 'dp', right if step < 0 else left)  28.4 us
    ppermute x1, waiting for transfers between devices, exchange_four(): h_far = lax.ppermute(second, 'aug', over_x)  8.93 us
    dot_general x4, matrix products, per_device(): term = jnp.dot(h_piece.T, g_piece, preferred_element_type=jnp.float32)  7.77 us
    ppermute x1, waiting for transfers between devices, exchange_four(): h_far_relay = lax.ppermute(cols(a ^ 3), 'aug', over_x)  7.71 us
    dot_general x4, matrix products, project_back(): lax.dot_general(rows, down_weight, (((1,), (1,)), ((), ())), preferred_el...  5.78 us
    ppermute x1, starting transfers between devices, exchange_four(): h_far_relay = lax.ppermute(cols(a ^ 3), 'aug', over_x)  2.94 us
    ppermute x1, waiting for transfers between devices, exchange_four(): g_far = lax.ppermute(grad_rows, 'aug', over_x)  2.56 us
  transfers between devices with their start and end apart: 38, of which 20 were waited for; matrix products, arithmetic and copies ran while one was open for 11% of the time, Pallas kernels for 0%

profile of v16, /device:TPU:0, one launch (start us, length us, event | category | flops | bytes accessed | tf_op | source)
XLA Modules:
  0.0 111.0 jit_solution(17181061794019026686)
XLA Ops:
  0.7 2.2 %dynamic-slice_bitcast_fusion = (bf16[128,1280]{1,0:T(8,128)(2,1)}, bf16[128,1280]{1,0:T(8,128)(2,1)S(1)}, bf16[128,1280]{1,0:T(8,128)(2,1)}) fusion(bf16[1,1,128,5120]{3,2,1,0:T(8,128)(2,1)} %param.6, s32[]{:T(128)S(6)} %select_n.691, s32[]{:T(128)S(6)} %select_n.689, s32[]{:T(128)S(6)} %select_n.690), kind=kLoop, calls=%fused_computation.21 | loop fusion | bytes 1966092 | tf_op jit(solution)/shard_map/dynamic_slice | solution.py:101
  2.9 2.9 %collective-permute-start = (bf16[128,1280]{1,0:T(8,128)(2,1)S(1)}, bf16[128,1280]{1,0:T(8,128)(2,1)S(1)}, u32[]{:S(2)}, u32[]{:S(2)}) collective-permute-start(bf16[128,1280]{1,0:T(8,128)(2,1)S(1)} %get-tuple-element.85), channel_id=1, source_target_pairs={{0,16},{8,24},{16,0},{24,8},{1,17},{9,25},{17,1},{25,9},{2,18},{10... | collective-permute-start | bytes 983048 | tf_op jit(solution)/shard_map/ppermute | solution.py:106
  5.8 7.7 %collective-permute-done = bf16[128,1280]{1,0:T(8,128)(2,1)S(1)} collective-permute-done((bf16[128,1280]{1,0:T(8,128)(2,1)S(1)}, bf16[128,1280]{1,0:T(8,128)(2,1)S(1)}, u32[]{:S(2)}, u32[]{:S(2)}) %collective-permute-start) | collective-permute-done | bytes 327712 | tf_op jit(solution)/shard_map/ppermute | solution.py:106
  13.5 0.7 copy-done.6
  14.3 1.7 %collective-permute-start.1 = (bf16[128,1280]{1,0:T(8,128)(2,1)}, bf16[128,1280]{1,0:T(8,128)(2,1)}, u32[]{:S(2)}, u32[]{:S(2)}) collective-permute-start(bf16[128,1280]{1,0:T(8,128)(2,1)} %get-tuple-element.41), channel_id=1, source_target_pairs={{0,16},{8,24},{16,0},{24,8},{1,17},{9,25},{17,1},{25,9},{2,18},{10... | collective-permute-start | bytes 983048 | tf_op jit(solution)/shard_map/ppermute | solution.py:110
  16.3 8.9 %collective-permute-done.1 = bf16[128,1280]{1,0:T(8,128)(2,1)} collective-permute-done((bf16[128,1280]{1,0:T(8,128)(2,1)}, bf16[128,1280]{1,0:T(8,128)(2,1)}, u32[]{:S(2)}, u32[]{:S(2)}) %collective-permute-start.1) | collective-permute-done | bytes 327712 | tf_op jit(solution)/shard_map/ppermute | solution.py:110
  25.2 0.5 collective-permute-start.2
  25.7 2.1 %fusion.6 = f32[1280,1280]{1,0:T(8,128)S(1)} fusion(bf16[1,1,128,5120]{3,2,1,0:T(8,128)(2,1)} %param.6, s32[]{:T(128)S(6)} %select_n.688, bf16[1,1,128,1280]{3,2,1,0:T(8,128)(2,1)} %param.7), kind=kOutput, calls=%fused_computation.19 | convolution fusion | flops 419430400 | bytes 7208964 | tf_op jit(solution)/shard_map/dot_general | solution.py:154
  27.9 2.6 %collective-permute-done.4 = bf16[128,1280]{1,0:T(8,128)(2,1)} collective-permute-done((bf16[128,1280]{1,0:T(8,128)(2,1)}, bf16[128,1280]{1,0:T(8,128)(2,1)}, u32[]{:S(2)}, u32[]{:S(2)}) %collective-permute-start.4) | collective-permute-done | bytes 327712 | tf_op jit(solution)/shard_map/ppermute | solution.py:105
  30.5 1.0 convolution_add_fusion.2
  31.6 2.1 %convolution_add_fusion.1 = f32[1280,1280]{1,0:T(8,128)S(1)} fusion(f32[1280,1280]{1,0:T(8,128)S(1)} %convolution_add_fusion.2, bf16[128,1280]{1,0:T(8,128)(2,1)} %collective-permute-done.1, bf16[128,1280]{1,0:T(8,128)(2,1)} %collective-permute-done.4), kind=kOutput, calls=%fused_computation.1 | convolution fusion | flops 421068800 | bytes 13762560 | tf_op jit(solution)/shard_map/dot_general | solution.py:154
  33.7 2.5 %multiply_reduce_fusion = (f32[]{:T(128)}, f32[1280,1280]{1,0:T(8,128)S(1)}) fusion(f32[1280,1280]{1,0:T(8,128)S(1)} %convolution_add_fusion.1, bf16[128,1280]{1,0:T(8,128)(2,1)S(1)} %collective-permute-done.5, bf16[128,1280]{1,0:T(8,128)(2,1)S(1)} %collective-permute-done.6), kind=kOutput, calls=%fused_computation.4 | convolution fusion | flops 425984000 | bytes 13762564 | tf_op jit(solution)/shard_map/dot_general | solution.py:154
  36.2 1.4 %collective-permute-start.8 = (f32[1]{0:T(128)}, f32[1]{0:T(128)}, u32[]{:S(2)}, u32[]{:S(2)}) collective-permute-start(f32[1]{0:T(128)} %bitcast.5), channel_id=1, source_target_pairs={{0,16},{8,24},{16,0},{24,8},{1,17},{9,25},{17,1},{25,9},{2,18},{10... | collective-permute-start | bytes 20 | tf_op jit(solution)/shard_map/ppermute | solution.py:126
  37.6 0.4 collective-permute-start.9
  38.1 0.3 collective-permute-start.7
  38.4 1.0 collective-permute-done.7
  42.1 1.6 %collective-permute-start.10 = (f32[40,1280]{1,0:T(8,128)S(1)}, f32[40,1280]{1,0:T(8,128)S(1)}, u32[]{:S(2)}, u32[]{:S(2)}) collective-permute-start(f32[40,1280]{1,0:T(8,128)S(1)} %get-tuple-element.80), channel_id=1, source_target_pairs={{0,1},{1,3},{3,5},{5,7},{7,6},{6,4},{4,2},{2,0},{8,9},{9,11},{11,1... | collective-permute-start | bytes 614408 | tf_op jit(solution)/shard_map/ppermute | solution.py:85
  43.7 0.5 collective-permute-start.17
  44.2 1.5 %collective-permute-start.24 = (f32[40,1280]{1,0:T(8,128)S(1)}, f32[40,1280]{1,0:T(8,128)S(1)}, u32[]{:S(2)}, u32[]{:S(2)}) collective-permute-start(f32[40,1280]{1,0:T(8,128)S(1)} %get-tuple-element.82), channel_id=1, source_target_pairs={{0,1},{1,3},{3,5},{5,7},{7,6},{6,4},{4,2},{2,0},{8,9},{9,11},{11,1... | collective-permute-start | bytes 614408 | tf_op jit(solution)/shard_map/ppermute | solution.py:85
  45.8 0.5 collective-permute-start.31
  46.5 1.2 %fusion.4 = bf16[512,1280]{1,0:T(8,128)(2,1)S(1)} fusion(bf16[512,1280]{1,0:T(8,128)(2,1)S(1)} %broadcast_in_dim.2, s32[]{:T(128)S(6)} %select_n.859, bf16[128,1280]{1,0:T(8,128)(2,1)S(1)} %bitcast.116, bf16[1280,1280]{1,0:T(8,128)(2,1)S(1)} %copy-done), kind=kOutput, calls=%fused_computation.12 | convolution fusion | flops 419594240 | bytes 3932164 | tf_op jit(solution)/shard_map/dot_general | solution.py:17
  47.7 2.4 %collective-permute-done.10 = f32[40,1280]{1,0:T(8,128)S(1)} collective-permute-done((f32[40,1280]{1,0:T(8,128)S(1)}, f32[40,1280]{1,0:T(8,128)S(1)}, u32[]{:S(2)}, u32[]{:S(2)}) %collective-permute-start.10) | collective-permute-done | bytes 204832 | tf_op jit(solution)/shard_map/ppermute | solution.py:85
  50.1 1.6 %collective-permute-start.11 = (f32[40,1280]{1,0:T(8,128)S(1)}, f32[40,1280]{1,0:T(8,128)S(1)}, u32[]{:S(2)}, u32[]{:S(2)}) collective-permute-start(f32[40,1280]{1,0:T(8,128)S(1)} %add.518), channel_id=1, source_target_pairs={{0,1},{1,3},{3,5},{5,7},{7,6},{6,4},{4,2},{2,0},{8,9},{9,11},{11,1... | collective-permute-start | bytes 614408 | tf_op jit(solution)/shard_map/ppermute | solution.py:85
  51.7 0.6 collective-permute-start.18
  52.3 2.2 %collective-permute-done.24 = f32[40,1280]{1,0:T(8,128)S(1)} collective-permute-done((f32[40,1280]{1,0:T(8,128)S(1)}, f32[40,1280]{1,0:T(8,128)S(1)}, u32[]{:S(2)}, u32[]{:S(2)}) %collective-permute-start.24) | collective-permute-done | bytes 204832 | tf_op jit(solution)/shard_map/ppermute | solution.py:85
  54.5 1.6 %collective-permute-start.25 = (f32[40,1280]{1,0:T(8,128)S(1)}, f32[40,1280]{1,0:T(8,128)S(1)}, u32[]{:S(2)}, u32[]{:S(2)}) collective-permute-start(f32[40,1280]{1,0:T(8,128)S(1)} %add.580), channel_id=1, source_target_pairs={{0,1},{1,3},{3,5},{5,7},{7,6},{6,4},{4,2},{2,0},{8,9},{9,11},{11,1... | collective-permute-start | bytes 614408 | tf_op jit(solution)/shard_map/ppermute | solution.py:85
  56.1 0.6 collective-permute-start.32
  56.8 1.2 %fusion.3 = bf16[512,1280]{1,0:T(8,128)(2,1)S(1)} fusion(bf16[512,1280]{1,0:T(8,128)(2,1)S(1)} %fusion.4, s32[]{:T(128)S(6)} %select_n.860, bf16[128,1280]{1,0:T(8,128)(2,1)S(1)} %collective-permute-done.3, bf16[1280,1280]{1,0:T(8,128)(2,1)S(1)} %copy-done), kind=kOutput, calls=%fused_computation.10 | convolution fusion | flops 419594240 | bytes 3932164 | tf_op jit(solution)/shard_map/dot_general | solution.py:17
  58.0 0.9 collective-permute-done.11
  58.9 1.6 %collective-permute-start.12 = (f32[40,1280]{1,0:T(8,128)S(1)}, f32[40,1280]{1,0:T(8,128)S(1)}, u32[]{:S(2)}, u32[]{:S(2)}) collective-permute-start(f32[40,1280]{1,0:T(8,128)S(1)} %add.521), channel_id=1, source_target_pairs={{0,1},{1,3},{3,5},{5,7},{7,6},{6,4},{4,2},{2,0},{8,9},{9,11},{11,1... | collective-permute-start | bytes 614408 | tf_op jit(solution)/shard_map/ppermute | solution.py:85
  60.5 0.6 collective-permute-start.19
  61.1 2.2 %collective-permute-done.25 = f32[40,1280]{1,0:T(8,128)S(1)} collective-permute-done((f32[40,1280]{1,0:T(8,128)S(1)}, f32[40,1280]{1,0:T(8,128)S(1)}, u32[]{:S(2)}, u32[]{:S(2)}) %collective-permute-start.25) | collective-permute-done | bytes 204832 | tf_op jit(solution)/shard_map/ppermute | solution.py:85
  63.3 1.6 %collective-permute-start.26 = (f32[40,1280]{1,0:T(8,128)S(1)}, f32[40,1280]{1,0:T(8,128)S(1)}, u32[]{:S(2)}, u32[]{:S(2)}) collective-permute-start(f32[40,1280]{1,0:T(8,128)S(1)} %add.583), channel_id=1, source_target_pairs={{0,1},{1,3},{3,5},{5,7},{7,6},{6,4},{4,2},{2,0},{8,9},{9,11},{11,1... | collective-permute-start | bytes 614408 | tf_op jit(solution)/shard_map/ppermute | solution.py:85
  64.9 0.6 collective-permute-start.33
  65.6 2.2 %fusion.2 = bf16[512,1280]{1,0:T(8,128)(2,1)S(1)} fusion(bf16[512,1280]{1,0:T(8,128)(2,1)S(1)} %fusion.3, s32[]{:T(128)S(6)} %select_n.861, bf16[128,1280]{1,0:T(8,128)(2,1)} %collective-permute-done.4, bf16[1280,1280]{1,0:T(8,128)(2,1)S(1)} %copy-done), kind=kOutput, calls=%fused_computation.8 | convolution fusion | flops 419594240 | bytes 3932164 | tf_op jit(solution)/shard_map/dot_general | solution.py:17
  67.8 1.6 %collective-permute-start.13 = (f32[40,1280]{1,0:T(8,128)S(1)}, f32[40,1280]{1,0:T(8,128)S(1)}, u32[]{:S(2)}, u32[]{:S(2)}) collective-permute-start(f32[40,1280]{1,0:T(8,128)S(1)} %add.524), channel_id=1, source_target_pairs={{0,1},{1,3},{3,5},{5,7},{7,6},{6,4},{4,2},{2,0},{8,9},{9,11},{11,1... | collective-permute-start | bytes 614408 | tf_op jit(solution)/shard_map/ppermute | solution.py:85
  69.4 0.6 collective-permute-start.20
  70.0 2.1 %collective-permute-done.26 = f32[40,1280]{1,0:T(8,128)S(1)} collective-permute-done((f32[40,1280]{1,0:T(8,128)S(1)}, f32[40,1280]{1,0:T(8,128)S(1)}, u32[]{:S(2)}, u32[]{:S(2)}) %collective-permute-start.26) | collective-permute-done | bytes 204832 | tf_op jit(solution)/shard_map/ppermute | solution.py:85
  72.1 1.6 %collective-permute-start.27 = (f32[40,1280]{1,0:T(8,128)S(1)}, f32[40,1280]{1,0:T(8,128)S(1)}, u32[]{:S(2)}, u32[]{:S(2)}) collective-permute-start(f32[40,1280]{1,0:T(8,128)S(1)} %add.586), channel_id=1, source_target_pairs={{0,1},{1,3},{3,5},{5,7},{7,6},{6,4},{4,2},{2,0},{8,9},{9,11},{11,1... | collective-permute-start | bytes 614408 | tf_op jit(solution)/shard_map/ppermute | solution.py:85
  73.7 0.6 collective-permute-start.34
  74.4 1.2 %fusion.1 = bf16[512,1280]{1,0:T(8,128)(2,1)S(1)} fusion(bf16[512,1280]{1,0:T(8,128)(2,1)S(1)} %fusion.2, s32[]{:T(128)S(6)} %select_n.862, bf16[128,1280]{1,0:T(8,128)(2,1)S(1)} %collective-permute-done.6, bf16[1280,1280]{1,0:T(8,128)(2,1)S(1)} %copy-done), kind=kOutput, calls=%fused_computation.6 | convolution fusion | flops 419594240 | bytes 3932164 | tf_op jit(solution)/shard_map/dot_general | solution.py:17
  75.6 0.9 collective-permute-done.13
  76.5 1.6 %collective-permute-start.14 = (f32[40,1280]{1,0:T(8,128)S(1)}, f32[40,1280]{1,0:T(8,128)S(1)}, u32[]{:S(2)}, u32[]{:S(2)}) collective-permute-start(f32[40,1280]{1,0:T(8,128)S(1)} %add.527), channel_id=1, source_target_pairs={{0,1},{1,3},{3,5},{5,7},{7,6},{6,4},{4,2},{2,0},{8,9},{9,11},{11,1... | collective-permute-start | bytes 614408 | tf_op jit(solution)/shard_map/ppermute | solution.py:85
  78.1 0.6 collective-permute-start.21
  78.6 2.2 %collective-permute-done.27 = f32[40,1280]{1,0:T(8,128)S(1)} collective-permute-done((f32[40,1280]{1,0:T(8,128)S(1)}, f32[40,1280]{1,0:T(8,128)S(1)}, u32[]{:S(2)}, u32[]{:S(2)}) %collective-permute-start.27) | collective-permute-done | bytes 204832 | tf_op jit(solution)/shard_map/ppermute | solution.py:85
  80.9 1.6 %collective-permute-start.28 = (f32[40,1280]{1,0:T(8,128)S(1)}, f32[40,1280]{1,0:T(8,128)S(1)}, u32[]{:S(2)}, u32[]{:S(2)}) collective-permute-start(f32[40,1280]{1,0:T(8,128)S(1)} %add.589), channel_id=1, source_target_pairs={{0,1},{1,3},{3,5},{5,7},{7,6},{6,4},{4,2},{2,0},{8,9},{9,11},{11,1... | collective-permute-start | bytes 614408 | tf_op jit(solution)/shard_map/ppermute | solution.py:85
  82.5 0.6 collective-permute-start.35
  83.2 2.0 %collective-permute-done.14 = f32[40,1280]{1,0:T(8,128)S(1)} collective-permute-done((f32[40,1280]{1,0:T(8,128)S(1)}, f32[40,1280]{1,0:T(8,128)S(1)}, u32[]{:S(2)}, u32[]{:S(2)}) %collective-permute-start.14) | collective-permute-done | bytes 204832 | tf_op jit(solution)/shard_map/ppermute | solution.py:85
  85.2 1.6 %collective-permute-start.15 = (f32[40,1280]{1,0:T(8,128)S(1)}, f32[40,1280]{1,0:T(8,128)S(1)}, u32[]{:S(2)}, u32[]{:S(2)}) collective-permute-start(f32[40,1280]{1,0:T(8,128)S(1)} %add.530), channel_id=1, source_target_pairs={{0,1},{1,3},{3,5},{5,7},{7,6},{6,4},{4,2},{2,0},{8,9},{9,11},{11,1... | collective-permute-start | bytes 614408 | tf_op jit(solution)/shard_map/ppermute | solution.py:85
  86.8 0.6 collective-permute-start.22
  87.4 2.2 %collective-permute-done.28 = f32[40,1280]{1,0:T(8,128)S(1)} collective-permute-done((f32[40,1280]{1,0:T(8,128)S(1)}, f32[40,1280]{1,0:T(8,128)S(1)}, u32[]{:S(2)}, u32[]{:S(2)}) %collective-permute-start.28) | collective-permute-done | bytes 204832 | tf_op jit(solution)/shard_map/ppermute | solution.py:85
  89.6 1.6 %collective-permute-start.29 = (f32[40,1280]{1,0:T(8,128)S(1)}, f32[40,1280]{1,0:T(8,128)S(1)}, u32[]{:S(2)}, u32[]{:S(2)}) collective-permute-start(f32[40,1280]{1,0:T(8,128)S(1)} %add.592), channel_id=1, source_target_pairs={{0,1},{1,3},{3,5},{5,7},{7,6},{6,4},{4,2},{2,0},{8,9},{9,11},{11,1... | collective-permute-start | bytes 614408 | tf_op jit(solution)/shard_map/ppermute | solution.py:85
  91.2 0.6 collective-permute-start.36
  91.9 2.1 %collective-permute-done.15 = f32[40,1280]{1,0:T(8,128)S(1)} collective-permute-done((f32[40,1280]{1,0:T(8,128)S(1)}, f32[40,1280]{1,0:T(8,128)S(1)}, u32[]{:S(2)}, u32[]{:S(2)}) %collective-permute-start.15) | collective-permute-done | bytes 204832 | tf_op jit(solution)/shard_map/ppermute | solution.py:85
  94.0 1.6 %collective-permute-start.16 = (f32[40,1280]{1,0:T(8,128)S(1)}, f32[40,1280]{1,0:T(8,128)S(1)}, u32[]{:S(2)}, u32[]{:S(2)}) collective-permute-start(f32[40,1280]{1,0:T(8,128)S(1)} %add.533), channel_id=1, source_target_pairs={{0,1},{1,3},{3,5},{5,7},{7,6},{6,4},{4,2},{2,0},{8,9},{9,11},{11,1... | collective-permute-start | bytes 614408 | tf_op jit(solution)/shard_map/ppermute | solution.py:85
  95.6 0.6 collective-permute-start.23
  96.2 2.2 %collective-permute-done.29 = f32[40,1280]{1,0:T(8,128)S(1)} collective-permute-done((f32[40,1280]{1,0:T(8,128)S(1)}, f32[40,1280]{1,0:T(8,128)S(1)}, u32[]{:S(2)}, u32[]{:S(2)}) %collective-permute-start.29) | collective-permute-done | bytes 204832 | tf_op jit(solution)/shard_map/ppermute | solution.py:85
  98.4 1.6 %collective-permute-start.30 = (f32[40,1280]{1,0:T(8,128)S(1)}, f32[40,1280]{1,0:T(8,128)S(1)}, u32[]{:S(2)}, u32[]{:S(2)}) collective-permute-start(f32[40,1280]{1,0:T(8,128)S(1)} %add.595), channel_id=1, source_target_pairs={{0,1},{1,3},{3,5},{5,7},{7,6},{6,4},{4,2},{2,0},{8,9},{9,11},{11,1... | collective-permute-start | bytes 614408 | tf_op jit(solution)/shard_map/ppermute | solution.py:85
  100.0 0.6 collective-permute-start.37
  100.7 2.1 %collective-permute-done.16 = f32[40,1280]{1,0:T(8,128)S(1)} collective-permute-done((f32[40,1280]{1,0:T(8,128)S(1)}, f32[40,1280]{1,0:T(8,128)S(1)}, u32[]{:S(2)}, u32[]{:S(2)}) %collective-permute-start.16) | collective-permute-done | bytes 204832 | tf_op jit(solution)/shard_map/ppermute | solution.py:85
  102.8 1.5 %collective-permute-done.23 = f32[40,1280]{1,0:T(8,128)S(1)} collective-permute-done((f32[40,1280]{1,0:T(8,128)S(1)}, f32[40,1280]{1,0:T(8,128)S(1)}, u32[]{:S(2)}, u32[]{:S(2)}) %collective-permute-start.23) | collective-permute-done | bytes 204832 | tf_op jit(solution)/shard_map/ppermute | solution.py:85
  104.4 2.2 %collective-permute-done.30 = f32[40,1280]{1,0:T(8,128)S(1)} collective-permute-done((f32[40,1280]{1,0:T(8,128)S(1)}, f32[40,1280]{1,0:T(8,128)S(1)}, u32[]{:S(2)}, u32[]{:S(2)}) %collective-permute-start.30) | collective-permute-done | bytes 204832 | tf_op jit(solution)/shard_map/ppermute | solution.py:85
  106.6 1.2 %collective-permute-done.37 = f32[40,1280]{1,0:T(8,128)S(1)} collective-permute-done((f32[40,1280]{1,0:T(8,128)S(1)}, f32[40,1280]{1,0:T(8,128)S(1)}, u32[]{:S(2)}, u32[]{:S(2)}) %collective-permute-start.37) | collective-permute-done | bytes 204832 | tf_op jit(solution)/shard_map/ppermute | solution.py:85
  107.9 2.0 %add_divide_fusion = (f32[160,1280]{1,0:T(8,128)}, f32[160,1280]{1,0:T(8,128)}, f32[160,1280]{1,0:T(8,128)}, f32[160,1280]{1,0:T(8,128)}) fusion(f32[160,1280]{1,0:T(8,128)S(1)} %copy-done.3, f32[160,1280]{1,0:T(8,128)S(1)} %copy-done.4, f32[160,1280]{1,0:T(8,128)S(1)} %copy-done.5, f32[40,1280]{1,0:T(8,128)S(1)} %add.621, f32[40,1280]{1,0:T(8,128)S(1)} %add.598, ...), kind=kLoop, calls=%fused_computation.16 | loop fusion | flops 3481600 | bytes 6553600 | tf_op jit(solution)/shard_map/div | solution.py:205
  (96 shorter events, 2.1 us)
Async XLA Ops:
  0.6 45.8 %copy-start = (bf16[1280,1280]{1,0:T(8,128)(2,1)S(1)}, bf16[1280,1280]{1,0:T(8,128)(2,1)}, u32[]{:S(2)}) copy-start(bf16[1280,1280]{1,0:T(8,128)(2,1)} %param.8) | copy-start | bytes 9830404
  2.9 10.6 %collective-permute-start = (bf16[128,1280]{1,0:T(8,128)(2,1)S(1)}, bf16[128,1280]{1,0:T(8,128)(2,1)S(1)}, u32[]{:S(2)}, u32[]{:S(2)}) collective-permute-start(bf16[128,1280]{1,0:T(8,128)(2,1)S(1)} %get-tuple-element.85), channel_id=1, source_target_pairs={{0,16},{8,24},{16,0},{24,8},{1,17},{9,25},{17,1},{25,9},{2,18},{10... | collective-permute-start | bytes 983048 | tf_op jit(solution)/shard_map/ppermute | solution.py:106
  13.5 0.7 copy-start.6
  14.3 11.0 %collective-permute-start.1 = (bf16[128,1280]{1,0:T(8,128)(2,1)}, bf16[128,1280]{1,0:T(8,128)(2,1)}, u32[]{:S(2)}, u32[]{:S(2)}) collective-permute-start(bf16[128,1280]{1,0:T(8,128)(2,1)} %get-tuple-element.41), channel_id=1, source_target_pairs={{0,16},{8,24},{16,0},{24,8},{1,17},{9,25},{17,1},{25,9},{2,18},{10... | collective-permute-start | bytes 983048 | tf_op jit(solution)/shard_map/ppermute | solution.py:110
  16.0 14.5 %collective-permute-start.4 = (bf16[128,1280]{1,0:T(8,128)(2,1)}, bf16[128,1280]{1,0:T(8,128)(2,1)}, u32[]{:S(2)}, u32[]{:S(2)}) collective-permute-start(bf16[128,1280]{1,0:T(8,128)(2,1)} %bitcast.114), channel_id=1, source_target_pairs={{0,16},{8,24},{16,0},{24,8},{1,17},{9,25},{17,1},{25,9},{2,18},{10... | collective-permute-start | bytes 983048 | tf_op jit(solution)/shard_map/ppermute | solution.py:105
  16.3 11.6 %copy-start.7 = (bf16[128,1280]{1,0:T(8,128)(2,1)S(1)}, bf16[128,1280]{1,0:T(8,128)(2,1)}, u32[]{:S(2)}) copy-start(bf16[128,1280]{1,0:T(8,128)(2,1)} %copy-done.6) | copy-start | bytes 983044
  25.2 5.3 %collective-permute-start.3 = (bf16[128,1280]{1,0:T(8,128)(2,1)}, bf16[128,1280]{1,0:T(8,128)(2,1)S(1)}, u32[]{:S(2)}, u32[]{:S(2)}) collective-permute-start(bf16[128,1280]{1,0:T(8,128)(2,1)} %bitcast.115), channel_id=1, source_target_pairs={{0,8},{8,0},{16,24},{24,16},{1,9},{9,1},{17,25},{25,17},{2,10},{10... | collective-permute-start | bytes 983048 | tf_op jit(solution)/shard_map/ppermute | solution.py:112
  25.2 5.3 %collective-permute-start.2 = (bf16[128,1280]{1,0:T(8,128)(2,1)}, bf16[128,1280]{1,0:T(8,128)(2,1)S(1)}, u32[]{:S(2)}, u32[]{:S(2)}) collective-permute-start(bf16[128,1280]{1,0:T(8,128)(2,1)} %get-tuple-element.42), channel_id=1, source_target_pairs={{0,8},{8,0},{16,24},{24,16},{1,9},{9,1},{17,25},{25,17},{2,10},{10... | collective-permute-start | bytes 983048 | tf_op jit(solution)/shard_map/ppermute | solution.py:113
  27.9 5.8 %collective-permute-start.5 = (bf16[128,1280]{1,0:T(8,128)(2,1)S(1)}, bf16[128,1280]{1,0:T(8,128)(2,1)S(1)}, u32[]{:S(2)}, u32[]{:S(2)}) collective-permute-start(bf16[128,1280]{1,0:T(8,128)(2,1)S(1)} %copy-done.7), channel_id=1, source_target_pairs={{0,8},{8,0},{16,24},{24,16},{1,9},{9,1},{17,25},{25,17},{2,10},{10... | collective-permute-start | bytes 983048 | tf_op jit(solution)/shard_map/ppermute | solution.py:108
  30.5 3.2 %collective-permute-start.6 = (bf16[128,1280]{1,0:T(8,128)(2,1)}, bf16[128,1280]{1,0:T(8,128)(2,1)S(1)}, u32[]{:S(2)}, u32[]{:S(2)}) collective-permute-start(bf16[128,1280]{1,0:T(8,128)(2,1)} %collective-permute-done.4), channel_id=1, source_target_pairs={{0,8},{8,0},{16,24},{24,16},{1,9},{9,1},{17,25},{25,17},{2,10},{10... | collective-permute-start | bytes 983048 | tf_op jit(solution)/shard_map/ppermute | solution.py:107
  33.7 12.8 %copy-start.1 = (bf16[1,1,128,1280]{3,2,1,0:T(8,128)(2,1)S(1)}, bf16[1,1,128,1280]{3,2,1,0:T(8,128)(2,1)}, u32[]{:S(2)}) copy-start(bf16[1,1,128,1280]{3,2,1,0:T(8,128)(2,1)} %param.7) | copy-start | bytes 983044
  36.2 4.4 %collective-permute-start.8 = (f32[1]{0:T(128)}, f32[1]{0:T(128)}, u32[]{:S(2)}, u32[]{:S(2)}) collective-permute-start(f32[1]{0:T(128)} %bitcast.5), channel_id=1, source_target_pairs={{0,16},{8,24},{16,0},{24,8},{1,17},{9,25},{17,1},{25,9},{2,18},{10... | collective-permute-start | bytes 20 | tf_op jit(solution)/shard_map/ppermute | solution.py:126
  37.6 3.1 %collective-permute-start.9 = (f32[1]{0:T(128)}, f32[1]{0:T(128)}, u32[]{:S(2)}, u32[]{:S(2)}) collective-permute-start(f32[1]{0:T(128)} %bitcast.5), channel_id=1, source_target_pairs={{0,24},{8,16},{16,8},{24,0},{1,25},{9,17},{17,9},{25,1},{2,26},{10... | collective-permute-start | bytes 20 | tf_op jit(solution)/shard_map/ppermute | solution.py:126
  38.1 1.2 %collective-permute-start.7 = (f32[1]{0:T(128)}, f32[1]{0:T(128)}, u32[]{:S(2)}, u32[]{:S(2)}) collective-permute-start(f32[1]{0:T(128)} %bitcast.5), channel_id=1, source_target_pairs={{0,8},{8,0},{16,24},{24,16},{1,9},{9,1},{17,25},{25,17},{2,10},{10... | collective-permute-start | bytes 20 | tf_op jit(solution)/shard_map/ppermute | solution.py:126
  42.1 8.0 %collective-permute-start.10 = (f32[40,1280]{1,0:T(8,128)S(1)}, f32[40,1280]{1,0:T(8,128)S(1)}, u32[]{:S(2)}, u32[]{:S(2)}) collective-permute-start(f32[40,1280]{1,0:T(8,128)S(1)} %get-tuple-element.80), channel_id=1, source_target_pairs={{0,1},{1,3},{3,5},{5,7},{7,6},{6,4},{4,2},{2,0},{8,9},{9,11},{11,1... | collective-permute-start | bytes 614408 | tf_op jit(solution)/shard_map/ppermute | solution.py:85
  43.7 8.0 %collective-permute-start.17 = (f32[40,1280]{1,0:T(8,128)S(1)}, f32[40,1280]{1,0:T(8,128)S(1)}, u32[]{:S(2)}, u32[]{:S(2)}) collective-permute-start(f32[40,1280]{1,0:T(8,128)S(1)} %get-tuple-element.83), channel_id=1, source_target_pairs={{0,2},{1,0},{3,1},{5,3},{7,5},{6,7},{4,6},{2,4},{8,10},{9,8},{11,9... | collective-permute-start | bytes 614408 | tf_op jit(solution)/shard_map/ppermute | solution.py:85
  44.2 10.3 %collective-permute-start.24 = (f32[40,1280]{1,0:T(8,128)S(1)}, f32[40,1280]{1,0:T(8,128)S(1)}, u32[]{:S(2)}, u32[]{:S(2)}) collective-permute-start(f32[40,1280]{1,0:T(8,128)S(1)} %get-tuple-element.82), channel_id=1, source_target_pairs={{0,1},{1,3},{3,5},{5,7},{7,6},{6,4},{4,2},{2,0},{8,9},{9,11},{11,1... | collective-permute-start | bytes 614408 | tf_op jit(solution)/shard_map/ppermute | solution.py:85
  45.8 10.3 %collective-permute-start.31 = (f32[40,1280]{1,0:T(8,128)S(1)}, f32[40,1280]{1,0:T(8,128)S(1)}, u32[]{:S(2)}, u32[]{:S(2)}) collective-permute-start(f32[40,1280]{1,0:T(8,128)S(1)} %get-tuple-element.81), channel_id=1, source_target_pairs={{0,2},{1,0},{3,1},{5,3},{7,5},{6,7},{4,6},{2,4},{8,10},{9,8},{11,9... | collective-permute-start | bytes 614408 | tf_op jit(solution)/shard_map/ppermute | solution.py:85
  50.1 8.8 %collective-permute-start.11 = (f32[40,1280]{1,0:T(8,128)S(1)}, f32[40,1280]{1,0:T(8,128)S(1)}, u32[]{:S(2)}, u32[]{:S(2)}) collective-permute-start(f32[40,1280]{1,0:T(8,128)S(1)} %add.518), channel_id=1, source_target_pairs={{0,1},{1,3},{3,5},{5,7},{7,6},{6,4},{4,2},{2,0},{8,9},{9,11},{11,1... | collective-permute-start | bytes 614408 | tf_op jit(solution)/shard_map/ppermute | solution.py:85
  51.7 8.8 %collective-permute-start.18 = (f32[40,1280]{1,0:T(8,128)S(1)}, f32[40,1280]{1,0:T(8,128)S(1)}, u32[]{:S(2)}, u32[]{:S(2)}) collective-permute-start(f32[40,1280]{1,0:T(8,128)S(1)} %add.545), channel_id=1, source_target_pairs={{0,2},{1,0},{3,1},{5,3},{7,5},{6,7},{4,6},{2,4},{8,10},{9,8},{11,9... | collective-permute-start | bytes 614408 | tf_op jit(solution)/shard_map/ppermute | solution.py:85
  54.5 8.8 %collective-permute-start.25 = (f32[40,1280]{1,0:T(8,128)S(1)}, f32[40,1280]{1,0:T(8,128)S(1)}, u32[]{:S(2)}, u32[]{:S(2)}) collective-permute-start(f32[40,1280]{1,0:T(8,128)S(1)} %add.580), channel_id=1, source_target_pairs={{0,1},{1,3},{3,5},{5,7},{7,6},{6,4},{4,2},{2,0},{8,9},{9,11},{11,1... | collective-permute-start | bytes 614408 | tf_op jit(solution)/shard_map/ppermute | solution.py:85
  56.1 8.7 %collective-permute-start.32 = (f32[40,1280]{1,0:T(8,128)S(1)}, f32[40,1280]{1,0:T(8,128)S(1)}, u32[]{:S(2)}, u32[]{:S(2)}) collective-permute-start(f32[40,1280]{1,0:T(8,128)S(1)} %add.603), channel_id=1, source_target_pairs={{0,2},{1,0},{3,1},{5,3},{7,5},{6,7},{4,6},{2,4},{8,10},{9,8},{11,9... | collective-permute-start | bytes 614408 | tf_op jit(solution)/shard_map/ppermute | solution.py:85
  58.9 8.9 %collective-permute-start.12 = (f32[40,1280]{1,0:T(8,128)S(1)}, f32[40,1280]{1,0:T(8,128)S(1)}, u32[]{:S(2)}, u32[]{:S(2)}) collective-permute-start(f32[40,1280]{1,0:T(8,128)S(1)} %add.521), channel_id=1, source_target_pairs={{0,1},{1,3},{3,5},{5,7},{7,6},{6,4},{4,2},{2,0},{8,9},{9,11},{11,1... | collective-permute-start | bytes 614408 | tf_op jit(solution)/shard_map/ppermute | solution.py:85
  60.5 8.9 %collective-permute-start.19 = (f32[40,1280]{1,0:T(8,128)S(1)}, f32[40,1280]{1,0:T(8,128)S(1)}, u32[]{:S(2)}, u32[]{:S(2)}) collective-permute-start(f32[40,1280]{1,0:T(8,128)S(1)} %add.550), channel_id=1, source_target_pairs={{0,2},{1,0},{3,1},{5,3},{7,5},{6,7},{4,6},{2,4},{8,10},{9,8},{11,9... | collective-permute-start | bytes 614408 | tf_op jit(solution)/shard_map/ppermute | solution.py:85
  63.3 8.8 %collective-permute-start.26 = (f32[40,1280]{1,0:T(8,128)S(1)}, f32[40,1280]{1,0:T(8,128)S(1)}, u32[]{:S(2)}, u32[]{:S(2)}) collective-permute-start(f32[40,1280]{1,0:T(8,128)S(1)} %add.583), channel_id=1, source_target_pairs={{0,1},{1,3},{3,5},{5,7},{7,6},{6,4},{4,2},{2,0},{8,9},{9,11},{11,1... | collective-permute-start | bytes 614408 | tf_op jit(solution)/shard_map/ppermute | solution.py:85
  64.9 8.8 %collective-permute-start.33 = (f32[40,1280]{1,0:T(8,128)S(1)}, f32[40,1280]{1,0:T(8,128)S(1)}, u32[]{:S(2)}, u32[]{:S(2)}) collective-permute-start(f32[40,1280]{1,0:T(8,128)S(1)} %add.606), channel_id=1, source_target_pairs={{0,2},{1,0},{3,1},{5,3},{7,5},{6,7},{4,6},{2,4},{8,10},{9,8},{11,9... | collective-permute-start | bytes 614408 | tf_op jit(solution)/shard_map/ppermute | solution.py:85
  67.8 8.6 %collective-permute-start.13 = (f32[40,1280]{1,0:T(8,128)S(1)}, f32[40,1280]{1,0:T(8,128)S(1)}, u32[]{:S(2)}, u32[]{:S(2)}) collective-permute-start(f32[40,1280]{1,0:T(8,128)S(1)} %add.524), channel_id=1, source_target_pairs={{0,1},{1,3},{3,5},{5,7},{7,6},{6,4},{4,2},{2,0},{8,9},{9,11},{11,1... | collective-permute-start | bytes 614408 | tf_op jit(solution)/shard_map/ppermute | solution.py:85
  69.4 8.6 %collective-permute-start.20 = (f32[40,1280]{1,0:T(8,128)S(1)}, f32[40,1280]{1,0:T(8,128)S(1)}, u32[]{:S(2)}, u32[]{:S(2)}) collective-permute-start(f32[40,1280]{1,0:T(8,128)S(1)} %add.555), channel_id=1, source_target_pairs={{0,2},{1,0},{3,1},{5,3},{7,5},{6,7},{4,6},{2,4},{8,10},{9,8},{11,9... | collective-permute-start | bytes 614408 | tf_op jit(solution)/shard_map/ppermute | solution.py:85
  72.1 8.7 %collective-permute-start.27 = (f32[40,1280]{1,0:T(8,128)S(1)}, f32[40,1280]{1,0:T(8,128)S(1)}, u32[]{:S(2)}, u32[]{:S(2)}) collective-permute-start(f32[40,1280]{1,0:T(8,128)S(1)} %add.586), channel_id=1, source_target_pairs={{0,1},{1,3},{3,5},{5,7},{7,6},{6,4},{4,2},{2,0},{8,9},{9,11},{11,1... | collective-permute-start | bytes 614408 | tf_op jit(solution)/shard_map/ppermute | solution.py:85
  73.7 8.8 %collective-permute-start.34 = (f32[40,1280]{1,0:T(8,128)S(1)}, f32[40,1280]{1,0:T(8,128)S(1)}, u32[]{:S(2)}, u32[]{:S(2)}) collective-permute-start(f32[40,1280]{1,0:T(8,128)S(1)} %add.609), channel_id=1, source_target_pairs={{0,2},{1,0},{3,1},{5,3},{7,5},{6,7},{4,6},{2,4},{8,10},{9,8},{11,9... | collective-permute-start | bytes 614408 | tf_op jit(solution)/shard_map/ppermute | solution.py:85
  75.6 28.8 %copy-start.2 = (bf16[512,1280]{1,0:T(8,128)(2,1)}, bf16[512,1280]{1,0:T(8,128)(2,1)S(1)}, u32[]{:S(2)}) copy-start(bf16[512,1280]{1,0:T(8,128)(2,1)S(1)} %fusion.1) | copy-start | bytes 3932164
  76.5 8.7 %collective-permute-start.14 = (f32[40,1280]{1,0:T(8,128)S(1)}, f32[40,1280]{1,0:T(8,128)S(1)}, u32[]{:S(2)}, u32[]{:S(2)}) collective-permute-start(f32[40,1280]{1,0:T(8,128)S(1)} %add.527), channel_id=1, source_target_pairs={{0,1},{1,3},{3,5},{5,7},{7,6},{6,4},{4,2},{2,0},{8,9},{9,11},{11,1... | collective-permute-start | bytes 614408 | tf_op jit(solution)/shard_map/ppermute | solution.py:85
  78.1 8.7 %collective-permute-start.21 = (f32[40,1280]{1,0:T(8,128)S(1)}, f32[40,1280]{1,0:T(8,128)S(1)}, u32[]{:S(2)}, u32[]{:S(2)}) collective-permute-start(f32[40,1280]{1,0:T(8,128)S(1)} %add.560), channel_id=1, source_target_pairs={{0,2},{1,0},{3,1},{5,3},{7,5},{6,7},{4,6},{2,4},{8,10},{9,8},{11,9... | collective-permute-start | bytes 614408 | tf_op jit(solution)/shard_map/ppermute | solution.py:85
  80.9 27.0 %copy-start.3 = (f32[160,1280]{1,0:T(8,128)S(1)}, f32[160,1280]{1,0:T(8,128)}, u32[]{:S(2)}) copy-start(f32[160,1280]{1,0:T(8,128)} %param.11) | copy-start | bytes 2457604
  80.9 27.0 %copy-start.4 = (f32[160,1280]{1,0:T(8,128)S(1)}, f32[160,1280]{1,0:T(8,128)}, u32[]{:S(2)}) copy-start(f32[160,1280]{1,0:T(8,128)} %param.10) | copy-start | bytes 2457604
  80.9 27.0 %copy-start.5 = (f32[160,1280]{1,0:T(8,128)S(1)}, f32[160,1280]{1,0:T(8,128)}, u32[]{:S(2)}) copy-start(f32[160,1280]{1,0:T(8,128)} %param.9) | copy-start | bytes 2457604
  80.9 8.7 %collective-permute-start.28 = (f32[40,1280]{1,0:T(8,128)S(1)}, f32[40,1280]{1,0:T(8,128)S(1)}, u32[]{:S(2)}, u32[]{:S(2)}) collective-permute-start(f32[40,1280]{1,0:T(8,128)S(1)} %add.589), channel_id=1, source_target_pairs={{0,1},{1,3},{3,5},{5,7},{7,6},{6,4},{4,2},{2,0},{8,9},{9,11},{11,1... | collective-permute-start | bytes 614408 | tf_op jit(solution)/shard_map/ppermute | solution.py:85
  82.5 8.7 %collective-permute-start.35 = (f32[40,1280]{1,0:T(8,128)S(1)}, f32[40,1280]{1,0:T(8,128)S(1)}, u32[]{:S(2)}, u32[]{:S(2)}) collective-permute-start(f32[40,1280]{1,0:T(8,128)S(1)} %add.612), channel_id=1, source_target_pairs={{0,2},{1,0},{3,1},{5,3},{7,5},{6,7},{4,6},{2,4},{8,10},{9,8},{11,9... | collective-permute-start | bytes 614408 | tf_op jit(solution)/shard_map/ppermute | solution.py:85
  85.2 8.8 %collective-permute-start.15 = (f32[40,1280]{1,0:T(8,128)S(1)}, f32[40,1280]{1,0:T(8,128)S(1)}, u32[]{:S(2)}, u32[]{:S(2)}) collective-permute-start(f32[40,1280]{1,0:T(8,128)S(1)} %add.530), channel_id=1, source_target_pairs={{0,1},{1,3},{3,5},{5,7},{7,6},{6,4},{4,2},{2,0},{8,9},{9,11},{11,1... | collective-permute-start | bytes 614408 | tf_op jit(solution)/shard_map/ppermute | solution.py:85
  86.8 8.8 %collective-permute-start.22 = (f32[40,1280]{1,0:T(8,128)S(1)}, f32[40,1280]{1,0:T(8,128)S(1)}, u32[]{:S(2)}, u32[]{:S(2)}) collective-permute-start(f32[40,1280]{1,0:T(8,128)S(1)} %add.565), channel_id=1, source_target_pairs={{0,2},{1,0},{3,1},{5,3},{7,5},{6,7},{4,6},{2,4},{8,10},{9,8},{11,9... | collective-permute-start | bytes 614408 | tf_op jit(solution)/shard_map/ppermute | solution.py:85
  89.6 8.7 %collective-permute-start.29 = (f32[40,1280]{1,0:T(8,128)S(1)}, f32[40,1280]{1,0:T(8,128)S(1)}, u32[]{:S(2)}, u32[]{:S(2)}) collective-permute-start(f32[40,1280]{1,0:T(8,128)S(1)} %add.592), channel_id=1, source_target_pairs={{0,1},{1,3},{3,5},{5,7},{7,6},{6,4},{4,2},{2,0},{8,9},{9,11},{11,1... | collective-permute-start | bytes 614408 | tf_op jit(solution)/shard_map/ppermute | solution.py:85
  91.2 8.7 %collective-permute-start.36 = (f32[40,1280]{1,0:T(8,128)S(1)}, f32[40,1280]{1,0:T(8,128)S(1)}, u32[]{:S(2)}, u32[]{:S(2)}) collective-permute-start(f32[40,1280]{1,0:T(8,128)S(1)} %add.615), channel_id=1, source_target_pairs={{0,2},{1,0},{3,1},{5,3},{7,5},{6,7},{4,6},{2,4},{8,10},{9,8},{11,9... | collective-permute-start | bytes 614408 | tf_op jit(solution)/shard_map/ppermute | solution.py:85
  94.0 8.7 %collective-permute-start.16 = (f32[40,1280]{1,0:T(8,128)S(1)}, f32[40,1280]{1,0:T(8,128)S(1)}, u32[]{:S(2)}, u32[]{:S(2)}) collective-permute-start(f32[40,1280]{1,0:T(8,128)S(1)} %add.533), channel_id=1, source_target_pairs={{0,1},{1,3},{3,5},{5,7},{7,6},{6,4},{4,2},{2,0},{8,9},{9,11},{11,1... | collective-permute-start | bytes 614408 | tf_op jit(solution)/shard_map/ppermute | solution.py:85
  95.6 8.7 %collective-permute-start.23 = (f32[40,1280]{1,0:T(8,128)S(1)}, f32[40,1280]{1,0:T(8,128)S(1)}, u32[]{:S(2)}, u32[]{:S(2)}) collective-permute-start(f32[40,1280]{1,0:T(8,128)S(1)} %add.570), channel_id=1, source_target_pairs={{0,2},{1,0},{3,1},{5,3},{7,5},{6,7},{4,6},{2,4},{8,10},{9,8},{11,9... | collective-permute-start | bytes 614408 | tf_op jit(solution)/shard_map/ppermute | solution.py:85
  98.4 8.2 %collective-permute-start.30 = (f32[40,1280]{1,0:T(8,128)S(1)}, f32[40,1280]{1,0:T(8,128)S(1)}, u32[]{:S(2)}, u32[]{:S(2)}) collective-permute-start(f32[40,1280]{1,0:T(8,128)S(1)} %add.595), channel_id=1, source_target_pairs={{0,1},{1,3},{3,5},{5,7},{7,6},{6,4},{4,2},{2,0},{8,9},{9,11},{11,1... | collective-permute-start | bytes 614408 | tf_op jit(solution)/shard_map/ppermute | solution.py:85
  100.0 7.8 %collective-permute-start.37 = (f32[40,1280]{1,0:T(8,128)S(1)}, f32[40,1280]{1,0:T(8,128)S(1)}, u32[]{:S(2)}, u32[]{:S(2)}) collective-permute-start(f32[40,1280]{1,0:T(8,128)S(1)} %add.618), channel_id=1, source_target_pairs={{0,2},{1,0},{3,1},{5,3},{7,5},{6,7},{4,6},{2,4},{8,10},{9,8},{11,9... | collective-permute-start | bytes 614408 | tf_op jit(solution)/shard_map/ppermute | solution.py:85

commit v17 on v14

--- a/solution.py
+++ b/solution.py
@@ -156,9 +156,9 @@
         summed = summed[None]
 
         def project_all(step, after):
-            if step >= len(blocks):
+            if step < 1 or step > len(blocks):
                 return None
-            at, _, g_piece = blocks[step]
+            at, _, g_piece = blocks[step - 1]
             _, g_piece = lax.optimization_barrier((after, g_piece))
             return at, project_back(g_piece, down_weight).astype(jnp.bfloat16)
 
@@ -193,9 +193,11 @@
     owned, deferred = ring_reduce_scatter(parts, ring, pieces, project_all)
     if hidden_grad is None:
         out = jnp.zeros((views * local_rows, slice_width), jnp.bfloat16)
-        for item in deferred:
-            if item is not None:
-                out = lax.dynamic_update_slice_in_dim(out, item[1], item[0], axis=0)
+        items = [item for item in deferred if item is not None]
+        for at, _, g_piece in blocks[len(items):]:
+            items.append((at, project_back(g_piece, down_weight).astype(jnp.bfloat16)))
+        for at, back in items:
+            out = lax.dynamic_update_slice_in_dim(out, back, at, axis=0)
         hidden_grad = out.reshape(views, images_here, patches, slice_width)
     clipped_mean = owned / images_all
     noisy = clipped_mean + noise_ratio * clip * noise / images_all

time: 108 us -> 108 us (level)
  no operation moved by 1% of the time
where the time goes in v17:
time: 108 us; the launch traced here: 107 us
  waiting for transfers between devices  45.5 us (42%)
  starting transfers between devices  37.6 us (35%)
  matrix products  13.4 us (12%)
  between operations  4.84 us (4%)
  other arithmetic  3.49 us (3%)
  local copies, waits for them, and re-layouts  2.42 us (2%)
    ppermute x28, starting transfers between devices, ring_reduce_scatter(): lax.ppermute(v, 'dp', right if step < 0 else left)  29.8 us
    ppermute x28, waiting for transfers between devices, ring_reduce_scatter(): lax.ppermute(v, 'dp', right if step < 0 else left)  27.9 us
    ppermute x1, waiting for transfers between devices, exchange_four(): h_far_relay = lax.ppermute(cols(a ^ 3), 'aug', over_x)  8.81 us
    dot_general x4, matrix products, per_device(): term = jnp.dot(h_piece.T, g_piece, preferred_element_type=jnp.float32)  7.67 us
    dot_general x4, matrix products, project_back(): lax.dot_general(rows, down_weight, (((1,), (1,)), ((), ())), preferred_el...  5.77 us
    ppermute x1, waiting for transfers between devices, exchange_four(): h_far = lax.ppermute(second, 'aug', over_x)  5.45 us
    ppermute x1, starting transfers between devices, exchange_four(): h_far_relay = lax.ppermute(cols(a ^ 3), 'aug', over_x)  2.94 us
    dynamic_slice x1, local copies, waits for them, and re-layouts, cols(): return lax.dynamic_slice_in_dim(h_rows, b * sw, sw, axis=1)  2.29 us
  transfers between devices with their start and end apart: 38, of which 20 were waited for; matrix products, arithmetic and copies ran while one was open for 12% of the time, Pallas kernels for 0%

profile of v17, /device:TPU:0, one launch (start us, length us, event | category | flops | bytes accessed | tf_op | source)
XLA Modules:
  0.0 107.3 jit_solution(16966396178649489912)
XLA Ops:
  0.7 2.3 %dynamic-slice_bitcast_fusion = (bf16[128,1280]{1,0:T(8,128)(2,1)}, bf16[128,1280]{1,0:T(8,128)(2,1)}, bf16[128,1280]{1,0:T(8,128)(2,1)}) fusion(bf16[1,1,128,5120]{3,2,1,0:T(8,128)(2,1)} %param.6, s32[]{:T(128)S(6)} %select_n.691, s32[]{:T(128)S(6)} %select_n.689, s32[]{:T(128)S(6)} %select_n.690), kind=kLoop, calls=%fused_computation.21 | loop fusion | bytes 1966092 | tf_op jit(solution)/shard_map/dynamic_slice | solution.py:101
  3.0 2.9 %collective-permute-start = (bf16[128,1280]{1,0:T(8,128)(2,1)}, bf16[128,1280]{1,0:T(8,128)(2,1)}, u32[]{:S(2)}, u32[]{:S(2)}) collective-permute-start(bf16[128,1280]{1,0:T(8,128)(2,1)} %get-tuple-element.85), channel_id=1, source_target_pairs={{0,16},{8,24},{16,0},{24,8},{1,17},{9,25},{17,1},{25,9},{2,18},{10... | collective-permute-start | bytes 983048 | tf_op jit(solution)/shard_map/ppermute | solution.py:106
  5.9 8.8 %collective-permute-done = bf16[128,1280]{1,0:T(8,128)(2,1)} collective-permute-done((bf16[128,1280]{1,0:T(8,128)(2,1)}, bf16[128,1280]{1,0:T(8,128)(2,1)}, u32[]{:S(2)}, u32[]{:S(2)}) %collective-permute-start) | collective-permute-done | bytes 327712 | tf_op jit(solution)/shard_map/ppermute | solution.py:106
  14.8 0.5 collective-permute-start.1
  15.3 2.1 %fusion.6 = f32[1280,1280]{1,0:T(8,128)S(1)} fusion(bf16[1,1,128,5120]{3,2,1,0:T(8,128)(2,1)} %param.6, s32[]{:T(128)S(6)} %select_n.688, bf16[1,1,128,1280]{3,2,1,0:T(8,128)(2,1)} %param.7), kind=kOutput, calls=%fused_computation.19 | convolution fusion | flops 419430400 | bytes 7208964 | tf_op jit(solution)/shard_map/dot_general | solution.py:154
  17.4 2.1 %collective-permute-start.3 = (bf16[128,1280]{1,0:T(8,128)(2,1)S(1)}, bf16[128,1280]{1,0:T(8,128)(2,1)S(1)}, u32[]{:S(2)}, u32[]{:S(2)}) collective-permute-start(bf16[128,1280]{1,0:T(8,128)(2,1)S(1)} %copy-done.6), channel_id=1, source_target_pairs={{0,16},{8,24},{16,0},{24,8},{1,17},{9,25},{17,1},{25,9},{2,18},{10... | collective-permute-start | bytes 983048 | tf_op jit(solution)/shard_map/ppermute | solution.py:113
  19.5 1.8 %collective-permute-done.4 = bf16[128,1280]{1,0:T(8,128)(2,1)} collective-permute-done((bf16[128,1280]{1,0:T(8,128)(2,1)}, bf16[128,1280]{1,0:T(8,128)(2,1)}, u32[]{:S(2)}, u32[]{:S(2)}) %collective-permute-start.4) | collective-permute-done | bytes 327712 | tf_op jit(solution)/shard_map/ppermute | solution.py:105
  21.4 1.0 convolution_add_fusion.2
  22.4 5.5 %collective-permute-done.3 = bf16[128,1280]{1,0:T(8,128)(2,1)S(1)} collective-permute-done((bf16[128,1280]{1,0:T(8,128)(2,1)S(1)}, bf16[128,1280]{1,0:T(8,128)(2,1)S(1)}, u32[]{:S(2)}, u32[]{:S(2)}) %collective-permute-start.3) | collective-permute-done | bytes 327712 | tf_op jit(solution)/shard_map/ppermute | solution.py:113
  27.9 2.0 %convolution_add_fusion.1 = f32[1280,1280]{1,0:T(8,128)S(1)} fusion(f32[1280,1280]{1,0:T(8,128)S(1)} %convolution_add_fusion.2, bf16[128,1280]{1,0:T(8,128)(2,1)S(1)} %collective-permute-done.3, bf16[128,1280]{1,0:T(8,128)(2,1)} %collective-permute-done.4), kind=kOutput, calls=%fused_computation.1 | convolution fusion | flops 421068800 | bytes 13762560 | tf_op jit(solution)/shard_map/dot_general | solution.py:154
  29.9 2.5 %multiply_reduce_fusion = (f32[]{:T(128)}, f32[1280,1280]{1,0:T(8,128)S(1)}) fusion(f32[1280,1280]{1,0:T(8,128)S(1)} %convolution_add_fusion.1, bf16[128,1280]{1,0:T(8,128)(2,1)S(1)} %collective-permute-done.5, bf16[128,1280]{1,0:T(8,128)(2,1)S(1)} %collective-permute-done.6), kind=kOutput, calls=%fused_computation.4 | convolution fusion | flops 425984000 | bytes 13762564 | tf_op jit(solution)/shard_map/dot_general | solution.py:154
  32.4 1.7 %collective-permute-start.8 = (f32[1]{0:T(128)}, f32[1]{0:T(128)}, u32[]{:S(2)}, u32[]{:S(2)}) collective-permute-start(f32[1]{0:T(128)} %bitcast.5), channel_id=1, source_target_pairs={{0,16},{8,24},{16,0},{24,8},{1,17},{9,25},{17,1},{25,9},{2,18},{10... | collective-permute-start | bytes 20 | tf_op jit(solution)/shard_map/ppermute | solution.py:126
  34.2 0.4 collective-permute-start.7
  34.6 1.0 collective-permute-done.7
  36.8 0.5 collective-permute-done.9
  38.6 0.1 dynamic-slice_multiply_fusion.3
  38.8 1.6 %collective-permute-start.10 = (f32[40,1280]{1,0:T(8,128)S(1)}, f32[40,1280]{1,0:T(8,128)S(1)}, u32[]{:S(2)}, u32[]{:S(2)}) collective-permute-start(f32[40,1280]{1,0:T(8,128)S(1)} %get-tuple-element.80), channel_id=1, source_target_pairs={{0,1},{1,3},{3,5},{5,7},{7,6},{6,4},{4,2},{2,0},{8,9},{9,11},{11,1... | collective-permute-start | bytes 614408 | tf_op jit(solution)/shard_map/ppermute | solution.py:85
  40.3 0.5 collective-permute-start.17
  40.8 1.5 %collective-permute-start.24 = (f32[40,1280]{1,0:T(8,128)S(1)}, f32[40,1280]{1,0:T(8,128)S(1)}, u32[]{:S(2)}, u32[]{:S(2)}) collective-permute-start(f32[40,1280]{1,0:T(8,128)S(1)} %get-tuple-element.82), channel_id=1, source_target_pairs={{0,1},{1,3},{3,5},{5,7},{7,6},{6,4},{4,2},{2,0},{8,9},{9,11},{11,1... | collective-permute-start | bytes 614408 | tf_op jit(solution)/shard_map/ppermute | solution.py:85
  42.3 0.5 collective-permute-start.31
  43.0 3.8 %collective-permute-done.10 = f32[40,1280]{1,0:T(8,128)S(1)} collective-permute-done((f32[40,1280]{1,0:T(8,128)S(1)}, f32[40,1280]{1,0:T(8,128)S(1)}, u32[]{:S(2)}, u32[]{:S(2)}) %collective-permute-start.10) | collective-permute-done | bytes 204832 | tf_op jit(solution)/shard_map/ppermute | solution.py:85
  46.8 1.5 %collective-permute-start.11 = (f32[40,1280]{1,0:T(8,128)S(1)}, f32[40,1280]{1,0:T(8,128)S(1)}, u32[]{:S(2)}, u32[]{:S(2)}) collective-permute-start(f32[40,1280]{1,0:T(8,128)S(1)} %add.518), channel_id=1, source_target_pairs={{0,1},{1,3},{3,5},{5,7},{7,6},{6,4},{4,2},{2,0},{8,9},{9,11},{11,1... | collective-permute-start | bytes 614408 | tf_op jit(solution)/shard_map/ppermute | solution.py:85
  48.4 0.6 collective-permute-start.18
  49.0 2.2 %collective-permute-done.24 = f32[40,1280]{1,0:T(8,128)S(1)} collective-permute-done((f32[40,1280]{1,0:T(8,128)S(1)}, f32[40,1280]{1,0:T(8,128)S(1)}, u32[]{:S(2)}, u32[]{:S(2)}) %collective-permute-start.24) | collective-permute-done | bytes 204832 | tf_op jit(solution)/shard_map/ppermute | solution.py:85
  51.2 1.5 %collective-permute-start.25 = (f32[40,1280]{1,0:T(8,128)S(1)}, f32[40,1280]{1,0:T(8,128)S(1)}, u32[]{:S(2)}, u32[]{:S(2)}) collective-permute-start(f32[40,1280]{1,0:T(8,128)S(1)} %add.580), channel_id=1, source_target_pairs={{0,1},{1,3},{3,5},{5,7},{7,6},{6,4},{4,2},{2,0},{8,9},{9,11},{11,1... | collective-permute-start | bytes 614408 | tf_op jit(solution)/shard_map/ppermute | solution.py:85
  52.8 0.6 collective-permute-start.32
  53.6 1.2 %fusion.4 = bf16[512,1280]{1,0:T(8,128)(2,1)S(1)} fusion(bf16[512,1280]{1,0:T(8,128)(2,1)S(1)} %broadcast_in_dim.2, s32[]{:T(128)S(6)} %select_n.859, bf16[128,1280]{1,0:T(8,128)(2,1)S(1)} %bitcast.116, bf16[1280,1280]{1,0:T(8,128)(2,1)S(1)} %copy-done), kind=kOutput, calls=%fused_computation.12 | convolution fusion | flops 419594240 | bytes 3932164 | tf_op jit(solution)/shard_map/dot_general | solution.py:17
  54.8 0.8 collective-permute-done.11
  55.6 1.5 %collective-permute-start.12 = (f32[40,1280]{1,0:T(8,128)S(1)}, f32[40,1280]{1,0:T(8,128)S(1)}, u32[]{:S(2)}, u32[]{:S(2)}) collective-permute-start(f32[40,1280]{1,0:T(8,128)S(1)} %add.521), channel_id=1, source_target_pairs={{0,1},{1,3},{3,5},{5,7},{7,6},{6,4},{4,2},{2,0},{8,9},{9,11},{11,1... | collective-permute-start | bytes 614408 | tf_op jit(solution)/shard_map/ppermute | solution.py:85
  57.1 0.6 collective-permute-start.19
  57.7 2.2 %collective-permute-done.25 = f32[40,1280]{1,0:T(8,128)S(1)} collective-permute-done((f32[40,1280]{1,0:T(8,128)S(1)}, f32[40,1280]{1,0:T(8,128)S(1)}, u32[]{:S(2)}, u32[]{:S(2)}) %collective-permute-start.25) | collective-permute-done | bytes 204832 | tf_op jit(solution)/shard_map/ppermute | solution.py:85
  60.0 1.5 %collective-permute-start.26 = (f32[40,1280]{1,0:T(8,128)S(1)}, f32[40,1280]{1,0:T(8,128)S(1)}, u32[]{:S(2)}, u32[]{:S(2)}) collective-permute-start(f32[40,1280]{1,0:T(8,128)S(1)} %add.583), channel_id=1, source_target_pairs={{0,1},{1,3},{3,5},{5,7},{7,6},{6,4},{4,2},{2,0},{8,9},{9,11},{11,1... | collective-permute-start | bytes 614408 | tf_op jit(solution)/shard_map/ppermute | solution.py:85
  61.5 0.6 collective-permute-start.33
  62.2 1.2 %fusion.3 = bf16[512,1280]{1,0:T(8,128)(2,1)S(1)} fusion(bf16[512,1280]{1,0:T(8,128)(2,1)S(1)} %fusion.4, s32[]{:T(128)S(6)} %select_n.860, bf16[128,1280]{1,0:T(8,128)(2,1)S(1)} %collective-permute-done.2, bf16[1280,1280]{1,0:T(8,128)(2,1)S(1)} %copy-done), kind=kOutput, calls=%fused_computation.10 | convolution fusion | flops 419594240 | bytes 3932164 | tf_op jit(solution)/shard_map/dot_general | solution.py:17
  63.4 0.9 collective-permute-done.12
  64.3 1.5 %collective-permute-start.13 = (f32[40,1280]{1,0:T(8,128)S(1)}, f32[40,1280]{1,0:T(8,128)S(1)}, u32[]{:S(2)}, u32[]{:S(2)}) collective-permute-start(f32[40,1280]{1,0:T(8,128)S(1)} %add.524), channel_id=1, source_target_pairs={{0,1},{1,3},{3,5},{5,7},{7,6},{6,4},{4,2},{2,0},{8,9},{9,11},{11,1... | collective-permute-start | bytes 614408 | tf_op jit(solution)/shard_map/ppermute | solution.py:85
  65.9 0.6 collective-permute-start.20
  66.5 2.2 %collective-permute-done.26 = f32[40,1280]{1,0:T(8,128)S(1)} collective-permute-done((f32[40,1280]{1,0:T(8,128)S(1)}, f32[40,1280]{1,0:T(8,128)S(1)}, u32[]{:S(2)}, u32[]{:S(2)}) %collective-permute-start.26) | collective-permute-done | bytes 204832 | tf_op jit(solution)/shard_map/ppermute | solution.py:85
  68.7 1.5 %collective-permute-start.27 = (f32[40,1280]{1,0:T(8,128)S(1)}, f32[40,1280]{1,0:T(8,128)S(1)}, u32[]{:S(2)}, u32[]{:S(2)}) collective-permute-start(f32[40,1280]{1,0:T(8,128)S(1)} %add.586), channel_id=1, source_target_pairs={{0,1},{1,3},{3,5},{5,7},{7,6},{6,4},{4,2},{2,0},{8,9},{9,11},{11,1... | collective-permute-start | bytes 614408 | tf_op jit(solution)/shard_map/ppermute | solution.py:85
  70.3 0.6 collective-permute-start.34
  71.0 2.2 %fusion.2 = bf16[512,1280]{1,0:T(8,128)(2,1)S(1)} fusion(bf16[512,1280]{1,0:T(8,128)(2,1)S(1)} %fusion.3, s32[]{:T(128)S(6)} %select_n.861, bf16[128,1280]{1,0:T(8,128)(2,1)} %collective-permute-done.4, bf16[1280,1280]{1,0:T(8,128)(2,1)S(1)} %copy-done), kind=kOutput, calls=%fused_computation.8 | convolution fusion | flops 419594240 | bytes 3932164 | tf_op jit(solution)/shard_map/dot_general | solution.py:17
  73.2 1.5 %collective-permute-start.14 = (f32[40,1280]{1,0:T(8,128)S(1)}, f32[40,1280]{1,0:T(8,128)S(1)}, u32[]{:S(2)}, u32[]{:S(2)}) collective-permute-start(f32[40,1280]{1,0:T(8,128)S(1)} %add.527), channel_id=1, source_target_pairs={{0,1},{1,3},{3,5},{5,7},{7,6},{6,4},{4,2},{2,0},{8,9},{9,11},{11,1... | collective-permute-start | bytes 614408 | tf_op jit(solution)/shard_map/ppermute | solution.py:85
  74.8 0.6 collective-permute-start.21
  75.4 2.1 %collective-permute-done.27 = f32[40,1280]{1,0:T(8,128)S(1)} collective-permute-done((f32[40,1280]{1,0:T(8,128)S(1)}, f32[40,1280]{1,0:T(8,128)S(1)}, u32[]{:S(2)}, u32[]{:S(2)}) %collective-permute-start.27) | collective-permute-done | bytes 204832 | tf_op jit(solution)/shard_map/ppermute | solution.py:85
  77.5 1.5 %collective-permute-start.28 = (f32[40,1280]{1,0:T(8,128)S(1)}, f32[40,1280]{1,0:T(8,128)S(1)}, u32[]{:S(2)}, u32[]{:S(2)}) collective-permute-start(f32[40,1280]{1,0:T(8,128)S(1)} %add.589), channel_id=1, source_target_pairs={{0,1},{1,3},{3,5},{5,7},{7,6},{6,4},{4,2},{2,0},{8,9},{9,11},{11,1... | collective-permute-start | bytes 614408 | tf_op jit(solution)/shard_map/ppermute | solution.py:85
  79.1 0.8 collective-permute-start.35
  80.0 1.2 %fusion.1 = bf16[512,1280]{1,0:T(8,128)(2,1)S(1)} fusion(bf16[512,1280]{1,0:T(8,128)(2,1)S(1)} %fusion.2, s32[]{:T(128)S(6)} %select_n.862, bf16[128,1280]{1,0:T(8,128)(2,1)S(1)} %collective-permute-done.6, bf16[1280,1280]{1,0:T(8,128)(2,1)S(1)} %copy-done), kind=kOutput, calls=%fused_computation.6 | convolution fusion | flops 419594240 | bytes 3932164 | tf_op jit(solution)/shard_map/dot_general | solution.py:17
  81.2 0.6 collective-permute-done.14
  81.9 1.5 %collective-permute-start.15 = (f32[40,1280]{1,0:T(8,128)S(1)}, f32[40,1280]{1,0:T(8,128)S(1)}, u32[]{:S(2)}, u32[]{:S(2)}) collective-permute-start(f32[40,1280]{1,0:T(8,128)S(1)} %add.530), channel_id=1, source_target_pairs={{0,1},{1,3},{3,5},{5,7},{7,6},{6,4},{4,2},{2,0},{8,9},{9,11},{11,1... | collective-permute-start | bytes 614408 | tf_op jit(solution)/shard_map/ppermute | solution.py:85
  83.5 0.6 collective-permute-start.22
  84.1 2.2 %collective-permute-done.28 = f32[40,1280]{1,0:T(8,128)S(1)} collective-permute-done((f32[40,1280]{1,0:T(8,128)S(1)}, f32[40,1280]{1,0:T(8,128)S(1)}, u32[]{:S(2)}, u32[]{:S(2)}) %collective-permute-start.28) | collective-permute-done | bytes 204832 | tf_op jit(solution)/shard_map/ppermute | solution.py:85
  86.3 1.5 %collective-permute-start.29 = (f32[40,1280]{1,0:T(8,128)S(1)}, f32[40,1280]{1,0:T(8,128)S(1)}, u32[]{:S(2)}, u32[]{:S(2)}) collective-permute-start(f32[40,1280]{1,0:T(8,128)S(1)} %add.592), channel_id=1, source_target_pairs={{0,1},{1,3},{3,5},{5,7},{7,6},{6,4},{4,2},{2,0},{8,9},{9,11},{11,1... | collective-permute-start | bytes 614408 | tf_op jit(solution)/shard_map/ppermute | solution.py:85
  87.9 0.6 collective-permute-start.36
  88.6 2.1 %collective-permute-done.15 = f32[40,1280]{1,0:T(8,128)S(1)} collective-permute-done((f32[40,1280]{1,0:T(8,128)S(1)}, f32[40,1280]{1,0:T(8,128)S(1)}, u32[]{:S(2)}, u32[]{:S(2)}) %collective-permute-start.15) | collective-permute-done | bytes 204832 | tf_op jit(solution)/shard_map/ppermute | solution.py:85
  90.7 1.5 %collective-permute-start.16 = (f32[40,1280]{1,0:T(8,128)S(1)}, f32[40,1280]{1,0:T(8,128)S(1)}, u32[]{:S(2)}, u32[]{:S(2)}) collective-permute-start(f32[40,1280]{1,0:T(8,128)S(1)} %add.533), channel_id=1, source_target_pairs={{0,1},{1,3},{3,5},{5,7},{7,6},{6,4},{4,2},{2,0},{8,9},{9,11},{11,1... | collective-permute-start | bytes 614408 | tf_op jit(solution)/shard_map/ppermute | solution.py:85
  92.3 0.6 collective-permute-start.23
  92.8 2.2 %collective-permute-done.29 = f32[40,1280]{1,0:T(8,128)S(1)} collective-permute-done((f32[40,1280]{1,0:T(8,128)S(1)}, f32[40,1280]{1,0:T(8,128)S(1)}, u32[]{:S(2)}, u32[]{:S(2)}) %collective-permute-start.29) | collective-permute-done | bytes 204832 | tf_op jit(solution)/shard_map/ppermute | solution.py:85
  95.1 1.5 %collective-permute-start.30 = (f32[40,1280]{1,0:T(8,128)S(1)}, f32[40,1280]{1,0:T(8,128)S(1)}, u32[]{:S(2)}, u32[]{:S(2)}) collective-permute-start(f32[40,1280]{1,0:T(8,128)S(1)} %add.595), channel_id=1, source_target_pairs={{0,1},{1,3},{3,5},{5,7},{7,6},{6,4},{4,2},{2,0},{8,9},{9,11},{11,1... | collective-permute-start | bytes 614408 | tf_op jit(solution)/shard_map/ppermute | solution.py:85
  96.6 0.6 collective-permute-start.37
  97.3 2.1 %collective-permute-done.16 = f32[40,1280]{1,0:T(8,128)S(1)} collective-permute-done((f32[40,1280]{1,0:T(8,128)S(1)}, f32[40,1280]{1,0:T(8,128)S(1)}, u32[]{:S(2)}, u32[]{:S(2)}) %collective-permute-start.16) | collective-permute-done | bytes 204832 | tf_op jit(solution)/shard_map/ppermute | solution.py:85
  99.5 1.5 %collective-permute-done.23 = f32[40,1280]{1,0:T(8,128)S(1)} collective-permute-done((f32[40,1280]{1,0:T(8,128)S(1)}, f32[40,1280]{1,0:T(8,128)S(1)}, u32[]{:S(2)}, u32[]{:S(2)}) %collective-permute-start.23) | collective-permute-done | bytes 204832 | tf_op jit(solution)/shard_map/ppermute | solution.py:85
  101.0 1.7 %collective-permute-done.30 = f32[40,1280]{1,0:T(8,128)S(1)} collective-permute-done((f32[40,1280]{1,0:T(8,128)S(1)}, f32[40,1280]{1,0:T(8,128)S(1)}, u32[]{:S(2)}, u32[]{:S(2)}) %collective-permute-start.30) | collective-permute-done | bytes 204832 | tf_op jit(solution)/shard_map/ppermute | solution.py:85
  102.7 1.4 %collective-permute-done.37 = f32[40,1280]{1,0:T(8,128)S(1)} collective-permute-done((f32[40,1280]{1,0:T(8,128)S(1)}, f32[40,1280]{1,0:T(8,128)S(1)}, u32[]{:S(2)}, u32[]{:S(2)}) %collective-permute-start.37) | collective-permute-done | bytes 204832 | tf_op jit(solution)/shard_map/ppermute | solution.py:85
  104.2 2.0 %add_divide_fusion = (f32[160,1280]{1,0:T(8,128)}, f32[160,1280]{1,0:T(8,128)}, f32[160,1280]{1,0:T(8,128)}, f32[160,1280]{1,0:T(8,128)}) fusion(f32[160,1280]{1,0:T(8,128)S(1)} %copy-done.3, f32[160,1280]{1,0:T(8,128)S(1)} %copy-done.4, f32[160,1280]{1,0:T(8,128)S(1)} %copy-done.5, f32[40,1280]{1,0:T(8,128)S(1)} %add.621, f32[40,1280]{1,0:T(8,128)S(1)} %add.598, ...), kind=kLoop, calls=%fused_computation.16 | loop fusion | flops 3481600 | bytes 6553600 | tf_op jit(solution)/shard_map/div | solution.py:207
  (94 shorter events, 1.6 us)
Async XLA Ops:
  0.6 52.9 %copy-start = (bf16[1280,1280]{1,0:T(8,128)(2,1)S(1)}, bf16[1280,1280]{1,0:T(8,128)(2,1)}, u32[]{:S(2)}) copy-start(bf16[1280,1280]{1,0:T(8,128)(2,1)} %param.8) | copy-start | bytes 9830404
  3.0 11.8 %collective-permute-start = (bf16[128,1280]{1,0:T(8,128)(2,1)}, bf16[128,1280]{1,0:T(8,128)(2,1)}, u32[]{:S(2)}, u32[]{:S(2)}) collective-permute-start(bf16[128,1280]{1,0:T(8,128)(2,1)} %get-tuple-element.85), channel_id=1, source_target_pairs={{0,16},{8,24},{16,0},{24,8},{1,17},{9,25},{17,1},{25,9},{2,18},{10... | collective-permute-start | bytes 983048 | tf_op jit(solution)/shard_map/ppermute | solution.py:106
  5.9 15.4 %collective-permute-start.4 = (bf16[128,1280]{1,0:T(8,128)(2,1)}, bf16[128,1280]{1,0:T(8,128)(2,1)}, u32[]{:S(2)}, u32[]{:S(2)}) collective-permute-start(bf16[128,1280]{1,0:T(8,128)(2,1)} %bitcast.114), channel_id=1, source_target_pairs={{0,16},{8,24},{16,0},{24,8},{1,17},{9,25},{17,1},{25,9},{2,18},{10... | collective-permute-start | bytes 983048 | tf_op jit(solution)/shard_map/ppermute | solution.py:105
  5.9 11.4 %copy-start.6 = (bf16[128,1280]{1,0:T(8,128)(2,1)S(1)}, bf16[128,1280]{1,0:T(8,128)(2,1)}, u32[]{:S(2)}) copy-start(bf16[128,1280]{1,0:T(8,128)(2,1)} %get-tuple-element.43) | copy-start | bytes 983044
  14.8 6.6 %collective-permute-start.2 = (bf16[128,1280]{1,0:T(8,128)(2,1)}, bf16[128,1280]{1,0:T(8,128)(2,1)S(1)}, u32[]{:S(2)}, u32[]{:S(2)}) collective-permute-start(bf16[128,1280]{1,0:T(8,128)(2,1)} %bitcast.115), channel_id=1, source_target_pairs={{0,8},{8,0},{16,24},{24,16},{1,9},{9,1},{17,25},{25,17},{2,10},{10... | collective-permute-start | bytes 983048 | tf_op jit(solution)/shard_map/ppermute | solution.py:108
  14.8 6.6 %collective-permute-start.1 = (bf16[128,1280]{1,0:T(8,128)(2,1)}, bf16[128,1280]{1,0:T(8,128)(2,1)S(1)}, u32[]{:S(2)}, u32[]{:S(2)}) collective-permute-start(bf16[128,1280]{1,0:T(8,128)(2,1)} %get-tuple-element.41), channel_id=1, source_target_pairs={{0,8},{8,0},{16,24},{24,16},{1,9},{9,1},{17,25},{25,17},{2,10},{10... | collective-permute-start | bytes 983048 | tf_op jit(solution)/shard_map/ppermute | solution.py:109
  17.4 10.5 %collective-permute-start.3 = (bf16[128,1280]{1,0:T(8,128)(2,1)S(1)}, bf16[128,1280]{1,0:T(8,128)(2,1)S(1)}, u32[]{:S(2)}, u32[]{:S(2)}) collective-permute-start(bf16[128,1280]{1,0:T(8,128)(2,1)S(1)} %copy-done.6), channel_id=1, source_target_pairs={{0,16},{8,24},{16,0},{24,8},{1,17},{9,25},{17,1},{25,9},{2,18},{10... | collective-permute-start | bytes 983048 | tf_op jit(solution)/shard_map/ppermute | solution.py:113
  19.5 10.4 %collective-permute-start.5 = (bf16[128,1280]{1,0:T(8,128)(2,1)}, bf16[128,1280]{1,0:T(8,128)(2,1)S(1)}, u32[]{:S(2)}, u32[]{:S(2)}) collective-permute-start(bf16[128,1280]{1,0:T(8,128)(2,1)} %collective-permute-done), channel_id=1, source_target_pairs={{0,8},{8,0},{16,24},{24,16},{1,9},{9,1},{17,25},{25,17},{2,10},{10... | collective-permute-start | bytes 983048 | tf_op jit(solution)/shard_map/ppermute | solution.py:111
  21.3 8.6 %collective-permute-start.6 = (bf16[128,1280]{1,0:T(8,128)(2,1)}, bf16[128,1280]{1,0:T(8,128)(2,1)S(1)}, u32[]{:S(2)}, u32[]{:S(2)}) collective-permute-start(bf16[128,1280]{1,0:T(8,128)(2,1)} %collective-permute-done.4), channel_id=1, source_target_pairs={{0,8},{8,0},{16,24},{24,16},{1,9},{9,1},{17,25},{25,17},{2,10},{10... | collective-permute-start | bytes 983048 | tf_op jit(solution)/shard_map/ppermute | solution.py:110
  32.4 21.2 %copy-start.1 = (bf16[1,1,128,1280]{3,2,1,0:T(8,128)(2,1)S(1)}, bf16[1,1,128,1280]{3,2,1,0:T(8,128)(2,1)}, u32[]{:S(2)}) copy-start(bf16[1,1,128,1280]{3,2,1,0:T(8,128)(2,1)} %param.7) | copy-start | bytes 983044
  32.4 4.4 %collective-permute-start.8 = (f32[1]{0:T(128)}, f32[1]{0:T(128)}, u32[]{:S(2)}, u32[]{:S(2)}) collective-permute-start(f32[1]{0:T(128)} %bitcast.5), channel_id=1, source_target_pairs={{0,16},{8,24},{16,0},{24,8},{1,17},{9,25},{17,1},{25,9},{2,18},{10... | collective-permute-start | bytes 20 | tf_op jit(solution)/shard_map/ppermute | solution.py:126
  34.2 3.2 %collective-permute-start.9 = (f32[1]{0:T(128)}, f32[1]{0:T(128)}, u32[]{:S(2)}, u32[]{:S(2)}) collective-permute-start(f32[1]{0:T(128)} %bitcast.5), channel_id=1, source_target_pairs={{0,24},{8,16},{16,8},{24,0},{1,25},{9,17},{17,9},{25,1},{2,26},{10... | collective-permute-start | bytes 20 | tf_op jit(solution)/shard_map/ppermute | solution.py:126
  34.2 1.3 %collective-permute-start.7 = (f32[1]{0:T(128)}, f32[1]{0:T(128)}, u32[]{:S(2)}, u32[]{:S(2)}) collective-permute-start(f32[1]{0:T(128)} %bitcast.5), channel_id=1, source_target_pairs={{0,8},{8,0},{16,24},{24,16},{1,9},{9,1},{17,25},{25,17},{2,10},{10... | collective-permute-start | bytes 20 | tf_op jit(solution)/shard_map/ppermute | solution.py:126
  38.8 8.0 %collective-permute-start.10 = (f32[40,1280]{1,0:T(8,128)S(1)}, f32[40,1280]{1,0:T(8,128)S(1)}, u32[]{:S(2)}, u32[]{:S(2)}) collective-permute-start(f32[40,1280]{1,0:T(8,128)S(1)} %get-tuple-element.80), channel_id=1, source_target_pairs={{0,1},{1,3},{3,5},{5,7},{7,6},{6,4},{4,2},{2,0},{8,9},{9,11},{11,1... | collective-permute-start | bytes 614408 | tf_op jit(solution)/shard_map/ppermute | solution.py:85
  40.3 8.0 %collective-permute-start.17 = (f32[40,1280]{1,0:T(8,128)S(1)}, f32[40,1280]{1,0:T(8,128)S(1)}, u32[]{:S(2)}, u32[]{:S(2)}) collective-permute-start(f32[40,1280]{1,0:T(8,128)S(1)} %get-tuple-element.83), channel_id=1, source_target_pairs={{0,2},{1,0},{3,1},{5,3},{7,5},{6,7},{4,6},{2,4},{8,10},{9,8},{11,9... | collective-permute-start | bytes 614408 | tf_op jit(solution)/shard_map/ppermute | solution.py:85
  40.8 10.3 %collective-permute-start.24 = (f32[40,1280]{1,0:T(8,128)S(1)}, f32[40,1280]{1,0:T(8,128)S(1)}, u32[]{:S(2)}, u32[]{:S(2)}) collective-permute-start(f32[40,1280]{1,0:T(8,128)S(1)} %get-tuple-element.82), channel_id=1, source_target_pairs={{0,1},{1,3},{3,5},{5,7},{7,6},{6,4},{4,2},{2,0},{8,9},{9,11},{11,1... | collective-permute-start | bytes 614408 | tf_op jit(solution)/shard_map/ppermute | solution.py:85
  42.3 10.4 %collective-permute-start.31 = (f32[40,1280]{1,0:T(8,128)S(1)}, f32[40,1280]{1,0:T(8,128)S(1)}, u32[]{:S(2)}, u32[]{:S(2)}) collective-permute-start(f32[40,1280]{1,0:T(8,128)S(1)} %get-tuple-element.81), channel_id=1, source_target_pairs={{0,2},{1,0},{3,1},{5,3},{7,5},{6,7},{4,6},{2,4},{8,10},{9,8},{11,9... | collective-permute-start | bytes 614408 | tf_op jit(solution)/shard_map/ppermute | solution.py:85
  46.8 8.7 %collective-permute-start.11 = (f32[40,1280]{1,0:T(8,128)S(1)}, f32[40,1280]{1,0:T(8,128)S(1)}, u32[]{:S(2)}, u32[]{:S(2)}) collective-permute-start(f32[40,1280]{1,0:T(8,128)S(1)} %add.518), channel_id=1, source_target_pairs={{0,1},{1,3},{3,5},{5,7},{7,6},{6,4},{4,2},{2,0},{8,9},{9,11},{11,1... | collective-permute-start | bytes 614408 | tf_op jit(solution)/shard_map/ppermute | solution.py:85
  48.4 8.7 %collective-permute-start.18 = (f32[40,1280]{1,0:T(8,128)S(1)}, f32[40,1280]{1,0:T(8,128)S(1)}, u32[]{:S(2)}, u32[]{:S(2)}) collective-permute-start(f32[40,1280]{1,0:T(8,128)S(1)} %add.545), channel_id=1, source_target_pairs={{0,2},{1,0},{3,1},{5,3},{7,5},{6,7},{4,6},{2,4},{8,10},{9,8},{11,9... | collective-permute-start | bytes 614408 | tf_op jit(solution)/shard_map/ppermute | solution.py:85
  51.2 8.7 %collective-permute-start.25 = (f32[40,1280]{1,0:T(8,128)S(1)}, f32[40,1280]{1,0:T(8,128)S(1)}, u32[]{:S(2)}, u32[]{:S(2)}) collective-permute-start(f32[40,1280]{1,0:T(8,128)S(1)} %add.580), channel_id=1, source_target_pairs={{0,1},{1,3},{3,5},{5,7},{7,6},{6,4},{4,2},{2,0},{8,9},{9,11},{11,1... | collective-permute-start | bytes 614408 | tf_op jit(solution)/shard_map/ppermute | solution.py:85
  52.8 8.7 %collective-permute-start.32 = (f32[40,1280]{1,0:T(8,128)S(1)}, f32[40,1280]{1,0:T(8,128)S(1)}, u32[]{:S(2)}, u32[]{:S(2)}) collective-permute-start(f32[40,1280]{1,0:T(8,128)S(1)} %add.603), channel_id=1, source_target_pairs={{0,2},{1,0},{3,1},{5,3},{7,5},{6,7},{4,6},{2,4},{8,10},{9,8},{11,9... | collective-permute-start | bytes 614408 | tf_op jit(solution)/shard_map/ppermute | solution.py:85
  55.6 8.7 %collective-permute-start.12 = (f32[40,1280]{1,0:T(8,128)S(1)}, f32[40,1280]{1,0:T(8,128)S(1)}, u32[]{:S(2)}, u32[]{:S(2)}) collective-permute-start(f32[40,1280]{1,0:T(8,128)S(1)} %add.521), channel_id=1, source_target_pairs={{0,1},{1,3},{3,5},{5,7},{7,6},{6,4},{4,2},{2,0},{8,9},{9,11},{11,1... | collective-permute-start | bytes 614408 | tf_op jit(solution)/shard_map/ppermute | solution.py:85
  57.1 8.7 %collective-permute-start.19 = (f32[40,1280]{1,0:T(8,128)S(1)}, f32[40,1280]{1,0:T(8,128)S(1)}, u32[]{:S(2)}, u32[]{:S(2)}) collective-permute-start(f32[40,1280]{1,0:T(8,128)S(1)} %add.550), channel_id=1, source_target_pairs={{0,2},{1,0},{3,1},{5,3},{7,5},{6,7},{4,6},{2,4},{8,10},{9,8},{11,9... | collective-permute-start | bytes 614408 | tf_op jit(solution)/shard_map/ppermute | solution.py:85
  60.0 8.7 %collective-permute-start.26 = (f32[40,1280]{1,0:T(8,128)S(1)}, f32[40,1280]{1,0:T(8,128)S(1)}, u32[]{:S(2)}, u32[]{:S(2)}) collective-permute-start(f32[40,1280]{1,0:T(8,128)S(1)} %add.583), channel_id=1, source_target_pairs={{0,1},{1,3},{3,5},{5,7},{7,6},{6,4},{4,2},{2,0},{8,9},{9,11},{11,1... | collective-permute-start | bytes 614408 | tf_op jit(solution)/shard_map/ppermute | solution.py:85
  61.5 8.7 %collective-permute-start.33 = (f32[40,1280]{1,0:T(8,128)S(1)}, f32[40,1280]{1,0:T(8,128)S(1)}, u32[]{:S(2)}, u32[]{:S(2)}) collective-permute-start(f32[40,1280]{1,0:T(8,128)S(1)} %add.606), channel_id=1, source_target_pairs={{0,2},{1,0},{3,1},{5,3},{7,5},{6,7},{4,6},{2,4},{8,10},{9,8},{11,9... | collective-permute-start | bytes 614408 | tf_op jit(solution)/shard_map/ppermute | solution.py:85
  64.3 8.9 %collective-permute-start.13 = (f32[40,1280]{1,0:T(8,128)S(1)}, f32[40,1280]{1,0:T(8,128)S(1)}, u32[]{:S(2)}, u32[]{:S(2)}) collective-permute-start(f32[40,1280]{1,0:T(8,128)S(1)} %add.524), channel_id=1, source_target_pairs={{0,1},{1,3},{3,5},{5,7},{7,6},{6,4},{4,2},{2,0},{8,9},{9,11},{11,1... | collective-permute-start | bytes 614408 | tf_op jit(solution)/shard_map/ppermute | solution.py:85
  65.9 8.9 %collective-permute-start.20 = (f32[40,1280]{1,0:T(8,128)S(1)}, f32[40,1280]{1,0:T(8,128)S(1)}, u32[]{:S(2)}, u32[]{:S(2)}) collective-permute-start(f32[40,1280]{1,0:T(8,128)S(1)} %add.555), channel_id=1, source_target_pairs={{0,2},{1,0},{3,1},{5,3},{7,5},{6,7},{4,6},{2,4},{8,10},{9,8},{11,9... | collective-permute-start | bytes 614408 | tf_op jit(solution)/shard_map/ppermute | solution.py:85
  68.7 8.7 %collective-permute-start.27 = (f32[40,1280]{1,0:T(8,128)S(1)}, f32[40,1280]{1,0:T(8,128)S(1)}, u32[]{:S(2)}, u32[]{:S(2)}) collective-permute-start(f32[40,1280]{1,0:T(8,128)S(1)} %add.586), channel_id=1, source_target_pairs={{0,1},{1,3},{3,5},{5,7},{7,6},{6,4},{4,2},{2,0},{8,9},{9,11},{11,1... | collective-permute-start | bytes 614408 | tf_op jit(solution)/shard_map/ppermute | solution.py:85
  70.3 8.7 %collective-permute-start.34 = (f32[40,1280]{1,0:T(8,128)S(1)}, f32[40,1280]{1,0:T(8,128)S(1)}, u32[]{:S(2)}, u32[]{:S(2)}) collective-permute-start(f32[40,1280]{1,0:T(8,128)S(1)} %add.609), channel_id=1, source_target_pairs={{0,2},{1,0},{3,1},{5,3},{7,5},{6,7},{4,6},{2,4},{8,10},{9,8},{11,9... | collective-permute-start | bytes 614408 | tf_op jit(solution)/shard_map/ppermute | solution.py:85
  73.2 8.6 %collective-permute-start.14 = (f32[40,1280]{1,0:T(8,128)S(1)}, f32[40,1280]{1,0:T(8,128)S(1)}, u32[]{:S(2)}, u32[]{:S(2)}) collective-permute-start(f32[40,1280]{1,0:T(8,128)S(1)} %add.527), channel_id=1, source_target_pairs={{0,1},{1,3},{3,5},{5,7},{7,6},{6,4},{4,2},{2,0},{8,9},{9,11},{11,1... | collective-permute-start | bytes 614408 | tf_op jit(solution)/shard_map/ppermute | solution.py:85
  74.8 8.6 %collective-permute-start.21 = (f32[40,1280]{1,0:T(8,128)S(1)}, f32[40,1280]{1,0:T(8,128)S(1)}, u32[]{:S(2)}, u32[]{:S(2)}) collective-permute-start(f32[40,1280]{1,0:T(8,128)S(1)} %add.560), channel_id=1, source_target_pairs={{0,2},{1,0},{3,1},{5,3},{7,5},{6,7},{4,6},{2,4},{8,10},{9,8},{11,9... | collective-permute-start | bytes 614408 | tf_op jit(solution)/shard_map/ppermute | solution.py:85
  77.5 8.7 %collective-permute-start.28 = (f32[40,1280]{1,0:T(8,128)S(1)}, f32[40,1280]{1,0:T(8,128)S(1)}, u32[]{:S(2)}, u32[]{:S(2)}) collective-permute-start(f32[40,1280]{1,0:T(8,128)S(1)} %add.589), channel_id=1, source_target_pairs={{0,1},{1,3},{3,5},{5,7},{7,6},{6,4},{4,2},{2,0},{8,9},{9,11},{11,1... | collective-permute-start | bytes 614408 | tf_op jit(solution)/shard_map/ppermute | solution.py:85
  79.1 8.7 %collective-permute-start.35 = (f32[40,1280]{1,0:T(8,128)S(1)}, f32[40,1280]{1,0:T(8,128)S(1)}, u32[]{:S(2)}, u32[]{:S(2)}) collective-permute-start(f32[40,1280]{1,0:T(8,128)S(1)} %add.612), channel_id=1, source_target_pairs={{0,2},{1,0},{3,1},{5,3},{7,5},{6,7},{4,6},{2,4},{8,10},{9,8},{11,9... | collective-permute-start | bytes 614408 | tf_op jit(solution)/shard_map/ppermute | solution.py:85
  80.0 24.2 %copy-start.3 = (f32[160,1280]{1,0:T(8,128)S(1)}, f32[160,1280]{1,0:T(8,128)}, u32[]{:S(2)}) copy-start(f32[160,1280]{1,0:T(8,128)} %param.11) | copy-start | bytes 2457604
  80.0 24.2 %copy-start.4 = (f32[160,1280]{1,0:T(8,128)S(1)}, f32[160,1280]{1,0:T(8,128)}, u32[]{:S(2)}) copy-start(f32[160,1280]{1,0:T(8,128)} %param.10) | copy-start | bytes 2457604
  80.0 24.2 %copy-start.5 = (f32[160,1280]{1,0:T(8,128)S(1)}, f32[160,1280]{1,0:T(8,128)}, u32[]{:S(2)}) copy-start(f32[160,1280]{1,0:T(8,128)} %param.9) | copy-start | bytes 2457604
  81.2 25.0 %copy-start.2 = (bf16[512,1280]{1,0:T(8,128)(2,1)}, bf16[512,1280]{1,0:T(8,128)(2,1)S(1)}, u32[]{:S(2)}) copy-start(bf16[512,1280]{1,0:T(8,128)(2,1)S(1)} %fusion.1) | copy-start | bytes 3932164
  81.9 8.7 %collective-permute-start.15 = (f32[40,1280]{1,0:T(8,128)S(1)}, f32[40,1280]{1,0:T(8,128)S(1)}, u32[]{:S(2)}, u32[]{:S(2)}) collective-permute-start(f32[40,1280]{1,0:T(8,128)S(1)} %add.530), channel_id=1, source_target_pairs={{0,1},{1,3},{3,5},{5,7},{7,6},{6,4},{4,2},{2,0},{8,9},{9,11},{11,1... | collective-permute-start | bytes 614408 | tf_op jit(solution)/shard_map/ppermute | solution.py:85
  83.5 8.7 %collective-permute-start.22 = (f32[40,1280]{1,0:T(8,128)S(1)}, f32[40,1280]{1,0:T(8,128)S(1)}, u32[]{:S(2)}, u32[]{:S(2)}) collective-permute-start(f32[40,1280]{1,0:T(8,128)S(1)} %add.565), channel_id=1, source_target_pairs={{0,2},{1,0},{3,1},{5,3},{7,5},{6,7},{4,6},{2,4},{8,10},{9,8},{11,9... | collective-permute-start | bytes 614408 | tf_op jit(solution)/shard_map/ppermute | solution.py:85
  86.3 8.7 %collective-permute-start.29 = (f32[40,1280]{1,0:T(8,128)S(1)}, f32[40,1280]{1,0:T(8,128)S(1)}, u32[]{:S(2)}, u32[]{:S(2)}) collective-permute-start(f32[40,1280]{1,0:T(8,128)S(1)} %add.592), channel_id=1, source_target_pairs={{0,1},{1,3},{3,5},{5,7},{7,6},{6,4},{4,2},{2,0},{8,9},{9,11},{11,1... | collective-permute-start | bytes 614408 | tf_op jit(solution)/shard_map/ppermute | solution.py:85
  87.9 8.7 %collective-permute-start.36 = (f32[40,1280]{1,0:T(8,128)S(1)}, f32[40,1280]{1,0:T(8,128)S(1)}, u32[]{:S(2)}, u32[]{:S(2)}) collective-permute-start(f32[40,1280]{1,0:T(8,128)S(1)} %add.615), channel_id=1, source_target_pairs={{0,2},{1,0},{3,1},{5,3},{7,5},{6,7},{4,6},{2,4},{8,10},{9,8},{11,9... | collective-permute-start | bytes 614408 | tf_op jit(solution)/shard_map/ppermute | solution.py:85
  90.7 8.7 %collective-permute-start.16 = (f32[40,1280]{1,0:T(8,128)S(1)}, f32[40,1280]{1,0:T(8,128)S(1)}, u32[]{:S(2)}, u32[]{:S(2)}) collective-permute-start(f32[40,1280]{1,0:T(8,128)S(1)} %add.533), channel_id=1, source_target_pairs={{0,1},{1,3},{3,5},{5,7},{7,6},{6,4},{4,2},{2,0},{8,9},{9,11},{11,1... | collective-permute-start | bytes 614408 | tf_op jit(solution)/shard_map/ppermute | solution.py:85
  92.3 8.7 %collective-permute-start.23 = (f32[40,1280]{1,0:T(8,128)S(1)}, f32[40,1280]{1,0:T(8,128)S(1)}, u32[]{:S(2)}, u32[]{:S(2)}) collective-permute-start(f32[40,1280]{1,0:T(8,128)S(1)} %add.570), channel_id=1, source_target_pairs={{0,2},{1,0},{3,1},{5,3},{7,5},{6,7},{4,6},{2,4},{8,10},{9,8},{11,9... | collective-permute-start | bytes 614408 | tf_op jit(solution)/shard_map/ppermute | solution.py:85
  95.1 7.6 %collective-permute-start.30 = (f32[40,1280]{1,0:T(8,128)S(1)}, f32[40,1280]{1,0:T(8,128)S(1)}, u32[]{:S(2)}, u32[]{:S(2)}) collective-permute-start(f32[40,1280]{1,0:T(8,128)S(1)} %add.595), channel_id=1, source_target_pairs={{0,1},{1,3},{3,5},{5,7},{7,6},{6,4},{4,2},{2,0},{8,9},{9,11},{11,1... | collective-permute-start | bytes 614408 | tf_op jit(solution)/shard_map/ppermute | solution.py:85
  96.6 7.5 %collective-permute-start.37 = (f32[40,1280]{1,0:T(8,128)S(1)}, f32[40,1280]{1,0:T(8,128)S(1)}, u32[]{:S(2)}, u32[]{:S(2)}) collective-permute-start(f32[40,1280]{1,0:T(8,128)S(1)} %add.618), channel_id=1, source_target_pairs={{0,2},{1,0},{3,1},{5,3},{7,5},{6,7},{4,6},{2,4},{8,10},{9,8},{11,9... | collective-permute-start | bytes 614408 | tf_op jit(solution)/shard_map/ppermute | solution.py:85

commit v18 on v17

--- a/solution.py
+++ b/solution.py
@@ -174,7 +174,12 @@
         hidden_grad = back_rows.astype(jnp.bfloat16).reshape(views, images_here, patches, slice_width)
         project_all = None
     grads = summed / views
-    partial_value = jnp.sum(grads * grads, axis=(1, 2))
+    groups_of_rows = 10 if grads.shape[1] % 80 == 0 else 1
+    per_group = jnp.sum(
+        (grads * grads).reshape(grads.shape[0], groups_of_rows, -1, grads.shape[2]),
+        axis=(2, 3),
+    )
+    partial_value = jnp.sum(lax.optimization_barrier(per_group), axis=1)
     squares = butterfly_sum(partial_value, views)
     image_norms = jnp.sqrt(squares)
     factor = clip / jnp.maximum(image_norms, clip)

time: 108 us -> 111 us (1.028)
  other arithmetic: 3.49 us -> 10.9 us
  waiting for transfers between devices: 45.5 us -> 40.1 us
  matrix products: 13.4 us -> 14.8 us
    reduce_sum x28, other arithmetic: 0.65 us -> 6.22 us  [parts(): jnp.sum(factor[:, None, None] * rows, axis=0)]
    ppermute x28, waiting for transfers between devices: 27.9 us -> 22.4 us  [ring_reduce_scatter(): lax.ppermute(v, 'dp', right if step < 0 else left)]
    dot_general x4, matrix products: 7.67 us -> 9.08 us  [per_device(): term = jnp.dot(h_piece.T, g_piece, preferred_element_type=jnp.float32)]
    mul x1, other arithmetic: 0.1 us -> 1.3 us  [parts(): factor[:, None, None] * rows]
  transfers between devices with their start and end apart: 38 -> 38, of which waited for: 20 -> 19; matrix products, arithmetic and copies ran while one was open for 12% -> 16% of each run, Pallas kernels for 0% -> 0%
where the time goes in v18:
time: 111 us
  waiting for transfers between devices  40.1 us (36%)
  starting transfers between devices  37.4 us (34%)
  matrix products  14.8 us (13%)
  other arithmetic  10.9 us (10%)
  between operations  4.9 us (4%)
  local copies, waits for them, and re-layouts  2.45 us (2%)
    ppermute x28, starting transfers between devices, ring_reduce_scatter(): lax.ppermute(v, 'dp', right if step < 0 else left)  29.7 us
    ppermute x28, waiting for transfers between devices, ring_reduce_scatter(): lax.ppermute(v, 'dp', right if step < 0 else left)  22.4 us
    dot_general x4, matrix products, per_device(): term = jnp.dot(h_piece.T, g_piece, preferred_element_type=jnp.float32)  9.08 us
    ppermute x1, waiting for transfers between devices, exchange_four(): h_far_relay = lax.ppermute(cols(a ^ 3), 'aug', over_x)  8.81 us
    reduce_sum x28, other arithmetic, parts(): jnp.sum(factor[:, None, None] * rows, axis=0)  6.22 us
    dot_general x4, matrix products, project_back(): lax.dot_general(rows, down_weight, (((1,), (1,)), ((), ())), preferred_el...  5.77 us
    ppermute x1, waiting for transfers between devices, exchange_four(): h_far = lax.ppermute(second, 'aug', over_x)  5.43 us
    ppermute x1, starting transfers between devices, exchange_four(): h_far_relay = lax.ppermute(cols(a ^ 3), 'aug', over_x)  2.94 us
  transfers between devices with their start and end apart: 38, of which 19 were waited for; matrix products, arithmetic and copies ran while one was open for 16% of the time, Pallas kernels for 0%

profile of v18, /device:TPU:0, one launch (start us, length us, event | category | flops | bytes accessed | tf_op | source)
XLA Modules:
  0.0 110.6 jit_solution(13255593904596455900)
XLA Ops:
  0.7 2.3 %dynamic-slice_bitcast_fusion = (bf16[128,1280]{1,0:T(8,128)(2,1)}, bf16[128,1280]{1,0:T(8,128)(2,1)}, bf16[128,1280]{1,0:T(8,128)(2,1)}) fusion(bf16[1,1,128,5120]{3,2,1,0:T(8,128)(2,1)} %param.6, s32[]{:T(128)S(6)} %select_n.691, s32[]{:T(128)S(6)} %select_n.689, s32[]{:T(128)S(6)} %select_n.690), kind=kLoop, calls=%fused_computation.21 | loop fusion | bytes 1966092 | tf_op jit(solution)/shard_map/dynamic_slice | solution.py:101
  3.0 2.9 %collective-permute-start = (bf16[128,1280]{1,0:T(8,128)(2,1)}, bf16[128,1280]{1,0:T(8,128)(2,1)}, u32[]{:S(2)}, u32[]{:S(2)}) collective-permute-start(bf16[128,1280]{1,0:T(8,128)(2,1)} %get-tuple-element.85), channel_id=1, source_target_pairs={{0,16},{8,24},{16,0},{24,8},{1,17},{9,25},{17,1},{25,9},{2,18},{10... | collective-permute-start | bytes 983048 | tf_op jit(solution)/shard_map/ppermute | solution.py:106
  5.9 8.8 %collective-permute-done = bf16[128,1280]{1,0:T(8,128)(2,1)} collective-permute-done((bf16[128,1280]{1,0:T(8,128)(2,1)}, bf16[128,1280]{1,0:T(8,128)(2,1)}, u32[]{:S(2)}, u32[]{:S(2)}) %collective-permute-start) | collective-permute-done | bytes 327712 | tf_op jit(solution)/shard_map/ppermute | solution.py:106
  15.3 2.1 %fusion.6 = f32[1280,1280]{1,0:T(8,128)S(1)} fusion(bf16[1,1,128,5120]{3,2,1,0:T(8,128)(2,1)} %param.6, s32[]{:T(128)S(6)} %select_n.688, bf16[1,1,128,1280]{3,2,1,0:T(8,128)(2,1)} %param.7), kind=kOutput, calls=%fused_computation.19 | convolution fusion | flops 419430400 | bytes 7208964 | tf_op jit(solution)/shard_map/dot_general | solution.py:154
  17.4 2.1 %collective-permute-start.3 = (bf16[128,1280]{1,0:T(8,128)(2,1)S(1)}, bf16[128,1280]{1,0:T(8,128)(2,1)S(1)}, u32[]{:S(2)}, u32[]{:S(2)}) collective-permute-start(bf16[128,1280]{1,0:T(8,128)(2,1)S(1)} %copy-done.11), channel_id=1, source_target_pairs={{0,16},{8,24},{16,0},{24,8},{1,17},{9,25},{17,1},{25,9},{2,18},{10... | collective-permute-start | bytes 983048 | tf_op jit(solution)/shard_map/ppermute | solution.py:113
  19.5 1.8 %collective-permute-done.4 = bf16[128,1280]{1,0:T(8,128)(2,1)} collective-permute-done((bf16[128,1280]{1,0:T(8,128)(2,1)}, bf16[128,1280]{1,0:T(8,128)(2,1)}, u32[]{:S(2)}, u32[]{:S(2)}) %collective-permute-start.4) | collective-permute-done | bytes 327712 | tf_op jit(solution)/shard_map/ppermute | solution.py:105
  21.4 1.0 convolution_add_fusion.2
  22.4 5.4 %collective-permute-done.3 = bf16[128,1280]{1,0:T(8,128)(2,1)S(1)} collective-permute-done((bf16[128,1280]{1,0:T(8,128)(2,1)S(1)}, bf16[128,1280]{1,0:T(8,128)(2,1)S(1)}, u32[]{:S(2)}, u32[]{:S(2)}) %collective-permute-start.3) | collective-permute-done | bytes 327712 | tf_op jit(solution)/shard_map/ppermute | solution.py:113
  27.9 2.0 %convolution_add_fusion.1 = f32[1280,1280]{1,0:T(8,128)S(1)} fusion(f32[1280,1280]{1,0:T(8,128)S(1)} %convolution_add_fusion.2, bf16[128,1280]{1,0:T(8,128)(2,1)S(1)} %collective-permute-done.3, bf16[128,1280]{1,0:T(8,128)(2,1)} %collective-permute-done.4), kind=kOutput, calls=%fused_computation.1 | convolution fusion | flops 421068800 | bytes 13762560 | tf_op jit(solution)/shard_map/dot_general | solution.py:154
  29.9 3.9 %multiply_reduce_fusion = (f32[1280]{0:T(1024)S(1)}, f32[1280,1280]{1,0:T(8,128)}) fusion(f32[1280,1280]{1,0:T(8,128)S(1)} %convolution_add_fusion.1, bf16[128,1280]{1,0:T(8,128)(2,1)S(1)} %collective-permute-done.5, bf16[128,1280]{1,0:T(8,128)(2,1)S(1)} %collective-permute-done.6), kind=kOutput, calls=%fused_computation.4 | convolution fusion | flops 425982720 | bytes 13767680 | tf_op jit(solution)/shard_map/dot_general | solution.py:154
  33.9 0.6 reduce_sum.141
  34.6 1.7 %collective-permute-start.8 = (f32[1]{0:T(128)}, f32[1]{0:T(128)}, u32[]{:S(2)}, u32[]{:S(2)}) collective-permute-start(f32[1]{0:T(128)} %bitcast.7), channel_id=1, source_target_pairs={{0,16},{8,24},{16,0},{24,8},{1,17},{9,25},{17,1},{25,9},{2,18},{10... | collective-permute-start | bytes 20 | tf_op jit(solution)/shard_map/ppermute | solution.py:126
  36.7 1.0 collective-permute-done.7
  40.8 1.3 %dynamic-slice_multiply_fusion.3 = (f32[40,1280]{1,0:T(8,128)S(1)}, f32[40,1280]{1,0:T(8,128)S(1)}, f32[40,1280]{1,0:T(8,128)S(1)}, f32[40,1280]{1,0:T(8,128)S(1)}) fusion(f32[1280,1280]{1,0:T(8,128)} %get-tuple-element.88, s32[]{:T(128)S(6)} %select_n.707, f32[]{:T(128)} %bitcast.8, s32[]{:T(128)S(6)} %select_n.851, s32[]{:T(128)S(6)} %select_n.843, ...), kind=kLoop, calls=%fused_computation.56 | loop fusion | flops 204800 | bytes 1638420 | tf_op jit(solution)/shard_map/mul | solution.py:196
  42.2 1.6 %collective-permute-start.10 = (f32[40,1280]{1,0:T(8,128)S(1)}, f32[40,1280]{1,0:T(8,128)S(1)}, u32[]{:S(2)}, u32[]{:S(2)}) collective-permute-start(f32[40,1280]{1,0:T(8,128)S(1)} %get-tuple-element.80), channel_id=1, source_target_pairs={{0,1},{1,3},{3,5},{5,7},{7,6},{6,4},{4,2},{2,0},{8,9},{9,11},{11,1... | collective-permute-start | bytes 614408 | tf_op jit(solution)/shard_map/ppermute | solution.py:85
  44.2 1.5 %collective-permute-start.24 = (f32[40,1280]{1,0:T(8,128)S(1)}, f32[40,1280]{1,0:T(8,128)S(1)}, u32[]{:S(2)}, u32[]{:S(2)}) collective-permute-start(f32[40,1280]{1,0:T(8,128)S(1)} %get-tuple-element.82), channel_id=1, source_target_pairs={{0,1},{1,3},{3,5},{5,7},{7,6},{6,4},{4,2},{2,0},{8,9},{9,11},{11,1... | collective-permute-start | bytes 614408 | tf_op jit(solution)/shard_map/ppermute | solution.py:85
  46.3 0.9 multiply_bitcast_fusion.27
  47.2 1.0 multiply_bitcast_fusion.20
  48.2 1.0 multiply_bitcast_fusion.13
  49.1 1.0 multiply_bitcast_fusion.6
  50.2 1.5 %collective-permute-start.11 = (f32[40,1280]{1,0:T(8,128)S(1)}, f32[40,1280]{1,0:T(8,128)S(1)}, u32[]{:S(2)}, u32[]{:S(2)}) collective-permute-start(f32[40,1280]{1,0:T(8,128)S(1)} %add.518), channel_id=1, source_target_pairs={{0,1},{1,3},{3,5},{5,7},{7,6},{6,4},{4,2},{2,0},{8,9},{9,11},{11,1... | collective-permute-start | bytes 614408 | tf_op jit(solution)/shard_map/ppermute | solution.py:85
  51.8 0.6 collective-permute-start.18
  52.4 2.2 %collective-permute-done.24 = f32[40,1280]{1,0:T(8,128)S(1)} collective-permute-done((f32[40,1280]{1,0:T(8,128)S(1)}, f32[40,1280]{1,0:T(8,128)S(1)}, u32[]{:S(2)}, u32[]{:S(2)}) %collective-permute-start.24) | collective-permute-done | bytes 204832 | tf_op jit(solution)/shard_map/ppermute | solution.py:85
  54.6 1.5 %collective-permute-start.25 = (f32[40,1280]{1,0:T(8,128)S(1)}, f32[40,1280]{1,0:T(8,128)S(1)}, u32[]{:S(2)}, u32[]{:S(2)}) collective-permute-start(f32[40,1280]{1,0:T(8,128)S(1)} %add.580), channel_id=1, source_target_pairs={{0,1},{1,3},{3,5},{5,7},{7,6},{6,4},{4,2},{2,0},{8,9},{9,11},{11,1... | collective-permute-start | bytes 614408 | tf_op jit(solution)/shard_map/ppermute | solution.py:85
  56.2 0.6 collective-permute-start.32
  56.8 0.9 multiply_bitcast_fusion.26
  57.7 1.0 multiply_bitcast_fusion.19
  58.9 1.2 %fusion.4 = bf16[512,1280]{1,0:T(8,128)(2,1)S(1)} fusion(bf16[512,1280]{1,0:T(8,128)(2,1)S(1)} %broadcast_in_dim.2, s32[]{:T(128)S(6)} %select_n.859, bf16[128,1280]{1,0:T(8,128)(2,1)S(1)} %bitcast.119, bf16[1280,1280]{1,0:T(8,128)(2,1)S(1)} %copy-done), kind=kOutput, calls=%fused_computation.12 | convolution fusion | flops 419594240 | bytes 3932164 | tf_op jit(solution)/shard_map/dot_general | solution.py:17
  60.1 1.5 %collective-permute-start.12 = (f32[40,1280]{1,0:T(8,128)S(1)}, f32[40,1280]{1,0:T(8,128)S(1)}, u32[]{:S(2)}, u32[]{:S(2)}) collective-permute-start(f32[40,1280]{1,0:T(8,128)S(1)} %add.521), channel_id=1, source_target_pairs={{0,1},{1,3},{3,5},{5,7},{7,6},{6,4},{4,2},{2,0},{8,9},{9,11},{11,1... | collective-permute-start | bytes 614408 | tf_op jit(solution)/shard_map/ppermute | solution.py:85
  61.7 0.6 collective-permute-start.19
  62.3 1.1 collective-permute-done.25
  63.4 1.5 %collective-permute-start.26 = (f32[40,1280]{1,0:T(8,128)S(1)}, f32[40,1280]{1,0:T(8,128)S(1)}, u32[]{:S(2)}, u32[]{:S(2)}) collective-permute-start(f32[40,1280]{1,0:T(8,128)S(1)} %add.583), channel_id=1, source_target_pairs={{0,1},{1,3},{3,5},{5,7},{7,6},{6,4},{4,2},{2,0},{8,9},{9,11},{11,1... | collective-permute-start | bytes 614408 | tf_op jit(solution)/shard_map/ppermute | solution.py:85
  65.0 0.6 collective-permute-start.33
  65.7 1.2 %fusion.3 = bf16[512,1280]{1,0:T(8,128)(2,1)S(1)} fusion(bf16[512,1280]{1,0:T(8,128)(2,1)S(1)} %fusion.4, s32[]{:T(128)S(6)} %select_n.860, bf16[128,1280]{1,0:T(8,128)(2,1)S(1)} %copy-done.7, bf16[1280,1280]{1,0:T(8,128)(2,1)S(1)} %copy-done), kind=kOutput, calls=%fused_computation.10 | convolution fusion | flops 419594240 | bytes 3932164 | tf_op jit(solution)/shard_map/dot_general | solution.py:17
  66.9 1.3 %collective-permute-done.12 = f32[40,1280]{1,0:T(8,128)S(1)} collective-permute-done((f32[40,1280]{1,0:T(8,128)S(1)}, f32[40,1280]{1,0:T(8,128)S(1)}, u32[]{:S(2)}, u32[]{:S(2)}) %collective-permute-start.12) | collective-permute-done | bytes 204832 | tf_op jit(solution)/shard_map/ppermute | solution.py:85
  68.2 1.5 %collective-permute-start.13 = (f32[40,1280]{1,0:T(8,128)S(1)}, f32[40,1280]{1,0:T(8,128)S(1)}, u32[]{:S(2)}, u32[]{:S(2)}) collective-permute-start(f32[40,1280]{1,0:T(8,128)S(1)} %add.524), channel_id=1, source_target_pairs={{0,1},{1,3},{3,5},{5,7},{7,6},{6,4},{4,2},{2,0},{8,9},{9,11},{11,1... | collective-permute-start | bytes 614408 | tf_op jit(solution)/shard_map/ppermute | solution.py:85
  69.8 0.6 collective-permute-start.20
  70.4 2.2 %collective-permute-done.26 = f32[40,1280]{1,0:T(8,128)S(1)} collective-permute-done((f32[40,1280]{1,0:T(8,128)S(1)}, f32[40,1280]{1,0:T(8,128)S(1)}, u32[]{:S(2)}, u32[]{:S(2)}) %collective-permute-start.26) | collective-permute-done | bytes 204832 | tf_op jit(solution)/shard_map/ppermute | solution.py:85
  72.6 1.5 %collective-permute-start.27 = (f32[40,1280]{1,0:T(8,128)S(1)}, f32[40,1280]{1,0:T(8,128)S(1)}, u32[]{:S(2)}, u32[]{:S(2)}) collective-permute-start(f32[40,1280]{1,0:T(8,128)S(1)} %add.586), channel_id=1, source_target_pairs={{0,1},{1,3},{3,5},{5,7},{7,6},{6,4},{4,2},{2,0},{8,9},{9,11},{11,1... | collective-permute-start | bytes 614408 | tf_op jit(solution)/shard_map/ppermute | solution.py:85
  74.2 0.6 collective-permute-start.34
  74.9 2.2 %fusion.2 = bf16[512,1280]{1,0:T(8,128)(2,1)S(1)} fusion(bf16[512,1280]{1,0:T(8,128)(2,1)S(1)} %fusion.3, s32[]{:T(128)S(6)} %select_n.861, bf16[128,1280]{1,0:T(8,128)(2,1)} %collective-permute-done.4, bf16[1280,1280]{1,0:T(8,128)(2,1)S(1)} %copy-done), kind=kOutput, calls=%fused_computation.8 | convolution fusion | flops 419594240 | bytes 3932164 | tf_op jit(solution)/shard_map/dot_general | solution.py:17
  77.1 1.5 %collective-permute-start.14 = (f32[40,1280]{1,0:T(8,128)S(1)}, f32[40,1280]{1,0:T(8,128)S(1)}, u32[]{:S(2)}, u32[]{:S(2)}) collective-permute-start(f32[40,1280]{1,0:T(8,128)S(1)} %add.527), channel_id=1, source_target_pairs={{0,1},{1,3},{3,5},{5,7},{7,6},{6,4},{4,2},{2,0},{8,9},{9,11},{11,1... | collective-permute-start | bytes 614408 | tf_op jit(solution)/shard_map/ppermute | solution.py:85
  78.7 0.6 collective-permute-start.21
  79.3 2.1 %collective-permute-done.27 = f32[40,1280]{1,0:T(8,128)S(1)} collective-permute-done((f32[40,1280]{1,0:T(8,128)S(1)}, f32[40,1280]{1,0:T(8,128)S(1)}, u32[]{:S(2)}, u32[]{:S(2)}) %collective-permute-start.27) | collective-permute-done | bytes 204832 | tf_op jit(solution)/shard_map/ppermute | solution.py:85
  81.4 1.5 %collective-permute-start.28 = (f32[40,1280]{1,0:T(8,128)S(1)}, f32[40,1280]{1,0:T(8,128)S(1)}, u32[]{:S(2)}, u32[]{:S(2)}) collective-permute-start(f32[40,1280]{1,0:T(8,128)S(1)} %add.589), channel_id=1, source_target_pairs={{0,1},{1,3},{3,5},{5,7},{7,6},{6,4},{4,2},{2,0},{8,9},{9,11},{11,1... | collective-permute-start | bytes 614408 | tf_op jit(solution)/shard_map/ppermute | solution.py:85
  82.9 0.6 collective-permute-start.35
  83.7 1.2 %fusion.1 = bf16[512,1280]{1,0:T(8,128)(2,1)S(1)} fusion(bf16[512,1280]{1,0:T(8,128)(2,1)S(1)} %fusion.2, s32[]{:T(128)S(6)} %select_n.862, bf16[128,1280]{1,0:T(8,128)(2,1)S(1)} %copy-done.4, bf16[1280,1280]{1,0:T(8,128)(2,1)S(1)} %copy-done), kind=kOutput, calls=%fused_computation.6 | convolution fusion | flops 419594240 | bytes 3932164 | tf_op jit(solution)/shard_map/dot_general | solution.py:17
  84.9 0.8 collective-permute-done.14
  85.8 1.5 %collective-permute-start.15 = (f32[40,1280]{1,0:T(8,128)S(1)}, f32[40,1280]{1,0:T(8,128)S(1)}, u32[]{:S(2)}, u32[]{:S(2)}) collective-permute-start(f32[40,1280]{1,0:T(8,128)S(1)} %add.530), channel_id=1, source_target_pairs={{0,1},{1,3},{3,5},{5,7},{7,6},{6,4},{4,2},{2,0},{8,9},{9,11},{11,1... | collective-permute-start | bytes 614408 | tf_op jit(solution)/shard_map/ppermute | solution.py:85
  87.3 0.6 collective-permute-start.22
  87.9 2.2 %collective-permute-done.28 = f32[40,1280]{1,0:T(8,128)S(1)} collective-permute-done((f32[40,1280]{1,0:T(8,128)S(1)}, f32[40,1280]{1,0:T(8,128)S(1)}, u32[]{:S(2)}, u32[]{:S(2)}) %collective-permute-start.28) | collective-permute-done | bytes 204832 | tf_op jit(solution)/shard_map/ppermute | solution.py:85
  90.1 1.5 %collective-permute-start.29 = (f32[40,1280]{1,0:T(8,128)S(1)}, f32[40,1280]{1,0:T(8,128)S(1)}, u32[]{:S(2)}, u32[]{:S(2)}) collective-permute-start(f32[40,1280]{1,0:T(8,128)S(1)} %add.592), channel_id=1, source_target_pairs={{0,1},{1,3},{3,5},{5,7},{7,6},{6,4},{4,2},{2,0},{8,9},{9,11},{11,1... | collective-permute-start | bytes 614408 | tf_op jit(solution)/shard_map/ppermute | solution.py:85
  91.7 0.6 collective-permute-start.36
  92.4 2.1 %collective-permute-done.15 = f32[40,1280]{1,0:T(8,128)S(1)} collective-permute-done((f32[40,1280]{1,0:T(8,128)S(1)}, f32[40,1280]{1,0:T(8,128)S(1)}, u32[]{:S(2)}, u32[]{:S(2)}) %collective-permute-start.15) | collective-permute-done | bytes 204832 | tf_op jit(solution)/shard_map/ppermute | solution.py:85
  94.5 1.5 %collective-permute-start.16 = (f32[40,1280]{1,0:T(8,128)S(1)}, f32[40,1280]{1,0:T(8,128)S(1)}, u32[]{:S(2)}, u32[]{:S(2)}) collective-permute-start(f32[40,1280]{1,0:T(8,128)S(1)} %add.533), channel_id=1, source_target_pairs={{0,1},{1,3},{3,5},{5,7},{7,6},{6,4},{4,2},{2,0},{8,9},{9,11},{11,1... | collective-permute-start | bytes 614408 | tf_op jit(solution)/shard_map/ppermute | solution.py:85
  96.1 0.6 collective-permute-start.23
  96.7 2.2 %collective-permute-done.29 = f32[40,1280]{1,0:T(8,128)S(1)} collective-permute-done((f32[40,1280]{1,0:T(8,128)S(1)}, f32[40,1280]{1,0:T(8,128)S(1)}, u32[]{:S(2)}, u32[]{:S(2)}) %collective-permute-start.29) | collective-permute-done | bytes 204832 | tf_op jit(solution)/shard_map/ppermute | solution.py:85
  98.9 1.5 %collective-permute-start.30 = (f32[40,1280]{1,0:T(8,128)S(1)}, f32[40,1280]{1,0:T(8,128)S(1)}, u32[]{:S(2)}, u32[]{:S(2)}) collective-permute-start(f32[40,1280]{1,0:T(8,128)S(1)} %add.595), channel_id=1, source_target_pairs={{0,1},{1,3},{3,5},{5,7},{7,6},{6,4},{4,2},{2,0},{8,9},{9,11},{11,1... | collective-permute-start | bytes 614408 | tf_op jit(solution)/shard_map/ppermute | solution.py:85
  100.5 0.6 collective-permute-start.37
  101.2 2.1 %collective-permute-done.16 = f32[40,1280]{1,0:T(8,128)S(1)} collective-permute-done((f32[40,1280]{1,0:T(8,128)S(1)}, f32[40,1280]{1,0:T(8,128)S(1)}, u32[]{:S(2)}, u32[]{:S(2)}) %collective-permute-start.16) | collective-permute-done | bytes 204832 | tf_op jit(solution)/shard_map/ppermute | solution.py:85
  103.3 1.6 %collective-permute-done.23 = f32[40,1280]{1,0:T(8,128)S(1)} collective-permute-done((f32[40,1280]{1,0:T(8,128)S(1)}, f32[40,1280]{1,0:T(8,128)S(1)}, u32[]{:S(2)}, u32[]{:S(2)}) %collective-permute-start.23) | collective-permute-done | bytes 204832 | tf_op jit(solution)/shard_map/ppermute | solution.py:85
  104.9 1.2 %collective-permute-done.30 = f32[40,1280]{1,0:T(8,128)S(1)} collective-permute-done((f32[40,1280]{1,0:T(8,128)S(1)}, f32[40,1280]{1,0:T(8,128)S(1)}, u32[]{:S(2)}, u32[]{:S(2)}) %collective-permute-start.30) | collective-permute-done | bytes 204832 | tf_op jit(solution)/shard_map/ppermute | solution.py:85
  106.1 1.4 %collective-permute-done.37 = f32[40,1280]{1,0:T(8,128)S(1)} collective-permute-done((f32[40,1280]{1,0:T(8,128)S(1)}, f32[40,1280]{1,0:T(8,128)S(1)}, u32[]{:S(2)}, u32[]{:S(2)}) %collective-permute-start.37) | collective-permute-done | bytes 204832 | tf_op jit(solution)/shard_map/ppermute | solution.py:85
  107.5 2.0 %add_divide_fusion = (f32[160,1280]{1,0:T(8,128)}, f32[160,1280]{1,0:T(8,128)}, f32[160,1280]{1,0:T(8,128)}, f32[160,1280]{1,0:T(8,128)}) fusion(f32[160,1280]{1,0:T(8,128)S(1)} %copy-done.8, f32[160,1280]{1,0:T(8,128)S(1)} %copy-done.9, f32[160,1280]{1,0:T(8,128)S(1)} %copy-done.10, f32[40,1280]{1,0:T(8,128)S(1)} %add.621, f32[40,1280]{1,0:T(8,128)S(1)} %add.598, ...), kind=kLoop, calls=%fused_computation.16 | loop fusion | flops 3481600 | bytes 6553600 | tf_op jit(solution)/shard_map/div | solution.py:212
  (106 shorter events, 4.2 us)
Async XLA Ops:
  0.6 58.2 %copy-start = (bf16[1280,1280]{1,0:T(8,128)(2,1)S(1)}, bf16[1280,1280]{1,0:T(8,128)(2,1)}, u32[]{:S(2)}) copy-start(bf16[1280,1280]{1,0:T(8,128)(2,1)} %param.8) | copy-start | bytes 9830404
  3.0 11.8 %collective-permute-start = (bf16[128,1280]{1,0:T(8,128)(2,1)}, bf16[128,1280]{1,0:T(8,128)(2,1)}, u32[]{:S(2)}, u32[]{:S(2)}) collective-permute-start(bf16[128,1280]{1,0:T(8,128)(2,1)} %get-tuple-element.85), channel_id=1, source_target_pairs={{0,16},{8,24},{16,0},{24,8},{1,17},{9,25},{17,1},{25,9},{2,18},{10... | collective-permute-start | bytes 983048 | tf_op jit(solution)/shard_map/ppermute | solution.py:106
  5.9 15.4 %collective-permute-start.4 = (bf16[128,1280]{1,0:T(8,128)(2,1)}, bf16[128,1280]{1,0:T(8,128)(2,1)}, u32[]{:S(2)}, u32[]{:S(2)}) collective-permute-start(bf16[128,1280]{1,0:T(8,128)(2,1)} %bitcast.117), channel_id=1, source_target_pairs={{0,16},{8,24},{16,0},{24,8},{1,17},{9,25},{17,1},{25,9},{2,18},{10... | collective-permute-start | bytes 983048 | tf_op jit(solution)/shard_map/ppermute | solution.py:105
  5.9 11.4 %copy-start.11 = (bf16[128,1280]{1,0:T(8,128)(2,1)S(1)}, bf16[128,1280]{1,0:T(8,128)(2,1)}, u32[]{:S(2)}) copy-start(bf16[128,1280]{1,0:T(8,128)(2,1)} %get-tuple-element.43) | copy-start | bytes 983044
  14.8 6.6 %collective-permute-start.2 = (bf16[128,1280]{1,0:T(8,128)(2,1)}, bf16[128,1280]{1,0:T(8,128)(2,1)S(1)}, u32[]{:S(2)}, u32[]{:S(2)}) collective-permute-start(bf16[128,1280]{1,0:T(8,128)(2,1)} %bitcast.118), channel_id=1, source_target_pairs={{0,8},{8,0},{16,24},{24,16},{1,9},{9,1},{17,25},{25,17},{2,10},{10... | collective-permute-start | bytes 983048 | tf_op jit(solution)/shard_map/ppermute | solution.py:108
  14.8 6.6 %collective-permute-start.1 = (bf16[128,1280]{1,0:T(8,128)(2,1)}, bf16[128,1280]{1,0:T(8,128)(2,1)S(1)}, u32[]{:S(2)}, u32[]{:S(2)}) collective-permute-start(bf16[128,1280]{1,0:T(8,128)(2,1)} %get-tuple-element.41), channel_id=1, source_target_pairs={{0,8},{8,0},{16,24},{24,16},{1,9},{9,1},{17,25},{25,17},{2,10},{10... | collective-permute-start | bytes 983048 | tf_op jit(solution)/shard_map/ppermute | solution.py:109
  17.4 10.5 %collective-permute-start.3 = (bf16[128,1280]{1,0:T(8,128)(2,1)S(1)}, bf16[128,1280]{1,0:T(8,128)(2,1)S(1)}, u32[]{:S(2)}, u32[]{:S(2)}) collective-permute-start(bf16[128,1280]{1,0:T(8,128)(2,1)S(1)} %copy-done.11), channel_id=1, source_target_pairs={{0,16},{8,24},{16,0},{24,8},{1,17},{9,25},{17,1},{25,9},{2,18},{10... | collective-permute-start | bytes 983048 | tf_op jit(solution)/shard_map/ppermute | solution.py:113
  19.5 10.4 %collective-permute-start.5 = (bf16[128,1280]{1,0:T(8,128)(2,1)}, bf16[128,1280]{1,0:T(8,128)(2,1)S(1)}, u32[]{:S(2)}, u32[]{:S(2)}) collective-permute-start(bf16[128,1280]{1,0:T(8,128)(2,1)} %collective-permute-done), channel_id=1, source_target_pairs={{0,8},{8,0},{16,24},{24,16},{1,9},{9,1},{17,25},{25,17},{2,10},{10... | collective-permute-start | bytes 983048 | tf_op jit(solution)/shard_map/ppermute | solution.py:111
  21.3 8.6 %collective-permute-start.6 = (bf16[128,1280]{1,0:T(8,128)(2,1)}, bf16[128,1280]{1,0:T(8,128)(2,1)S(1)}, u32[]{:S(2)}, u32[]{:S(2)}) collective-permute-start(bf16[128,1280]{1,0:T(8,128)(2,1)} %collective-permute-done.4), channel_id=1, source_target_pairs={{0,8},{8,0},{16,24},{24,16},{1,9},{9,1},{17,25},{25,17},{2,10},{10... | collective-permute-start | bytes 983048 | tf_op jit(solution)/shard_map/ppermute | solution.py:110
  21.4 1.1 copy-start.6
  29.9 3.9 %copy-start.3 = (bf16[128,1280]{1,0:T(8,128)(2,1)}, bf16[128,1280]{1,0:T(8,128)(2,1)S(1)}, u32[]{:S(2)}) copy-start(bf16[128,1280]{1,0:T(8,128)(2,1)S(1)} %collective-permute-done.6) | copy-start | bytes 983044
  34.5 24.1 %copy-start.1 = (f32[1280,1280]{1,0:T(8,128)S(1)}, f32[1280,1280]{1,0:T(8,128)}, u32[]{:S(2)}) copy-start(f32[1280,1280]{1,0:T(8,128)} %get-tuple-element.88) | copy-start | bytes 19660804
  34.6 24.3 %copy-start.2 = (bf16[1,1,128,1280]{3,2,1,0:T(8,128)(2,1)S(1)}, bf16[1,1,128,1280]{3,2,1,0:T(8,128)(2,1)}, u32[]{:S(2)}) copy-start(bf16[1,1,128,1280]{3,2,1,0:T(8,128)(2,1)} %param.7) | copy-start | bytes 983044
  34.6 4.4 %collective-permute-start.8 = (f32[1]{0:T(128)}, f32[1]{0:T(128)}, u32[]{:S(2)}, u32[]{:S(2)}) collective-permute-start(f32[1]{0:T(128)} %bitcast.7), channel_id=1, source_target_pairs={{0,16},{8,24},{16,0},{24,8},{1,17},{9,25},{17,1},{25,9},{2,18},{10... | collective-permute-start | bytes 20 | tf_op jit(solution)/shard_map/ppermute | solution.py:126
  36.3 3.2 %collective-permute-start.9 = (f32[1]{0:T(128)}, f32[1]{0:T(128)}, u32[]{:S(2)}, u32[]{:S(2)}) collective-permute-start(f32[1]{0:T(128)} %bitcast.7), channel_id=1, source_target_pairs={{0,24},{8,16},{16,8},{24,0},{1,25},{9,17},{17,9},{25,1},{2,26},{10... | collective-permute-start | bytes 20 | tf_op jit(solution)/shard_map/ppermute | solution.py:126
  36.3 1.3 %collective-permute-start.7 = (f32[1]{0:T(128)}, f32[1]{0:T(128)}, u32[]{:S(2)}, u32[]{:S(2)}) collective-permute-start(f32[1]{0:T(128)} %bitcast.7), channel_id=1, source_target_pairs={{0,8},{8,0},{16,24},{24,16},{1,9},{9,1},{17,25},{25,17},{2,10},{10... | collective-permute-start | bytes 20 | tf_op jit(solution)/shard_map/ppermute | solution.py:126
  42.2 8.0 %collective-permute-start.10 = (f32[40,1280]{1,0:T(8,128)S(1)}, f32[40,1280]{1,0:T(8,128)S(1)}, u32[]{:S(2)}, u32[]{:S(2)}) collective-permute-start(f32[40,1280]{1,0:T(8,128)S(1)} %get-tuple-element.80), channel_id=1, source_target_pairs={{0,1},{1,3},{3,5},{5,7},{7,6},{6,4},{4,2},{2,0},{8,9},{9,11},{11,1... | collective-permute-start | bytes 614408 | tf_op jit(solution)/shard_map/ppermute | solution.py:85
  43.7 8.0 %collective-permute-start.17 = (f32[40,1280]{1,0:T(8,128)S(1)}, f32[40,1280]{1,0:T(8,128)S(1)}, u32[]{:S(2)}, u32[]{:S(2)}) collective-permute-start(f32[40,1280]{1,0:T(8,128)S(1)} %get-tuple-element.83), channel_id=1, source_target_pairs={{0,2},{1,0},{3,1},{5,3},{7,5},{6,7},{4,6},{2,4},{8,10},{9,8},{11,9... | collective-permute-start | bytes 614408 | tf_op jit(solution)/shard_map/ppermute | solution.py:85
  44.2 10.3 %collective-permute-start.24 = (f32[40,1280]{1,0:T(8,128)S(1)}, f32[40,1280]{1,0:T(8,128)S(1)}, u32[]{:S(2)}, u32[]{:S(2)}) collective-permute-start(f32[40,1280]{1,0:T(8,128)S(1)} %get-tuple-element.82), channel_id=1, source_target_pairs={{0,1},{1,3},{3,5},{5,7},{7,6},{6,4},{4,2},{2,0},{8,9},{9,11},{11,1... | collective-permute-start | bytes 614408 | tf_op jit(solution)/shard_map/ppermute | solution.py:85
  45.8 10.4 %collective-permute-start.31 = (f32[40,1280]{1,0:T(8,128)S(1)}, f32[40,1280]{1,0:T(8,128)S(1)}, u32[]{:S(2)}, u32[]{:S(2)}) collective-permute-start(f32[40,1280]{1,0:T(8,128)S(1)} %get-tuple-element.81), channel_id=1, source_target_pairs={{0,2},{1,0},{3,1},{5,3},{7,5},{6,7},{4,6},{2,4},{8,10},{9,8},{11,9... | collective-permute-start | bytes 614408 | tf_op jit(solution)/shard_map/ppermute | solution.py:85
  50.2 15.5 %copy-start.7 = (bf16[128,1280]{1,0:T(8,128)(2,1)S(1)}, bf16[128,1280]{1,0:T(8,128)(2,1)}, u32[]{:S(2)}) copy-start(bf16[128,1280]{1,0:T(8,128)(2,1)} %copy-done.6) | copy-start | bytes 983044
  50.2 9.8 %collective-permute-start.11 = (f32[40,1280]{1,0:T(8,128)S(1)}, f32[40,1280]{1,0:T(8,128)S(1)}, u32[]{:S(2)}, u32[]{:S(2)}) collective-permute-start(f32[40,1280]{1,0:T(8,128)S(1)} %add.518), channel_id=1, source_target_pairs={{0,1},{1,3},{3,5},{5,7},{7,6},{6,4},{4,2},{2,0},{8,9},{9,11},{11,1... | collective-permute-start | bytes 614408 | tf_op jit(solution)/shard_map/ppermute | solution.py:85
  51.8 9.9 %collective-permute-start.18 = (f32[40,1280]{1,0:T(8,128)S(1)}, f32[40,1280]{1,0:T(8,128)S(1)}, u32[]{:S(2)}, u32[]{:S(2)}) collective-permute-start(f32[40,1280]{1,0:T(8,128)S(1)} %add.545), channel_id=1, source_target_pairs={{0,2},{1,0},{3,1},{5,3},{7,5},{6,7},{4,6},{2,4},{8,10},{9,8},{11,9... | collective-permute-start | bytes 614408 | tf_op jit(solution)/shard_map/ppermute | solution.py:85
  54.6 8.8 %collective-permute-start.25 = (f32[40,1280]{1,0:T(8,128)S(1)}, f32[40,1280]{1,0:T(8,128)S(1)}, u32[]{:S(2)}, u32[]{:S(2)}) collective-permute-start(f32[40,1280]{1,0:T(8,128)S(1)} %add.580), channel_id=1, source_target_pairs={{0,1},{1,3},{3,5},{5,7},{7,6},{6,4},{4,2},{2,0},{8,9},{9,11},{11,1... | collective-permute-start | bytes 614408 | tf_op jit(solution)/shard_map/ppermute | solution.py:85
  56.2 8.8 %collective-permute-start.32 = (f32[40,1280]{1,0:T(8,128)S(1)}, f32[40,1280]{1,0:T(8,128)S(1)}, u32[]{:S(2)}, u32[]{:S(2)}) collective-permute-start(f32[40,1280]{1,0:T(8,128)S(1)} %add.603), channel_id=1, source_target_pairs={{0,2},{1,0},{3,1},{5,3},{7,5},{6,7},{4,6},{2,4},{8,10},{9,8},{11,9... | collective-permute-start | bytes 614408 | tf_op jit(solution)/shard_map/ppermute | solution.py:85
  60.1 8.1 %collective-permute-start.12 = (f32[40,1280]{1,0:T(8,128)S(1)}, f32[40,1280]{1,0:T(8,128)S(1)}, u32[]{:S(2)}, u32[]{:S(2)}) collective-permute-start(f32[40,1280]{1,0:T(8,128)S(1)} %add.521), channel_id=1, source_target_pairs={{0,1},{1,3},{3,5},{5,7},{7,6},{6,4},{4,2},{2,0},{8,9},{9,11},{11,1... | collective-permute-start | bytes 614408 | tf_op jit(solution)/shard_map/ppermute | solution.py:85
  61.7 8.1 %collective-permute-start.19 = (f32[40,1280]{1,0:T(8,128)S(1)}, f32[40,1280]{1,0:T(8,128)S(1)}, u32[]{:S(2)}, u32[]{:S(2)}) collective-permute-start(f32[40,1280]{1,0:T(8,128)S(1)} %add.550), channel_id=1, source_target_pairs={{0,2},{1,0},{3,1},{5,3},{7,5},{6,7},{4,6},{2,4},{8,10},{9,8},{11,9... | collective-permute-start | bytes 614408 | tf_op jit(solution)/shard_map/ppermute | solution.py:85
  63.4 9.2 %collective-permute-start.26 = (f32[40,1280]{1,0:T(8,128)S(1)}, f32[40,1280]{1,0:T(8,128)S(1)}, u32[]{:S(2)}, u32[]{:S(2)}) collective-permute-start(f32[40,1280]{1,0:T(8,128)S(1)} %add.583), channel_id=1, source_target_pairs={{0,1},{1,3},{3,5},{5,7},{7,6},{6,4},{4,2},{2,0},{8,9},{9,11},{11,1... | collective-permute-start | bytes 614408 | tf_op jit(solution)/shard_map/ppermute | solution.py:85
  65.0 9.2 %collective-permute-start.33 = (f32[40,1280]{1,0:T(8,128)S(1)}, f32[40,1280]{1,0:T(8,128)S(1)}, u32[]{:S(2)}, u32[]{:S(2)}) collective-permute-start(f32[40,1280]{1,0:T(8,128)S(1)} %add.606), channel_id=1, source_target_pairs={{0,2},{1,0},{3,1},{5,3},{7,5},{6,7},{4,6},{2,4},{8,10},{9,8},{11,9... | collective-permute-start | bytes 614408 | tf_op jit(solution)/shard_map/ppermute | solution.py:85
  66.9 16.8 %copy-start.4 = (bf16[128,1280]{1,0:T(8,128)(2,1)S(1)}, bf16[128,1280]{1,0:T(8,128)(2,1)}, u32[]{:S(2)}) copy-start(bf16[128,1280]{1,0:T(8,128)(2,1)} %copy-done.3) | copy-start | bytes 983044
  68.2 8.9 %collective-permute-start.13 = (f32[40,1280]{1,0:T(8,128)S(1)}, f32[40,1280]{1,0:T(8,128)S(1)}, u32[]{:S(2)}, u32[]{:S(2)}) collective-permute-start(f32[40,1280]{1,0:T(8,128)S(1)} %add.524), channel_id=1, source_target_pairs={{0,1},{1,3},{3,5},{5,7},{7,6},{6,4},{4,2},{2,0},{8,9},{9,11},{11,1... | collective-permute-start | bytes 614408 | tf_op jit(solution)/shard_map/ppermute | solution.py:85
  69.8 8.9 %collective-permute-start.20 = (f32[40,1280]{1,0:T(8,128)S(1)}, f32[40,1280]{1,0:T(8,128)S(1)}, u32[]{:S(2)}, u32[]{:S(2)}) collective-permute-start(f32[40,1280]{1,0:T(8,128)S(1)} %add.555), channel_id=1, source_target_pairs={{0,2},{1,0},{3,1},{5,3},{7,5},{6,7},{4,6},{2,4},{8,10},{9,8},{11,9... | collective-permute-start | bytes 614408 | tf_op jit(solution)/shard_map/ppermute | solution.py:85
  72.6 8.8 %collective-permute-start.27 = (f32[40,1280]{1,0:T(8,128)S(1)}, f32[40,1280]{1,0:T(8,128)S(1)}, u32[]{:S(2)}, u32[]{:S(2)}) collective-permute-start(f32[40,1280]{1,0:T(8,128)S(1)} %add.586), channel_id=1, source_target_pairs={{0,1},{1,3},{3,5},{5,7},{7,6},{6,4},{4,2},{2,0},{8,9},{9,11},{11,1... | collective-permute-start | bytes 614408 | tf_op jit(solution)/shard_map/ppermute | solution.py:85
  74.2 8.8 %collective-permute-start.34 = (f32[40,1280]{1,0:T(8,128)S(1)}, f32[40,1280]{1,0:T(8,128)S(1)}, u32[]{:S(2)}, u32[]{:S(2)}) collective-permute-start(f32[40,1280]{1,0:T(8,128)S(1)} %add.609), channel_id=1, source_target_pairs={{0,2},{1,0},{3,1},{5,3},{7,5},{6,7},{4,6},{2,4},{8,10},{9,8},{11,9... | collective-permute-start | bytes 614408 | tf_op jit(solution)/shard_map/ppermute | solution.py:85
  77.1 8.6 %collective-permute-start.14 = (f32[40,1280]{1,0:T(8,128)S(1)}, f32[40,1280]{1,0:T(8,128)S(1)}, u32[]{:S(2)}, u32[]{:S(2)}) collective-permute-start(f32[40,1280]{1,0:T(8,128)S(1)} %add.527), channel_id=1, source_target_pairs={{0,1},{1,3},{3,5},{5,7},{7,6},{6,4},{4,2},{2,0},{8,9},{9,11},{11,1... | collective-permute-start | bytes 614408 | tf_op jit(solution)/shard_map/ppermute | solution.py:85
  78.7 8.6 %collective-permute-start.21 = (f32[40,1280]{1,0:T(8,128)S(1)}, f32[40,1280]{1,0:T(8,128)S(1)}, u32[]{:S(2)}, u32[]{:S(2)}) collective-permute-start(f32[40,1280]{1,0:T(8,128)S(1)} %add.560), channel_id=1, source_target_pairs={{0,2},{1,0},{3,1},{5,3},{7,5},{6,7},{4,6},{2,4},{8,10},{9,8},{11,9... | collective-permute-start | bytes 614408 | tf_op jit(solution)/shard_map/ppermute | solution.py:85
  81.4 8.8 %collective-permute-start.28 = (f32[40,1280]{1,0:T(8,128)S(1)}, f32[40,1280]{1,0:T(8,128)S(1)}, u32[]{:S(2)}, u32[]{:S(2)}) collective-permute-start(f32[40,1280]{1,0:T(8,128)S(1)} %add.589), channel_id=1, source_target_pairs={{0,1},{1,3},{3,5},{5,7},{7,6},{6,4},{4,2},{2,0},{8,9},{9,11},{11,1... | collective-permute-start | bytes 614408 | tf_op jit(solution)/shard_map/ppermute | solution.py:85
  82.9 8.8 %collective-permute-start.35 = (f32[40,1280]{1,0:T(8,128)S(1)}, f32[40,1280]{1,0:T(8,128)S(1)}, u32[]{:S(2)}, u32[]{:S(2)}) collective-permute-start(f32[40,1280]{1,0:T(8,128)S(1)} %add.612), channel_id=1, source_target_pairs={{0,2},{1,0},{3,1},{5,3},{7,5},{6,7},{4,6},{2,4},{8,10},{9,8},{11,9... | collective-permute-start | bytes 614408 | tf_op jit(solution)/shard_map/ppermute | solution.py:85
  83.7 23.8 %copy-start.8 = (f32[160,1280]{1,0:T(8,128)S(1)}, f32[160,1280]{1,0:T(8,128)}, u32[]{:S(2)}) copy-start(f32[160,1280]{1,0:T(8,128)} %param.11) | copy-start | bytes 2457604
  83.7 23.8 %copy-start.9 = (f32[160,1280]{1,0:T(8,128)S(1)}, f32[160,1280]{1,0:T(8,128)}, u32[]{:S(2)}) copy-start(f32[160,1280]{1,0:T(8,128)} %param.10) | copy-start | bytes 2457604
  83.7 23.8 %copy-start.10 = (f32[160,1280]{1,0:T(8,128)S(1)}, f32[160,1280]{1,0:T(8,128)}, u32[]{:S(2)}) copy-start(f32[160,1280]{1,0:T(8,128)} %param.9) | copy-start | bytes 2457604
  84.9 24.6 %copy-start.5 = (bf16[512,1280]{1,0:T(8,128)(2,1)}, bf16[512,1280]{1,0:T(8,128)(2,1)S(1)}, u32[]{:S(2)}) copy-start(bf16[512,1280]{1,0:T(8,128)(2,1)S(1)} %fusion.1) | copy-start | bytes 3932164
  85.8 8.7 %collective-permute-start.15 = (f32[40,1280]{1,0:T(8,128)S(1)}, f32[40,1280]{1,0:T(8,128)S(1)}, u32[]{:S(2)}, u32[]{:S(2)}) collective-permute-start(f32[40,1280]{1,0:T(8,128)S(1)} %add.530), channel_id=1, source_target_pairs={{0,1},{1,3},{3,5},{5,7},{7,6},{6,4},{4,2},{2,0},{8,9},{9,11},{11,1... | collective-permute-start | bytes 614408 | tf_op jit(solution)/shard_map/ppermute | solution.py:85
  87.3 8.7 %collective-permute-start.22 = (f32[40,1280]{1,0:T(8,128)S(1)}, f32[40,1280]{1,0:T(8,128)S(1)}, u32[]{:S(2)}, u32[]{:S(2)}) collective-permute-start(f32[40,1280]{1,0:T(8,128)S(1)} %add.565), channel_id=1, source_target_pairs={{0,2},{1,0},{3,1},{5,3},{7,5},{6,7},{4,6},{2,4},{8,10},{9,8},{11,9... | collective-permute-start | bytes 614408 | tf_op jit(solution)/shard_map/ppermute | solution.py:85
  90.1 8.7 %collective-permute-start.29 = (f32[40,1280]{1,0:T(8,128)S(1)}, f32[40,1280]{1,0:T(8,128)S(1)}, u32[]{:S(2)}, u32[]{:S(2)}) collective-permute-start(f32[40,1280]{1,0:T(8,128)S(1)} %add.592), channel_id=1, source_target_pairs={{0,1},{1,3},{3,5},{5,7},{7,6},{6,4},{4,2},{2,0},{8,9},{9,11},{11,1... | collective-permute-start | bytes 614408 | tf_op jit(solution)/shard_map/ppermute | solution.py:85
  91.7 8.7 %collective-permute-start.36 = (f32[40,1280]{1,0:T(8,128)S(1)}, f32[40,1280]{1,0:T(8,128)S(1)}, u32[]{:S(2)}, u32[]{:S(2)}) collective-permute-start(f32[40,1280]{1,0:T(8,128)S(1)} %add.615), channel_id=1, source_target_pairs={{0,2},{1,0},{3,1},{5,3},{7,5},{6,7},{4,6},{2,4},{8,10},{9,8},{11,9... | collective-permute-start | bytes 614408 | tf_op jit(solution)/shard_map/ppermute | solution.py:85
  94.5 8.7 %collective-permute-start.16 = (f32[40,1280]{1,0:T(8,128)S(1)}, f32[40,1280]{1,0:T(8,128)S(1)}, u32[]{:S(2)}, u32[]{:S(2)}) collective-permute-start(f32[40,1280]{1,0:T(8,128)S(1)} %add.533), channel_id=1, source_target_pairs={{0,1},{1,3},{3,5},{5,7},{7,6},{6,4},{4,2},{2,0},{8,9},{9,11},{11,1... | collective-permute-start | bytes 614408 | tf_op jit(solution)/shard_map/ppermute | solution.py:85
  96.1 8.7 %collective-permute-start.23 = (f32[40,1280]{1,0:T(8,128)S(1)}, f32[40,1280]{1,0:T(8,128)S(1)}, u32[]{:S(2)}, u32[]{:S(2)}) collective-permute-start(f32[40,1280]{1,0:T(8,128)S(1)} %add.570), channel_id=1, source_target_pairs={{0,2},{1,0},{3,1},{5,3},{7,5},{6,7},{4,6},{2,4},{8,10},{9,8},{11,9... | collective-permute-start | bytes 614408 | tf_op jit(solution)/shard_map/ppermute | solution.py:85
  98.9 7.1 %collective-permute-start.30 = (f32[40,1280]{1,0:T(8,128)S(1)}, f32[40,1280]{1,0:T(8,128)S(1)}, u32[]{:S(2)}, u32[]{:S(2)}) collective-permute-start(f32[40,1280]{1,0:T(8,128)S(1)} %add.595), channel_id=1, source_target_pairs={{0,1},{1,3},{3,5},{5,7},{7,6},{6,4},{4,2},{2,0},{8,9},{9,11},{11,1... | collective-permute-start | bytes 614408 | tf_op jit(solution)/shard_map/ppermute | solution.py:85
  100.5 6.9 %collective-permute-start.37 = (f32[40,1280]{1,0:T(8,128)S(1)}, f32[40,1280]{1,0:T(8,128)S(1)}, u32[]{:S(2)}, u32[]{:S(2)}) collective-permute-start(f32[40,1280]{1,0:T(8,128)S(1)} %add.618), channel_id=1, source_target_pairs={{0,2},{1,0},{3,1},{5,3},{7,5},{6,7},{4,6},{2,4},{8,10},{9,8},{11,9... | collective-permute-start | bytes 614408 | tf_op jit(solution)/shard_map/ppermute | solution.py:85
